TPU v7x, 32 devices: a whole 2x2x4 slice. The times are simulated.
32 devices in a mesh: groups: 2 (over y), lon: 16 (over z, x, core).
Axes of the slice: x: 2, y: 2, z: 4, core: 2. Of those that a mesh axis runs over, the one named last changes fastest.
Arguments:
- features: bfloat16 [4, 256, 32, 256], P(None, ('groups', 'lon')), parts along dimension 1, may hold values from -6 to 6
- target: bfloat16 [256, 32, 256], P(('groups', 'lon')), parts along dimension 0, may hold values from -6 to 6
- south_rim: bfloat16 [4, 256, 3, 256], P(None, ('groups', 'lon')), parts along dimension 1, may hold values from -6 to 6
- kmt: int32 [256, 32], P(('groups', 'lon')), parts along dimension 0, may hold values from 0 to 19
- dw_kernel: float32 [7, 7, 256], replicated, may hold values from -0.875 to 0.875
- dw_bias: float32 [256], replicated, may hold values from -3 to 3
- ln_gain: float32 [256], replicated, may hold values from 0.25 to 1.75
- ln_bias: float32 [256], replicated, may hold values from -3 to 3
- w_in: bfloat16 [256, 1024], replicated, may hold values from -0.375 to 0.375
- b_in: float32 [1024], replicated, may hold values from -3 to 3
- w_out: bfloat16 [1024, 256], replicated, may hold values from -0.1875 to 0.1875
- b_out: float32 [256], replicated, may hold values from -3 to 3
- layer_scale: float32 [256], replicated, may hold values from 0.3 to 1.5
Outputs:
- predicted: bfloat16 [4, 256, 32, 256], P(None, ('groups', 'lon')), parts along dimension 1
- crps_field: float32 [256, 32, 256], P(('groups', 'lon')), parts along dimension 0
- grad_features: bfloat16 [4, 256, 32, 256], P(None, ('groups', 'lon')), parts along dimension 1
- grad_kernel: float32 [14, 7, 256], P('groups'), parts along dimension 0
- grad_dw_bias: float32 [512], P('groups'), parts along dimension 0
- grad_ln_gain: float32 [512], P('groups'), parts along dimension 0
- grad_ln_bias: float32 [512], P('groups'), parts along dimension 0
- grad_w_in: float32 [512, 1024], P('groups'), parts along dimension 0
- grad_b_in: float32 [2048], P('groups'), parts along dimension 0
- grad_w_out: float32 [2048, 256], P('groups'), parts along dimension 0
- grad_b_out: float32 [512], P('groups'), parts along dimension 0
- grad_scale: float32 [512], P('groups'), parts along dimension 0
There are 2 independent parts, one for each index of `groups`. A program takes and returns all parts, laid end to end along the dimension named above; an argument that names none is the same for every part. Nothing has to cross between parts.
All inputs are finite; a program needn't handle non-finite values.
Results may differ from a plain program's by a relative error of at most 0.0075.
Values may be sent and summed in bfloat16 or wider, within the bound.
No kernel may reach another device: no remote copies, remote signals or barrier semaphores. Data moves between devices by JAX's collectives and lax.ppermute only.
A program may use at most 64 MiB of HBM per device.

v0:
```python
import math

import jax
import jax.numpy as jnp
from jax import lax
from jax.sharding import PartitionSpec as P

LEVELS = 19


SMOOTH = 0.25
EPSILON = 1e-06


def swapped(x, axis, bit):
    return lax.ppermute(x, axis, [(i, i ^ 1 << bit) for i in range(lax.axis_size(axis))])


def with_halo(x, sides, width):
    for axis, dim in sides:
        size, length = (lax.axis_size(axis), x.shape[dim])
        up = [(i, (i + 1) % size) for i in range(size)]
        down = [(j, i) for i, j in up]
        last = lax.slice_in_dim(x, length - width, length, axis=dim)
        leading = lax.slice_in_dim(x, 0, width, axis=dim)
        before = lax.ppermute(last, axis, up)
        after = lax.ppermute(leading, axis, down)
        x = jnp.concatenate([before, x, after], axis=dim)
    return x


def smooth_abs(value):
    return jnp.sqrt(value * value + SMOOTH * SMOOTH) - SMOOTH


def smooth_slope(value):
    return value / jnp.sqrt(value * value + SMOOTH * SMOOTH)


def local_step(
    extended,
    features,
    target,
    kmt,
    dw_kernel,
    dw_bias,
    ln_gain,
    ln_bias,
    w_in,
    b_in,
    w_out,
    b_out,
    layer_scale,
):
    members, lon_dev, lat_rows, chans = features.shape
    depth = jnp.zeros(features.shape, jnp.float32) + dw_bias
    for lon_off in range(7):
        for lat_off in range(7):
            depth = depth + dw_kernel[lon_off, lat_off] * extended[
                :, lon_off : lon_off + lon_dev, lat_off : lat_off + lat_rows, :
            ].astype(jnp.float32)
    mean_val = jnp.mean(depth, axis=-1, keepdims=True)
    centred = depth - mean_val
    variance = jnp.mean(centred * centred, axis=-1, keepdims=True)
    inv_std = lax.rsqrt(variance + EPSILON)
    unit = centred * inv_std
    normed = (unit * ln_gain + ln_bias).astype(jnp.bfloat16)
    level_of = jnp.arange(chans, dtype=jnp.int32) * LEVELS // chans
    wet_mask = (level_of[None, None, :] < kmt[:, :, None]).astype(jnp.float32)
    rows = lon_dev * lat_rows
    pre_acts = []
    hiddens = []
    outputs = []
    for member in range(members):
        flat_rows = normed[member].reshape(rows, chans)
        pre_act = jnp.dot(flat_rows, w_in, preferred_element_type=jnp.float32) + b_in
        hidden = jax.nn.gelu(pre_act).astype(jnp.bfloat16)
        pre_acts.append(pre_act)
        hiddens.append(hidden)
        outputs.append(
            (jnp.dot(hidden, w_out, preferred_element_type=jnp.float32) + b_out).reshape(
                lon_dev, lat_rows, chans
            )
        )
    branch = jnp.stack(outputs)
    pred = wet_mask * (features.astype(jnp.float32) + layer_scale * branch)
    target_full = target.astype(jnp.float32)
    pair_weight = 1.0 / (members * (members - 1))
    skill = jnp.zeros(target.shape, jnp.float32)
    spread = jnp.zeros(target.shape, jnp.float32)
    for member in range(members):
        skill = skill + smooth_abs(pred[member] - target_full)
        for other in range(member + 1, members):
            spread = spread + smooth_abs(pred[member] - pred[other])
    crps_field = wet_mask * (skill / members - pair_weight * spread)
    grad_list = []
    for member in range(members):
        slope_sum = jnp.zeros(target.shape, jnp.float32)
        for other in range(members):
            if other != member:
                slope_sum = slope_sum + smooth_slope(pred[member] - pred[other])
        grad_list.append(
            wet_mask
            * (smooth_slope(pred[member] - target_full) / members - pair_weight * slope_sum)
        )
    grad_pred = jnp.stack(grad_list)
    grad_scale = jnp.sum(grad_pred * branch, axis=(0, 1, 2))
    grad_b_out = jnp.zeros((chans,), jnp.float32)
    grad_w_out = jnp.zeros(w_out.shape, jnp.float32)
    grad_b_in = jnp.zeros(b_in.shape, jnp.float32)
    grad_w_in = jnp.zeros(w_in.shape, jnp.float32)
    normed_grads = []
    contract_rows = (((0,), (0,)), ((), ()))
    contract_cols = (((1,), (1,)), ((), ()))
    for member in range(members):
        grad_out = (grad_pred[member] * layer_scale).reshape(rows, chans)
        grad_b_out = grad_b_out + jnp.sum(grad_out, axis=0)
        out_half = grad_out.astype(jnp.bfloat16)
        grad_w_out = grad_w_out + lax.dot_general(
            hiddens[member], out_half, contract_rows, preferred_element_type=jnp.float32
        )
        grad_hidden = lax.dot_general(
            out_half, w_out, contract_cols, preferred_element_type=jnp.float32
        )
        grad_pre = jax.vjp(jax.nn.gelu, pre_acts[member])[1](grad_hidden)[0]
        grad_b_in = grad_b_in + jnp.sum(grad_pre, axis=0)
        pre_half = grad_pre.astype(jnp.bfloat16)
        grad_w_in = grad_w_in + lax.dot_general(
            normed[member].reshape(rows, chans),
            pre_half,
            contract_rows,
            preferred_element_type=jnp.float32,
        )
        normed_grads.append(
            lax.dot_general(
                pre_half, w_in, contract_cols, preferred_element_type=jnp.float32
            ).reshape(lon_dev, lat_rows, chans)
        )
    grad_normed = jnp.stack(normed_grads)
    grad_ln_gain = jnp.sum(grad_normed * unit, axis=(0, 1, 2))
    grad_ln_bias = jnp.sum(grad_normed, axis=(0, 1, 2))
    grad_unit = grad_normed * ln_gain
    grad_depth = inv_std * (
        grad_unit
        - jnp.mean(grad_unit, axis=-1, keepdims=True)
        - unit * jnp.mean(grad_unit * unit, axis=-1, keepdims=True)
    )
    grad_dw_bias = jnp.sum(grad_depth, axis=(0, 1, 2))
    kernel_rows = []
    for lon_off in range(7):
        kernel_cols = []
        for lat_off in range(7):
            kernel_cols.append(
                jnp.sum(
                    grad_depth
                    * extended[
                        :, lon_off : lon_off + lon_dev, lat_off : lat_off + lat_rows, :
                    ].astype(jnp.float32),
                    axis=(0, 1, 2),
                )
            )
        kernel_rows.append(jnp.stack(kernel_cols))
    grad_kernel = jnp.stack(kernel_rows)
    grads = (
        grad_kernel,
        grad_dw_bias,
        grad_ln_gain,
        grad_ln_bias,
        grad_w_in,
        grad_b_in,
        grad_w_out,
        grad_b_out,
        grad_scale,
    )
    return (pred.astype(jnp.bfloat16), crps_field, grad_pred, grad_depth, grads)


def mirror_rows(top_rows):
    picked = top_rows
    for bit_index in range(lax.axis_size("lon").bit_length() - 1):
        picked = swapped(picked, "lon", bit_index)
    return picked[:, ::-1, ::-1, :]


def mirror_grads(fold_rows):
    picked = fold_rows
    for bit_index in range(lax.axis_size("lon").bit_length() - 1):
        picked = swapped(picked.astype(jnp.bfloat16), "lon", bit_index).astype(picked.dtype)
    return picked[:, ::-1, ::-1, :]


def on_device(
    features,
    target,
    south_rim,
    kmt,
    dw_kernel,
    dw_bias,
    ln_gain,
    ln_bias,
    w_in,
    b_in,
    w_out,
    b_out,
    layer_scale,
):
    members, lon_dev, lat_rows, chans = features.shape
    params = (dw_kernel, dw_bias, ln_gain, ln_bias, w_in, b_in, w_out, b_out, layer_scale)
    north_rows = mirror_rows(features[:, :, lat_rows - 3 :, :])
    joined = jnp.concatenate([south_rim, features, north_rows], axis=2)
    extended = with_halo(joined, (("lon", 1),), 3)
    predicted, crps_field, grad_pred, grad_depth, grads = local_step(
        extended, features, target, kmt, *params
    )
    grad_halo = with_halo(grad_depth, (("lon", 1),), 3)
    padded = jnp.pad(grad_halo, ((0, 0), (0, 0), (6, 6), (0, 0)))
    grad_ext = jnp.zeros((members, lon_dev, lat_rows + 6, chans), jnp.float32)
    for lon_off in range(7):
        for lat_off in range(7):
            grad_ext = (
                grad_ext
                + dw_kernel[lon_off, lat_off]
                * padded[
                    :,
                    6 - lon_off : 6 - lon_off + lon_dev,
                    6 - lat_off : 6 - lat_off + lat_rows + 6,
                    :,
                ]
            )
    back_rows = mirror_grads(grad_ext[:, :, lat_rows + 3 :, :])
    inner = grad_pred + grad_ext[:, :, 3 : lat_rows + 3, :]
    grad_features = jnp.concatenate(
        [inner[:, :, : lat_rows - 3, :], inner[:, :, lat_rows - 3 :, :] + back_rows], axis=2
    ).astype(jnp.bfloat16)
    (
        kernel_sum,
        dw_bias_sum,
        gain_sum,
        bias_sum,
        w_in_sum,
        b_in_sum,
        w_out_sum,
        b_out_sum,
        scale_sum,
    ) = grads
    totals = lax.psum(
        (
            kernel_sum,
            dw_bias_sum,
            gain_sum,
            bias_sum,
            w_in_sum,
            b_in_sum,
            w_out_sum,
            b_out_sum,
            scale_sum,
        ),
        "lon",
    )
    factor = 1.0 / math.sqrt(members * lat_rows * lon_dev * lax.axis_size("lon"))
    return (
        predicted,
        crps_field,
        grad_features,
        totals[0] * factor,
        totals[1] * factor,
        totals[2] * factor,
        totals[3] * factor,
        totals[4] * factor,
        totals[5] * factor,
        totals[6] * factor,
        totals[7] * factor,
        totals[8] * factor,
    )


def solution(mesh):
    placed = (
        P(None, ("groups", "lon"), None, None),
        P(("groups", "lon"), None, None),
        P(None, ("groups", "lon"), None, None),
        P(("groups", "lon"), None),
        P(),
        P(),
        P(),
        P(),
        P(),
        P(),
        P(),
        P(),
        P(),
    )
    return jax.shard_map(
        on_device,
        mesh=mesh,
        in_specs=placed,
        out_specs=(
            P(None, ("groups", "lon"), None, None),
            P(("groups", "lon"), None, None),
            P(None, ("groups", "lon"), None, None),
            P("groups", None, None),
            P("groups"),
            P("groups"),
            P("groups"),
            P("groups", None),
            P("groups"),
            P("groups", None),
            P("groups"),
            P("groups"),
        ),
        check_vma=False,
    )
```

profile of v0, /device:TPU:0, one launch (start us, length us, event | category | flops | bytes accessed | tf_op | source)
XLA Modules:
  0.0 199.0 jit_solution(578861992452421414)
XLA Ops:
  7.3 1.0 slice.681
  8.3 0.5 collective-permute-start
  8.8 0.9 collective-permute-done
  9.7 2.8 %collective-permute-start.1 = (bf16[4,8,3,256]{3,2,1,0:T(4,128)(2,1)S(1)}, bf16[4,8,3,256]{3,2,1,0:T(4,128)(2,1)S(1)}, u32[]{:S(2)}, u32[]{:S(2)}) collective-permute-start(bf16[4,8,3,256]{3,2,1,0:T(4,128)(2,1)S(1)} %collective-permute-done), channel_id=1, source_target_pairs={{0,2},{1,3},{2,0},{3,1},{4,6},{5,7},{6,4},{7,5},{8,10},{9,11},{10,... | collective-permute-start | bytes 147464 | tf_op jit(solution)/shard_map/ppermute | solution.py:16
  12.5 1.0 fusion.211
  13.7 1.3 collective-permute-done.1
  15.0 1.9 collective-permute-start.2
  16.9 1.0 fusion.212
  18.1 1.1 collective-permute-done.2
  19.2 3.0 %collective-permute-start.3 = (bf16[4,8,3,256]{3,2,1,0:T(4,128)(2,1)S(1)}, bf16[4,8,3,256]{3,2,1,0:T(4,128)(2,1)S(1)}, u32[]{:S(2)}, u32[]{:S(2)}) collective-permute-start(bf16[4,8,3,256]{3,2,1,0:T(4,128)(2,1)S(1)} %collective-permute-done.2), channel_id=1, source_target_pairs={{0,8},{1,9},{2,10},{3,11},{4,12},{5,13},{6,14},{7,15},{8,0},{9,1},... | collective-permute-start | bytes 147464 | tf_op jit(solution)/shard_map/ppermute | solution.py:16
  22.2 1.5 fusion.213
  23.7 0.8 copy.25
  24.7 1.3 pad_maximum_fusion.9
  26.1 4.4 %collective-permute-start.5 = (bf16[4,3,38,256]{3,2,1,0:T(8,128)(2,1)S(1)}, bf16[4,3,38,256]{3,2,1,0:T(8,128)(2,1)S(1)}, u32[]{:S(2)}, u32[]{:S(2)}) collective-permute-start(bf16[4,3,38,256]{3,2,1,0:T(8,128)(2,1)S(1)} %get-tuple-element.113), channel_id=1, source_target_pairs={{1,0},{2,1},{3,2},{4,3},{5,4},{6,5},{7,6},{8,7},{9,8},{10,9},{11,1... | collective-permute-start | bytes 700424 | tf_op jit(solution)/shard_map/ppermute | solution.py:27
  30.7 3.8 %collective-permute-done.4 = bf16[4,3,38,256]{3,2,1,0:T(8,128)(2,1)S(1)} collective-permute-done((bf16[4,3,38,256]{3,2,1,0:T(8,128)(2,1)S(1)}, bf16[4,3,38,256]{3,2,1,0:T(8,128)(2,1)S(1)}, u32[]{:S(2)}, u32[]{:S(2)}) %collective-permute-start.4) | collective-permute-done | bytes 233504 | tf_op jit(solution)/shard_map/ppermute | solution.py:26
  35.3 9.3 %fusion.207 = (f32[4,8,32]{2,1,0:T(8,128)S(1)}, f32[4,8,32,256]{3,2,1,0:T(8,128)S(1)}) fusion(bf16[4,11,38,256]{3,2,1,0:T(8,128)(2,1)S(1)} %get-tuple-element.111, f32[256]{0:T(256)} %bitcast.48, f32[256]{0:T(256)} %bitcast.47, f32[256]{0:T(256)S(1)} %bitcast.332, f32[256]{0:T(256)S(1)} %bitcast.334, f32[256]{0:T(256)S(1)} %bitcast.336, ...), kind=kLoop, calls=%fused_computation.470 | loop fusion | flops 43514880 | bytes 23746560 | tf_op jit(solution)/shard_map/reduce_sum | solution.py:62
  45.5 0.6 copy-done.1
  46.8 0.5 convolution_add_fusion.13
  47.3 0.5 convolution_add_fusion.12
  48.1 0.5 convolution_add_fusion.11
  48.9 0.5 convolution_add_fusion.10
  49.6 1.0 fusion.205
  50.6 3.1 %multiply_reduce_fusion.7 = (f32[256]{0:T(256)}, f32[256]{0:T(256)}, f32[256]{0:T(256)}, f32[256]{0:T(256)}, f32[8,32,256]{2,1,0:T(8,128)S(1)}, /*index=5*/f32[8...) fusion(f32[256]{0:T(256)S(1)} %copy-done.16, ...), kind=kLoop, calls=%fused_computation.423 | loop fusion | flops 7863296 | bytes 2497536 | tf_op jit(solution)/shard_map/reduce_sum | solution.py:117
  53.8 0.6 fusion.196
  54.4 1.5 fusion.199
  56.2 0.9 fusion.216
  57.2 1.5 fusion.197
  58.7 1.5 fusion.201
  60.2 1.5 fusion.203
  61.7 0.9 fusion.217
  62.6 0.9 fusion.215
  63.5 0.9 fusion.214
  64.4 1.0 multiply_reduce_fusion.1
  65.4 4.0 %fusion.145 = (f32[256]{0:T(256)}, f32[256]{0:T(256)}, f32[256]{0:T(256)}, f32[256]{0:T(256)}, f32[256]{0:T(256)}, /*index=5*/f32[256]{0:T(256)}, f32[256]{0:T(2...) fusion(bf16[4,11,38,256]{3,2,1,0:T(8,128)(2,1)S(1)} %get-tuple-, ...), kind=kLoop, calls=%fused_computation.319 | loop fusion | flops 16772608 | bytes 12618752 | tf_op jit(solution)/shard_map/reduce_sum | solution.py:154
  69.4 2.4 %fusion.127 = (f32[256]{0:T(256)}, f32[256]{0:T(256)}, f32[256]{0:T(256)}, f32[256]{0:T(256)}, f32[256]{0:T(256)}, /*index=5*/f32[256]{0:T(256)}, f32[256]{0:T(2...) fusion(f32[4,8,32,256]{3,2,1,0:T(8,128)S(1)} %get-tuple-element.100, ...), kind=kLoop, calls=%fused_computation.301 | loop fusion | flops 12842240 | bytes 3255296 | tf_op jit(solution)/shard_map/reduce_sum | solution.py:154
  71.7 2.5 %fusion.94 = (f32[256]{0:T(256)S(1)}, f32[256]{0:T(256)S(1)}, f32[256]{0:T(256)S(1)}, f32[256]{0:T(256)S(1)}, f32[256]{0:T(256)S(1)}, /*index=5*/f32[256]{0:T(25...) fusion(f32[4,8,32,256]{3,2,1,0:T(8,128)S(1)} %get-tuple-element, ...), kind=kLoop, calls=%fused_computation.268 | loop fusion | flops 14151168 | bytes 10504192 | tf_op jit(solution)/shard_map/reduce_sum | solution.py:154
  74.7 1.0 fusion.209
  75.7 0.6 convolution_add_fusion.2
  76.3 0.6 convolution_add_fusion.1
  76.8 1.6 convolution_add_fusion
  79.0 1.3 convolution_add_fusion.3
  80.7 1.7 collective-permute-start.6
  82.4 2.9 %collective-permute-start.7 = (f32[4,3,32,256]{3,2,1,0:T(8,128)}, f32[4,3,32,256]{3,2,1,0:T(8,128)}, u32[]{:S(2)}, u32[]{:S(2)}) collective-permute-start(f32[4,3,32,256]{3,2,1,0:T(8,128)} %get-tuple-element.109), channel_id=1, source_target_pairs={{1,0},{2,1},{3,2},{4,3},{5,4},{6,5},{7,6},{8,7},{9,8},{10,9},{11,1... | collective-permute-start | bytes 1179656 | tf_op jit(solution)/shard_map/ppermute | solution.py:27
  85.8 0.7 add_add_fusion.1
  86.5 0.7 add_add_fusion
  87.6 3.4 %collective-permute-done.6 = f32[4,3,32,256]{3,2,1,0:T(8,128)S(1)} collective-permute-done((f32[4,3,32,256]{3,2,1,0:T(8,128)}, f32[4,3,32,256]{3,2,1,0:T(8,128)S(1)}, u32[]{:S(2)}, u32[]{:S(2)}) %collective-permute-start.6) | collective-permute-done | bytes 393248 | tf_op jit(solution)/shard_map/ppermute | solution.py:26
  91.0 1.6 collective-permute-done.7
  92.6 1.4 select_maximum_fusion
  94.4 10.0 %fusion.1 = f32[4,8,38,256]{3,2,1,0:T(8,128)S(1)} fusion(f32[4,14,44,256]{3,2,1,0:T(8,128)S(1)} %select_maximum_fusion, f32[256]{0:T(256)} %bitcast.48, f32[256]{0:T(256)} %bitcast.47, f32[256]{0:T(256)S(1)} %bitcast.333, f32[256]{0:T(256)S(1)} %bitcast.335, f32[256]{0:T(256)S(1)} %bitcast.337, f32[256]{0:T(256)S(1)} %bitcast.339, f32[256]{0:T(256)S(1)} %bitcast.341, ...), kind=kLoop, calls=%fused_computation.123 | loop fusion | flops 30195712 | bytes 62309376 | tf_op jit(solution)/shard_map/add | solution.py:221
  105.3 64.4 %all-reduce.1 = (f32[7,7,256]{2,1,0:T(8,128)S(1)}, f32[256]{0:T(256)S(1)}, f32[256]{0:T(256)S(1)}, f32[256]{0:T(256)S(1)}, f32[1024]{0:T(1024)S(1)}, /*index=5*/f32[256]{0:T(256)S(1)}, f32[256]{0:T(256)S(1)}) all-reduce(f32[7,7,256]{2,1,0:T(8,128)S(1)} %copy-done.12, ...), channel_id=1, replica_groups=mesh['groups'=2,'lon'=16] {'lon'}, use_global_device_ids=true, to_apply=%region_53.54 | all-reduce | flops 14848 | bytes 118784 | tf_op jit(solution)/shard_map/psum | solution.py:246
  169.7 0.6 broadcast_multiply_fusion.2
  170.3 0.6 broadcast_multiply_fusion.6
  170.9 0.6 broadcast_multiply_fusion.10
  171.4 0.6 broadcast_multiply_fusion.11
  172.0 0.7 collective-permute-done.8
  172.7 0.6 broadcast_multiply_fusion.7
  173.3 3.7 %collective-permute-done.9 = bf16[4,8,3,256]{3,2,1,0:T(4,128)(2,1)S(1)} collective-permute-done((bf16[4,8,3,256]{3,2,1,0:T(4,128)(2,1)S(1)}, bf16[4,8,3,256]{3,2,1,0:T(4,128)(2,1)S(1)}, u32[]{:S(2)}, u32[]{:S(2)}) %collective-permute-start.9) | collective-permute-done | bytes 49184 | tf_op jit(solution)/shard_map/ppermute | solution.py:16
  177.0 0.6 broadcast_multiply_fusion.8
  177.5 4.2 %collective-permute-done.10 = bf16[4,8,3,256]{3,2,1,0:T(4,128)(2,1)S(1)} collective-permute-done((bf16[4,8,3,256]{3,2,1,0:T(4,128)(2,1)S(1)}, bf16[4,8,3,256]{3,2,1,0:T(4,128)(2,1)S(1)}, u32[]{:S(2)}, u32[]{:S(2)}) %collective-permute-start.10) | collective-permute-done | bytes 49184 | tf_op jit(solution)/shard_map/ppermute | solution.py:16
  181.7 0.6 broadcast_multiply_fusion.9
  182.4 5.2 %collective-permute-done.11 = bf16[4,8,3,256]{3,2,1,0:T(4,128)(2,1)S(1)} collective-permute-done((bf16[4,8,3,256]{3,2,1,0:T(4,128)(2,1)S(1)}, bf16[4,8,3,256]{3,2,1,0:T(4,128)(2,1)S(1)}, u32[]{:S(2)}, u32[]{:S(2)}) %collective-permute-start.11) | collective-permute-done | bytes 49184 | tf_op jit(solution)/shard_map/ppermute | solution.py:16
  187.8 0.9 pad_maximum_fusion.6
  188.7 2.4 %broadcast_multiply_fusion = f32[1024,256]{1,0:T(8,128)} fusion(f32[1024,256]{1,0:T(8,128)} %get-tuple-element.87), kind=kLoop, calls=%fused_computation.386 | loop fusion | flops 262144 | bytes 2097152 | tf_op jit(solution)/shard_map/mul | solution.py:271
  191.1 1.1 broadcast_multiply_fusion.1
  (307 shorter events, 6.5 us)
Async XLA Ops:
  7.2 39.6 %copy-start = (bf16[1024,256]{1,0:T(8,128)(2,1)S(1)}, bf16[1024,256]{1,0:T(8,128)(2,1)}, u32[]{:S(2)}) copy-start(bf16[1024,256]{1,0:T(8,128)(2,1)} %param.23) | copy-start | bytes 1572868
  7.2 27.3 %copy-start.2 = (bf16[4,8,32,256]{3,2,1,0:T(8,128)(2,1)S(1)}, bf16[4,8,32,256]{3,2,1,0:T(8,128)(2,1)}, u32[]{:S(2)}) copy-start(bf16[4,8,32,256]{3,2,1,0:T(8,128)(2,1)} %param.13) | copy-start | bytes 1572868
  7.2 23.3 %copy-start.14 = (s32[8,32]{1,0:T(8,128)S(1)}, s32[8,32]{1,0:T(8,128)}, u32[]{:S(2)}) copy-start(s32[8,32]{1,0:T(8,128)} %param.16) | copy-start | bytes 3076
  7.2 181.5 %all-reduce.5.cloned.1.call-start = ((), (), s32[]{:S(2)}) async-start(), calls=%async_computation | async-start | bytes 4194304 | tf_op jit(solution)/shard_map/psum | solution.py:246
  8.3 1.4 collective-permute-start
  9.7 5.3 %collective-permute-start.1 = (bf16[4,8,3,256]{3,2,1,0:T(4,128)(2,1)S(1)}, bf16[4,8,3,256]{3,2,1,0:T(4,128)(2,1)S(1)}, u32[]{:S(2)}, u32[]{:S(2)}) collective-permute-start(bf16[4,8,3,256]{3,2,1,0:T(4,128)(2,1)S(1)} %collective-permute-done), channel_id=1, source_target_pairs={{0,2},{1,3},{2,0},{3,1},{4,6},{5,7},{6,4},{7,5},{8,10},{9,11},{10,... | collective-permute-start | bytes 147464 | tf_op jit(solution)/shard_map/ppermute | solution.py:16
  13.5 21.4 %copy-start.17 = (f32[1,1,256]{2,1,0:T(1,128)}, f32[1,1,256]{2,1,0:T(1,128)S(1)}, u32[]{:S(2)}) copy-start(f32[1,1,256]{2,1,0:T(1,128)S(1)} %get-tuple-element.121) | copy-start | bytes 3076
  13.5 21.4 %copy-start.19 = (f32[1,1,256]{2,1,0:T(1,128)}, f32[1,1,256]{2,1,0:T(1,128)S(1)}, u32[]{:S(2)}) copy-start(f32[1,1,256]{2,1,0:T(1,128)S(1)} %get-tuple-element.122) | copy-start | bytes 3076
  13.6 21.4 %copy-start.21 = (f32[1,1,256]{2,1,0:T(1,128)}, f32[1,1,256]{2,1,0:T(1,128)S(1)}, u32[]{:S(2)}) copy-start(f32[1,1,256]{2,1,0:T(1,128)S(1)} %get-tuple-element.123) | copy-start | bytes 3076
  13.6 21.4 %copy-start.23 = (f32[1,1,256]{2,1,0:T(1,128)}, f32[1,1,256]{2,1,0:T(1,128)S(1)}, u32[]{:S(2)}) copy-start(f32[1,1,256]{2,1,0:T(1,128)S(1)} %get-tuple-element.124) | copy-start | bytes 3076
  13.6 21.4 %copy-start.25 = (f32[1,1,256]{2,1,0:T(1,128)}, f32[1,1,256]{2,1,0:T(1,128)S(1)}, u32[]{:S(2)}) copy-start(f32[1,1,256]{2,1,0:T(1,128)S(1)} %get-tuple-element.125) | copy-start | bytes 3076
  13.6 21.4 %copy-start.27 = (f32[1,1,256]{2,1,0:T(1,128)}, f32[1,1,256]{2,1,0:T(1,128)S(1)}, u32[]{:S(2)}) copy-start(f32[1,1,256]{2,1,0:T(1,128)S(1)} %get-tuple-element.126) | copy-start | bytes 3076
  13.6 21.4 %copy-start.29 = (f32[1,1,256]{2,1,0:T(1,128)}, f32[1,1,256]{2,1,0:T(1,128)S(1)}, u32[]{:S(2)}) copy-start(f32[1,1,256]{2,1,0:T(1,128)S(1)} %get-tuple-element.127) | copy-start | bytes 3076
  13.6 21.4 %copy-start.31 = (f32[1,1,256]{2,1,0:T(1,128)}, f32[1,1,256]{2,1,0:T(1,128)S(1)}, u32[]{:S(2)}) copy-start(f32[1,1,256]{2,1,0:T(1,128)S(1)} %get-tuple-element.128) | copy-start | bytes 3076
  13.6 21.4 %copy-start.33 = (f32[1,1,256]{2,1,0:T(1,128)}, f32[1,1,256]{2,1,0:T(1,128)S(1)}, u32[]{:S(2)}) copy-start(f32[1,1,256]{2,1,0:T(1,128)S(1)} %get-tuple-element.129) | copy-start | bytes 3076
  13.6 21.4 %copy-start.35 = (f32[1,1,256]{2,1,0:T(1,128)}, f32[1,1,256]{2,1,0:T(1,128)S(1)}, u32[]{:S(2)}) copy-start(f32[1,1,256]{2,1,0:T(1,128)S(1)} %get-tuple-element.130) | copy-start | bytes 3076
  13.6 21.4 %copy-start.37 = (f32[1,1,256]{2,1,0:T(1,128)}, f32[1,1,256]{2,1,0:T(1,128)S(1)}, u32[]{:S(2)}) copy-start(f32[1,1,256]{2,1,0:T(1,128)S(1)} %get-tuple-element.131) | copy-start | bytes 3076
  13.6 21.4 %copy-start.39 = (f32[1,1,256]{2,1,0:T(1,128)}, f32[1,1,256]{2,1,0:T(1,128)S(1)}, u32[]{:S(2)}) copy-start(f32[1,1,256]{2,1,0:T(1,128)S(1)} %get-tuple-element.132) | copy-start | bytes 3076
  13.7 21.4 %copy-start.41 = (f32[1,1,256]{2,1,0:T(1,128)}, f32[1,1,256]{2,1,0:T(1,128)S(1)}, u32[]{:S(2)}) copy-start(f32[1,1,256]{2,1,0:T(1,128)S(1)} %get-tuple-element.133) | copy-start | bytes 3076
  13.7 21.4 %copy-start.43 = (f32[1,1,256]{2,1,0:T(1,128)}, f32[1,1,256]{2,1,0:T(1,128)S(1)}, u32[]{:S(2)}) copy-start(f32[1,1,256]{2,1,0:T(1,128)S(1)} %get-tuple-element.134) | copy-start | bytes 3076
  13.7 21.4 %copy-start.45 = (f32[1,1,256]{2,1,0:T(1,128)}, f32[1,1,256]{2,1,0:T(1,128)S(1)}, u32[]{:S(2)}) copy-start(f32[1,1,256]{2,1,0:T(1,128)S(1)} %get-tuple-element.135) | copy-start | bytes 3076
  13.7 21.4 %copy-start.47 = (f32[1,1,256]{2,1,0:T(1,128)}, f32[1,1,256]{2,1,0:T(1,128)S(1)}, u32[]{:S(2)}) copy-start(f32[1,1,256]{2,1,0:T(1,128)S(1)} %get-tuple-element.136) | copy-start | bytes 3076
  15.0 4.3 %collective-permute-start.2 = (bf16[4,8,3,256]{3,2,1,0:T(4,128)(2,1)S(1)}, bf16[4,8,3,256]{3,2,1,0:T(4,128)(2,1)S(1)}, u32[]{:S(2)}, u32[]{:S(2)}) collective-permute-start(bf16[4,8,3,256]{3,2,1,0:T(4,128)(2,1)S(1)} %collective-permute-done.1), channel_id=1, source_target_pairs={{0,4},{1,5},{2,6},{3,7},{4,0},{5,1},{6,2},{7,3},{8,12},{9,13},{10,... | collective-permute-start | bytes 147464 | tf_op jit(solution)/shard_map/ppermute | solution.py:16
  17.9 17.1 %copy-start.49 = (f32[1,1,256]{2,1,0:T(1,128)}, f32[1,1,256]{2,1,0:T(1,128)S(1)}, u32[]{:S(2)}) copy-start(f32[1,1,256]{2,1,0:T(1,128)S(1)} %get-tuple-element.137) | copy-start | bytes 3076
  17.9 17.1 %copy-start.51 = (f32[1,1,256]{2,1,0:T(1,128)}, f32[1,1,256]{2,1,0:T(1,128)S(1)}, u32[]{:S(2)}) copy-start(f32[1,1,256]{2,1,0:T(1,128)S(1)} %get-tuple-element.138) | copy-start | bytes 3076
  17.9 17.1 %copy-start.53 = (f32[1,1,256]{2,1,0:T(1,128)}, f32[1,1,256]{2,1,0:T(1,128)S(1)}, u32[]{:S(2)}) copy-start(f32[1,1,256]{2,1,0:T(1,128)S(1)} %get-tuple-element.139) | copy-start | bytes 3076
  17.9 17.1 %copy-start.55 = (f32[1,1,256]{2,1,0:T(1,128)}, f32[1,1,256]{2,1,0:T(1,128)S(1)}, u32[]{:S(2)}) copy-start(f32[1,1,256]{2,1,0:T(1,128)S(1)} %get-tuple-element.140) | copy-start | bytes 3076
  18.0 17.1 %copy-start.57 = (f32[1,1,256]{2,1,0:T(1,128)}, f32[1,1,256]{2,1,0:T(1,128)S(1)}, u32[]{:S(2)}) copy-start(f32[1,1,256]{2,1,0:T(1,128)S(1)} %get-tuple-element.141) | copy-start | bytes 3076
  18.0 17.1 %copy-start.59 = (f32[1,1,256]{2,1,0:T(1,128)}, f32[1,1,256]{2,1,0:T(1,128)S(1)}, u32[]{:S(2)}) copy-start(f32[1,1,256]{2,1,0:T(1,128)S(1)} %get-tuple-element.142) | copy-start | bytes 3076
  18.0 17.1 %copy-start.61 = (f32[1,1,256]{2,1,0:T(1,128)}, f32[1,1,256]{2,1,0:T(1,128)S(1)}, u32[]{:S(2)}) copy-start(f32[1,1,256]{2,1,0:T(1,128)S(1)} %get-tuple-element.143) | copy-start | bytes 3076
  18.0 17.1 %copy-start.63 = (f32[1,1,256]{2,1,0:T(1,128)}, f32[1,1,256]{2,1,0:T(1,128)S(1)}, u32[]{:S(2)}) copy-start(f32[1,1,256]{2,1,0:T(1,128)S(1)} %get-tuple-element.144) | copy-start | bytes 3076
  18.0 17.1 %copy-start.65 = (f32[1,1,256]{2,1,0:T(1,128)}, f32[1,1,256]{2,1,0:T(1,128)S(1)}, u32[]{:S(2)}) copy-start(f32[1,1,256]{2,1,0:T(1,128)S(1)} %get-tuple-element.145) | copy-start | bytes 3076
  18.0 17.1 %copy-start.67 = (f32[1,1,256]{2,1,0:T(1,128)}, f32[1,1,256]{2,1,0:T(1,128)S(1)}, u32[]{:S(2)}) copy-start(f32[1,1,256]{2,1,0:T(1,128)S(1)} %get-tuple-element.146) | copy-start | bytes 3076
  18.0 17.1 %copy-start.69 = (f32[1,1,256]{2,1,0:T(1,128)}, f32[1,1,256]{2,1,0:T(1,128)S(1)}, u32[]{:S(2)}) copy-start(f32[1,1,256]{2,1,0:T(1,128)S(1)} %get-tuple-element.147) | copy-start | bytes 3076
  18.0 17.1 %copy-start.71 = (f32[1,1,256]{2,1,0:T(1,128)}, f32[1,1,256]{2,1,0:T(1,128)S(1)}, u32[]{:S(2)}) copy-start(f32[1,1,256]{2,1,0:T(1,128)S(1)} %get-tuple-element.148) | copy-start | bytes 3076
  18.0 17.1 %copy-start.73 = (f32[1,1,256]{2,1,0:T(1,128)}, f32[1,1,256]{2,1,0:T(1,128)S(1)}, u32[]{:S(2)}) copy-start(f32[1,1,256]{2,1,0:T(1,128)S(1)} %get-tuple-element.149) | copy-start | bytes 3076
  18.1 17.1 %copy-start.75 = (f32[1,1,256]{2,1,0:T(1,128)}, f32[1,1,256]{2,1,0:T(1,128)S(1)}, u32[]{:S(2)}) copy-start(f32[1,1,256]{2,1,0:T(1,128)S(1)} %get-tuple-element.150) | copy-start | bytes 3076
  18.1 17.1 %copy-start.77 = (f32[1,1,256]{2,1,0:T(1,128)}, f32[1,1,256]{2,1,0:T(1,128)S(1)}, u32[]{:S(2)}) copy-start(f32[1,1,256]{2,1,0:T(1,128)S(1)} %get-tuple-element.151) | copy-start | bytes 3076
  18.1 17.1 %copy-start.79 = (f32[1,1,256]{2,1,0:T(1,128)}, f32[1,1,256]{2,1,0:T(1,128)S(1)}, u32[]{:S(2)}) copy-start(f32[1,1,256]{2,1,0:T(1,128)S(1)} %get-tuple-element.152) | copy-start | bytes 3076
  18.1 17.1 %copy-start.81 = (f32[1,1,256]{2,1,0:T(1,128)}, f32[1,1,256]{2,1,0:T(1,128)S(1)}, u32[]{:S(2)}) copy-start(f32[1,1,256]{2,1,0:T(1,128)S(1)} %get-tuple-element.153) | copy-start | bytes 3076
  18.1 17.1 %copy-start.83 = (f32[1,1,256]{2,1,0:T(1,128)}, f32[1,1,256]{2,1,0:T(1,128)S(1)}, u32[]{:S(2)}) copy-start(f32[1,1,256]{2,1,0:T(1,128)S(1)} %get-tuple-element.154) | copy-start | bytes 3076
  18.1 17.1 %copy-start.85 = (f32[1,1,256]{2,1,0:T(1,128)}, f32[1,1,256]{2,1,0:T(1,128)S(1)}, u32[]{:S(2)}) copy-start(f32[1,1,256]{2,1,0:T(1,128)S(1)} %get-tuple-element.155) | copy-start | bytes 3076
  19.2 5.3 %collective-permute-start.3 = (bf16[4,8,3,256]{3,2,1,0:T(4,128)(2,1)S(1)}, bf16[4,8,3,256]{3,2,1,0:T(4,128)(2,1)S(1)}, u32[]{:S(2)}, u32[]{:S(2)}) collective-permute-start(bf16[4,8,3,256]{3,2,1,0:T(4,128)(2,1)S(1)} %collective-permute-done.2), channel_id=1, source_target_pairs={{0,8},{1,9},{2,10},{3,11},{4,12},{5,13},{6,14},{7,15},{8,0},{9,1},... | collective-permute-start | bytes 147464 | tf_op jit(solution)/shard_map/ppermute | solution.py:16
  23.7 11.6 %copy-start.87 = (f32[1,1,256]{2,1,0:T(1,128)}, f32[1,1,256]{2,1,0:T(1,128)S(1)}, u32[]{:S(2)}) copy-start(f32[1,1,256]{2,1,0:T(1,128)S(1)} %get-tuple-element.156) | copy-start | bytes 3076
  23.7 11.6 %copy-start.89 = (f32[1,1,256]{2,1,0:T(1,128)}, f32[1,1,256]{2,1,0:T(1,128)S(1)}, u32[]{:S(2)}) copy-start(f32[1,1,256]{2,1,0:T(1,128)S(1)} %get-tuple-element.157) | copy-start | bytes 3076
  23.7 11.6 %copy-start.91 = (f32[1,1,256]{2,1,0:T(1,128)}, f32[1,1,256]{2,1,0:T(1,128)S(1)}, u32[]{:S(2)}) copy-start(f32[1,1,256]{2,1,0:T(1,128)S(1)} %get-tuple-element.159) | copy-start | bytes 3076
  23.7 11.6 %copy-start.92 = (f32[1,1,256]{2,1,0:T(1,128)}, f32[1,1,256]{2,1,0:T(1,128)S(1)}, u32[]{:S(2)}) copy-start(f32[1,1,256]{2,1,0:T(1,128)S(1)} %get-tuple-element.160) | copy-start | bytes 3076
  26.0 8.5 %collective-permute-start.4 = (bf16[4,3,38,256]{3,2,1,0:T(8,128)(2,1)S(1)}, bf16[4,3,38,256]{3,2,1,0:T(8,128)(2,1)S(1)}, u32[]{:S(2)}, u32[]{:S(2)}) collective-permute-start(bf16[4,3,38,256]{3,2,1,0:T(8,128)(2,1)S(1)} %get-tuple-element.112), channel_id=1, source_target_pairs={{0,1},{1,2},{2,3},{3,4},{4,5},{5,6},{6,7},{7,8},{8,9},{9,10},{10,1... | collective-permute-start | bytes 700424 | tf_op jit(solution)/shard_map/ppermute | solution.py:26
  26.1 8.4 %collective-permute-start.5 = (bf16[4,3,38,256]{3,2,1,0:T(8,128)(2,1)S(1)}, bf16[4,3,38,256]{3,2,1,0:T(8,128)(2,1)S(1)}, u32[]{:S(2)}, u32[]{:S(2)}) collective-permute-start(bf16[4,3,38,256]{3,2,1,0:T(8,128)(2,1)S(1)} %get-tuple-element.113), channel_id=1, source_target_pairs={{1,0},{2,1},{3,2},{4,3},{5,4},{6,5},{7,6},{8,7},{9,8},{10,9},{11,1... | collective-permute-start | bytes 700424 | tf_op jit(solution)/shard_map/ppermute | solution.py:27
  35.3 9.8 %copy-start.15 = (f32[256]{0:T(256)S(1)}, f32[256]{0:T(256)}, u32[]{:S(2)}) copy-start(f32[256]{0:T(256)} %param.19) | copy-start | bytes 3076
  35.3 9.8 %copy-start.128 = (f32[256]{0:T(256)S(1)}, f32[256]{0:T(256)}, u32[]{:S(2)}) copy-start(f32[256]{0:T(256)} %param.20) | copy-start | bytes 3076
  80.7 10.3 %collective-permute-start.6 = (f32[4,3,32,256]{3,2,1,0:T(8,128)}, f32[4,3,32,256]{3,2,1,0:T(8,128)S(1)}, u32[]{:S(2)}, u32[]{:S(2)}) collective-permute-start(f32[4,3,32,256]{3,2,1,0:T(8,128)} %get-tuple-element.108), channel_id=1, source_target_pairs={{0,1},{1,2},{2,3},{3,4},{4,5},{5,6},{6,7},{7,8},{8,9},{9,10},{10,1... | collective-permute-start | bytes 1179656 | tf_op jit(solution)/shard_map/ppermute | solution.py:26
  82.4 10.2 %collective-permute-start.7 = (f32[4,3,32,256]{3,2,1,0:T(8,128)}, f32[4,3,32,256]{3,2,1,0:T(8,128)}, u32[]{:S(2)}, u32[]{:S(2)}) collective-permute-start(f32[4,3,32,256]{3,2,1,0:T(8,128)} %get-tuple-element.109), channel_id=1, source_target_pairs={{1,0},{2,1},{3,2},{4,3},{5,4},{6,5},{7,6},{8,7},{9,8},{10,9},{11,1... | collective-permute-start | bytes 1179656 | tf_op jit(solution)/shard_map/ppermute | solution.py:27
  85.8 6.8 %copy-start.11 = (f32[7,7,256]{2,1,0:T(8,128)}, f32[7,7,256]{2,1,0:T(8,128)S(1)}, u32[]{:S(2)}) copy-start(f32[7,7,256]{2,1,0:T(8,128)S(1)} %constant_dynamic-update-slice_fusion) | copy-start | bytes 150532
  87.3 6.8 %copy-start.24 = (f32[1,1,256]{2,1,0:T(1,128)S(1)}, f32[1,1,256]{2,1,0:T(1,128)}, u32[]{:S(2)}) copy-start(f32[1,1,256]{2,1,0:T(1,128)} %copy-done.23) | copy-start | bytes 3076
  87.3 6.8 %copy-start.26 = (f32[1,1,256]{2,1,0:T(1,128)S(1)}, f32[1,1,256]{2,1,0:T(1,128)}, u32[]{:S(2)}) copy-start(f32[1,1,256]{2,1,0:T(1,128)} %copy-done.25) | copy-start | bytes 3076
  87.3 6.8 %copy-start.28 = (f32[1,1,256]{2,1,0:T(1,128)S(1)}, f32[1,1,256]{2,1,0:T(1,128)}, u32[]{:S(2)}) copy-start(f32[1,1,256]{2,1,0:T(1,128)} %copy-done.27) | copy-start | bytes 3076
  94.3 10.1 %copy-start.4 = (f32[256,256]{1,0:T(8,128)S(1)}, f32[256,256]{1,0:T(8,128)}, u32[]{:S(2)}) copy-start(f32[256,256]{1,0:T(8,128)} %copy-done.3) | copy-start | bytes 786436
  94.4 10.1 %copy-start.6 = (f32[256,256]{1,0:T(8,128)S(1)}, f32[256,256]{1,0:T(8,128)}, u32[]{:S(2)}) copy-start(f32[256,256]{1,0:T(8,128)} %copy-done.5) | copy-start | bytes 786436
  94.4 10.1 %copy-start.8 = (f32[256,256]{1,0:T(8,128)S(1)}, f32[256,256]{1,0:T(8,128)}, u32[]{:S(2)}) copy-start(f32[256,256]{1,0:T(8,128)} %copy-done.7) | copy-start | bytes 786436
  171.4 1.3 collective-permute-start.8
  172.7 4.3 %collective-permute-start.9 = (bf16[4,8,3,256]{3,2,1,0:T(4,128)(2,1)S(1)}, bf16[4,8,3,256]{3,2,1,0:T(4,128)(2,1)S(1)}, u32[]{:S(2)}, u32[]{:S(2)}) collective-permute-start(bf16[4,8,3,256]{3,2,1,0:T(4,128)(2,1)S(1)} %collective-permute-done.8), channel_id=1, source_target_pairs={{0,2},{1,3},{2,0},{3,1},{4,6},{5,7},{6,4},{7,5},{8,10},{9,11},{10,... | collective-permute-start | bytes 147464 | tf_op jit(solution)/shard_map/ppermute | solution.py:16
  177.0 4.8 %collective-permute-start.10 = (bf16[4,8,3,256]{3,2,1,0:T(4,128)(2,1)S(1)}, bf16[4,8,3,256]{3,2,1,0:T(4,128)(2,1)S(1)}, u32[]{:S(2)}, u32[]{:S(2)}) collective-permute-start(bf16[4,8,3,256]{3,2,1,0:T(4,128)(2,1)S(1)} %collective-permute-done.9), channel_id=1, source_target_pairs={{0,4},{1,5},{2,6},{3,7},{4,0},{5,1},{6,2},{7,3},{8,12},{9,13},{10,... | collective-permute-start | bytes 147464 | tf_op jit(solution)/shard_map/ppermute | solution.py:16
  181.7 5.9 %collective-permute-start.11 = (bf16[4,8,3,256]{3,2,1,0:T(4,128)(2,1)S(1)}, bf16[4,8,3,256]{3,2,1,0:T(4,128)(2,1)S(1)}, u32[]{:S(2)}, u32[]{:S(2)}) collective-permute-start(bf16[4,8,3,256]{3,2,1,0:T(4,128)(2,1)S(1)} %collective-permute-done.10), channel_id=1, source_target_pairs={{0,8},{1,9},{2,10},{3,11},{4,12},{5,13},{6,14},{7,15},{8,0},{9,1},... | collective-permute-start | bytes 147464 | tf_op jit(solution)/shard_map/ppermute | solution.py:16
  (79 other events, 410.1 us)
Sparse Core Ops, SparseCore 0:
  85.4 98.8 all-reduce.4
where the time goes:
time: 200 us; the launch traced here: 199 us
  blocking collectives  64.4 us (32%)
  other arithmetic  48 us (24%)
  waiting for transfers between devices  25.9 us (13%)
  matrix products  18.3 us (9%)
  starting transfers between devices  17.3 us (9%)
  between operations  16.2 us (8%)
  local copies, waits for them, and re-layouts  8.82 us (4%)
    psum x1, blocking collectives, on_device(): lax.psum((kernel_sum, dw_bias_sum, gain_sum, bias_sum, w_in_sum, b_in_sum...  64.4 us
    ppermute x8, waiting for transfers between devices, swapped(): lax.ppermute(x, axis, [(i, i ^ 1 << bit) for i in range(lax.axis_size(axi...  17.1 us
    add x1, other arithmetic, on_device(): grad_ext + dw_kernel[lon_off, lat_off] * padded[:, 6 - lon_off:6 - lon_of...  10 us
    reduce_sum x4, other arithmetic, local_step(): jnp.sum(grad_depth * extended[:, lon_off:lon_off + lon_dev, lat_off:lat_o...  9.35 us
    reduce_sum x1, other arithmetic, local_step(): mean_val = jnp.mean(depth, axis=-1, keepdims=True)  9.33 us
    ppermute x8, starting transfers between devices, swapped(): lax.ppermute(x, axis, [(i, i ^ 1 << bit) for i in range(lax.axis_size(axi...  8.26 us
    ppermute x2, starting transfers between devices, with_halo(): after = lax.ppermute(leading, axis, down)  7.3 us
    ppermute x2, waiting for transfers between devices, with_halo(): before = lax.ppermute(last, axis, up)  7.21 us
  transfers between devices with their start and end apart: 13, of which 10 were waited for; matrix products, arithmetic and copies ran while one was open for 12% of the time, Pallas kernels for 0%

commit v1 on v0

--- a/solution.py
+++ b/solution.py
@@ -175,18 +175,57 @@
     return (pred.astype(jnp.bfloat16), crps_field, grad_pred, grad_depth, grads)
 
 
+def mirrored(x, axis):
+    size = lax.axis_size(axis)
+    return lax.ppermute(x, axis, [(i, size - 1 - i) for i in range(size)])
+
+
 def mirror_rows(top_rows):
-    picked = top_rows
-    for bit_index in range(lax.axis_size("lon").bit_length() - 1):
-        picked = swapped(picked, "lon", bit_index)
+    return mirrored(top_rows, "lon")[:, ::-1, ::-1, :]
+
+
+def mirror_grads(fold_rows):
+    picked = mirrored(fold_rows.astype(jnp.bfloat16), "lon").astype(fold_rows.dtype)
     return picked[:, ::-1, ::-1, :]
 
 
-def mirror_grads(fold_rows):
-    picked = fold_rows
-    for bit_index in range(lax.axis_size("lon").bit_length() - 1):
-        picked = swapped(picked.astype(jnp.bfloat16), "lon", bit_index).astype(picked.dtype)
-    return picked[:, ::-1, ::-1, :]
+def halving_allreduce(flat, axis, gather_dtype):
+    size = lax.axis_size(axis)
+    bits = size.bit_length() - 1
+    idx = lax.axis_index(axis)
+    cur = flat
+    for bit in range(bits):
+        half = cur.shape[0] // 2
+        mine = (idx >> bit) & 1
+        keep = lax.dynamic_slice_in_dim(cur, mine * half, half)
+        send = lax.dynamic_slice_in_dim(cur, (1 - mine) * half, half)
+        cur = keep + swapped(send, axis, bit)
+    cur = cur.astype(gather_dtype)
+    for bit in reversed(range(bits)):
+        mine = (idx >> bit) & 1
+        recv = swapped(cur, axis, bit)
+        cur = jnp.where(mine == 0, jnp.concatenate([cur, recv]), jnp.concatenate([recv, cur]))
+    return cur.astype(flat.dtype)
+
+
+def butterfly_allreduce(flat, axis):
+    for bit in range(lax.axis_size(axis).bit_length() - 1):
+        flat = flat + swapped(flat, axis, bit)
+    return flat
+
+
+def pack(arrays, multiple):
+    flat = jnp.concatenate([a.reshape(-1) for a in arrays])
+    extra = -flat.shape[0] % multiple
+    return jnp.pad(flat, (0, extra))
+
+
+def unpack(flat, arrays):
+    out, at = [], 0
+    for a in arrays:
+        out.append(flat[at : at + a.size].reshape(a.shape))
+        at += a.size
+    return out
 
 
 def on_device(
@@ -243,19 +282,23 @@
         b_out_sum,
         scale_sum,
     ) = grads
-    totals = lax.psum(
-        (
-            kernel_sum,
-            dw_bias_sum,
-            gain_sum,
-            bias_sum,
-            w_in_sum,
-            b_in_sum,
-            w_out_sum,
-            b_out_sum,
-            scale_sum,
-        ),
-        "lon",
+    lon_size = lax.axis_size("lon")
+    big = (w_in_sum, w_out_sum, b_in_sum, b_out_sum, scale_sum, gain_sum, bias_sum)
+    big_tot = unpack(
+        halving_allreduce(pack(big, lon_size * 1024), "lon", jnp.bfloat16), big
+    )
+    small = (kernel_sum, dw_bias_sum)
+    small_tot = unpack(butterfly_allreduce(pack(small, 128), "lon"), small)
+    totals = (
+        small_tot[0],
+        small_tot[1],
+        big_tot[5],
+        big_tot[6],
+        big_tot[0],
+        big_tot[2],
+        big_tot[1],
+        big_tot[3],
+        big_tot[4],
     )
     factor = 1.0 / math.sqrt(members * lat_rows * lon_dev * lax.axis_size("lon"))
     return (

time: 200 us -> 171 us (0.85)
  blocking collectives: 64.4 us -> 0 us
  waiting for transfers between devices: 25.9 us -> 47.2 us
  local copies, waits for them, and re-layouts: 8.82 us -> 23.3 us
  between operations: 16.2 us -> 3.01 us
  other arithmetic: 48 us -> 55.8 us
  starting transfers between devices: 17.3 us -> 24.7 us
  matrix products: 18.3 us -> 16.3 us
    psum x1 -> x0, blocking collectives: 64.4 us -> none  [on_device(): lax.psum((kernel_sum, dw_bias_sum, gain_sum, bias_sum, w_in_sum, b_in_sum...]
    ppermute x8 -> x12, waiting for transfers between devices: 17.1 us -> 42.5 us  [swapped(): lax.ppermute(x, axis, [(i, i ^ 1 << bit) for i in range(lax.axis_size(axi...]
    unnamed x267 -> x283, local copies, waits for them, and re-layouts: 2.63 us -> 11.3 us
    ppermute x0 -> x2, starting transfers between devices: none -> 5.55 us  [mirrored(): return lax.ppermute(x, axis, [(i, size - 1 - i) for i in range(size)])]
    add x2 -> x7, other arithmetic: 1.42 us -> 4.3 us  [the longest x3 3.45 us: halving_allreduce(): cur = keep + swapped(send, axis, bit)]
    ppermute x2, waiting for transfers between devices: 7.21 us -> 4.66 us  [with_halo(): before = lax.ppermute(last, axis, up)]
    dynamic_slice x0 -> x4, local copies, waits for them, and re-layouts: none -> 2.08 us  [halving_allreduce(): send = lax.dynamic_slice_in_dim(cur, (1 - mine) * half, half)]
    ppermute x8 -> x12, starting transfers between devices: 8.26 us -> 10.2 us  [swapped(): lax.ppermute(x, axis, [(i, i ^ 1 << bit) for i in range(lax.axis_size(axi...]
  transfers between devices with their start and end apart: 13 -> 18, of which waited for: 10 -> 10; matrix products, arithmetic and copies ran while one was open for 12% -> 13% of each run, Pallas kernels for 0% -> 0%
where the time goes in v1:
time: 171 us; the launch traced here: 170 us
  other arithmetic  55.8 us (33%)
  waiting for transfers between devices  47.2 us (28%)
  starting transfers between devices  24.7 us (14%)
  local copies, waits for them, and re-layouts  23.3 us (14%)
  matrix products  16.3 us (10%)
  between operations  3.01 us (2%)
    ppermute x12, waiting for transfers between devices, swapped(): lax.ppermute(x, axis, [(i, i ^ 1 << bit) for i in range(lax.axis_size(axi...  42.5 us
    unnamed x283, local copies, waits for them, and re-layouts  11.3 us
    add x1, other arithmetic, on_device(): grad_ext + dw_kernel[lon_off, lat_off] * padded[:, 6 - lon_off:6 - lon_of...  10.3 us
    ppermute x12, starting transfers between devices, swapped(): lax.ppermute(x, axis, [(i, i ^ 1 << bit) for i in range(lax.axis_size(axi...  10.2 us
    reduce_sum x4, other arithmetic, local_step(): jnp.sum(grad_depth * extended[:, lon_off:lon_off + lon_dev, lat_off:lat_o...  9.35 us
    reduce_sum x1, other arithmetic, local_step(): mean_val = jnp.mean(depth, axis=-1, keepdims=True)  9.25 us
    ppermute x2, starting transfers between devices, with_halo(): after = lax.ppermute(leading, axis, down)  7.65 us
    dot_general x4, matrix products, local_step(): lax.dot_general(out_half, w_out, contract_cols, preferred_element_type=jn...  5.97 us
  transfers between devices with their start and end apart: 18, of which 10 were waited for; matrix products, arithmetic and copies ran while one was open for 13% of the time, Pallas kernels for 0%

profile of v1, /device:TPU:0, one launch (start us, length us, event | category | flops | bytes accessed | tf_op | source)
XLA Modules:
  0.0 170.3 jit_solution(15310192154007037569)
XLA Ops:
  0.7 1.0 slice.716
  1.7 5.5 %collective-permute-start = (bf16[4,8,3,256]{3,2,1,0:T(4,128)(2,1)S(1)}, bf16[4,8,3,256]{3,2,1,0:T(4,128)(2,1)S(1)}, u32[]{:S(2)}, u32[]{:S(2)}) collective-permute-start(bf16[4,8,3,256]{3,2,1,0:T(4,128)(2,1)S(1)} %slice.716), channel_id=1, source_target_pairs={{0,15},{1,14},{2,13},{3,12},{4,11},{5,10},{6,9},{7,8},{8,7},{9,6},... | collective-permute-start | bytes 147464 | tf_op jit(solution)/shard_map/ppermute | solution.py:180
  7.2 1.0 fusion.217
  8.4 1.0 fusion.218
  9.6 1.5 fusion.219
  11.1 0.8 copy.25
  12.2 1.3 pad_maximum_fusion.13
  13.5 0.7 collective-permute-start.1
  14.2 3.8 %collective-permute-start.2 = (bf16[4,3,38,256]{3,2,1,0:T(8,128)(2,1)S(1)}, bf16[4,3,38,256]{3,2,1,0:T(8,128)(2,1)S(1)}, u32[]{:S(2)}, u32[]{:S(2)}) collective-permute-start(bf16[4,3,38,256]{3,2,1,0:T(8,128)(2,1)S(1)} %get-tuple-element.108), channel_id=1, source_target_pairs={{1,0},{2,1},{3,2},{4,3},{5,4},{6,5},{7,6},{8,7},{9,8},{10,9},{11,1... | collective-permute-start | bytes 700424 | tf_op jit(solution)/shard_map/ppermute | solution.py:27
  18.5 0.8 compare_convert_fusion
  19.3 2.6 %collective-permute-done.1 = bf16[4,3,38,256]{3,2,1,0:T(8,128)(2,1)S(1)} collective-permute-done((bf16[4,3,38,256]{3,2,1,0:T(8,128)(2,1)S(1)}, bf16[4,3,38,256]{3,2,1,0:T(8,128)(2,1)S(1)}, u32[]{:S(2)}, u32[]{:S(2)}) %collective-permute-start.1) | collective-permute-done | bytes 233504 | tf_op jit(solution)/shard_map/ppermute | solution.py:26
  22.7 9.2 %fusion.213 = (f32[4,8,32]{2,1,0:T(8,128)S(1)}, f32[4,8,32,256]{3,2,1,0:T(8,128)S(1)}) fusion(bf16[4,11,38,256]{3,2,1,0:T(8,128)(2,1)S(1)} %get-tuple-element.106, f32[256]{0:T(256)} %bitcast.48, f32[256]{0:T(256)} %bitcast.47, f32[256]{0:T(256)S(1)} %bitcast.340, f32[256]{0:T(256)S(1)} %bitcast.342, f32[256]{0:T(256)S(1)} %bitcast.344, ...), kind=kLoop, calls=%fused_computation.500 | loop fusion | flops 43514880 | bytes 23746560 | tf_op jit(solution)/shard_map/reduce_sum | solution.py:62
  36.9 1.1 fusion.211
  38.0 3.8 %multiply_reduce_fusion.7 = (f32[256]{0:T(256)}, f32[256]{0:T(256)}, f32[256]{0:T(256)}, f32[256]{0:T(256)}, f32[8,32,256]{2,1,0:T(8,128)S(1)}, /*index=5*/f32[8...) fusion(f32[256]{0:T(256)S(1)} %copy-done.14, ...), kind=kLoop, calls=%fused_computation.444 | loop fusion | flops 7863296 | bytes 2497536 | tf_op jit(solution)/shard_map/reduce_sum | solution.py:117
  42.5 1.5 fusion.205
  44.3 0.9 fusion.222
  45.3 1.5 fusion.203
  46.8 1.5 fusion.207
  48.2 1.5 fusion.209
  49.7 0.9 fusion.223
  50.6 0.9 fusion.221
  51.6 0.9 fusion.220
  52.4 1.0 multiply_reduce_fusion
  53.4 4.0 %fusion.149 = (f32[256]{0:T(256)}, f32[256]{0:T(256)}, f32[256]{0:T(256)}, f32[256]{0:T(256)}, f32[256]{0:T(256)}, /*index=5*/f32[256]{0:T(256)}, f32[256]{0:T(2...) fusion(bf16[4,11,38,256]{3,2,1,0:T(8,128)(2,1)S(1)} %get-tuple-, ...), kind=kLoop, calls=%fused_computation.326 | loop fusion | flops 16772608 | bytes 12618752 | tf_op jit(solution)/shard_map/reduce_sum | solution.py:154
  57.5 0.9 fusion.215
  58.4 2.3 %fusion.131 = (f32[256]{0:T(256)}, f32[256]{0:T(256)}, f32[256]{0:T(256)}, f32[256]{0:T(256)S(1)}, f32[256]{0:T(256)}, /*index=5*/f32[256]{0:T(256)}, f32[256]{0...) fusion(f32[4,8,32,256]{3,2,1,0:T(8,128)S(1)} %get-tuple-element.91, ...), kind=kLoop, calls=%fused_computation.308 | loop fusion | flops 12842240 | bytes 3255296 | tf_op jit(solution)/shard_map/reduce_sum | solution.py:154
  60.8 2.5 %fusion.98 = (f32[256]{0:T(256)S(1)}, f32[256]{0:T(256)S(1)}, f32[256]{0:T(256)S(1)}, f32[256]{0:T(256)S(1)}, f32[256]{0:T(256)S(1)}, /*index=5*/f32[256]{0:T(25...) fusion(f32[4,8,32,256]{3,2,1,0:T(8,128)S(1)} %get-tuple-element, ...), kind=kLoop, calls=%fused_computation.275 | loop fusion | flops 14151168 | bytes 10504192 | tf_op jit(solution)/shard_map/reduce_sum | solution.py:154
  67.2 1.1 constant_dynamic-update-slice_fusion.7
  69.2 3.9 %collective-permute-start.4 = (f32[4,3,32,256]{3,2,1,0:T(8,128)}, f32[4,3,32,256]{3,2,1,0:T(8,128)}, u32[]{:S(2)}, u32[]{:S(2)}) collective-permute-start(f32[4,3,32,256]{3,2,1,0:T(8,128)} %get-tuple-element.104), channel_id=1, source_target_pairs={{1,0},{2,1},{3,2},{4,3},{5,4},{6,5},{7,6},{8,7},{9,8},{10,9},{11,1... | collective-permute-start | bytes 1179656 | tf_op jit(solution)/shard_map/ppermute | solution.py:27
  73.0 1.1 constant_dynamic-update-slice_fusion.13
  75.2 1.3 constant_dynamic-update-slice_fusion.11
  76.8 2.0 %collective-permute-done.3 = f32[4,3,32,256]{3,2,1,0:T(8,128)S(1)} collective-permute-done((f32[4,3,32,256]{3,2,1,0:T(8,128)}, f32[4,3,32,256]{3,2,1,0:T(8,128)S(1)}, u32[]{:S(2)}, u32[]{:S(2)}) %collective-permute-start.3) | collective-permute-done | bytes 393248 | tf_op jit(solution)/shard_map/ppermute | solution.py:26
  78.8 1.4 select_maximum_fusion
  80.6 10.3 %fusion.3 = f32[4,8,38,256]{3,2,1,0:T(8,128)S(1)} fusion(f32[4,14,44,256]{3,2,1,0:T(8,128)S(1)} %select_maximum_fusion, f32[256]{0:T(256)} %bitcast.48, f32[256]{0:T(256)} %bitcast.47, f32[256]{0:T(256)S(1)} %bitcast.341, f32[256]{0:T(256)S(1)} %bitcast.343, f32[256]{0:T(256)S(1)} %bitcast.345, f32[256]{0:T(256)S(1)} %bitcast.347, f32[256]{0:T(256)S(1)} %bitcast.349, ...), kind=kLoop, calls=%fused_computation.127 | loop fusion | flops 30195712 | bytes 62309376 | tf_op jit(solution)/shard_map/add | solution.py:260
  91.0 1.3 multiply_reduce_fusion.1
  92.2 1.3 constant_dynamic-update-slice_fusion.10
  93.5 1.3 constant_dynamic-update-slice_fusion.9
  94.8 1.3 constant_dynamic-update-slice_fusion.8
  96.1 1.3 pad_dynamic-slice_fusion
  97.4 2.2 %collective-permute-start.10 = (f32[270336]{0:T(1024)S(1)}, f32[270336]{0:T(1024)S(1)}, u32[]{:S(2)}, u32[]{:S(2)}) collective-permute-start(f32[270336]{0:T(1024)S(1)} %pad_dynamic-slice_fusion), channel_id=1, source_target_pairs={{0,1},{1,0},{2,3},{3,2},{4,5},{5,4},{6,7},{7,6},{8,9},{9,8},{10,11... | collective-permute-start | bytes 3244040 | tf_op jit(solution)/shard_map/ppermute | solution.py:16
  102.6 1.4 fusion.51
  105.4 0.8 reshape.178
  106.3 12.1 %collective-permute-done.11 = f32[135168]{0:T(1024)} collective-permute-done((f32[135168]{0:T(1024)S(1)}, f32[135168]{0:T(1024)}, u32[]{:S(2)}, u32[]{:S(2)}) %collective-permute-start.11) | collective-permute-done | bytes 540704 | tf_op jit(solution)/shard_map/ppermute | solution.py:16
  118.4 1.1 dynamic-slice_add_fusion
  119.5 0.7 dynamic_slice.29
  120.3 0.6 collective-permute-start.7
  120.9 3.6 %collective-permute-done.7 = f32[12800]{0:T(1024)S(1)} collective-permute-done((f32[12800]{0:T(1024)S(1)}, f32[12800]{0:T(1024)S(1)}, u32[]{:S(2)}, u32[]{:S(2)}) %collective-permute-start.7) | collective-permute-done | bytes 51232 | tf_op jit(solution)/shard_map/ppermute | solution.py:16
  124.5 2.1 %collective-permute-start.8 = (f32[12800]{0:T(1024)S(1)}, f32[12800]{0:T(1024)S(1)}, u32[]{:S(2)}, u32[]{:S(2)}) collective-permute-start(f32[12800]{0:T(1024)S(1)} %add.777), channel_id=1, source_target_pairs={{0,4},{1,5},{2,6},{3,7},{4,0},{5,1},{6,2},{7,3},{8,12},{9,13},{10,... | collective-permute-start | bytes 153608 | tf_op jit(solution)/shard_map/ppermute | solution.py:16
  126.5 2.6 %collective-permute-done.8 = f32[12800]{0:T(1024)S(1)} collective-permute-done((f32[12800]{0:T(1024)S(1)}, f32[12800]{0:T(1024)S(1)}, u32[]{:S(2)}, u32[]{:S(2)}) %collective-permute-start.8) | collective-permute-done | bytes 51232 | tf_op jit(solution)/shard_map/ppermute | solution.py:16
  129.1 1.7 collective-permute-start.9
  130.8 3.5 %collective-permute-done.9 = f32[12800]{0:T(1024)} collective-permute-done((f32[12800]{0:T(1024)S(1)}, f32[12800]{0:T(1024)}, u32[]{:S(2)}, u32[]{:S(2)}) %collective-permute-start.9) | collective-permute-done | bytes 51232 | tf_op jit(solution)/shard_map/ppermute | solution.py:16
  134.3 0.8 add.779
  135.1 1.0 dynamic-slice_add_fusion.1
  136.2 1.7 collective-permute-start.13
  138.0 8.0 %collective-permute-done.13 = f32[33792]{0:T(1024)S(1)} collective-permute-done((f32[33792]{0:T(1024)S(1)}, f32[33792]{0:T(1024)S(1)}, u32[]{:S(2)}, u32[]{:S(2)}) %collective-permute-start.13) | collective-permute-done | bytes 135200 | tf_op jit(solution)/shard_map/ppermute | solution.py:16
  147.6 4.0 %collective-permute-done.14 = bf16[33792]{0:T(1024)(128)(2,1)S(1)} collective-permute-done((bf16[33792]{0:T(1024)(128)(2,1)S(1)}, bf16[33792]{0:T(1024)(128)(2,1)S(1)}, u32[]{:S(2)}, u32[]{:S(2)}) %collective-permute-start.14) | collective-permute-done | bytes 67616 | tf_op jit(solution)/shard_map/ppermute | solution.py:16
  151.8 4.9 %collective-permute-done.15 = bf16[67584]{0:T(1024)(128)(2,1)S(1)} collective-permute-done((bf16[67584]{0:T(1024)(128)(2,1)S(1)}, bf16[67584]{0:T(1024)(128)(2,1)S(1)}, u32[]{:S(2)}, u32[]{:S(2)}) %collective-permute-start.15) | collective-permute-done | bytes 135200 | tf_op jit(solution)/shard_map/ppermute | solution.py:16
  156.8 1.5 collective-permute-start.16
  158.3 0.9 pad_maximum_fusion.10
  159.5 3.8 %collective-permute-done.16 = bf16[135168]{0:T(1024)(128)(2,1)S(1)} collective-permute-done((bf16[135168]{0:T(1024)(128)(2,1)S(1)}, bf16[135168]{0:T(1024)(128)(2,1)S(1)}, u32[]{:S(2)}, u32[]{:S(2)}) %collective-permute-start.16) | collective-permute-done | bytes 270368 | tf_op jit(solution)/shard_map/ppermute | solution.py:16
  163.8 0.8 concatenate.202
  165.0 1.2 maximum_select_fusion.3
  167.8 1.1 convert_multiply_fusion.98
  169.2 1.2 convert_multiply_fusion.99
  (364 shorter events, 22.0 us)
Async XLA Ops:
  0.6 33.5 %copy-start = (bf16[1024,256]{1,0:T(8,128)(2,1)S(1)}, bf16[1024,256]{1,0:T(8,128)(2,1)}, u32[]{:S(2)}) copy-start(bf16[1024,256]{1,0:T(8,128)(2,1)} %param.23) | copy-start | bytes 1572868
  0.7 21.3 %copy-start.2 = (bf16[4,8,32,256]{3,2,1,0:T(8,128)(2,1)S(1)}, bf16[4,8,32,256]{3,2,1,0:T(8,128)(2,1)}, u32[]{:S(2)}) copy-start(bf16[4,8,32,256]{3,2,1,0:T(8,128)(2,1)} %param.13) | copy-start | bytes 1572868
  0.7 17.9 %copy-start.12 = (s32[8,32]{1,0:T(8,128)S(1)}, s32[8,32]{1,0:T(8,128)}, u32[]{:S(2)}) copy-start(s32[8,32]{1,0:T(8,128)} %param.16) | copy-start | bytes 3076
  1.7 10.2 %collective-permute-start = (bf16[4,8,3,256]{3,2,1,0:T(4,128)(2,1)S(1)}, bf16[4,8,3,256]{3,2,1,0:T(4,128)(2,1)S(1)}, u32[]{:S(2)}, u32[]{:S(2)}) collective-permute-start(bf16[4,8,3,256]{3,2,1,0:T(4,128)(2,1)S(1)} %slice.716), channel_id=1, source_target_pairs={{0,15},{1,14},{2,13},{3,12},{4,11},{5,10},{6,9},{7,8},{8,7},{9,6},... | collective-permute-start | bytes 147464 | tf_op jit(solution)/shard_map/ppermute | solution.py:180
  8.2 14.1 %copy-start.15 = (f32[1,1,256]{2,1,0:T(1,128)}, f32[1,1,256]{2,1,0:T(1,128)S(1)}, u32[]{:S(2)}) copy-start(f32[1,1,256]{2,1,0:T(1,128)S(1)} %get-tuple-element.114) | copy-start | bytes 3076
  8.2 14.1 %copy-start.17 = (f32[1,1,256]{2,1,0:T(1,128)}, f32[1,1,256]{2,1,0:T(1,128)S(1)}, u32[]{:S(2)}) copy-start(f32[1,1,256]{2,1,0:T(1,128)S(1)} %get-tuple-element.115) | copy-start | bytes 3076
  8.2 14.1 %copy-start.19 = (f32[1,1,256]{2,1,0:T(1,128)}, f32[1,1,256]{2,1,0:T(1,128)S(1)}, u32[]{:S(2)}) copy-start(f32[1,1,256]{2,1,0:T(1,128)S(1)} %get-tuple-element.116) | copy-start | bytes 3076
  8.2 14.1 %copy-start.21 = (f32[1,1,256]{2,1,0:T(1,128)}, f32[1,1,256]{2,1,0:T(1,128)S(1)}, u32[]{:S(2)}) copy-start(f32[1,1,256]{2,1,0:T(1,128)S(1)} %get-tuple-element.117) | copy-start | bytes 3076
  8.2 14.1 %copy-start.23 = (f32[1,1,256]{2,1,0:T(1,128)}, f32[1,1,256]{2,1,0:T(1,128)S(1)}, u32[]{:S(2)}) copy-start(f32[1,1,256]{2,1,0:T(1,128)S(1)} %get-tuple-element.118) | copy-start | bytes 3076
  8.2 14.1 %copy-start.25 = (f32[1,1,256]{2,1,0:T(1,128)}, f32[1,1,256]{2,1,0:T(1,128)S(1)}, u32[]{:S(2)}) copy-start(f32[1,1,256]{2,1,0:T(1,128)S(1)} %get-tuple-element.119) | copy-start | bytes 3076
  8.2 14.1 %copy-start.27 = (f32[1,1,256]{2,1,0:T(1,128)}, f32[1,1,256]{2,1,0:T(1,128)S(1)}, u32[]{:S(2)}) copy-start(f32[1,1,256]{2,1,0:T(1,128)S(1)} %get-tuple-element.120) | copy-start | bytes 3076
  8.3 14.1 %copy-start.29 = (f32[1,1,256]{2,1,0:T(1,128)}, f32[1,1,256]{2,1,0:T(1,128)S(1)}, u32[]{:S(2)}) copy-start(f32[1,1,256]{2,1,0:T(1,128)S(1)} %get-tuple-element.121) | copy-start | bytes 3076
  8.3 14.1 %copy-start.31 = (f32[1,1,256]{2,1,0:T(1,128)}, f32[1,1,256]{2,1,0:T(1,128)S(1)}, u32[]{:S(2)}) copy-start(f32[1,1,256]{2,1,0:T(1,128)S(1)} %get-tuple-element.122) | copy-start | bytes 3076
  8.3 14.1 %copy-start.33 = (f32[1,1,256]{2,1,0:T(1,128)}, f32[1,1,256]{2,1,0:T(1,128)S(1)}, u32[]{:S(2)}) copy-start(f32[1,1,256]{2,1,0:T(1,128)S(1)} %get-tuple-element.123) | copy-start | bytes 3076
  8.3 14.1 %copy-start.35 = (f32[1,1,256]{2,1,0:T(1,128)}, f32[1,1,256]{2,1,0:T(1,128)S(1)}, u32[]{:S(2)}) copy-start(f32[1,1,256]{2,1,0:T(1,128)S(1)} %get-tuple-element.124) | copy-start | bytes 3076
  8.3 14.1 %copy-start.37 = (f32[1,1,256]{2,1,0:T(1,128)}, f32[1,1,256]{2,1,0:T(1,128)S(1)}, u32[]{:S(2)}) copy-start(f32[1,1,256]{2,1,0:T(1,128)S(1)} %get-tuple-element.125) | copy-start | bytes 3076
  8.3 14.1 %copy-start.39 = (f32[1,1,256]{2,1,0:T(1,128)}, f32[1,1,256]{2,1,0:T(1,128)S(1)}, u32[]{:S(2)}) copy-start(f32[1,1,256]{2,1,0:T(1,128)S(1)} %get-tuple-element.126) | copy-start | bytes 3076
  8.3 14.1 %copy-start.41 = (f32[1,1,256]{2,1,0:T(1,128)}, f32[1,1,256]{2,1,0:T(1,128)S(1)}, u32[]{:S(2)}) copy-start(f32[1,1,256]{2,1,0:T(1,128)S(1)} %get-tuple-element.127) | copy-start | bytes 3076
  8.3 14.1 %copy-start.43 = (f32[1,1,256]{2,1,0:T(1,128)}, f32[1,1,256]{2,1,0:T(1,128)S(1)}, u32[]{:S(2)}) copy-start(f32[1,1,256]{2,1,0:T(1,128)S(1)} %get-tuple-element.128) | copy-start | bytes 3076
  8.3 14.1 %copy-start.45 = (f32[1,1,256]{2,1,0:T(1,128)}, f32[1,1,256]{2,1,0:T(1,128)S(1)}, u32[]{:S(2)}) copy-start(f32[1,1,256]{2,1,0:T(1,128)S(1)} %get-tuple-element.129) | copy-start | bytes 3076
  8.3 14.1 %copy-start.47 = (f32[1,1,256]{2,1,0:T(1,128)}, f32[1,1,256]{2,1,0:T(1,128)S(1)}, u32[]{:S(2)}) copy-start(f32[1,1,256]{2,1,0:T(1,128)S(1)} %get-tuple-element.130) | copy-start | bytes 3076
  8.4 14.1 %copy-start.49 = (f32[1,1,256]{2,1,0:T(1,128)}, f32[1,1,256]{2,1,0:T(1,128)S(1)}, u32[]{:S(2)}) copy-start(f32[1,1,256]{2,1,0:T(1,128)S(1)} %get-tuple-element.131) | copy-start | bytes 3076
  9.4 13.1 %copy-start.51 = (f32[1,1,256]{2,1,0:T(1,128)}, f32[1,1,256]{2,1,0:T(1,128)S(1)}, u32[]{:S(2)}) copy-start(f32[1,1,256]{2,1,0:T(1,128)S(1)} %get-tuple-element.132) | copy-start | bytes 3076
  9.4 13.1 %copy-start.53 = (f32[1,1,256]{2,1,0:T(1,128)}, f32[1,1,256]{2,1,0:T(1,128)S(1)}, u32[]{:S(2)}) copy-start(f32[1,1,256]{2,1,0:T(1,128)S(1)} %get-tuple-element.133) | copy-start | bytes 3076
  9.4 13.1 %copy-start.55 = (f32[1,1,256]{2,1,0:T(1,128)}, f32[1,1,256]{2,1,0:T(1,128)S(1)}, u32[]{:S(2)}) copy-start(f32[1,1,256]{2,1,0:T(1,128)S(1)} %get-tuple-element.134) | copy-start | bytes 3076
  9.4 13.1 %copy-start.57 = (f32[1,1,256]{2,1,0:T(1,128)}, f32[1,1,256]{2,1,0:T(1,128)S(1)}, u32[]{:S(2)}) copy-start(f32[1,1,256]{2,1,0:T(1,128)S(1)} %get-tuple-element.135) | copy-start | bytes 3076
  9.4 13.1 %copy-start.59 = (f32[1,1,256]{2,1,0:T(1,128)}, f32[1,1,256]{2,1,0:T(1,128)S(1)}, u32[]{:S(2)}) copy-start(f32[1,1,256]{2,1,0:T(1,128)S(1)} %get-tuple-element.136) | copy-start | bytes 3076
  9.4 13.1 %copy-start.61 = (f32[1,1,256]{2,1,0:T(1,128)}, f32[1,1,256]{2,1,0:T(1,128)S(1)}, u32[]{:S(2)}) copy-start(f32[1,1,256]{2,1,0:T(1,128)S(1)} %get-tuple-element.137) | copy-start | bytes 3076
  9.5 13.1 %copy-start.63 = (f32[1,1,256]{2,1,0:T(1,128)}, f32[1,1,256]{2,1,0:T(1,128)S(1)}, u32[]{:S(2)}) copy-start(f32[1,1,256]{2,1,0:T(1,128)S(1)} %get-tuple-element.138) | copy-start | bytes 3076
  9.5 13.1 %copy-start.65 = (f32[1,1,256]{2,1,0:T(1,128)}, f32[1,1,256]{2,1,0:T(1,128)S(1)}, u32[]{:S(2)}) copy-start(f32[1,1,256]{2,1,0:T(1,128)S(1)} %get-tuple-element.139) | copy-start | bytes 3076
  9.5 13.1 %copy-start.67 = (f32[1,1,256]{2,1,0:T(1,128)}, f32[1,1,256]{2,1,0:T(1,128)S(1)}, u32[]{:S(2)}) copy-start(f32[1,1,256]{2,1,0:T(1,128)S(1)} %get-tuple-element.140) | copy-start | bytes 3076
  9.5 13.1 %copy-start.69 = (f32[1,1,256]{2,1,0:T(1,128)}, f32[1,1,256]{2,1,0:T(1,128)S(1)}, u32[]{:S(2)}) copy-start(f32[1,1,256]{2,1,0:T(1,128)S(1)} %get-tuple-element.141) | copy-start | bytes 3076
  9.5 13.1 %copy-start.71 = (f32[1,1,256]{2,1,0:T(1,128)}, f32[1,1,256]{2,1,0:T(1,128)S(1)}, u32[]{:S(2)}) copy-start(f32[1,1,256]{2,1,0:T(1,128)S(1)} %get-tuple-element.142) | copy-start | bytes 3076
  9.5 13.1 %copy-start.73 = (f32[1,1,256]{2,1,0:T(1,128)}, f32[1,1,256]{2,1,0:T(1,128)S(1)}, u32[]{:S(2)}) copy-start(f32[1,1,256]{2,1,0:T(1,128)S(1)} %get-tuple-element.143) | copy-start | bytes 3076
  9.5 13.1 %copy-start.75 = (f32[1,1,256]{2,1,0:T(1,128)}, f32[1,1,256]{2,1,0:T(1,128)S(1)}, u32[]{:S(2)}) copy-start(f32[1,1,256]{2,1,0:T(1,128)S(1)} %get-tuple-element.144) | copy-start | bytes 3076
  9.5 13.1 %copy-start.77 = (f32[1,1,256]{2,1,0:T(1,128)}, f32[1,1,256]{2,1,0:T(1,128)S(1)}, u32[]{:S(2)}) copy-start(f32[1,1,256]{2,1,0:T(1,128)S(1)} %get-tuple-element.145) | copy-start | bytes 3076
  9.5 13.1 %copy-start.79 = (f32[1,1,256]{2,1,0:T(1,128)}, f32[1,1,256]{2,1,0:T(1,128)S(1)}, u32[]{:S(2)}) copy-start(f32[1,1,256]{2,1,0:T(1,128)S(1)} %get-tuple-element.146) | copy-start | bytes 3076
  9.5 13.1 %copy-start.81 = (f32[1,1,256]{2,1,0:T(1,128)}, f32[1,1,256]{2,1,0:T(1,128)S(1)}, u32[]{:S(2)}) copy-start(f32[1,1,256]{2,1,0:T(1,128)S(1)} %get-tuple-element.147) | copy-start | bytes 3076
  9.6 13.1 %copy-start.83 = (f32[1,1,256]{2,1,0:T(1,128)}, f32[1,1,256]{2,1,0:T(1,128)S(1)}, u32[]{:S(2)}) copy-start(f32[1,1,256]{2,1,0:T(1,128)S(1)} %get-tuple-element.148) | copy-start | bytes 3076
  9.6 13.1 %copy-start.85 = (f32[1,1,256]{2,1,0:T(1,128)}, f32[1,1,256]{2,1,0:T(1,128)S(1)}, u32[]{:S(2)}) copy-start(f32[1,1,256]{2,1,0:T(1,128)S(1)} %get-tuple-element.149) | copy-start | bytes 3076
  9.6 13.1 %copy-start.87 = (f32[1,1,256]{2,1,0:T(1,128)}, f32[1,1,256]{2,1,0:T(1,128)S(1)}, u32[]{:S(2)}) copy-start(f32[1,1,256]{2,1,0:T(1,128)S(1)} %get-tuple-element.150) | copy-start | bytes 3076
  11.1 20.9 %copy-start.89 = (f32[1,1,256]{2,1,0:T(1,128)}, f32[1,1,256]{2,1,0:T(1,128)S(1)}, u32[]{:S(2)}) copy-start(f32[1,1,256]{2,1,0:T(1,128)S(1)} %get-tuple-element.151) | copy-start | bytes 3076
  11.1 20.9 %copy-start.90 = (f32[1,1,256]{2,1,0:T(1,128)}, f32[1,1,256]{2,1,0:T(1,128)S(1)}, u32[]{:S(2)}) copy-start(f32[1,1,256]{2,1,0:T(1,128)S(1)} %get-tuple-element.152) | copy-start | bytes 3076
  13.5 8.5 %collective-permute-start.1 = (bf16[4,3,38,256]{3,2,1,0:T(8,128)(2,1)S(1)}, bf16[4,3,38,256]{3,2,1,0:T(8,128)(2,1)S(1)}, u32[]{:S(2)}, u32[]{:S(2)}) collective-permute-start(bf16[4,3,38,256]{3,2,1,0:T(8,128)(2,1)S(1)} %get-tuple-element.107), channel_id=1, source_target_pairs={{0,1},{1,2},{2,3},{3,4},{4,5},{5,6},{6,7},{7,8},{8,9},{9,10},{10,1... | collective-permute-start | bytes 700424 | tf_op jit(solution)/shard_map/ppermute | solution.py:26
  14.2 7.8 %collective-permute-start.2 = (bf16[4,3,38,256]{3,2,1,0:T(8,128)(2,1)S(1)}, bf16[4,3,38,256]{3,2,1,0:T(8,128)(2,1)S(1)}, u32[]{:S(2)}, u32[]{:S(2)}) collective-permute-start(bf16[4,3,38,256]{3,2,1,0:T(8,128)(2,1)S(1)} %get-tuple-element.108), channel_id=1, source_target_pairs={{1,0},{2,1},{3,2},{4,3},{5,4},{6,5},{7,6},{8,7},{9,8},{10,9},{11,1... | collective-permute-start | bytes 700424 | tf_op jit(solution)/shard_map/ppermute | solution.py:27
  68.5 10.3 %collective-permute-start.3 = (f32[4,3,32,256]{3,2,1,0:T(8,128)}, f32[4,3,32,256]{3,2,1,0:T(8,128)S(1)}, u32[]{:S(2)}, u32[]{:S(2)}) collective-permute-start(f32[4,3,32,256]{3,2,1,0:T(8,128)} %get-tuple-element.103), channel_id=1, source_target_pairs={{0,1},{1,2},{2,3},{3,4},{4,5},{5,6},{6,7},{7,8},{8,9},{9,10},{10,1... | collective-permute-start | bytes 1179656 | tf_op jit(solution)/shard_map/ppermute | solution.py:26
  69.2 9.7 %collective-permute-start.4 = (f32[4,3,32,256]{3,2,1,0:T(8,128)}, f32[4,3,32,256]{3,2,1,0:T(8,128)}, u32[]{:S(2)}, u32[]{:S(2)}) collective-permute-start(f32[4,3,32,256]{3,2,1,0:T(8,128)} %get-tuple-element.104), channel_id=1, source_target_pairs={{1,0},{2,1},{3,2},{4,3},{5,4},{6,5},{7,6},{8,7},{9,8},{10,9},{11,1... | collective-permute-start | bytes 1179656 | tf_op jit(solution)/shard_map/ppermute | solution.py:27
  80.6 10.3 %copy-start.5 = (f32[256,256]{1,0:T(8,128)S(1)}, f32[256,256]{1,0:T(8,128)}, u32[]{:S(2)}) copy-start(f32[256,256]{1,0:T(8,128)} %copy-done.4) | copy-start | bytes 786436
  80.6 10.3 %copy-start.7 = (f32[256,256]{1,0:T(8,128)S(1)}, f32[256,256]{1,0:T(8,128)}, u32[]{:S(2)}) copy-start(f32[256,256]{1,0:T(8,128)} %copy-done.6) | copy-start | bytes 786436
  80.6 10.3 %copy-start.9 = (f32[256,256]{1,0:T(8,128)S(1)}, f32[256,256]{1,0:T(8,128)}, u32[]{:S(2)}) copy-start(f32[256,256]{1,0:T(8,128)} %copy-done.8) | copy-start | bytes 786436
  97.4 5.3 %collective-permute-start.10 = (f32[270336]{0:T(1024)S(1)}, f32[270336]{0:T(1024)S(1)}, u32[]{:S(2)}, u32[]{:S(2)}) collective-permute-start(f32[270336]{0:T(1024)S(1)} %pad_dynamic-slice_fusion), channel_id=1, source_target_pairs={{0,1},{1,0},{2,3},{3,2},{4,5},{5,4},{6,7},{7,6},{8,9},{9,8},{10,11... | collective-permute-start | bytes 3244040 | tf_op jit(solution)/shard_map/ppermute | solution.py:16
  104.0 14.3 %collective-permute-start.11 = (f32[135168]{0:T(1024)S(1)}, f32[135168]{0:T(1024)}, u32[]{:S(2)}, u32[]{:S(2)}) collective-permute-start(f32[135168]{0:T(1024)S(1)} %dynamic_slice.27), channel_id=1, source_target_pairs={{0,2},{1,3},{2,0},{3,1},{4,6},{5,7},{6,4},{7,5},{8,10},{9,11},{10,... | collective-permute-start | bytes 1622024 | tf_op jit(solution)/shard_map/ppermute | solution.py:16
  106.2 14.0 %collective-permute-start.6 = (f32[12800]{0:T(1024)S(1)}, f32[12800]{0:T(1024)S(1)}, u32[]{:S(2)}, u32[]{:S(2)}) collective-permute-start(f32[12800]{0:T(1024)S(1)} %pad_maximum_fusion.14), channel_id=1, source_target_pairs={{0,1},{1,0},{2,3},{3,2},{4,5},{5,4},{6,7},{7,6},{8,9},{9,8},{10,11... | collective-permute-start | bytes 153608 | tf_op jit(solution)/shard_map/ppermute | solution.py:16
  120.2 27.1 %copy-start.3 = (f32[4,8,32,256]{3,2,1,0:T(8,128)S(1)}, f32[4,8,32,256]{3,2,1,0:T(8,128)}, u32[]{:S(2)}) copy-start(f32[4,8,32,256]{3,2,1,0:T(8,128)} %get-tuple-element.102) | copy-start | bytes 3145732
  120.2 14.9 %collective-permute-start.12 = (f32[67584]{0:T(1024)}, f32[67584]{0:T(1024)}, u32[]{:S(2)}, u32[]{:S(2)}) collective-permute-start(f32[67584]{0:T(1024)} %dynamic_slice.29), channel_id=1, source_target_pairs={{0,4},{1,5},{2,6},{3,7},{4,0},{5,1},{6,2},{7,3},{8,12},{9,13},{10,... | collective-permute-start | bytes 811016 | tf_op jit(solution)/shard_map/ppermute | solution.py:16
  120.3 4.2 %collective-permute-start.7 = (f32[12800]{0:T(1024)S(1)}, f32[12800]{0:T(1024)S(1)}, u32[]{:S(2)}, u32[]{:S(2)}) collective-permute-start(f32[12800]{0:T(1024)S(1)} %fusion.264), channel_id=1, source_target_pairs={{0,2},{1,3},{2,0},{3,1},{4,6},{5,7},{6,4},{7,5},{8,10},{9,11},{10,... | collective-permute-start | bytes 153608 | tf_op jit(solution)/shard_map/ppermute | solution.py:16
  124.5 4.6 %collective-permute-start.8 = (f32[12800]{0:T(1024)S(1)}, f32[12800]{0:T(1024)S(1)}, u32[]{:S(2)}, u32[]{:S(2)}) collective-permute-start(f32[12800]{0:T(1024)S(1)} %add.777), channel_id=1, source_target_pairs={{0,4},{1,5},{2,6},{3,7},{4,0},{5,1},{6,2},{7,3},{8,12},{9,13},{10,... | collective-permute-start | bytes 153608 | tf_op jit(solution)/shard_map/ppermute | solution.py:16
  129.1 5.2 %collective-permute-start.9 = (f32[12800]{0:T(1024)S(1)}, f32[12800]{0:T(1024)}, u32[]{:S(2)}, u32[]{:S(2)}) collective-permute-start(f32[12800]{0:T(1024)S(1)} %add.778), channel_id=1, source_target_pairs={{0,8},{1,9},{2,10},{3,11},{4,12},{5,13},{6,14},{7,15},{8,0},{9,1},... | collective-permute-start | bytes 153608 | tf_op jit(solution)/shard_map/ppermute | solution.py:16
  136.2 9.8 %collective-permute-start.13 = (f32[33792]{0:T(1024)S(1)}, f32[33792]{0:T(1024)S(1)}, u32[]{:S(2)}, u32[]{:S(2)}) collective-permute-start(f32[33792]{0:T(1024)S(1)} %dynamic_slice.31), channel_id=1, source_target_pairs={{0,8},{1,9},{2,10},{3,11},{4,12},{5,13},{6,14},{7,15},{8,0},{9,1},... | collective-permute-start | bytes 405512 | tf_op jit(solution)/shard_map/ppermute | solution.py:16
  137.9 9.5 %collective-permute-start.5 = (bf16[4,8,3,256]{3,2,1,0:T(4,128)(2,1)S(1)}, bf16[4,8,3,256]{3,2,1,0:T(4,128)(2,1)S(1)}, u32[]{:S(2)}, u32[]{:S(2)}) collective-permute-start(bf16[4,8,3,256]{3,2,1,0:T(4,128)(2,1)S(1)} %slice.1508), channel_id=1, source_target_pairs={{0,15},{1,14},{2,13},{3,12},{4,11},{5,10},{6,9},{7,8},{8,7},{9,6},... | collective-permute-start | bytes 147464 | tf_op jit(solution)/shard_map/ppermute | solution.py:180
  146.0 5.6 %collective-permute-start.14 = (bf16[33792]{0:T(1024)(128)(2,1)S(1)}, bf16[33792]{0:T(1024)(128)(2,1)S(1)}, u32[]{:S(2)}, u32[]{:S(2)}) collective-permute-start(bf16[33792]{0:T(1024)(128)(2,1)S(1)} %add_convert_fusion.1), channel_id=1, source_target_pairs={{0,8},{1,9},{2,10},{3,11},{4,12},{5,13},{6,14},{7,15},{8,0},{9,1},... | collective-permute-start | bytes 202760 | tf_op jit(solution)/shard_map/ppermute | solution.py:16
  151.6 5.1 %collective-permute-start.15 = (bf16[67584]{0:T(1024)(128)(2,1)S(1)}, bf16[67584]{0:T(1024)(128)(2,1)S(1)}, u32[]{:S(2)}, u32[]{:S(2)}) collective-permute-start(bf16[67584]{0:T(1024)(128)(2,1)S(1)} %maximum_select_fusion.8), channel_id=1, source_target_pairs={{0,4},{1,5},{2,6},{3,7},{4,0},{5,1},{6,2},{7,3},{8,12},{9,13},{10,... | collective-permute-start | bytes 405512 | tf_op jit(solution)/shard_map/ppermute | solution.py:16
  156.8 6.5 %collective-permute-start.16 = (bf16[135168]{0:T(1024)(128)(2,1)S(1)}, bf16[135168]{0:T(1024)(128)(2,1)S(1)}, u32[]{:S(2)}, u32[]{:S(2)}) collective-permute-start(bf16[135168]{0:T(1024)(128)(2,1)S(1)} %maximum_select_fusion.5), channel_id=1, source_target_pairs={{0,2},{1,3},{2,0},{3,1},{4,6},{5,7},{6,4},{7,5},{8,10},{9,11},{10,... | collective-permute-start | bytes 811016 | tf_op jit(solution)/shard_map/ppermute | solution.py:16
  163.4 2.8 %collective-permute-start.17 = (bf16[270336]{0:T(1024)(128)(2,1)S(1)}, bf16[270336]{0:T(1024)(128)(2,1)S(1)}, u32[]{:S(2)}, u32[]{:S(2)}) collective-permute-start(bf16[270336]{0:T(1024)(128)(2,1)S(1)} %maximum_select_fusion.1), channel_id=1, source_target_pairs={{0,1},{1,0},{2,3},{3,2},{4,5},{5,4},{6,7},{7,6},{8,9},{9,8},{10,11... | collective-permute-start | bytes 1622024 | tf_op jit(solution)/shard_map/ppermute | solution.py:16
  (89 other events, 378.7 us)

commit v2 on v1

--- a/solution.py
+++ b/solution.py
@@ -189,23 +189,34 @@
     return picked[:, ::-1, ::-1, :]
 
 
-def halving_allreduce(flat, axis, gather_dtype):
-    size = lax.axis_size(axis)
-    bits = size.bit_length() - 1
+def halving_allreduce(flat, axis, gather_dtype, order):
     idx = lax.axis_index(axis)
     cur = flat
-    for bit in range(bits):
+    for bit in order:
         half = cur.shape[0] // 2
         mine = (idx >> bit) & 1
         keep = lax.dynamic_slice_in_dim(cur, mine * half, half)
         send = lax.dynamic_slice_in_dim(cur, (1 - mine) * half, half)
         cur = keep + swapped(send, axis, bit)
     cur = cur.astype(gather_dtype)
-    for bit in reversed(range(bits)):
+    for bit in reversed(order):
         mine = (idx >> bit) & 1
         recv = swapped(cur, axis, bit)
         cur = jnp.where(mine == 0, jnp.concatenate([cur, recv]), jnp.concatenate([recv, cur]))
     return cur.astype(flat.dtype)
+
+
+def split_allreduce(flat, axis, gather_dtype):
+    bits = list(range(lax.axis_size(axis).bit_length() - 1))
+    orders = [bits]
+    if len(bits) > 2:
+        orders.append([bits[0], bits[2], bits[1]] + bits[3:])
+    length = flat.shape[0] // len(orders)
+    parts = [
+        halving_allreduce(flat[k * length : (k + 1) * length], axis, gather_dtype, order)
+        for k, order in enumerate(orders)
+    ]
+    return jnp.concatenate(parts)
 
 
 def butterfly_allreduce(flat, axis):
@@ -283,10 +294,13 @@
         scale_sum,
     ) = grads
     lon_size = lax.axis_size("lon")
-    big = (w_in_sum, w_out_sum, b_in_sum, b_out_sum, scale_sum, gain_sum, bias_sum)
-    big_tot = unpack(
-        halving_allreduce(pack(big, lon_size * 1024), "lon", jnp.bfloat16), big
-    )
+    early = (w_out_sum, b_out_sum, scale_sum)
+    early_tot = unpack(
+        split_allreduce(pack(early, lon_size * 2048), "lon", jnp.bfloat16), early
+    )
+    late = (w_in_sum, b_in_sum, gain_sum, bias_sum)
+    late_tot = unpack(split_allreduce(pack(late, lon_size * 2048), "lon", jnp.bfloat16), late)
+    big_tot = (late_tot[0], early_tot[0], late_tot[1], early_tot[1], early_tot[2], late_tot[2], late_tot[3])
     small = (kernel_sum, dw_bias_sum)
     small_tot = unpack(butterfly_allreduce(pack(small, 128), "lon"), small)
     totals = (

time: 171 us -> 189 us (1.11)
  starting transfers between devices: 24.7 us -> 42.2 us
  other arithmetic: 55.8 us -> 52.6 us
  matrix products: 16.3 us -> 18.6 us
    ppermute x12 -> x36, starting transfers between devices: 10.2 us -> 26.8 us  [swapped(): lax.ppermute(x, axis, [(i, i ^ 1 << bit) for i in range(lax.axis_size(axi...]
    unnamed x283 -> x293, local copies, waits for them, and re-layouts: 11.3 us -> 5.93 us
    ppermute x12 -> x36, waiting for transfers between devices: 42.5 us -> 45.8 us  [swapped(): lax.ppermute(x, axis, [(i, i ^ 1 << bit) for i in range(lax.axis_size(axi...]
    dynamic_slice x4 -> x16, local copies, waits for them, and re-layouts: 2.08 us -> 5.14 us  [halving_allreduce(): send = lax.dynamic_slice_in_dim(cur, (1 - mine) * half, half)]
    another operation x7, local copies, waits for them, and re-layouts: 0.2 us -> 3 us  [local_step(): kernel_rows.append(jnp.stack(kernel_cols))]
    dot_general x4, matrix products: 1.28 us -> 3.55 us  [local_step(): lax.dot_general(normed[member].reshape(rows, chans), pre_half, contract_r...]
    add x3 -> x12, other arithmetic: 3.45 us -> 4.14 us  [halving_allreduce(): cur = keep + swapped(send, axis, bit)]
  transfers between devices with their start and end apart: 18 -> 42, of which waited for: 10 -> 22; matrix products, arithmetic and copies ran while one was open for 13% -> 21% of each run, Pallas kernels for 0% -> 0%
where the time goes in v2:
time: 189 us; the launch traced here: 188 us
  other arithmetic  52.6 us (28%)
  waiting for transfers between devices  49 us (26%)
  starting transfers between devices  42.2 us (22%)
  local copies, waits for them, and re-layouts  22.1 us (12%)
  matrix products  18.6 us (10%)
  between operations  3.38 us (2%)
    ppermute x36, waiting for transfers between devices, swapped(): lax.ppermute(x, axis, [(i, i ^ 1 << bit) for i in range(lax.axis_size(axi...  45.8 us
    ppermute x36, starting transfers between devices, swapped(): lax.ppermute(x, axis, [(i, i ^ 1 << bit) for i in range(lax.axis_size(axi...  26.8 us
    add x1, other arithmetic, on_device(): grad_ext + dw_kernel[lon_off, lat_off] * padded[:, 6 - lon_off:6 - lon_of...  10.4 us
    reduce_sum x4, other arithmetic, local_step(): jnp.sum(grad_depth * extended[:, lon_off:lon_off + lon_dev, lat_off:lat_o...  10 us
    reduce_sum x1, other arithmetic, local_step(): mean_val = jnp.mean(depth, axis=-1, keepdims=True)  9.3 us
    ppermute x2, starting transfers between devices, with_halo(): after = lax.ppermute(leading, axis, down)  8.16 us
    ppermute x2, starting transfers between devices, mirrored(): return lax.ppermute(x, axis, [(i, size - 1 - i) for i in range(size)])  6.53 us
    dot_general x4, matrix products, local_step(): lax.dot_general(out_half, w_out, contract_cols, preferred_element_type=jn...  5.97 us
  transfers between devices with their start and end apart: 42, of which 22 were waited for; matrix products, arithmetic and copies ran while one was open for 21% of the time, Pallas kernels for 0%

profile of v2, /device:TPU:0, one launch (start us, length us, event | category | flops | bytes accessed | tf_op | source)
XLA Modules:
  0.0 187.9 jit_solution(17653555043096629535)
XLA Ops:
  0.7 1.0 slice.738
  1.7 5.5 %collective-permute-start = (bf16[4,8,3,256]{3,2,1,0:T(4,128)(2,1)S(1)}, bf16[4,8,3,256]{3,2,1,0:T(4,128)(2,1)S(1)}, u32[]{:S(2)}, u32[]{:S(2)}) collective-permute-start(bf16[4,8,3,256]{3,2,1,0:T(4,128)(2,1)S(1)} %slice.738), channel_id=1, source_target_pairs={{0,15},{1,14},{2,13},{3,12},{4,11},{5,10},{6,9},{7,8},{8,7},{9,6},... | collective-permute-start | bytes 147464 | tf_op jit(solution)/shard_map/ppermute | solution.py:180
  8.2 1.0 fusion.220
  9.4 1.6 fusion.221
  12.7 1.3 pad_maximum_fusion.11
  14.8 3.8 %collective-permute-start.2 = (bf16[4,3,38,256]{3,2,1,0:T(8,128)(2,1)S(1)}, bf16[4,3,38,256]{3,2,1,0:T(8,128)(2,1)S(1)}, u32[]{:S(2)}, u32[]{:S(2)}) collective-permute-start(bf16[4,3,38,256]{3,2,1,0:T(8,128)(2,1)S(1)} %get-tuple-element.104), channel_id=1, source_target_pairs={{1,0},{2,1},{3,2},{4,3},{5,4},{6,5},{7,6},{8,7},{9,8},{10,9},{11,1... | collective-permute-start | bytes 700424 | tf_op jit(solution)/shard_map/ppermute | solution.py:27
  19.3 3.2 %collective-permute-done.1 = bf16[4,3,38,256]{3,2,1,0:T(8,128)(2,1)S(1)} collective-permute-done((bf16[4,3,38,256]{3,2,1,0:T(8,128)(2,1)S(1)}, bf16[4,3,38,256]{3,2,1,0:T(8,128)(2,1)S(1)}, u32[]{:S(2)}, u32[]{:S(2)}) %collective-permute-start.1) | collective-permute-done | bytes 233504 | tf_op jit(solution)/shard_map/ppermute | solution.py:26
  23.3 9.3 %fusion.216 = (f32[4,8,32]{2,1,0:T(8,128)S(1)}, f32[4,8,32,256]{3,2,1,0:T(8,128)S(1)}) fusion(bf16[4,11,38,256]{3,2,1,0:T(8,128)(2,1)S(1)} %get-tuple-element.102, f32[256]{0:T(256)S(1)} %bitcast.366, f32[256]{0:T(256)S(1)} %bitcast.368, f32[256]{0:T(256)S(1)} %bitcast.372, f32[256]{0:T(256)S(1)} %bitcast.374, f32[256]{0:T(256)S(1)} %bitcast.376, ...), kind=kLoop, calls=%fused_computation.534 | loop fusion | flops 43514880 | bytes 23746560 | tf_op jit(solution)/shard_map/reduce_sum | solution.py:62
  37.6 1.1 fusion.214
  38.7 3.8 %multiply_reduce_fusion.7 = (f32[256]{0:T(256)}, f32[256]{0:T(256)}, f32[256]{0:T(256)}, f32[256]{0:T(256)}, f32[8,32,256]{2,1,0:T(8,128)S(1)}, /*index=5*/f32[8...) fusion(f32[256]{0:T(256)S(1)} %copy-done.34, ...), kind=kLoop, calls=%fused_computation.454 | loop fusion | flops 7863296 | bytes 2497536 | tf_op jit(solution)/shard_map/reduce_sum | solution.py:117
  42.6 1.5 fusion.208
  44.7 1.5 fusion.206
  46.2 0.9 fusion.226
  47.1 1.5 fusion.210
  48.6 1.5 fusion.212
  50.0 0.9 fusion.223
  51.0 0.9 fusion.224
  52.8 1.0 multiply_reduce_fusion.1
  53.8 4.0 %fusion.145 = (f32[256]{0:T(256)}, f32[256]{0:T(256)}, f32[256]{0:T(256)}, f32[256]{0:T(256)}, f32[256]{0:T(256)}, /*index=5*/f32[256]{0:T(256)}, f32[256]{0:T(2...) fusion(bf16[4,11,38,256]{3,2,1,0:T(8,128)(2,1)S(1)} %get-tuple-, ...), kind=kLoop, calls=%fused_computation.319 | loop fusion | flops 16772608 | bytes 12618752 | tf_op jit(solution)/shard_map/reduce_sum | solution.py:154
  57.8 2.4 %fusion.127 = (f32[256]{0:T(256)}, f32[256]{0:T(256)}, f32[256]{0:T(256)}, f32[256]{0:T(256)S(1)}, f32[256]{0:T(256)}, /*index=5*/f32[256]{0:T(256)}, f32[256]{0...) fusion(f32[4,8,32,256]{3,2,1,0:T(8,128)S(1)} %get-tuple-element.91, ...), kind=kLoop, calls=%fused_computation.301 | loop fusion | flops 12842240 | bytes 3255296 | tf_op jit(solution)/shard_map/reduce_sum | solution.py:154
  60.6 3.2 %fusion.94 = (f32[256]{0:T(256)}, f32[256]{0:T(256)}, f32[256]{0:T(256)}, f32[256]{0:T(256)}, f32[256]{0:T(256)}, /*index=5*/f32[256]{0:T(256)}, f32[256]{0:T(25...) fusion(f32[4,8,32,256]{3,2,1,0:T(8,128)S(1)} %get-tuple-element, ...), kind=kLoop, calls=%fused_computation.268 | loop fusion | flops 14151168 | bytes 10504192 | tf_op jit(solution)/shard_map/reduce_sum | solution.py:154
  63.8 1.3 fusion.194
  65.1 1.0 fusion.218
  71.9 1.6 convolution_add_fusion.5
  77.7 4.4 %collective-permute-start.4 = (f32[4,3,32,256]{3,2,1,0:T(8,128)}, f32[4,3,32,256]{3,2,1,0:T(8,128)}, u32[]{:S(2)}, u32[]{:S(2)}) collective-permute-start(f32[4,3,32,256]{3,2,1,0:T(8,128)} %get-tuple-element.100), channel_id=1, source_target_pairs={{1,0},{2,1},{3,2},{4,3},{5,4},{6,5},{7,6},{8,7},{9,8},{10,9},{11,1... | collective-permute-start | bytes 1179656 | tf_op jit(solution)/shard_map/ppermute | solution.py:27
  82.6 8.0 %collective-permute-done.7 = f32[12800]{0:T(1024)S(1)} collective-permute-done((f32[12800]{0:T(1024)S(1)}, f32[12800]{0:T(1024)S(1)}, u32[]{:S(2)}, u32[]{:S(2)}) %collective-permute-start.7) | collective-permute-done | bytes 51232 | tf_op jit(solution)/shard_map/ppermute | solution.py:16
  90.7 4.0 %collective-permute-done.8 = f32[12800]{0:T(1024)S(1)} collective-permute-done((f32[12800]{0:T(1024)S(1)}, f32[12800]{0:T(1024)S(1)}, u32[]{:S(2)}, u32[]{:S(2)}) %collective-permute-start.8) | collective-permute-done | bytes 51232 | tf_op jit(solution)/shard_map/ppermute | solution.py:16
  96.8 1.5 copy.30
  98.3 1.5 collective-permute-done.9
  101.1 1.1 dynamic-slice_add_fusion.2
  102.5 1.0 dynamic-slice_add_fusion.1
  103.5 1.9 collective-permute-start.27
  107.0 1.5 select_maximum_fusion
  108.9 10.4 %fusion.1 = f32[4,8,38,256]{3,2,1,0:T(8,128)S(1)} fusion(f32[4,14,44,256]{3,2,1,0:T(8,128)S(1)} %select_maximum_fusion, f32[256]{0:T(256)S(1)} %bitcast.367, f32[256]{0:T(256)S(1)} %bitcast.369, f32[256]{0:T(256)S(1)} %bitcast.373, f32[256]{0:T(256)S(1)} %bitcast.375, f32[256]{0:T(256)S(1)} %bitcast.377, f32[256]{0:T(256)S(1)} %bitcast.379, ...), kind=kLoop, calls=%fused_computation.123 | loop fusion | flops 30195712 | bytes 62309376 | tf_op jit(solution)/shard_map/add | solution.py:271
  119.3 1.0 collective-permute-start.5
  123.8 1.1 collective-permute-start.20
  125.6 0.9 collective-permute-start.28
  126.5 0.9 rev.7
  127.5 0.9 dynamic-slice_add_fusion.7
  128.5 1.7 collective-permute-start.12
  131.1 1.4 collective-permute-start.21
  132.5 1.7 collective-permute-start.29
  134.2 1.4 collective-permute-start.13
  135.5 1.8 collective-permute-done.21
  137.5 1.2 collective-permute-done.29
  138.7 1.7 collective-permute-start.30
  140.4 1.4 collective-permute-start.14
  142.1 0.9 collective-permute-start.23
  143.5 1.2 collective-permute-start.31
  146.1 1.2 collective-permute-start.24
  150.6 1.5 collective-permute-done.32
  152.2 1.3 collective-permute-done.16
  154.1 1.0 dynamic-slice_add_fusion
  156.7 4.7 %collective-permute-done.35 = f32[36864]{0:T(1024)S(1)} collective-permute-done((f32[36864]{0:T(1024)S(1)}, f32[36864]{0:T(1024)S(1)}, u32[]{:S(2)}, u32[]{:S(2)}) %collective-permute-start.35) | collective-permute-done | bytes 147488 | tf_op jit(solution)/shard_map/ppermute | solution.py:16
  162.8 3.0 %collective-permute-done.36 = f32[18432]{0:T(1024)S(1)} collective-permute-done((f32[18432]{0:T(1024)S(1)}, f32[18432]{0:T(1024)S(1)}, u32[]{:S(2)}, u32[]{:S(2)}) %collective-permute-start.36) | collective-permute-done | bytes 73760 | tf_op jit(solution)/shard_map/ppermute | solution.py:16
  165.9 1.4 collective-permute-start.37
  167.4 3.8 %collective-permute-done.37 = f32[9216]{0:T(1024)S(1)} collective-permute-done((f32[9216]{0:T(1024)S(1)}, f32[9216]{0:T(1024)S(1)}, u32[]{:S(2)}, u32[]{:S(2)}) %collective-permute-start.37) | collective-permute-done | bytes 36896 | tf_op jit(solution)/shard_map/ppermute | solution.py:16
  171.2 1.0 collective-permute-start.38
  172.3 3.8 %collective-permute-done.38 = bf16[9216]{0:T(1024)(128)(2,1)S(1)} collective-permute-done((bf16[9216]{0:T(1024)(128)(2,1)S(1)}, bf16[9216]{0:T(1024)(128)(2,1)S(1)}, u32[]{:S(2)}, u32[]{:S(2)}) %collective-permute-start.38) | collective-permute-done | bytes 18464 | tf_op jit(solution)/shard_map/ppermute | solution.py:16
  176.3 1.1 convert_multiply_fusion.99
  177.4 2.7 %collective-permute-done.39 = bf16[18432]{0:T(1024)(128)(2,1)S(1)} collective-permute-done((bf16[18432]{0:T(1024)(128)(2,1)S(1)}, bf16[18432]{0:T(1024)(128)(2,1)S(1)}, u32[]{:S(2)}, u32[]{:S(2)}) %collective-permute-start.39) | collective-permute-done | bytes 36896 | tf_op jit(solution)/shard_map/ppermute | solution.py:16
  180.8 3.8 %collective-permute-done.40 = bf16[36864]{0:T(1024)(128)(2,1)S(1)} collective-permute-done((bf16[36864]{0:T(1024)(128)(2,1)S(1)}, bf16[36864]{0:T(1024)(128)(2,1)S(1)}, u32[]{:S(2)}, u32[]{:S(2)}) %collective-permute-start.40) | collective-permute-done | bytes 73760 | tf_op jit(solution)/shard_map/ppermute | solution.py:16
  184.8 1.3 collective-permute-done.41
  186.9 1.0 convert_multiply_fusion.98
  (471 shorter events, 42.8 us)
Async XLA Ops:
  0.6 34.1 %copy-start = (bf16[1024,256]{1,0:T(8,128)(2,1)S(1)}, bf16[1024,256]{1,0:T(8,128)(2,1)}, u32[]{:S(2)}) copy-start(bf16[1024,256]{1,0:T(8,128)(2,1)} %param.23) | copy-start | bytes 1572868
  0.7 21.9 %copy-start.2 = (bf16[4,8,32,256]{3,2,1,0:T(8,128)(2,1)S(1)}, bf16[4,8,32,256]{3,2,1,0:T(8,128)(2,1)}, u32[]{:S(2)}) copy-start(bf16[4,8,32,256]{3,2,1,0:T(8,128)(2,1)} %param.13) | copy-start | bytes 1572868
  0.7 17.9 %copy-start.32 = (s32[8,32]{1,0:T(8,128)S(1)}, s32[8,32]{1,0:T(8,128)}, u32[]{:S(2)}) copy-start(s32[8,32]{1,0:T(8,128)} %param.16) | copy-start | bytes 3076
  1.7 10.8 %collective-permute-start = (bf16[4,8,3,256]{3,2,1,0:T(4,128)(2,1)S(1)}, bf16[4,8,3,256]{3,2,1,0:T(4,128)(2,1)S(1)}, u32[]{:S(2)}, u32[]{:S(2)}) collective-permute-start(bf16[4,8,3,256]{3,2,1,0:T(4,128)(2,1)S(1)} %slice.738), channel_id=1, source_target_pairs={{0,15},{1,14},{2,13},{3,12},{4,11},{5,10},{6,9},{7,8},{8,7},{9,6},... | collective-permute-start | bytes 147464 | tf_op jit(solution)/shard_map/ppermute | solution.py:180
  8.1 14.8 %copy-start.35 = (f32[1,1,256]{2,1,0:T(1,128)}, f32[1,1,256]{2,1,0:T(1,128)S(1)}, u32[]{:S(2)}) copy-start(f32[1,1,256]{2,1,0:T(1,128)S(1)} %get-tuple-element.154) | copy-start | bytes 3076
  8.1 14.8 %copy-start.37 = (f32[1,1,256]{2,1,0:T(1,128)}, f32[1,1,256]{2,1,0:T(1,128)S(1)}, u32[]{:S(2)}) copy-start(f32[1,1,256]{2,1,0:T(1,128)S(1)} %get-tuple-element.155) | copy-start | bytes 3076
  8.1 14.8 %copy-start.39 = (f32[1,1,256]{2,1,0:T(1,128)}, f32[1,1,256]{2,1,0:T(1,128)S(1)}, u32[]{:S(2)}) copy-start(f32[1,1,256]{2,1,0:T(1,128)S(1)} %get-tuple-element.156) | copy-start | bytes 3076
  8.1 14.8 %copy-start.41 = (f32[1,1,256]{2,1,0:T(1,128)}, f32[1,1,256]{2,1,0:T(1,128)S(1)}, u32[]{:S(2)}) copy-start(f32[1,1,256]{2,1,0:T(1,128)S(1)} %get-tuple-element.157) | copy-start | bytes 3076
  8.1 14.8 %copy-start.43 = (f32[1,1,256]{2,1,0:T(1,128)}, f32[1,1,256]{2,1,0:T(1,128)S(1)}, u32[]{:S(2)}) copy-start(f32[1,1,256]{2,1,0:T(1,128)S(1)} %get-tuple-element.158) | copy-start | bytes 3076
  8.2 14.8 %copy-start.45 = (f32[1,1,256]{2,1,0:T(1,128)}, f32[1,1,256]{2,1,0:T(1,128)S(1)}, u32[]{:S(2)}) copy-start(f32[1,1,256]{2,1,0:T(1,128)S(1)} %get-tuple-element.159) | copy-start | bytes 3076
  8.2 14.8 %copy-start.47 = (f32[1,1,256]{2,1,0:T(1,128)}, f32[1,1,256]{2,1,0:T(1,128)S(1)}, u32[]{:S(2)}) copy-start(f32[1,1,256]{2,1,0:T(1,128)S(1)} %get-tuple-element.160) | copy-start | bytes 3076
  8.2 14.8 %copy-start.49 = (f32[1,1,256]{2,1,0:T(1,128)}, f32[1,1,256]{2,1,0:T(1,128)S(1)}, u32[]{:S(2)}) copy-start(f32[1,1,256]{2,1,0:T(1,128)S(1)} %get-tuple-element.161) | copy-start | bytes 3076
  9.2 13.8 %copy-start.51 = (f32[1,1,256]{2,1,0:T(1,128)}, f32[1,1,256]{2,1,0:T(1,128)S(1)}, u32[]{:S(2)}) copy-start(f32[1,1,256]{2,1,0:T(1,128)S(1)} %get-tuple-element.113) | copy-start | bytes 3076
  9.2 13.8 %copy-start.53 = (f32[1,1,256]{2,1,0:T(1,128)}, f32[1,1,256]{2,1,0:T(1,128)S(1)}, u32[]{:S(2)}) copy-start(f32[1,1,256]{2,1,0:T(1,128)S(1)} %get-tuple-element.114) | copy-start | bytes 3076
  9.2 13.8 %copy-start.55 = (f32[1,1,256]{2,1,0:T(1,128)}, f32[1,1,256]{2,1,0:T(1,128)S(1)}, u32[]{:S(2)}) copy-start(f32[1,1,256]{2,1,0:T(1,128)S(1)} %get-tuple-element.115) | copy-start | bytes 3076
  9.2 13.8 %copy-start.57 = (f32[1,1,256]{2,1,0:T(1,128)}, f32[1,1,256]{2,1,0:T(1,128)S(1)}, u32[]{:S(2)}) copy-start(f32[1,1,256]{2,1,0:T(1,128)S(1)} %get-tuple-element.116) | copy-start | bytes 3076
  9.2 13.8 %copy-start.59 = (f32[1,1,256]{2,1,0:T(1,128)}, f32[1,1,256]{2,1,0:T(1,128)S(1)}, u32[]{:S(2)}) copy-start(f32[1,1,256]{2,1,0:T(1,128)S(1)} %get-tuple-element.117) | copy-start | bytes 3076
  9.2 13.8 %copy-start.61 = (f32[1,1,256]{2,1,0:T(1,128)}, f32[1,1,256]{2,1,0:T(1,128)S(1)}, u32[]{:S(2)}) copy-start(f32[1,1,256]{2,1,0:T(1,128)S(1)} %get-tuple-element.118) | copy-start | bytes 3076
  9.2 13.8 %copy-start.63 = (f32[1,1,256]{2,1,0:T(1,128)}, f32[1,1,256]{2,1,0:T(1,128)S(1)}, u32[]{:S(2)}) copy-start(f32[1,1,256]{2,1,0:T(1,128)S(1)} %get-tuple-element.119) | copy-start | bytes 3076
  9.2 13.8 %copy-start.65 = (f32[1,1,256]{2,1,0:T(1,128)}, f32[1,1,256]{2,1,0:T(1,128)S(1)}, u32[]{:S(2)}) copy-start(f32[1,1,256]{2,1,0:T(1,128)S(1)} %get-tuple-element.120) | copy-start | bytes 3076
  9.3 13.8 %copy-start.67 = (f32[1,1,256]{2,1,0:T(1,128)}, f32[1,1,256]{2,1,0:T(1,128)S(1)}, u32[]{:S(2)}) copy-start(f32[1,1,256]{2,1,0:T(1,128)S(1)} %get-tuple-element.121) | copy-start | bytes 3076
  9.3 13.8 %copy-start.69 = (f32[1,1,256]{2,1,0:T(1,128)}, f32[1,1,256]{2,1,0:T(1,128)S(1)}, u32[]{:S(2)}) copy-start(f32[1,1,256]{2,1,0:T(1,128)S(1)} %get-tuple-element.122) | copy-start | bytes 3076
  11.1 21.5 %copy-start.101 = (f32[1,1,256]{2,1,0:T(1,128)}, f32[1,1,256]{2,1,0:T(1,128)S(1)}, u32[]{:S(2)}) copy-start(f32[1,1,256]{2,1,0:T(1,128)S(1)} %get-tuple-element.138) | copy-start | bytes 3076
  14.0 8.5 %collective-permute-start.1 = (bf16[4,3,38,256]{3,2,1,0:T(8,128)(2,1)S(1)}, bf16[4,3,38,256]{3,2,1,0:T(8,128)(2,1)S(1)}, u32[]{:S(2)}, u32[]{:S(2)}) collective-permute-start(bf16[4,3,38,256]{3,2,1,0:T(8,128)(2,1)S(1)} %get-tuple-element.103), channel_id=1, source_target_pairs={{0,1},{1,2},{2,3},{3,4},{4,5},{5,6},{6,7},{7,8},{8,9},{9,10},{10,1... | collective-permute-start | bytes 700424 | tf_op jit(solution)/shard_map/ppermute | solution.py:26
  14.8 7.8 %collective-permute-start.2 = (bf16[4,3,38,256]{3,2,1,0:T(8,128)(2,1)S(1)}, bf16[4,3,38,256]{3,2,1,0:T(8,128)(2,1)S(1)}, u32[]{:S(2)}, u32[]{:S(2)}) collective-permute-start(bf16[4,3,38,256]{3,2,1,0:T(8,128)(2,1)S(1)} %get-tuple-element.104), channel_id=1, source_target_pairs={{1,0},{2,1},{3,2},{4,3},{5,4},{6,5},{7,6},{8,7},{9,8},{10,9},{11,1... | collective-permute-start | bytes 700424 | tf_op jit(solution)/shard_map/ppermute | solution.py:27
  71.3 10.9 %collective-permute-start.6 = (f32[12800]{0:T(1024)S(1)}, f32[12800]{0:T(1024)S(1)}, u32[]{:S(2)}, u32[]{:S(2)}) collective-permute-start(f32[12800]{0:T(1024)S(1)} %pad_maximum_fusion.12), channel_id=1, source_target_pairs={{0,1},{1,0},{2,3},{3,2},{4,5},{5,4},{6,7},{7,6},{8,9},{9,8},{10,11... | collective-permute-start | bytes 153608 | tf_op jit(solution)/shard_map/ppermute | solution.py:16
  76.0 25.1 %collective-permute-start.18 = (f32[73728]{0:T(1024)}, f32[73728]{0:T(1024)}, u32[]{:S(2)}, u32[]{:S(2)}) collective-permute-start(f32[73728]{0:T(1024)} %dynamic_slice.105), channel_id=1, source_target_pairs={{0,1},{1,0},{2,3},{3,2},{4,5},{5,4},{6,7},{7,6},{8,9},{9,8},{10,11... | collective-permute-start | bytes 884744 | tf_op jit(solution)/shard_map/ppermute | solution.py:16
  77.2 25.3 %collective-permute-start.26 = (f32[73728]{0:T(1024)}, f32[73728]{0:T(1024)}, u32[]{:S(2)}, u32[]{:S(2)}) collective-permute-start(f32[73728]{0:T(1024)} %dynamic_slice.113), channel_id=1, source_target_pairs={{0,1},{1,0},{2,3},{3,2},{4,5},{5,4},{6,7},{7,6},{8,9},{9,8},{10,11... | collective-permute-start | bytes 884744 | tf_op jit(solution)/shard_map/ppermute | solution.py:16
  77.7 29.3 %collective-permute-start.3 = (f32[4,3,32,256]{3,2,1,0:T(8,128)}, f32[4,3,32,256]{3,2,1,0:T(8,128)}, u32[]{:S(2)}, u32[]{:S(2)}) collective-permute-start(f32[4,3,32,256]{3,2,1,0:T(8,128)} %get-tuple-element.99), channel_id=1, source_target_pairs={{0,1},{1,2},{2,3},{3,4},{4,5},{5,6},{6,7},{7,8},{8,9},{9,10},{10,1... | collective-permute-start | bytes 1179656 | tf_op jit(solution)/shard_map/ppermute | solution.py:26
  77.7 29.3 %collective-permute-start.4 = (f32[4,3,32,256]{3,2,1,0:T(8,128)}, f32[4,3,32,256]{3,2,1,0:T(8,128)}, u32[]{:S(2)}, u32[]{:S(2)}) collective-permute-start(f32[4,3,32,256]{3,2,1,0:T(8,128)} %get-tuple-element.100), channel_id=1, source_target_pairs={{1,0},{2,1},{3,2},{4,3},{5,4},{6,5},{7,6},{8,7},{9,8},{10,9},{11,1... | collective-permute-start | bytes 1179656 | tf_op jit(solution)/shard_map/ppermute | solution.py:27
  82.2 8.3 %collective-permute-start.7 = (f32[12800]{0:T(1024)S(1)}, f32[12800]{0:T(1024)S(1)}, u32[]{:S(2)}, u32[]{:S(2)}) collective-permute-start(f32[12800]{0:T(1024)S(1)} %fusion.267), channel_id=1, source_target_pairs={{0,2},{1,3},{2,0},{3,1},{4,6},{5,7},{6,4},{7,5},{8,10},{9,11},{10,... | collective-permute-start | bytes 153608 | tf_op jit(solution)/shard_map/ppermute | solution.py:16
  90.5 4.2 %collective-permute-start.8 = (f32[12800]{0:T(1024)S(1)}, f32[12800]{0:T(1024)S(1)}, u32[]{:S(2)}, u32[]{:S(2)}) collective-permute-start(f32[12800]{0:T(1024)S(1)} %add.847), channel_id=1, source_target_pairs={{0,4},{1,5},{2,6},{3,7},{4,0},{5,1},{6,2},{7,3},{8,12},{9,13},{10,... | collective-permute-start | bytes 153608 | tf_op jit(solution)/shard_map/ppermute | solution.py:16
  94.7 5.1 %collective-permute-start.9 = (f32[12800]{0:T(1024)S(1)}, f32[12800]{0:T(1024)S(1)}, u32[]{:S(2)}, u32[]{:S(2)}) collective-permute-start(f32[12800]{0:T(1024)S(1)} %add.848), channel_id=1, source_target_pairs={{0,8},{1,9},{2,10},{3,11},{4,12},{5,13},{6,14},{7,15},{8,0},{9,1},... | collective-permute-start | bytes 153608 | tf_op jit(solution)/shard_map/ppermute | solution.py:16
  99.9 5.5 %collective-permute-start.10 = (f32[73728]{0:T(1024)}, f32[73728]{0:T(1024)S(1)}, u32[]{:S(2)}, u32[]{:S(2)}) collective-permute-start(f32[73728]{0:T(1024)} %dynamic_slice.97), channel_id=1, source_target_pairs={{0,1},{1,0},{2,3},{3,2},{4,5},{5,4},{6,7},{7,6},{8,9},{9,8},{10,11... | collective-permute-start | bytes 884744 | tf_op jit(solution)/shard_map/ppermute | solution.py:16
  102.2 21.0 %collective-permute-start.19 = (f32[36864]{0:T(1024)S(1)}, f32[36864]{0:T(1024)S(1)}, u32[]{:S(2)}, u32[]{:S(2)}) collective-permute-start(f32[36864]{0:T(1024)S(1)} %dynamic_slice.107), channel_id=1, source_target_pairs={{0,2},{1,3},{2,0},{3,1},{4,6},{5,7},{6,4},{7,5},{8,10},{9,11},{10,... | collective-permute-start | bytes 442376 | tf_op jit(solution)/shard_map/ppermute | solution.py:16
  103.5 21.4 %collective-permute-start.27 = (f32[36864]{0:T(1024)S(1)}, f32[36864]{0:T(1024)S(1)}, u32[]{:S(2)}, u32[]{:S(2)}) collective-permute-start(f32[36864]{0:T(1024)S(1)} %dynamic_slice.115), channel_id=1, source_target_pairs={{0,2},{1,3},{2,0},{3,1},{4,6},{5,7},{6,4},{7,5},{8,10},{9,11},{10,... | collective-permute-start | bytes 442376 | tf_op jit(solution)/shard_map/ppermute | solution.py:16
  106.4 21.1 %collective-permute-start.11 = (f32[36864]{0:T(1024)}, f32[36864]{0:T(1024)}, u32[]{:S(2)}, u32[]{:S(2)}) collective-permute-start(f32[36864]{0:T(1024)} %dynamic_slice.99), channel_id=1, source_target_pairs={{0,4},{1,5},{2,6},{3,7},{4,0},{5,1},{6,2},{7,3},{8,12},{9,13},{10,... | collective-permute-start | bytes 442376 | tf_op jit(solution)/shard_map/ppermute | solution.py:16
  119.3 7.2 %collective-permute-start.5 = (bf16[4,8,3,256]{3,2,1,0:T(4,128)(2,1)S(1)}, bf16[4,8,3,256]{3,2,1,0:T(4,128)(2,1)}, u32[]{:S(2)}, u32[]{:S(2)}) collective-permute-start(bf16[4,8,3,256]{3,2,1,0:T(4,128)(2,1)S(1)} %slice.1540), channel_id=1, source_target_pairs={{0,15},{1,14},{2,13},{3,12},{4,11},{5,10},{6,9},{7,8},{8,7},{9,6},... | collective-permute-start | bytes 147464 | tf_op jit(solution)/shard_map/ppermute | solution.py:180
  122.5 31.6 %collective-permute-start.34 = (f32[73728]{0:T(1024)}, f32[73728]{0:T(1024)}, u32[]{:S(2)}, u32[]{:S(2)}) collective-permute-start(f32[73728]{0:T(1024)} %dynamic_slice.121), channel_id=1, source_target_pairs={{0,1},{1,0},{2,3},{3,2},{4,5},{5,4},{6,7},{7,6},{8,9},{9,8},{10,11... | collective-permute-start | bytes 884744 | tf_op jit(solution)/shard_map/ppermute | solution.py:16
  123.8 7.2 %collective-permute-start.20 = (f32[18432]{0:T(1024)}, f32[18432]{0:T(1024)S(1)}, u32[]{:S(2)}, u32[]{:S(2)}) collective-permute-start(f32[18432]{0:T(1024)} %dynamic_slice.109), channel_id=1, source_target_pairs={{0,4},{1,5},{2,6},{3,7},{4,0},{5,1},{6,2},{7,3},{8,12},{9,13},{10,... | collective-permute-start | bytes 221192 | tf_op jit(solution)/shard_map/ppermute | solution.py:16
  125.6 6.8 %collective-permute-start.28 = (f32[18432]{0:T(1024)}, f32[18432]{0:T(1024)S(1)}, u32[]{:S(2)}, u32[]{:S(2)}) collective-permute-start(f32[18432]{0:T(1024)} %dynamic_slice.117), channel_id=1, source_target_pairs={{0,4},{1,5},{2,6},{3,7},{4,0},{5,1},{6,2},{7,3},{8,12},{9,13},{10,... | collective-permute-start | bytes 221192 | tf_op jit(solution)/shard_map/ppermute | solution.py:16
  128.5 5.7 %collective-permute-start.12 = (f32[18432]{0:T(1024)S(1)}, f32[18432]{0:T(1024)S(1)}, u32[]{:S(2)}, u32[]{:S(2)}) collective-permute-start(f32[18432]{0:T(1024)S(1)} %dynamic_slice.101), channel_id=1, source_target_pairs={{0,2},{1,3},{2,0},{3,1},{4,6},{5,7},{6,4},{7,5},{8,10},{9,11},{10,... | collective-permute-start | bytes 221192 | tf_op jit(solution)/shard_map/ppermute | solution.py:16
  131.1 6.2 %collective-permute-start.21 = (f32[9216]{0:T(1024)S(1)}, f32[9216]{0:T(1024)S(1)}, u32[]{:S(2)}, u32[]{:S(2)}) collective-permute-start(f32[9216]{0:T(1024)S(1)} %dynamic_slice.111), channel_id=1, source_target_pairs={{0,8},{1,9},{2,10},{3,11},{4,12},{5,13},{6,14},{7,15},{8,0},{9,1},... | collective-permute-start | bytes 110600 | tf_op jit(solution)/shard_map/ppermute | solution.py:16
  132.5 6.2 %collective-permute-start.29 = (f32[9216]{0:T(1024)S(1)}, f32[9216]{0:T(1024)S(1)}, u32[]{:S(2)}, u32[]{:S(2)}) collective-permute-start(f32[9216]{0:T(1024)S(1)} %dynamic_slice.119), channel_id=1, source_target_pairs={{0,8},{1,9},{2,10},{3,11},{4,12},{5,13},{6,14},{7,15},{8,0},{9,1},... | collective-permute-start | bytes 110600 | tf_op jit(solution)/shard_map/ppermute | solution.py:16
  134.2 6.2 %collective-permute-start.13 = (f32[9216]{0:T(1024)S(1)}, f32[9216]{0:T(1024)S(1)}, u32[]{:S(2)}, u32[]{:S(2)}) collective-permute-start(f32[9216]{0:T(1024)S(1)} %dynamic_slice.103), channel_id=1, source_target_pairs={{0,8},{1,9},{2,10},{3,11},{4,12},{5,13},{6,14},{7,15},{8,0},{9,1},... | collective-permute-start | bytes 110600 | tf_op jit(solution)/shard_map/ppermute | solution.py:16
  137.3 4.7 %collective-permute-start.22 = (bf16[9216]{0:T(1024)(128)(2,1)S(1)}, bf16[9216]{0:T(1024)(128)(2,1)S(1)}, u32[]{:S(2)}, u32[]{:S(2)}) collective-permute-start(bf16[9216]{0:T(1024)(128)(2,1)S(1)} %add_convert_fusion.3), channel_id=1, source_target_pairs={{0,8},{1,9},{2,10},{3,11},{4,12},{5,13},{6,14},{7,15},{8,0},{9,1},... | collective-permute-start | bytes 55304 | tf_op jit(solution)/shard_map/ppermute | solution.py:16
  138.7 4.7 %collective-permute-start.30 = (bf16[9216]{0:T(1024)(128)(2,1)S(1)}, bf16[9216]{0:T(1024)(128)(2,1)S(1)}, u32[]{:S(2)}, u32[]{:S(2)}) collective-permute-start(bf16[9216]{0:T(1024)(128)(2,1)S(1)} %add_convert_fusion.2), channel_id=1, source_target_pairs={{0,8},{1,9},{2,10},{3,11},{4,12},{5,13},{6,14},{7,15},{8,0},{9,1},... | collective-permute-start | bytes 55304 | tf_op jit(solution)/shard_map/ppermute | solution.py:16
  140.4 4.7 %collective-permute-start.14 = (bf16[9216]{0:T(1024)(128)(2,1)S(1)}, bf16[9216]{0:T(1024)(128)(2,1)S(1)}, u32[]{:S(2)}, u32[]{:S(2)}) collective-permute-start(bf16[9216]{0:T(1024)(128)(2,1)S(1)} %add_convert_fusion.4), channel_id=1, source_target_pairs={{0,8},{1,9},{2,10},{3,11},{4,12},{5,13},{6,14},{7,15},{8,0},{9,1},... | collective-permute-start | bytes 55304 | tf_op jit(solution)/shard_map/ppermute | solution.py:16
  142.1 4.0 %collective-permute-start.23 = (bf16[18432]{0:T(1024)(128)(2,1)S(1)}, bf16[18432]{0:T(1024)(128)(2,1)S(1)}, u32[]{:S(2)}, u32[]{:S(2)}) collective-permute-start(bf16[18432]{0:T(1024)(128)(2,1)S(1)} %maximum_select_fusion.23), channel_id=1, source_target_pairs={{0,4},{1,5},{2,6},{3,7},{4,0},{5,1},{6,2},{7,3},{8,12},{9,13},{10,... | collective-permute-start | bytes 110600 | tf_op jit(solution)/shard_map/ppermute | solution.py:16
  143.5 4.2 %collective-permute-start.31 = (bf16[18432]{0:T(1024)(128)(2,1)S(1)}, bf16[18432]{0:T(1024)(128)(2,1)S(1)}, u32[]{:S(2)}, u32[]{:S(2)}) collective-permute-start(bf16[18432]{0:T(1024)(128)(2,1)S(1)} %maximum_select_fusion.24), channel_id=1, source_target_pairs={{0,4},{1,5},{2,6},{3,7},{4,0},{5,1},{6,2},{7,3},{8,12},{9,13},{10,... | collective-permute-start | bytes 110600 | tf_op jit(solution)/shard_map/ppermute | solution.py:16
  145.1 4.0 %collective-permute-start.15 = (bf16[18432]{0:T(1024)(128)(2,1)S(1)}, bf16[18432]{0:T(1024)(128)(2,1)S(1)}, u32[]{:S(2)}, u32[]{:S(2)}) collective-permute-start(bf16[18432]{0:T(1024)(128)(2,1)S(1)} %maximum_select_fusion.22), channel_id=1, source_target_pairs={{0,2},{1,3},{2,0},{3,1},{4,6},{5,7},{6,4},{7,5},{8,10},{9,11},{10,... | collective-permute-start | bytes 110600 | tf_op jit(solution)/shard_map/ppermute | solution.py:16
  146.1 4.4 %collective-permute-start.24 = (bf16[36864]{0:T(1024)(128)(2,1)S(1)}, bf16[36864]{0:T(1024)(128)(2,1)S(1)}, u32[]{:S(2)}, u32[]{:S(2)}) collective-permute-start(bf16[36864]{0:T(1024)(128)(2,1)S(1)} %maximum_select_fusion.17), channel_id=1, source_target_pairs={{0,2},{1,3},{2,0},{3,1},{4,6},{5,7},{6,4},{7,5},{8,10},{9,11},{10,... | collective-permute-start | bytes 221192 | tf_op jit(solution)/shard_map/ppermute | solution.py:16
  147.7 4.4 %collective-permute-start.32 = (bf16[36864]{0:T(1024)(128)(2,1)S(1)}, bf16[36864]{0:T(1024)(128)(2,1)S(1)}, u32[]{:S(2)}, u32[]{:S(2)}) collective-permute-start(bf16[36864]{0:T(1024)(128)(2,1)S(1)} %maximum_select_fusion.19), channel_id=1, source_target_pairs={{0,2},{1,3},{2,0},{3,1},{4,6},{5,7},{6,4},{7,5},{8,10},{9,11},{10,... | collective-permute-start | bytes 221192 | tf_op jit(solution)/shard_map/ppermute | solution.py:16
  149.2 4.4 %collective-permute-start.16 = (bf16[36864]{0:T(1024)(128)(2,1)S(1)}, bf16[36864]{0:T(1024)(128)(2,1)S(1)}, u32[]{:S(2)}, u32[]{:S(2)}) collective-permute-start(bf16[36864]{0:T(1024)(128)(2,1)S(1)} %maximum_select_fusion.16), channel_id=1, source_target_pairs={{0,4},{1,5},{2,6},{3,7},{4,0},{5,1},{6,2},{7,3},{8,12},{9,13},{10,... | collective-permute-start | bytes 221192 | tf_op jit(solution)/shard_map/ppermute | solution.py:16
  150.6 12.2 %collective-permute-start.25 = (bf16[73728]{0:T(1024)(128)(2,1)S(1)}, bf16[73728]{0:T(1024)(128)(2,1)S(1)}, u32[]{:S(2)}, u32[]{:S(2)}) collective-permute-start(bf16[73728]{0:T(1024)(128)(2,1)S(1)} %maximum_select_fusion.8), channel_id=1, source_target_pairs={{0,1},{1,0},{2,3},{3,2},{4,5},{5,4},{6,7},{7,6},{8,9},{9,8},{10,11... | collective-permute-start | bytes 442376 | tf_op jit(solution)/shard_map/ppermute | solution.py:16
  152.2 25.2 %collective-permute-start.33 = (bf16[73728]{0:T(1024)(128)(2,1)S(1)}, bf16[73728]{0:T(1024)(128)(2,1)S(1)}, u32[]{:S(2)}, u32[]{:S(2)}) collective-permute-start(bf16[73728]{0:T(1024)(128)(2,1)S(1)} %maximum_select_fusion.11), channel_id=1, source_target_pairs={{0,1},{1,0},{2,3},{3,2},{4,5},{5,4},{6,7},{7,6},{8,9},{9,8},{10,11... | collective-permute-start | bytes 442376 | tf_op jit(solution)/shard_map/ppermute | solution.py:16
  153.6 2.3 %collective-permute-start.17 = (bf16[73728]{0:T(1024)(128)(2,1)S(1)}, bf16[73728]{0:T(1024)(128)(2,1)S(1)}, u32[]{:S(2)}, u32[]{:S(2)}) collective-permute-start(bf16[73728]{0:T(1024)(128)(2,1)S(1)} %maximum_select_fusion.6), channel_id=1, source_target_pairs={{0,1},{1,0},{2,3},{3,2},{4,5},{5,4},{6,7},{7,6},{8,9},{9,8},{10,11... | collective-permute-start | bytes 442376 | tf_op jit(solution)/shard_map/ppermute | solution.py:16
  155.1 6.3 %collective-permute-start.35 = (f32[36864]{0:T(1024)S(1)}, f32[36864]{0:T(1024)S(1)}, u32[]{:S(2)}, u32[]{:S(2)}) collective-permute-start(f32[36864]{0:T(1024)S(1)} %dynamic_slice.123), channel_id=1, source_target_pairs={{0,4},{1,5},{2,6},{3,7},{4,0},{5,1},{6,2},{7,3},{8,12},{9,13},{10,... | collective-permute-start | bytes 442376 | tf_op jit(solution)/shard_map/ppermute | solution.py:16
  161.4 4.4 %collective-permute-start.36 = (f32[18432]{0:T(1024)S(1)}, f32[18432]{0:T(1024)S(1)}, u32[]{:S(2)}, u32[]{:S(2)}) collective-permute-start(f32[18432]{0:T(1024)S(1)} %dynamic_slice.125), channel_id=1, source_target_pairs={{0,2},{1,3},{2,0},{3,1},{4,6},{5,7},{6,4},{7,5},{8,10},{9,11},{10,... | collective-permute-start | bytes 221192 | tf_op jit(solution)/shard_map/ppermute | solution.py:16
  165.9 5.3 %collective-permute-start.37 = (f32[9216]{0:T(1024)S(1)}, f32[9216]{0:T(1024)S(1)}, u32[]{:S(2)}, u32[]{:S(2)}) collective-permute-start(f32[9216]{0:T(1024)S(1)} %dynamic_slice.127), channel_id=1, source_target_pairs={{0,8},{1,9},{2,10},{3,11},{4,12},{5,13},{6,14},{7,15},{8,0},{9,1},... | collective-permute-start | bytes 110600 | tf_op jit(solution)/shard_map/ppermute | solution.py:16
  171.2 4.9 %collective-permute-start.38 = (bf16[9216]{0:T(1024)(128)(2,1)S(1)}, bf16[9216]{0:T(1024)(128)(2,1)S(1)}, u32[]{:S(2)}, u32[]{:S(2)}) collective-permute-start(bf16[9216]{0:T(1024)(128)(2,1)S(1)} %add_convert_fusion.1), channel_id=1, source_target_pairs={{0,8},{1,9},{2,10},{3,11},{4,12},{5,13},{6,14},{7,15},{8,0},{9,1},... | collective-permute-start | bytes 55304 | tf_op jit(solution)/shard_map/ppermute | solution.py:16
  176.1 4.0 %collective-permute-start.39 = (bf16[18432]{0:T(1024)(128)(2,1)S(1)}, bf16[18432]{0:T(1024)(128)(2,1)S(1)}, u32[]{:S(2)}, u32[]{:S(2)}) collective-permute-start(bf16[18432]{0:T(1024)(128)(2,1)S(1)} %maximum_select_fusion.25), channel_id=1, source_target_pairs={{0,2},{1,3},{2,0},{3,1},{4,6},{5,7},{6,4},{7,5},{8,10},{9,11},{10,... | collective-permute-start | bytes 110600 | tf_op jit(solution)/shard_map/ppermute | solution.py:16
  180.2 4.4 %collective-permute-start.40 = (bf16[36864]{0:T(1024)(128)(2,1)S(1)}, bf16[36864]{0:T(1024)(128)(2,1)S(1)}, u32[]{:S(2)}, u32[]{:S(2)}) collective-permute-start(bf16[36864]{0:T(1024)(128)(2,1)S(1)} %maximum_select_fusion.21), channel_id=1, source_target_pairs={{0,4},{1,5},{2,6},{3,7},{4,0},{5,1},{6,2},{7,3},{8,12},{9,13},{10,... | collective-permute-start | bytes 221192 | tf_op jit(solution)/shard_map/ppermute | solution.py:16
  184.6 1.4 collective-permute-start.41
  (118 other events, 661.5 us)

commit v3 on v2

--- a/solution.py
+++ b/solution.py
@@ -256,9 +256,32 @@
 ):
     members, lon_dev, lat_rows, chans = features.shape
     params = (dw_kernel, dw_bias, ln_gain, ln_bias, w_in, b_in, w_out, b_out, layer_scale)
-    north_rows = mirror_rows(features[:, :, lat_rows - 3 :, :])
-    joined = jnp.concatenate([south_rim, features, north_rows], axis=2)
-    extended = with_halo(joined, (("lon", 1),), 3)
+    top_rows = features[:, :, lat_rows - 3 :, :]
+    north_rows = mirror_rows(top_rows)
+    joined = jnp.concatenate([south_rim, features], axis=2)
+    lon_size = lax.axis_size("lon")
+    before = lax.ppermute(
+        joined[:, lon_dev - 3 :], "lon", [(i, (i + 1) % lon_size) for i in range(lon_size)]
+    )
+    after = lax.ppermute(
+        joined[:, :3], "lon", [((i + 1) % lon_size, i) for i in range(lon_size)]
+    )
+    north_before = lax.ppermute(
+        top_rows[:, :3], "lon", [(i, (lon_size - i) % lon_size) for i in range(lon_size)]
+    )[:, ::-1, ::-1, :]
+    north_after = lax.ppermute(
+        top_rows[:, lon_dev - 3 :],
+        "lon",
+        [(i, (2 * lon_size - 2 - i) % lon_size) for i in range(lon_size)],
+    )[:, ::-1, ::-1, :]
+    extended = jnp.concatenate(
+        [
+            jnp.concatenate([before, north_before], axis=2),
+            jnp.concatenate([joined, north_rows], axis=2),
+            jnp.concatenate([after, north_after], axis=2),
+        ],
+        axis=1,
+    )
     predicted, crps_field, grad_pred, grad_depth, grads = local_step(
         extended, features, target, kmt, *params
     )
@@ -294,13 +317,8 @@
         scale_sum,
     ) = grads
     lon_size = lax.axis_size("lon")
-    early = (w_out_sum, b_out_sum, scale_sum)
-    early_tot = unpack(
-        split_allreduce(pack(early, lon_size * 2048), "lon", jnp.bfloat16), early
-    )
-    late = (w_in_sum, b_in_sum, gain_sum, bias_sum)
-    late_tot = unpack(split_allreduce(pack(late, lon_size * 2048), "lon", jnp.bfloat16), late)
-    big_tot = (late_tot[0], early_tot[0], late_tot[1], early_tot[1], early_tot[2], late_tot[2], late_tot[3])
+    big = (w_in_sum, w_out_sum, b_in_sum, b_out_sum, scale_sum, gain_sum, bias_sum)
+    big_tot = unpack(split_allreduce(pack(big, lon_size * 2048), "lon", jnp.bfloat16), big)
     small = (kernel_sum, dw_bias_sum)
     small_tot = unpack(butterfly_allreduce(pack(small, 128), "lon"), small)
     totals = (

time: 189 us -> 197 us (1.042)
  starting transfers between devices: 42.2 us -> 34.6 us
  waiting for transfers between devices: 49 us -> 55.9 us
  local copies, waits for them, and re-layouts: 22.1 us -> 27 us
  other arithmetic: 52.6 us -> 56.4 us
    ppermute x0 -> x4, starting transfers between devices: none -> 14.6 us  [the longest x1 9.35 us: on_device(): lax.ppermute(top_rows[:, lon_dev - 3:], 'lon', [(i, (2 * lon_size - 2 - i...]
    ppermute x36 -> x20, starting transfers between devices: 26.8 us -> 15.4 us  [swapped(): lax.ppermute(x, axis, [(i, i ^ 1 << bit) for i in range(lax.axis_size(axi...]
    ppermute x36 -> x20, waiting for transfers between devices: 45.8 us -> 54.9 us  [swapped(): lax.ppermute(x, axis, [(i, i ^ 1 << bit) for i in range(lax.axis_size(axi...]
    ppermute x2, starting transfers between devices: 6.53 us -> 0.14 us  [mirrored(): return lax.ppermute(x, axis, [(i, size - 1 - i) for i in range(size)])]
    unnamed x293 -> x261, local copies, waits for them, and re-layouts: 5.93 us -> 12 us
    dynamic_slice x16 -> x7, local copies, waits for them, and re-layouts: 5.14 us -> 0.97 us  [halving_allreduce(): send = lax.dynamic_slice_in_dim(cur, (1 - mine) * half, half)]
    ppermute x2 -> x1, starting transfers between devices: 8.16 us -> 4 us  [with_halo(): after = lax.ppermute(leading, axis, down)]
    ppermute x2 -> x1, waiting for transfers between devices: 3.19 us -> 0.01 us  [with_halo(): before = lax.ppermute(last, axis, up)]
  transfers between devices with their start and end apart: 42 -> 28, of which waited for: 22 -> 14; matrix products, arithmetic and copies ran while one was open for 21% -> 21% of each run, Pallas kernels for 0% -> 0%
where the time goes in v3:
time: 197 us; the launch traced here: 196 us
  other arithmetic  56.4 us (29%)
  waiting for transfers between devices  55.9 us (28%)
  starting transfers between devices  34.6 us (18%)
  local copies, waits for them, and re-layouts  27 us (14%)
  matrix products  18.6 us (9%)
  between operations  3.03 us (2%)
    ppermute x20, waiting for transfers between devices, swapped(): lax.ppermute(x, axis, [(i, i ^ 1 << bit) for i in range(lax.axis_size(axi...  54.9 us
    ppermute x20, starting transfers between devices, swapped(): lax.ppermute(x, axis, [(i, i ^ 1 << bit) for i in range(lax.axis_size(axi...  15.4 us
    unnamed x261, local copies, waits for them, and re-layouts  12 us
    reduce_sum x4, other arithmetic, local_step(): jnp.sum(grad_depth * extended[:, lon_off:lon_off + lon_dev, lat_off:lat_o...  10.6 us
    add x1, other arithmetic, on_device(): grad_ext + dw_kernel[lon_off, lat_off] * padded[:, 6 - lon_off:6 - lon_of...  10.3 us
    ppermute x1, starting transfers between devices, on_device(): lax.ppermute(top_rows[:, lon_dev - 3:], 'lon', [(i, (2 * lon_size - 2 - i...  9.35 us
    reduce_sum x1, other arithmetic, local_step(): mean_val = jnp.mean(depth, axis=-1, keepdims=True)  9.24 us
    dot_general x4, matrix products, local_step(): lax.dot_general(out_half, w_out, contract_cols, preferred_element_type=jn...  5.97 us
  transfers between devices with their start and end apart: 28, of which 14 were waited for; matrix products, arithmetic and copies ran while one was open for 21% of the time, Pallas kernels for 0%

profile of v3, /device:TPU:0, one launch (start us, length us, event | category | flops | bytes accessed | tf_op | source)
XLA Modules:
  0.0 195.5 jit_solution(16251881908061011695)
XLA Ops:
  0.7 0.9 fusion.220
  2.3 9.4 %collective-permute-start.4 = (bf16[4,3,3,256]{3,2,1,0:T(4,128)(2,1)S(1)}, bf16[4,3,3,256]{3,2,1,0:T(4,128)(2,1)S(1)}, u32[]{:S(2)}, u32[]{:S(2)}) collective-permute-start(bf16[4,3,3,256]{3,2,1,0:T(4,128)(2,1)S(1)} %get-tuple-element.114), channel_id=1, source_target_pairs={{0,14},{1,13},{2,12},{3,11},{4,10},{5,9},{6,8},{7,7},{8,6},{9,5},{... | collective-permute-start | bytes 55304 | tf_op jit(solution)/shard_map/ppermute | solution.py:272
  11.7 0.9 slice.731
  13.5 1.2 fusion.197
  14.9 4.4 %collective-permute-start.3 = (bf16[4,3,35,256]{3,2,1,0:T(8,128)(2,1)S(1)}, bf16[4,3,35,256]{3,2,1,0:T(8,128)(2,1)S(1)}, u32[]{:S(2)}, u32[]{:S(2)}) collective-permute-start(bf16[4,3,35,256]{3,2,1,0:T(8,128)(2,1)S(1)} %get-tuple-element.108), channel_id=1, source_target_pairs={{1,0},{2,1},{3,2},{4,3},{5,4},{6,5},{7,6},{8,7},{9,8},{10,9},{11,1... | collective-permute-start | bytes 645128 | tf_op jit(solution)/shard_map/ppermute | solution.py:266
  22.2 1.0 collective-permute-done
  24.1 9.2 %fusion.216 = (f32[4,8,32]{2,1,0:T(8,128)S(1)}, f32[4,8,32,256]{3,2,1,0:T(8,128)S(1)}) fusion(bf16[4,11,38,256]{3,2,1,0:T(8,128)(2,1)S(1)} %get-tuple-element.106, f32[256]{0:T(256)} %bitcast.48, f32[256]{0:T(256)} %bitcast.47, f32[256]{0:T(256)S(1)} %bitcast.344, f32[256]{0:T(256)S(1)} %bitcast.346, f32[256]{0:T(256)S(1)} %bitcast.348, ...), kind=kLoop, calls=%fused_computation.516 | loop fusion | flops 43514880 | bytes 23746560 | tf_op jit(solution)/shard_map/reduce_sum | solution.py:62
  38.3 1.1 fusion.214
  39.4 3.8 %multiply_reduce_fusion.7 = (f32[256]{0:T(256)}, f32[256]{0:T(256)}, f32[256]{0:T(256)}, f32[256]{0:T(256)}, f32[8,32,256]{2,1,0:T(8,128)S(1)}, /*index=5*/f32[8...) fusion(f32[256]{0:T(256)S(1)} %copy-done.33, ...), kind=kLoop, calls=%fused_computation.453 | loop fusion | flops 7863296 | bytes 2497536 | tf_op jit(solution)/shard_map/reduce_sum | solution.py:117
  43.3 1.5 fusion.208
  45.4 1.5 fusion.206
  46.8 0.9 fusion.227
  47.7 1.5 fusion.210
  49.2 1.5 fusion.212
  50.7 0.9 fusion.224
  51.6 0.9 fusion.225
  52.5 0.9 fusion.226
  53.4 0.9 multiply_reduce_fusion
  54.4 4.1 %fusion.147 = (f32[256]{0:T(256)}, f32[256]{0:T(256)}, f32[256]{0:T(256)}, f32[256]{0:T(256)}, f32[256]{0:T(256)}, /*index=5*/f32[256]{0:T(256)}, f32[256]{0:T(2...) fusion(bf16[4,11,38,256]{3,2,1,0:T(8,128)(2,1)S(1)} %get-tuple-, ...), kind=kLoop, calls=%fused_computation.330 | loop fusion | flops 16772608 | bytes 12618752 | tf_op jit(solution)/shard_map/reduce_sum | solution.py:154
  58.4 2.4 %fusion.129 = (f32[256]{0:T(256)}, f32[256]{0:T(256)}, f32[256]{0:T(256)}, f32[256]{0:T(256)S(1)}, f32[256]{0:T(256)}, /*index=5*/f32[256]{0:T(256)}, f32[256]{0...) fusion(f32[4,8,32,256]{3,2,1,0:T(8,128)S(1)} %get-tuple-element.91, ...), kind=kLoop, calls=%fused_computation.312 | loop fusion | flops 12842240 | bytes 3255296 | tf_op jit(solution)/shard_map/reduce_sum | solution.py:154
  60.8 1.0 fusion.78
  61.8 3.2 %fusion.96 = (f32[256]{0:T(256)}, f32[256]{0:T(256)}, f32[256]{0:T(256)}, f32[256]{0:T(256)}, f32[256]{0:T(256)}, /*index=5*/f32[256]{0:T(256)}, f32[256]{0:T(25...) fusion(f32[4,8,32,256]{3,2,1,0:T(8,128)S(1)} %get-tuple-element, ...), kind=kLoop, calls=%fused_computation.279 | loop fusion | flops 14151168 | bytes 10504192 | tf_op jit(solution)/shard_map/reduce_sum | solution.py:154
  65.0 1.3 fusion.193
  77.9 1.4 reshape.188
  80.1 2.4 %collective-permute-start.8 = (f32[12800]{0:T(1024)S(1)}, f32[12800]{0:T(1024)S(1)}, u32[]{:S(2)}, u32[]{:S(2)}) collective-permute-start(f32[12800]{0:T(1024)S(1)} %pad_maximum_fusion.9), channel_id=1, source_target_pairs={{0,1},{1,0},{2,3},{3,2},{4,5},{5,4},{6,7},{7,6},{8,9},{9,8},{10,11... | collective-permute-start | bytes 153608 | tf_op jit(solution)/shard_map/ppermute | solution.py:16
  82.5 1.7 convolution_add_fusion.5
  85.9 1.2 constant_dynamic-update-slice_fusion.7
  87.1 1.1 fusion.174
  88.1 0.9 fusion.218
  89.7 4.0 %collective-permute-start.6 = (f32[4,3,32,256]{3,2,1,0:T(8,128)}, f32[4,3,32,256]{3,2,1,0:T(8,128)}, u32[]{:S(2)}, u32[]{:S(2)}) collective-permute-start(f32[4,3,32,256]{3,2,1,0:T(8,128)} %get-tuple-element.104), channel_id=1, source_target_pairs={{1,0},{2,1},{3,2},{4,3},{5,4},{6,5},{7,6},{8,7},{9,8},{10,9},{11,1... | collective-permute-start | bytes 1179656 | tf_op jit(solution)/shard_map/ppermute | solution.py:27
  93.8 1.1 constant_dynamic-update-slice_fusion.13
  94.9 8.7 %collective-permute-done.9 = f32[12800]{0:T(1024)S(1)} collective-permute-done((f32[12800]{0:T(1024)S(1)}, f32[12800]{0:T(1024)S(1)}, u32[]{:S(2)}, u32[]{:S(2)}) %collective-permute-start.9) | collective-permute-done | bytes 51232 | tf_op jit(solution)/shard_map/ppermute | solution.py:16
  104.4 3.5 %collective-permute-done.10 = f32[12800]{0:T(1024)S(1)} collective-permute-done((f32[12800]{0:T(1024)S(1)}, f32[12800]{0:T(1024)S(1)}, u32[]{:S(2)}, u32[]{:S(2)}) %collective-permute-start.10) | collective-permute-done | bytes 51232 | tf_op jit(solution)/shard_map/ppermute | solution.py:16
  108.0 1.3 constant_dynamic-update-slice_fusion.11
  109.3 4.0 %collective-permute-done.11 = f32[12800]{0:T(1024)S(1)} collective-permute-done((f32[12800]{0:T(1024)S(1)}, f32[12800]{0:T(1024)S(1)}, u32[]{:S(2)}, u32[]{:S(2)}) %collective-permute-start.11) | collective-permute-done | bytes 51232 | tf_op jit(solution)/shard_map/ppermute | solution.py:16
  114.9 1.5 select_maximum_fusion
  116.8 10.3 %fusion.3 = f32[4,8,38,256]{3,2,1,0:T(8,128)S(1)} fusion(f32[4,14,44,256]{3,2,1,0:T(8,128)S(1)} %select_maximum_fusion, f32[256]{0:T(256)} %bitcast.48, f32[256]{0:T(256)} %bitcast.47, f32[256]{0:T(256)S(1)} %bitcast.345, f32[256]{0:T(256)S(1)} %bitcast.347, f32[256]{0:T(256)S(1)} %bitcast.349, f32[256]{0:T(256)S(1)} %bitcast.351, f32[256]{0:T(256)S(1)} %bitcast.353, ...), kind=kLoop, calls=%fused_computation.126 | loop fusion | flops 30195712 | bytes 62309376 | tf_op jit(solution)/shard_map/add | solution.py:294
  127.7 1.3 constant_dynamic-update-slice_fusion.10
  129.0 1.3 constant_dynamic-update-slice_fusion.9
  130.3 1.3 constant_dynamic-update-slice_fusion.8
  131.6 1.3 fusion.176
  133.0 1.3 pad_slice_fusion
  134.4 0.8 dynamic_slice.49
  135.2 2.4 %collective-permute-start.12 = (f32[139264]{0:T(1024)}, f32[139264]{0:T(1024)}, u32[]{:S(2)}, u32[]{:S(2)}) collective-permute-start(f32[139264]{0:T(1024)} %dynamic_slice.49), channel_id=1, source_target_pairs={{0,1},{1,0},{2,3},{3,2},{4,5},{5,4},{6,7},{7,6},{8,9},{9,8},{10,11... | collective-permute-start | bytes 1671176 | tf_op jit(solution)/shard_map/ppermute | solution.py:16
  137.9 4.6 %collective-permute-done.21 = f32[69632]{0:T(1024)S(1)} collective-permute-done((f32[69632]{0:T(1024)S(1)}, f32[69632]{0:T(1024)S(1)}, u32[]{:S(2)}, u32[]{:S(2)}) %collective-permute-start.21) | collective-permute-done | bytes 278560 | tf_op jit(solution)/shard_map/ppermute | solution.py:16
  142.7 1.0 fusion.204
  143.7 4.7 %collective-permute-done.22 = f32[34816]{0:T(1024)S(1)} collective-permute-done((f32[34816]{0:T(1024)S(1)}, f32[34816]{0:T(1024)S(1)}, u32[]{:S(2)}, u32[]{:S(2)}) %collective-permute-start.22) | collective-permute-done | bytes 139296 | tf_op jit(solution)/shard_map/ppermute | solution.py:16
  148.4 1.1 collective-permute-start.23
  149.5 0.9 pad_maximum_fusion.7
  150.3 3.9 %collective-permute-done.23 = f32[17408]{0:T(1024)S(1)} collective-permute-done((f32[17408]{0:T(1024)S(1)}, f32[17408]{0:T(1024)S(1)}, u32[]{:S(2)}, u32[]{:S(2)}) %collective-permute-start.23) | collective-permute-done | bytes 69664 | tf_op jit(solution)/shard_map/ppermute | solution.py:16
  154.9 1.1 dynamic-slice_add_fusion
  156.0 2.3 %collective-permute-start.13 = (f32[69632]{0:T(1024)S(1)}, f32[69632]{0:T(1024)S(1)}, u32[]{:S(2)}, u32[]{:S(2)}) collective-permute-start(f32[69632]{0:T(1024)S(1)} %dynamic_slice.51), channel_id=1, source_target_pairs={{0,4},{1,5},{2,6},{3,7},{4,0},{5,1},{6,2},{7,3},{8,12},{9,13},{10,... | collective-permute-start | bytes 835592 | tf_op jit(solution)/shard_map/ppermute | solution.py:16
  158.3 0.9 collective-permute-done.24
  159.4 4.8 %collective-permute-done.13 = f32[69632]{0:T(1024)S(1)} collective-permute-done((f32[69632]{0:T(1024)S(1)}, f32[69632]{0:T(1024)S(1)}, u32[]{:S(2)}, u32[]{:S(2)}) %collective-permute-start.13) | collective-permute-done | bytes 278560 | tf_op jit(solution)/shard_map/ppermute | solution.py:16
  164.3 1.6 collective-permute-start.14
  166.8 2.8 %collective-permute-done.14 = f32[34816]{0:T(1024)S(1)} collective-permute-done((f32[34816]{0:T(1024)S(1)}, f32[34816]{0:T(1024)S(1)}, u32[]{:S(2)}, u32[]{:S(2)}) %collective-permute-start.14) | collective-permute-done | bytes 139296 | tf_op jit(solution)/shard_map/ppermute | solution.py:16
  169.7 1.4 collective-permute-start.15
  171.1 5.3 %collective-permute-done.15 = f32[17408]{0:T(1024)S(1)} collective-permute-done((f32[17408]{0:T(1024)S(1)}, f32[17408]{0:T(1024)S(1)}, u32[]{:S(2)}, u32[]{:S(2)}) %collective-permute-start.15) | collective-permute-done | bytes 69664 | tf_op jit(solution)/shard_map/ppermute | solution.py:16
  176.8 4.6 %collective-permute-done.16 = bf16[17408]{0:T(1024)(128)(2,1)S(1)} collective-permute-done((bf16[17408]{0:T(1024)(128)(2,1)S(1)}, bf16[17408]{0:T(1024)(128)(2,1)S(1)}, u32[]{:S(2)}, u32[]{:S(2)}) %collective-permute-start.16) | collective-permute-done | bytes 34848 | tf_op jit(solution)/shard_map/ppermute | solution.py:16
  181.4 1.8 collective-permute-start.17
  183.4 2.4 %collective-permute-done.17 = bf16[34816]{0:T(1024)(128)(2,1)S(1)} collective-permute-done((bf16[34816]{0:T(1024)(128)(2,1)S(1)}, bf16[34816]{0:T(1024)(128)(2,1)S(1)}, u32[]{:S(2)}, u32[]{:S(2)}) %collective-permute-start.17) | collective-permute-done | bytes 69664 | tf_op jit(solution)/shard_map/ppermute | solution.py:16
  186.4 4.5 %collective-permute-done.18 = bf16[69632]{0:T(1024)(128)(2,1)S(1)} collective-permute-done((bf16[69632]{0:T(1024)(128)(2,1)S(1)}, bf16[69632]{0:T(1024)(128)(2,1)S(1)}, u32[]{:S(2)}, u32[]{:S(2)}) %collective-permute-start.18) | collective-permute-done | bytes 139296 | tf_op jit(solution)/shard_map/ppermute | solution.py:16
  191.5 1.1 convert_multiply_fusion.99
  194.5 1.0 convert_multiply_fusion.98
  (383 shorter events, 33.4 us)
Async XLA Ops:
  0.6 34.8 %copy-start = (bf16[1024,256]{1,0:T(8,128)(2,1)S(1)}, bf16[1024,256]{1,0:T(8,128)(2,1)}, u32[]{:S(2)}) copy-start(bf16[1024,256]{1,0:T(8,128)(2,1)} %param.23) | copy-start | bytes 1572868
  0.7 22.6 %copy-start.4 = (bf16[4,8,32,256]{3,2,1,0:T(8,128)(2,1)S(1)}, bf16[4,8,32,256]{3,2,1,0:T(8,128)(2,1)}, u32[]{:S(2)}) copy-start(bf16[4,8,32,256]{3,2,1,0:T(8,128)(2,1)} %param.13) | copy-start | bytes 1572868
  0.7 19.2 %copy-start.30 = (f32[7,7,256]{2,1,0:T(8,128)S(1)}, f32[7,7,256]{2,1,0:T(8,128)}, u32[]{:S(2)}) copy-start(f32[7,7,256]{2,1,0:T(8,128)} %param.17) | copy-start | bytes 150532
  0.7 19.4 %copy-start.31 = (s32[8,32]{1,0:T(8,128)S(1)}, s32[8,32]{1,0:T(8,128)}, u32[]{:S(2)}) copy-start(s32[8,32]{1,0:T(8,128)} %param.16) | copy-start | bytes 3076
  1.6 20.1 %collective-permute-start.1 = (bf16[4,3,3,256]{3,2,1,0:T(4,128)(2,1)S(1)}, bf16[4,3,3,256]{3,2,1,0:T(4,128)(2,1)S(1)}, u32[]{:S(2)}, u32[]{:S(2)}) collective-permute-start(bf16[4,3,3,256]{3,2,1,0:T(4,128)(2,1)S(1)} %get-tuple-element.113), channel_id=1, source_target_pairs={{0,0},{1,15},{2,14},{3,13},{4,12},{5,11},{6,10},{7,9},{8,8},{9,7},... | collective-permute-start | bytes 55304 | tf_op jit(solution)/shard_map/ppermute | solution.py:269
  2.3 19.6 %collective-permute-start.4 = (bf16[4,3,3,256]{3,2,1,0:T(4,128)(2,1)S(1)}, bf16[4,3,3,256]{3,2,1,0:T(4,128)(2,1)S(1)}, u32[]{:S(2)}, u32[]{:S(2)}) collective-permute-start(bf16[4,3,3,256]{3,2,1,0:T(4,128)(2,1)S(1)} %get-tuple-element.114), channel_id=1, source_target_pairs={{0,14},{1,13},{2,12},{3,11},{4,10},{5,9},{6,8},{7,7},{8,6},{9,5},{... | collective-permute-start | bytes 55304 | tf_op jit(solution)/shard_map/ppermute | solution.py:272
  12.6 9.4 %collective-permute-start.2 = (bf16[4,8,3,256]{3,2,1,0:T(4,128)(2,1)S(1)}, bf16[4,8,3,256]{3,2,1,0:T(4,128)(2,1)S(1)}, u32[]{:S(2)}, u32[]{:S(2)}) collective-permute-start(bf16[4,8,3,256]{3,2,1,0:T(4,128)(2,1)S(1)} %slice.731), channel_id=1, source_target_pairs={{0,15},{1,14},{2,13},{3,12},{4,11},{5,10},{6,9},{7,8},{8,7},{9,6},... | collective-permute-start | bytes 147464 | tf_op jit(solution)/shard_map/ppermute | solution.py:180
  14.7 8.5 %collective-permute-start = (bf16[4,3,35,256]{3,2,1,0:T(8,128)(2,1)S(1)}, bf16[4,3,35,256]{3,2,1,0:T(8,128)(2,1)S(1)}, u32[]{:S(2)}, u32[]{:S(2)}) collective-permute-start(bf16[4,3,35,256]{3,2,1,0:T(8,128)(2,1)S(1)} %get-tuple-element.107), channel_id=1, source_target_pairs={{0,1},{1,2},{2,3},{3,4},{4,5},{5,6},{6,7},{7,8},{8,9},{9,10},{10,1... | collective-permute-start | bytes 645128 | tf_op jit(solution)/shard_map/ppermute | solution.py:263
  14.9 8.3 %collective-permute-start.3 = (bf16[4,3,35,256]{3,2,1,0:T(8,128)(2,1)S(1)}, bf16[4,3,35,256]{3,2,1,0:T(8,128)(2,1)S(1)}, u32[]{:S(2)}, u32[]{:S(2)}) collective-permute-start(bf16[4,3,35,256]{3,2,1,0:T(8,128)(2,1)S(1)} %get-tuple-element.108), channel_id=1, source_target_pairs={{1,0},{2,1},{3,2},{4,3},{5,4},{6,5},{7,6},{8,7},{9,8},{10,9},{11,1... | collective-permute-start | bytes 645128 | tf_op jit(solution)/shard_map/ppermute | solution.py:266
  19.9 3.8 %copy-start.34 = (f32[1,1,256]{2,1,0:T(1,128)}, f32[1,1,256]{2,1,0:T(1,128)S(1)}, u32[]{:S(2)}) copy-start(f32[1,1,256]{2,1,0:T(1,128)S(1)} %get-tuple-element.116) | copy-start | bytes 3076
  19.9 3.8 %copy-start.36 = (f32[1,1,256]{2,1,0:T(1,128)}, f32[1,1,256]{2,1,0:T(1,128)S(1)}, u32[]{:S(2)}) copy-start(f32[1,1,256]{2,1,0:T(1,128)S(1)} %get-tuple-element.117) | copy-start | bytes 3076
  19.9 3.8 %copy-start.38 = (f32[1,1,256]{2,1,0:T(1,128)}, f32[1,1,256]{2,1,0:T(1,128)S(1)}, u32[]{:S(2)}) copy-start(f32[1,1,256]{2,1,0:T(1,128)S(1)} %get-tuple-element.118) | copy-start | bytes 3076
  19.9 3.8 %copy-start.40 = (f32[1,1,256]{2,1,0:T(1,128)}, f32[1,1,256]{2,1,0:T(1,128)S(1)}, u32[]{:S(2)}) copy-start(f32[1,1,256]{2,1,0:T(1,128)S(1)} %get-tuple-element.119) | copy-start | bytes 3076
  19.9 3.8 %copy-start.42 = (f32[1,1,256]{2,1,0:T(1,128)}, f32[1,1,256]{2,1,0:T(1,128)S(1)}, u32[]{:S(2)}) copy-start(f32[1,1,256]{2,1,0:T(1,128)S(1)} %get-tuple-element.120) | copy-start | bytes 3076
  19.9 3.8 %copy-start.44 = (f32[1,1,256]{2,1,0:T(1,128)}, f32[1,1,256]{2,1,0:T(1,128)S(1)}, u32[]{:S(2)}) copy-start(f32[1,1,256]{2,1,0:T(1,128)S(1)} %get-tuple-element.121) | copy-start | bytes 3076
  19.9 3.8 %copy-start.46 = (f32[1,1,256]{2,1,0:T(1,128)}, f32[1,1,256]{2,1,0:T(1,128)S(1)}, u32[]{:S(2)}) copy-start(f32[1,1,256]{2,1,0:T(1,128)S(1)} %get-tuple-element.122) | copy-start | bytes 3076
  19.9 3.8 %copy-start.48 = (f32[1,1,256]{2,1,0:T(1,128)}, f32[1,1,256]{2,1,0:T(1,128)S(1)}, u32[]{:S(2)}) copy-start(f32[1,1,256]{2,1,0:T(1,128)S(1)} %get-tuple-element.123) | copy-start | bytes 3076
  20.0 3.8 %copy-start.50 = (f32[1,1,256]{2,1,0:T(1,128)}, f32[1,1,256]{2,1,0:T(1,128)S(1)}, u32[]{:S(2)}) copy-start(f32[1,1,256]{2,1,0:T(1,128)S(1)} %get-tuple-element.124) | copy-start | bytes 3076
  20.0 3.8 %copy-start.52 = (f32[1,1,256]{2,1,0:T(1,128)}, f32[1,1,256]{2,1,0:T(1,128)S(1)}, u32[]{:S(2)}) copy-start(f32[1,1,256]{2,1,0:T(1,128)S(1)} %get-tuple-element.125) | copy-start | bytes 3076
  20.0 3.8 %copy-start.54 = (f32[1,1,256]{2,1,0:T(1,128)}, f32[1,1,256]{2,1,0:T(1,128)S(1)}, u32[]{:S(2)}) copy-start(f32[1,1,256]{2,1,0:T(1,128)S(1)} %get-tuple-element.126) | copy-start | bytes 3076
  24.1 9.7 %copy-start.32 = (f32[256]{0:T(256)S(1)}, f32[256]{0:T(256)}, u32[]{:S(2)}) copy-start(f32[256]{0:T(256)} %param.19) | copy-start | bytes 3076
  24.1 9.7 %copy-start.122 = (f32[256]{0:T(256)S(1)}, f32[256]{0:T(256)}, u32[]{:S(2)}) copy-start(f32[256]{0:T(256)} %param.20) | copy-start | bytes 3076
  68.0 14.5 %copy-start.18 = (bf16[1,8,32,256]{3,2,1,0:T(8,128)(2,1)S(1)}, bf16[1,8,32,256]{3,2,1,0:T(8,128)(2,1)}, u32[]{:S(2)}) copy-start(bf16[1,8,32,256]{3,2,1,0:T(8,128)(2,1)} %copy-done.17) | copy-start | bytes 393220
  80.1 4.1 %copy-start.10 = (bf16[256,1024]{1,0:T(8,128)(2,1)S(1)}, bf16[256,1024]{1,0:T(8,128)(2,1)}, u32[]{:S(2)}) copy-start(bf16[256,1024]{1,0:T(8,128)(2,1)} %copy-done.9) | copy-start | bytes 1572868
  80.1 4.1 %copy-start.16 = (bf16[1,8,32,256]{3,2,1,0:T(8,128)(2,1)S(1)}, bf16[1,8,32,256]{3,2,1,0:T(8,128)(2,1)}, u32[]{:S(2)}) copy-start(bf16[1,8,32,256]{3,2,1,0:T(8,128)(2,1)} %copy-done.15) | copy-start | bytes 393220
  80.1 13.6 %collective-permute-start.8 = (f32[12800]{0:T(1024)S(1)}, f32[12800]{0:T(1024)S(1)}, u32[]{:S(2)}, u32[]{:S(2)}) collective-permute-start(f32[12800]{0:T(1024)S(1)} %pad_maximum_fusion.9), channel_id=1, source_target_pairs={{0,1},{1,0},{2,3},{3,2},{4,5},{5,4},{6,7},{7,6},{8,9},{9,8},{10,11... | collective-permute-start | bytes 153608 | tf_op jit(solution)/shard_map/ppermute | solution.py:16
  88.1 5.6 %copy-start.27 = (f32[12544]{0:T(1024)S(1)}, f32[12544]{0:T(1024)}, u32[]{:S(2)}) copy-start(f32[12544]{0:T(1024)} %reshape.188) | copy-start | bytes 150532
  89.1 14.6 %copy-start.113 = (f32[1024]{0:T(1024)S(1)}, f32[1024]{0:T(1024)}, u32[]{:S(2)}) copy-start(f32[1024]{0:T(1024)} %get-tuple-element.85) | copy-start | bytes 12292
  89.1 14.7 %copy-start.114 = (f32[1024]{0:T(1024)S(1)}, f32[1024]{0:T(1024)}, u32[]{:S(2)}) copy-start(f32[1024]{0:T(1024)} %get-tuple-element.83) | copy-start | bytes 12292
  89.1 14.7 %copy-start.115 = (f32[1024]{0:T(1024)S(1)}, f32[1024]{0:T(1024)}, u32[]{:S(2)}) copy-start(f32[1024]{0:T(1024)} %get-tuple-element.87) | copy-start | bytes 12292
  89.1 14.7 %copy-start.116 = (f32[1024]{0:T(1024)S(1)}, f32[1024]{0:T(1024)}, u32[]{:S(2)}) copy-start(f32[1024]{0:T(1024)} %get-tuple-element.89) | copy-start | bytes 12292
  89.1 18.9 %copy-start.109 = (f32[256]{0:T(256)S(1)}, f32[256]{0:T(256)}, u32[]{:S(2)}) copy-start(f32[256]{0:T(256)} %get-tuple-element.75) | copy-start | bytes 3076
  89.1 18.9 %copy-start.110 = (f32[256]{0:T(256)S(1)}, f32[256]{0:T(256)}, u32[]{:S(2)}) copy-start(f32[256]{0:T(256)} %get-tuple-element.76) | copy-start | bytes 3076
  89.1 18.9 %copy-start.111 = (f32[256]{0:T(256)S(1)}, f32[256]{0:T(256)}, u32[]{:S(2)}) copy-start(f32[256]{0:T(256)} %get-tuple-element.77) | copy-start | bytes 3076
  89.1 18.9 %copy-start.112 = (f32[256]{0:T(256)S(1)}, f32[256]{0:T(256)}, u32[]{:S(2)}) copy-start(f32[256]{0:T(256)} %get-tuple-element.78) | copy-start | bytes 3076
  89.1 42.5 %collective-permute-start.20 = (f32[139264]{0:T(1024)}, f32[139264]{0:T(1024)}, u32[]{:S(2)}, u32[]{:S(2)}) collective-permute-start(f32[139264]{0:T(1024)} %fusion.174), channel_id=1, source_target_pairs={{0,1},{1,0},{2,3},{3,2},{4,5},{5,4},{6,7},{7,6},{8,9},{9,8},{10,11... | collective-permute-start | bytes 1671176 | tf_op jit(solution)/shard_map/ppermute | solution.py:16
  89.3 25.6 %collective-permute-start.5 = (f32[4,3,32,256]{3,2,1,0:T(8,128)}, f32[4,3,32,256]{3,2,1,0:T(8,128)}, u32[]{:S(2)}, u32[]{:S(2)}) collective-permute-start(f32[4,3,32,256]{3,2,1,0:T(8,128)} %get-tuple-element.103), channel_id=1, source_target_pairs={{0,1},{1,2},{2,3},{3,4},{4,5},{5,6},{6,7},{7,8},{8,9},{9,10},{10,1... | collective-permute-start | bytes 1179656 | tf_op jit(solution)/shard_map/ppermute | solution.py:26
  89.7 25.2 %collective-permute-start.6 = (f32[4,3,32,256]{3,2,1,0:T(8,128)}, f32[4,3,32,256]{3,2,1,0:T(8,128)}, u32[]{:S(2)}, u32[]{:S(2)}) collective-permute-start(f32[4,3,32,256]{3,2,1,0:T(8,128)} %get-tuple-element.104), channel_id=1, source_target_pairs={{1,0},{2,1},{3,2},{4,3},{5,4},{6,5},{7,6},{8,7},{9,8},{10,9},{11,1... | collective-permute-start | bytes 1179656 | tf_op jit(solution)/shard_map/ppermute | solution.py:27
  93.7 9.9 %collective-permute-start.9 = (f32[12800]{0:T(1024)S(1)}, f32[12800]{0:T(1024)S(1)}, u32[]{:S(2)}, u32[]{:S(2)}) collective-permute-start(f32[12800]{0:T(1024)S(1)} %fusion.268), channel_id=1, source_target_pairs={{0,2},{1,3},{2,0},{3,1},{4,6},{5,7},{6,4},{7,5},{8,10},{9,11},{10,... | collective-permute-start | bytes 153608 | tf_op jit(solution)/shard_map/ppermute | solution.py:16
  103.6 4.2 %collective-permute-start.10 = (f32[12800]{0:T(1024)S(1)}, f32[12800]{0:T(1024)S(1)}, u32[]{:S(2)}, u32[]{:S(2)}) collective-permute-start(f32[12800]{0:T(1024)S(1)} %add.805), channel_id=1, source_target_pairs={{0,4},{1,5},{2,6},{3,7},{4,0},{5,1},{6,2},{7,3},{8,12},{9,13},{10,... | collective-permute-start | bytes 153608 | tf_op jit(solution)/shard_map/ppermute | solution.py:16
  107.8 5.5 %collective-permute-start.11 = (f32[12800]{0:T(1024)S(1)}, f32[12800]{0:T(1024)S(1)}, u32[]{:S(2)}, u32[]{:S(2)}) collective-permute-start(f32[12800]{0:T(1024)S(1)} %add.806), channel_id=1, source_target_pairs={{0,8},{1,9},{2,10},{3,11},{4,12},{5,13},{6,14},{7,15},{8,0},{9,1},... | collective-permute-start | bytes 153608 | tf_op jit(solution)/shard_map/ppermute | solution.py:16
  116.7 10.5 %copy-start.7 = (f32[8,32,256]{2,1,0:T(8,128)S(1)}, f32[8,32,256]{2,1,0:T(8,128)}, u32[]{:S(2)}) copy-start(f32[8,32,256]{2,1,0:T(8,128)} %copy-done.6) | copy-start | bytes 786436
  116.7 10.5 %copy-start.20 = (f32[256,256]{1,0:T(8,128)S(1)}, f32[256,256]{1,0:T(8,128)}, u32[]{:S(2)}) copy-start(f32[256,256]{1,0:T(8,128)} %copy-done.19) | copy-start | bytes 786436
  116.7 10.5 %copy-start.22 = (f32[256,256]{1,0:T(8,128)S(1)}, f32[256,256]{1,0:T(8,128)}, u32[]{:S(2)}) copy-start(f32[256,256]{1,0:T(8,128)} %copy-done.21) | copy-start | bytes 786436
  116.8 10.5 %copy-start.24 = (f32[256,256]{1,0:T(8,128)S(1)}, f32[256,256]{1,0:T(8,128)}, u32[]{:S(2)}) copy-start(f32[256,256]{1,0:T(8,128)} %copy-done.23) | copy-start | bytes 786436
  116.8 10.5 %copy-start.26 = (f32[256,256]{1,0:T(8,128)S(1)}, f32[256,256]{1,0:T(8,128)}, u32[]{:S(2)}) copy-start(f32[256,256]{1,0:T(8,128)} %copy-done.25) | copy-start | bytes 786436
  127.1 10.6 %collective-permute-start.7 = (bf16[4,8,3,256]{3,2,1,0:T(4,128)(2,1)S(1)}, bf16[4,8,3,256]{3,2,1,0:T(4,128)(2,1)S(1)}, u32[]{:S(2)}, u32[]{:S(2)}) collective-permute-start(bf16[4,8,3,256]{3,2,1,0:T(4,128)(2,1)S(1)} %slice.1550), channel_id=1, source_target_pairs={{0,15},{1,14},{2,13},{3,12},{4,11},{5,10},{6,9},{7,8},{8,7},{9,6},... | collective-permute-start | bytes 147464 | tf_op jit(solution)/shard_map/ppermute | solution.py:180
  127.3 4.3 %copy-start.3 = (f32[32,8,8,128]{3,1,2,0:T(8,128)S(1)}, f32[32,8,8,128]{3,1,2,0:T(8,128)}, u32[]{:S(2)}) copy-start(f32[32,8,8,128]{3,1,2,0:T(8,128)} %copy-done.2) | copy-start | bytes 3145732
  127.7 6.6 %copy-start.5 = (f32[4,8,32,256]{3,2,1,0:T(8,128)}, f32[4,8,32,256]{3,2,1,0:T(8,128)S(1)}, u32[]{:S(2)}) copy-start(f32[4,8,32,256]{3,2,1,0:T(8,128)S(1)} %get-tuple-element.102) | copy-start | bytes 3145732
  133.0 9.6 %collective-permute-start.21 = (f32[69632]{0:T(1024)S(1)}, f32[69632]{0:T(1024)S(1)}, u32[]{:S(2)}, u32[]{:S(2)}) collective-permute-start(f32[69632]{0:T(1024)S(1)} %dynamic_slice.59), channel_id=1, source_target_pairs={{0,2},{1,3},{2,0},{3,1},{4,6},{5,7},{6,4},{7,5},{8,10},{9,11},{10,... | collective-permute-start | bytes 835592 | tf_op jit(solution)/shard_map/ppermute | solution.py:16
  135.2 19.6 %collective-permute-start.12 = (f32[139264]{0:T(1024)}, f32[139264]{0:T(1024)}, u32[]{:S(2)}, u32[]{:S(2)}) collective-permute-start(f32[139264]{0:T(1024)} %dynamic_slice.49), channel_id=1, source_target_pairs={{0,1},{1,0},{2,3},{3,2},{4,5},{5,4},{6,7},{7,6},{8,9},{9,8},{10,11... | collective-permute-start | bytes 1671176 | tf_op jit(solution)/shard_map/ppermute | solution.py:16
  142.6 5.8 %collective-permute-start.22 = (f32[34816]{0:T(1024)S(1)}, f32[34816]{0:T(1024)S(1)}, u32[]{:S(2)}, u32[]{:S(2)}) collective-permute-start(f32[34816]{0:T(1024)S(1)} %dynamic_slice.61), channel_id=1, source_target_pairs={{0,4},{1,5},{2,6},{3,7},{4,0},{5,1},{6,2},{7,3},{8,12},{9,13},{10,... | collective-permute-start | bytes 417800 | tf_op jit(solution)/shard_map/ppermute | solution.py:16
  148.4 5.8 %collective-permute-start.23 = (f32[17408]{0:T(1024)S(1)}, f32[17408]{0:T(1024)S(1)}, u32[]{:S(2)}, u32[]{:S(2)}) collective-permute-start(f32[17408]{0:T(1024)S(1)} %dynamic_slice.63), channel_id=1, source_target_pairs={{0,8},{1,9},{2,10},{3,11},{4,12},{5,13},{6,14},{7,15},{8,0},{9,1},... | collective-permute-start | bytes 208904 | tf_op jit(solution)/shard_map/ppermute | solution.py:16
  154.2 5.0 %collective-permute-start.24 = (bf16[17408]{0:T(1024)(128)(2,1)S(1)}, bf16[17408]{0:T(1024)(128)(2,1)S(1)}, u32[]{:S(2)}, u32[]{:S(2)}) collective-permute-start(bf16[17408]{0:T(1024)(128)(2,1)S(1)} %add_convert_fusion.1), channel_id=1, source_target_pairs={{0,8},{1,9},{2,10},{3,11},{4,12},{5,13},{6,14},{7,15},{8,0},{9,1},... | collective-permute-start | bytes 104456 | tf_op jit(solution)/shard_map/ppermute | solution.py:16
  156.0 8.3 %collective-permute-start.13 = (f32[69632]{0:T(1024)S(1)}, f32[69632]{0:T(1024)S(1)}, u32[]{:S(2)}, u32[]{:S(2)}) collective-permute-start(f32[69632]{0:T(1024)S(1)} %dynamic_slice.51), channel_id=1, source_target_pairs={{0,4},{1,5},{2,6},{3,7},{4,0},{5,1},{6,2},{7,3},{8,12},{9,13},{10,... | collective-permute-start | bytes 835592 | tf_op jit(solution)/shard_map/ppermute | solution.py:16
  159.3 6.7 %collective-permute-start.25 = (bf16[34816]{0:T(1024)(128)(2,1)S(1)}, bf16[34816]{0:T(1024)(128)(2,1)S(1)}, u32[]{:S(2)}, u32[]{:S(2)}) collective-permute-start(bf16[34816]{0:T(1024)(128)(2,1)S(1)} %maximum_select_fusion.15), channel_id=1, source_target_pairs={{0,4},{1,5},{2,6},{3,7},{4,0},{5,1},{6,2},{7,3},{8,12},{9,13},{10,... | collective-permute-start | bytes 208904 | tf_op jit(solution)/shard_map/ppermute | solution.py:16
  164.3 5.3 %collective-permute-start.14 = (f32[34816]{0:T(1024)S(1)}, f32[34816]{0:T(1024)S(1)}, u32[]{:S(2)}, u32[]{:S(2)}) collective-permute-start(f32[34816]{0:T(1024)S(1)} %dynamic_slice.53), channel_id=1, source_target_pairs={{0,2},{1,3},{2,0},{3,1},{4,6},{5,7},{6,4},{7,5},{8,10},{9,11},{10,... | collective-permute-start | bytes 417800 | tf_op jit(solution)/shard_map/ppermute | solution.py:16
  166.0 10.5 %collective-permute-start.26 = (bf16[69632]{0:T(1024)(128)(2,1)S(1)}, bf16[69632]{0:T(1024)(128)(2,1)S(1)}, u32[]{:S(2)}, u32[]{:S(2)}) collective-permute-start(bf16[69632]{0:T(1024)(128)(2,1)S(1)} %maximum_select_fusion.10), channel_id=1, source_target_pairs={{0,2},{1,3},{2,0},{3,1},{4,6},{5,7},{6,4},{7,5},{8,10},{9,11},{10,... | collective-permute-start | bytes 417800 | tf_op jit(solution)/shard_map/ppermute | solution.py:16
  169.7 6.7 %collective-permute-start.15 = (f32[17408]{0:T(1024)S(1)}, f32[17408]{0:T(1024)S(1)}, u32[]{:S(2)}, u32[]{:S(2)}) collective-permute-start(f32[17408]{0:T(1024)S(1)} %dynamic_slice.55), channel_id=1, source_target_pairs={{0,8},{1,9},{2,10},{3,11},{4,12},{5,13},{6,14},{7,15},{8,0},{9,1},... | collective-permute-start | bytes 208904 | tf_op jit(solution)/shard_map/ppermute | solution.py:16
  176.4 5.0 %collective-permute-start.16 = (bf16[17408]{0:T(1024)(128)(2,1)S(1)}, bf16[17408]{0:T(1024)(128)(2,1)S(1)}, u32[]{:S(2)}, u32[]{:S(2)}) collective-permute-start(bf16[17408]{0:T(1024)(128)(2,1)S(1)} %add_convert_fusion.2), channel_id=1, source_target_pairs={{0,8},{1,9},{2,10},{3,11},{4,12},{5,13},{6,14},{7,15},{8,0},{9,1},... | collective-permute-start | bytes 104456 | tf_op jit(solution)/shard_map/ppermute | solution.py:16
  176.6 9.7 %collective-permute-start.27 = (bf16[139264]{0:T(1024)(128)(2,1)S(1)}, bf16[139264]{0:T(1024)(128)(2,1)S(1)}, u32[]{:S(2)}, u32[]{:S(2)}) collective-permute-start(bf16[139264]{0:T(1024)(128)(2,1)S(1)} %maximum_select_fusion.5), channel_id=1, source_target_pairs={{0,1},{1,0},{2,3},{3,2},{4,5},{5,4},{6,7},{7,6},{8,9},{9,8},{10,11... | collective-permute-start | bytes 835592 | tf_op jit(solution)/shard_map/ppermute | solution.py:16
  181.4 4.4 %collective-permute-start.17 = (bf16[34816]{0:T(1024)(128)(2,1)S(1)}, bf16[34816]{0:T(1024)(128)(2,1)S(1)}, u32[]{:S(2)}, u32[]{:S(2)}) collective-permute-start(bf16[34816]{0:T(1024)(128)(2,1)S(1)} %maximum_select_fusion.14), channel_id=1, source_target_pairs={{0,2},{1,3},{2,0},{3,1},{4,6},{5,7},{6,4},{7,5},{8,10},{9,11},{10,... | collective-permute-start | bytes 208904 | tf_op jit(solution)/shard_map/ppermute | solution.py:16
  185.9 5.1 %collective-permute-start.18 = (bf16[69632]{0:T(1024)(128)(2,1)S(1)}, bf16[69632]{0:T(1024)(128)(2,1)S(1)}, u32[]{:S(2)}, u32[]{:S(2)}) collective-permute-start(bf16[69632]{0:T(1024)(128)(2,1)S(1)} %maximum_select_fusion.9), channel_id=1, source_target_pairs={{0,4},{1,5},{2,6},{3,7},{4,0},{5,1},{6,2},{7,3},{8,12},{9,13},{10,... | collective-permute-start | bytes 417800 | tf_op jit(solution)/shard_map/ppermute | solution.py:16
  191.1 1.8 collective-permute-start.19
  (88 other events, 212.3 us)

commit v4 on v1

--- a/solution.py
+++ b/solution.py
@@ -208,6 +208,36 @@
     return cur.astype(flat.dtype)
 
 
+def radix_allreduce(flat, axis, gather_dtype):
+    size = lax.axis_size(axis)
+    nbits = size.bit_length() - 1
+    groups = [list(range(b, min(b + 2, nbits))) for b in range(0, nbits, 2)]
+    idx = lax.axis_index(axis)
+    cur = flat
+    for bits in groups:
+        radix, low = 1 << len(bits), bits[0]
+        sub = (idx >> low) & (radix - 1)
+        part = cur.shape[0] // radix
+        total = lax.dynamic_slice_in_dim(cur, sub * part, part)
+        for d in range(1, radix):
+            send = lax.dynamic_slice_in_dim(cur, (sub ^ d) * part, part)
+            total = total + lax.ppermute(send, axis, [(i, i ^ (d << low)) for i in range(size)])
+        cur = total
+    cur = cur.astype(gather_dtype)
+    for bits in reversed(groups):
+        radix, low = 1 << len(bits), bits[0]
+        sub = (idx >> low) & (radix - 1)
+        part = cur.shape[0]
+        full = lax.dynamic_update_slice_in_dim(
+            jnp.zeros((part * radix,), cur.dtype), cur, sub * part, 0
+        )
+        for d in range(1, radix):
+            recv = lax.ppermute(cur, axis, [(i, i ^ (d << low)) for i in range(size)])
+            full = lax.dynamic_update_slice_in_dim(full, recv, (sub ^ d) * part, 0)
+        cur = full
+    return cur.astype(flat.dtype)
+
+
 def butterfly_allreduce(flat, axis):
     for bit in range(lax.axis_size(axis).bit_length() - 1):
         flat = flat + swapped(flat, axis, bit)
@@ -283,23 +313,18 @@
         scale_sum,
     ) = grads
     lon_size = lax.axis_size("lon")
-    big = (w_in_sum, w_out_sum, b_in_sum, b_out_sum, scale_sum, gain_sum, bias_sum)
-    big_tot = unpack(
-        halving_allreduce(pack(big, lon_size * 1024), "lon", jnp.bfloat16), big
-    )
-    small = (kernel_sum, dw_bias_sum)
-    small_tot = unpack(butterfly_allreduce(pack(small, 128), "lon"), small)
-    totals = (
-        small_tot[0],
-        small_tot[1],
-        big_tot[5],
-        big_tot[6],
-        big_tot[0],
-        big_tot[2],
-        big_tot[1],
-        big_tot[3],
-        big_tot[4],
-    )
+    sums = (
+        kernel_sum,
+        dw_bias_sum,
+        gain_sum,
+        bias_sum,
+        w_in_sum,
+        b_in_sum,
+        w_out_sum,
+        b_out_sum,
+        scale_sum,
+    )
+    totals = unpack(radix_allreduce(pack(sums, lon_size * 1024), "lon", jnp.bfloat16), sums)
     factor = 1.0 / math.sqrt(members * lat_rows * lon_dev * lax.axis_size("lon"))
     return (
         predicted,

time: 171 us -> 174 us (1.018)
  local copies, waits for them, and re-layouts: 23.3 us -> 36.5 us
  other arithmetic: 55.8 us -> 44.6 us
  starting transfers between devices: 24.7 us -> 27.1 us
    dynamic_update_slice x0 -> x7, local copies, waits for them, and re-layouts: none -> 13 us  [the longest x6 10.3 us: radix_allreduce(): full = lax.dynamic_update_slice_in_dim(full, recv, (sub ^ d) * part, 0)]
    ppermute x12, waiting for transfers between devices: 42.5 us -> 36.7 us  [the longest x6 33.2 us: radix_allreduce(): lax.ppermute(send, axis, [(i, i ^ d << low) for i in range(size)])]
    ppermute x2, waiting for transfers between devices: 0.01 us -> 5.65 us  [mirrored(): return lax.ppermute(x, axis, [(i, size - 1 - i) for i in range(size)])]
    add x7 -> x1, other arithmetic: 4.3 us -> 1.5 us  [radix_allreduce(): total + lax.ppermute(send, axis, [(i, i ^ d << low) for i in range(size)])]
    mul x0 -> x2, local copies, waits for them, and re-layouts: none -> 2.39 us  [the longest x1 1.26 us: on_device(): totals[6] * factor]
    unnamed x2 -> x4, other arithmetic: 1.88 us -> 3.97 us
    select_n x9 -> x0, other arithmetic: 1.97 us -> none  [halving_allreduce(): jnp.where(mine == 0, jnp.concatenate([cur, recv]), jnp.concatenate([recv,...]
    unnamed x283 -> x190, local copies, waits for them, and re-layouts: 11.3 us -> 12.6 us
  transfers between devices with their start and end apart: 18 -> 18, of which waited for: 10 -> 9; matrix products, arithmetic and copies ran while one was open for 13% -> 16% of each run, Pallas kernels for 0% -> 0%
where the time goes in v4:
time: 174 us; the launch traced here: 173 us
  waiting for transfers between devices  46.2 us (27%)
  other arithmetic  44.6 us (26%)
  local copies, waits for them, and re-layouts  36.5 us (21%)
  starting transfers between devices  27.1 us (16%)
  matrix products  16.4 us (9%)
  between operations  2.28 us (1%)
    ppermute x6, waiting for transfers between devices, radix_allreduce(): lax.ppermute(send, axis, [(i, i ^ d << low) for i in range(size)])  33.2 us
    unnamed x190, local copies, waits for them, and re-layouts  12.6 us
    dynamic_update_slice x6, local copies, waits for them, and re-layouts, radix_allreduce(): full = lax.dynamic_update_slice_in_dim(full, recv, (sub ^ d) * part, 0)  10.3 us
    reduce_sum x4, other arithmetic, local_step(): jnp.sum(grad_depth * extended[:, lon_off:lon_off + lon_dev, lat_off:lat_o...  9.36 us
    add x1, other arithmetic, on_device(): grad_ext + dw_kernel[lon_off, lat_off] * padded[:, 6 - lon_off:6 - lon_of...  9.32 us
    reduce_sum x1, other arithmetic, local_step(): mean_val = jnp.mean(depth, axis=-1, keepdims=True)  8.62 us
    ppermute x2, starting transfers between devices, with_halo(): after = lax.ppermute(leading, axis, down)  7.49 us
    ppermute x6, starting transfers between devices, radix_allreduce(): recv = lax.ppermute(cur, axis, [(i, i ^ d << low) for i in range(size)])  6.38 us
  transfers between devices with their start and end apart: 18, of which 9 were waited for; matrix products, arithmetic and copies ran while one was open for 16% of the time, Pallas kernels for 0%

profile of v4, /device:TPU:0, one launch (start us, length us, event | category | flops | bytes accessed | tf_op | source)
XLA Modules:
  0.0 173.0 jit_solution(17445046951243576338)
XLA Ops:
  0.7 1.0 slice.724
  1.7 5.5 %collective-permute-start = (bf16[4,8,3,256]{3,2,1,0:T(4,128)(2,1)S(1)}, bf16[4,8,3,256]{3,2,1,0:T(4,128)(2,1)S(1)}, u32[]{:S(2)}, u32[]{:S(2)}) collective-permute-start(bf16[4,8,3,256]{3,2,1,0:T(4,128)(2,1)S(1)} %slice.724), channel_id=1, source_target_pairs={{0,15},{1,14},{2,13},{3,12},{4,11},{5,10},{6,9},{7,8},{8,7},{9,6},... | collective-permute-start | bytes 147464 | tf_op jit(solution)/shard_map/ppermute | solution.py:180
  7.2 1.0 fusion.218
  8.2 1.0 fusion.219
  9.2 0.9 fusion.220
  10.3 0.8 copy.25
  11.3 1.3 pad_maximum_fusion.9
  13.3 3.8 %collective-permute-start.2 = (bf16[4,3,38,256]{3,2,1,0:T(8,128)(2,1)S(1)}, bf16[4,3,38,256]{3,2,1,0:T(8,128)(2,1)S(1)}, u32[]{:S(2)}, u32[]{:S(2)}) collective-permute-start(bf16[4,3,38,256]{3,2,1,0:T(8,128)(2,1)S(1)} %get-tuple-element.116), channel_id=1, source_target_pairs={{1,0},{2,1},{3,2},{4,3},{5,4},{6,5},{7,6},{8,7},{9,8},{10,9},{11,1... | collective-permute-start | bytes 700424 | tf_op jit(solution)/shard_map/ppermute | solution.py:27
  17.3 3.8 %collective-permute-done.1 = bf16[4,3,38,256]{3,2,1,0:T(8,128)(2,1)S(1)} collective-permute-done((bf16[4,3,38,256]{3,2,1,0:T(8,128)(2,1)S(1)}, bf16[4,3,38,256]{3,2,1,0:T(8,128)(2,1)S(1)}, u32[]{:S(2)}, u32[]{:S(2)}) %collective-permute-start.1) | collective-permute-done | bytes 233504 | tf_op jit(solution)/shard_map/ppermute | solution.py:26
  21.6 8.6 %fusion.213 = (f32[4,8,32]{2,1,0:T(8,128)S(1)}, f32[4,8,32,256]{3,2,1,0:T(8,128)S(1)}) fusion(bf16[4,11,38,256]{3,2,1,0:T(8,128)(2,1)S(1)} %get-tuple-element.114, f32[256]{0:T(256)S(1)} %bitcast.432, f32[256]{0:T(256)S(1)} %bitcast.434, f32[256]{0:T(256)S(1)} %bitcast.340, f32[256]{0:T(256)S(1)} %bitcast.342, f32[256]{0:T(256)S(1)} %bitcast.344, ...), kind=kLoop, calls=%fused_computation.487 | loop fusion | flops 43514880 | bytes 23746560 | tf_op jit(solution)/shard_map/reduce_sum | solution.py:62
  35.2 1.0 fusion.211
  36.2 3.1 %multiply_reduce_fusion.7 = (f32[256]{0:T(256)}, f32[256]{0:T(256)}, f32[256]{0:T(256)}, f32[256]{0:T(256)}, f32[8,32,256]{2,1,0:T(8,128)S(1)}, /*index=5*/f32[8...) fusion(f32[256]{0:T(256)S(1)} %copy-done.24, ...), kind=kLoop, calls=%fused_computation.432 | loop fusion | flops 7863296 | bytes 2497536 | tf_op jit(solution)/shard_map/reduce_sum | solution.py:117
  40.2 1.5 fusion.205
  42.0 0.9 fusion.223
  42.9 1.5 fusion.203
  44.4 1.5 fusion.207
  45.9 1.5 fusion.209
  47.4 0.9 fusion.224
  48.3 0.9 fusion.222
  49.3 0.9 fusion.221
  50.2 1.0 multiply_reduce_fusion.1
  51.1 4.0 %fusion.147 = (f32[256]{0:T(256)}, f32[256]{0:T(256)}, f32[256]{0:T(256)}, f32[256]{0:T(256)}, f32[256]{0:T(256)}, /*index=5*/f32[256]{0:T(256)}, f32[256]{0:T(2...) fusion(bf16[4,11,38,256]{3,2,1,0:T(8,128)(2,1)S(1)} %get-tuple-, ...), kind=kLoop, calls=%fused_computation.325 | loop fusion | flops 16772608 | bytes 12618752 | tf_op jit(solution)/shard_map/reduce_sum | solution.py:154
  55.2 2.3 %fusion.129 = (f32[256]{0:T(256)}, f32[256]{0:T(256)}, f32[256]{0:T(256)}, f32[256]{0:T(256)}, f32[256]{0:T(256)}, /*index=5*/f32[256]{0:T(256)}, f32[256]{0:T(2...) fusion(f32[4,8,32,256]{3,2,1,0:T(8,128)S(1)} %get-tuple-element.93, ...), kind=kLoop, calls=%fused_computation.307 | loop fusion | flops 12842240 | bytes 3255296 | tf_op jit(solution)/shard_map/reduce_sum | solution.py:154
  57.5 2.5 %fusion.96 = (f32[256]{0:T(256)S(1)}, f32[256]{0:T(256)S(1)}, f32[256]{0:T(256)S(1)}, f32[256]{0:T(256)S(1)}, f32[256]{0:T(256)S(1)}, /*index=5*/f32[256]{0:T(25...) fusion(f32[4,8,32,256]{3,2,1,0:T(8,128)S(1)} %get-tuple-element, ...), kind=kLoop, calls=%fused_computation.274 | loop fusion | flops 14151168 | bytes 10504192 | tf_op jit(solution)/shard_map/reduce_sum | solution.py:154
  60.5 0.9 fusion.215
  65.0 1.2 copy.27
  66.8 0.8 collective-permute-start.3
  67.5 3.7 %collective-permute-start.4 = (f32[4,3,32,256]{3,2,1,0:T(8,128)}, f32[4,3,32,256]{3,2,1,0:T(8,128)S(1)}, u32[]{:S(2)}, u32[]{:S(2)}) collective-permute-start(f32[4,3,32,256]{3,2,1,0:T(8,128)} %get-tuple-element.112), channel_id=1, source_target_pairs={{1,0},{2,1},{3,2},{4,3},{5,4},{6,5},{7,6},{8,7},{9,8},{10,9},{11,1... | collective-permute-start | bytes 1179656 | tf_op jit(solution)/shard_map/ppermute | solution.py:27
  71.3 1.4 constant_dynamic-update-slice_fusion.7
  72.7 1.3 constant_dynamic-update-slice_fusion.15
  74.0 1.3 constant_dynamic-update-slice_fusion.14
  75.3 1.3 constant_dynamic-update-slice_fusion.13
  76.6 2.3 %constant_dynamic-update-slice_fusion.12 = f32[539136]{0:T(1024)} fusion(f32[539136]{0:T(1024)} %constant_dynamic-update-slice_fusion.13, f32[262144]{0:T(1024)} %bitcast.301), kind=kLoop, calls=%fused_computation.467 | loop fusion | bytes 2097152
  78.9 1.4 constant_dynamic-update-slice_fusion.11
  80.3 1.1 constant_dynamic-update-slice_fusion.10
  81.4 1.3 constant_dynamic-update-slice_fusion.9
  83.5 9.3 %fusion.3 = f32[4,8,38,256]{3,2,1,0:T(8,128)S(1)} fusion(f32[4,14,44,256]{3,2,1,0:T(8,128)S(1)} %select_maximum_fusion, f32[256]{0:T(256)S(1)} %bitcast.433, f32[256]{0:T(256)S(1)} %bitcast.435, f32[256]{0:T(256)S(1)} %bitcast.341, f32[256]{0:T(256)S(1)} %bitcast.343, f32[256]{0:T(256)S(1)} %bitcast.345, f32[256]{0:T(256)S(1)} %bitcast.347, ...), kind=kLoop, calls=%fused_computation.129 | loop fusion | flops 30195712 | bytes 62309376 | tf_op jit(solution)/shard_map/add | solution.py:290
  92.9 1.3 multiply_reduce_fusion
  94.2 1.1 copy-done.3
  95.3 1.2 pad_dynamic-slice_fusion.2
  96.5 1.9 %collective-permute-start.8 = (f32[135168]{0:T(1024)S(1)}, f32[135168]{0:T(1024)}, u32[]{:S(2)}, u32[]{:S(2)}) collective-permute-start(f32[135168]{0:T(1024)S(1)} %get-tuple-element.107), channel_id=1, source_target_pairs={{0,3},{1,2},{2,1},{3,0},{4,7},{5,6},{6,5},{7,4},{8,11},{9,10},{10,... | collective-permute-start | bytes 1622024 | tf_op jit(solution)/shard_map/ppermute | solution.py:224
  98.8 13.1 %collective-permute-done.7 = f32[135168]{0:T(1024)} collective-permute-done((f32[135168]{0:T(1024)}, f32[135168]{0:T(1024)}, u32[]{:S(2)}, u32[]{:S(2)}) %collective-permute-start.7) | collective-permute-done | bytes 540704 | tf_op jit(solution)/shard_map/ppermute | solution.py:224
  111.9 10.8 %collective-permute-done.8 = f32[135168]{0:T(1024)} collective-permute-done((f32[135168]{0:T(1024)S(1)}, f32[135168]{0:T(1024)}, u32[]{:S(2)}, u32[]{:S(2)}) %collective-permute-start.8) | collective-permute-done | bytes 540704 | tf_op jit(solution)/shard_map/ppermute | solution.py:224
  122.7 1.5 fusion.176
  124.4 3.4 %collective-permute-start.9 = (f32[33792]{0:T(1024)S(1)}, f32[33792]{0:T(1024)S(1)}, u32[]{:S(2)}, u32[]{:S(2)}) collective-permute-start(f32[33792]{0:T(1024)S(1)} %get-tuple-element.117), channel_id=1, source_target_pairs={{0,4},{1,5},{2,6},{3,7},{4,0},{5,1},{6,2},{7,3},{8,12},{9,13},{10,... | collective-permute-start | bytes 405512 | tf_op jit(solution)/shard_map/ppermute | solution.py:224
  127.8 6.8 %collective-permute-done.10 = f32[33792]{0:T(1024)S(1)} collective-permute-done((f32[33792]{0:T(1024)S(1)}, f32[33792]{0:T(1024)S(1)}, u32[]{:S(2)}, u32[]{:S(2)}) %collective-permute-start.10) | collective-permute-done | bytes 135200 | tf_op jit(solution)/shard_map/ppermute | solution.py:224
  134.6 2.1 %collective-permute-done.9 = f32[33792]{0:T(1024)S(1)} collective-permute-done((f32[33792]{0:T(1024)S(1)}, f32[33792]{0:T(1024)S(1)}, u32[]{:S(2)}, u32[]{:S(2)}) %collective-permute-start.9) | collective-permute-done | bytes 135200 | tf_op jit(solution)/shard_map/ppermute | solution.py:224
  138.2 3.1 %collective-permute-start.14 = (bf16[33792]{0:T(1024)(128)(2,1)S(1)}, bf16[33792]{0:T(1024)(128)(2,1)S(1)}, u32[]{:S(2)}, u32[]{:S(2)}) collective-permute-start(bf16[33792]{0:T(1024)(128)(2,1)S(1)} %get-tuple-element.80), channel_id=1, source_target_pairs={{0,12},{1,13},{2,14},{3,15},{4,8},{5,9},{6,10},{7,11},{8,4},{9,5},... | collective-permute-start | bytes 202760 | tf_op jit(solution)/shard_map/ppermute | solution.py:235
  141.2 1.0 slice.1516
  142.2 0.9 collective-permute-start.5
  143.2 5.6 %collective-permute-done.5 = bf16[4,8,3,256]{3,2,1,0:T(4,128)(2,1)S(1)} collective-permute-done((bf16[4,8,3,256]{3,2,1,0:T(4,128)(2,1)S(1)}, bf16[4,8,3,256]{3,2,1,0:T(4,128)(2,1)S(1)}, u32[]{:S(2)}, u32[]{:S(2)}) %collective-permute-start.5) | collective-permute-done | bytes 49184 | tf_op jit(solution)/shard_map/ppermute | solution.py:180
  149.1 0.9 dynamic_update_slice.25
  149.9 0.9 dynamic_update_slice.26
  150.8 0.8 dynamic_update_slice.27
  152.3 1.3 collective-permute-start.17
  153.6 0.9 pad_maximum_fusion.6
  154.6 2.7 %dynamic_update_slice.28 = bf16[540672]{0:T(1024)(128)(2,1)S(1)} dynamic-update-slice(bf16[540672]{0:T(1024)(128)(2,1)S(1)} %broadcast_in_dim.4, bf16[135168]{0:T(1024)(128)(2,1)S(1)} %dynamic_update_slice.27, s32[]{:T(128)S(6)} %select_n.42) | dynamic-update-slice | bytes 540676 | tf_op jit(solution)/shard_map/dynamic_update_slice | solution.py:231
  157.2 2.6 %dynamic_update_slice.29 = bf16[540672]{0:T(1024)(128)(2,1)S(1)} dynamic-update-slice(bf16[540672]{0:T(1024)(128)(2,1)S(1)} %dynamic_update_slice.28, bf16[135168]{0:T(1024)(128)(2,1)S(1)} %collective-permute-done.15, s32[]{:T(128)S(6)} %select_n.43) | dynamic-update-slice | bytes 540676 | tf_op jit(solution)/shard_map/dynamic_update_slice | solution.py:236
  159.9 1.1 collective-permute-done.16
  161.1 2.6 %dynamic_update_slice.30 = bf16[540672]{0:T(1024)(128)(2,1)S(1)} dynamic-update-slice(bf16[540672]{0:T(1024)(128)(2,1)S(1)} %dynamic_update_slice.29, bf16[135168]{0:T(1024)(128)(2,1)S(1)} %collective-permute-done.16, s32[]{:T(128)S(6)} %select_n.44) | dynamic-update-slice | bytes 540676 | tf_op jit(solution)/shard_map/dynamic_update_slice | solution.py:236
  163.7 2.3 %collective-permute-done.17 = bf16[135168]{0:T(1024)(128)(2,1)S(1)} collective-permute-done((bf16[135168]{0:T(1024)(128)(2,1)S(1)}, bf16[135168]{0:T(1024)(128)(2,1)S(1)}, u32[]{:S(2)}, u32[]{:S(2)}) %collective-permute-start.17) | collective-permute-done | bytes 270368 | tf_op jit(solution)/shard_map/ppermute | solution.py:235
  165.9 2.5 %dynamic_update_slice.31 = bf16[540672]{0:T(1024)(128)(2,1)S(1)} dynamic-update-slice(bf16[540672]{0:T(1024)(128)(2,1)S(1)} %dynamic_update_slice.30, bf16[135168]{0:T(1024)(128)(2,1)S(1)} %collective-permute-done.17, s32[]{:T(128)S(6)} %select_n.45) | dynamic-update-slice | bytes 540676 | tf_op jit(solution)/shard_map/dynamic_update_slice | solution.py:236
  170.0 1.1 mul.1877
  171.1 1.3 mul.1881
  (254 shorter events, 17.4 us)
Async XLA Ops:
  0.6 31.7 %copy-start = (bf16[1024,256]{1,0:T(8,128)(2,1)S(1)}, bf16[1024,256]{1,0:T(8,128)(2,1)}, u32[]{:S(2)}) copy-start(bf16[1024,256]{1,0:T(8,128)(2,1)} %param.23) | copy-start | bytes 1572868
  0.7 20.4 %copy-start.2 = (bf16[4,8,32,256]{3,2,1,0:T(8,128)(2,1)S(1)}, bf16[4,8,32,256]{3,2,1,0:T(8,128)(2,1)}, u32[]{:S(2)}) copy-start(bf16[4,8,32,256]{3,2,1,0:T(8,128)(2,1)} %param.13) | copy-start | bytes 1572868
  0.7 16.5 %copy-start.22 = (s32[8,32]{1,0:T(8,128)S(1)}, s32[8,32]{1,0:T(8,128)}, u32[]{:S(2)}) copy-start(s32[8,32]{1,0:T(8,128)} %param.16) | copy-start | bytes 3076
  1.7 9.4 %collective-permute-start = (bf16[4,8,3,256]{3,2,1,0:T(4,128)(2,1)S(1)}, bf16[4,8,3,256]{3,2,1,0:T(4,128)(2,1)S(1)}, u32[]{:S(2)}, u32[]{:S(2)}) collective-permute-start(bf16[4,8,3,256]{3,2,1,0:T(4,128)(2,1)S(1)} %slice.724), channel_id=1, source_target_pairs={{0,15},{1,14},{2,13},{3,12},{4,11},{5,10},{6,9},{7,8},{8,7},{9,6},... | collective-permute-start | bytes 147464 | tf_op jit(solution)/shard_map/ppermute | solution.py:180
  9.2 12.3 %copy-start.25 = (f32[1,1,256]{2,1,0:T(1,128)}, f32[1,1,256]{2,1,0:T(1,128)S(1)}, u32[]{:S(2)}) copy-start(f32[1,1,256]{2,1,0:T(1,128)S(1)} %get-tuple-element.160) | copy-start | bytes 3076
  9.2 12.3 %copy-start.27 = (f32[1,1,256]{2,1,0:T(1,128)}, f32[1,1,256]{2,1,0:T(1,128)S(1)}, u32[]{:S(2)}) copy-start(f32[1,1,256]{2,1,0:T(1,128)S(1)} %get-tuple-element.161) | copy-start | bytes 3076
  10.2 11.3 %copy-start.29 = (f32[1,1,256]{2,1,0:T(1,128)}, f32[1,1,256]{2,1,0:T(1,128)S(1)}, u32[]{:S(2)}) copy-start(f32[1,1,256]{2,1,0:T(1,128)S(1)} %get-tuple-element.162) | copy-start | bytes 3076
  10.2 11.3 %copy-start.31 = (f32[1,1,256]{2,1,0:T(1,128)}, f32[1,1,256]{2,1,0:T(1,128)S(1)}, u32[]{:S(2)}) copy-start(f32[1,1,256]{2,1,0:T(1,128)S(1)} %get-tuple-element.163) | copy-start | bytes 3076
  10.2 11.3 %copy-start.33 = (f32[1,1,256]{2,1,0:T(1,128)}, f32[1,1,256]{2,1,0:T(1,128)S(1)}, u32[]{:S(2)}) copy-start(f32[1,1,256]{2,1,0:T(1,128)S(1)} %get-tuple-element.164) | copy-start | bytes 3076
  10.2 11.3 %copy-start.35 = (f32[1,1,256]{2,1,0:T(1,128)}, f32[1,1,256]{2,1,0:T(1,128)S(1)}, u32[]{:S(2)}) copy-start(f32[1,1,256]{2,1,0:T(1,128)S(1)} %get-tuple-element.165) | copy-start | bytes 3076
  10.2 11.3 %copy-start.37 = (f32[1,1,256]{2,1,0:T(1,128)}, f32[1,1,256]{2,1,0:T(1,128)S(1)}, u32[]{:S(2)}) copy-start(f32[1,1,256]{2,1,0:T(1,128)S(1)} %get-tuple-element.166) | copy-start | bytes 3076
  10.2 11.3 %copy-start.39 = (f32[1,1,256]{2,1,0:T(1,128)}, f32[1,1,256]{2,1,0:T(1,128)S(1)}, u32[]{:S(2)}) copy-start(f32[1,1,256]{2,1,0:T(1,128)S(1)} %get-tuple-element.167) | copy-start | bytes 3076
  10.2 11.3 %copy-start.41 = (f32[1,1,256]{2,1,0:T(1,128)}, f32[1,1,256]{2,1,0:T(1,128)S(1)}, u32[]{:S(2)}) copy-start(f32[1,1,256]{2,1,0:T(1,128)S(1)} %get-tuple-element.168) | copy-start | bytes 3076
  10.2 11.3 %copy-start.43 = (f32[1,1,256]{2,1,0:T(1,128)}, f32[1,1,256]{2,1,0:T(1,128)S(1)}, u32[]{:S(2)}) copy-start(f32[1,1,256]{2,1,0:T(1,128)S(1)} %get-tuple-element.169) | copy-start | bytes 3076
  10.2 11.3 %copy-start.45 = (f32[1,1,256]{2,1,0:T(1,128)}, f32[1,1,256]{2,1,0:T(1,128)S(1)}, u32[]{:S(2)}) copy-start(f32[1,1,256]{2,1,0:T(1,128)S(1)} %get-tuple-element.170) | copy-start | bytes 3076
  10.2 11.3 %copy-start.47 = (f32[1,1,256]{2,1,0:T(1,128)}, f32[1,1,256]{2,1,0:T(1,128)S(1)}, u32[]{:S(2)}) copy-start(f32[1,1,256]{2,1,0:T(1,128)S(1)} %get-tuple-element.171) | copy-start | bytes 3076
  10.2 11.3 %copy-start.49 = (f32[1,1,256]{2,1,0:T(1,128)}, f32[1,1,256]{2,1,0:T(1,128)S(1)}, u32[]{:S(2)}) copy-start(f32[1,1,256]{2,1,0:T(1,128)S(1)} %get-tuple-element.172) | copy-start | bytes 3076
  12.6 8.5 %collective-permute-start.1 = (bf16[4,3,38,256]{3,2,1,0:T(8,128)(2,1)S(1)}, bf16[4,3,38,256]{3,2,1,0:T(8,128)(2,1)S(1)}, u32[]{:S(2)}, u32[]{:S(2)}) collective-permute-start(bf16[4,3,38,256]{3,2,1,0:T(8,128)(2,1)S(1)} %get-tuple-element.115), channel_id=1, source_target_pairs={{0,1},{1,2},{2,3},{3,4},{4,5},{5,6},{6,7},{7,8},{8,9},{9,10},{10,1... | collective-permute-start | bytes 700424 | tf_op jit(solution)/shard_map/ppermute | solution.py:26
  13.3 7.8 %collective-permute-start.2 = (bf16[4,3,38,256]{3,2,1,0:T(8,128)(2,1)S(1)}, bf16[4,3,38,256]{3,2,1,0:T(8,128)(2,1)S(1)}, u32[]{:S(2)}, u32[]{:S(2)}) collective-permute-start(bf16[4,3,38,256]{3,2,1,0:T(8,128)(2,1)S(1)} %get-tuple-element.116), channel_id=1, source_target_pairs={{1,0},{2,1},{3,2},{4,3},{5,4},{6,5},{7,6},{8,7},{9,8},{10,9},{11,1... | collective-permute-start | bytes 700424 | tf_op jit(solution)/shard_map/ppermute | solution.py:27
  17.3 4.3 %copy-start.85 = (f32[256]{0:T(256)S(1)}, f32[256]{0:T(256)}, u32[]{:S(2)}) copy-start(f32[256]{0:T(256)} %param.18) | copy-start | bytes 3076
  21.6 9.1 %copy-start.23 = (f32[256]{0:T(256)S(1)}, f32[256]{0:T(256)}, u32[]{:S(2)}) copy-start(f32[256]{0:T(256)} %param.19) | copy-start | bytes 3076
  21.6 9.1 %copy-start.86 = (f32[256]{0:T(256)S(1)}, f32[256]{0:T(256)}, u32[]{:S(2)}) copy-start(f32[256]{0:T(256)} %param.20) | copy-start | bytes 3076
  32.9 2.1 %copy-start.12 = (f32[256,256]{1,0:T(8,128)}, f32[256,256]{1,0:T(8,128)S(1)}, u32[]{:S(2)}) copy-start(f32[256,256]{1,0:T(8,128)S(1)} %convolution_add_fusion.13) | copy-start | bytes 786436
  64.9 1.7 copy-start.64
  64.9 1.7 copy-start.65
  64.9 1.7 copy-start.66
  64.9 1.7 copy-start.67
  65.0 1.7 copy-start.57
  65.0 1.7 copy-start.58
  65.0 1.7 copy-start.59
  65.0 1.7 copy-start.60
  65.0 1.7 copy-start.61
  65.0 1.7 copy-start.62
  65.0 1.7 copy-start.63
  65.0 7.7 %copy-start.56 = (f32[256]{0:T(256)S(1)}, f32[256]{0:T(256)}, u32[]{:S(2)}) copy-start(f32[256]{0:T(256)} %get-tuple-element.67) | copy-start | bytes 3076
  65.0 9.0 %copy-start.51 = (f32[256]{0:T(256)S(1)}, f32[256]{0:T(256)}, u32[]{:S(2)}) copy-start(f32[256]{0:T(256)} %get-tuple-element.12) | copy-start | bytes 3076
  66.8 16.0 %collective-permute-start.3 = (f32[4,3,32,256]{3,2,1,0:T(8,128)}, f32[4,3,32,256]{3,2,1,0:T(8,128)S(1)}, u32[]{:S(2)}, u32[]{:S(2)}) collective-permute-start(f32[4,3,32,256]{3,2,1,0:T(8,128)} %get-tuple-element.111), channel_id=1, source_target_pairs={{0,1},{1,2},{2,3},{3,4},{4,5},{5,6},{6,7},{7,8},{8,9},{9,10},{10,1... | collective-permute-start | bytes 1179656 | tf_op jit(solution)/shard_map/ppermute | solution.py:26
  67.5 15.2 %collective-permute-start.4 = (f32[4,3,32,256]{3,2,1,0:T(8,128)}, f32[4,3,32,256]{3,2,1,0:T(8,128)S(1)}, u32[]{:S(2)}, u32[]{:S(2)}) collective-permute-start(f32[4,3,32,256]{3,2,1,0:T(8,128)} %get-tuple-element.112), channel_id=1, source_target_pairs={{1,0},{2,1},{3,2},{4,3},{5,4},{6,5},{7,6},{8,7},{9,8},{10,9},{11,1... | collective-permute-start | bytes 1179656 | tf_op jit(solution)/shard_map/ppermute | solution.py:27
  78.9 2.5 %copy-start.52 = (f32[256]{0:T(256)S(1)}, f32[256]{0:T(256)}, u32[]{:S(2)}) copy-start(f32[256]{0:T(256)} %get-tuple-element.75) | copy-start | bytes 3076
  78.9 2.5 %copy-start.53 = (f32[256]{0:T(256)S(1)}, f32[256]{0:T(256)}, u32[]{:S(2)}) copy-start(f32[256]{0:T(256)} %get-tuple-element.76) | copy-start | bytes 3076
  78.9 2.5 %copy-start.54 = (f32[256]{0:T(256)S(1)}, f32[256]{0:T(256)}, u32[]{:S(2)}) copy-start(f32[256]{0:T(256)} %get-tuple-element.77) | copy-start | bytes 3076
  78.9 2.5 %copy-start.55 = (f32[256]{0:T(256)S(1)}, f32[256]{0:T(256)}, u32[]{:S(2)}) copy-start(f32[256]{0:T(256)} %get-tuple-element.78) | copy-start | bytes 3076
  83.4 9.4 %copy-start.7 = (f32[8,32,256]{2,1,0:T(8,128)S(1)}, f32[8,32,256]{2,1,0:T(8,128)}, u32[]{:S(2)}) copy-start(f32[8,32,256]{2,1,0:T(8,128)} %copy-done.6) | copy-start | bytes 786436
  83.4 9.4 %copy-start.9 = (f32[8,32,256]{2,1,0:T(8,128)S(1)}, f32[8,32,256]{2,1,0:T(8,128)}, u32[]{:S(2)}) copy-start(f32[8,32,256]{2,1,0:T(8,128)} %copy-done.8) | copy-start | bytes 786436
  83.4 9.4 %copy-start.11 = (f32[8,32,256]{2,1,0:T(8,128)S(1)}, f32[8,32,256]{2,1,0:T(8,128)}, u32[]{:S(2)}) copy-start(f32[8,32,256]{2,1,0:T(8,128)} %copy-done.10) | copy-start | bytes 786436
  83.5 9.4 %copy-start.13 = (f32[256,256]{1,0:T(8,128)S(1)}, f32[256,256]{1,0:T(8,128)}, u32[]{:S(2)}) copy-start(f32[256,256]{1,0:T(8,128)} %copy-done.12) | copy-start | bytes 786436
  83.5 9.4 %copy-start.15 = (f32[256,256]{1,0:T(8,128)S(1)}, f32[256,256]{1,0:T(8,128)}, u32[]{:S(2)}) copy-start(f32[256,256]{1,0:T(8,128)} %copy-done.14) | copy-start | bytes 786436
  83.5 9.4 %copy-start.17 = (f32[256,256]{1,0:T(8,128)S(1)}, f32[256,256]{1,0:T(8,128)}, u32[]{:S(2)}) copy-start(f32[256,256]{1,0:T(8,128)} %copy-done.16) | copy-start | bytes 786436
  83.5 9.4 %copy-start.19 = (f32[256,256]{1,0:T(8,128)S(1)}, f32[256,256]{1,0:T(8,128)}, u32[]{:S(2)}) copy-start(f32[256,256]{1,0:T(8,128)} %copy-done.18) | copy-start | bytes 786436
  92.9 2.4 %copy-start.3 = (f32[539136]{0:T(1024)S(1)}, f32[539136]{0:T(1024)}, u32[]{:S(2)}) copy-start(f32[539136]{0:T(1024)} %constant_dynamic-update-slice_fusion.9) | copy-start | bytes 6469636
  96.5 2.3 %collective-permute-start.6 = (f32[135168]{0:T(1024)}, f32[135168]{0:T(1024)}, u32[]{:S(2)}, u32[]{:S(2)}) collective-permute-start(f32[135168]{0:T(1024)} %get-tuple-element.105), channel_id=1, source_target_pairs={{0,1},{1,0},{2,3},{3,2},{4,5},{5,4},{6,7},{7,6},{8,9},{9,8},{10,11... | collective-permute-start | bytes 1622024 | tf_op jit(solution)/shard_map/ppermute | solution.py:224
  96.5 15.4 %collective-permute-start.7 = (f32[135168]{0:T(1024)}, f32[135168]{0:T(1024)}, u32[]{:S(2)}, u32[]{:S(2)}) collective-permute-start(f32[135168]{0:T(1024)} %get-tuple-element.106), channel_id=1, source_target_pairs={{0,2},{1,3},{2,0},{3,1},{4,6},{5,7},{6,4},{7,5},{8,10},{9,11},{10,... | collective-permute-start | bytes 1622024 | tf_op jit(solution)/shard_map/ppermute | solution.py:224
  96.5 26.2 %collective-permute-start.8 = (f32[135168]{0:T(1024)S(1)}, f32[135168]{0:T(1024)}, u32[]{:S(2)}, u32[]{:S(2)}) collective-permute-start(f32[135168]{0:T(1024)S(1)} %get-tuple-element.107), channel_id=1, source_target_pairs={{0,3},{1,2},{2,1},{3,0},{4,7},{5,6},{6,5},{7,4},{8,11},{9,10},{10,... | collective-permute-start | bytes 1622024 | tf_op jit(solution)/shard_map/ppermute | solution.py:224
  124.2 18.9 %copy-start.5 = (f32[4,8,32,256]{3,2,1,0:T(8,128)S(1)}, f32[4,8,32,256]{3,2,1,0:T(8,128)}, u32[]{:S(2)}) copy-start(f32[4,8,32,256]{3,2,1,0:T(8,128)} %get-tuple-element.110) | copy-start | bytes 3145732
  124.3 10.3 %collective-permute-start.10 = (f32[33792]{0:T(1024)S(1)}, f32[33792]{0:T(1024)S(1)}, u32[]{:S(2)}, u32[]{:S(2)}) collective-permute-start(f32[33792]{0:T(1024)S(1)} %get-tuple-element.119), channel_id=1, source_target_pairs={{0,8},{1,9},{2,10},{3,11},{4,12},{5,13},{6,14},{7,15},{8,0},{9,1},... | collective-permute-start | bytes 405512 | tf_op jit(solution)/shard_map/ppermute | solution.py:224
  124.3 10.2 %collective-permute-start.11 = (f32[33792]{0:T(1024)S(1)}, f32[33792]{0:T(1024)S(1)}, u32[]{:S(2)}, u32[]{:S(2)}) collective-permute-start(f32[33792]{0:T(1024)S(1)} %get-tuple-element.118), channel_id=1, source_target_pairs={{0,12},{1,13},{2,14},{3,15},{4,8},{5,9},{6,10},{7,11},{8,4},{9,5},... | collective-permute-start | bytes 405512 | tf_op jit(solution)/shard_map/ppermute | solution.py:224
  124.4 12.3 %collective-permute-start.9 = (f32[33792]{0:T(1024)S(1)}, f32[33792]{0:T(1024)S(1)}, u32[]{:S(2)}, u32[]{:S(2)}) collective-permute-start(f32[33792]{0:T(1024)S(1)} %get-tuple-element.117), channel_id=1, source_target_pairs={{0,4},{1,5},{2,6},{3,7},{4,0},{5,1},{6,2},{7,3},{8,12},{9,13},{10,... | collective-permute-start | bytes 405512 | tf_op jit(solution)/shard_map/ppermute | solution.py:224
  136.8 12.2 %collective-permute-start.12 = (bf16[33792]{0:T(1024)(128)(2,1)S(1)}, bf16[33792]{0:T(1024)(128)(2,1)S(1)}, u32[]{:S(2)}, u32[]{:S(2)}) collective-permute-start(bf16[33792]{0:T(1024)(128)(2,1)S(1)} %get-tuple-element.80), channel_id=1, source_target_pairs={{0,4},{1,5},{2,6},{3,7},{4,0},{5,1},{6,2},{7,3},{8,12},{9,13},{10,... | collective-permute-start | bytes 202760 | tf_op jit(solution)/shard_map/ppermute | solution.py:235
  137.5 12.5 %collective-permute-start.13 = (bf16[33792]{0:T(1024)(128)(2,1)S(1)}, bf16[33792]{0:T(1024)(128)(2,1)S(1)}, u32[]{:S(2)}, u32[]{:S(2)}) collective-permute-start(bf16[33792]{0:T(1024)(128)(2,1)S(1)} %get-tuple-element.80), channel_id=1, source_target_pairs={{0,8},{1,9},{2,10},{3,11},{4,12},{5,13},{6,14},{7,15},{8,0},{9,1},... | collective-permute-start | bytes 202760 | tf_op jit(solution)/shard_map/ppermute | solution.py:235
  138.2 12.6 %collective-permute-start.14 = (bf16[33792]{0:T(1024)(128)(2,1)S(1)}, bf16[33792]{0:T(1024)(128)(2,1)S(1)}, u32[]{:S(2)}, u32[]{:S(2)}) collective-permute-start(bf16[33792]{0:T(1024)(128)(2,1)S(1)} %get-tuple-element.80), channel_id=1, source_target_pairs={{0,12},{1,13},{2,14},{3,15},{4,8},{5,9},{6,10},{7,11},{8,4},{9,5},... | collective-permute-start | bytes 202760 | tf_op jit(solution)/shard_map/ppermute | solution.py:235
  142.2 6.6 %collective-permute-start.5 = (bf16[4,8,3,256]{3,2,1,0:T(4,128)(2,1)S(1)}, bf16[4,8,3,256]{3,2,1,0:T(4,128)(2,1)S(1)}, u32[]{:S(2)}, u32[]{:S(2)}) collective-permute-start(bf16[4,8,3,256]{3,2,1,0:T(4,128)(2,1)S(1)} %slice.1516), channel_id=1, source_target_pairs={{0,15},{1,14},{2,13},{3,12},{4,11},{5,10},{6,9},{7,8},{8,7},{9,6},... | collective-permute-start | bytes 147464 | tf_op jit(solution)/shard_map/ppermute | solution.py:180
  151.6 5.6 %collective-permute-start.15 = (bf16[135168]{0:T(1024)(128)(2,1)S(1)}, bf16[135168]{0:T(1024)(128)(2,1)S(1)}, u32[]{:S(2)}, u32[]{:S(2)}) collective-permute-start(bf16[135168]{0:T(1024)(128)(2,1)S(1)} %dynamic_update_slice.27), channel_id=1, source_target_pairs={{0,1},{1,0},{2,3},{3,2},{4,5},{5,4},{6,7},{7,6},{8,9},{9,8},{10,11... | collective-permute-start | bytes 811016 | tf_op jit(solution)/shard_map/ppermute | solution.py:235
  151.7 9.3 %collective-permute-start.16 = (bf16[135168]{0:T(1024)(128)(2,1)S(1)}, bf16[135168]{0:T(1024)(128)(2,1)S(1)}, u32[]{:S(2)}, u32[]{:S(2)}) collective-permute-start(bf16[135168]{0:T(1024)(128)(2,1)S(1)} %dynamic_update_slice.27), channel_id=1, source_target_pairs={{0,2},{1,3},{2,0},{3,1},{4,6},{5,7},{6,4},{7,5},{8,10},{9,11},{10,... | collective-permute-start | bytes 811016 | tf_op jit(solution)/shard_map/ppermute | solution.py:235
  152.3 13.7 %collective-permute-start.17 = (bf16[135168]{0:T(1024)(128)(2,1)S(1)}, bf16[135168]{0:T(1024)(128)(2,1)S(1)}, u32[]{:S(2)}, u32[]{:S(2)}) collective-permute-start(bf16[135168]{0:T(1024)(128)(2,1)S(1)} %dynamic_update_slice.27), channel_id=1, source_target_pairs={{0,3},{1,2},{2,1},{3,0},{4,7},{5,6},{6,5},{7,4},{8,11},{9,10},{10,... | collective-permute-start | bytes 811016 | tf_op jit(solution)/shard_map/ppermute | solution.py:235
  (42 other events, 48.2 us)

commit v5 on v4

--- a/solution.py
+++ b/solution.py
@@ -211,7 +211,7 @@
 def radix_allreduce(flat, axis, gather_dtype):
     size = lax.axis_size(axis)
     nbits = size.bit_length() - 1
-    groups = [list(range(b, min(b + 2, nbits))) for b in range(0, nbits, 2)]
+    groups = [[0]] + [list(range(b, min(b + 2, nbits))) for b in range(1, nbits, 2)]
     idx = lax.axis_index(axis)
     cur = flat
     for bits in groups:

time: 174 us -> 175 us (level)
  local copies, waits for them, and re-layouts: 36.5 us -> 44.9 us
  waiting for transfers between devices: 46.2 us -> 38.5 us
  other arithmetic: 44.6 us -> 48.3 us
  starting transfers between devices: 27.1 us -> 23.5 us
    ppermute x6 -> x5, waiting for transfers between devices: 33.2 us -> 23.3 us  [radix_allreduce(): lax.ppermute(send, axis, [(i, i ^ d << low) for i in range(size)])]
    dynamic_update_slice x1 -> x2, local copies, waits for them, and re-layouts: 2.65 us -> 6.48 us  [radix_allreduce(): lax.dynamic_update_slice_in_dim(jnp.zeros((part * radix,), cur.dtype), cu...]
    another operation x7, local copies, waits for them, and re-layouts: 0.2 us -> 3.63 us  [local_step(): kernel_rows.append(jnp.stack(kernel_cols))]
    ppermute x6 -> x5, waiting for transfers between devices: 3.44 us -> 6.63 us  [radix_allreduce(): recv = lax.ppermute(cur, axis, [(i, i ^ d << low) for i in range(size)])]
    ppermute x6 -> x5, starting transfers between devices: 6.38 us -> 3.7 us  [radix_allreduce(): recv = lax.ppermute(cur, axis, [(i, i ^ d << low) for i in range(size)])]
    add x1 -> x2, other arithmetic: 1.5 us -> 3.45 us  [radix_allreduce(): total + lax.ppermute(send, axis, [(i, i ^ d << low) for i in range(size)])]
    ppermute x6 -> x5, starting transfers between devices: 5.4 us -> 3.61 us  [radix_allreduce(): lax.ppermute(send, axis, [(i, i ^ d << low) for i in range(size)])]
    dynamic_update_slice x6 -> x5, local copies, waits for them, and re-layouts: 10.3 us -> 9.96 us  [radix_allreduce(): full = lax.dynamic_update_slice_in_dim(full, recv, (sub ^ d) * part, 0)]
  transfers between devices with their start and end apart: 18 -> 16, of which waited for: 9 -> 9; matrix products, arithmetic and copies ran while one was open for 16% -> 16% of each run, Pallas kernels for 0% -> 0%
where the time goes in v5:
time: 175 us; the launch traced here: 174 us
  other arithmetic  48.3 us (28%)
  local copies, waits for them, and re-layouts  44.9 us (26%)
  waiting for transfers between devices  38.5 us (22%)
  starting transfers between devices  23.5 us (13%)
  matrix products  16.3 us (9%)
  between operations  2.78 us (2%)
    ppermute x5, waiting for transfers between devices, radix_allreduce(): lax.ppermute(send, axis, [(i, i ^ d << low) for i in range(size)])  23.3 us
    unnamed x240, local copies, waits for them, and re-layouts  12.3 us
    add x1, other arithmetic, on_device(): grad_ext + dw_kernel[lon_off, lat_off] * padded[:, 6 - lon_off:6 - lon_of...  10.1 us
    reduce_sum x4, other arithmetic, local_step(): jnp.sum(grad_depth * extended[:, lon_off:lon_off + lon_dev, lat_off:lat_o...  9.99 us
    dynamic_update_slice x5, local copies, waits for them, and re-layouts, radix_allreduce(): full = lax.dynamic_update_slice_in_dim(full, recv, (sub ^ d) * part, 0)  9.96 us
    reduce_sum x1, other arithmetic, local_step(): mean_val = jnp.mean(depth, axis=-1, keepdims=True)  9.28 us
    ppermute x2, starting transfers between devices, with_halo(): after = lax.ppermute(leading, axis, down)  7.64 us
    ppermute x2, starting transfers between devices, mirrored(): return lax.ppermute(x, axis, [(i, size - 1 - i) for i in range(size)])  7.16 us
  transfers between devices with their start and end apart: 16, of which 9 were waited for; matrix products, arithmetic and copies ran while one was open for 16% of the time, Pallas kernels for 0%

profile of v5, /device:TPU:0, one launch (start us, length us, event | category | flops | bytes accessed | tf_op | source)
XLA Modules:
  0.0 174.3 jit_solution(4376492888836545384)
XLA Ops:
  0.7 1.0 slice.724
  1.7 5.5 %collective-permute-start = (bf16[4,8,3,256]{3,2,1,0:T(4,128)(2,1)S(1)}, bf16[4,8,3,256]{3,2,1,0:T(4,128)(2,1)S(1)}, u32[]{:S(2)}, u32[]{:S(2)}) collective-permute-start(bf16[4,8,3,256]{3,2,1,0:T(4,128)(2,1)S(1)} %slice.724), channel_id=1, source_target_pairs={{0,15},{1,14},{2,13},{3,12},{4,11},{5,10},{6,9},{7,8},{8,7},{9,6},... | collective-permute-start | bytes 147464 | tf_op jit(solution)/shard_map/ppermute | solution.py:180
  7.2 1.0 fusion.216
  8.3 1.0 fusion.217
  9.5 1.5 fusion.218
  11.1 0.8 copy.25
  12.1 1.3 pad_maximum_fusion.9
  14.1 3.8 %collective-permute-start.2 = (bf16[4,3,38,256]{3,2,1,0:T(8,128)(2,1)S(1)}, bf16[4,3,38,256]{3,2,1,0:T(8,128)(2,1)S(1)}, u32[]{:S(2)}, u32[]{:S(2)}) collective-permute-start(bf16[4,3,38,256]{3,2,1,0:T(8,128)(2,1)S(1)} %get-tuple-element.116), channel_id=1, source_target_pairs={{1,0},{2,1},{3,2},{4,3},{5,4},{6,5},{7,6},{8,7},{9,8},{10,9},{11,1... | collective-permute-start | bytes 700424 | tf_op jit(solution)/shard_map/ppermute | solution.py:27
  18.1 3.8 %collective-permute-done.1 = bf16[4,3,38,256]{3,2,1,0:T(8,128)(2,1)S(1)} collective-permute-done((bf16[4,3,38,256]{3,2,1,0:T(8,128)(2,1)S(1)}, bf16[4,3,38,256]{3,2,1,0:T(8,128)(2,1)S(1)}, u32[]{:S(2)}, u32[]{:S(2)}) %collective-permute-start.1) | collective-permute-done | bytes 233504 | tf_op jit(solution)/shard_map/ppermute | solution.py:26
  22.7 9.3 %fusion.211 = (f32[4,8,32]{2,1,0:T(8,128)S(1)}, f32[4,8,32,256]{3,2,1,0:T(8,128)S(1)}) fusion(bf16[4,11,38,256]{3,2,1,0:T(8,128)(2,1)S(1)} %get-tuple-element.114, f32[256]{0:T(256)} %bitcast.48, f32[256]{0:T(256)} %bitcast.47, f32[256]{0:T(256)S(1)} %bitcast.340, f32[256]{0:T(256)S(1)} %bitcast.342, f32[256]{0:T(256)S(1)} %bitcast.344, ...), kind=kLoop, calls=%fused_computation.484 | loop fusion | flops 43514880 | bytes 23746560 | tf_op jit(solution)/shard_map/reduce_sum | solution.py:62
  36.9 1.0 fusion.209
  38.0 3.1 %multiply_reduce_fusion.7 = (f32[256]{0:T(256)}, f32[256]{0:T(256)}, f32[256]{0:T(256)}, f32[256]{0:T(256)}, f32[8,32,256]{2,1,0:T(8,128)S(1)}, /*index=5*/f32[8...) fusion(f32[256]{0:T(256)S(1)} %copy-done.20, ...), kind=kLoop, calls=%fused_computation.429 | loop fusion | flops 7863296 | bytes 2497536 | tf_op jit(solution)/shard_map/reduce_sum | solution.py:117
  41.8 1.5 fusion.203
  43.6 0.9 fusion.221
  44.5 1.5 fusion.201
  46.0 1.5 fusion.205
  47.5 1.5 fusion.207
  49.0 0.9 fusion.222
  49.9 0.9 fusion.220
  50.8 0.9 fusion.219
  52.4 4.1 %fusion.148 = (f32[256]{0:T(256)}, f32[256]{0:T(256)}, f32[256]{0:T(256)}, f32[256]{0:T(256)}, f32[256]{0:T(256)}, /*index=5*/f32[256]{0:T(256)}, f32[256]{0:T(2...) fusion(bf16[4,11,38,256]{3,2,1,0:T(8,128)(2,1)S(1)} %get-tuple-, ...), kind=kLoop, calls=%fused_computation.324 | loop fusion | flops 16772608 | bytes 12618752 | tf_op jit(solution)/shard_map/reduce_sum | solution.py:154
  56.5 2.3 %fusion.130 = (f32[256]{0:T(256)}, f32[256]{0:T(256)}, f32[256]{0:T(256)}, f32[256]{0:T(256)}, f32[256]{0:T(256)}, /*index=5*/f32[256]{0:T(256)}, f32[256]{0:T(2...) fusion(f32[4,8,32,256]{3,2,1,0:T(8,128)S(1)} %get-tuple-element.93, ...), kind=kLoop, calls=%fused_computation.306 | loop fusion | flops 12842240 | bytes 3255296 | tf_op jit(solution)/shard_map/reduce_sum | solution.py:154
  58.8 3.2 %fusion.97 = (f32[256]{0:T(256)}, f32[256]{0:T(256)}, f32[256]{0:T(256)}, f32[256]{0:T(256)}, f32[256]{0:T(256)}, /*index=5*/f32[256]{0:T(256)}, f32[256]{0:T(25...) fusion(f32[4,8,32,256]{3,2,1,0:T(8,128)S(1)} %get-tuple-element, ...), kind=kLoop, calls=%fused_computation.273 | loop fusion | flops 14151168 | bytes 10504192 | tf_op jit(solution)/shard_map/reduce_sum | solution.py:154
  62.4 0.9 fusion.214
  66.7 1.2 copy.27
  70.1 0.7 stack.263
  72.3 3.9 %collective-permute-start.4 = (f32[4,3,32,256]{3,2,1,0:T(8,128)}, f32[4,3,32,256]{3,2,1,0:T(8,128)S(1)}, u32[]{:S(2)}, u32[]{:S(2)}) collective-permute-start(f32[4,3,32,256]{3,2,1,0:T(8,128)} %get-tuple-element.112), channel_id=1, source_target_pairs={{1,0},{2,1},{3,2},{4,3},{5,4},{6,5},{7,6},{8,7},{9,8},{10,9},{11,1... | collective-permute-start | bytes 1179656 | tf_op jit(solution)/shard_map/ppermute | solution.py:27
  76.2 1.4 constant_dynamic-update-slice_fusion.7
  77.6 1.3 constant_dynamic-update-slice_fusion.15
  78.9 1.3 constant_dynamic-update-slice_fusion.14
  80.2 1.3 constant_dynamic-update-slice_fusion.13
  81.6 2.3 %constant_dynamic-update-slice_fusion.12 = f32[539136]{0:T(1024)} fusion(f32[539136]{0:T(1024)} %constant_dynamic-update-slice_fusion.13, f32[262144]{0:T(1024)} %bitcast.301), kind=kLoop, calls=%fused_computation.464 | loop fusion | bytes 2097152
  83.8 1.4 constant_dynamic-update-slice_fusion.11
  85.2 1.1 constant_dynamic-update-slice_fusion.10
  86.3 1.3 constant_dynamic-update-slice_fusion.9
  88.7 10.1 %fusion.3 = f32[4,8,38,256]{3,2,1,0:T(8,128)S(1)} fusion(f32[4,14,44,256]{3,2,1,0:T(8,128)S(1)} %select_maximum_fusion, f32[256]{0:T(256)} %bitcast.48, f32[256]{0:T(256)} %bitcast.47, f32[256]{0:T(256)S(1)} %bitcast.341, f32[256]{0:T(256)S(1)} %bitcast.343, f32[256]{0:T(256)S(1)} %bitcast.345, f32[256]{0:T(256)S(1)} %bitcast.347, f32[256]{0:T(256)S(1)} %bitcast.349, ...), kind=kLoop, calls=%fused_computation.127 | loop fusion | flops 30195712 | bytes 62309376 | tf_op jit(solution)/shard_map/add | solution.py:290
  98.9 1.3 multiply_reduce_fusion
  100.2 1.1 copy-done.3
  101.3 1.2 pad_dynamic-slice_fusion
  102.5 3.0 %collective-permute-done.6 = f32[270336]{0:T(1024)} collective-permute-done((f32[270336]{0:T(1024)}, f32[270336]{0:T(1024)}, u32[]{:S(2)}, u32[]{:S(2)}) %collective-permute-start.6) | collective-permute-done | bytes 1081376 | tf_op jit(solution)/shard_map/ppermute | solution.py:224
  105.5 2.4 %fusion.51 = f32[270336]{0:T(1024)} fusion(f32[270336]{0:T(1024)} %collective-permute-done.6, s32[]{:T(128)S(6)} %select_n.42, f32[539136]{0:T(1024)S(1)} %constant_dynamic-update-slice_fusion.8), kind=kLoop, calls=%fused_computation.227 | loop fusion | flops 270336 | bytes 4319236 | tf_op jit(solution)/shard_map/add | solution.py:224
  108.0 1.2 fusion.213
  109.3 3.4 %collective-permute-start.9 = (f32[67584]{0:T(1024)S(1)}, f32[67584]{0:T(1024)S(1)}, u32[]{:S(2)}, u32[]{:S(2)}) collective-permute-start(f32[67584]{0:T(1024)S(1)} %get-tuple-element.107), channel_id=1, source_target_pairs={{0,6},{1,7},{2,4},{3,5},{4,2},{5,3},{6,0},{7,1},{8,14},{9,15},{10,... | collective-permute-start | bytes 811016 | tf_op jit(solution)/shard_map/ppermute | solution.py:224
  112.7 5.0 %collective-permute-done.7 = f32[67584]{0:T(1024)S(1)} collective-permute-done((f32[67584]{0:T(1024)S(1)}, f32[67584]{0:T(1024)S(1)}, u32[]{:S(2)}, u32[]{:S(2)}) %collective-permute-start.7) | collective-permute-done | bytes 270368 | tf_op jit(solution)/shard_map/ppermute | solution.py:224
  117.7 0.9 collective-permute-done.8
  118.6 6.1 %collective-permute-done.9 = f32[67584]{0:T(1024)S(1)} collective-permute-done((f32[67584]{0:T(1024)S(1)}, f32[67584]{0:T(1024)S(1)}, u32[]{:S(2)}, u32[]{:S(2)}) %collective-permute-start.9) | collective-permute-done | bytes 270368 | tf_op jit(solution)/shard_map/ppermute | solution.py:224
  124.7 1.0 add_add_fusion
  125.8 8.3 %collective-permute-done.10 = f32[33792]{0:T(1024)S(1)} collective-permute-done((f32[33792]{0:T(1024)S(1)}, f32[33792]{0:T(1024)S(1)}, u32[]{:S(2)}, u32[]{:S(2)}) %collective-permute-start.10) | collective-permute-done | bytes 135200 | tf_op jit(solution)/shard_map/ppermute | solution.py:224
  134.2 5.2 %collective-permute-done.11 = bf16[33792]{0:T(1024)(128)(2,1)S(1)} collective-permute-done((bf16[33792]{0:T(1024)(128)(2,1)S(1)}, bf16[33792]{0:T(1024)(128)(2,1)S(1)}, u32[]{:S(2)}, u32[]{:S(2)}) %collective-permute-start.11) | collective-permute-done | bytes 67616 | tf_op jit(solution)/shard_map/ppermute | solution.py:235
  140.1 0.7 collective-permute-start.12
  140.9 2.8 %collective-permute-start.14 = (bf16[67584]{0:T(1024)(128)(2,1)S(1)}, bf16[67584]{0:T(1024)(128)(2,1)S(1)}, u32[]{:S(2)}, u32[]{:S(2)}) collective-permute-start(bf16[67584]{0:T(1024)(128)(2,1)S(1)} %dynamic_update_slice.25), channel_id=1, source_target_pairs={{0,6},{1,7},{2,4},{3,5},{4,2},{5,3},{6,0},{7,1},{8,14},{9,15},{10,... | collective-permute-start | bytes 405512 | tf_op jit(solution)/shard_map/ppermute | solution.py:235
  143.7 1.5 dynamic_update_slice.26
  145.2 1.5 collective-permute-done.12
  146.7 1.4 dynamic_update_slice.27
  148.1 1.5 dynamic_update_slice.28
  149.6 1.4 dynamic_update_slice.29
  151.1 1.0 slice.1516
  152.0 1.7 collective-permute-start.5
  153.8 4.8 %collective-permute-done.5 = bf16[4,8,3,256]{3,2,1,0:T(4,128)(2,1)S(1)} collective-permute-done((bf16[4,8,3,256]{3,2,1,0:T(4,128)(2,1)S(1)}, bf16[4,8,3,256]{3,2,1,0:T(4,128)(2,1)S(1)}, u32[]{:S(2)}, u32[]{:S(2)}) %collective-permute-start.5) | collective-permute-done | bytes 49184 | tf_op jit(solution)/shard_map/ppermute | solution.py:180
  158.8 0.9 pad_maximum_fusion.6
  159.8 5.0 %dynamic_update_slice.30 = bf16[540672]{0:T(1024)(128)(2,1)S(1)} dynamic-update-slice(bf16[540672]{0:T(1024)(128)(2,1)S(1)} %broadcast_in_dim.6, bf16[270336]{0:T(1024)(128)(2,1)S(1)} %dynamic_update_slice.29, s32[]{:T(128)S(6)} %select_n.42) | dynamic-update-slice | bytes 1081348 | tf_op jit(solution)/shard_map/dynamic_update_slice | solution.py:231
  164.8 5.0 %dynamic_update_slice.31 = bf16[540672]{0:T(1024)(128)(2,1)S(1)} dynamic-update-slice(bf16[540672]{0:T(1024)(128)(2,1)S(1)} %dynamic_update_slice.30, bf16[270336]{0:T(1024)(128)(2,1)S(1)} %collective-permute-done.15, s32[]{:T(128)S(6)} %select_n.43) | dynamic-update-slice | bytes 1081348 | tf_op jit(solution)/shard_map/dynamic_update_slice | solution.py:236
  171.3 1.1 mul.1877
  172.4 1.3 mul.1881
  (303 shorter events, 19.6 us)
Async XLA Ops:
  0.6 33.5 %copy-start = (bf16[1024,256]{1,0:T(8,128)(2,1)S(1)}, bf16[1024,256]{1,0:T(8,128)(2,1)}, u32[]{:S(2)}) copy-start(bf16[1024,256]{1,0:T(8,128)(2,1)} %param.23) | copy-start | bytes 1572868
  0.7 21.2 %copy-start.2 = (bf16[4,8,32,256]{3,2,1,0:T(8,128)(2,1)S(1)}, bf16[4,8,32,256]{3,2,1,0:T(8,128)(2,1)}, u32[]{:S(2)}) copy-start(bf16[4,8,32,256]{3,2,1,0:T(8,128)(2,1)} %param.13) | copy-start | bytes 1572868
  0.7 17.3 %copy-start.18 = (s32[8,32]{1,0:T(8,128)S(1)}, s32[8,32]{1,0:T(8,128)}, u32[]{:S(2)}) copy-start(s32[8,32]{1,0:T(8,128)} %param.16) | copy-start | bytes 3076
  1.7 10.2 %collective-permute-start = (bf16[4,8,3,256]{3,2,1,0:T(4,128)(2,1)S(1)}, bf16[4,8,3,256]{3,2,1,0:T(4,128)(2,1)S(1)}, u32[]{:S(2)}, u32[]{:S(2)}) collective-permute-start(bf16[4,8,3,256]{3,2,1,0:T(4,128)(2,1)S(1)} %slice.724), channel_id=1, source_target_pairs={{0,15},{1,14},{2,13},{3,12},{4,11},{5,10},{6,9},{7,8},{8,7},{9,6},... | collective-permute-start | bytes 147464 | tf_op jit(solution)/shard_map/ppermute | solution.py:180
  8.2 14.1 %copy-start.21 = (f32[1,1,256]{2,1,0:T(1,128)}, f32[1,1,256]{2,1,0:T(1,128)S(1)}, u32[]{:S(2)}) copy-start(f32[1,1,256]{2,1,0:T(1,128)S(1)} %get-tuple-element.129) | copy-start | bytes 3076
  8.2 14.1 %copy-start.23 = (f32[1,1,256]{2,1,0:T(1,128)}, f32[1,1,256]{2,1,0:T(1,128)S(1)}, u32[]{:S(2)}) copy-start(f32[1,1,256]{2,1,0:T(1,128)S(1)} %get-tuple-element.130) | copy-start | bytes 3076
  8.2 14.1 %copy-start.25 = (f32[1,1,256]{2,1,0:T(1,128)}, f32[1,1,256]{2,1,0:T(1,128)S(1)}, u32[]{:S(2)}) copy-start(f32[1,1,256]{2,1,0:T(1,128)S(1)} %get-tuple-element.131) | copy-start | bytes 3076
  8.2 14.1 %copy-start.27 = (f32[1,1,256]{2,1,0:T(1,128)}, f32[1,1,256]{2,1,0:T(1,128)S(1)}, u32[]{:S(2)}) copy-start(f32[1,1,256]{2,1,0:T(1,128)S(1)} %get-tuple-element.132) | copy-start | bytes 3076
  8.2 14.1 %copy-start.29 = (f32[1,1,256]{2,1,0:T(1,128)}, f32[1,1,256]{2,1,0:T(1,128)S(1)}, u32[]{:S(2)}) copy-start(f32[1,1,256]{2,1,0:T(1,128)S(1)} %get-tuple-element.133) | copy-start | bytes 3076
  8.2 14.1 %copy-start.31 = (f32[1,1,256]{2,1,0:T(1,128)}, f32[1,1,256]{2,1,0:T(1,128)S(1)}, u32[]{:S(2)}) copy-start(f32[1,1,256]{2,1,0:T(1,128)S(1)} %get-tuple-element.134) | copy-start | bytes 3076
  8.2 14.1 %copy-start.33 = (f32[1,1,256]{2,1,0:T(1,128)}, f32[1,1,256]{2,1,0:T(1,128)S(1)}, u32[]{:S(2)}) copy-start(f32[1,1,256]{2,1,0:T(1,128)S(1)} %get-tuple-element.135) | copy-start | bytes 3076
  8.3 14.1 %copy-start.35 = (f32[1,1,256]{2,1,0:T(1,128)}, f32[1,1,256]{2,1,0:T(1,128)S(1)}, u32[]{:S(2)}) copy-start(f32[1,1,256]{2,1,0:T(1,128)S(1)} %get-tuple-element.136) | copy-start | bytes 3076
  8.3 14.1 %copy-start.37 = (f32[1,1,256]{2,1,0:T(1,128)}, f32[1,1,256]{2,1,0:T(1,128)S(1)}, u32[]{:S(2)}) copy-start(f32[1,1,256]{2,1,0:T(1,128)S(1)} %get-tuple-element.137) | copy-start | bytes 3076
  8.3 14.1 %copy-start.39 = (f32[1,1,256]{2,1,0:T(1,128)}, f32[1,1,256]{2,1,0:T(1,128)S(1)}, u32[]{:S(2)}) copy-start(f32[1,1,256]{2,1,0:T(1,128)S(1)} %get-tuple-element.138) | copy-start | bytes 3076
  8.3 14.1 %copy-start.41 = (f32[1,1,256]{2,1,0:T(1,128)}, f32[1,1,256]{2,1,0:T(1,128)S(1)}, u32[]{:S(2)}) copy-start(f32[1,1,256]{2,1,0:T(1,128)S(1)} %get-tuple-element.139) | copy-start | bytes 3076
  9.3 13.1 %copy-start.43 = (f32[1,1,256]{2,1,0:T(1,128)}, f32[1,1,256]{2,1,0:T(1,128)S(1)}, u32[]{:S(2)}) copy-start(f32[1,1,256]{2,1,0:T(1,128)S(1)} %get-tuple-element.140) | copy-start | bytes 3076
  9.3 13.1 %copy-start.45 = (f32[1,1,256]{2,1,0:T(1,128)}, f32[1,1,256]{2,1,0:T(1,128)S(1)}, u32[]{:S(2)}) copy-start(f32[1,1,256]{2,1,0:T(1,128)S(1)} %get-tuple-element.141) | copy-start | bytes 3076
  9.3 13.1 %copy-start.47 = (f32[1,1,256]{2,1,0:T(1,128)}, f32[1,1,256]{2,1,0:T(1,128)S(1)}, u32[]{:S(2)}) copy-start(f32[1,1,256]{2,1,0:T(1,128)S(1)} %get-tuple-element.142) | copy-start | bytes 3076
  9.4 13.1 %copy-start.49 = (f32[1,1,256]{2,1,0:T(1,128)}, f32[1,1,256]{2,1,0:T(1,128)S(1)}, u32[]{:S(2)}) copy-start(f32[1,1,256]{2,1,0:T(1,128)S(1)} %get-tuple-element.143) | copy-start | bytes 3076
  9.4 13.1 %copy-start.51 = (f32[1,1,256]{2,1,0:T(1,128)}, f32[1,1,256]{2,1,0:T(1,128)S(1)}, u32[]{:S(2)}) copy-start(f32[1,1,256]{2,1,0:T(1,128)S(1)} %get-tuple-element.144) | copy-start | bytes 3076
  9.4 13.1 %copy-start.53 = (f32[1,1,256]{2,1,0:T(1,128)}, f32[1,1,256]{2,1,0:T(1,128)S(1)}, u32[]{:S(2)}) copy-start(f32[1,1,256]{2,1,0:T(1,128)S(1)} %get-tuple-element.145) | copy-start | bytes 3076
  9.4 13.1 %copy-start.55 = (f32[1,1,256]{2,1,0:T(1,128)}, f32[1,1,256]{2,1,0:T(1,128)S(1)}, u32[]{:S(2)}) copy-start(f32[1,1,256]{2,1,0:T(1,128)S(1)} %get-tuple-element.146) | copy-start | bytes 3076
  9.4 13.1 %copy-start.57 = (f32[1,1,256]{2,1,0:T(1,128)}, f32[1,1,256]{2,1,0:T(1,128)S(1)}, u32[]{:S(2)}) copy-start(f32[1,1,256]{2,1,0:T(1,128)S(1)} %get-tuple-element.147) | copy-start | bytes 3076
  9.4 13.1 %copy-start.59 = (f32[1,1,256]{2,1,0:T(1,128)}, f32[1,1,256]{2,1,0:T(1,128)S(1)}, u32[]{:S(2)}) copy-start(f32[1,1,256]{2,1,0:T(1,128)S(1)} %get-tuple-element.148) | copy-start | bytes 3076
  9.4 13.1 %copy-start.61 = (f32[1,1,256]{2,1,0:T(1,128)}, f32[1,1,256]{2,1,0:T(1,128)S(1)}, u32[]{:S(2)}) copy-start(f32[1,1,256]{2,1,0:T(1,128)S(1)} %get-tuple-element.149) | copy-start | bytes 3076
  9.4 13.1 %copy-start.63 = (f32[1,1,256]{2,1,0:T(1,128)}, f32[1,1,256]{2,1,0:T(1,128)S(1)}, u32[]{:S(2)}) copy-start(f32[1,1,256]{2,1,0:T(1,128)S(1)} %get-tuple-element.150) | copy-start | bytes 3076
  9.4 13.1 %copy-start.65 = (f32[1,1,256]{2,1,0:T(1,128)}, f32[1,1,256]{2,1,0:T(1,128)S(1)}, u32[]{:S(2)}) copy-start(f32[1,1,256]{2,1,0:T(1,128)S(1)} %get-tuple-element.151) | copy-start | bytes 3076
  9.4 13.1 %copy-start.67 = (f32[1,1,256]{2,1,0:T(1,128)}, f32[1,1,256]{2,1,0:T(1,128)S(1)}, u32[]{:S(2)}) copy-start(f32[1,1,256]{2,1,0:T(1,128)S(1)} %get-tuple-element.152) | copy-start | bytes 3076
  9.5 13.1 %copy-start.69 = (f32[1,1,256]{2,1,0:T(1,128)}, f32[1,1,256]{2,1,0:T(1,128)S(1)}, u32[]{:S(2)}) copy-start(f32[1,1,256]{2,1,0:T(1,128)S(1)} %get-tuple-element.153) | copy-start | bytes 3076
  9.5 13.1 %copy-start.71 = (f32[1,1,256]{2,1,0:T(1,128)}, f32[1,1,256]{2,1,0:T(1,128)S(1)}, u32[]{:S(2)}) copy-start(f32[1,1,256]{2,1,0:T(1,128)S(1)} %get-tuple-element.154) | copy-start | bytes 3076
  9.5 13.1 %copy-start.73 = (f32[1,1,256]{2,1,0:T(1,128)}, f32[1,1,256]{2,1,0:T(1,128)S(1)}, u32[]{:S(2)}) copy-start(f32[1,1,256]{2,1,0:T(1,128)S(1)} %get-tuple-element.155) | copy-start | bytes 3076
  9.5 13.1 %copy-start.75 = (f32[1,1,256]{2,1,0:T(1,128)}, f32[1,1,256]{2,1,0:T(1,128)S(1)}, u32[]{:S(2)}) copy-start(f32[1,1,256]{2,1,0:T(1,128)S(1)} %get-tuple-element.156) | copy-start | bytes 3076
  9.5 13.1 %copy-start.77 = (f32[1,1,256]{2,1,0:T(1,128)}, f32[1,1,256]{2,1,0:T(1,128)S(1)}, u32[]{:S(2)}) copy-start(f32[1,1,256]{2,1,0:T(1,128)S(1)} %get-tuple-element.157) | copy-start | bytes 3076
  9.5 13.1 %copy-start.79 = (f32[1,1,256]{2,1,0:T(1,128)}, f32[1,1,256]{2,1,0:T(1,128)S(1)}, u32[]{:S(2)}) copy-start(f32[1,1,256]{2,1,0:T(1,128)S(1)} %get-tuple-element.158) | copy-start | bytes 3076
  11.0 11.6 %copy-start.81 = (f32[1,1,256]{2,1,0:T(1,128)}, f32[1,1,256]{2,1,0:T(1,128)S(1)}, u32[]{:S(2)}) copy-start(f32[1,1,256]{2,1,0:T(1,128)S(1)} %get-tuple-element.159) | copy-start | bytes 3076
  11.0 11.6 %copy-start.83 = (f32[1,1,256]{2,1,0:T(1,128)}, f32[1,1,256]{2,1,0:T(1,128)S(1)}, u32[]{:S(2)}) copy-start(f32[1,1,256]{2,1,0:T(1,128)S(1)} %get-tuple-element.160) | copy-start | bytes 3076
  11.0 11.6 %copy-start.85 = (f32[1,1,256]{2,1,0:T(1,128)}, f32[1,1,256]{2,1,0:T(1,128)S(1)}, u32[]{:S(2)}) copy-start(f32[1,1,256]{2,1,0:T(1,128)S(1)} %get-tuple-element.161) | copy-start | bytes 3076
  11.0 11.6 %copy-start.87 = (f32[1,1,256]{2,1,0:T(1,128)}, f32[1,1,256]{2,1,0:T(1,128)S(1)}, u32[]{:S(2)}) copy-start(f32[1,1,256]{2,1,0:T(1,128)S(1)} %get-tuple-element.162) | copy-start | bytes 3076
  11.0 11.6 %copy-start.89 = (f32[1,1,256]{2,1,0:T(1,128)}, f32[1,1,256]{2,1,0:T(1,128)S(1)}, u32[]{:S(2)}) copy-start(f32[1,1,256]{2,1,0:T(1,128)S(1)} %get-tuple-element.163) | copy-start | bytes 3076
  11.0 11.6 %copy-start.91 = (f32[1,1,256]{2,1,0:T(1,128)}, f32[1,1,256]{2,1,0:T(1,128)S(1)}, u32[]{:S(2)}) copy-start(f32[1,1,256]{2,1,0:T(1,128)S(1)} %get-tuple-element.164) | copy-start | bytes 3076
  11.0 11.6 %copy-start.92 = (f32[1,1,256]{2,1,0:T(1,128)}, f32[1,1,256]{2,1,0:T(1,128)S(1)}, u32[]{:S(2)}) copy-start(f32[1,1,256]{2,1,0:T(1,128)S(1)} %get-tuple-element.165) | copy-start | bytes 3076
  11.0 11.6 %copy-start.93 = (f32[1,1,256]{2,1,0:T(1,128)}, f32[1,1,256]{2,1,0:T(1,128)S(1)}, u32[]{:S(2)}) copy-start(f32[1,1,256]{2,1,0:T(1,128)S(1)} %get-tuple-element.166) | copy-start | bytes 3076
  11.1 11.6 %copy-start.94 = (f32[1,1,256]{2,1,0:T(1,128)}, f32[1,1,256]{2,1,0:T(1,128)S(1)}, u32[]{:S(2)}) copy-start(f32[1,1,256]{2,1,0:T(1,128)S(1)} %get-tuple-element.167) | copy-start | bytes 3076
  13.4 8.5 %collective-permute-start.1 = (bf16[4,3,38,256]{3,2,1,0:T(8,128)(2,1)S(1)}, bf16[4,3,38,256]{3,2,1,0:T(8,128)(2,1)S(1)}, u32[]{:S(2)}, u32[]{:S(2)}) collective-permute-start(bf16[4,3,38,256]{3,2,1,0:T(8,128)(2,1)S(1)} %get-tuple-element.115), channel_id=1, source_target_pairs={{0,1},{1,2},{2,3},{3,4},{4,5},{5,6},{6,7},{7,8},{8,9},{9,10},{10,1... | collective-permute-start | bytes 700424 | tf_op jit(solution)/shard_map/ppermute | solution.py:26
  14.1 7.8 %collective-permute-start.2 = (bf16[4,3,38,256]{3,2,1,0:T(8,128)(2,1)S(1)}, bf16[4,3,38,256]{3,2,1,0:T(8,128)(2,1)S(1)}, u32[]{:S(2)}, u32[]{:S(2)}) collective-permute-start(bf16[4,3,38,256]{3,2,1,0:T(8,128)(2,1)S(1)} %get-tuple-element.116), channel_id=1, source_target_pairs={{1,0},{2,1},{3,2},{4,3},{5,4},{6,5},{7,6},{8,7},{9,8},{10,9},{11,1... | collective-permute-start | bytes 700424 | tf_op jit(solution)/shard_map/ppermute | solution.py:27
  71.7 16.2 %collective-permute-start.3 = (f32[4,3,32,256]{3,2,1,0:T(8,128)}, f32[4,3,32,256]{3,2,1,0:T(8,128)S(1)}, u32[]{:S(2)}, u32[]{:S(2)}) collective-permute-start(f32[4,3,32,256]{3,2,1,0:T(8,128)} %get-tuple-element.111), channel_id=1, source_target_pairs={{0,1},{1,2},{2,3},{3,4},{4,5},{5,6},{6,7},{7,8},{8,9},{9,10},{10,1... | collective-permute-start | bytes 1179656 | tf_op jit(solution)/shard_map/ppermute | solution.py:26
  72.3 15.6 %collective-permute-start.4 = (f32[4,3,32,256]{3,2,1,0:T(8,128)}, f32[4,3,32,256]{3,2,1,0:T(8,128)S(1)}, u32[]{:S(2)}, u32[]{:S(2)}) collective-permute-start(f32[4,3,32,256]{3,2,1,0:T(8,128)} %get-tuple-element.112), channel_id=1, source_target_pairs={{1,0},{2,1},{3,2},{4,3},{5,4},{6,5},{7,6},{8,7},{9,8},{10,9},{11,1... | collective-permute-start | bytes 1179656 | tf_op jit(solution)/shard_map/ppermute | solution.py:27
  88.7 10.2 %copy-start.7 = (f32[8,32,256]{2,1,0:T(8,128)S(1)}, f32[8,32,256]{2,1,0:T(8,128)}, u32[]{:S(2)}) copy-start(f32[8,32,256]{2,1,0:T(8,128)} %copy-done.6) | copy-start | bytes 786436
  88.7 10.2 %copy-start.9 = (f32[256,256]{1,0:T(8,128)S(1)}, f32[256,256]{1,0:T(8,128)}, u32[]{:S(2)}) copy-start(f32[256,256]{1,0:T(8,128)} %copy-done.8) | copy-start | bytes 786436
  88.7 10.2 %copy-start.11 = (f32[256,256]{1,0:T(8,128)S(1)}, f32[256,256]{1,0:T(8,128)}, u32[]{:S(2)}) copy-start(f32[256,256]{1,0:T(8,128)} %copy-done.10) | copy-start | bytes 786436
  88.7 10.2 %copy-start.13 = (f32[256,256]{1,0:T(8,128)S(1)}, f32[256,256]{1,0:T(8,128)}, u32[]{:S(2)}) copy-start(f32[256,256]{1,0:T(8,128)} %copy-done.12) | copy-start | bytes 786436
  88.7 10.2 %copy-start.15 = (f32[256,256]{1,0:T(8,128)S(1)}, f32[256,256]{1,0:T(8,128)}, u32[]{:S(2)}) copy-start(f32[256,256]{1,0:T(8,128)} %copy-done.14) | copy-start | bytes 786436
  102.5 3.0 %collective-permute-start.6 = (f32[270336]{0:T(1024)}, f32[270336]{0:T(1024)}, u32[]{:S(2)}, u32[]{:S(2)}) collective-permute-start(f32[270336]{0:T(1024)} %pad_dynamic-slice_fusion), channel_id=1, source_target_pairs={{0,1},{1,0},{2,3},{3,2},{4,5},{5,4},{6,7},{7,6},{8,9},{9,8},{10,11... | collective-permute-start | bytes 3244040 | tf_op jit(solution)/shard_map/ppermute | solution.py:224
  109.1 8.6 %collective-permute-start.7 = (f32[67584]{0:T(1024)S(1)}, f32[67584]{0:T(1024)S(1)}, u32[]{:S(2)}, u32[]{:S(2)}) collective-permute-start(f32[67584]{0:T(1024)S(1)} %get-tuple-element.106), channel_id=1, source_target_pairs={{0,2},{1,3},{2,0},{3,1},{4,6},{5,7},{6,4},{7,5},{8,10},{9,11},{10,... | collective-permute-start | bytes 811016 | tf_op jit(solution)/shard_map/ppermute | solution.py:224
  109.2 9.4 %collective-permute-start.8 = (f32[67584]{0:T(1024)S(1)}, f32[67584]{0:T(1024)S(1)}, u32[]{:S(2)}, u32[]{:S(2)}) collective-permute-start(f32[67584]{0:T(1024)S(1)} %get-tuple-element.108), channel_id=1, source_target_pairs={{0,4},{1,5},{2,6},{3,7},{4,0},{5,1},{6,2},{7,3},{8,12},{9,13},{10,... | collective-permute-start | bytes 811016 | tf_op jit(solution)/shard_map/ppermute | solution.py:224
  109.3 15.4 %collective-permute-start.9 = (f32[67584]{0:T(1024)S(1)}, f32[67584]{0:T(1024)S(1)}, u32[]{:S(2)}, u32[]{:S(2)}) collective-permute-start(f32[67584]{0:T(1024)S(1)} %get-tuple-element.107), channel_id=1, source_target_pairs={{0,6},{1,7},{2,4},{3,5},{4,2},{5,3},{6,0},{7,1},{8,14},{9,15},{10,... | collective-permute-start | bytes 811016 | tf_op jit(solution)/shard_map/ppermute | solution.py:224
  125.7 28.0 %copy-start.5 = (f32[4,8,32,256]{3,2,1,0:T(8,128)S(1)}, f32[4,8,32,256]{3,2,1,0:T(8,128)}, u32[]{:S(2)}) copy-start(f32[4,8,32,256]{3,2,1,0:T(8,128)} %get-tuple-element.110) | copy-start | bytes 3145732
  125.8 8.3 %collective-permute-start.10 = (f32[33792]{0:T(1024)S(1)}, f32[33792]{0:T(1024)S(1)}, u32[]{:S(2)}, u32[]{:S(2)}) collective-permute-start(f32[33792]{0:T(1024)S(1)} %dynamic_slice.31), channel_id=1, source_target_pairs={{0,8},{1,9},{2,10},{3,11},{4,12},{5,13},{6,14},{7,15},{8,0},{9,1},... | collective-permute-start | bytes 405512 | tf_op jit(solution)/shard_map/ppermute | solution.py:224
  134.2 5.3 %collective-permute-start.11 = (bf16[33792]{0:T(1024)(128)(2,1)S(1)}, bf16[33792]{0:T(1024)(128)(2,1)S(1)}, u32[]{:S(2)}, u32[]{:S(2)}) collective-permute-start(bf16[33792]{0:T(1024)(128)(2,1)S(1)} %get-tuple-element.80), channel_id=1, source_target_pairs={{0,8},{1,9},{2,10},{3,11},{4,12},{5,13},{6,14},{7,15},{8,0},{9,1},... | collective-permute-start | bytes 202760 | tf_op jit(solution)/shard_map/ppermute | solution.py:235
  140.1 6.5 %collective-permute-start.12 = (bf16[67584]{0:T(1024)(128)(2,1)S(1)}, bf16[67584]{0:T(1024)(128)(2,1)S(1)}, u32[]{:S(2)}, u32[]{:S(2)}) collective-permute-start(bf16[67584]{0:T(1024)(128)(2,1)S(1)} %dynamic_update_slice.25), channel_id=1, source_target_pairs={{0,2},{1,3},{2,0},{3,1},{4,6},{5,7},{6,4},{7,5},{8,10},{9,11},{10,... | collective-permute-start | bytes 405512 | tf_op jit(solution)/shard_map/ppermute | solution.py:235
  140.9 7.2 %collective-permute-start.13 = (bf16[67584]{0:T(1024)(128)(2,1)S(1)}, bf16[67584]{0:T(1024)(128)(2,1)S(1)}, u32[]{:S(2)}, u32[]{:S(2)}) collective-permute-start(bf16[67584]{0:T(1024)(128)(2,1)S(1)} %dynamic_update_slice.25), channel_id=1, source_target_pairs={{0,4},{1,5},{2,6},{3,7},{4,0},{5,1},{6,2},{7,3},{8,12},{9,13},{10,... | collective-permute-start | bytes 405512 | tf_op jit(solution)/shard_map/ppermute | solution.py:235
  140.9 8.7 %collective-permute-start.14 = (bf16[67584]{0:T(1024)(128)(2,1)S(1)}, bf16[67584]{0:T(1024)(128)(2,1)S(1)}, u32[]{:S(2)}, u32[]{:S(2)}) collective-permute-start(bf16[67584]{0:T(1024)(128)(2,1)S(1)} %dynamic_update_slice.25), channel_id=1, source_target_pairs={{0,6},{1,7},{2,4},{3,5},{4,2},{5,3},{6,0},{7,1},{8,14},{9,15},{10,... | collective-permute-start | bytes 405512 | tf_op jit(solution)/shard_map/ppermute | solution.py:235
  151.0 13.8 %collective-permute-start.15 = (bf16[270336]{0:T(1024)(128)(2,1)S(1)}, bf16[270336]{0:T(1024)(128)(2,1)S(1)}, u32[]{:S(2)}, u32[]{:S(2)}) collective-permute-start(bf16[270336]{0:T(1024)(128)(2,1)S(1)} %dynamic_update_slice.29), channel_id=1, source_target_pairs={{0,1},{1,0},{2,3},{3,2},{4,5},{5,4},{6,7},{7,6},{8,9},{9,8},{10,11... | collective-permute-start | bytes 1622024 | tf_op jit(solution)/shard_map/ppermute | solution.py:235
  152.0 6.5 %collective-permute-start.5 = (bf16[4,8,3,256]{3,2,1,0:T(4,128)(2,1)S(1)}, bf16[4,8,3,256]{3,2,1,0:T(4,128)(2,1)S(1)}, u32[]{:S(2)}, u32[]{:S(2)}) collective-permute-start(bf16[4,8,3,256]{3,2,1,0:T(4,128)(2,1)S(1)} %slice.1516), channel_id=1, source_target_pairs={{0,15},{1,14},{2,13},{3,12},{4,11},{5,10},{6,9},{7,8},{8,7},{9,6},... | collective-permute-start | bytes 147464 | tf_op jit(solution)/shard_map/ppermute | solution.py:180
  (65 other events, 126.9 us)

commit v6 on v5

--- a/solution.py
+++ b/solution.py
@@ -227,14 +227,17 @@
     for bits in reversed(groups):
         radix, low = 1 << len(bits), bits[0]
         sub = (idx >> low) & (radix - 1)
-        part = cur.shape[0]
-        full = lax.dynamic_update_slice_in_dim(
-            jnp.zeros((part * radix,), cur.dtype), cur, sub * part, 0
-        )
-        for d in range(1, radix):
-            recv = lax.ppermute(cur, axis, [(i, i ^ (d << low)) for i in range(size)])
-            full = lax.dynamic_update_slice_in_dim(full, recv, (sub ^ d) * part, 0)
-        cur = full
+        pieces = [cur] + [
+            lax.ppermute(cur, axis, [(i, i ^ (d << low)) for i in range(size)])
+            for d in range(1, radix)
+        ]
+        placed = []
+        for p in range(radix):
+            pick = pieces[p ^ (radix - 1)]
+            for s in range(radix - 1):
+                pick = jnp.where(sub == s, pieces[p ^ s], pick)
+            placed.append(pick)
+        cur = jnp.concatenate(placed)
     return cur.astype(flat.dtype)
 
 

time: 175 us -> 159 us (0.909)
  local copies, waits for them, and re-layouts: 44.9 us -> 25 us
  waiting for transfers between devices: 38.5 us -> 40.6 us
    dynamic_update_slice x7 -> x0, local copies, waits for them, and re-layouts: 16.4 us -> none  [the longest x5 9.96 us: radix_allreduce(): full = lax.dynamic_update_slice_in_dim(full, recv, (sub ^ d) * part, 0)]
    another operation x7, local copies, waits for them, and re-layouts: 3.63 us -> 0.2 us  [local_step(): kernel_rows.append(jnp.stack(kernel_cols))]
    ppermute x5, waiting for transfers between devices: 6.63 us -> 9.01 us  [radix_allreduce(): lax.ppermute(cur, axis, [(i, i ^ d << low) for i in range(size)])]
    unnamed x240 -> x294, local copies, waits for them, and re-layouts: 12.3 us -> 13.6 us
  transfers between devices with their start and end apart: 16 -> 16, of which waited for: 9 -> 11; matrix products, arithmetic and copies ran while one was open for 16% -> 11% of each run, Pallas kernels for 0% -> 0%
where the time goes in v6:
time: 159 us; the launch traced here: 158 us
  other arithmetic  48.7 us (31%)
  waiting for transfers between devices  40.6 us (26%)
  local copies, waits for them, and re-layouts  25 us (16%)
  starting transfers between devices  23.9 us (15%)
  matrix products  16.3 us (10%)
  between operations  3.09 us (2%)
    ppermute x5, waiting for transfers between devices, radix_allreduce(): lax.ppermute(send, axis, [(i, i ^ d << low) for i in range(size)])  23.3 us
    unnamed x294, local copies, waits for them, and re-layouts  13.6 us
    add x1, other arithmetic, on_device(): grad_ext + dw_kernel[lon_off, lat_off] * padded[:, 6 - lon_off:6 - lon_of...  10.3 us
    reduce_sum x4, other arithmetic, local_step(): jnp.sum(grad_depth * extended[:, lon_off:lon_off + lon_dev, lat_off:lat_o...  9.36 us
    reduce_sum x1, other arithmetic, local_step(): mean_val = jnp.mean(depth, axis=-1, keepdims=True)  9.33 us
    ppermute x5, waiting for transfers between devices, radix_allreduce(): lax.ppermute(cur, axis, [(i, i ^ d << low) for i in range(size)])  9.01 us
    ppermute x2, starting transfers between devices, with_halo(): after = lax.ppermute(leading, axis, down)  7.64 us
    ppermute x2, starting transfers between devices, mirrored(): return lax.ppermute(x, axis, [(i, size - 1 - i) for i in range(size)])  7.56 us
  transfers between devices with their start and end apart: 16, of which 11 were waited for; matrix products, arithmetic and copies ran while one was open for 11% of the time, Pallas kernels for 0%

profile of v6, /device:TPU:0, one launch (start us, length us, event | category | flops | bytes accessed | tf_op | source)
XLA Modules:
  0.0 157.7 jit_solution(4961538893046807604)
XLA Ops:
  0.7 1.0 slice.720
  1.7 5.5 %collective-permute-start = (bf16[4,8,3,256]{3,2,1,0:T(4,128)(2,1)S(1)}, bf16[4,8,3,256]{3,2,1,0:T(4,128)(2,1)S(1)}, u32[]{:S(2)}, u32[]{:S(2)}) collective-permute-start(bf16[4,8,3,256]{3,2,1,0:T(4,128)(2,1)S(1)} %slice.720), channel_id=1, source_target_pairs={{0,15},{1,14},{2,13},{3,12},{4,11},{5,10},{6,9},{7,8},{8,7},{9,6},... | collective-permute-start | bytes 147464 | tf_op jit(solution)/shard_map/ppermute | solution.py:180
  7.2 1.0 fusion.215
  8.3 1.0 fusion.216
  9.6 1.5 fusion.217
  11.1 0.8 copy.25
  12.2 1.3 pad_maximum_fusion.11
  13.5 0.7 collective-permute-start.1
  14.2 3.8 %collective-permute-start.2 = (bf16[4,3,38,256]{3,2,1,0:T(8,128)(2,1)S(1)}, bf16[4,3,38,256]{3,2,1,0:T(8,128)(2,1)S(1)}, u32[]{:S(2)}, u32[]{:S(2)}) collective-permute-start(bf16[4,3,38,256]{3,2,1,0:T(8,128)(2,1)S(1)} %get-tuple-element.114), channel_id=1, source_target_pairs={{1,0},{2,1},{3,2},{4,3},{5,4},{6,5},{7,6},{8,7},{9,8},{10,9},{11,1... | collective-permute-start | bytes 700424 | tf_op jit(solution)/shard_map/ppermute | solution.py:27
  18.1 3.8 %collective-permute-done.1 = bf16[4,3,38,256]{3,2,1,0:T(8,128)(2,1)S(1)} collective-permute-done((bf16[4,3,38,256]{3,2,1,0:T(8,128)(2,1)S(1)}, bf16[4,3,38,256]{3,2,1,0:T(8,128)(2,1)S(1)}, u32[]{:S(2)}, u32[]{:S(2)}) %collective-permute-start.1) | collective-permute-done | bytes 233504 | tf_op jit(solution)/shard_map/ppermute | solution.py:26
  22.7 9.3 %fusion.210 = (f32[4,8,32]{2,1,0:T(8,128)S(1)}, f32[4,8,32,256]{3,2,1,0:T(8,128)S(1)}) fusion(bf16[4,11,38,256]{3,2,1,0:T(8,128)(2,1)S(1)} %get-tuple-element.112, f32[256]{0:T(256)} %bitcast.48, f32[256]{0:T(256)} %bitcast.47, f32[256]{0:T(256)S(1)} %bitcast.340, f32[256]{0:T(256)S(1)} %bitcast.342, f32[256]{0:T(256)S(1)} %bitcast.344, ...), kind=kLoop, calls=%fused_computation.495 | loop fusion | flops 43514880 | bytes 23746560 | tf_op jit(solution)/shard_map/reduce_sum | solution.py:62
  32.9 0.6 copy-done.1
  37.0 1.0 fusion.208
  38.1 3.1 %multiply_reduce_fusion.7 = (f32[256]{0:T(256)}, f32[256]{0:T(256)}, f32[256]{0:T(256)}, f32[256]{0:T(256)}, f32[8,32,256]{2,1,0:T(8,128)S(1)}, /*index=5*/f32[8...) fusion(f32[256]{0:T(256)S(1)} %copy-done.26, ...), kind=kLoop, calls=%fused_computation.433 | loop fusion | flops 7863296 | bytes 2497536 | tf_op jit(solution)/shard_map/reduce_sum | solution.py:117
  42.0 1.5 fusion.202
  43.9 0.9 fusion.220
  44.8 1.5 fusion.200
  46.3 1.5 fusion.204
  47.8 1.5 fusion.206
  49.3 0.9 fusion.221
  50.2 0.9 fusion.219
  51.0 0.9 fusion.218
  52.0 0.9 multiply_reduce_fusion.1
  52.9 4.0 %fusion.148 = (f32[256]{0:T(256)}, f32[256]{0:T(256)}, f32[256]{0:T(256)}, f32[256]{0:T(256)}, f32[256]{0:T(256)}, /*index=5*/f32[256]{0:T(256)}, f32[256]{0:T(2...) fusion(bf16[4,11,38,256]{3,2,1,0:T(8,128)(2,1)S(1)} %get-tuple-, ...), kind=kLoop, calls=%fused_computation.324 | loop fusion | flops 16772608 | bytes 12618752 | tf_op jit(solution)/shard_map/reduce_sum | solution.py:154
  56.9 2.4 %fusion.130 = (f32[256]{0:T(256)}, f32[256]{0:T(256)}, f32[256]{0:T(256)}, f32[256]{0:T(256)}, f32[256]{0:T(256)}, /*index=5*/f32[256]{0:T(256)}, f32[256]{0:T(2...) fusion(f32[4,8,32,256]{3,2,1,0:T(8,128)S(1)} %get-tuple-element.91, ...), kind=kLoop, calls=%fused_computation.306 | loop fusion | flops 12842240 | bytes 3255296 | tf_op jit(solution)/shard_map/reduce_sum | solution.py:154
  59.3 2.5 %fusion.97 = (f32[256]{0:T(256)S(1)}, f32[256]{0:T(256)S(1)}, f32[256]{0:T(256)S(1)}, f32[256]{0:T(256)S(1)}, f32[256]{0:T(256)S(1)}, /*index=5*/f32[256]{0:T(25...) fusion(f32[4,8,32,256]{3,2,1,0:T(8,128)S(1)} %get-tuple-element, ...), kind=kLoop, calls=%fused_computation.273 | loop fusion | flops 14151168 | bytes 10504192 | tf_op jit(solution)/shard_map/reduce_sum | solution.py:154
  62.2 0.8 fusion.213
  66.7 1.2 copy.27
  68.4 0.6 collective-permute-start.3
  69.1 3.9 %collective-permute-start.4 = (f32[4,3,32,256]{3,2,1,0:T(8,128)S(1)}, f32[4,3,32,256]{3,2,1,0:T(8,128)S(1)}, u32[]{:S(2)}, u32[]{:S(2)}) collective-permute-start(f32[4,3,32,256]{3,2,1,0:T(8,128)S(1)} %get-tuple-element.110), channel_id=1, source_target_pairs={{1,0},{2,1},{3,2},{4,3},{5,4},{6,5},{7,6},{8,7},{9,8},{10,9},{11,1... | collective-permute-start | bytes 1179656 | tf_op jit(solution)/shard_map/ppermute | solution.py:27
  72.9 1.4 constant_dynamic-update-slice_fusion.7
  74.4 1.3 constant_dynamic-update-slice_fusion.15
  75.7 1.3 constant_dynamic-update-slice_fusion.14
  77.0 1.3 constant_dynamic-update-slice_fusion.13
  78.3 2.3 %constant_dynamic-update-slice_fusion.12 = f32[539136]{0:T(1024)} fusion(f32[539136]{0:T(1024)} %constant_dynamic-update-slice_fusion.13, f32[262144]{0:T(1024)} %bitcast.301), kind=kLoop, calls=%fused_computation.475 | loop fusion | bytes 2097152
  81.2 1.1 constant_dynamic-update-slice_fusion.10
  82.3 1.3 constant_dynamic-update-slice_fusion.9
  84.7 10.3 %fusion.3 = f32[4,8,38,256]{3,2,1,0:T(8,128)S(1)} fusion(f32[4,14,44,256]{3,2,1,0:T(8,128)S(1)} %select_maximum_fusion, f32[256]{0:T(256)} %bitcast.48, f32[256]{0:T(256)} %bitcast.47, f32[256]{0:T(256)S(1)} %bitcast.341, f32[256]{0:T(256)S(1)} %bitcast.343, f32[256]{0:T(256)S(1)} %bitcast.345, f32[256]{0:T(256)S(1)} %bitcast.347, f32[256]{0:T(256)S(1)} %bitcast.349, ...), kind=kLoop, calls=%fused_computation.127 | loop fusion | flops 30195712 | bytes 62309376 | tf_op jit(solution)/shard_map/add | solution.py:293
  95.1 1.3 multiply_reduce_fusion
  96.4 1.1 copy-done.3
  97.5 1.1 pad_dynamic-slice_fusion
  98.6 3.0 %collective-permute-done.6 = f32[270336]{0:T(1024)} collective-permute-done((f32[270336]{0:T(1024)}, f32[270336]{0:T(1024)}, u32[]{:S(2)}, u32[]{:S(2)}) %collective-permute-start.6) | collective-permute-done | bytes 1081376 | tf_op jit(solution)/shard_map/ppermute | solution.py:224
  101.7 1.4 fusion.51
  103.1 1.0 copy-done.5
  104.3 3.4 %collective-permute-start.9 = (f32[67584]{0:T(1024)S(1)}, f32[67584]{0:T(1024)S(1)}, u32[]{:S(2)}, u32[]{:S(2)}) collective-permute-start(f32[67584]{0:T(1024)S(1)} %get-tuple-element.105), channel_id=1, source_target_pairs={{0,6},{1,7},{2,4},{3,5},{4,2},{5,3},{6,0},{7,1},{8,14},{9,15},{10,... | collective-permute-start | bytes 811016 | tf_op jit(solution)/shard_map/ppermute | solution.py:224
  107.7 5.0 %collective-permute-done.7 = f32[67584]{0:T(1024)S(1)} collective-permute-done((f32[67584]{0:T(1024)S(1)}, f32[67584]{0:T(1024)S(1)}, u32[]{:S(2)}, u32[]{:S(2)}) %collective-permute-start.7) | collective-permute-done | bytes 270368 | tf_op jit(solution)/shard_map/ppermute | solution.py:224
  112.7 0.9 collective-permute-done.8
  113.6 6.1 %collective-permute-done.9 = f32[67584]{0:T(1024)S(1)} collective-permute-done((f32[67584]{0:T(1024)S(1)}, f32[67584]{0:T(1024)S(1)}, u32[]{:S(2)}, u32[]{:S(2)}) %collective-permute-start.9) | collective-permute-done | bytes 270368 | tf_op jit(solution)/shard_map/ppermute | solution.py:224
  119.7 1.0 add_add_fusion
  120.8 8.3 %collective-permute-done.10 = f32[33792]{0:T(1024)S(1)} collective-permute-done((f32[33792]{0:T(1024)S(1)}, f32[33792]{0:T(1024)S(1)}, u32[]{:S(2)}, u32[]{:S(2)}) %collective-permute-start.10) | collective-permute-done | bytes 135200 | tf_op jit(solution)/shard_map/ppermute | solution.py:224
  129.2 5.2 %collective-permute-done.11 = bf16[33792]{0:T(1024)(128)(2,1)S(1)} collective-permute-done((bf16[33792]{0:T(1024)(128)(2,1)S(1)}, bf16[33792]{0:T(1024)(128)(2,1)S(1)}, u32[]{:S(2)}, u32[]{:S(2)}) %collective-permute-start.11) | collective-permute-done | bytes 67616 | tf_op jit(solution)/shard_map/ppermute | solution.py:231
  134.5 0.7 collective-permute-start.13
  135.2 2.7 %collective-permute-start.14 = (bf16[67584]{0:T(1024)(128)(2,1)S(1)}, bf16[67584]{0:T(1024)(128)(2,1)S(1)}, u32[]{:S(2)}, u32[]{:S(2)}) collective-permute-start(bf16[67584]{0:T(1024)(128)(2,1)S(1)} %pad_maximum_fusion.12), channel_id=1, source_target_pairs={{0,6},{1,7},{2,4},{3,5},{4,2},{5,3},{6,0},{7,1},{8,14},{9,15},{10,... | collective-permute-start | bytes 405512 | tf_op jit(solution)/shard_map/ppermute | solution.py:231
  138.0 2.2 %collective-permute-done.12 = bf16[67584]{0:T(1024)(128)(2,1)S(1)} collective-permute-done((bf16[67584]{0:T(1024)(128)(2,1)S(1)}, bf16[67584]{0:T(1024)(128)(2,1)S(1)}, u32[]{:S(2)}, u32[]{:S(2)}) %collective-permute-start.12) | collective-permute-done | bytes 135200 | tf_op jit(solution)/shard_map/ppermute | solution.py:231
  140.4 1.4 collective-permute-done.14
  142.1 1.0 slice.1502
  143.1 2.1 %collective-permute-start.5 = (bf16[4,8,3,256]{3,2,1,0:T(4,128)(2,1)S(1)}, bf16[4,8,3,256]{3,2,1,0:T(4,128)(2,1)S(1)}, u32[]{:S(2)}, u32[]{:S(2)}) collective-permute-start(bf16[4,8,3,256]{3,2,1,0:T(4,128)(2,1)S(1)} %slice.1502), channel_id=1, source_target_pairs={{0,15},{1,14},{2,13},{3,12},{4,11},{5,10},{6,9},{7,8},{8,7},{9,6},... | collective-permute-start | bytes 147464 | tf_op jit(solution)/shard_map/ppermute | solution.py:180
  145.2 4.5 %collective-permute-done.5 = bf16[4,8,3,256]{3,2,1,0:T(4,128)(2,1)S(1)} collective-permute-done((bf16[4,8,3,256]{3,2,1,0:T(4,128)(2,1)S(1)}, bf16[4,8,3,256]{3,2,1,0:T(4,128)(2,1)S(1)}, u32[]{:S(2)}, u32[]{:S(2)}) %collective-permute-start.5) | collective-permute-done | bytes 49184 | tf_op jit(solution)/shard_map/ppermute | solution.py:180
  150.0 0.9 pad_maximum_fusion.8
  150.9 1.2 broadcast_select_fusion.1
  152.9 1.0 concatenate.99
  154.6 1.3 reshape.156
  155.9 0.6 mul.1859
  156.5 1.1 convert_multiply_fusion.99
  (353 shorter events, 14.3 us)
Async XLA Ops:
  0.6 33.5 %copy-start = (bf16[1024,256]{1,0:T(8,128)(2,1)S(1)}, bf16[1024,256]{1,0:T(8,128)(2,1)}, u32[]{:S(2)}) copy-start(bf16[1024,256]{1,0:T(8,128)(2,1)} %param.23) | copy-start | bytes 1572868
  0.7 21.3 %copy-start.2 = (bf16[4,8,32,256]{3,2,1,0:T(8,128)(2,1)S(1)}, bf16[4,8,32,256]{3,2,1,0:T(8,128)(2,1)}, u32[]{:S(2)}) copy-start(bf16[4,8,32,256]{3,2,1,0:T(8,128)(2,1)} %param.13) | copy-start | bytes 1572868
  0.7 17.3 %copy-start.24 = (s32[8,32]{1,0:T(8,128)S(1)}, s32[8,32]{1,0:T(8,128)}, u32[]{:S(2)}) copy-start(s32[8,32]{1,0:T(8,128)} %param.16) | copy-start | bytes 3076
  1.7 10.2 %collective-permute-start = (bf16[4,8,3,256]{3,2,1,0:T(4,128)(2,1)S(1)}, bf16[4,8,3,256]{3,2,1,0:T(4,128)(2,1)S(1)}, u32[]{:S(2)}, u32[]{:S(2)}) collective-permute-start(bf16[4,8,3,256]{3,2,1,0:T(4,128)(2,1)S(1)} %slice.720), channel_id=1, source_target_pairs={{0,15},{1,14},{2,13},{3,12},{4,11},{5,10},{6,9},{7,8},{8,7},{9,6},... | collective-permute-start | bytes 147464 | tf_op jit(solution)/shard_map/ppermute | solution.py:180
  8.2 14.1 %copy-start.27 = (f32[1,1,256]{2,1,0:T(1,128)}, f32[1,1,256]{2,1,0:T(1,128)S(1)}, u32[]{:S(2)}) copy-start(f32[1,1,256]{2,1,0:T(1,128)S(1)} %get-tuple-element.129) | copy-start | bytes 3076
  8.2 14.1 %copy-start.29 = (f32[1,1,256]{2,1,0:T(1,128)}, f32[1,1,256]{2,1,0:T(1,128)S(1)}, u32[]{:S(2)}) copy-start(f32[1,1,256]{2,1,0:T(1,128)S(1)} %get-tuple-element.130) | copy-start | bytes 3076
  8.2 14.1 %copy-start.31 = (f32[1,1,256]{2,1,0:T(1,128)}, f32[1,1,256]{2,1,0:T(1,128)S(1)}, u32[]{:S(2)}) copy-start(f32[1,1,256]{2,1,0:T(1,128)S(1)} %get-tuple-element.131) | copy-start | bytes 3076
  8.2 14.1 %copy-start.33 = (f32[1,1,256]{2,1,0:T(1,128)}, f32[1,1,256]{2,1,0:T(1,128)S(1)}, u32[]{:S(2)}) copy-start(f32[1,1,256]{2,1,0:T(1,128)S(1)} %get-tuple-element.132) | copy-start | bytes 3076
  8.2 14.1 %copy-start.35 = (f32[1,1,256]{2,1,0:T(1,128)}, f32[1,1,256]{2,1,0:T(1,128)S(1)}, u32[]{:S(2)}) copy-start(f32[1,1,256]{2,1,0:T(1,128)S(1)} %get-tuple-element.133) | copy-start | bytes 3076
  8.2 14.1 %copy-start.37 = (f32[1,1,256]{2,1,0:T(1,128)}, f32[1,1,256]{2,1,0:T(1,128)S(1)}, u32[]{:S(2)}) copy-start(f32[1,1,256]{2,1,0:T(1,128)S(1)} %get-tuple-element.134) | copy-start | bytes 3076
  8.2 14.1 %copy-start.39 = (f32[1,1,256]{2,1,0:T(1,128)}, f32[1,1,256]{2,1,0:T(1,128)S(1)}, u32[]{:S(2)}) copy-start(f32[1,1,256]{2,1,0:T(1,128)S(1)} %get-tuple-element.135) | copy-start | bytes 3076
  8.3 14.1 %copy-start.41 = (f32[1,1,256]{2,1,0:T(1,128)}, f32[1,1,256]{2,1,0:T(1,128)S(1)}, u32[]{:S(2)}) copy-start(f32[1,1,256]{2,1,0:T(1,128)S(1)} %get-tuple-element.136) | copy-start | bytes 3076
  8.3 14.1 %copy-start.43 = (f32[1,1,256]{2,1,0:T(1,128)}, f32[1,1,256]{2,1,0:T(1,128)S(1)}, u32[]{:S(2)}) copy-start(f32[1,1,256]{2,1,0:T(1,128)S(1)} %get-tuple-element.137) | copy-start | bytes 3076
  8.3 14.1 %copy-start.45 = (f32[1,1,256]{2,1,0:T(1,128)}, f32[1,1,256]{2,1,0:T(1,128)S(1)}, u32[]{:S(2)}) copy-start(f32[1,1,256]{2,1,0:T(1,128)S(1)} %get-tuple-element.138) | copy-start | bytes 3076
  8.3 14.1 %copy-start.47 = (f32[1,1,256]{2,1,0:T(1,128)}, f32[1,1,256]{2,1,0:T(1,128)S(1)}, u32[]{:S(2)}) copy-start(f32[1,1,256]{2,1,0:T(1,128)S(1)} %get-tuple-element.139) | copy-start | bytes 3076
  8.3 14.1 %copy-start.49 = (f32[1,1,256]{2,1,0:T(1,128)}, f32[1,1,256]{2,1,0:T(1,128)S(1)}, u32[]{:S(2)}) copy-start(f32[1,1,256]{2,1,0:T(1,128)S(1)} %get-tuple-element.140) | copy-start | bytes 3076
  8.3 14.1 %copy-start.51 = (f32[1,1,256]{2,1,0:T(1,128)}, f32[1,1,256]{2,1,0:T(1,128)S(1)}, u32[]{:S(2)}) copy-start(f32[1,1,256]{2,1,0:T(1,128)S(1)} %get-tuple-element.141) | copy-start | bytes 3076
  8.3 14.1 %copy-start.53 = (f32[1,1,256]{2,1,0:T(1,128)}, f32[1,1,256]{2,1,0:T(1,128)S(1)}, u32[]{:S(2)}) copy-start(f32[1,1,256]{2,1,0:T(1,128)S(1)} %get-tuple-element.142) | copy-start | bytes 3076
  8.3 14.1 %copy-start.55 = (f32[1,1,256]{2,1,0:T(1,128)}, f32[1,1,256]{2,1,0:T(1,128)S(1)}, u32[]{:S(2)}) copy-start(f32[1,1,256]{2,1,0:T(1,128)S(1)} %get-tuple-element.143) | copy-start | bytes 3076
  9.4 13.1 %copy-start.57 = (f32[1,1,256]{2,1,0:T(1,128)}, f32[1,1,256]{2,1,0:T(1,128)S(1)}, u32[]{:S(2)}) copy-start(f32[1,1,256]{2,1,0:T(1,128)S(1)} %get-tuple-element.144) | copy-start | bytes 3076
  9.4 13.1 %copy-start.59 = (f32[1,1,256]{2,1,0:T(1,128)}, f32[1,1,256]{2,1,0:T(1,128)S(1)}, u32[]{:S(2)}) copy-start(f32[1,1,256]{2,1,0:T(1,128)S(1)} %get-tuple-element.145) | copy-start | bytes 3076
  9.4 13.1 %copy-start.61 = (f32[1,1,256]{2,1,0:T(1,128)}, f32[1,1,256]{2,1,0:T(1,128)S(1)}, u32[]{:S(2)}) copy-start(f32[1,1,256]{2,1,0:T(1,128)S(1)} %get-tuple-element.146) | copy-start | bytes 3076
  9.4 13.1 %copy-start.63 = (f32[1,1,256]{2,1,0:T(1,128)}, f32[1,1,256]{2,1,0:T(1,128)S(1)}, u32[]{:S(2)}) copy-start(f32[1,1,256]{2,1,0:T(1,128)S(1)} %get-tuple-element.147) | copy-start | bytes 3076
  9.4 13.1 %copy-start.65 = (f32[1,1,256]{2,1,0:T(1,128)}, f32[1,1,256]{2,1,0:T(1,128)S(1)}, u32[]{:S(2)}) copy-start(f32[1,1,256]{2,1,0:T(1,128)S(1)} %get-tuple-element.148) | copy-start | bytes 3076
  9.4 13.1 %copy-start.67 = (f32[1,1,256]{2,1,0:T(1,128)}, f32[1,1,256]{2,1,0:T(1,128)S(1)}, u32[]{:S(2)}) copy-start(f32[1,1,256]{2,1,0:T(1,128)S(1)} %get-tuple-element.149) | copy-start | bytes 3076
  9.4 13.1 %copy-start.69 = (f32[1,1,256]{2,1,0:T(1,128)}, f32[1,1,256]{2,1,0:T(1,128)S(1)}, u32[]{:S(2)}) copy-start(f32[1,1,256]{2,1,0:T(1,128)S(1)} %get-tuple-element.150) | copy-start | bytes 3076
  9.4 13.1 %copy-start.71 = (f32[1,1,256]{2,1,0:T(1,128)}, f32[1,1,256]{2,1,0:T(1,128)S(1)}, u32[]{:S(2)}) copy-start(f32[1,1,256]{2,1,0:T(1,128)S(1)} %get-tuple-element.151) | copy-start | bytes 3076
  9.5 13.1 %copy-start.73 = (f32[1,1,256]{2,1,0:T(1,128)}, f32[1,1,256]{2,1,0:T(1,128)S(1)}, u32[]{:S(2)}) copy-start(f32[1,1,256]{2,1,0:T(1,128)S(1)} %get-tuple-element.152) | copy-start | bytes 3076
  9.5 13.1 %copy-start.75 = (f32[1,1,256]{2,1,0:T(1,128)}, f32[1,1,256]{2,1,0:T(1,128)S(1)}, u32[]{:S(2)}) copy-start(f32[1,1,256]{2,1,0:T(1,128)S(1)} %get-tuple-element.153) | copy-start | bytes 3076
  9.5 13.1 %copy-start.77 = (f32[1,1,256]{2,1,0:T(1,128)}, f32[1,1,256]{2,1,0:T(1,128)S(1)}, u32[]{:S(2)}) copy-start(f32[1,1,256]{2,1,0:T(1,128)S(1)} %get-tuple-element.154) | copy-start | bytes 3076
  9.5 13.1 %copy-start.79 = (f32[1,1,256]{2,1,0:T(1,128)}, f32[1,1,256]{2,1,0:T(1,128)S(1)}, u32[]{:S(2)}) copy-start(f32[1,1,256]{2,1,0:T(1,128)S(1)} %get-tuple-element.155) | copy-start | bytes 3076
  9.5 13.1 %copy-start.81 = (f32[1,1,256]{2,1,0:T(1,128)}, f32[1,1,256]{2,1,0:T(1,128)S(1)}, u32[]{:S(2)}) copy-start(f32[1,1,256]{2,1,0:T(1,128)S(1)} %get-tuple-element.156) | copy-start | bytes 3076
  9.5 13.1 %copy-start.83 = (f32[1,1,256]{2,1,0:T(1,128)}, f32[1,1,256]{2,1,0:T(1,128)S(1)}, u32[]{:S(2)}) copy-start(f32[1,1,256]{2,1,0:T(1,128)S(1)} %get-tuple-element.157) | copy-start | bytes 3076
  9.5 13.1 %copy-start.85 = (f32[1,1,256]{2,1,0:T(1,128)}, f32[1,1,256]{2,1,0:T(1,128)S(1)}, u32[]{:S(2)}) copy-start(f32[1,1,256]{2,1,0:T(1,128)S(1)} %get-tuple-element.158) | copy-start | bytes 3076
  9.5 13.1 %copy-start.87 = (f32[1,1,256]{2,1,0:T(1,128)}, f32[1,1,256]{2,1,0:T(1,128)S(1)}, u32[]{:S(2)}) copy-start(f32[1,1,256]{2,1,0:T(1,128)S(1)} %get-tuple-element.159) | copy-start | bytes 3076
  9.5 13.1 %copy-start.89 = (f32[1,1,256]{2,1,0:T(1,128)}, f32[1,1,256]{2,1,0:T(1,128)S(1)}, u32[]{:S(2)}) copy-start(f32[1,1,256]{2,1,0:T(1,128)S(1)} %get-tuple-element.160) | copy-start | bytes 3076
  9.5 13.1 %copy-start.91 = (f32[1,1,256]{2,1,0:T(1,128)}, f32[1,1,256]{2,1,0:T(1,128)S(1)}, u32[]{:S(2)}) copy-start(f32[1,1,256]{2,1,0:T(1,128)S(1)} %get-tuple-element.161) | copy-start | bytes 3076
  9.6 13.1 %copy-start.93 = (f32[1,1,256]{2,1,0:T(1,128)}, f32[1,1,256]{2,1,0:T(1,128)S(1)}, u32[]{:S(2)}) copy-start(f32[1,1,256]{2,1,0:T(1,128)S(1)} %get-tuple-element.162) | copy-start | bytes 3076
  11.1 11.6 %copy-start.94 = (f32[1,1,256]{2,1,0:T(1,128)}, f32[1,1,256]{2,1,0:T(1,128)S(1)}, u32[]{:S(2)}) copy-start(f32[1,1,256]{2,1,0:T(1,128)S(1)} %get-tuple-element.163) | copy-start | bytes 3076
  11.1 11.6 %copy-start.95 = (f32[1,1,256]{2,1,0:T(1,128)}, f32[1,1,256]{2,1,0:T(1,128)S(1)}, u32[]{:S(2)}) copy-start(f32[1,1,256]{2,1,0:T(1,128)S(1)} %get-tuple-element.164) | copy-start | bytes 3076
  11.1 11.6 %copy-start.96 = (f32[1,1,256]{2,1,0:T(1,128)}, f32[1,1,256]{2,1,0:T(1,128)S(1)}, u32[]{:S(2)}) copy-start(f32[1,1,256]{2,1,0:T(1,128)S(1)} %get-tuple-element.165) | copy-start | bytes 3076
  11.1 11.6 %copy-start.97 = (f32[1,1,256]{2,1,0:T(1,128)}, f32[1,1,256]{2,1,0:T(1,128)S(1)}, u32[]{:S(2)}) copy-start(f32[1,1,256]{2,1,0:T(1,128)S(1)} %get-tuple-element.166) | copy-start | bytes 3076
  11.1 11.6 %copy-start.98 = (f32[1,1,256]{2,1,0:T(1,128)}, f32[1,1,256]{2,1,0:T(1,128)S(1)}, u32[]{:S(2)}) copy-start(f32[1,1,256]{2,1,0:T(1,128)S(1)} %get-tuple-element.167) | copy-start | bytes 3076
  13.5 8.5 %collective-permute-start.1 = (bf16[4,3,38,256]{3,2,1,0:T(8,128)(2,1)S(1)}, bf16[4,3,38,256]{3,2,1,0:T(8,128)(2,1)S(1)}, u32[]{:S(2)}, u32[]{:S(2)}) collective-permute-start(bf16[4,3,38,256]{3,2,1,0:T(8,128)(2,1)S(1)} %get-tuple-element.113), channel_id=1, source_target_pairs={{0,1},{1,2},{2,3},{3,4},{4,5},{5,6},{6,7},{7,8},{8,9},{9,10},{10,1... | collective-permute-start | bytes 700424 | tf_op jit(solution)/shard_map/ppermute | solution.py:26
  14.2 7.8 %collective-permute-start.2 = (bf16[4,3,38,256]{3,2,1,0:T(8,128)(2,1)S(1)}, bf16[4,3,38,256]{3,2,1,0:T(8,128)(2,1)S(1)}, u32[]{:S(2)}, u32[]{:S(2)}) collective-permute-start(bf16[4,3,38,256]{3,2,1,0:T(8,128)(2,1)S(1)} %get-tuple-element.114), channel_id=1, source_target_pairs={{1,0},{2,1},{3,2},{4,3},{5,4},{6,5},{7,6},{8,7},{9,8},{10,9},{11,1... | collective-permute-start | bytes 700424 | tf_op jit(solution)/shard_map/ppermute | solution.py:27
  67.9 12.7 %copy-start.133 = (f32[1024]{0:T(1024)S(1)}, f32[1024]{0:T(1024)}, u32[]{:S(2)}) copy-start(f32[1024]{0:T(1024)} %get-tuple-element.85) | copy-start | bytes 12292
  67.9 12.7 %copy-start.134 = (f32[1024]{0:T(1024)S(1)}, f32[1024]{0:T(1024)}, u32[]{:S(2)}) copy-start(f32[1024]{0:T(1024)} %get-tuple-element.83) | copy-start | bytes 12292
  67.9 12.7 %copy-start.135 = (f32[1024]{0:T(1024)S(1)}, f32[1024]{0:T(1024)}, u32[]{:S(2)}) copy-start(f32[1024]{0:T(1024)} %get-tuple-element.87) | copy-start | bytes 12292
  67.9 12.7 %copy-start.136 = (f32[1024]{0:T(1024)S(1)}, f32[1024]{0:T(1024)}, u32[]{:S(2)}) copy-start(f32[1024]{0:T(1024)} %get-tuple-element.89) | copy-start | bytes 12292
  68.4 15.4 %collective-permute-start.3 = (f32[4,3,32,256]{3,2,1,0:T(8,128)}, f32[4,3,32,256]{3,2,1,0:T(8,128)S(1)}, u32[]{:S(2)}, u32[]{:S(2)}) collective-permute-start(f32[4,3,32,256]{3,2,1,0:T(8,128)} %get-tuple-element.109), channel_id=1, source_target_pairs={{0,1},{1,2},{2,3},{3,4},{4,5},{5,6},{6,7},{7,8},{8,9},{9,10},{10,1... | collective-permute-start | bytes 1179656 | tf_op jit(solution)/shard_map/ppermute | solution.py:26
  69.1 14.8 %collective-permute-start.4 = (f32[4,3,32,256]{3,2,1,0:T(8,128)S(1)}, f32[4,3,32,256]{3,2,1,0:T(8,128)S(1)}, u32[]{:S(2)}, u32[]{:S(2)}) collective-permute-start(f32[4,3,32,256]{3,2,1,0:T(8,128)S(1)} %get-tuple-element.110), channel_id=1, source_target_pairs={{1,0},{2,1},{3,2},{4,3},{5,4},{6,5},{7,6},{8,7},{9,8},{10,9},{11,1... | collective-permute-start | bytes 1179656 | tf_op jit(solution)/shard_map/ppermute | solution.py:27
  84.6 10.4 %copy-start.8 = (f32[8,32,256]{2,1,0:T(8,128)S(1)}, f32[8,32,256]{2,1,0:T(8,128)}, u32[]{:S(2)}) copy-start(f32[8,32,256]{2,1,0:T(8,128)} %copy-done.7) | copy-start | bytes 786436
  98.6 3.0 %collective-permute-start.6 = (f32[270336]{0:T(1024)}, f32[270336]{0:T(1024)}, u32[]{:S(2)}, u32[]{:S(2)}) collective-permute-start(f32[270336]{0:T(1024)} %pad_dynamic-slice_fusion), channel_id=1, source_target_pairs={{0,1},{1,0},{2,3},{3,2},{4,5},{5,4},{6,7},{7,6},{8,9},{9,8},{10,11... | collective-permute-start | bytes 3244040 | tf_op jit(solution)/shard_map/ppermute | solution.py:224
  104.1 8.6 %collective-permute-start.7 = (f32[67584]{0:T(1024)S(1)}, f32[67584]{0:T(1024)S(1)}, u32[]{:S(2)}, u32[]{:S(2)}) collective-permute-start(f32[67584]{0:T(1024)S(1)} %get-tuple-element.104), channel_id=1, source_target_pairs={{0,2},{1,3},{2,0},{3,1},{4,6},{5,7},{6,4},{7,5},{8,10},{9,11},{10,... | collective-permute-start | bytes 811016 | tf_op jit(solution)/shard_map/ppermute | solution.py:224
  104.2 9.4 %collective-permute-start.8 = (f32[67584]{0:T(1024)S(1)}, f32[67584]{0:T(1024)S(1)}, u32[]{:S(2)}, u32[]{:S(2)}) collective-permute-start(f32[67584]{0:T(1024)S(1)} %get-tuple-element.106), channel_id=1, source_target_pairs={{0,4},{1,5},{2,6},{3,7},{4,0},{5,1},{6,2},{7,3},{8,12},{9,13},{10,... | collective-permute-start | bytes 811016 | tf_op jit(solution)/shard_map/ppermute | solution.py:224
  104.3 15.4 %collective-permute-start.9 = (f32[67584]{0:T(1024)S(1)}, f32[67584]{0:T(1024)S(1)}, u32[]{:S(2)}, u32[]{:S(2)}) collective-permute-start(f32[67584]{0:T(1024)S(1)} %get-tuple-element.105), channel_id=1, source_target_pairs={{0,6},{1,7},{2,4},{3,5},{4,2},{5,3},{6,0},{7,1},{8,14},{9,15},{10,... | collective-permute-start | bytes 811016 | tf_op jit(solution)/shard_map/ppermute | solution.py:224
  120.8 8.3 %collective-permute-start.10 = (f32[33792]{0:T(1024)S(1)}, f32[33792]{0:T(1024)S(1)}, u32[]{:S(2)}, u32[]{:S(2)}) collective-permute-start(f32[33792]{0:T(1024)S(1)} %dynamic_slice.31), channel_id=1, source_target_pairs={{0,8},{1,9},{2,10},{3,11},{4,12},{5,13},{6,14},{7,15},{8,0},{9,1},... | collective-permute-start | bytes 405512 | tf_op jit(solution)/shard_map/ppermute | solution.py:224
  129.1 5.3 %collective-permute-start.11 = (bf16[33792]{0:T(1024)(128)(2,1)S(1)}, bf16[33792]{0:T(1024)(128)(2,1)S(1)}, u32[]{:S(2)}, u32[]{:S(2)}) collective-permute-start(bf16[33792]{0:T(1024)(128)(2,1)S(1)} %add_convert_fusion.1), channel_id=1, source_target_pairs={{0,8},{1,9},{2,10},{3,11},{4,12},{5,13},{6,14},{7,15},{8,0},{9,1},... | collective-permute-start | bytes 202760 | tf_op jit(solution)/shard_map/ppermute | solution.py:231
  134.4 10.8 %copy-start.6 = (f32[4,8,32,256]{3,2,1,0:T(8,128)S(1)}, f32[4,8,32,256]{3,2,1,0:T(8,128)}, u32[]{:S(2)}) copy-start(f32[4,8,32,256]{3,2,1,0:T(8,128)} %get-tuple-element.108) | copy-start | bytes 3145732
  134.4 5.7 %collective-permute-start.12 = (bf16[67584]{0:T(1024)(128)(2,1)S(1)}, bf16[67584]{0:T(1024)(128)(2,1)S(1)}, u32[]{:S(2)}, u32[]{:S(2)}) collective-permute-start(bf16[67584]{0:T(1024)(128)(2,1)S(1)} %pad_maximum_fusion.12), channel_id=1, source_target_pairs={{0,4},{1,5},{2,6},{3,7},{4,0},{5,1},{6,2},{7,3},{8,12},{9,13},{10,... | collective-permute-start | bytes 405512 | tf_op jit(solution)/shard_map/ppermute | solution.py:231
  134.5 5.9 %collective-permute-start.13 = (bf16[67584]{0:T(1024)(128)(2,1)S(1)}, bf16[67584]{0:T(1024)(128)(2,1)S(1)}, u32[]{:S(2)}, u32[]{:S(2)}) collective-permute-start(bf16[67584]{0:T(1024)(128)(2,1)S(1)} %pad_maximum_fusion.12), channel_id=1, source_target_pairs={{0,2},{1,3},{2,0},{3,1},{4,6},{5,7},{6,4},{7,5},{8,10},{9,11},{10,... | collective-permute-start | bytes 405512 | tf_op jit(solution)/shard_map/ppermute | solution.py:231
  135.2 6.6 %collective-permute-start.14 = (bf16[67584]{0:T(1024)(128)(2,1)S(1)}, bf16[67584]{0:T(1024)(128)(2,1)S(1)}, u32[]{:S(2)}, u32[]{:S(2)}) collective-permute-start(bf16[67584]{0:T(1024)(128)(2,1)S(1)} %pad_maximum_fusion.12), channel_id=1, source_target_pairs={{0,6},{1,7},{2,4},{3,5},{4,2},{5,3},{6,0},{7,1},{8,14},{9,15},{10,... | collective-permute-start | bytes 405512 | tf_op jit(solution)/shard_map/ppermute | solution.py:231
  142.0 8.8 %collective-permute-start.15 = (bf16[270336]{0:T(1024)(128)(2,1)S(1)}, bf16[270336]{0:T(1024)(128)(2,1)}, u32[]{:S(2)}, u32[]{:S(2)}) collective-permute-start(bf16[270336]{0:T(1024)(128)(2,1)S(1)} %pad_maximum_fusion.4), channel_id=1, source_target_pairs={{0,1},{1,0},{2,3},{3,2},{4,5},{5,4},{6,7},{7,6},{8,9},{9,8},{10,11... | collective-permute-start | bytes 1622024 | tf_op jit(solution)/shard_map/ppermute | solution.py:231
  143.1 6.6 %collective-permute-start.5 = (bf16[4,8,3,256]{3,2,1,0:T(4,128)(2,1)S(1)}, bf16[4,8,3,256]{3,2,1,0:T(4,128)(2,1)S(1)}, u32[]{:S(2)}, u32[]{:S(2)}) collective-permute-start(bf16[4,8,3,256]{3,2,1,0:T(4,128)(2,1)S(1)} %slice.1502), channel_id=1, source_target_pairs={{0,15},{1,14},{2,13},{3,12},{4,11},{5,10},{6,9},{7,8},{8,7},{9,6},... | collective-permute-start | bytes 147464 | tf_op jit(solution)/shard_map/ppermute | solution.py:180
  (92 other events, 201.2 us)

commit v7 on v6

--- a/solution.py
+++ b/solution.py
@@ -208,7 +208,7 @@
     return cur.astype(flat.dtype)
 
 
-def radix_allreduce(flat, axis, gather_dtype):
+def radix_allreduce(flat, axis, gather_dtype, tie):
     size = lax.axis_size(axis)
     nbits = size.bit_length() - 1
     groups = [[0]] + [list(range(b, min(b + 2, nbits))) for b in range(1, nbits, 2)]
@@ -223,6 +223,8 @@
             send = lax.dynamic_slice_in_dim(cur, (sub ^ d) * part, part)
             total = total + lax.ppermute(send, axis, [(i, i ^ (d << low)) for i in range(size)])
         cur = total
+        if bits == groups[0]:
+            cur, tie = lax.optimization_barrier((cur, tie))
     cur = cur.astype(gather_dtype)
     for bits in reversed(groups):
         radix, low = 1 << len(bits), bits[0]
@@ -238,7 +240,7 @@
                 pick = jnp.where(sub == s, pieces[p ^ s], pick)
             placed.append(pick)
         cur = jnp.concatenate(placed)
-    return cur.astype(flat.dtype)
+    return cur.astype(flat.dtype), tie
 
 
 def butterfly_allreduce(flat, axis):
@@ -286,6 +288,11 @@
     )
     grad_halo = with_halo(grad_depth, (("lon", 1),), 3)
     padded = jnp.pad(grad_halo, ((0, 0), (0, 0), (6, 6), (0, 0)))
+    lon_size = lax.axis_size("lon")
+    reduced, padded = radix_allreduce(
+        pack(grads, lon_size * 1024), "lon", jnp.bfloat16, padded
+    )
+    totals = unpack(reduced, grads)
     grad_ext = jnp.zeros((members, lon_dev, lat_rows + 6, chans), jnp.float32)
     for lon_off in range(7):
         for lat_off in range(7):
@@ -304,30 +311,6 @@
     grad_features = jnp.concatenate(
         [inner[:, :, : lat_rows - 3, :], inner[:, :, lat_rows - 3 :, :] + back_rows], axis=2
     ).astype(jnp.bfloat16)
-    (
-        kernel_sum,
-        dw_bias_sum,
-        gain_sum,
-        bias_sum,
-        w_in_sum,
-        b_in_sum,
-        w_out_sum,
-        b_out_sum,
-        scale_sum,
-    ) = grads
-    lon_size = lax.axis_size("lon")
-    sums = (
-        kernel_sum,
-        dw_bias_sum,
-        gain_sum,
-        bias_sum,
-        w_in_sum,
-        b_in_sum,
-        w_out_sum,
-        b_out_sum,
-        scale_sum,
-    )
-    totals = unpack(radix_allreduce(pack(sums, lon_size * 1024), "lon", jnp.bfloat16), sums)
     factor = 1.0 / math.sqrt(members * lat_rows * lon_dev * lax.axis_size("lon"))
     return (
         predicted,

time: 159 us -> 170 us (1.069)
  other arithmetic: 48.7 us -> 54.4 us
  local copies, waits for them, and re-layouts: 25 us -> 29.7 us
  matrix products: 16.3 us -> 18.8 us
  waiting for transfers between devices: 40.6 us -> 38.7 us
    another operation x7, local copies, waits for them, and re-layouts: 0.2 us -> 5.03 us  [local_step(): kernel_rows.append(jnp.stack(kernel_cols))]
    ppermute x2, waiting for transfers between devices: 3.83 us -> 8.17 us  [with_halo(): before = lax.ppermute(last, axis, up)]
    ppermute x5, waiting for transfers between devices: 9.01 us -> 5.51 us  [radix_allreduce(): lax.ppermute(cur, axis, [(i, i ^ d << low) for i in range(size)])]
    unnamed x4, other arithmetic: 3.19 us -> 0.02 us
    dynamic_slice x3, local copies, waits for them, and re-layouts: 1.21 us -> 3.93 us  [radix_allreduce(): send = lax.dynamic_slice_in_dim(cur, (sub ^ d) * part, part)]
    unnamed x294 -> x212, local copies, waits for them, and re-layouts: 13.6 us -> 11.2 us
    dot_general x4, matrix products: 1.28 us -> 3.7 us  [local_step(): lax.dot_general(normed[member].reshape(rows, chans), pre_half, contract_r...]
    ppermute x5, waiting for transfers between devices: 23.3 us -> 21.2 us  [radix_allreduce(): lax.ppermute(send, axis, [(i, i ^ d << low) for i in range(size)])]
  transfers between devices with their start and end apart: 16 -> 16, of which waited for: 11 -> 7; matrix products, arithmetic and copies ran while one was open for 11% -> 12% of each run, Pallas kernels for 0% -> 0%
where the time goes in v7:
time: 170 us; the launch traced here: 168 us
  other arithmetic  54.4 us (32%)
  waiting for transfers between devices  38.7 us (23%)
  local copies, waits for them, and re-layouts  29.7 us (17%)
  starting transfers between devices  24.6 us (14%)
  matrix products  18.8 us (11%)
  between operations  2.28 us (1%)
    ppermute x5, waiting for transfers between devices, radix_allreduce(): lax.ppermute(send, axis, [(i, i ^ d << low) for i in range(size)])  21.2 us
    unnamed x212, local copies, waits for them, and re-layouts  11.2 us
    add x1, other arithmetic, on_device(): grad_ext + dw_kernel[lon_off, lat_off] * padded[:, 6 - lon_off:6 - lon_of...  10.7 us
    reduce_sum x4, other arithmetic, local_step(): jnp.sum(grad_depth * extended[:, lon_off:lon_off + lon_dev, lat_off:lat_o...  10.6 us
    reduce_sum x1, other arithmetic, local_step(): mean_val = jnp.mean(depth, axis=-1, keepdims=True)  9.35 us
    ppermute x2, starting transfers between devices, with_halo(): after = lax.ppermute(leading, axis, down)  8.2 us
    ppermute x2, waiting for transfers between devices, with_halo(): before = lax.ppermute(last, axis, up)  8.17 us
    dot_general x4, matrix products, local_step(): lax.dot_general(out_half, w_out, contract_cols, preferred_element_type=jn...  5.96 us
  transfers between devices with their start and end apart: 16, of which 7 were waited for; matrix products, arithmetic and copies ran while one was open for 12% of the time, Pallas kernels for 0%

profile of v7, /device:TPU:0, one launch (start us, length us, event | category | flops | bytes accessed | tf_op | source)
XLA Modules:
  0.0 168.5 jit_solution(1507986209597102015)
XLA Ops:
  0.7 1.0 slice.720
  1.7 5.5 %collective-permute-start = (bf16[4,8,3,256]{3,2,1,0:T(4,128)(2,1)S(1)}, bf16[4,8,3,256]{3,2,1,0:T(4,128)(2,1)S(1)}, u32[]{:S(2)}, u32[]{:S(2)}) collective-permute-start(bf16[4,8,3,256]{3,2,1,0:T(4,128)(2,1)S(1)} %slice.720), channel_id=1, source_target_pairs={{0,15},{1,14},{2,13},{3,12},{4,11},{5,10},{6,9},{7,8},{8,7},{9,6},... | collective-permute-start | bytes 147464 | tf_op jit(solution)/shard_map/ppermute | solution.py:180
  7.2 1.0 fusion.167
  8.4 1.0 fusion.168
  9.6 1.5 fusion.169
  11.1 0.8 copy.25
  12.2 1.3 pad_maximum_fusion.11
  13.5 0.7 collective-permute-start.1
  14.2 3.8 %collective-permute-start.2 = (bf16[4,3,38,256]{3,2,1,0:T(8,128)(2,1)S(1)}, bf16[4,3,38,256]{3,2,1,0:T(8,128)(2,1)S(1)}, u32[]{:S(2)}, u32[]{:S(2)}) collective-permute-start(bf16[4,3,38,256]{3,2,1,0:T(8,128)(2,1)S(1)} %get-tuple-element.116), channel_id=1, source_target_pairs={{1,0},{2,1},{3,2},{4,3},{5,4},{6,5},{7,6},{8,7},{9,8},{10,9},{11,1... | collective-permute-start | bytes 700424 | tf_op jit(solution)/shard_map/ppermute | solution.py:27
  18.5 0.8 compare_convert_fusion
  19.3 2.6 %collective-permute-done.1 = bf16[4,3,38,256]{3,2,1,0:T(8,128)(2,1)S(1)} collective-permute-done((bf16[4,3,38,256]{3,2,1,0:T(8,128)(2,1)S(1)}, bf16[4,3,38,256]{3,2,1,0:T(8,128)(2,1)S(1)}, u32[]{:S(2)}, u32[]{:S(2)}) %collective-permute-start.1) | collective-permute-done | bytes 233504 | tf_op jit(solution)/shard_map/ppermute | solution.py:26
  22.8 9.4 %fusion.162 = (f32[4,8,32]{2,1,0:T(8,128)S(1)}, f32[4,8,32,256]{3,2,1,0:T(8,128)S(1)}) fusion(bf16[4,11,38,256]{3,2,1,0:T(8,128)(2,1)S(1)} %get-tuple-element.114, f32[256]{0:T(256)} %bitcast.48, f32[256]{0:T(256)} %bitcast.47, f32[256]{0:T(256)S(1)} %bitcast.344, f32[256]{0:T(256)S(1)} %bitcast.346, f32[256]{0:T(256)S(1)} %bitcast.348, ...), kind=kLoop, calls=%fused_computation.399 | loop fusion | flops 43514880 | bytes 23746560 | tf_op jit(solution)/shard_map/reduce_sum | solution.py:62
  37.1 1.1 fusion.160
  38.1 3.8 %multiply_reduce_fusion.7 = (f32[256]{0:T(256)}, f32[256]{0:T(256)}, f32[256]{0:T(256)}, f32[256]{0:T(256)}, f32[8,32,256]{2,1,0:T(8,128)S(1)}, /*index=5*/f32[8...) fusion(f32[256]{0:T(256)S(1)} %copy-done.40, ...), kind=kLoop, calls=%fused_computation.337 | loop fusion | flops 7863296 | bytes 2497536 | tf_op jit(solution)/shard_map/reduce_sum | solution.py:117
  42.0 1.5 fusion.154
  44.1 1.5 fusion.152
  45.6 0.9 fusion.173
  46.5 1.5 fusion.156
  48.0 1.5 fusion.158
  49.5 0.9 fusion.170
  50.5 0.9 fusion.171
  51.4 0.9 fusion.172
  52.3 1.0 multiply_reduce_fusion.1
  53.3 4.0 %fusion.100 = (f32[256]{0:T(256)}, f32[256]{0:T(256)}, f32[256]{0:T(256)}, f32[256]{0:T(256)}, f32[256]{0:T(256)}, /*index=5*/f32[256]{0:T(256)}, f32[256]{0:T(2...) fusion(bf16[4,11,38,256]{3,2,1,0:T(8,128)(2,1)S(1)} %get-tuple-, ...), kind=kLoop, calls=%fused_computation.228 | loop fusion | flops 16772608 | bytes 12618752 | tf_op jit(solution)/shard_map/reduce_sum | solution.py:154
  57.4 2.3 %fusion.82 = (f32[256]{0:T(256)}, f32[256]{0:T(256)}, f32[256]{0:T(256)}, f32[256]{0:T(256)}, f32[256]{0:T(256)}, /*index=5*/f32[256]{0:T(256)}, f32[256]{0:T(25...) fusion(f32[4,8,32,256]{3,2,1,0:T(8,128)S(1)} %get-tuple-element.95, ...), kind=kLoop, calls=%fused_computation.210 | loop fusion | flops 12842240 | bytes 3255296 | tf_op jit(solution)/shard_map/reduce_sum | solution.py:154
  59.7 1.0 fusion.31
  60.7 3.2 %fusion.49 = (f32[256]{0:T(256)}, f32[256]{0:T(256)}, f32[256]{0:T(256)}, f32[256]{0:T(256)}, f32[256]{0:T(256)}, /*index=5*/f32[256]{0:T(256)}, f32[256]{0:T(25...) fusion(f32[4,8,32,256]{3,2,1,0:T(8,128)S(1)} %get-tuple-element, ...), kind=kLoop, calls=%fused_computation.177 | loop fusion | flops 14151168 | bytes 10504192 | tf_op jit(solution)/shard_map/reduce_sum | solution.py:154
  63.9 1.3 fusion.140
  67.5 0.7 stack.227
  68.9 0.7 stack.236
  70.2 0.7 stack.245
  71.5 0.7 stack.254
  72.8 0.7 stack.263
  74.1 0.7 stack.272
  75.5 0.7 stack.281
  76.8 1.4 reshape.151
  78.2 1.8 %convolution_add_fusion.5 = f32[256,1024]{1,0:T(8,128)S(1)} fusion(f32[256,1024]{1,0:T(8,128)} %fusion.140, bf16[256,256]{1,0:T(8,128)(2,1)S(1)} %bitcast.325, bf16[256,1024]{1,0:T(8,128)(2,1)} %copy-done.14), kind=kOutput, calls=%fused_computation.25 | convolution fusion | flops 134479872 | bytes 2752512 | tf_op jit(solution)/shard_map/dot_general | solution.py:128
  81.7 1.0 copy-done.4
  84.5 1.3 pad_dynamic-slice_fusion
  86.9 4.4 %collective-permute-start.5 = (f32[4,3,32,256]{3,2,1,0:T(8,128)S(1)}, f32[4,3,32,256]{3,2,1,0:T(8,128)}, u32[]{:S(2)}, u32[]{:S(2)}) collective-permute-start(f32[4,3,32,256]{3,2,1,0:T(8,128)S(1)} %get-tuple-element.112), channel_id=1, source_target_pairs={{1,0},{2,1},{3,2},{4,3},{5,4},{6,5},{7,6},{8,7},{9,8},{10,9},{11,1... | collective-permute-start | bytes 1179656 | tf_op jit(solution)/shard_map/ppermute | solution.py:27
  91.3 5.6 %collective-permute-done.4 = f32[4,3,32,256]{3,2,1,0:T(8,128)S(1)} collective-permute-done((f32[4,3,32,256]{3,2,1,0:T(8,128)S(1)}, f32[4,3,32,256]{3,2,1,0:T(8,128)S(1)}, u32[]{:S(2)}, u32[]{:S(2)}) %collective-permute-start.4) | collective-permute-done | bytes 393248 | tf_op jit(solution)/shard_map/ppermute | solution.py:26
  96.9 0.7 copy-done.34
  97.6 1.8 %select_maximum_fusion = f32[4,14,44,256]{3,2,1,0:T(8,128)S(1)} fusion(f32[4,3,32,256]{3,2,1,0:T(8,128)} %collective-permute-done.5, f32[4,8,32,256]{3,2,1,0:T(8,128)} %copy-done.1, f32[4,3,32,256]{3,2,1,0:T(8,128)} %copy-done.34), kind=kLoop, calls=%fused_computation.2 | loop fusion | flops 5046272 | bytes 4358144 | tf_op jit(solution)/shard_map/concatenate | solution.py:28
  99.5 2.4 %fusion.3 = f32[270336]{0:T(1024)} fusion(f32[270336]{0:T(1024)} %collective-permute-done.3, s32[]{:T(128)S(6)} %select_n.114, f32[539136]{0:T(1024)S(1)} %copy-done.6), kind=kLoop, calls=%fused_computation.131 | loop fusion | flops 270336 | bytes 4319236 | tf_op jit(solution)/shard_map/add | solution.py:224
  101.9 2.0 %fusion.164 = (f32[67584]{0:T(1024)}, f32[67584]{0:T(1024)}, f32[67584]{0:T(1024)}) fusion(f32[270336]{0:T(1024)} %fusion.3, s32[]{:T(128)S(6)} %select_n.120, s32[]{:T(128)S(6)} %select_n.122, s32[]{:T(128)S(6)} %select_n.121), kind=kLoop, calls=%fused_computation.400 | loop fusion | bytes 1622028 | tf_op jit(solution)/shard_map/dynamic_slice | solution.py:223
  103.9 1.3 collective-permute-start.7
  105.2 2.2 %collective-permute-start.8 = (f32[67584]{0:T(1024)}, f32[67584]{0:T(1024)}, u32[]{:S(2)}, u32[]{:S(2)}) collective-permute-start(f32[67584]{0:T(1024)} %get-tuple-element.110), channel_id=1, source_target_pairs={{0,4},{1,5},{2,6},{3,7},{4,0},{5,1},{6,2},{7,3},{8,12},{9,13},{10,... | collective-permute-start | bytes 811016 | tf_op jit(solution)/shard_map/ppermute | solution.py:224
  107.4 11.8 %collective-permute-done.7 = f32[67584]{0:T(1024)} collective-permute-done((f32[67584]{0:T(1024)}, f32[67584]{0:T(1024)}, u32[]{:S(2)}, u32[]{:S(2)}) %collective-permute-start.7) | collective-permute-done | bytes 270368 | tf_op jit(solution)/shard_map/ppermute | solution.py:224
  119.3 1.2 collective-permute-done.8
  120.5 1.2 add_add_fusion
  123.1 1.3 collective-permute-start.10
  124.4 8.1 %collective-permute-done.10 = f32[33792]{0:T(1024)} collective-permute-done((f32[33792]{0:T(1024)}, f32[33792]{0:T(1024)}, u32[]{:S(2)}, u32[]{:S(2)}) %collective-permute-start.10) | collective-permute-done | bytes 135200 | tf_op jit(solution)/shard_map/ppermute | solution.py:224
  132.5 1.6 add_convert_fusion.1
  134.1 5.5 %collective-permute-done.11 = bf16[33792]{0:T(1024)(128)(2,1)} collective-permute-done((bf16[33792]{0:T(1024)(128)(2,1)}, bf16[33792]{0:T(1024)(128)(2,1)}, u32[]{:S(2)}, u32[]{:S(2)}) %collective-permute-start.11) | collective-permute-done | bytes 67616 | tf_op jit(solution)/shard_map/ppermute | solution.py:233
  139.6 0.9 broadcast_select_fusion.3
  140.9 3.2 %collective-permute-start.12 = (bf16[67584]{0:T(1024)(128)(2,1)S(1)}, bf16[67584]{0:T(1024)(128)(2,1)S(1)}, u32[]{:S(2)}, u32[]{:S(2)}) collective-permute-start(bf16[67584]{0:T(1024)(128)(2,1)S(1)} %pad_maximum_fusion.12), channel_id=1, source_target_pairs={{0,4},{1,5},{2,6},{3,7},{4,0},{5,1},{6,2},{7,3},{8,12},{9,13},{10,... | collective-permute-start | bytes 405512 | tf_op jit(solution)/shard_map/ppermute | solution.py:233
  144.1 10.7 %multiply_add_fusion = f32[4,8,38,256]{3,2,1,0:T(8,128)S(1)} fusion(f32[4,14,44,256]{3,2,1,0:T(8,128)S(1)} %select_maximum_fusion, f32[256]{0:T(256)} %bitcast.48, f32[256]{0:T(256)} %bitcast.47, f32[256]{0:T(256)S(1)} %bitcast.345, f32[256]{0:T(256)S(1)} %bitcast.347, f32[256]{0:T(256)S(1)} %bitcast.349, f32[256]{0:T(256)} %bitcast.351, f32[256]{0:T(256)} %bitcast.353, ...), kind=kLoop, calls=%fused_computation.126 | loop fusion | flops 30195712 | bytes 62309376 | tf_op jit(solution)/shard_map/add | solution.py:300
  155.1 0.8 pad_maximum_fusion.4
  156.0 1.2 collective-permute-start.15
  157.5 3.8 %collective-permute-done.6 = bf16[4,8,3,256]{3,2,1,0:T(4,128)(2,1)S(1)} collective-permute-done((bf16[4,8,3,256]{3,2,1,0:T(4,128)(2,1)S(1)}, bf16[4,8,3,256]{3,2,1,0:T(4,128)(2,1)S(1)}, u32[]{:S(2)}, u32[]{:S(2)}) %collective-permute-start.6) | collective-permute-done | bytes 49184 | tf_op jit(solution)/shard_map/ppermute | solution.py:180
  161.6 0.9 pad_maximum_fusion.8
  162.5 1.2 broadcast_select_fusion.1
  166.1 1.3 reshape.156
  167.3 1.1 convert_multiply_fusion.99
  (272 shorter events, 22.5 us)
Async XLA Ops:
  0.6 33.6 %copy-start = (bf16[1024,256]{1,0:T(8,128)(2,1)S(1)}, bf16[1024,256]{1,0:T(8,128)(2,1)}, u32[]{:S(2)}) copy-start(bf16[1024,256]{1,0:T(8,128)(2,1)} %param.23) | copy-start | bytes 1572868
  0.7 21.3 %copy-start.3 = (bf16[4,8,32,256]{3,2,1,0:T(8,128)(2,1)S(1)}, bf16[4,8,32,256]{3,2,1,0:T(8,128)(2,1)}, u32[]{:S(2)}) copy-start(bf16[4,8,32,256]{3,2,1,0:T(8,128)(2,1)} %param.13) | copy-start | bytes 1572868
  0.7 17.9 %copy-start.38 = (s32[8,32]{1,0:T(8,128)S(1)}, s32[8,32]{1,0:T(8,128)}, u32[]{:S(2)}) copy-start(s32[8,32]{1,0:T(8,128)} %param.16) | copy-start | bytes 3076
  1.7 10.2 %collective-permute-start = (bf16[4,8,3,256]{3,2,1,0:T(4,128)(2,1)S(1)}, bf16[4,8,3,256]{3,2,1,0:T(4,128)(2,1)S(1)}, u32[]{:S(2)}, u32[]{:S(2)}) collective-permute-start(bf16[4,8,3,256]{3,2,1,0:T(4,128)(2,1)S(1)} %slice.720), channel_id=1, source_target_pairs={{0,15},{1,14},{2,13},{3,12},{4,11},{5,10},{6,9},{7,8},{8,7},{9,6},... | collective-permute-start | bytes 147464 | tf_op jit(solution)/shard_map/ppermute | solution.py:180
  8.2 14.1 %copy-start.41 = (f32[1,1,256]{2,1,0:T(1,128)}, f32[1,1,256]{2,1,0:T(1,128)S(1)}, u32[]{:S(2)}) copy-start(f32[1,1,256]{2,1,0:T(1,128)S(1)} %get-tuple-element.129) | copy-start | bytes 3076
  8.2 14.1 %copy-start.43 = (f32[1,1,256]{2,1,0:T(1,128)}, f32[1,1,256]{2,1,0:T(1,128)S(1)}, u32[]{:S(2)}) copy-start(f32[1,1,256]{2,1,0:T(1,128)S(1)} %get-tuple-element.130) | copy-start | bytes 3076
  8.2 14.1 %copy-start.45 = (f32[1,1,256]{2,1,0:T(1,128)}, f32[1,1,256]{2,1,0:T(1,128)S(1)}, u32[]{:S(2)}) copy-start(f32[1,1,256]{2,1,0:T(1,128)S(1)} %get-tuple-element.131) | copy-start | bytes 3076
  8.2 14.1 %copy-start.46 = (f32[1,1,256]{2,1,0:T(1,128)}, f32[1,1,256]{2,1,0:T(1,128)S(1)}, u32[]{:S(2)}) copy-start(f32[1,1,256]{2,1,0:T(1,128)S(1)} %get-tuple-element.132) | copy-start | bytes 3076
  8.2 14.1 %copy-start.47 = (f32[1,1,256]{2,1,0:T(1,128)}, f32[1,1,256]{2,1,0:T(1,128)S(1)}, u32[]{:S(2)}) copy-start(f32[1,1,256]{2,1,0:T(1,128)S(1)} %get-tuple-element.133) | copy-start | bytes 3076
  8.2 14.1 %copy-start.48 = (f32[1,1,256]{2,1,0:T(1,128)}, f32[1,1,256]{2,1,0:T(1,128)S(1)}, u32[]{:S(2)}) copy-start(f32[1,1,256]{2,1,0:T(1,128)S(1)} %get-tuple-element.134) | copy-start | bytes 3076
  8.2 14.1 %copy-start.49 = (f32[1,1,256]{2,1,0:T(1,128)}, f32[1,1,256]{2,1,0:T(1,128)S(1)}, u32[]{:S(2)}) copy-start(f32[1,1,256]{2,1,0:T(1,128)S(1)} %get-tuple-element.135) | copy-start | bytes 3076
  8.3 14.1 %copy-start.50 = (f32[1,1,256]{2,1,0:T(1,128)}, f32[1,1,256]{2,1,0:T(1,128)S(1)}, u32[]{:S(2)}) copy-start(f32[1,1,256]{2,1,0:T(1,128)S(1)} %get-tuple-element.136) | copy-start | bytes 3076
  8.3 14.1 %copy-start.51 = (f32[1,1,256]{2,1,0:T(1,128)}, f32[1,1,256]{2,1,0:T(1,128)S(1)}, u32[]{:S(2)}) copy-start(f32[1,1,256]{2,1,0:T(1,128)S(1)} %get-tuple-element.137) | copy-start | bytes 3076
  8.3 14.1 %copy-start.52 = (f32[1,1,256]{2,1,0:T(1,128)}, f32[1,1,256]{2,1,0:T(1,128)S(1)}, u32[]{:S(2)}) copy-start(f32[1,1,256]{2,1,0:T(1,128)S(1)} %get-tuple-element.138) | copy-start | bytes 3076
  8.3 14.1 %copy-start.53 = (f32[1,1,256]{2,1,0:T(1,128)}, f32[1,1,256]{2,1,0:T(1,128)S(1)}, u32[]{:S(2)}) copy-start(f32[1,1,256]{2,1,0:T(1,128)S(1)} %get-tuple-element.139) | copy-start | bytes 3076
  8.3 14.1 %copy-start.54 = (f32[1,1,256]{2,1,0:T(1,128)}, f32[1,1,256]{2,1,0:T(1,128)S(1)}, u32[]{:S(2)}) copy-start(f32[1,1,256]{2,1,0:T(1,128)S(1)} %get-tuple-element.140) | copy-start | bytes 3076
  8.3 14.1 %copy-start.55 = (f32[1,1,256]{2,1,0:T(1,128)}, f32[1,1,256]{2,1,0:T(1,128)S(1)}, u32[]{:S(2)}) copy-start(f32[1,1,256]{2,1,0:T(1,128)S(1)} %get-tuple-element.141) | copy-start | bytes 3076
  8.3 14.1 %copy-start.56 = (f32[1,1,256]{2,1,0:T(1,128)}, f32[1,1,256]{2,1,0:T(1,128)S(1)}, u32[]{:S(2)}) copy-start(f32[1,1,256]{2,1,0:T(1,128)S(1)} %get-tuple-element.142) | copy-start | bytes 3076
  8.3 14.1 %copy-start.57 = (f32[1,1,256]{2,1,0:T(1,128)}, f32[1,1,256]{2,1,0:T(1,128)S(1)}, u32[]{:S(2)}) copy-start(f32[1,1,256]{2,1,0:T(1,128)S(1)} %get-tuple-element.143) | copy-start | bytes 3076
  8.3 14.1 %copy-start.58 = (f32[1,1,256]{2,1,0:T(1,128)}, f32[1,1,256]{2,1,0:T(1,128)S(1)}, u32[]{:S(2)}) copy-start(f32[1,1,256]{2,1,0:T(1,128)S(1)} %get-tuple-element.144) | copy-start | bytes 3076
  8.3 14.1 %copy-start.59 = (f32[1,1,256]{2,1,0:T(1,128)}, f32[1,1,256]{2,1,0:T(1,128)S(1)}, u32[]{:S(2)}) copy-start(f32[1,1,256]{2,1,0:T(1,128)S(1)} %get-tuple-element.145) | copy-start | bytes 3076
  9.4 13.1 %copy-start.60 = (f32[1,1,256]{2,1,0:T(1,128)}, f32[1,1,256]{2,1,0:T(1,128)S(1)}, u32[]{:S(2)}) copy-start(f32[1,1,256]{2,1,0:T(1,128)S(1)} %get-tuple-element.146) | copy-start | bytes 3076
  9.4 13.1 %copy-start.61 = (f32[1,1,256]{2,1,0:T(1,128)}, f32[1,1,256]{2,1,0:T(1,128)S(1)}, u32[]{:S(2)}) copy-start(f32[1,1,256]{2,1,0:T(1,128)S(1)} %get-tuple-element.147) | copy-start | bytes 3076
  9.4 13.1 %copy-start.62 = (f32[1,1,256]{2,1,0:T(1,128)}, f32[1,1,256]{2,1,0:T(1,128)S(1)}, u32[]{:S(2)}) copy-start(f32[1,1,256]{2,1,0:T(1,128)S(1)} %get-tuple-element.148) | copy-start | bytes 3076
  9.4 13.1 %copy-start.63 = (f32[1,1,256]{2,1,0:T(1,128)}, f32[1,1,256]{2,1,0:T(1,128)S(1)}, u32[]{:S(2)}) copy-start(f32[1,1,256]{2,1,0:T(1,128)S(1)} %get-tuple-element.149) | copy-start | bytes 3076
  9.4 13.1 %copy-start.64 = (f32[1,1,256]{2,1,0:T(1,128)}, f32[1,1,256]{2,1,0:T(1,128)S(1)}, u32[]{:S(2)}) copy-start(f32[1,1,256]{2,1,0:T(1,128)S(1)} %get-tuple-element.150) | copy-start | bytes 3076
  9.4 13.1 %copy-start.65 = (f32[1,1,256]{2,1,0:T(1,128)}, f32[1,1,256]{2,1,0:T(1,128)S(1)}, u32[]{:S(2)}) copy-start(f32[1,1,256]{2,1,0:T(1,128)S(1)} %get-tuple-element.151) | copy-start | bytes 3076
  9.4 13.1 %copy-start.66 = (f32[1,1,256]{2,1,0:T(1,128)}, f32[1,1,256]{2,1,0:T(1,128)S(1)}, u32[]{:S(2)}) copy-start(f32[1,1,256]{2,1,0:T(1,128)S(1)} %get-tuple-element.152) | copy-start | bytes 3076
  9.5 13.1 %copy-start.67 = (f32[1,1,256]{2,1,0:T(1,128)}, f32[1,1,256]{2,1,0:T(1,128)S(1)}, u32[]{:S(2)}) copy-start(f32[1,1,256]{2,1,0:T(1,128)S(1)} %get-tuple-element.153) | copy-start | bytes 3076
  9.5 13.1 %copy-start.68 = (f32[1,1,256]{2,1,0:T(1,128)}, f32[1,1,256]{2,1,0:T(1,128)S(1)}, u32[]{:S(2)}) copy-start(f32[1,1,256]{2,1,0:T(1,128)S(1)} %get-tuple-element.154) | copy-start | bytes 3076
  9.5 13.1 %copy-start.69 = (f32[1,1,256]{2,1,0:T(1,128)}, f32[1,1,256]{2,1,0:T(1,128)S(1)}, u32[]{:S(2)}) copy-start(f32[1,1,256]{2,1,0:T(1,128)S(1)} %get-tuple-element.155) | copy-start | bytes 3076
  9.5 13.1 %copy-start.70 = (f32[1,1,256]{2,1,0:T(1,128)}, f32[1,1,256]{2,1,0:T(1,128)S(1)}, u32[]{:S(2)}) copy-start(f32[1,1,256]{2,1,0:T(1,128)S(1)} %get-tuple-element.156) | copy-start | bytes 3076
  9.5 13.1 %copy-start.71 = (f32[1,1,256]{2,1,0:T(1,128)}, f32[1,1,256]{2,1,0:T(1,128)S(1)}, u32[]{:S(2)}) copy-start(f32[1,1,256]{2,1,0:T(1,128)S(1)} %get-tuple-element.157) | copy-start | bytes 3076
  9.5 13.1 %copy-start.72 = (f32[1,1,256]{2,1,0:T(1,128)}, f32[1,1,256]{2,1,0:T(1,128)S(1)}, u32[]{:S(2)}) copy-start(f32[1,1,256]{2,1,0:T(1,128)S(1)} %get-tuple-element.158) | copy-start | bytes 3076
  9.5 13.1 %copy-start.73 = (f32[1,1,256]{2,1,0:T(1,128)}, f32[1,1,256]{2,1,0:T(1,128)S(1)}, u32[]{:S(2)}) copy-start(f32[1,1,256]{2,1,0:T(1,128)S(1)} %get-tuple-element.159) | copy-start | bytes 3076
  9.5 13.1 %copy-start.74 = (f32[1,1,256]{2,1,0:T(1,128)}, f32[1,1,256]{2,1,0:T(1,128)S(1)}, u32[]{:S(2)}) copy-start(f32[1,1,256]{2,1,0:T(1,128)S(1)} %get-tuple-element.160) | copy-start | bytes 3076
  9.5 13.1 %copy-start.75 = (f32[1,1,256]{2,1,0:T(1,128)}, f32[1,1,256]{2,1,0:T(1,128)S(1)}, u32[]{:S(2)}) copy-start(f32[1,1,256]{2,1,0:T(1,128)S(1)} %get-tuple-element.161) | copy-start | bytes 3076
  9.5 13.1 %copy-start.76 = (f32[1,1,256]{2,1,0:T(1,128)}, f32[1,1,256]{2,1,0:T(1,128)S(1)}, u32[]{:S(2)}) copy-start(f32[1,1,256]{2,1,0:T(1,128)S(1)} %get-tuple-element.162) | copy-start | bytes 3076
  9.6 13.1 %copy-start.77 = (f32[1,1,256]{2,1,0:T(1,128)}, f32[1,1,256]{2,1,0:T(1,128)S(1)}, u32[]{:S(2)}) copy-start(f32[1,1,256]{2,1,0:T(1,128)S(1)} %get-tuple-element.163) | copy-start | bytes 3076
  9.6 13.1 %copy-start.78 = (f32[1,1,256]{2,1,0:T(1,128)}, f32[1,1,256]{2,1,0:T(1,128)S(1)}, u32[]{:S(2)}) copy-start(f32[1,1,256]{2,1,0:T(1,128)S(1)} %get-tuple-element.164) | copy-start | bytes 3076
  11.1 11.6 %copy-start.79 = (f32[1,1,256]{2,1,0:T(1,128)}, f32[1,1,256]{2,1,0:T(1,128)S(1)}, u32[]{:S(2)}) copy-start(f32[1,1,256]{2,1,0:T(1,128)S(1)} %get-tuple-element.165) | copy-start | bytes 3076
  11.1 11.6 %copy-start.80 = (f32[1,1,256]{2,1,0:T(1,128)}, f32[1,1,256]{2,1,0:T(1,128)S(1)}, u32[]{:S(2)}) copy-start(f32[1,1,256]{2,1,0:T(1,128)S(1)} %get-tuple-element.166) | copy-start | bytes 3076
  11.1 11.6 %copy-start.81 = (f32[1,1,256]{2,1,0:T(1,128)}, f32[1,1,256]{2,1,0:T(1,128)S(1)}, u32[]{:S(2)}) copy-start(f32[1,1,256]{2,1,0:T(1,128)S(1)} %get-tuple-element.167) | copy-start | bytes 3076
  13.5 8.5 %collective-permute-start.1 = (bf16[4,3,38,256]{3,2,1,0:T(8,128)(2,1)S(1)}, bf16[4,3,38,256]{3,2,1,0:T(8,128)(2,1)S(1)}, u32[]{:S(2)}, u32[]{:S(2)}) collective-permute-start(bf16[4,3,38,256]{3,2,1,0:T(8,128)(2,1)S(1)} %get-tuple-element.115), channel_id=1, source_target_pairs={{0,1},{1,2},{2,3},{3,4},{4,5},{5,6},{6,7},{7,8},{8,9},{9,10},{10,1... | collective-permute-start | bytes 700424 | tf_op jit(solution)/shard_map/ppermute | solution.py:26
  14.2 7.8 %collective-permute-start.2 = (bf16[4,3,38,256]{3,2,1,0:T(8,128)(2,1)S(1)}, bf16[4,3,38,256]{3,2,1,0:T(8,128)(2,1)S(1)}, u32[]{:S(2)}, u32[]{:S(2)}) collective-permute-start(bf16[4,3,38,256]{3,2,1,0:T(8,128)(2,1)S(1)} %get-tuple-element.116), channel_id=1, source_target_pairs={{1,0},{2,1},{3,2},{4,3},{5,4},{6,5},{7,6},{8,7},{9,8},{10,9},{11,1... | collective-permute-start | bytes 700424 | tf_op jit(solution)/shard_map/ppermute | solution.py:27
  41.9 41.6 %copy-start.7 = (f32[8,32,256]{2,1,0:T(8,128)}, f32[8,32,256]{2,1,0:T(8,128)S(1)}, u32[]{:S(2)}) copy-start(f32[8,32,256]{2,1,0:T(8,128)S(1)} %get-tuple-element.84) | copy-start | bytes 786436
  41.9 41.6 %copy-start.9 = (f32[8,32,256]{2,1,0:T(8,128)}, f32[8,32,256]{2,1,0:T(8,128)S(1)}, u32[]{:S(2)}) copy-start(f32[8,32,256]{2,1,0:T(8,128)S(1)} %get-tuple-element.85) | copy-start | bytes 786436
  57.4 29.4 %copy-start.1 = (f32[4,8,32,256]{3,2,1,0:T(8,128)}, f32[4,8,32,256]{3,2,1,0:T(8,128)S(1)}, u32[]{:S(2)}) copy-start(f32[4,8,32,256]{3,2,1,0:T(8,128)S(1)} %get-tuple-element.95) | copy-start | bytes 3145732
  67.0 11.2 %copy-start.24 = (bf16[1,8,32,256]{3,2,1,0:T(8,128)(2,1)S(1)}, bf16[1,8,32,256]{3,2,1,0:T(8,128)(2,1)}, u32[]{:S(2)}) copy-start(bf16[1,8,32,256]{3,2,1,0:T(8,128)(2,1)} %copy-done.23) | copy-start | bytes 393220
  86.2 13.3 %collective-permute-start.3 = (f32[270336]{0:T(1024)}, f32[270336]{0:T(1024)}, u32[]{:S(2)}, u32[]{:S(2)}) collective-permute-start(f32[270336]{0:T(1024)} %pad_dynamic-slice_fusion), channel_id=1, source_target_pairs={{0,1},{1,0},{2,3},{3,2},{4,5},{5,4},{6,7},{7,6},{8,9},{9,8},{10,11... | collective-permute-start | bytes 3244040 | tf_op jit(solution)/shard_map/ppermute | solution.py:224
  86.8 10.1 %collective-permute-start.4 = (f32[4,3,32,256]{3,2,1,0:T(8,128)S(1)}, f32[4,3,32,256]{3,2,1,0:T(8,128)S(1)}, u32[]{:S(2)}, u32[]{:S(2)}) collective-permute-start(f32[4,3,32,256]{3,2,1,0:T(8,128)S(1)} %get-tuple-element.111), channel_id=1, source_target_pairs={{0,1},{1,2},{2,3},{3,4},{4,5},{5,6},{6,7},{7,8},{8,9},{9,10},{10,1... | collective-permute-start | bytes 1179656 | tf_op jit(solution)/shard_map/ppermute | solution.py:26
  86.9 10.7 %collective-permute-start.5 = (f32[4,3,32,256]{3,2,1,0:T(8,128)S(1)}, f32[4,3,32,256]{3,2,1,0:T(8,128)}, u32[]{:S(2)}, u32[]{:S(2)}) collective-permute-start(f32[4,3,32,256]{3,2,1,0:T(8,128)S(1)} %get-tuple-element.112), channel_id=1, source_target_pairs={{1,0},{2,1},{3,2},{4,3},{5,4},{6,5},{7,6},{8,7},{9,8},{10,9},{11,1... | collective-permute-start | bytes 1179656 | tf_op jit(solution)/shard_map/ppermute | solution.py:27
  103.9 40.2 %copy-start.42 = (f32[1,1,256]{2,1,0:T(1,128)S(1)}, f32[1,1,256]{2,1,0:T(1,128)}, u32[]{:S(2)}) copy-start(f32[1,1,256]{2,1,0:T(1,128)} %copy-done.41) | copy-start | bytes 3076
  103.9 40.2 %copy-start.44 = (f32[1,1,256]{2,1,0:T(1,128)S(1)}, f32[1,1,256]{2,1,0:T(1,128)}, u32[]{:S(2)}) copy-start(f32[1,1,256]{2,1,0:T(1,128)} %copy-done.43) | copy-start | bytes 3076
  103.9 15.3 %collective-permute-start.7 = (f32[67584]{0:T(1024)}, f32[67584]{0:T(1024)}, u32[]{:S(2)}, u32[]{:S(2)}) collective-permute-start(f32[67584]{0:T(1024)} %get-tuple-element.108), channel_id=1, source_target_pairs={{0,2},{1,3},{2,0},{3,1},{4,6},{5,7},{6,4},{7,5},{8,10},{9,11},{10,... | collective-permute-start | bytes 811016 | tf_op jit(solution)/shard_map/ppermute | solution.py:224
  105.2 14.0 %collective-permute-start.9 = (f32[67584]{0:T(1024)}, f32[67584]{0:T(1024)}, u32[]{:S(2)}, u32[]{:S(2)}) collective-permute-start(f32[67584]{0:T(1024)} %get-tuple-element.109), channel_id=1, source_target_pairs={{0,6},{1,7},{2,4},{3,5},{4,2},{5,3},{6,0},{7,1},{8,14},{9,15},{10,... | collective-permute-start | bytes 811016 | tf_op jit(solution)/shard_map/ppermute | solution.py:224
  105.2 15.3 %collective-permute-start.8 = (f32[67584]{0:T(1024)}, f32[67584]{0:T(1024)}, u32[]{:S(2)}, u32[]{:S(2)}) collective-permute-start(f32[67584]{0:T(1024)} %get-tuple-element.110), channel_id=1, source_target_pairs={{0,4},{1,5},{2,6},{3,7},{4,0},{5,1},{6,2},{7,3},{8,12},{9,13},{10,... | collective-permute-start | bytes 811016 | tf_op jit(solution)/shard_map/ppermute | solution.py:224
  123.1 9.4 %collective-permute-start.10 = (f32[33792]{0:T(1024)}, f32[33792]{0:T(1024)}, u32[]{:S(2)}, u32[]{:S(2)}) collective-permute-start(f32[33792]{0:T(1024)} %dynamic_slice.31), channel_id=1, source_target_pairs={{0,8},{1,9},{2,10},{3,11},{4,12},{5,13},{6,14},{7,15},{8,0},{9,1},... | collective-permute-start | bytes 405512 | tf_op jit(solution)/shard_map/ppermute | solution.py:224
  134.1 5.5 %collective-permute-start.11 = (bf16[33792]{0:T(1024)(128)(2,1)}, bf16[33792]{0:T(1024)(128)(2,1)}, u32[]{:S(2)}, u32[]{:S(2)}) collective-permute-start(bf16[33792]{0:T(1024)(128)(2,1)} %add_convert_fusion.1), channel_id=1, source_target_pairs={{0,8},{1,9},{2,10},{3,11},{4,12},{5,13},{6,14},{7,15},{8,0},{9,1},... | collective-permute-start | bytes 202760 | tf_op jit(solution)/shard_map/ppermute | solution.py:233
  140.6 14.4 %collective-permute-start.14 = (bf16[67584]{0:T(1024)(128)(2,1)S(1)}, bf16[67584]{0:T(1024)(128)(2,1)S(1)}, u32[]{:S(2)}, u32[]{:S(2)}) collective-permute-start(bf16[67584]{0:T(1024)(128)(2,1)S(1)} %pad_maximum_fusion.12), channel_id=1, source_target_pairs={{0,6},{1,7},{2,4},{3,5},{4,2},{5,3},{6,0},{7,1},{8,14},{9,15},{10,... | collective-permute-start | bytes 405512 | tf_op jit(solution)/shard_map/ppermute | solution.py:233
  140.6 14.3 %collective-permute-start.13 = (bf16[67584]{0:T(1024)(128)(2,1)S(1)}, bf16[67584]{0:T(1024)(128)(2,1)S(1)}, u32[]{:S(2)}, u32[]{:S(2)}) collective-permute-start(bf16[67584]{0:T(1024)(128)(2,1)S(1)} %pad_maximum_fusion.12), channel_id=1, source_target_pairs={{0,2},{1,3},{2,0},{3,1},{4,6},{5,7},{6,4},{7,5},{8,10},{9,11},{10,... | collective-permute-start | bytes 405512 | tf_op jit(solution)/shard_map/ppermute | solution.py:233
  140.9 14.0 %collective-permute-start.12 = (bf16[67584]{0:T(1024)(128)(2,1)S(1)}, bf16[67584]{0:T(1024)(128)(2,1)S(1)}, u32[]{:S(2)}, u32[]{:S(2)}) collective-permute-start(bf16[67584]{0:T(1024)(128)(2,1)S(1)} %pad_maximum_fusion.12), channel_id=1, source_target_pairs={{0,4},{1,5},{2,6},{3,7},{4,0},{5,1},{6,2},{7,3},{8,12},{9,13},{10,... | collective-permute-start | bytes 405512 | tf_op jit(solution)/shard_map/ppermute | solution.py:233
  154.9 6.5 %collective-permute-start.6 = (bf16[4,8,3,256]{3,2,1,0:T(4,128)(2,1)S(1)}, bf16[4,8,3,256]{3,2,1,0:T(4,128)(2,1)S(1)}, u32[]{:S(2)}, u32[]{:S(2)}) collective-permute-start(bf16[4,8,3,256]{3,2,1,0:T(4,128)(2,1)S(1)} %slice.1261), channel_id=1, source_target_pairs={{0,15},{1,14},{2,13},{3,12},{4,11},{5,10},{6,9},{7,8},{8,7},{9,6},... | collective-permute-start | bytes 147464 | tf_op jit(solution)/shard_map/ppermute | solution.py:180
  156.0 6.5 %collective-permute-start.15 = (bf16[270336]{0:T(1024)(128)(2,1)}, bf16[270336]{0:T(1024)(128)(2,1)}, u32[]{:S(2)}, u32[]{:S(2)}) collective-permute-start(bf16[270336]{0:T(1024)(128)(2,1)} %pad_maximum_fusion.4), channel_id=1, source_target_pairs={{0,1},{1,0},{2,3},{3,2},{4,5},{5,4},{6,7},{7,6},{8,9},{9,8},{10,11... | collective-permute-start | bytes 1622024 | tf_op jit(solution)/shard_map/ppermute | solution.py:233
  (51 other events, 94.5 us)

commit v8 on v6

--- a/solution.py
+++ b/solution.py
@@ -106,7 +106,7 @@
     grad_pred = jnp.stack(grad_list)
     grad_scale = jnp.sum(grad_pred * branch, axis=(0, 1, 2))
     grad_b_out = jnp.zeros((chans,), jnp.float32)
-    grad_w_out = jnp.zeros(w_out.shape, jnp.float32)
+    grad_w_out = jnp.zeros(w_out.shape[::-1], jnp.float32)
     grad_b_in = jnp.zeros(b_in.shape, jnp.float32)
     grad_w_in = jnp.zeros(w_in.shape, jnp.float32)
     normed_grads = []
@@ -117,7 +117,7 @@
         grad_b_out = grad_b_out + jnp.sum(grad_out, axis=0)
         out_half = grad_out.astype(jnp.bfloat16)
         grad_w_out = grad_w_out + lax.dot_general(
-            hiddens[member], out_half, contract_rows, preferred_element_type=jnp.float32
+            out_half, hiddens[member], contract_rows, preferred_element_type=jnp.float32
         )
         grad_hidden = lax.dot_general(
             out_half, w_out, contract_cols, preferred_element_type=jnp.float32
@@ -208,23 +208,26 @@
     return cur.astype(flat.dtype)
 
 
-def radix_allreduce(flat, axis, gather_dtype):
+def radix_allreduce(block, axis, gather_dtype):
     size = lax.axis_size(axis)
     nbits = size.bit_length() - 1
     groups = [[0]] + [list(range(b, min(b + 2, nbits))) for b in range(1, nbits, 2)]
     idx = lax.axis_index(axis)
-    cur = flat
+    cur = block
+    dims = []
     for bits in groups:
         radix, low = 1 << len(bits), bits[0]
         sub = (idx >> low) & (radix - 1)
-        part = cur.shape[0] // radix
-        total = lax.dynamic_slice_in_dim(cur, sub * part, part)
+        dim = 1 if cur.shape[1] // radix >= 128 else 0
+        part = cur.shape[dim] // radix
+        total = lax.dynamic_slice_in_dim(cur, sub * part, part, axis=dim)
         for d in range(1, radix):
-            send = lax.dynamic_slice_in_dim(cur, (sub ^ d) * part, part)
+            send = lax.dynamic_slice_in_dim(cur, (sub ^ d) * part, part, axis=dim)
             total = total + lax.ppermute(send, axis, [(i, i ^ (d << low)) for i in range(size)])
         cur = total
+        dims.append(dim)
     cur = cur.astype(gather_dtype)
-    for bits in reversed(groups):
+    for bits, dim in reversed(list(zip(groups, dims))):
         radix, low = 1 << len(bits), bits[0]
         sub = (idx >> low) & (radix - 1)
         pieces = [cur] + [
@@ -237,8 +240,8 @@
             for s in range(radix - 1):
                 pick = jnp.where(sub == s, pieces[p ^ s], pick)
             placed.append(pick)
-        cur = jnp.concatenate(placed)
-    return cur.astype(flat.dtype)
+        cur = jnp.concatenate(placed, axis=dim)
+    return cur.astype(block.dtype)
 
 
 def butterfly_allreduce(flat, axis):
@@ -316,18 +319,27 @@
         scale_sum,
     ) = grads
     lon_size = lax.axis_size("lon")
-    sums = (
-        kernel_sum,
-        dw_bias_sum,
-        gain_sum,
-        bias_sum,
-        w_in_sum,
-        b_in_sum,
-        w_out_sum,
-        b_out_sum,
-        scale_sum,
-    )
-    totals = unpack(radix_allreduce(pack(sums, lon_size * 1024), "lon", jnp.bfloat16), sums)
+    small = (kernel_sum, dw_bias_sum, gain_sum, bias_sum, b_in_sum, b_out_sum, scale_sum)
+    width = w_in_sum.shape[1]
+    big_rows = w_in_sum.shape[0] + w_out_sum.shape[0]
+    small_rows = -(-sum(a.size for a in small) // width)
+    small_rows += -(big_rows + small_rows) % lon_size
+    block = jnp.concatenate(
+        [w_in_sum, w_out_sum, pack(small, small_rows * width).reshape(small_rows, width)]
+    )
+    block = radix_allreduce(block, "lon", jnp.bfloat16)
+    small_tot = unpack(block[big_rows:].reshape(-1), small)
+    totals = (
+        small_tot[0],
+        small_tot[1],
+        small_tot[2],
+        small_tot[3],
+        block[: w_in_sum.shape[0]],
+        small_tot[4],
+        block[w_in_sum.shape[0] : big_rows].T,
+        small_tot[5],
+        small_tot[6],
+    )
     factor = 1.0 / math.sqrt(members * lat_rows * lon_dev * lax.axis_size("lon"))
     return (
         predicted,

time: 159 us -> 174 us (1.094)
  matrix products: 16.3 us -> 20.7 us
  other arithmetic: 48.7 us -> 53 us
  waiting for transfers between devices: 40.6 us -> 44 us
  starting transfers between devices: 23.9 us -> 26.3 us
    another operation x7, local copies, waits for them, and re-layouts: 0.2 us -> 5.06 us  [local_step(): kernel_rows.append(jnp.stack(kernel_cols))]
    unnamed x294 -> x272, local copies, waits for them, and re-layouts: 13.6 us -> 9.03 us
    dot_general x4, matrix products: 1.28 us -> 4.69 us  [local_step(): lax.dot_general(normed[member].reshape(rows, chans), pre_half, contract_r...]
    unnamed x4 -> x5, other arithmetic: 3.19 us -> 0.03 us
    ppermute x5, starting transfers between devices: 3.61 us -> 6.29 us  [radix_allreduce(): lax.ppermute(send, axis, [(i, i ^ d << low) for i in range(size)])]
    ppermute x5, waiting for transfers between devices: 9.01 us -> 11.3 us  [radix_allreduce(): lax.ppermute(cur, axis, [(i, i ^ d << low) for i in range(size)])]
    ppermute x2, waiting for transfers between devices: 3.83 us -> 6.09 us  [with_halo(): before = lax.ppermute(last, axis, up)]
  transfers between devices with their start and end apart: 16 -> 16, of which waited for: 11 -> 10; matrix products, arithmetic and copies ran while one was open for 11% -> 5% of each run, Pallas kernels for 0% -> 0%
where the time goes in v8:
time: 174 us; the launch traced here: 173 us
  other arithmetic  53 us (30%)
  waiting for transfers between devices  44 us (25%)
  starting transfers between devices  26.3 us (15%)
  local copies, waits for them, and re-layouts  26.1 us (15%)
  matrix products  20.7 us (12%)
  between operations  2.81 us (2%)
    ppermute x5, waiting for transfers between devices, radix_allreduce(): lax.ppermute(send, axis, [(i, i ^ d << low) for i in range(size)])  22.1 us
    ppermute x5, waiting for transfers between devices, radix_allreduce(): lax.ppermute(cur, axis, [(i, i ^ d << low) for i in range(size)])  11.3 us
    reduce_sum x4, other arithmetic, local_step(): jnp.sum(grad_depth * extended[:, lon_off:lon_off + lon_dev, lat_off:lat_o...  10.6 us
    add x1, other arithmetic, on_device(): grad_ext + dw_kernel[lon_off, lat_off] * padded[:, 6 - lon_off:6 - lon_of...  10.2 us
    reduce_sum x1, other arithmetic, local_step(): mean_val = jnp.mean(depth, axis=-1, keepdims=True)  9.36 us
    unnamed x272, local copies, waits for them, and re-layouts  9.03 us
    ppermute x2, starting transfers between devices, with_halo(): after = lax.ppermute(leading, axis, down)  7.62 us
    ppermute x2, starting transfers between devices, mirrored(): return lax.ppermute(x, axis, [(i, size - 1 - i) for i in range(size)])  7.43 us
  transfers between devices with their start and end apart: 16, of which 10 were waited for; matrix products, arithmetic and copies ran while one was open for 5% of the time, Pallas kernels for 0%

profile of v8, /device:TPU:0, one launch (start us, length us, event | category | flops | bytes accessed | tf_op | source)
XLA Modules:
  0.0 173.0 jit_solution(12993980624388195717)
XLA Ops:
  0.7 1.0 slice.713
  1.7 5.5 %collective-permute-start = (bf16[4,8,3,256]{3,2,1,0:T(4,128)(2,1)S(1)}, bf16[4,8,3,256]{3,2,1,0:T(4,128)(2,1)S(1)}, u32[]{:S(2)}, u32[]{:S(2)}) collective-permute-start(bf16[4,8,3,256]{3,2,1,0:T(4,128)(2,1)S(1)} %slice.713), channel_id=1, source_target_pairs={{0,15},{1,14},{2,13},{3,12},{4,11},{5,10},{6,9},{7,8},{8,7},{9,6},... | collective-permute-start | bytes 147464 | tf_op jit(solution)/shard_map/ppermute | solution.py:180
  7.2 1.0 fusion.212
  8.4 1.0 fusion.213
  9.6 1.5 fusion.214
  11.1 0.8 copy.25
  12.2 1.3 pad_maximum_fusion.11
  13.5 0.7 collective-permute-start.1
  14.2 3.8 %collective-permute-start.2 = (bf16[4,3,38,256]{3,2,1,0:T(8,128)(2,1)S(1)}, bf16[4,3,38,256]{3,2,1,0:T(8,128)(2,1)S(1)}, u32[]{:S(2)}, u32[]{:S(2)}) collective-permute-start(bf16[4,3,38,256]{3,2,1,0:T(8,128)(2,1)S(1)} %get-tuple-element.121), channel_id=1, source_target_pairs={{1,0},{2,1},{3,2},{4,3},{5,4},{6,5},{7,6},{8,7},{9,8},{10,9},{11,1... | collective-permute-start | bytes 700424 | tf_op jit(solution)/shard_map/ppermute | solution.py:27
  18.5 0.8 compare_convert_fusion
  19.3 2.6 %collective-permute-done.1 = bf16[4,3,38,256]{3,2,1,0:T(8,128)(2,1)S(1)} collective-permute-done((bf16[4,3,38,256]{3,2,1,0:T(8,128)(2,1)S(1)}, bf16[4,3,38,256]{3,2,1,0:T(8,128)(2,1)S(1)}, u32[]{:S(2)}, u32[]{:S(2)}) %collective-permute-start.1) | collective-permute-done | bytes 233504 | tf_op jit(solution)/shard_map/ppermute | solution.py:26
  22.7 9.4 %fusion.208 = (f32[4,8,32]{2,1,0:T(8,128)S(1)}, f32[4,8,32,256]{3,2,1,0:T(8,128)S(1)}) fusion(bf16[4,11,38,256]{3,2,1,0:T(8,128)(2,1)S(1)} %get-tuple-element.119, f32[256]{0:T(256)} %bitcast.48, f32[256]{0:T(256)} %bitcast.47, f32[256]{0:T(256)S(1)} %bitcast.340, f32[256]{0:T(256)S(1)} %bitcast.342, f32[256]{0:T(256)S(1)} %bitcast.344, ...), kind=kLoop, calls=%fused_computation.496 | loop fusion | flops 43514880 | bytes 23746560 | tf_op jit(solution)/shard_map/reduce_sum | solution.py:62
  37.1 1.0 fusion.206
  38.1 3.8 %multiply_reduce_fusion.7 = (f32[256]{0:T(256)}, f32[256]{0:T(256)}, f32[256]{0:T(256)}, f32[256]{0:T(256)}, f32[8,32,256]{2,1,0:T(8,128)S(1)}, /*index=5*/f32[8...) fusion(f32[256]{0:T(256)S(1)} %copy-done.38, ...), kind=kLoop, calls=%fused_computation.431 | loop fusion | flops 7863296 | bytes 2497536 | tf_op jit(solution)/shard_map/reduce_sum | solution.py:117
  42.0 1.5 fusion.200
  44.1 1.5 fusion.198
  45.6 0.9 fusion.218
  46.5 1.5 fusion.202
  48.0 1.5 fusion.204
  49.5 0.9 fusion.215
  50.5 0.9 fusion.216
  51.4 0.9 fusion.217
  52.3 1.0 multiply_reduce_fusion.1
  53.3 4.1 %fusion.145 = (f32[256]{0:T(256)}, f32[256]{0:T(256)}, f32[256]{0:T(256)}, f32[256]{0:T(256)}, f32[256]{0:T(256)}, /*index=5*/f32[256]{0:T(256)}, f32[256]{0:T(2...) fusion(bf16[4,11,38,256]{3,2,1,0:T(8,128)(2,1)S(1)} %get-tuple-, ...), kind=kLoop, calls=%fused_computation.322 | loop fusion | flops 16772608 | bytes 12618752 | tf_op jit(solution)/shard_map/reduce_sum | solution.py:154
  57.4 2.3 %fusion.127 = (f32[256]{0:T(256)}, f32[256]{0:T(256)}, f32[256]{0:T(256)}, f32[256]{0:T(256)}, f32[256]{0:T(256)}, /*index=5*/f32[256]{0:T(256)}, f32[256]{0:T(2...) fusion(f32[4,8,32,256]{3,2,1,0:T(8,128)S(1)} %get-tuple-element.103, ...), kind=kLoop, calls=%fused_computation.304 | loop fusion | flops 12842240 | bytes 3255296 | tf_op jit(solution)/shard_map/reduce_sum | solution.py:154
  59.7 1.0 fusion.76
  60.7 3.2 %fusion.94 = (f32[256]{0:T(256)}, f32[256]{0:T(256)}, f32[256]{0:T(256)}, f32[256]{0:T(256)}, f32[256]{0:T(256)}, /*index=5*/f32[256]{0:T(256)}, f32[256]{0:T(25...) fusion(f32[4,8,32,256]{3,2,1,0:T(8,128)S(1)} %get-tuple-element, ...), kind=kLoop, calls=%fused_computation.271 | loop fusion | flops 14151168 | bytes 10504192 | tf_op jit(solution)/shard_map/reduce_sum | solution.py:154
  63.9 1.3 fusion.186
  65.2 0.9 fusion.210
  67.2 0.7 stack.227
  71.2 0.7 stack.254
  72.5 0.7 stack.263
  73.9 0.7 stack.272
  76.5 1.4 reshape.145
  78.0 1.8 %convolution_add_fusion.5 = f32[256,1024]{1,0:T(8,128)S(1)} fusion(f32[256,1024]{1,0:T(8,128)} %fusion.186, bf16[256,256]{1,0:T(8,128)(2,1)S(1)} %bitcast.319, bf16[256,1024]{1,0:T(8,128)(2,1)} %copy-done.9), kind=kOutput, calls=%fused_computation.22 | convolution fusion | flops 134479872 | bytes 2752512 | tf_op jit(solution)/shard_map/dot_general | solution.py:128
  81.0 1.3 convolution_add_fusion.3
  82.9 3.9 %collective-permute-start.4 = (f32[4,3,32,256]{3,2,1,0:T(8,128)S(1)}, f32[4,3,32,256]{3,2,1,0:T(8,128)S(1)}, u32[]{:S(2)}, u32[]{:S(2)}) collective-permute-start(f32[4,3,32,256]{3,2,1,0:T(8,128)S(1)} %copy-done.30), channel_id=1, source_target_pairs={{1,0},{2,1},{3,2},{4,3},{5,4},{6,5},{7,6},{8,7},{9,8},{10,9},{11,1... | collective-permute-start | bytes 1179656 | tf_op jit(solution)/shard_map/ppermute | solution.py:27
  87.0 1.5 convolution_add_fusion
  88.8 3.5 %collective-permute-done.3 = f32[4,3,32,256]{3,2,1,0:T(8,128)S(1)} collective-permute-done((f32[4,3,32,256]{3,2,1,0:T(8,128)S(1)}, f32[4,3,32,256]{3,2,1,0:T(8,128)S(1)}, u32[]{:S(2)}, u32[]{:S(2)}) %collective-permute-start.3) | collective-permute-done | bytes 393248 | tf_op jit(solution)/shard_map/ppermute | solution.py:26
  93.1 10.2 %fusion.1 = f32[4,8,38,256]{3,2,1,0:T(8,128)S(1)} fusion(f32[4,14,44,256]{3,2,1,0:T(8,128)S(1)} %select_maximum_fusion, f32[256]{0:T(256)} %bitcast.48, f32[256]{0:T(256)} %bitcast.47, f32[256]{0:T(256)S(1)} %bitcast.341, f32[256]{0:T(256)S(1)} %bitcast.343, f32[256]{0:T(256)S(1)} %bitcast.345, f32[256]{0:T(256)S(1)} %bitcast.347, f32[256]{0:T(256)S(1)} %bitcast.349, ...), kind=kLoop, calls=%fused_computation.124 | loop fusion | flops 30195712 | bytes 62309376 | tf_op jit(solution)/shard_map/add | solution.py:296
  103.4 1.3 multiply_reduce_fusion
  104.8 1.7 pad_maximum_fusion
  106.5 1.1 constant_dynamic-slice_fusion.4
  107.6 2.1 %collective-permute-start.6 = (f32[528,512]{1,0:T(8,128)}, f32[528,512]{1,0:T(8,128)}, u32[]{:S(2)}, u32[]{:S(2)}) collective-permute-start(f32[528,512]{1,0:T(8,128)} %constant_dynamic-slice_fusion.4), channel_id=1, source_target_pairs={{0,1},{1,0},{2,3},{3,2},{4,5},{5,4},{6,7},{7,6},{8,9},{9,8},{10,11... | collective-permute-start | bytes 3244040 | tf_op jit(solution)/shard_map/ppermute | solution.py:226
  109.7 2.7 %collective-permute-done.6 = f32[528,512]{1,0:T(8,128)} collective-permute-done((f32[528,512]{1,0:T(8,128)}, f32[528,512]{1,0:T(8,128)}, u32[]{:S(2)}, u32[]{:S(2)}) %collective-permute-start.6) | collective-permute-done | bytes 1081376 | tf_op jit(solution)/shard_map/ppermute | solution.py:226
  112.4 2.5 %dynamic-slice_add_fusion = f32[528,512]{1,0:T(8,128)} fusion(f32[528,512]{1,0:T(8,128)} %collective-permute-done.6, f32[528,1024]{1,0:T(8,128)S(1)} %pad_maximum_fusion, s32[]{:T(128)S(6)} %select_n.117), kind=kLoop, calls=%fused_computation.225 | loop fusion | flops 270336 | bytes 3244036 | tf_op jit(solution)/shard_map/add | solution.py:226
  114.8 1.2 constant_dynamic-slice_fusion.3
  116.3 3.3 %collective-permute-start.8 = (f32[528,128]{1,0:T(8,128)S(1)}, f32[528,128]{1,0:T(8,128)S(1)}, u32[]{:S(2)}, u32[]{:S(2)}) collective-permute-start(f32[528,128]{1,0:T(8,128)S(1)} %get-tuple-element.113), channel_id=1, source_target_pairs={{0,4},{1,5},{2,6},{3,7},{4,0},{5,1},{6,2},{7,3},{8,12},{9,13},{10,... | collective-permute-start | bytes 811016 | tf_op jit(solution)/shard_map/ppermute | solution.py:226
  119.6 11.1 %collective-permute-done.7 = f32[528,128]{1,0:T(8,128)S(1)} collective-permute-done((f32[528,128]{1,0:T(8,128)S(1)}, f32[528,128]{1,0:T(8,128)S(1)}, u32[]{:S(2)}, u32[]{:S(2)}) %collective-permute-start.7) | collective-permute-done | bytes 270368 | tf_op jit(solution)/shard_map/ppermute | solution.py:226
  130.6 1.2 collective-permute-done.8
  131.9 1.0 add_add_fusion
  133.6 7.2 %collective-permute-done.10 = f32[264,128]{1,0:T(8,128)S(1)} collective-permute-done((f32[264,128]{1,0:T(8,128)S(1)}, f32[264,128]{1,0:T(8,128)S(1)}, u32[]{:S(2)}, u32[]{:S(2)}) %collective-permute-start.10) | collective-permute-done | bytes 135200 | tf_op jit(solution)/shard_map/ppermute | solution.py:226
  140.9 6.3 %collective-permute-done.11 = bf16[264,128]{1,0:T(8,128)(2,1)S(1)} collective-permute-done((bf16[264,128]{1,0:T(8,128)(2,1)S(1)}, bf16[264,128]{1,0:T(8,128)(2,1)S(1)}, u32[]{:S(2)}, u32[]{:S(2)}) %collective-permute-start.11) | collective-permute-done | bytes 67616 | tf_op jit(solution)/shard_map/ppermute | solution.py:234
  148.0 2.8 %collective-permute-start.12 = (bf16[528,128]{1,0:T(8,128)(2,1)S(1)}, bf16[528,128]{1,0:T(8,128)(2,1)S(1)}, u32[]{:S(2)}, u32[]{:S(2)}) collective-permute-start(bf16[528,128]{1,0:T(8,128)(2,1)S(1)} %pad_maximum_fusion.12), channel_id=1, source_target_pairs={{0,4},{1,5},{2,6},{3,7},{4,0},{5,1},{6,2},{7,3},{8,12},{9,13},{10,... | collective-permute-start | bytes 405512 | tf_op jit(solution)/shard_map/ppermute | solution.py:234
  150.8 3.9 %collective-permute-done.14 = bf16[528,128]{1,0:T(8,128)(2,1)S(1)} collective-permute-done((bf16[528,128]{1,0:T(8,128)(2,1)S(1)}, bf16[528,128]{1,0:T(8,128)(2,1)S(1)}, u32[]{:S(2)}, u32[]{:S(2)}) %collective-permute-start.14) | collective-permute-done | bytes 135200 | tf_op jit(solution)/shard_map/ppermute | solution.py:234
  154.7 1.1 collective-permute-done.13
  156.1 1.0 slice.1502
  157.1 1.9 %collective-permute-start.5 = (bf16[4,8,3,256]{3,2,1,0:T(4,128)(2,1)S(1)}, bf16[4,8,3,256]{3,2,1,0:T(4,128)(2,1)S(1)}, u32[]{:S(2)}, u32[]{:S(2)}) collective-permute-start(bf16[4,8,3,256]{3,2,1,0:T(4,128)(2,1)S(1)} %slice.1502), channel_id=1, source_target_pairs={{0,15},{1,14},{2,13},{3,12},{4,11},{5,10},{6,9},{7,8},{8,7},{9,6},... | collective-permute-start | bytes 147464 | tf_op jit(solution)/shard_map/ppermute | solution.py:180
  159.2 4.5 %collective-permute-done.5 = bf16[4,8,3,256]{3,2,1,0:T(4,128)(2,1)S(1)} collective-permute-done((bf16[4,8,3,256]{3,2,1,0:T(4,128)(2,1)S(1)}, bf16[4,8,3,256]{3,2,1,0:T(4,128)(2,1)S(1)}, u32[]{:S(2)}, u32[]{:S(2)}) %collective-permute-start.5) | collective-permute-done | bytes 49184 | tf_op jit(solution)/shard_map/ppermute | solution.py:180
  163.9 0.9 pad_maximum_fusion.8
  164.8 1.3 broadcast_select_fusion.1
  167.4 1.1 fusion.172
  169.4 2.5 %copy.27 = f32[1024,256]{1,0:T(8,128)} copy(f32[1024,256]{0,1:T(8,128)} %fusion.172) | data formatting | bytes 2097152
  171.9 1.0 slice_multiply_fusion.49
  (333 shorter events, 21.2 us)
Async XLA Ops:
  0.6 33.6 %copy-start = (bf16[1024,256]{1,0:T(8,128)(2,1)S(1)}, bf16[1024,256]{1,0:T(8,128)(2,1)}, u32[]{:S(2)}) copy-start(bf16[1024,256]{1,0:T(8,128)(2,1)} %param.23) | copy-start | bytes 1572868
  0.7 21.3 %copy-start.2 = (bf16[4,8,32,256]{3,2,1,0:T(8,128)(2,1)S(1)}, bf16[4,8,32,256]{3,2,1,0:T(8,128)(2,1)}, u32[]{:S(2)}) copy-start(bf16[4,8,32,256]{3,2,1,0:T(8,128)(2,1)} %param.13) | copy-start | bytes 1572868
  0.7 17.9 %copy-start.36 = (s32[8,32]{1,0:T(8,128)S(1)}, s32[8,32]{1,0:T(8,128)}, u32[]{:S(2)}) copy-start(s32[8,32]{1,0:T(8,128)} %param.16) | copy-start | bytes 3076
  1.7 10.2 %collective-permute-start = (bf16[4,8,3,256]{3,2,1,0:T(4,128)(2,1)S(1)}, bf16[4,8,3,256]{3,2,1,0:T(4,128)(2,1)S(1)}, u32[]{:S(2)}, u32[]{:S(2)}) collective-permute-start(bf16[4,8,3,256]{3,2,1,0:T(4,128)(2,1)S(1)} %slice.713), channel_id=1, source_target_pairs={{0,15},{1,14},{2,13},{3,12},{4,11},{5,10},{6,9},{7,8},{8,7},{9,6},... | collective-permute-start | bytes 147464 | tf_op jit(solution)/shard_map/ppermute | solution.py:180
  8.2 14.1 %copy-start.39 = (f32[1,1,256]{2,1,0:T(1,128)}, f32[1,1,256]{2,1,0:T(1,128)S(1)}, u32[]{:S(2)}) copy-start(f32[1,1,256]{2,1,0:T(1,128)S(1)} %get-tuple-element.139) | copy-start | bytes 3076
  8.2 14.1 %copy-start.41 = (f32[1,1,256]{2,1,0:T(1,128)}, f32[1,1,256]{2,1,0:T(1,128)S(1)}, u32[]{:S(2)}) copy-start(f32[1,1,256]{2,1,0:T(1,128)S(1)} %get-tuple-element.140) | copy-start | bytes 3076
  8.2 14.1 %copy-start.43 = (f32[1,1,256]{2,1,0:T(1,128)}, f32[1,1,256]{2,1,0:T(1,128)S(1)}, u32[]{:S(2)}) copy-start(f32[1,1,256]{2,1,0:T(1,128)S(1)} %get-tuple-element.141) | copy-start | bytes 3076
  8.2 14.1 %copy-start.45 = (f32[1,1,256]{2,1,0:T(1,128)}, f32[1,1,256]{2,1,0:T(1,128)S(1)}, u32[]{:S(2)}) copy-start(f32[1,1,256]{2,1,0:T(1,128)S(1)} %get-tuple-element.142) | copy-start | bytes 3076
  8.2 14.1 %copy-start.47 = (f32[1,1,256]{2,1,0:T(1,128)}, f32[1,1,256]{2,1,0:T(1,128)S(1)}, u32[]{:S(2)}) copy-start(f32[1,1,256]{2,1,0:T(1,128)S(1)} %get-tuple-element.143) | copy-start | bytes 3076
  8.2 14.1 %copy-start.49 = (f32[1,1,256]{2,1,0:T(1,128)}, f32[1,1,256]{2,1,0:T(1,128)S(1)}, u32[]{:S(2)}) copy-start(f32[1,1,256]{2,1,0:T(1,128)S(1)} %get-tuple-element.144) | copy-start | bytes 3076
  8.2 14.1 %copy-start.51 = (f32[1,1,256]{2,1,0:T(1,128)}, f32[1,1,256]{2,1,0:T(1,128)S(1)}, u32[]{:S(2)}) copy-start(f32[1,1,256]{2,1,0:T(1,128)S(1)} %get-tuple-element.145) | copy-start | bytes 3076
  8.3 14.1 %copy-start.53 = (f32[1,1,256]{2,1,0:T(1,128)}, f32[1,1,256]{2,1,0:T(1,128)S(1)}, u32[]{:S(2)}) copy-start(f32[1,1,256]{2,1,0:T(1,128)S(1)} %get-tuple-element.146) | copy-start | bytes 3076
  8.3 14.1 %copy-start.55 = (f32[1,1,256]{2,1,0:T(1,128)}, f32[1,1,256]{2,1,0:T(1,128)S(1)}, u32[]{:S(2)}) copy-start(f32[1,1,256]{2,1,0:T(1,128)S(1)} %get-tuple-element.147) | copy-start | bytes 3076
  8.3 14.1 %copy-start.57 = (f32[1,1,256]{2,1,0:T(1,128)}, f32[1,1,256]{2,1,0:T(1,128)S(1)}, u32[]{:S(2)}) copy-start(f32[1,1,256]{2,1,0:T(1,128)S(1)} %get-tuple-element.148) | copy-start | bytes 3076
  8.3 14.1 %copy-start.59 = (f32[1,1,256]{2,1,0:T(1,128)}, f32[1,1,256]{2,1,0:T(1,128)S(1)}, u32[]{:S(2)}) copy-start(f32[1,1,256]{2,1,0:T(1,128)S(1)} %get-tuple-element.149) | copy-start | bytes 3076
  8.3 14.1 %copy-start.61 = (f32[1,1,256]{2,1,0:T(1,128)}, f32[1,1,256]{2,1,0:T(1,128)S(1)}, u32[]{:S(2)}) copy-start(f32[1,1,256]{2,1,0:T(1,128)S(1)} %get-tuple-element.150) | copy-start | bytes 3076
  8.3 14.1 %copy-start.63 = (f32[1,1,256]{2,1,0:T(1,128)}, f32[1,1,256]{2,1,0:T(1,128)S(1)}, u32[]{:S(2)}) copy-start(f32[1,1,256]{2,1,0:T(1,128)S(1)} %get-tuple-element.151) | copy-start | bytes 3076
  8.3 14.1 %copy-start.65 = (f32[1,1,256]{2,1,0:T(1,128)}, f32[1,1,256]{2,1,0:T(1,128)S(1)}, u32[]{:S(2)}) copy-start(f32[1,1,256]{2,1,0:T(1,128)S(1)} %get-tuple-element.152) | copy-start | bytes 3076
  8.3 14.1 %copy-start.67 = (f32[1,1,256]{2,1,0:T(1,128)}, f32[1,1,256]{2,1,0:T(1,128)S(1)}, u32[]{:S(2)}) copy-start(f32[1,1,256]{2,1,0:T(1,128)S(1)} %get-tuple-element.153) | copy-start | bytes 3076
  8.3 14.1 %copy-start.69 = (f32[1,1,256]{2,1,0:T(1,128)}, f32[1,1,256]{2,1,0:T(1,128)S(1)}, u32[]{:S(2)}) copy-start(f32[1,1,256]{2,1,0:T(1,128)S(1)} %get-tuple-element.154) | copy-start | bytes 3076
  8.3 14.1 %copy-start.71 = (f32[1,1,256]{2,1,0:T(1,128)}, f32[1,1,256]{2,1,0:T(1,128)S(1)}, u32[]{:S(2)}) copy-start(f32[1,1,256]{2,1,0:T(1,128)S(1)} %get-tuple-element.155) | copy-start | bytes 3076
  9.4 13.1 %copy-start.73 = (f32[1,1,256]{2,1,0:T(1,128)}, f32[1,1,256]{2,1,0:T(1,128)S(1)}, u32[]{:S(2)}) copy-start(f32[1,1,256]{2,1,0:T(1,128)S(1)} %get-tuple-element.156) | copy-start | bytes 3076
  9.4 13.1 %copy-start.75 = (f32[1,1,256]{2,1,0:T(1,128)}, f32[1,1,256]{2,1,0:T(1,128)S(1)}, u32[]{:S(2)}) copy-start(f32[1,1,256]{2,1,0:T(1,128)S(1)} %get-tuple-element.157) | copy-start | bytes 3076
  9.4 13.1 %copy-start.77 = (f32[1,1,256]{2,1,0:T(1,128)}, f32[1,1,256]{2,1,0:T(1,128)S(1)}, u32[]{:S(2)}) copy-start(f32[1,1,256]{2,1,0:T(1,128)S(1)} %get-tuple-element.158) | copy-start | bytes 3076
  9.4 13.1 %copy-start.79 = (f32[1,1,256]{2,1,0:T(1,128)}, f32[1,1,256]{2,1,0:T(1,128)S(1)}, u32[]{:S(2)}) copy-start(f32[1,1,256]{2,1,0:T(1,128)S(1)} %get-tuple-element.159) | copy-start | bytes 3076
  9.4 13.1 %copy-start.81 = (f32[1,1,256]{2,1,0:T(1,128)}, f32[1,1,256]{2,1,0:T(1,128)S(1)}, u32[]{:S(2)}) copy-start(f32[1,1,256]{2,1,0:T(1,128)S(1)} %get-tuple-element.160) | copy-start | bytes 3076
  9.4 13.1 %copy-start.83 = (f32[1,1,256]{2,1,0:T(1,128)}, f32[1,1,256]{2,1,0:T(1,128)S(1)}, u32[]{:S(2)}) copy-start(f32[1,1,256]{2,1,0:T(1,128)S(1)} %get-tuple-element.161) | copy-start | bytes 3076
  9.5 13.1 %copy-start.85 = (f32[1,1,256]{2,1,0:T(1,128)}, f32[1,1,256]{2,1,0:T(1,128)S(1)}, u32[]{:S(2)}) copy-start(f32[1,1,256]{2,1,0:T(1,128)S(1)} %get-tuple-element.162) | copy-start | bytes 3076
  9.5 13.1 %copy-start.87 = (f32[1,1,256]{2,1,0:T(1,128)}, f32[1,1,256]{2,1,0:T(1,128)S(1)}, u32[]{:S(2)}) copy-start(f32[1,1,256]{2,1,0:T(1,128)S(1)} %get-tuple-element.163) | copy-start | bytes 3076
  9.5 13.1 %copy-start.89 = (f32[1,1,256]{2,1,0:T(1,128)}, f32[1,1,256]{2,1,0:T(1,128)S(1)}, u32[]{:S(2)}) copy-start(f32[1,1,256]{2,1,0:T(1,128)S(1)} %get-tuple-element.164) | copy-start | bytes 3076
  9.5 13.1 %copy-start.91 = (f32[1,1,256]{2,1,0:T(1,128)}, f32[1,1,256]{2,1,0:T(1,128)S(1)}, u32[]{:S(2)}) copy-start(f32[1,1,256]{2,1,0:T(1,128)S(1)} %get-tuple-element.165) | copy-start | bytes 3076
  9.5 13.1 %copy-start.93 = (f32[1,1,256]{2,1,0:T(1,128)}, f32[1,1,256]{2,1,0:T(1,128)S(1)}, u32[]{:S(2)}) copy-start(f32[1,1,256]{2,1,0:T(1,128)S(1)} %get-tuple-element.166) | copy-start | bytes 3076
  9.5 13.1 %copy-start.95 = (f32[1,1,256]{2,1,0:T(1,128)}, f32[1,1,256]{2,1,0:T(1,128)S(1)}, u32[]{:S(2)}) copy-start(f32[1,1,256]{2,1,0:T(1,128)S(1)} %get-tuple-element.167) | copy-start | bytes 3076
  9.5 13.1 %copy-start.97 = (f32[1,1,256]{2,1,0:T(1,128)}, f32[1,1,256]{2,1,0:T(1,128)S(1)}, u32[]{:S(2)}) copy-start(f32[1,1,256]{2,1,0:T(1,128)S(1)} %get-tuple-element.168) | copy-start | bytes 3076
  9.5 13.1 %copy-start.99 = (f32[1,1,256]{2,1,0:T(1,128)}, f32[1,1,256]{2,1,0:T(1,128)S(1)}, u32[]{:S(2)}) copy-start(f32[1,1,256]{2,1,0:T(1,128)S(1)} %get-tuple-element.169) | copy-start | bytes 3076
  9.5 13.1 %copy-start.101 = (f32[1,1,256]{2,1,0:T(1,128)}, f32[1,1,256]{2,1,0:T(1,128)S(1)}, u32[]{:S(2)}) copy-start(f32[1,1,256]{2,1,0:T(1,128)S(1)} %get-tuple-element.170) | copy-start | bytes 3076
  9.5 13.1 %copy-start.103 = (f32[1,1,256]{2,1,0:T(1,128)}, f32[1,1,256]{2,1,0:T(1,128)S(1)}, u32[]{:S(2)}) copy-start(f32[1,1,256]{2,1,0:T(1,128)S(1)} %get-tuple-element.171) | copy-start | bytes 3076
  9.6 13.1 %copy-start.105 = (f32[1,1,256]{2,1,0:T(1,128)}, f32[1,1,256]{2,1,0:T(1,128)S(1)}, u32[]{:S(2)}) copy-start(f32[1,1,256]{2,1,0:T(1,128)S(1)} %get-tuple-element.172) | copy-start | bytes 3076
  9.6 13.1 %copy-start.107 = (f32[1,1,256]{2,1,0:T(1,128)}, f32[1,1,256]{2,1,0:T(1,128)S(1)}, u32[]{:S(2)}) copy-start(f32[1,1,256]{2,1,0:T(1,128)S(1)} %get-tuple-element.173) | copy-start | bytes 3076
  9.6 13.1 %copy-start.109 = (f32[1,1,256]{2,1,0:T(1,128)}, f32[1,1,256]{2,1,0:T(1,128)S(1)}, u32[]{:S(2)}) copy-start(f32[1,1,256]{2,1,0:T(1,128)S(1)} %get-tuple-element.174) | copy-start | bytes 3076
  11.1 11.6 %copy-start.110 = (f32[1,1,256]{2,1,0:T(1,128)}, f32[1,1,256]{2,1,0:T(1,128)S(1)}, u32[]{:S(2)}) copy-start(f32[1,1,256]{2,1,0:T(1,128)S(1)} %get-tuple-element.175) | copy-start | bytes 3076
  11.1 11.6 %copy-start.111 = (f32[1,1,256]{2,1,0:T(1,128)}, f32[1,1,256]{2,1,0:T(1,128)S(1)}, u32[]{:S(2)}) copy-start(f32[1,1,256]{2,1,0:T(1,128)S(1)} %get-tuple-element.176) | copy-start | bytes 3076
  11.1 11.6 %copy-start.112 = (f32[1,1,256]{2,1,0:T(1,128)}, f32[1,1,256]{2,1,0:T(1,128)S(1)}, u32[]{:S(2)}) copy-start(f32[1,1,256]{2,1,0:T(1,128)S(1)} %get-tuple-element.177) | copy-start | bytes 3076
  13.5 8.5 %collective-permute-start.1 = (bf16[4,3,38,256]{3,2,1,0:T(8,128)(2,1)S(1)}, bf16[4,3,38,256]{3,2,1,0:T(8,128)(2,1)S(1)}, u32[]{:S(2)}, u32[]{:S(2)}) collective-permute-start(bf16[4,3,38,256]{3,2,1,0:T(8,128)(2,1)S(1)} %get-tuple-element.120), channel_id=1, source_target_pairs={{0,1},{1,2},{2,3},{3,4},{4,5},{5,6},{6,7},{7,8},{8,9},{9,10},{10,1... | collective-permute-start | bytes 700424 | tf_op jit(solution)/shard_map/ppermute | solution.py:26
  14.2 7.8 %collective-permute-start.2 = (bf16[4,3,38,256]{3,2,1,0:T(8,128)(2,1)S(1)}, bf16[4,3,38,256]{3,2,1,0:T(8,128)(2,1)S(1)}, u32[]{:S(2)}, u32[]{:S(2)}) collective-permute-start(bf16[4,3,38,256]{3,2,1,0:T(8,128)(2,1)S(1)} %get-tuple-element.121), channel_id=1, source_target_pairs={{1,0},{2,1},{3,2},{4,3},{5,4},{6,5},{7,6},{8,7},{9,8},{10,9},{11,1... | collective-permute-start | bytes 700424 | tf_op jit(solution)/shard_map/ppermute | solution.py:27
  33.9 14.1 %copy-start.4 = (f32[256,1024]{1,0:T(8,128)}, f32[256,1024]{1,0:T(8,128)S(1)}, u32[]{:S(2)}) copy-start(f32[256,1024]{1,0:T(8,128)S(1)} %convolution_add_fusion.6) | copy-start | bytes 3145732
  66.7 11.3 %copy-start.19 = (bf16[1,8,32,256]{3,2,1,0:T(8,128)(2,1)S(1)}, bf16[1,8,32,256]{3,2,1,0:T(8,128)(2,1)}, u32[]{:S(2)}) copy-start(bf16[1,8,32,256]{3,2,1,0:T(8,128)(2,1)} %copy-done.18) | copy-start | bytes 393220
  82.3 10.0 %collective-permute-start.3 = (f32[4,3,32,256]{3,2,1,0:T(8,128)S(1)}, f32[4,3,32,256]{3,2,1,0:T(8,128)S(1)}, u32[]{:S(2)}, u32[]{:S(2)}) collective-permute-start(f32[4,3,32,256]{3,2,1,0:T(8,128)S(1)} %copy-done.31), channel_id=1, source_target_pairs={{0,1},{1,2},{2,3},{3,4},{4,5},{5,6},{6,7},{7,8},{8,9},{9,10},{10,1... | collective-permute-start | bytes 1179656 | tf_op jit(solution)/shard_map/ppermute | solution.py:26
  82.9 9.4 %collective-permute-start.4 = (f32[4,3,32,256]{3,2,1,0:T(8,128)S(1)}, f32[4,3,32,256]{3,2,1,0:T(8,128)S(1)}, u32[]{:S(2)}, u32[]{:S(2)}) collective-permute-start(f32[4,3,32,256]{3,2,1,0:T(8,128)S(1)} %copy-done.30), channel_id=1, source_target_pairs={{1,0},{2,1},{3,2},{4,3},{5,4},{6,5},{7,6},{8,7},{9,8},{10,9},{11,1... | collective-permute-start | bytes 1179656 | tf_op jit(solution)/shard_map/ppermute | solution.py:27
  93.1 10.3 %copy-start.8 = (f32[8,32,256]{2,1,0:T(8,128)S(1)}, f32[8,32,256]{2,1,0:T(8,128)}, u32[]{:S(2)}) copy-start(f32[8,32,256]{2,1,0:T(8,128)} %copy-done.7) | copy-start | bytes 786436
  93.1 10.3 %copy-start.21 = (f32[256,256]{1,0:T(8,128)S(1)}, f32[256,256]{1,0:T(8,128)}, u32[]{:S(2)}) copy-start(f32[256,256]{1,0:T(8,128)} %copy-done.20) | copy-start | bytes 786436
  93.1 10.3 %copy-start.23 = (f32[256,256]{1,0:T(8,128)S(1)}, f32[256,256]{1,0:T(8,128)}, u32[]{:S(2)}) copy-start(f32[256,256]{1,0:T(8,128)} %copy-done.22) | copy-start | bytes 786436
  107.6 4.7 %collective-permute-start.6 = (f32[528,512]{1,0:T(8,128)}, f32[528,512]{1,0:T(8,128)}, u32[]{:S(2)}, u32[]{:S(2)}) collective-permute-start(f32[528,512]{1,0:T(8,128)} %constant_dynamic-slice_fusion.4), channel_id=1, source_target_pairs={{0,1},{1,0},{2,3},{3,2},{4,5},{5,4},{6,7},{7,6},{8,9},{9,8},{10,11... | collective-permute-start | bytes 3244040 | tf_op jit(solution)/shard_map/ppermute | solution.py:226
  116.0 14.6 %collective-permute-start.7 = (f32[528,128]{1,0:T(8,128)S(1)}, f32[528,128]{1,0:T(8,128)S(1)}, u32[]{:S(2)}, u32[]{:S(2)}) collective-permute-start(f32[528,128]{1,0:T(8,128)S(1)} %get-tuple-element.111), channel_id=1, source_target_pairs={{0,2},{1,3},{2,0},{3,1},{4,6},{5,7},{6,4},{7,5},{8,10},{9,11},{10,... | collective-permute-start | bytes 811016 | tf_op jit(solution)/shard_map/ppermute | solution.py:226
  116.3 14.3 %collective-permute-start.9 = (f32[528,128]{1,0:T(8,128)S(1)}, f32[528,128]{1,0:T(8,128)S(1)}, u32[]{:S(2)}, u32[]{:S(2)}) collective-permute-start(f32[528,128]{1,0:T(8,128)S(1)} %get-tuple-element.112), channel_id=1, source_target_pairs={{0,6},{1,7},{2,4},{3,5},{4,2},{5,3},{6,0},{7,1},{8,14},{9,15},{10,... | collective-permute-start | bytes 811016 | tf_op jit(solution)/shard_map/ppermute | solution.py:226
  116.3 15.6 %collective-permute-start.8 = (f32[528,128]{1,0:T(8,128)S(1)}, f32[528,128]{1,0:T(8,128)S(1)}, u32[]{:S(2)}, u32[]{:S(2)}) collective-permute-start(f32[528,128]{1,0:T(8,128)S(1)} %get-tuple-element.113), channel_id=1, source_target_pairs={{0,4},{1,5},{2,6},{3,7},{4,0},{5,1},{6,2},{7,3},{8,12},{9,13},{10,... | collective-permute-start | bytes 811016 | tf_op jit(solution)/shard_map/ppermute | solution.py:226
  132.9 7.8 %collective-permute-start.10 = (f32[264,128]{1,0:T(8,128)S(1)}, f32[264,128]{1,0:T(8,128)S(1)}, u32[]{:S(2)}, u32[]{:S(2)}) collective-permute-start(f32[264,128]{1,0:T(8,128)S(1)} %constant_dynamic-slice_fusion), channel_id=1, source_target_pairs={{0,8},{1,9},{2,10},{3,11},{4,12},{5,13},{6,14},{7,15},{8,0},{9,1},... | collective-permute-start | bytes 405512 | tf_op jit(solution)/shard_map/ppermute | solution.py:226
  140.8 6.4 %collective-permute-start.11 = (bf16[264,128]{1,0:T(8,128)(2,1)S(1)}, bf16[264,128]{1,0:T(8,128)(2,1)S(1)}, u32[]{:S(2)}, u32[]{:S(2)}) collective-permute-start(bf16[264,128]{1,0:T(8,128)(2,1)S(1)} %add_convert_fusion.1), channel_id=1, source_target_pairs={{0,8},{1,9},{2,10},{3,11},{4,12},{5,13},{6,14},{7,15},{8,0},{9,1},... | collective-permute-start | bytes 202760 | tf_op jit(solution)/shard_map/ppermute | solution.py:234
  147.2 11.9 %copy-start.6 = (f32[4,8,32,256]{3,2,1,0:T(8,128)S(1)}, f32[4,8,32,256]{3,2,1,0:T(8,128)}, u32[]{:S(2)}) copy-start(f32[4,8,32,256]{3,2,1,0:T(8,128)} %get-tuple-element.115) | copy-start | bytes 3145732
  147.2 7.5 %collective-permute-start.14 = (bf16[528,128]{1,0:T(8,128)(2,1)S(1)}, bf16[528,128]{1,0:T(8,128)(2,1)S(1)}, u32[]{:S(2)}, u32[]{:S(2)}) collective-permute-start(bf16[528,128]{1,0:T(8,128)(2,1)S(1)} %pad_maximum_fusion.12), channel_id=1, source_target_pairs={{0,6},{1,7},{2,4},{3,5},{4,2},{5,3},{6,0},{7,1},{8,14},{9,15},{10,... | collective-permute-start | bytes 405512 | tf_op jit(solution)/shard_map/ppermute | solution.py:234
  147.3 8.5 %collective-permute-start.13 = (bf16[528,128]{1,0:T(8,128)(2,1)S(1)}, bf16[528,128]{1,0:T(8,128)(2,1)S(1)}, u32[]{:S(2)}, u32[]{:S(2)}) collective-permute-start(bf16[528,128]{1,0:T(8,128)(2,1)S(1)} %pad_maximum_fusion.12), channel_id=1, source_target_pairs={{0,2},{1,3},{2,0},{3,1},{4,6},{5,7},{6,4},{7,5},{8,10},{9,11},{10,... | collective-permute-start | bytes 405512 | tf_op jit(solution)/shard_map/ppermute | solution.py:234
  148.0 7.8 %collective-permute-start.12 = (bf16[528,128]{1,0:T(8,128)(2,1)S(1)}, bf16[528,128]{1,0:T(8,128)(2,1)S(1)}, u32[]{:S(2)}, u32[]{:S(2)}) collective-permute-start(bf16[528,128]{1,0:T(8,128)(2,1)S(1)} %pad_maximum_fusion.12), channel_id=1, source_target_pairs={{0,4},{1,5},{2,6},{3,7},{4,0},{5,1},{6,2},{7,3},{8,12},{9,13},{10,... | collective-permute-start | bytes 405512 | tf_op jit(solution)/shard_map/ppermute | solution.py:234
  156.1 8.7 %collective-permute-start.15 = (bf16[528,512]{1,0:T(8,128)(2,1)S(1)}, bf16[528,512]{1,0:T(8,128)(2,1)}, u32[]{:S(2)}, u32[]{:S(2)}) collective-permute-start(bf16[528,512]{1,0:T(8,128)(2,1)S(1)} %pad_maximum_fusion.5), channel_id=1, source_target_pairs={{0,1},{1,0},{2,3},{3,2},{4,5},{5,4},{6,7},{7,6},{8,9},{9,8},{10,11... | collective-permute-start | bytes 1622024 | tf_op jit(solution)/shard_map/ppermute | solution.py:234
  157.1 6.5 %collective-permute-start.5 = (bf16[4,8,3,256]{3,2,1,0:T(4,128)(2,1)S(1)}, bf16[4,8,3,256]{3,2,1,0:T(4,128)(2,1)S(1)}, u32[]{:S(2)}, u32[]{:S(2)}) collective-permute-start(bf16[4,8,3,256]{3,2,1,0:T(4,128)(2,1)S(1)} %slice.1502), channel_id=1, source_target_pairs={{0,15},{1,14},{2,13},{3,12},{4,11},{5,10},{6,9},{7,8},{8,7},{9,6},... | collective-permute-start | bytes 147464 | tf_op jit(solution)/shard_map/ppermute | solution.py:180
  (82 other events, 332.7 us)

commit v9 on v8

--- a/solution.py
+++ b/solution.py
@@ -106,7 +106,7 @@
     grad_pred = jnp.stack(grad_list)
     grad_scale = jnp.sum(grad_pred * branch, axis=(0, 1, 2))
     grad_b_out = jnp.zeros((chans,), jnp.float32)
-    grad_w_out = jnp.zeros(w_out.shape[::-1], jnp.float32)
+    grad_w_out = jnp.zeros(w_out.shape, jnp.float32)
     grad_b_in = jnp.zeros(b_in.shape, jnp.float32)
     grad_w_in = jnp.zeros(w_in.shape, jnp.float32)
     normed_grads = []
@@ -117,7 +117,7 @@
         grad_b_out = grad_b_out + jnp.sum(grad_out, axis=0)
         out_half = grad_out.astype(jnp.bfloat16)
         grad_w_out = grad_w_out + lax.dot_general(
-            out_half, hiddens[member], contract_rows, preferred_element_type=jnp.float32
+            hiddens[member], out_half, contract_rows, preferred_element_type=jnp.float32
         )
         grad_hidden = lax.dot_general(
             out_half, w_out, contract_cols, preferred_element_type=jnp.float32
@@ -321,11 +321,15 @@
     lon_size = lax.axis_size("lon")
     small = (kernel_sum, dw_bias_sum, gain_sum, bias_sum, b_in_sum, b_out_sum, scale_sum)
     width = w_in_sum.shape[1]
-    big_rows = w_in_sum.shape[0] + w_out_sum.shape[0]
+    big_rows = (w_in_sum.size + w_out_sum.size) // width
     small_rows = -(-sum(a.size for a in small) // width)
     small_rows += -(big_rows + small_rows) % lon_size
     block = jnp.concatenate(
-        [w_in_sum, w_out_sum, pack(small, small_rows * width).reshape(small_rows, width)]
+        [
+            w_in_sum,
+            w_out_sum.reshape(-1, width),
+            pack(small, small_rows * width).reshape(small_rows, width),
+        ]
     )
     block = radix_allreduce(block, "lon", jnp.bfloat16)
     small_tot = unpack(block[big_rows:].reshape(-1), small)
@@ -336,7 +340,7 @@
         small_tot[3],
         block[: w_in_sum.shape[0]],
         small_tot[4],
-        block[w_in_sum.shape[0] : big_rows].T,
+        block[w_in_sum.shape[0] : big_rows].reshape(w_out_sum.shape),
         small_tot[5],
         small_tot[6],
     )

time: 174 us -> 179 us (1.029)
  local copies, waits for them, and re-layouts: 26.1 us -> 32.6 us
  other arithmetic: 53 us -> 57.2 us
  waiting for transfers between devices: 44 us -> 39.8 us
  starting transfers between devices: 26.3 us -> 23.3 us
    ppermute x2, waiting for transfers between devices: 6.09 us -> 2.61 us  [with_halo(): before = lax.ppermute(last, axis, up)]
    unnamed x5, other arithmetic: 0.03 us -> 3.19 us
    ppermute x5, starting transfers between devices: 6.29 us -> 3.61 us  [radix_allreduce(): lax.ppermute(send, axis, [(i, i ^ d << low) for i in range(size)])]
    mul x0 -> x1, local copies, waits for them, and re-layouts: none -> 2.49 us  [on_device(): totals[6] * factor]
    dot_general x4, matrix products: 4.69 us -> 7.06 us  [local_step(): lax.dot_general(normed[member].reshape(rows, chans), pre_half, contract_r...]
    unnamed x272 -> x255, local copies, waits for them, and re-layouts: 9.03 us -> 9.78 us
  transfers between devices with their start and end apart: 16 -> 16, of which waited for: 10 -> 10; matrix products, arithmetic and copies ran while one was open for 5% -> 11% of each run, Pallas kernels for 0% -> 0%
where the time goes in v9:
time: 179 us; the launch traced here: 178 us
  other arithmetic  57.2 us (32%)
  waiting for transfers between devices  39.8 us (22%)
  local copies, waits for them, and re-layouts  32.6 us (18%)
  starting transfers between devices  23.3 us (13%)
  matrix products  22.2 us (12%)
  between operations  2.67 us (1%)
    ppermute x5, waiting for transfers between devices, radix_allreduce(): lax.ppermute(send, axis, [(i, i ^ d << low) for i in range(size)])  22.6 us
    reduce_sum x4, other arithmetic, local_step(): jnp.sum(grad_depth * extended[:, lon_off:lon_off + lon_dev, lat_off:lat_o...  10.6 us
    add x1, other arithmetic, on_device(): grad_ext + dw_kernel[lon_off, lat_off] * padded[:, 6 - lon_off:6 - lon_of...  10.2 us
    unnamed x255, local copies, waits for them, and re-layouts  9.78 us
    ppermute x5, waiting for transfers between devices, radix_allreduce(): lax.ppermute(cur, axis, [(i, i ^ d << low) for i in range(size)])  9.65 us
    reduce_sum x1, other arithmetic, local_step(): mean_val = jnp.mean(depth, axis=-1, keepdims=True)  9.35 us
    ppermute x2, starting transfers between devices, with_halo(): after = lax.ppermute(leading, axis, down)  7.62 us
    dot_general x4, matrix products, local_step(): lax.dot_general(normed[member].reshape(rows, chans), pre_half, contract_r...  7.06 us
  transfers between devices with their start and end apart: 16, of which 10 were waited for; matrix products, arithmetic and copies ran while one was open for 11% of the time, Pallas kernels for 0%

profile of v9, /device:TPU:0, one launch (start us, length us, event | category | flops | bytes accessed | tf_op | source)
XLA Modules:
  0.0 177.8 jit_solution(7777271739681795528)
XLA Ops:
  0.7 1.0 slice.713
  1.7 5.5 %collective-permute-start = (bf16[4,8,3,256]{3,2,1,0:T(4,128)(2,1)S(1)}, bf16[4,8,3,256]{3,2,1,0:T(4,128)(2,1)S(1)}, u32[]{:S(2)}, u32[]{:S(2)}) collective-permute-start(bf16[4,8,3,256]{3,2,1,0:T(4,128)(2,1)S(1)} %slice.713), channel_id=1, source_target_pairs={{0,15},{1,14},{2,13},{3,12},{4,11},{5,10},{6,9},{7,8},{8,7},{9,6},... | collective-permute-start | bytes 147464 | tf_op jit(solution)/shard_map/ppermute | solution.py:180
  7.2 1.0 fusion.211
  8.4 1.0 fusion.212
  9.6 1.5 fusion.213
  12.2 1.3 pad_maximum_fusion.11
  14.2 3.8 %collective-permute-start.2 = (bf16[4,3,38,256]{3,2,1,0:T(8,128)(2,1)S(1)}, bf16[4,3,38,256]{3,2,1,0:T(8,128)(2,1)S(1)}, u32[]{:S(2)}, u32[]{:S(2)}) collective-permute-start(bf16[4,3,38,256]{3,2,1,0:T(8,128)(2,1)S(1)} %get-tuple-element.109), channel_id=1, source_target_pairs={{1,0},{2,1},{3,2},{4,3},{5,4},{6,5},{7,6},{8,7},{9,8},{10,9},{11,1... | collective-permute-start | bytes 700424 | tf_op jit(solution)/shard_map/ppermute | solution.py:27
  19.3 2.6 %collective-permute-done.1 = bf16[4,3,38,256]{3,2,1,0:T(8,128)(2,1)S(1)} collective-permute-done((bf16[4,3,38,256]{3,2,1,0:T(8,128)(2,1)S(1)}, bf16[4,3,38,256]{3,2,1,0:T(8,128)(2,1)S(1)}, u32[]{:S(2)}, u32[]{:S(2)}) %collective-permute-start.1) | collective-permute-done | bytes 233504 | tf_op jit(solution)/shard_map/ppermute | solution.py:26
  22.7 9.4 %fusion.207 = (f32[4,8,32]{2,1,0:T(8,128)S(1)}, f32[4,8,32,256]{3,2,1,0:T(8,128)S(1)}) fusion(bf16[4,11,38,256]{3,2,1,0:T(8,128)(2,1)S(1)} %get-tuple-element.107, f32[256]{0:T(256)} %bitcast.48, f32[256]{0:T(256)} %bitcast.47, f32[256]{0:T(256)S(1)} %bitcast.338, f32[256]{0:T(256)S(1)} %bitcast.340, f32[256]{0:T(256)S(1)} %bitcast.342, ...), kind=kLoop, calls=%fused_computation.495 | loop fusion | flops 43514880 | bytes 23746560 | tf_op jit(solution)/shard_map/reduce_sum | solution.py:62
  37.1 1.1 fusion.205
  38.1 3.8 %multiply_reduce_fusion.7 = (f32[256]{0:T(256)}, f32[256]{0:T(256)}, f32[256]{0:T(256)}, f32[256]{0:T(256)}, f32[8,32,256]{2,1,0:T(8,128)S(1)}, /*index=5*/f32[8...) fusion(f32[256]{0:T(256)S(1)} %copy-done.30, ...), kind=kLoop, calls=%fused_computation.430 | loop fusion | flops 7863296 | bytes 2497536 | tf_op jit(solution)/shard_map/reduce_sum | solution.py:117
  42.1 1.5 fusion.199
  44.1 1.5 fusion.197
  45.6 0.9 fusion.217
  46.5 1.5 fusion.201
  48.0 1.5 fusion.203
  49.5 0.9 fusion.214
  50.5 0.9 fusion.215
  51.4 0.9 fusion.216
  52.3 1.0 multiply_reduce_fusion.1
  53.3 4.1 %fusion.145 = (f32[256]{0:T(256)}, f32[256]{0:T(256)}, f32[256]{0:T(256)}, f32[256]{0:T(256)}, f32[256]{0:T(256)}, /*index=5*/f32[256]{0:T(256)}, f32[256]{0:T(2...) fusion(bf16[4,11,38,256]{3,2,1,0:T(8,128)(2,1)S(1)} %get-tuple-, ...), kind=kLoop, calls=%fused_computation.322 | loop fusion | flops 16772608 | bytes 12618752 | tf_op jit(solution)/shard_map/reduce_sum | solution.py:154
  57.4 2.3 %fusion.127 = (f32[256]{0:T(256)}, f32[256]{0:T(256)}, f32[256]{0:T(256)}, f32[256]{0:T(256)}, f32[256]{0:T(256)}, /*index=5*/f32[256]{0:T(256)}, f32[256]{0:T(2...) fusion(f32[4,8,32,256]{3,2,1,0:T(8,128)S(1)} %get-tuple-element.91, ...), kind=kLoop, calls=%fused_computation.304 | loop fusion | flops 12842240 | bytes 3255296 | tf_op jit(solution)/shard_map/reduce_sum | solution.py:154
  59.7 1.0 fusion.76
  60.7 3.2 %fusion.94 = (f32[256]{0:T(256)}, f32[256]{0:T(256)}, f32[256]{0:T(256)}, f32[256]{0:T(256)}, f32[256]{0:T(256)}, /*index=5*/f32[256]{0:T(256)}, f32[256]{0:T(25...) fusion(f32[4,8,32,256]{3,2,1,0:T(8,128)S(1)} %get-tuple-element, ...), kind=kLoop, calls=%fused_computation.271 | loop fusion | flops 14151168 | bytes 10504192 | tf_op jit(solution)/shard_map/reduce_sum | solution.py:154
  63.9 1.3 fusion.185
  65.2 1.0 fusion.209
  77.2 1.4 reshape.152
  78.6 1.8 convolution_add_fusion.5
  80.6 1.3 convolution_add_fusion.4
  82.5 3.9 %collective-permute-start.4 = (f32[4,3,32,256]{3,2,1,0:T(8,128)}, f32[4,3,32,256]{3,2,1,0:T(8,128)}, u32[]{:S(2)}, u32[]{:S(2)}) collective-permute-start(f32[4,3,32,256]{3,2,1,0:T(8,128)} %get-tuple-element.105), channel_id=1, source_target_pairs={{1,0},{2,1},{3,2},{4,3},{5,4},{6,5},{7,6},{8,7},{9,8},{10,9},{11,1... | collective-permute-start | bytes 1179656 | tf_op jit(solution)/shard_map/ppermute | solution.py:27
  86.3 1.4 constant_dynamic-update-slice_fusion.7
  87.8 1.3 constant_dynamic-update-slice_fusion.13
  89.1 1.3 constant_dynamic-update-slice_fusion.12
  90.4 1.3 constant_dynamic-update-slice_fusion.11
  92.3 1.3 constant_dynamic-update-slice_fusion.9
  93.6 1.3 reshape.151
  94.9 2.7 %convolution_add_fusion.3 = f32[256,1024]{1,0:T(8,128)} fusion(f32[256,1024]{1,0:T(8,128)} %convolution_add_fusion.4, bf16[256,256]{1,0:T(8,128)(2,1)S(1)} %bitcast.313, bf16[256,1024]{1,0:T(8,128)(2,1)} %copy-done.7), kind=kOutput, calls=%fused_computation.20 | convolution fusion | flops 134479872 | bytes 2752512 | tf_op jit(solution)/shard_map/dot_general | solution.py:128
  97.9 1.5 select_maximum_fusion
  99.8 10.2 %fusion.1 = f32[4,8,38,256]{3,2,1,0:T(8,128)S(1)} fusion(f32[4,14,44,256]{3,2,1,0:T(8,128)S(1)} %select_maximum_fusion, f32[256]{0:T(256)} %bitcast.48, f32[256]{0:T(256)} %bitcast.47, f32[256]{0:T(256)S(1)} %bitcast.339, f32[256]{0:T(256)S(1)} %bitcast.341, f32[256]{0:T(256)S(1)} %bitcast.343, f32[256]{0:T(256)S(1)} %bitcast.345, f32[256]{0:T(256)S(1)} %bitcast.347, ...), kind=kLoop, calls=%fused_computation.124 | loop fusion | flops 30195712 | bytes 62309376 | tf_op jit(solution)/shard_map/add | solution.py:296
  110.1 1.3 multiply_reduce_fusion
  111.5 1.3 constant_dynamic-update-slice_fusion.8
  112.7 0.8 pad.9
  113.6 1.7 pad_maximum_fusion
  115.3 1.1 constant_dynamic-slice_fusion.4
  116.4 3.0 %collective-permute-done.6 = f32[528,512]{1,0:T(8,128)} collective-permute-done((f32[528,512]{1,0:T(8,128)}, f32[528,512]{1,0:T(8,128)}, u32[]{:S(2)}, u32[]{:S(2)}) %collective-permute-start.6) | collective-permute-done | bytes 1081376 | tf_op jit(solution)/shard_map/ppermute | solution.py:226
  119.4 2.4 %dynamic-slice_add_fusion = f32[528,512]{1,0:T(8,128)} fusion(f32[528,512]{1,0:T(8,128)} %collective-permute-done.6, f32[528,1024]{1,0:T(8,128)S(1)} %pad_maximum_fusion, s32[]{:T(128)S(6)} %select_n.117), kind=kLoop, calls=%fused_computation.225 | loop fusion | flops 270336 | bytes 3244036 | tf_op jit(solution)/shard_map/add | solution.py:226
  121.8 1.2 constant_dynamic-slice_fusion.3
  123.2 3.4 %collective-permute-start.8 = (f32[528,128]{1,0:T(8,128)S(1)}, f32[528,128]{1,0:T(8,128)S(1)}, u32[]{:S(2)}, u32[]{:S(2)}) collective-permute-start(f32[528,128]{1,0:T(8,128)S(1)} %get-tuple-element.101), channel_id=1, source_target_pairs={{0,4},{1,5},{2,6},{3,7},{4,0},{5,1},{6,2},{7,3},{8,12},{9,13},{10,... | collective-permute-start | bytes 811016 | tf_op jit(solution)/shard_map/ppermute | solution.py:226
  126.6 10.8 %collective-permute-done.7 = f32[528,128]{1,0:T(8,128)S(1)} collective-permute-done((f32[528,128]{1,0:T(8,128)S(1)}, f32[528,128]{1,0:T(8,128)S(1)}, u32[]{:S(2)}, u32[]{:S(2)}) %collective-permute-start.7) | collective-permute-done | bytes 270368 | tf_op jit(solution)/shard_map/ppermute | solution.py:226
  137.4 1.2 collective-permute-done.8
  138.6 1.0 add_add_fusion
  139.8 7.5 %collective-permute-done.10 = f32[264,128]{1,0:T(8,128)S(1)} collective-permute-done((f32[264,128]{1,0:T(8,128)S(1)}, f32[264,128]{1,0:T(8,128)S(1)}, u32[]{:S(2)}, u32[]{:S(2)}) %collective-permute-start.10) | collective-permute-done | bytes 135200 | tf_op jit(solution)/shard_map/ppermute | solution.py:226
  147.4 5.2 %collective-permute-done.11 = bf16[264,128]{1,0:T(8,128)(2,1)S(1)} collective-permute-done((bf16[264,128]{1,0:T(8,128)(2,1)S(1)}, bf16[264,128]{1,0:T(8,128)(2,1)S(1)}, u32[]{:S(2)}, u32[]{:S(2)}) %collective-permute-start.11) | collective-permute-done | bytes 67616 | tf_op jit(solution)/shard_map/ppermute | solution.py:234
  152.7 1.4 collective-permute-start.13
  154.1 2.1 %collective-permute-start.12 = (bf16[528,128]{1,0:T(8,128)(2,1)S(1)}, bf16[528,128]{1,0:T(8,128)(2,1)S(1)}, u32[]{:S(2)}, u32[]{:S(2)}) collective-permute-start(bf16[528,128]{1,0:T(8,128)(2,1)S(1)} %pad_maximum_fusion.12), channel_id=1, source_target_pairs={{0,4},{1,5},{2,6},{3,7},{4,0},{5,1},{6,2},{7,3},{8,12},{9,13},{10,... | collective-permute-start | bytes 405512 | tf_op jit(solution)/shard_map/ppermute | solution.py:234
  156.2 3.2 %collective-permute-done.14 = bf16[528,128]{1,0:T(8,128)(2,1)S(1)} collective-permute-done((bf16[528,128]{1,0:T(8,128)(2,1)S(1)}, bf16[528,128]{1,0:T(8,128)(2,1)S(1)}, u32[]{:S(2)}, u32[]{:S(2)}) %collective-permute-start.14) | collective-permute-done | bytes 135200 | tf_op jit(solution)/shard_map/ppermute | solution.py:234
  161.0 1.0 slice.1502
  162.0 1.6 collective-permute-start.5
  163.6 4.9 %collective-permute-done.5 = bf16[4,8,3,256]{3,2,1,0:T(4,128)(2,1)S(1)} collective-permute-done((bf16[4,8,3,256]{3,2,1,0:T(4,128)(2,1)S(1)}, bf16[4,8,3,256]{3,2,1,0:T(4,128)(2,1)S(1)}, u32[]{:S(2)}, u32[]{:S(2)}) %collective-permute-start.5) | collective-permute-done | bytes 49184 | tf_op jit(solution)/shard_map/ppermute | solution.py:180
  168.8 0.9 pad_maximum_fusion.8
  169.7 1.3 broadcast_select_fusion.1
  172.2 1.1 convert_multiply_fusion.98
  174.2 2.5 %mul.1873 = f32[1024,256]{1,0:T(8,128)} reshape(f32[256,1024]{1,0:T(8,128)} %convert_multiply_fusion.98) | data formatting | bytes 2097152 | tf_op jit(solution)/shard_map/mul | solution.py:358
  176.7 1.0 slice_multiply_fusion.49
  (318 shorter events, 26.0 us)
Async XLA Ops:
  0.6 33.6 %copy-start = (bf16[1024,256]{1,0:T(8,128)(2,1)S(1)}, bf16[1024,256]{1,0:T(8,128)(2,1)}, u32[]{:S(2)}) copy-start(bf16[1024,256]{1,0:T(8,128)(2,1)} %param.23) | copy-start | bytes 1572868
  0.7 21.3 %copy-start.2 = (bf16[4,8,32,256]{3,2,1,0:T(8,128)(2,1)S(1)}, bf16[4,8,32,256]{3,2,1,0:T(8,128)(2,1)}, u32[]{:S(2)}) copy-start(bf16[4,8,32,256]{3,2,1,0:T(8,128)(2,1)} %param.13) | copy-start | bytes 1572868
  0.7 17.9 %copy-start.28 = (s32[8,32]{1,0:T(8,128)S(1)}, s32[8,32]{1,0:T(8,128)}, u32[]{:S(2)}) copy-start(s32[8,32]{1,0:T(8,128)} %param.16) | copy-start | bytes 3076
  1.7 10.2 %collective-permute-start = (bf16[4,8,3,256]{3,2,1,0:T(4,128)(2,1)S(1)}, bf16[4,8,3,256]{3,2,1,0:T(4,128)(2,1)S(1)}, u32[]{:S(2)}, u32[]{:S(2)}) collective-permute-start(bf16[4,8,3,256]{3,2,1,0:T(4,128)(2,1)S(1)} %slice.713), channel_id=1, source_target_pairs={{0,15},{1,14},{2,13},{3,12},{4,11},{5,10},{6,9},{7,8},{8,7},{9,6},... | collective-permute-start | bytes 147464 | tf_op jit(solution)/shard_map/ppermute | solution.py:180
  8.2 14.1 %copy-start.31 = (f32[1,1,256]{2,1,0:T(1,128)}, f32[1,1,256]{2,1,0:T(1,128)S(1)}, u32[]{:S(2)}) copy-start(f32[1,1,256]{2,1,0:T(1,128)S(1)} %get-tuple-element.127) | copy-start | bytes 3076
  8.2 14.1 %copy-start.33 = (f32[1,1,256]{2,1,0:T(1,128)}, f32[1,1,256]{2,1,0:T(1,128)S(1)}, u32[]{:S(2)}) copy-start(f32[1,1,256]{2,1,0:T(1,128)S(1)} %get-tuple-element.128) | copy-start | bytes 3076
  8.2 14.1 %copy-start.35 = (f32[1,1,256]{2,1,0:T(1,128)}, f32[1,1,256]{2,1,0:T(1,128)S(1)}, u32[]{:S(2)}) copy-start(f32[1,1,256]{2,1,0:T(1,128)S(1)} %get-tuple-element.129) | copy-start | bytes 3076
  8.2 14.1 %copy-start.37 = (f32[1,1,256]{2,1,0:T(1,128)}, f32[1,1,256]{2,1,0:T(1,128)S(1)}, u32[]{:S(2)}) copy-start(f32[1,1,256]{2,1,0:T(1,128)S(1)} %get-tuple-element.130) | copy-start | bytes 3076
  8.2 14.1 %copy-start.39 = (f32[1,1,256]{2,1,0:T(1,128)}, f32[1,1,256]{2,1,0:T(1,128)S(1)}, u32[]{:S(2)}) copy-start(f32[1,1,256]{2,1,0:T(1,128)S(1)} %get-tuple-element.131) | copy-start | bytes 3076
  8.2 14.1 %copy-start.41 = (f32[1,1,256]{2,1,0:T(1,128)}, f32[1,1,256]{2,1,0:T(1,128)S(1)}, u32[]{:S(2)}) copy-start(f32[1,1,256]{2,1,0:T(1,128)S(1)} %get-tuple-element.132) | copy-start | bytes 3076
  8.2 14.1 %copy-start.43 = (f32[1,1,256]{2,1,0:T(1,128)}, f32[1,1,256]{2,1,0:T(1,128)S(1)}, u32[]{:S(2)}) copy-start(f32[1,1,256]{2,1,0:T(1,128)S(1)} %get-tuple-element.133) | copy-start | bytes 3076
  8.3 14.1 %copy-start.45 = (f32[1,1,256]{2,1,0:T(1,128)}, f32[1,1,256]{2,1,0:T(1,128)S(1)}, u32[]{:S(2)}) copy-start(f32[1,1,256]{2,1,0:T(1,128)S(1)} %get-tuple-element.134) | copy-start | bytes 3076
  8.3 14.1 %copy-start.47 = (f32[1,1,256]{2,1,0:T(1,128)}, f32[1,1,256]{2,1,0:T(1,128)S(1)}, u32[]{:S(2)}) copy-start(f32[1,1,256]{2,1,0:T(1,128)S(1)} %get-tuple-element.135) | copy-start | bytes 3076
  8.3 14.1 %copy-start.49 = (f32[1,1,256]{2,1,0:T(1,128)}, f32[1,1,256]{2,1,0:T(1,128)S(1)}, u32[]{:S(2)}) copy-start(f32[1,1,256]{2,1,0:T(1,128)S(1)} %get-tuple-element.136) | copy-start | bytes 3076
  8.3 14.1 %copy-start.51 = (f32[1,1,256]{2,1,0:T(1,128)}, f32[1,1,256]{2,1,0:T(1,128)S(1)}, u32[]{:S(2)}) copy-start(f32[1,1,256]{2,1,0:T(1,128)S(1)} %get-tuple-element.137) | copy-start | bytes 3076
  8.3 14.1 %copy-start.53 = (f32[1,1,256]{2,1,0:T(1,128)}, f32[1,1,256]{2,1,0:T(1,128)S(1)}, u32[]{:S(2)}) copy-start(f32[1,1,256]{2,1,0:T(1,128)S(1)} %get-tuple-element.138) | copy-start | bytes 3076
  8.3 14.1 %copy-start.55 = (f32[1,1,256]{2,1,0:T(1,128)}, f32[1,1,256]{2,1,0:T(1,128)S(1)}, u32[]{:S(2)}) copy-start(f32[1,1,256]{2,1,0:T(1,128)S(1)} %get-tuple-element.139) | copy-start | bytes 3076
  8.3 14.1 %copy-start.57 = (f32[1,1,256]{2,1,0:T(1,128)}, f32[1,1,256]{2,1,0:T(1,128)S(1)}, u32[]{:S(2)}) copy-start(f32[1,1,256]{2,1,0:T(1,128)S(1)} %get-tuple-element.140) | copy-start | bytes 3076
  8.3 14.1 %copy-start.59 = (f32[1,1,256]{2,1,0:T(1,128)}, f32[1,1,256]{2,1,0:T(1,128)S(1)}, u32[]{:S(2)}) copy-start(f32[1,1,256]{2,1,0:T(1,128)S(1)} %get-tuple-element.141) | copy-start | bytes 3076
  8.3 14.1 %copy-start.61 = (f32[1,1,256]{2,1,0:T(1,128)}, f32[1,1,256]{2,1,0:T(1,128)S(1)}, u32[]{:S(2)}) copy-start(f32[1,1,256]{2,1,0:T(1,128)S(1)} %get-tuple-element.142) | copy-start | bytes 3076
  8.3 14.1 %copy-start.63 = (f32[1,1,256]{2,1,0:T(1,128)}, f32[1,1,256]{2,1,0:T(1,128)S(1)}, u32[]{:S(2)}) copy-start(f32[1,1,256]{2,1,0:T(1,128)S(1)} %get-tuple-element.143) | copy-start | bytes 3076
  9.4 13.1 %copy-start.65 = (f32[1,1,256]{2,1,0:T(1,128)}, f32[1,1,256]{2,1,0:T(1,128)S(1)}, u32[]{:S(2)}) copy-start(f32[1,1,256]{2,1,0:T(1,128)S(1)} %get-tuple-element.144) | copy-start | bytes 3076
  9.4 13.1 %copy-start.67 = (f32[1,1,256]{2,1,0:T(1,128)}, f32[1,1,256]{2,1,0:T(1,128)S(1)}, u32[]{:S(2)}) copy-start(f32[1,1,256]{2,1,0:T(1,128)S(1)} %get-tuple-element.145) | copy-start | bytes 3076
  9.4 13.1 %copy-start.69 = (f32[1,1,256]{2,1,0:T(1,128)}, f32[1,1,256]{2,1,0:T(1,128)S(1)}, u32[]{:S(2)}) copy-start(f32[1,1,256]{2,1,0:T(1,128)S(1)} %get-tuple-element.146) | copy-start | bytes 3076
  9.4 13.1 %copy-start.71 = (f32[1,1,256]{2,1,0:T(1,128)}, f32[1,1,256]{2,1,0:T(1,128)S(1)}, u32[]{:S(2)}) copy-start(f32[1,1,256]{2,1,0:T(1,128)S(1)} %get-tuple-element.147) | copy-start | bytes 3076
  9.4 13.1 %copy-start.73 = (f32[1,1,256]{2,1,0:T(1,128)}, f32[1,1,256]{2,1,0:T(1,128)S(1)}, u32[]{:S(2)}) copy-start(f32[1,1,256]{2,1,0:T(1,128)S(1)} %get-tuple-element.148) | copy-start | bytes 3076
  9.4 13.1 %copy-start.75 = (f32[1,1,256]{2,1,0:T(1,128)}, f32[1,1,256]{2,1,0:T(1,128)S(1)}, u32[]{:S(2)}) copy-start(f32[1,1,256]{2,1,0:T(1,128)S(1)} %get-tuple-element.149) | copy-start | bytes 3076
  9.4 13.1 %copy-start.77 = (f32[1,1,256]{2,1,0:T(1,128)}, f32[1,1,256]{2,1,0:T(1,128)S(1)}, u32[]{:S(2)}) copy-start(f32[1,1,256]{2,1,0:T(1,128)S(1)} %get-tuple-element.150) | copy-start | bytes 3076
  9.5 13.1 %copy-start.79 = (f32[1,1,256]{2,1,0:T(1,128)}, f32[1,1,256]{2,1,0:T(1,128)S(1)}, u32[]{:S(2)}) copy-start(f32[1,1,256]{2,1,0:T(1,128)S(1)} %get-tuple-element.151) | copy-start | bytes 3076
  9.5 13.1 %copy-start.81 = (f32[1,1,256]{2,1,0:T(1,128)}, f32[1,1,256]{2,1,0:T(1,128)S(1)}, u32[]{:S(2)}) copy-start(f32[1,1,256]{2,1,0:T(1,128)S(1)} %get-tuple-element.152) | copy-start | bytes 3076
  9.5 13.1 %copy-start.83 = (f32[1,1,256]{2,1,0:T(1,128)}, f32[1,1,256]{2,1,0:T(1,128)S(1)}, u32[]{:S(2)}) copy-start(f32[1,1,256]{2,1,0:T(1,128)S(1)} %get-tuple-element.153) | copy-start | bytes 3076
  9.5 13.1 %copy-start.85 = (f32[1,1,256]{2,1,0:T(1,128)}, f32[1,1,256]{2,1,0:T(1,128)S(1)}, u32[]{:S(2)}) copy-start(f32[1,1,256]{2,1,0:T(1,128)S(1)} %get-tuple-element.154) | copy-start | bytes 3076
  9.5 13.1 %copy-start.87 = (f32[1,1,256]{2,1,0:T(1,128)}, f32[1,1,256]{2,1,0:T(1,128)S(1)}, u32[]{:S(2)}) copy-start(f32[1,1,256]{2,1,0:T(1,128)S(1)} %get-tuple-element.155) | copy-start | bytes 3076
  9.5 13.1 %copy-start.89 = (f32[1,1,256]{2,1,0:T(1,128)}, f32[1,1,256]{2,1,0:T(1,128)S(1)}, u32[]{:S(2)}) copy-start(f32[1,1,256]{2,1,0:T(1,128)S(1)} %get-tuple-element.156) | copy-start | bytes 3076
  9.5 13.1 %copy-start.91 = (f32[1,1,256]{2,1,0:T(1,128)}, f32[1,1,256]{2,1,0:T(1,128)S(1)}, u32[]{:S(2)}) copy-start(f32[1,1,256]{2,1,0:T(1,128)S(1)} %get-tuple-element.157) | copy-start | bytes 3076
  9.5 13.1 %copy-start.93 = (f32[1,1,256]{2,1,0:T(1,128)}, f32[1,1,256]{2,1,0:T(1,128)S(1)}, u32[]{:S(2)}) copy-start(f32[1,1,256]{2,1,0:T(1,128)S(1)} %get-tuple-element.158) | copy-start | bytes 3076
  9.5 13.1 %copy-start.95 = (f32[1,1,256]{2,1,0:T(1,128)}, f32[1,1,256]{2,1,0:T(1,128)S(1)}, u32[]{:S(2)}) copy-start(f32[1,1,256]{2,1,0:T(1,128)S(1)} %get-tuple-element.159) | copy-start | bytes 3076
  9.5 13.1 %copy-start.97 = (f32[1,1,256]{2,1,0:T(1,128)}, f32[1,1,256]{2,1,0:T(1,128)S(1)}, u32[]{:S(2)}) copy-start(f32[1,1,256]{2,1,0:T(1,128)S(1)} %get-tuple-element.160) | copy-start | bytes 3076
  9.6 13.1 %copy-start.99 = (f32[1,1,256]{2,1,0:T(1,128)}, f32[1,1,256]{2,1,0:T(1,128)S(1)}, u32[]{:S(2)}) copy-start(f32[1,1,256]{2,1,0:T(1,128)S(1)} %get-tuple-element.161) | copy-start | bytes 3076
  9.6 13.1 %copy-start.101 = (f32[1,1,256]{2,1,0:T(1,128)}, f32[1,1,256]{2,1,0:T(1,128)S(1)}, u32[]{:S(2)}) copy-start(f32[1,1,256]{2,1,0:T(1,128)S(1)} %get-tuple-element.162) | copy-start | bytes 3076
  11.1 11.6 %copy-start.102 = (f32[1,1,256]{2,1,0:T(1,128)}, f32[1,1,256]{2,1,0:T(1,128)S(1)}, u32[]{:S(2)}) copy-start(f32[1,1,256]{2,1,0:T(1,128)S(1)} %get-tuple-element.163) | copy-start | bytes 3076
  11.1 11.6 %copy-start.103 = (f32[1,1,256]{2,1,0:T(1,128)}, f32[1,1,256]{2,1,0:T(1,128)S(1)}, u32[]{:S(2)}) copy-start(f32[1,1,256]{2,1,0:T(1,128)S(1)} %get-tuple-element.164) | copy-start | bytes 3076
  11.1 11.6 %copy-start.104 = (f32[1,1,256]{2,1,0:T(1,128)}, f32[1,1,256]{2,1,0:T(1,128)S(1)}, u32[]{:S(2)}) copy-start(f32[1,1,256]{2,1,0:T(1,128)S(1)} %get-tuple-element.165) | copy-start | bytes 3076
  13.5 8.5 %collective-permute-start.1 = (bf16[4,3,38,256]{3,2,1,0:T(8,128)(2,1)S(1)}, bf16[4,3,38,256]{3,2,1,0:T(8,128)(2,1)S(1)}, u32[]{:S(2)}, u32[]{:S(2)}) collective-permute-start(bf16[4,3,38,256]{3,2,1,0:T(8,128)(2,1)S(1)} %get-tuple-element.108), channel_id=1, source_target_pairs={{0,1},{1,2},{2,3},{3,4},{4,5},{5,6},{6,7},{7,8},{8,9},{9,10},{10,1... | collective-permute-start | bytes 700424 | tf_op jit(solution)/shard_map/ppermute | solution.py:26
  14.2 7.8 %collective-permute-start.2 = (bf16[4,3,38,256]{3,2,1,0:T(8,128)(2,1)S(1)}, bf16[4,3,38,256]{3,2,1,0:T(8,128)(2,1)S(1)}, u32[]{:S(2)}, u32[]{:S(2)}) collective-permute-start(bf16[4,3,38,256]{3,2,1,0:T(8,128)(2,1)S(1)} %get-tuple-element.109), channel_id=1, source_target_pairs={{1,0},{2,1},{3,2},{4,3},{5,4},{6,5},{7,6},{8,7},{9,8},{10,9},{11,1... | collective-permute-start | bytes 700424 | tf_op jit(solution)/shard_map/ppermute | solution.py:27
  67.3 11.3 %copy-start.16 = (bf16[1,8,32,256]{3,2,1,0:T(8,128)(2,1)S(1)}, bf16[1,8,32,256]{3,2,1,0:T(8,128)(2,1)}, u32[]{:S(2)}) copy-start(bf16[1,8,32,256]{3,2,1,0:T(8,128)(2,1)} %copy-done.15) | copy-start | bytes 393220
  80.5 11.8 %copy-start.106 = (f32[256]{0:T(256)S(1)}, f32[256]{0:T(256)}, u32[]{:S(2)}) copy-start(f32[256]{0:T(256)} %get-tuple-element.75) | copy-start | bytes 3076
  80.5 11.8 %copy-start.107 = (f32[256]{0:T(256)S(1)}, f32[256]{0:T(256)}, u32[]{:S(2)}) copy-start(f32[256]{0:T(256)} %get-tuple-element.76) | copy-start | bytes 3076
  80.6 11.8 %copy-start.108 = (f32[256]{0:T(256)S(1)}, f32[256]{0:T(256)}, u32[]{:S(2)}) copy-start(f32[256]{0:T(256)} %get-tuple-element.77) | copy-start | bytes 3076
  80.6 11.7 %copy-start.109 = (f32[256]{0:T(256)S(1)}, f32[256]{0:T(256)}, u32[]{:S(2)}) copy-start(f32[256]{0:T(256)} %get-tuple-element.78) | copy-start | bytes 3076
  81.9 13.0 %copy-start.12 = (bf16[1,8,32,256]{3,2,1,0:T(8,128)(2,1)S(1)}, bf16[1,8,32,256]{3,2,1,0:T(8,128)(2,1)}, u32[]{:S(2)}) copy-start(bf16[1,8,32,256]{3,2,1,0:T(8,128)(2,1)} %copy-done.11) | copy-start | bytes 393220
  81.9 16.0 %collective-permute-start.3 = (f32[4,3,32,256]{3,2,1,0:T(8,128)}, f32[4,3,32,256]{3,2,1,0:T(8,128)}, u32[]{:S(2)}, u32[]{:S(2)}) collective-permute-start(f32[4,3,32,256]{3,2,1,0:T(8,128)} %get-tuple-element.104), channel_id=1, source_target_pairs={{0,1},{1,2},{2,3},{3,4},{4,5},{5,6},{6,7},{7,8},{8,9},{9,10},{10,1... | collective-permute-start | bytes 1179656 | tf_op jit(solution)/shard_map/ppermute | solution.py:26
  82.5 15.4 %collective-permute-start.4 = (f32[4,3,32,256]{3,2,1,0:T(8,128)}, f32[4,3,32,256]{3,2,1,0:T(8,128)}, u32[]{:S(2)}, u32[]{:S(2)}) collective-permute-start(f32[4,3,32,256]{3,2,1,0:T(8,128)} %get-tuple-element.105), channel_id=1, source_target_pairs={{1,0},{2,1},{3,2},{4,3},{5,4},{6,5},{7,6},{8,7},{9,8},{10,9},{11,1... | collective-permute-start | bytes 1179656 | tf_op jit(solution)/shard_map/ppermute | solution.py:27
  116.4 3.0 %collective-permute-start.6 = (f32[528,512]{1,0:T(8,128)}, f32[528,512]{1,0:T(8,128)}, u32[]{:S(2)}, u32[]{:S(2)}) collective-permute-start(f32[528,512]{1,0:T(8,128)} %constant_dynamic-slice_fusion.4), channel_id=1, source_target_pairs={{0,1},{1,0},{2,3},{3,2},{4,5},{5,4},{6,7},{7,6},{8,9},{9,8},{10,11... | collective-permute-start | bytes 3244040 | tf_op jit(solution)/shard_map/ppermute | solution.py:226
  123.0 14.4 %collective-permute-start.7 = (f32[528,128]{1,0:T(8,128)S(1)}, f32[528,128]{1,0:T(8,128)S(1)}, u32[]{:S(2)}, u32[]{:S(2)}) collective-permute-start(f32[528,128]{1,0:T(8,128)S(1)} %get-tuple-element.99), channel_id=1, source_target_pairs={{0,2},{1,3},{2,0},{3,1},{4,6},{5,7},{6,4},{7,5},{8,10},{9,11},{10,... | collective-permute-start | bytes 811016 | tf_op jit(solution)/shard_map/ppermute | solution.py:226
  123.1 14.3 %collective-permute-start.9 = (f32[528,128]{1,0:T(8,128)S(1)}, f32[528,128]{1,0:T(8,128)S(1)}, u32[]{:S(2)}, u32[]{:S(2)}) collective-permute-start(f32[528,128]{1,0:T(8,128)S(1)} %get-tuple-element.100), channel_id=1, source_target_pairs={{0,6},{1,7},{2,4},{3,5},{4,2},{5,3},{6,0},{7,1},{8,14},{9,15},{10,... | collective-permute-start | bytes 811016 | tf_op jit(solution)/shard_map/ppermute | solution.py:226
  123.2 15.4 %collective-permute-start.8 = (f32[528,128]{1,0:T(8,128)S(1)}, f32[528,128]{1,0:T(8,128)S(1)}, u32[]{:S(2)}, u32[]{:S(2)}) collective-permute-start(f32[528,128]{1,0:T(8,128)S(1)} %get-tuple-element.101), channel_id=1, source_target_pairs={{0,4},{1,5},{2,6},{3,7},{4,0},{5,1},{6,2},{7,3},{8,12},{9,13},{10,... | collective-permute-start | bytes 811016 | tf_op jit(solution)/shard_map/ppermute | solution.py:226
  139.7 7.6 %collective-permute-start.10 = (f32[264,128]{1,0:T(8,128)S(1)}, f32[264,128]{1,0:T(8,128)S(1)}, u32[]{:S(2)}, u32[]{:S(2)}) collective-permute-start(f32[264,128]{1,0:T(8,128)S(1)} %constant_dynamic-slice_fusion), channel_id=1, source_target_pairs={{0,8},{1,9},{2,10},{3,11},{4,12},{5,13},{6,14},{7,15},{8,0},{9,1},... | collective-permute-start | bytes 405512 | tf_op jit(solution)/shard_map/ppermute | solution.py:226
  147.3 5.3 %collective-permute-start.11 = (bf16[264,128]{1,0:T(8,128)(2,1)S(1)}, bf16[264,128]{1,0:T(8,128)(2,1)S(1)}, u32[]{:S(2)}, u32[]{:S(2)}) collective-permute-start(bf16[264,128]{1,0:T(8,128)(2,1)S(1)} %add_convert_fusion.1), channel_id=1, source_target_pairs={{0,8},{1,9},{2,10},{3,11},{4,12},{5,13},{6,14},{7,15},{8,0},{9,1},... | collective-permute-start | bytes 202760 | tf_op jit(solution)/shard_map/ppermute | solution.py:234
  152.6 6.8 %collective-permute-start.14 = (bf16[528,128]{1,0:T(8,128)(2,1)S(1)}, bf16[528,128]{1,0:T(8,128)(2,1)S(1)}, u32[]{:S(2)}, u32[]{:S(2)}) collective-permute-start(bf16[528,128]{1,0:T(8,128)(2,1)S(1)} %pad_maximum_fusion.12), channel_id=1, source_target_pairs={{0,6},{1,7},{2,4},{3,5},{4,2},{5,3},{6,0},{7,1},{8,14},{9,15},{10,... | collective-permute-start | bytes 405512 | tf_op jit(solution)/shard_map/ppermute | solution.py:234
  152.7 7.2 %collective-permute-start.13 = (bf16[528,128]{1,0:T(8,128)(2,1)S(1)}, bf16[528,128]{1,0:T(8,128)(2,1)S(1)}, u32[]{:S(2)}, u32[]{:S(2)}) collective-permute-start(bf16[528,128]{1,0:T(8,128)(2,1)S(1)} %pad_maximum_fusion.12), channel_id=1, source_target_pairs={{0,2},{1,3},{2,0},{3,1},{4,6},{5,7},{6,4},{7,5},{8,10},{9,11},{10,... | collective-permute-start | bytes 405512 | tf_op jit(solution)/shard_map/ppermute | solution.py:234
  154.1 6.5 %collective-permute-start.12 = (bf16[528,128]{1,0:T(8,128)(2,1)S(1)}, bf16[528,128]{1,0:T(8,128)(2,1)S(1)}, u32[]{:S(2)}, u32[]{:S(2)}) collective-permute-start(bf16[528,128]{1,0:T(8,128)(2,1)S(1)} %pad_maximum_fusion.12), channel_id=1, source_target_pairs={{0,4},{1,5},{2,6},{3,7},{4,0},{5,1},{6,2},{7,3},{8,12},{9,13},{10,... | collective-permute-start | bytes 405512 | tf_op jit(solution)/shard_map/ppermute | solution.py:234
  160.9 8.7 %collective-permute-start.15 = (bf16[528,512]{1,0:T(8,128)(2,1)S(1)}, bf16[528,512]{1,0:T(8,128)(2,1)}, u32[]{:S(2)}, u32[]{:S(2)}) collective-permute-start(bf16[528,512]{1,0:T(8,128)(2,1)S(1)} %pad_maximum_fusion.5), channel_id=1, source_target_pairs={{0,1},{1,0},{2,3},{3,2},{4,5},{5,4},{6,7},{7,6},{8,9},{9,8},{10,11... | collective-permute-start | bytes 1622024 | tf_op jit(solution)/shard_map/ppermute | solution.py:234
  162.0 6.5 %collective-permute-start.5 = (bf16[4,8,3,256]{3,2,1,0:T(4,128)(2,1)S(1)}, bf16[4,8,3,256]{3,2,1,0:T(4,128)(2,1)S(1)}, u32[]{:S(2)}, u32[]{:S(2)}) collective-permute-start(bf16[4,8,3,256]{3,2,1,0:T(4,128)(2,1)S(1)} %slice.1502), channel_id=1, source_target_pairs={{0,15},{1,14},{2,13},{3,12},{4,11},{5,10},{6,9},{7,8},{8,7},{9,6},... | collective-permute-start | bytes 147464 | tf_op jit(solution)/shard_map/ppermute | solution.py:180
  (74 other events, 286.2 us)

commit v10 on v6

--- a/solution.py
+++ b/solution.py
@@ -208,7 +208,7 @@
     return cur.astype(flat.dtype)
 
 
-def radix_allreduce(flat, axis, gather_dtype):
+def radix_allreduce(flat, axis, gather_dtype, operand, work):
     size = lax.axis_size(axis)
     nbits = size.bit_length() - 1
     groups = [[0]] + [list(range(b, min(b + 2, nbits))) for b in range(1, nbits, 2)]
@@ -223,6 +223,11 @@
             send = lax.dynamic_slice_in_dim(cur, (sub ^ d) * part, part)
             total = total + lax.ppermute(send, axis, [(i, i ^ (d << low)) for i in range(size)])
         cur = total
+        if bits == groups[0]:
+            cur, operand = lax.optimization_barrier((cur, operand))
+            result = work(operand)
+        elif bits == groups[1]:
+            cur, result = lax.optimization_barrier((cur, result))
     cur = cur.astype(gather_dtype)
     for bits in reversed(groups):
         radix, low = 1 << len(bits), bits[0]
@@ -238,7 +243,7 @@
                 pick = jnp.where(sub == s, pieces[p ^ s], pick)
             placed.append(pick)
         cur = jnp.concatenate(placed)
-    return cur.astype(flat.dtype)
+    return cur.astype(flat.dtype), result
 
 
 def butterfly_allreduce(flat, axis):
@@ -286,24 +291,23 @@
     )
     grad_halo = with_halo(grad_depth, (("lon", 1),), 3)
     padded = jnp.pad(grad_halo, ((0, 0), (0, 0), (6, 6), (0, 0)))
-    grad_ext = jnp.zeros((members, lon_dev, lat_rows + 6, chans), jnp.float32)
-    for lon_off in range(7):
-        for lat_off in range(7):
-            grad_ext = (
-                grad_ext
-                + dw_kernel[lon_off, lat_off]
-                * padded[
-                    :,
-                    6 - lon_off : 6 - lon_off + lon_dev,
-                    6 - lat_off : 6 - lat_off + lat_rows + 6,
-                    :,
-                ]
-            )
-    back_rows = mirror_grads(grad_ext[:, :, lat_rows + 3 :, :])
-    inner = grad_pred + grad_ext[:, :, 3 : lat_rows + 3, :]
-    grad_features = jnp.concatenate(
-        [inner[:, :, : lat_rows - 3, :], inner[:, :, lat_rows - 3 :, :] + back_rows], axis=2
-    ).astype(jnp.bfloat16)
+
+    def backward_conv(operand):
+        grad_ext = jnp.zeros((members, lon_dev, lat_rows + 6, chans), jnp.float32)
+        for lon_off in range(7):
+            for lat_off in range(7):
+                grad_ext = (
+                    grad_ext
+                    + dw_kernel[lon_off, lat_off]
+                    * operand[
+                        :,
+                        6 - lon_off : 6 - lon_off + lon_dev,
+                        6 - lat_off : 6 - lat_off + lat_rows + 6,
+                        :,
+                    ]
+                )
+        return grad_ext
+
     (
         kernel_sum,
         dw_bias_sum,
@@ -327,7 +331,15 @@
         b_out_sum,
         scale_sum,
     )
-    totals = unpack(radix_allreduce(pack(sums, lon_size * 1024), "lon", jnp.bfloat16), sums)
+    reduced, grad_ext = radix_allreduce(
+        pack(sums, lon_size * 1024), "lon", jnp.bfloat16, padded, backward_conv
+    )
+    totals = unpack(reduced, sums)
+    back_rows = mirror_grads(grad_ext[:, :, lat_rows + 3 :, :])
+    inner = grad_pred + grad_ext[:, :, 3 : lat_rows + 3, :]
+    grad_features = jnp.concatenate(
+        [inner[:, :, : lat_rows - 3, :], inner[:, :, lat_rows - 3 :, :] + back_rows], axis=2
+    ).astype(jnp.bfloat16)
     factor = 1.0 / math.sqrt(members * lat_rows * lon_dev * lax.axis_size("lon"))
     return (
         predicted,

time: 159 us -> 154 us (0.969)
  waiting for transfers between devices: 40.6 us -> 28.8 us
  local copies, waits for them, and re-layouts: 25 us -> 29.3 us
  matrix products: 16.3 us -> 18.8 us
    ppermute x5, waiting for transfers between devices: 23.3 us -> 9.36 us  [radix_allreduce(): lax.ppermute(send, axis, [(i, i ^ d << low) for i in range(size)])]
    ppermute x2, waiting for transfers between devices: 3.83 us -> 9.6 us  [with_halo(): before = lax.ppermute(last, axis, up)]
    another operation x7, local copies, waits for them, and re-layouts: 0.2 us -> 5.09 us  [local_step(): kernel_rows.append(jnp.stack(kernel_cols))]
    ppermute x2, waiting for transfers between devices: 4.47 us -> 0.01 us  [mirrored(): return lax.ppermute(x, axis, [(i, size - 1 - i) for i in range(size)])]
    unnamed x4, other arithmetic: 3.19 us -> 0.02 us
    unnamed x294 -> x278, local copies, waits for them, and re-layouts: 13.6 us -> 10.5 us
    dot_general x4, matrix products: 1.28 us -> 3.7 us  [local_step(): lax.dot_general(normed[member].reshape(rows, chans), pre_half, contract_r...]
    ppermute x5, starting transfers between devices: 3.61 us -> 5.87 us  [radix_allreduce(): lax.ppermute(send, axis, [(i, i ^ d << low) for i in range(size)])]
  transfers between devices with their start and end apart: 16 -> 16, of which waited for: 11 -> 8; matrix products, arithmetic and copies ran while one was open for 11% -> 15% of each run, Pallas kernels for 0% -> 0%
where the time goes in v10:
time: 154 us; the launch traced here: 153 us
  other arithmetic  48.8 us (32%)
  local copies, waits for them, and re-layouts  29.3 us (19%)
  waiting for transfers between devices  28.8 us (19%)
  starting transfers between devices  24.3 us (16%)
  matrix products  18.8 us (12%)
  between operations  2.82 us (2%)
    reduce_sum x4, other arithmetic, local_step(): jnp.sum(grad_depth * extended[:, lon_off:lon_off + lon_dev, lat_off:lat_o...  10.6 us
    unnamed x278, local copies, waits for them, and re-layouts  10.5 us
    add x1, other arithmetic, backward_conv(): grad_ext + dw_kernel[lon_off, lat_off] * operand[:, 6 - lon_off:6 - lon_o...  10.2 us
    ppermute x5, waiting for transfers between devices, radix_allreduce(): lax.ppermute(cur, axis, [(i, i ^ d << low) for i in range(size)])  9.79 us
    ppermute x2, waiting for transfers between devices, with_halo(): before = lax.ppermute(last, axis, up)  9.6 us
    ppermute x5, waiting for transfers between devices, radix_allreduce(): lax.ppermute(send, axis, [(i, i ^ d << low) for i in range(size)])  9.36 us
    reduce_sum x1, other arithmetic, local_step(): mean_val = jnp.mean(depth, axis=-1, keepdims=True)  9.35 us
    ppermute x2, starting transfers between devices, with_halo(): after = lax.ppermute(leading, axis, down)  8.21 us
  transfers between devices with their start and end apart: 16, of which 8 were waited for; matrix products, arithmetic and copies ran while one was open for 15% of the time, Pallas kernels for 0%

profile of v10, /device:TPU:0, one launch (start us, length us, event | category | flops | bytes accessed | tf_op | source)
XLA Modules:
  0.0 152.9 jit_solution(10859558060050414892)
XLA Ops:
  0.7 1.0 slice.720
  1.7 5.5 %collective-permute-start = (bf16[4,8,3,256]{3,2,1,0:T(4,128)(2,1)S(1)}, bf16[4,8,3,256]{3,2,1,0:T(4,128)(2,1)S(1)}, u32[]{:S(2)}, u32[]{:S(2)}) collective-permute-start(bf16[4,8,3,256]{3,2,1,0:T(4,128)(2,1)S(1)} %slice.720), channel_id=1, source_target_pairs={{0,15},{1,14},{2,13},{3,12},{4,11},{5,10},{6,9},{7,8},{8,7},{9,6},... | collective-permute-start | bytes 147464 | tf_op jit(solution)/shard_map/ppermute | solution.py:180
  7.2 1.0 fusion.167
  8.4 1.0 fusion.168
  9.6 1.5 fusion.169
  11.1 0.8 copy.25
  12.2 1.3 pad_maximum_fusion.11
  13.5 0.7 collective-permute-start.1
  14.2 3.8 %collective-permute-start.2 = (bf16[4,3,38,256]{3,2,1,0:T(8,128)(2,1)S(1)}, bf16[4,3,38,256]{3,2,1,0:T(8,128)(2,1)S(1)}, u32[]{:S(2)}, u32[]{:S(2)}) collective-permute-start(bf16[4,3,38,256]{3,2,1,0:T(8,128)(2,1)S(1)} %get-tuple-element.120), channel_id=1, source_target_pairs={{1,0},{2,1},{3,2},{4,3},{5,4},{6,5},{7,6},{8,7},{9,8},{10,9},{11,1... | collective-permute-start | bytes 700424 | tf_op jit(solution)/shard_map/ppermute | solution.py:27
  18.1 3.8 %collective-permute-done.1 = bf16[4,3,38,256]{3,2,1,0:T(8,128)(2,1)S(1)} collective-permute-done((bf16[4,3,38,256]{3,2,1,0:T(8,128)(2,1)S(1)}, bf16[4,3,38,256]{3,2,1,0:T(8,128)(2,1)S(1)}, u32[]{:S(2)}, u32[]{:S(2)}) %collective-permute-start.1) | collective-permute-done | bytes 233504 | tf_op jit(solution)/shard_map/ppermute | solution.py:26
  22.7 9.3 %fusion.162 = (f32[4,8,32]{2,1,0:T(8,128)S(1)}, f32[4,8,32,256]{3,2,1,0:T(8,128)S(1)}) fusion(bf16[4,11,38,256]{3,2,1,0:T(8,128)(2,1)S(1)} %get-tuple-element.118, f32[256]{0:T(256)} %bitcast.48, f32[256]{0:T(256)} %bitcast.47, f32[256]{0:T(256)S(1)} %bitcast.344, f32[256]{0:T(256)S(1)} %bitcast.346, f32[256]{0:T(256)S(1)} %bitcast.348, ...), kind=kLoop, calls=%fused_computation.399 | loop fusion | flops 43514880 | bytes 23746560 | tf_op jit(solution)/shard_map/reduce_sum | solution.py:62
  37.1 1.1 fusion.160
  38.1 3.1 %multiply_reduce_fusion.7 = (f32[256]{0:T(256)}, f32[256]{0:T(256)}, f32[256]{0:T(256)}, f32[256]{0:T(256)}, f32[8,32,256]{2,1,0:T(8,128)S(1)}, /*index=5*/f32[8...) fusion(f32[256]{0:T(256)S(1)} %copy-done.36, ...), kind=kLoop, calls=%fused_computation.337 | loop fusion | flops 7863296 | bytes 2497536 | tf_op jit(solution)/shard_map/reduce_sum | solution.py:117
  41.3 1.5 fusion.154
  43.4 1.5 fusion.152
  44.9 0.9 fusion.173
  45.9 1.5 fusion.156
  47.3 1.5 fusion.158
  48.8 0.9 fusion.170
  49.8 0.9 fusion.171
  50.7 0.9 fusion.172
  51.6 1.0 multiply_reduce_fusion.1
  52.6 4.1 %fusion.100 = (f32[256]{0:T(256)}, f32[256]{0:T(256)}, f32[256]{0:T(256)}, f32[256]{0:T(256)}, f32[256]{0:T(256)}, /*index=5*/f32[256]{0:T(256)}, f32[256]{0:T(2...) fusion(bf16[4,11,38,256]{3,2,1,0:T(8,128)(2,1)S(1)} %get-tuple-, ...), kind=kLoop, calls=%fused_computation.228 | loop fusion | flops 16772608 | bytes 12618752 | tf_op jit(solution)/shard_map/reduce_sum | solution.py:154
  56.6 2.4 %fusion.82 = (f32[256]{0:T(256)}, f32[256]{0:T(256)}, f32[256]{0:T(256)}, f32[256]{0:T(256)}, f32[256]{0:T(256)}, /*index=5*/f32[256]{0:T(256)}, f32[256]{0:T(25...) fusion(f32[4,8,32,256]{3,2,1,0:T(8,128)S(1)} %get-tuple-element.99, ...), kind=kLoop, calls=%fused_computation.210 | loop fusion | flops 12842240 | bytes 3255296 | tf_op jit(solution)/shard_map/reduce_sum | solution.py:154
  59.0 1.0 fusion.31
  60.0 3.2 %fusion.49 = (f32[256]{0:T(256)}, f32[256]{0:T(256)}, f32[256]{0:T(256)}, f32[256]{0:T(256)}, f32[256]{0:T(256)}, /*index=5*/f32[256]{0:T(256)}, f32[256]{0:T(25...) fusion(f32[4,8,32,256]{3,2,1,0:T(8,128)S(1)} %get-tuple-element, ...), kind=kLoop, calls=%fused_computation.177 | loop fusion | flops 14151168 | bytes 10504192 | tf_op jit(solution)/shard_map/reduce_sum | solution.py:154
  63.2 1.3 fusion.140
  66.8 0.7 stack.227
  68.2 0.7 stack.236
  69.5 0.7 stack.245
  70.8 0.7 stack.254
  72.1 0.7 stack.263
  73.5 0.7 stack.272
  74.8 0.7 stack.281
  76.1 1.4 reshape.151
  77.6 1.8 %convolution_add_fusion.5 = f32[256,1024]{1,0:T(8,128)S(1)} fusion(f32[256,1024]{1,0:T(8,128)} %fusion.140, bf16[256,256]{1,0:T(8,128)(2,1)S(1)} %bitcast.325, bf16[256,1024]{1,0:T(8,128)(2,1)} %copy-done.9), kind=kOutput, calls=%fused_computation.25 | convolution fusion | flops 134479872 | bytes 2752512 | tf_op jit(solution)/shard_map/dot_general | solution.py:128
  81.0 1.0 copy-done.3
  83.9 1.3 pad_dynamic-slice_fusion
  86.1 0.9 fusion.165
  87.0 4.4 %collective-permute-start.5 = (f32[4,3,32,256]{3,2,1,0:T(8,128)}, f32[4,3,32,256]{3,2,1,0:T(8,128)S(1)}, u32[]{:S(2)}, u32[]{:S(2)}) collective-permute-start(f32[4,3,32,256]{3,2,1,0:T(8,128)} %get-tuple-element.116), channel_id=1, source_target_pairs={{1,0},{2,1},{3,2},{4,3},{5,4},{6,5},{7,6},{8,7},{9,8},{10,9},{11,1... | collective-permute-start | bytes 1179656 | tf_op jit(solution)/shard_map/ppermute | solution.py:27
  91.5 5.8 %collective-permute-done.4 = f32[4,3,32,256]{3,2,1,0:T(8,128)S(1)} collective-permute-done((f32[4,3,32,256]{3,2,1,0:T(8,128)}, f32[4,3,32,256]{3,2,1,0:T(8,128)S(1)}, u32[]{:S(2)}, u32[]{:S(2)}) %collective-permute-start.4) | collective-permute-done | bytes 393248 | tf_op jit(solution)/shard_map/ppermute | solution.py:26
  97.7 1.4 fusion.3
  99.6 1.4 collective-permute-start.6
  100.9 2.2 %collective-permute-start.7 = (f32[67584]{0:T(1024)S(1)}, f32[67584]{0:T(1024)S(1)}, u32[]{:S(2)}, u32[]{:S(2)}) collective-permute-start(f32[67584]{0:T(1024)S(1)} %get-tuple-element.114), channel_id=1, source_target_pairs={{0,4},{1,5},{2,6},{3,7},{4,0},{5,1},{6,2},{7,3},{8,12},{9,13},{10,... | collective-permute-start | bytes 811016 | tf_op jit(solution)/shard_map/ppermute | solution.py:224
  103.5 10.2 %multiply_add_fusion = f32[4,8,38,256]{3,2,1,0:T(8,128)S(1)} fusion(f32[4,14,44,256]{3,2,1,0:T(8,128)S(1)} %select_maximum_fusion, f32[256]{0:T(256)} %bitcast.48, f32[256]{0:T(256)} %bitcast.47, f32[256]{0:T(256)S(1)} %bitcast.345, f32[256]{0:T(256)S(1)} %bitcast.347, f32[256]{0:T(256)S(1)} %bitcast.349, f32[256]{0:T(256)S(1)} %bitcast.351, ...), kind=kLoop, calls=%fused_computation.126 | loop fusion | flops 30195712 | bytes 62309376 | tf_op jit(solution)/shard_map/add | solution.py:300
  113.7 0.7 collective-permute-done.6
  114.4 1.7 %collective-permute-done.7 = f32[67584]{0:T(1024)S(1)} collective-permute-done((f32[67584]{0:T(1024)S(1)}, f32[67584]{0:T(1024)S(1)}, u32[]{:S(2)}, u32[]{:S(2)}) %collective-permute-start.7) | collective-permute-done | bytes 270368 | tf_op jit(solution)/shard_map/ppermute | solution.py:224
  116.2 1.7 %collective-permute-start.10 = (f32[33792]{0:T(1024)S(1)}, f32[33792]{0:T(1024)S(1)}, u32[]{:S(2)}, u32[]{:S(2)}) collective-permute-start(f32[33792]{0:T(1024)S(1)} %dynamic_slice.31), channel_id=1, source_target_pairs={{0,8},{1,9},{2,10},{3,11},{4,12},{5,13},{6,14},{7,15},{8,0},{9,1},... | collective-permute-start | bytes 405512 | tf_op jit(solution)/shard_map/ppermute | solution.py:224
  118.0 6.9 %collective-permute-done.10 = f32[33792]{0:T(1024)S(1)} collective-permute-done((f32[33792]{0:T(1024)S(1)}, f32[33792]{0:T(1024)S(1)}, u32[]{:S(2)}, u32[]{:S(2)}) %collective-permute-start.10) | collective-permute-done | bytes 135200 | tf_op jit(solution)/shard_map/ppermute | solution.py:224
  125.0 5.5 %collective-permute-done.11 = bf16[33792]{0:T(1024)(128)(2,1)S(1)} collective-permute-done((bf16[33792]{0:T(1024)(128)(2,1)S(1)}, bf16[33792]{0:T(1024)(128)(2,1)S(1)}, u32[]{:S(2)}, u32[]{:S(2)}) %collective-permute-start.11) | collective-permute-done | bytes 67616 | tf_op jit(solution)/shard_map/ppermute | solution.py:236
  130.6 0.9 collective-permute-start.13
  131.5 2.6 %collective-permute-start.12 = (bf16[67584]{0:T(1024)(128)(2,1)S(1)}, bf16[67584]{0:T(1024)(128)(2,1)}, u32[]{:S(2)}, u32[]{:S(2)}) collective-permute-start(bf16[67584]{0:T(1024)(128)(2,1)S(1)} %pad_maximum_fusion.12), channel_id=1, source_target_pairs={{0,4},{1,5},{2,6},{3,7},{4,0},{5,1},{6,2},{7,3},{8,12},{9,13},{10,... | collective-permute-start | bytes 405512 | tf_op jit(solution)/shard_map/ppermute | solution.py:236
  134.6 3.4 %collective-permute-done.14 = bf16[67584]{0:T(1024)(128)(2,1)S(1)} collective-permute-done((bf16[67584]{0:T(1024)(128)(2,1)S(1)}, bf16[67584]{0:T(1024)(128)(2,1)S(1)}, u32[]{:S(2)}, u32[]{:S(2)}) %collective-permute-start.14) | collective-permute-done | bytes 135200 | tf_op jit(solution)/shard_map/ppermute | solution.py:236
  138.0 0.8 collective-permute-done.13
  139.5 1.2 select_select_fusion.3
  140.8 0.8 pad_maximum_fusion.4
  141.6 1.2 slice_add_fusion
  142.8 1.3 slice.1259
  144.1 0.9 rev.7
  145.0 1.0 fusion.150
  146.0 0.9 pad_maximum_fusion.8
  146.9 1.2 broadcast_select_fusion.1
  150.5 1.3 reshape.156
  151.8 1.1 convert_multiply_fusion.99
  (338 shorter events, 21.4 us)
Async XLA Ops:
  0.6 33.6 %copy-start = (bf16[1024,256]{1,0:T(8,128)(2,1)S(1)}, bf16[1024,256]{1,0:T(8,128)(2,1)}, u32[]{:S(2)}) copy-start(bf16[1024,256]{1,0:T(8,128)(2,1)} %param.23) | copy-start | bytes 1572868
  0.7 21.3 %copy-start.2 = (bf16[4,8,32,256]{3,2,1,0:T(8,128)(2,1)S(1)}, bf16[4,8,32,256]{3,2,1,0:T(8,128)(2,1)}, u32[]{:S(2)}) copy-start(bf16[4,8,32,256]{3,2,1,0:T(8,128)(2,1)} %param.13) | copy-start | bytes 1572868
  0.7 17.3 %copy-start.34 = (s32[8,32]{1,0:T(8,128)S(1)}, s32[8,32]{1,0:T(8,128)}, u32[]{:S(2)}) copy-start(s32[8,32]{1,0:T(8,128)} %param.16) | copy-start | bytes 3076
  1.7 10.2 %collective-permute-start = (bf16[4,8,3,256]{3,2,1,0:T(4,128)(2,1)S(1)}, bf16[4,8,3,256]{3,2,1,0:T(4,128)(2,1)S(1)}, u32[]{:S(2)}, u32[]{:S(2)}) collective-permute-start(bf16[4,8,3,256]{3,2,1,0:T(4,128)(2,1)S(1)} %slice.720), channel_id=1, source_target_pairs={{0,15},{1,14},{2,13},{3,12},{4,11},{5,10},{6,9},{7,8},{8,7},{9,6},... | collective-permute-start | bytes 147464 | tf_op jit(solution)/shard_map/ppermute | solution.py:180
  8.2 14.1 %copy-start.37 = (f32[1,1,256]{2,1,0:T(1,128)}, f32[1,1,256]{2,1,0:T(1,128)S(1)}, u32[]{:S(2)}) copy-start(f32[1,1,256]{2,1,0:T(1,128)S(1)} %get-tuple-element.133) | copy-start | bytes 3076
  8.2 14.1 %copy-start.39 = (f32[1,1,256]{2,1,0:T(1,128)}, f32[1,1,256]{2,1,0:T(1,128)S(1)}, u32[]{:S(2)}) copy-start(f32[1,1,256]{2,1,0:T(1,128)S(1)} %get-tuple-element.134) | copy-start | bytes 3076
  8.2 14.1 %copy-start.41 = (f32[1,1,256]{2,1,0:T(1,128)}, f32[1,1,256]{2,1,0:T(1,128)S(1)}, u32[]{:S(2)}) copy-start(f32[1,1,256]{2,1,0:T(1,128)S(1)} %get-tuple-element.135) | copy-start | bytes 3076
  8.2 14.1 %copy-start.43 = (f32[1,1,256]{2,1,0:T(1,128)}, f32[1,1,256]{2,1,0:T(1,128)S(1)}, u32[]{:S(2)}) copy-start(f32[1,1,256]{2,1,0:T(1,128)S(1)} %get-tuple-element.136) | copy-start | bytes 3076
  8.2 14.1 %copy-start.45 = (f32[1,1,256]{2,1,0:T(1,128)}, f32[1,1,256]{2,1,0:T(1,128)S(1)}, u32[]{:S(2)}) copy-start(f32[1,1,256]{2,1,0:T(1,128)S(1)} %get-tuple-element.137) | copy-start | bytes 3076
  8.2 14.1 %copy-start.47 = (f32[1,1,256]{2,1,0:T(1,128)}, f32[1,1,256]{2,1,0:T(1,128)S(1)}, u32[]{:S(2)}) copy-start(f32[1,1,256]{2,1,0:T(1,128)S(1)} %get-tuple-element.138) | copy-start | bytes 3076
  8.2 14.1 %copy-start.49 = (f32[1,1,256]{2,1,0:T(1,128)}, f32[1,1,256]{2,1,0:T(1,128)S(1)}, u32[]{:S(2)}) copy-start(f32[1,1,256]{2,1,0:T(1,128)S(1)} %get-tuple-element.139) | copy-start | bytes 3076
  8.3 14.1 %copy-start.51 = (f32[1,1,256]{2,1,0:T(1,128)}, f32[1,1,256]{2,1,0:T(1,128)S(1)}, u32[]{:S(2)}) copy-start(f32[1,1,256]{2,1,0:T(1,128)S(1)} %get-tuple-element.140) | copy-start | bytes 3076
  8.3 14.1 %copy-start.53 = (f32[1,1,256]{2,1,0:T(1,128)}, f32[1,1,256]{2,1,0:T(1,128)S(1)}, u32[]{:S(2)}) copy-start(f32[1,1,256]{2,1,0:T(1,128)S(1)} %get-tuple-element.141) | copy-start | bytes 3076
  8.3 14.1 %copy-start.55 = (f32[1,1,256]{2,1,0:T(1,128)}, f32[1,1,256]{2,1,0:T(1,128)S(1)}, u32[]{:S(2)}) copy-start(f32[1,1,256]{2,1,0:T(1,128)S(1)} %get-tuple-element.142) | copy-start | bytes 3076
  8.3 14.1 %copy-start.57 = (f32[1,1,256]{2,1,0:T(1,128)}, f32[1,1,256]{2,1,0:T(1,128)S(1)}, u32[]{:S(2)}) copy-start(f32[1,1,256]{2,1,0:T(1,128)S(1)} %get-tuple-element.143) | copy-start | bytes 3076
  8.3 14.1 %copy-start.59 = (f32[1,1,256]{2,1,0:T(1,128)}, f32[1,1,256]{2,1,0:T(1,128)S(1)}, u32[]{:S(2)}) copy-start(f32[1,1,256]{2,1,0:T(1,128)S(1)} %get-tuple-element.144) | copy-start | bytes 3076
  8.3 14.1 %copy-start.61 = (f32[1,1,256]{2,1,0:T(1,128)}, f32[1,1,256]{2,1,0:T(1,128)S(1)}, u32[]{:S(2)}) copy-start(f32[1,1,256]{2,1,0:T(1,128)S(1)} %get-tuple-element.145) | copy-start | bytes 3076
  8.3 14.1 %copy-start.63 = (f32[1,1,256]{2,1,0:T(1,128)}, f32[1,1,256]{2,1,0:T(1,128)S(1)}, u32[]{:S(2)}) copy-start(f32[1,1,256]{2,1,0:T(1,128)S(1)} %get-tuple-element.146) | copy-start | bytes 3076
  8.3 14.1 %copy-start.65 = (f32[1,1,256]{2,1,0:T(1,128)}, f32[1,1,256]{2,1,0:T(1,128)S(1)}, u32[]{:S(2)}) copy-start(f32[1,1,256]{2,1,0:T(1,128)S(1)} %get-tuple-element.147) | copy-start | bytes 3076
  8.3 14.1 %copy-start.67 = (f32[1,1,256]{2,1,0:T(1,128)}, f32[1,1,256]{2,1,0:T(1,128)S(1)}, u32[]{:S(2)}) copy-start(f32[1,1,256]{2,1,0:T(1,128)S(1)} %get-tuple-element.148) | copy-start | bytes 3076
  8.3 14.1 %copy-start.69 = (f32[1,1,256]{2,1,0:T(1,128)}, f32[1,1,256]{2,1,0:T(1,128)S(1)}, u32[]{:S(2)}) copy-start(f32[1,1,256]{2,1,0:T(1,128)S(1)} %get-tuple-element.149) | copy-start | bytes 3076
  9.4 13.1 %copy-start.71 = (f32[1,1,256]{2,1,0:T(1,128)}, f32[1,1,256]{2,1,0:T(1,128)S(1)}, u32[]{:S(2)}) copy-start(f32[1,1,256]{2,1,0:T(1,128)S(1)} %get-tuple-element.150) | copy-start | bytes 3076
  9.4 13.1 %copy-start.73 = (f32[1,1,256]{2,1,0:T(1,128)}, f32[1,1,256]{2,1,0:T(1,128)S(1)}, u32[]{:S(2)}) copy-start(f32[1,1,256]{2,1,0:T(1,128)S(1)} %get-tuple-element.151) | copy-start | bytes 3076
  9.4 13.1 %copy-start.75 = (f32[1,1,256]{2,1,0:T(1,128)}, f32[1,1,256]{2,1,0:T(1,128)S(1)}, u32[]{:S(2)}) copy-start(f32[1,1,256]{2,1,0:T(1,128)S(1)} %get-tuple-element.152) | copy-start | bytes 3076
  9.4 13.1 %copy-start.77 = (f32[1,1,256]{2,1,0:T(1,128)}, f32[1,1,256]{2,1,0:T(1,128)S(1)}, u32[]{:S(2)}) copy-start(f32[1,1,256]{2,1,0:T(1,128)S(1)} %get-tuple-element.153) | copy-start | bytes 3076
  9.4 13.1 %copy-start.79 = (f32[1,1,256]{2,1,0:T(1,128)}, f32[1,1,256]{2,1,0:T(1,128)S(1)}, u32[]{:S(2)}) copy-start(f32[1,1,256]{2,1,0:T(1,128)S(1)} %get-tuple-element.154) | copy-start | bytes 3076
  9.4 13.1 %copy-start.81 = (f32[1,1,256]{2,1,0:T(1,128)}, f32[1,1,256]{2,1,0:T(1,128)S(1)}, u32[]{:S(2)}) copy-start(f32[1,1,256]{2,1,0:T(1,128)S(1)} %get-tuple-element.155) | copy-start | bytes 3076
  9.5 13.1 %copy-start.83 = (f32[1,1,256]{2,1,0:T(1,128)}, f32[1,1,256]{2,1,0:T(1,128)S(1)}, u32[]{:S(2)}) copy-start(f32[1,1,256]{2,1,0:T(1,128)S(1)} %get-tuple-element.156) | copy-start | bytes 3076
  9.5 13.1 %copy-start.85 = (f32[1,1,256]{2,1,0:T(1,128)}, f32[1,1,256]{2,1,0:T(1,128)S(1)}, u32[]{:S(2)}) copy-start(f32[1,1,256]{2,1,0:T(1,128)S(1)} %get-tuple-element.157) | copy-start | bytes 3076
  9.5 13.1 %copy-start.87 = (f32[1,1,256]{2,1,0:T(1,128)}, f32[1,1,256]{2,1,0:T(1,128)S(1)}, u32[]{:S(2)}) copy-start(f32[1,1,256]{2,1,0:T(1,128)S(1)} %get-tuple-element.158) | copy-start | bytes 3076
  9.5 13.1 %copy-start.89 = (f32[1,1,256]{2,1,0:T(1,128)}, f32[1,1,256]{2,1,0:T(1,128)S(1)}, u32[]{:S(2)}) copy-start(f32[1,1,256]{2,1,0:T(1,128)S(1)} %get-tuple-element.159) | copy-start | bytes 3076
  9.5 13.1 %copy-start.91 = (f32[1,1,256]{2,1,0:T(1,128)}, f32[1,1,256]{2,1,0:T(1,128)S(1)}, u32[]{:S(2)}) copy-start(f32[1,1,256]{2,1,0:T(1,128)S(1)} %get-tuple-element.160) | copy-start | bytes 3076
  9.5 13.1 %copy-start.93 = (f32[1,1,256]{2,1,0:T(1,128)}, f32[1,1,256]{2,1,0:T(1,128)S(1)}, u32[]{:S(2)}) copy-start(f32[1,1,256]{2,1,0:T(1,128)S(1)} %get-tuple-element.161) | copy-start | bytes 3076
  9.5 13.1 %copy-start.95 = (f32[1,1,256]{2,1,0:T(1,128)}, f32[1,1,256]{2,1,0:T(1,128)S(1)}, u32[]{:S(2)}) copy-start(f32[1,1,256]{2,1,0:T(1,128)S(1)} %get-tuple-element.162) | copy-start | bytes 3076
  9.5 13.1 %copy-start.97 = (f32[1,1,256]{2,1,0:T(1,128)}, f32[1,1,256]{2,1,0:T(1,128)S(1)}, u32[]{:S(2)}) copy-start(f32[1,1,256]{2,1,0:T(1,128)S(1)} %get-tuple-element.163) | copy-start | bytes 3076
  9.5 13.1 %copy-start.99 = (f32[1,1,256]{2,1,0:T(1,128)}, f32[1,1,256]{2,1,0:T(1,128)S(1)}, u32[]{:S(2)}) copy-start(f32[1,1,256]{2,1,0:T(1,128)S(1)} %get-tuple-element.164) | copy-start | bytes 3076
  9.5 13.1 %copy-start.101 = (f32[1,1,256]{2,1,0:T(1,128)}, f32[1,1,256]{2,1,0:T(1,128)S(1)}, u32[]{:S(2)}) copy-start(f32[1,1,256]{2,1,0:T(1,128)S(1)} %get-tuple-element.165) | copy-start | bytes 3076
  9.6 13.1 %copy-start.103 = (f32[1,1,256]{2,1,0:T(1,128)}, f32[1,1,256]{2,1,0:T(1,128)S(1)}, u32[]{:S(2)}) copy-start(f32[1,1,256]{2,1,0:T(1,128)S(1)} %get-tuple-element.166) | copy-start | bytes 3076
  9.6 13.1 %copy-start.105 = (f32[1,1,256]{2,1,0:T(1,128)}, f32[1,1,256]{2,1,0:T(1,128)S(1)}, u32[]{:S(2)}) copy-start(f32[1,1,256]{2,1,0:T(1,128)S(1)} %get-tuple-element.167) | copy-start | bytes 3076
  9.6 13.1 %copy-start.107 = (f32[1,1,256]{2,1,0:T(1,128)}, f32[1,1,256]{2,1,0:T(1,128)S(1)}, u32[]{:S(2)}) copy-start(f32[1,1,256]{2,1,0:T(1,128)S(1)} %get-tuple-element.168) | copy-start | bytes 3076
  11.1 11.6 %copy-start.109 = (f32[1,1,256]{2,1,0:T(1,128)}, f32[1,1,256]{2,1,0:T(1,128)S(1)}, u32[]{:S(2)}) copy-start(f32[1,1,256]{2,1,0:T(1,128)S(1)} %get-tuple-element.169) | copy-start | bytes 3076
  11.1 11.6 %copy-start.111 = (f32[1,1,256]{2,1,0:T(1,128)}, f32[1,1,256]{2,1,0:T(1,128)S(1)}, u32[]{:S(2)}) copy-start(f32[1,1,256]{2,1,0:T(1,128)S(1)} %get-tuple-element.170) | copy-start | bytes 3076
  11.1 11.6 %copy-start.113 = (f32[1,1,256]{2,1,0:T(1,128)}, f32[1,1,256]{2,1,0:T(1,128)S(1)}, u32[]{:S(2)}) copy-start(f32[1,1,256]{2,1,0:T(1,128)S(1)} %get-tuple-element.171) | copy-start | bytes 3076
  13.5 8.5 %collective-permute-start.1 = (bf16[4,3,38,256]{3,2,1,0:T(8,128)(2,1)S(1)}, bf16[4,3,38,256]{3,2,1,0:T(8,128)(2,1)S(1)}, u32[]{:S(2)}, u32[]{:S(2)}) collective-permute-start(bf16[4,3,38,256]{3,2,1,0:T(8,128)(2,1)S(1)} %get-tuple-element.119), channel_id=1, source_target_pairs={{0,1},{1,2},{2,3},{3,4},{4,5},{5,6},{6,7},{7,8},{8,9},{9,10},{10,1... | collective-permute-start | bytes 700424 | tf_op jit(solution)/shard_map/ppermute | solution.py:26
  14.2 7.8 %collective-permute-start.2 = (bf16[4,3,38,256]{3,2,1,0:T(8,128)(2,1)S(1)}, bf16[4,3,38,256]{3,2,1,0:T(8,128)(2,1)S(1)}, u32[]{:S(2)}, u32[]{:S(2)}) collective-permute-start(bf16[4,3,38,256]{3,2,1,0:T(8,128)(2,1)S(1)} %get-tuple-element.120), channel_id=1, source_target_pairs={{1,0},{2,1},{3,2},{4,3},{5,4},{6,5},{7,6},{8,7},{9,8},{10,9},{11,1... | collective-permute-start | bytes 700424 | tf_op jit(solution)/shard_map/ppermute | solution.py:27
  22.7 9.8 %copy-start.35 = (f32[256]{0:T(256)S(1)}, f32[256]{0:T(256)}, u32[]{:S(2)}) copy-start(f32[256]{0:T(256)} %param.19) | copy-start | bytes 3076
  22.7 9.8 %copy-start.130 = (f32[256]{0:T(256)S(1)}, f32[256]{0:T(256)}, u32[]{:S(2)}) copy-start(f32[256]{0:T(256)} %param.20) | copy-start | bytes 3076
  66.3 11.3 %copy-start.19 = (bf16[1,8,32,256]{3,2,1,0:T(8,128)(2,1)S(1)}, bf16[1,8,32,256]{3,2,1,0:T(8,128)(2,1)}, u32[]{:S(2)}) copy-start(bf16[1,8,32,256]{3,2,1,0:T(8,128)(2,1)} %copy-done.18) | copy-start | bytes 393220
  85.5 12.1 %collective-permute-start.3 = (f32[270336]{0:T(1024)}, f32[270336]{0:T(1024)}, u32[]{:S(2)}, u32[]{:S(2)}) collective-permute-start(f32[270336]{0:T(1024)} %pad_dynamic-slice_fusion), channel_id=1, source_target_pairs={{0,1},{1,0},{2,3},{3,2},{4,5},{5,4},{6,7},{7,6},{8,9},{9,8},{10,11... | collective-permute-start | bytes 3244040 | tf_op jit(solution)/shard_map/ppermute | solution.py:224
  87.0 10.2 %collective-permute-start.4 = (f32[4,3,32,256]{3,2,1,0:T(8,128)}, f32[4,3,32,256]{3,2,1,0:T(8,128)S(1)}, u32[]{:S(2)}, u32[]{:S(2)}) collective-permute-start(f32[4,3,32,256]{3,2,1,0:T(8,128)} %get-tuple-element.115), channel_id=1, source_target_pairs={{0,1},{1,2},{2,3},{3,4},{4,5},{5,6},{6,7},{7,8},{8,9},{9,10},{10,1... | collective-permute-start | bytes 1179656 | tf_op jit(solution)/shard_map/ppermute | solution.py:26
  87.0 10.2 %collective-permute-start.5 = (f32[4,3,32,256]{3,2,1,0:T(8,128)}, f32[4,3,32,256]{3,2,1,0:T(8,128)S(1)}, u32[]{:S(2)}, u32[]{:S(2)}) collective-permute-start(f32[4,3,32,256]{3,2,1,0:T(8,128)} %get-tuple-element.116), channel_id=1, source_target_pairs={{1,0},{2,1},{3,2},{4,3},{5,4},{6,5},{7,6},{8,7},{9,8},{10,9},{11,1... | collective-permute-start | bytes 1179656 | tf_op jit(solution)/shard_map/ppermute | solution.py:27
  91.5 6.2 %copy-start.5 = (f32[539136]{0:T(1024)S(1)}, f32[539136]{0:T(1024)}, u32[]{:S(2)}) copy-start(f32[539136]{0:T(1024)} %copy-done.4) | copy-start | bytes 6469636
  99.6 14.9 %collective-permute-start.6 = (f32[67584]{0:T(1024)S(1)}, f32[67584]{0:T(1024)S(1)}, u32[]{:S(2)}, u32[]{:S(2)}) collective-permute-start(f32[67584]{0:T(1024)S(1)} %get-tuple-element.112), channel_id=1, source_target_pairs={{0,2},{1,3},{2,0},{3,1},{4,6},{5,7},{6,4},{7,5},{8,10},{9,11},{10,... | collective-permute-start | bytes 811016 | tf_op jit(solution)/shard_map/ppermute | solution.py:224
  100.9 13.5 %collective-permute-start.8 = (f32[67584]{0:T(1024)S(1)}, f32[67584]{0:T(1024)S(1)}, u32[]{:S(2)}, u32[]{:S(2)}) collective-permute-start(f32[67584]{0:T(1024)S(1)} %get-tuple-element.113), channel_id=1, source_target_pairs={{0,6},{1,7},{2,4},{3,5},{4,2},{5,3},{6,0},{7,1},{8,14},{9,15},{10,... | collective-permute-start | bytes 811016 | tf_op jit(solution)/shard_map/ppermute | solution.py:224
  100.9 15.2 %collective-permute-start.7 = (f32[67584]{0:T(1024)S(1)}, f32[67584]{0:T(1024)S(1)}, u32[]{:S(2)}, u32[]{:S(2)}) collective-permute-start(f32[67584]{0:T(1024)S(1)} %get-tuple-element.114), channel_id=1, source_target_pairs={{0,4},{1,5},{2,6},{3,7},{4,0},{5,1},{6,2},{7,3},{8,12},{9,13},{10,... | collective-permute-start | bytes 811016 | tf_op jit(solution)/shard_map/ppermute | solution.py:224
  116.2 8.6 %collective-permute-start.10 = (f32[33792]{0:T(1024)S(1)}, f32[33792]{0:T(1024)S(1)}, u32[]{:S(2)}, u32[]{:S(2)}) collective-permute-start(f32[33792]{0:T(1024)S(1)} %dynamic_slice.31), channel_id=1, source_target_pairs={{0,8},{1,9},{2,10},{3,11},{4,12},{5,13},{6,14},{7,15},{8,0},{9,1},... | collective-permute-start | bytes 405512 | tf_op jit(solution)/shard_map/ppermute | solution.py:224
  124.9 5.6 %collective-permute-start.11 = (bf16[33792]{0:T(1024)(128)(2,1)S(1)}, bf16[33792]{0:T(1024)(128)(2,1)S(1)}, u32[]{:S(2)}, u32[]{:S(2)}) collective-permute-start(bf16[33792]{0:T(1024)(128)(2,1)S(1)} %add_convert_fusion.1), channel_id=1, source_target_pairs={{0,8},{1,9},{2,10},{3,11},{4,12},{5,13},{6,14},{7,15},{8,0},{9,1},... | collective-permute-start | bytes 202760 | tf_op jit(solution)/shard_map/ppermute | solution.py:236
  130.5 8.3 %copy-start.28 = (bf16[33792]{0:T(1024)(128)(2,1)}, bf16[33792]{0:T(1024)(128)(2,1)S(1)}, u32[]{:S(2)}) copy-start(bf16[33792]{0:T(1024)(128)(2,1)S(1)} %get-tuple-element.130) | copy-start | bytes 202756
  130.5 11.1 %copy-start.8 = (f32[8,32,256]{2,1,0:T(8,128)S(1)}, f32[8,32,256]{2,1,0:T(8,128)}, u32[]{:S(2)}) copy-start(f32[8,32,256]{2,1,0:T(8,128)} %copy-done.6) | copy-start | bytes 786436
  130.6 7.5 %collective-permute-start.14 = (bf16[67584]{0:T(1024)(128)(2,1)S(1)}, bf16[67584]{0:T(1024)(128)(2,1)S(1)}, u32[]{:S(2)}, u32[]{:S(2)}) collective-permute-start(bf16[67584]{0:T(1024)(128)(2,1)S(1)} %pad_maximum_fusion.12), channel_id=1, source_target_pairs={{0,6},{1,7},{2,4},{3,5},{4,2},{5,3},{6,0},{7,1},{8,14},{9,15},{10,... | collective-permute-start | bytes 405512 | tf_op jit(solution)/shard_map/ppermute | solution.py:236
  130.6 8.2 %collective-permute-start.13 = (bf16[67584]{0:T(1024)(128)(2,1)S(1)}, bf16[67584]{0:T(1024)(128)(2,1)S(1)}, u32[]{:S(2)}, u32[]{:S(2)}) collective-permute-start(bf16[67584]{0:T(1024)(128)(2,1)S(1)} %pad_maximum_fusion.12), channel_id=1, source_target_pairs={{0,2},{1,3},{2,0},{3,1},{4,6},{5,7},{6,4},{7,5},{8,10},{9,11},{10,... | collective-permute-start | bytes 405512 | tf_op jit(solution)/shard_map/ppermute | solution.py:236
  131.5 8.0 %collective-permute-start.12 = (bf16[67584]{0:T(1024)(128)(2,1)S(1)}, bf16[67584]{0:T(1024)(128)(2,1)}, u32[]{:S(2)}, u32[]{:S(2)}) collective-permute-start(bf16[67584]{0:T(1024)(128)(2,1)S(1)} %pad_maximum_fusion.12), channel_id=1, source_target_pairs={{0,4},{1,5},{2,6},{3,7},{4,0},{5,1},{6,2},{7,3},{8,12},{9,13},{10,... | collective-permute-start | bytes 405512 | tf_op jit(solution)/shard_map/ppermute | solution.py:236
  134.2 9.9 %collective-permute-start.9 = (bf16[4,8,3,256]{3,2,1,0:T(4,128)(2,1)S(1)}, bf16[4,8,3,256]{3,2,1,0:T(4,128)(2,1)}, u32[]{:S(2)}, u32[]{:S(2)}) collective-permute-start(bf16[4,8,3,256]{3,2,1,0:T(4,128)(2,1)S(1)} %slice.1260), channel_id=1, source_target_pairs={{0,15},{1,14},{2,13},{3,12},{4,11},{5,10},{6,9},{7,8},{8,7},{9,6},... | collective-permute-start | bytes 147464 | tf_op jit(solution)/shard_map/ppermute | solution.py:180
  141.6 5.3 %collective-permute-start.15 = (bf16[270336]{0:T(1024)(128)(2,1)}, bf16[270336]{0:T(1024)(128)(2,1)}, u32[]{:S(2)}, u32[]{:S(2)}) collective-permute-start(bf16[270336]{0:T(1024)(128)(2,1)} %pad_maximum_fusion.4), channel_id=1, source_target_pairs={{0,1},{1,0},{2,3},{3,2},{4,5},{5,4},{6,7},{7,6},{8,9},{9,8},{10,11... | collective-permute-start | bytes 1622024 | tf_op jit(solution)/shard_map/ppermute | solution.py:236
  (84 other events, 216.6 us)

commit v11 on v10

--- a/solution.py
+++ b/solution.py
@@ -139,40 +139,34 @@
     grad_normed = jnp.stack(normed_grads)
     grad_ln_gain = jnp.sum(grad_normed * unit, axis=(0, 1, 2))
     grad_ln_bias = jnp.sum(grad_normed, axis=(0, 1, 2))
-    grad_unit = grad_normed * ln_gain
-    grad_depth = inv_std * (
-        grad_unit
-        - jnp.mean(grad_unit, axis=-1, keepdims=True)
-        - unit * jnp.mean(grad_unit * unit, axis=-1, keepdims=True)
-    )
-    grad_dw_bias = jnp.sum(grad_depth, axis=(0, 1, 2))
-    kernel_rows = []
-    for lon_off in range(7):
-        kernel_cols = []
-        for lat_off in range(7):
-            kernel_cols.append(
-                jnp.sum(
-                    grad_depth
-                    * extended[
-                        :, lon_off : lon_off + lon_dev, lat_off : lat_off + lat_rows, :
-                    ].astype(jnp.float32),
-                    axis=(0, 1, 2),
+
+    def depth_backward(grad_normed):
+        grad_unit = grad_normed * ln_gain
+        grad_depth = inv_std * (
+            grad_unit
+            - jnp.mean(grad_unit, axis=-1, keepdims=True)
+            - unit * jnp.mean(grad_unit * unit, axis=-1, keepdims=True)
+        )
+        grad_dw_bias = jnp.sum(grad_depth, axis=(0, 1, 2))
+        kernel_rows = []
+        for lon_off in range(7):
+            kernel_cols = []
+            for lat_off in range(7):
+                kernel_cols.append(
+                    jnp.sum(
+                        grad_depth
+                        * extended[
+                            :, lon_off : lon_off + lon_dev, lat_off : lat_off + lat_rows, :
+                        ].astype(jnp.float32),
+                        axis=(0, 1, 2),
+                    )
                 )
-            )
-        kernel_rows.append(jnp.stack(kernel_cols))
-    grad_kernel = jnp.stack(kernel_rows)
-    grads = (
-        grad_kernel,
-        grad_dw_bias,
-        grad_ln_gain,
-        grad_ln_bias,
-        grad_w_in,
-        grad_b_in,
-        grad_w_out,
-        grad_b_out,
-        grad_scale,
-    )
-    return (pred.astype(jnp.bfloat16), crps_field, grad_pred, grad_depth, grads)
+            kernel_rows.append(jnp.stack(kernel_cols))
+        grad_kernel = jnp.stack(kernel_rows)
+        return grad_depth, grad_kernel, grad_dw_bias
+
+    sums = (grad_ln_gain, grad_ln_bias, grad_w_in, grad_b_in, grad_w_out, grad_b_out, grad_scale)
+    return (pred.astype(jnp.bfloat16), crps_field, grad_pred, grad_normed, sums, depth_backward)
 
 
 def mirrored(x, axis):
@@ -227,7 +221,8 @@
             cur, operand = lax.optimization_barrier((cur, operand))
             result = work(operand)
         elif bits == groups[1]:
-            cur, result = lax.optimization_barrier((cur, result))
+            cur, first = lax.optimization_barrier((cur, result[0]))
+            result = (first,) + tuple(result[1:])
     cur = cur.astype(gather_dtype)
     for bits in reversed(groups):
         radix, low = 1 << len(bits), bits[0]
@@ -286,31 +281,39 @@
     north_rows = mirror_rows(features[:, :, lat_rows - 3 :, :])
     joined = jnp.concatenate([south_rim, features, north_rows], axis=2)
     extended = with_halo(joined, (("lon", 1),), 3)
-    predicted, crps_field, grad_pred, grad_depth, grads = local_step(
+    predicted, crps_field, grad_pred, grad_normed, sums, depth_backward = local_step(
         extended, features, target, kmt, *params
     )
-    grad_halo = with_halo(grad_depth, (("lon", 1),), 3)
-    padded = jnp.pad(grad_halo, ((0, 0), (0, 0), (6, 6), (0, 0)))
-
-    def backward_conv(operand):
+
+    def backward(grad_normed):
+        grad_depth, kernel_sum, dw_bias_sum = depth_backward(grad_normed)
+        grad_halo = with_halo(grad_depth, (("lon", 1),), 3)
+        padded = jnp.pad(grad_halo, ((0, 0), (0, 0), (6, 6), (0, 0)))
         grad_ext = jnp.zeros((members, lon_dev, lat_rows + 6, chans), jnp.float32)
         for lon_off in range(7):
             for lat_off in range(7):
                 grad_ext = (
                     grad_ext
                     + dw_kernel[lon_off, lat_off]
-                    * operand[
+                    * padded[
                         :,
                         6 - lon_off : 6 - lon_off + lon_dev,
                         6 - lat_off : 6 - lat_off + lat_rows + 6,
                         :,
                     ]
                 )
-        return grad_ext
-
-    (
-        kernel_sum,
-        dw_bias_sum,
+        return grad_ext, kernel_sum, dw_bias_sum
+
+    lon_size = lax.axis_size("lon")
+    reduced, (grad_ext, kernel_sum, dw_bias_sum) = radix_allreduce(
+        pack(sums, lon_size * 1024), "lon", jnp.bfloat16, grad_normed, backward
+    )
+    gain_sum, bias_sum, w_in_sum, b_in_sum, w_out_sum, b_out_sum, scale_sum = unpack(reduced, sums)
+    small = (kernel_sum, dw_bias_sum)
+    kernel_tot, dw_bias_tot = unpack(butterfly_allreduce(pack(small, 128), "lon"), small)
+    totals = (
+        kernel_tot,
+        dw_bias_tot,
         gain_sum,
         bias_sum,
         w_in_sum,
@@ -318,23 +321,7 @@
         w_out_sum,
         b_out_sum,
         scale_sum,
-    ) = grads
-    lon_size = lax.axis_size("lon")
-    sums = (
-        kernel_sum,
-        dw_bias_sum,
-        gain_sum,
-        bias_sum,
-        w_in_sum,
-        b_in_sum,
-        w_out_sum,
-        b_out_sum,
-        scale_sum,
-    )
-    reduced, grad_ext = radix_allreduce(
-        pack(sums, lon_size * 1024), "lon", jnp.bfloat16, padded, backward_conv
-    )
-    totals = unpack(reduced, sums)
+    )
     back_rows = mirror_grads(grad_ext[:, :, lat_rows + 3 :, :])
     inner = grad_pred + grad_ext[:, :, 3 : lat_rows + 3, :]
     grad_features = jnp.concatenate(

time: 154 us -> 147 us (0.955)
  local copies, waits for them, and re-layouts: 29.3 us -> 16.4 us
  waiting for transfers between devices: 28.8 us -> 37 us
  matrix products: 18.8 us -> 11.8 us
  starting transfers between devices: 24.3 us -> 28.7 us
    ppermute x5, waiting for transfers between devices: 9.36 us -> 17.7 us  [radix_allreduce(): lax.ppermute(send, axis, [(i, i ^ d << low) for i in range(size)])]
    ppermute x0 -> x4, waiting for transfers between devices: none -> 7.15 us  [swapped(): lax.ppermute(x, axis, [(i, i ^ 1 << bit) for i in range(lax.axis_size(axi...]
    ppermute x2, waiting for transfers between devices: 9.6 us -> 3.45 us  [with_halo(): before = lax.ppermute(last, axis, up)]
    unnamed x278 -> x294, local copies, waits for them, and re-layouts: 10.5 us -> 4.79 us
    another operation x8, local copies, waits for them, and re-layouts: 5.69 us -> 0.2 us  [the longest x7 0.2 us: depth_backward(): kernel_rows.append(jnp.stack(kernel_cols))]
    ppermute x0 -> x4, starting transfers between devices: none -> 5.48 us  [swapped(): lax.ppermute(x, axis, [(i, i ^ 1 << bit) for i in range(lax.axis_size(axi...]
    ppermute x5, starting transfers between devices: 5.87 us -> 3.41 us  [radix_allreduce(): lax.ppermute(send, axis, [(i, i ^ d << low) for i in range(size)])]
    dot_general x4, matrix products: 3.7 us -> 1.28 us  [local_step(): lax.dot_general(normed[member].reshape(rows, chans), pre_half, contract_r...]
  transfers between devices with their start and end apart: 16 -> 20, of which waited for: 8 -> 10; matrix products, arithmetic and copies ran while one was open for 15% -> 15% of each run, Pallas kernels for 0% -> 0%
where the time goes in v11:
time: 147 us
  other arithmetic  49.5 us (34%)
  waiting for transfers between devices  37 us (25%)
  starting transfers between devices  28.7 us (20%)
  local copies, waits for them, and re-layouts  16.4 us (11%)
  matrix products  11.8 us (8%)
  between operations  3.3 us (2%)
    ppermute x5, waiting for transfers between devices, radix_allreduce(): lax.ppermute(send, axis, [(i, i ^ d << low) for i in range(size)])  17.7 us
    add x1, other arithmetic, backward(): grad_ext + dw_kernel[lon_off, lat_off] * padded[:, 6 - lon_off:6 - lon_of...  10.2 us
    reduce_sum x1, other arithmetic, local_step(): mean_val = jnp.mean(depth, axis=-1, keepdims=True)  9.29 us
    reduce_sum x4, other arithmetic, depth_backward(): jnp.sum(grad_depth * extended[:, lon_off:lon_off + lon_dev, lat_off:lat_o...  9.12 us
    ppermute x2, starting transfers between devices, with_halo(): after = lax.ppermute(leading, axis, down)  7.86 us
    ppermute x5, waiting for transfers between devices, radix_allreduce(): lax.ppermute(cur, axis, [(i, i ^ d << low) for i in range(size)])  7.69 us
    ppermute x4, waiting for transfers between devices, swapped(): lax.ppermute(x, axis, [(i, i ^ 1 << bit) for i in range(lax.axis_size(axi...  7.15 us
    ppermute x2, starting transfers between devices, mirrored(): return lax.ppermute(x, axis, [(i, size - 1 - i) for i in range(size)])  5.55 us
  transfers between devices with their start and end apart: 20, of which 10 were waited for; matrix products, arithmetic and copies ran while one was open for 15% of the time, Pallas kernels for 0%

profile of v11, /device:TPU:0, one launch (start us, length us, event | category | flops | bytes accessed | tf_op | source)
XLA Modules:
  0.0 146.6 jit_solution(1700051485965681955)
XLA Ops:
  0.7 1.0 slice.712
  1.7 5.5 %collective-permute-start = (bf16[4,8,3,256]{3,2,1,0:T(4,128)(2,1)S(1)}, bf16[4,8,3,256]{3,2,1,0:T(4,128)(2,1)S(1)}, u32[]{:S(2)}, u32[]{:S(2)}) collective-permute-start(bf16[4,8,3,256]{3,2,1,0:T(4,128)(2,1)S(1)} %slice.712), channel_id=1, source_target_pairs={{0,15},{1,14},{2,13},{3,12},{4,11},{5,10},{6,9},{7,8},{8,7},{9,6},... | collective-permute-start | bytes 147464 | tf_op jit(solution)/shard_map/ppermute | solution.py:174
  7.2 1.6 %fusion.215 = (f32[1,1,256]{2,1,0:T(1,128)S(1)}, f32[1,1,256]{2,1,0:T(1,128)S(1)}, f32[1,1,256]{2,1,0:T(1,128)S(1)}, f32[1,1,256]{2,1,0:T(1,128)S(1)}, f32[1,1,2...) fusion(f32[7,7,256]{2,1,0:T(8,128)} %param.17), kind=kLoop, calls=%fused_computation.498 | loop fusion | bytes 38912 | tf_op jit(solution)/shard_map/slice | solution.py:59
  8.9 1.7 %fusion.216 = (f32[1,1,256]{2,1,0:T(1,128)}, f32[1,1,256]{2,1,0:T(1,128)}, f32[1,1,256]{2,1,0:T(1,128)}, f32[1,1,256]{2,1,0:T(1,128)}, f32[1,1,256]{2,1,0:T(1,12...) fusion(f32[7,7,256]{2,1,0:T(8,128)} %param.17), kind=kLoop, calls=%fused_computation.499 | loop fusion | bytes 38912 | tf_op jit(solution)/shard_map/slice | solution.py:59
  10.6 1.5 %fusion.217 = (f32[1,1,256]{2,1,0:T(1,128)}, f32[1,1,256]{2,1,0:T(1,128)}, f32[1,1,256]{2,1,0:T(1,128)}, f32[1,1,256]{2,1,0:T(1,128)}, f32[1,1,256]{2,1,0:T(1,12...) fusion(f32[7,7,256]{2,1,0:T(8,128)} %param.17), kind=kLoop, calls=%fused_computation.500 | loop fusion | bytes 22528 | tf_op jit(solution)/shard_map/slice | solution.py:59
  12.1 0.8 copy.25
  13.1 1.3 pad_maximum_fusion.11
  14.4 0.7 collective-permute-start.1
  15.1 3.8 %collective-permute-start.2 = (bf16[4,3,38,256]{3,2,1,0:T(8,128)(2,1)S(1)}, bf16[4,3,38,256]{3,2,1,0:T(8,128)(2,1)}, u32[]{:S(2)}, u32[]{:S(2)}) collective-permute-start(bf16[4,3,38,256]{3,2,1,0:T(8,128)(2,1)S(1)} %get-tuple-element.120), channel_id=1, source_target_pairs={{1,0},{2,1},{3,2},{4,3},{5,4},{6,5},{7,6},{8,7},{9,8},{10,9},{11,1... | collective-permute-start | bytes 700424 | tf_op jit(solution)/shard_map/ppermute | solution.py:27
  19.4 3.5 %collective-permute-done.1 = bf16[4,3,38,256]{3,2,1,0:T(8,128)(2,1)S(1)} collective-permute-done((bf16[4,3,38,256]{3,2,1,0:T(8,128)(2,1)S(1)}, bf16[4,3,38,256]{3,2,1,0:T(8,128)(2,1)S(1)}, u32[]{:S(2)}, u32[]{:S(2)}) %collective-permute-start.1) | collective-permute-done | bytes 233504 | tf_op jit(solution)/shard_map/ppermute | solution.py:26
  22.9 1.3 maximum_maximum_fusion
  24.7 9.3 %fusion.210 = (f32[4,8,32]{2,1,0:T(8,128)S(1)}, f32[4,8,32,256]{3,2,1,0:T(8,128)S(1)}) fusion(bf16[4,11,38,256]{3,2,1,0:T(8,128)(2,1)S(1)} %get-tuple-element.118, f32[256]{0:T(256)} %bitcast.432, f32[256]{0:T(256)} %bitcast.434, f32[256]{0:T(256)S(1)} %bitcast.340, f32[256]{0:T(256)S(1)} %bitcast.342, f32[256]{0:T(256)S(1)} %bitcast.344, ...), kind=kLoop, calls=%fused_computation.494 | loop fusion | flops 43514880 | bytes 23746560 | tf_op jit(solution)/shard_map/reduce_sum | solution.py:62
  34.4 1.1 add_convert_fusion
  37.5 0.5 convolution_add_fusion.11
  39.0 1.1 fusion.208
  40.1 2.5 %multiply_reduce_fusion.7 = (f32[256]{0:T(256)S(1)}, f32[256]{0:T(256)S(1)}, f32[256]{0:T(256)S(1)}, f32[256]{0:T(256)S(1)}, f32[8,32,256]{2,1,0:T(8,128)S(1)}, ...) fusion(f32[256]{0:T(256)S(1)} %copy-done.26, ...), kind=kLoop, calls=%fused_computation.434 | loop fusion | flops 7863296 | bytes 2497536 | tf_op jit(solution)/shard_map/reduce_sum | solution.py:117
  42.7 0.6 fusion.199
  43.3 0.9 fusion.202
  44.9 0.9 fusion.200
  45.8 0.6 convolution_add_fusion.2
  46.4 0.9 fusion.204
  47.3 0.6 convolution_add_fusion.1
  47.9 0.9 fusion.206
  48.9 0.6 fusion.1
  49.5 0.8 copy.28
  52.5 1.3 pad_maximum_fusion.2
  53.8 0.7 copy-done.8
  55.3 1.2 pad_dynamic-slice_fusion
  56.5 0.5 copy-done.9
  57.0 0.7 collective-permute-start.3
  57.7 2.7 %collective-permute-done.3 = f32[270336]{0:T(1024)} collective-permute-done((f32[270336]{0:T(1024)}, f32[270336]{0:T(1024)}, u32[]{:S(2)}, u32[]{:S(2)}) %collective-permute-start.3) | collective-permute-done | bytes 1081376 | tf_op jit(solution)/shard_map/ppermute | solution.py:218
  60.3 2.7 %fusion.51 = f32[270336]{0:T(1024)} fusion(f32[270336]{0:T(1024)} %collective-permute-done.3, s32[]{:T(128)S(6)} %select_n.114, f32[526336]{0:T(1024)} %copy-done.9), kind=kLoop, calls=%fused_computation.227 | loop fusion | flops 270336 | bytes 4268036 | tf_op jit(solution)/shard_map/add | solution.py:218
  63.0 0.6 multiply_reduce_fusion.4
  63.7 3.8 %fusion.148 = (f32[256]{0:T(256)S(1)}, f32[256]{0:T(256)}, f32[256]{0:T(256)}, f32[256]{0:T(256)}, f32[256]{0:T(256)}, /*index=5*/f32[256]{0:T(256)}, f32[256]{0...) fusion(bf16[4,11,38,256]{3,2,1,0:T(8,128)(2,1)S(1)} %get-tuple-, ...), kind=kLoop, calls=%fused_computation.325 | loop fusion | flops 15986176 | bytes 12618752 | tf_op jit(solution)/shard_map/reduce_sum | solution.py:156
  67.5 0.9 fusion.213
  68.9 2.4 %fusion.130 = (f32[256]{0:T(256)}, f32[256]{0:T(256)}, f32[256]{0:T(256)}, f32[256]{0:T(256)S(1)}, f32[256]{0:T(256)}, /*index=5*/f32[256]{0:T(256)}, f32[256]{0...) fusion(f32[4,8,32,256]{3,2,1,0:T(8,128)S(1)} %get-tuple-element.86, ...), kind=kLoop, calls=%fused_computation.307 | loop fusion | flops 12842240 | bytes 3255296 | tf_op jit(solution)/shard_map/reduce_sum | solution.py:156
  71.2 2.5 %fusion.97 = (f32[256]{0:T(256)S(1)}, f32[256]{0:T(256)S(1)}, f32[256]{0:T(256)S(1)}, f32[256]{0:T(256)S(1)}, f32[256]{0:T(256)S(1)}, /*index=5*/f32[256]{0:T(25...) fusion(f32[4,8,32,256]{3,2,1,0:T(8,128)S(1)} %get-tuple-element, ...), kind=kLoop, calls=%fused_computation.274 | loop fusion | flops 14151168 | bytes 10504192 | tf_op jit(solution)/shard_map/reduce_sum | solution.py:156
  74.9 4.1 %collective-permute-start.8 = (f32[4,3,32,256]{3,2,1,0:T(8,128)}, f32[4,3,32,256]{3,2,1,0:T(8,128)}, u32[]{:S(2)}, u32[]{:S(2)}) collective-permute-start(f32[4,3,32,256]{3,2,1,0:T(8,128)} %get-tuple-element.114), channel_id=1, source_target_pairs={{1,0},{2,1},{3,2},{4,3},{5,4},{6,5},{7,6},{8,7},{9,8},{10,9},{11,1... | collective-permute-start | bytes 1179656 | tf_op jit(solution)/shard_map/ppermute | solution.py:27
  79.9 1.0 collective-permute-done.10
  80.9 2.4 %collective-permute-start.6 = (f32[67584]{0:T(1024)S(1)}, f32[67584]{0:T(1024)S(1)}, u32[]{:S(2)}, u32[]{:S(2)}) collective-permute-start(f32[67584]{0:T(1024)S(1)} %get-tuple-element.111), channel_id=1, source_target_pairs={{0,6},{1,7},{2,4},{3,5},{4,2},{5,3},{6,0},{7,1},{8,14},{9,15},{10,... | collective-permute-start | bytes 811016 | tf_op jit(solution)/shard_map/ppermute | solution.py:218
  83.3 15.1 %collective-permute-done.4 = f32[67584]{0:T(1024)S(1)} collective-permute-done((f32[67584]{0:T(1024)S(1)}, f32[67584]{0:T(1024)S(1)}, u32[]{:S(2)}, u32[]{:S(2)}) %collective-permute-start.4) | collective-permute-done | bytes 270368 | tf_op jit(solution)/shard_map/ppermute | solution.py:218
  98.9 1.5 %select_maximum_fusion = f32[4,14,44,256]{3,2,1,0:T(8,128)S(1)} fusion(f32[4,3,32,256]{3,2,1,0:T(8,128)} %collective-permute-done.8, f32[4,8,32,256]{3,2,1,0:T(8,128)S(1)} %copy-done.2, f32[4,3,32,256]{3,2,1,0:T(8,128)} %collective-permute-done.7), kind=kLoop, calls=%fused_computation.2 | loop fusion | flops 5046272 | bytes 4358144 | tf_op jit(solution)/shard_map/concatenate | solution.py:28
  100.8 10.2 %fusion.3 = f32[4,8,38,256]{3,2,1,0:T(8,128)S(1)} fusion(f32[4,14,44,256]{3,2,1,0:T(8,128)S(1)} %select_maximum_fusion, f32[256]{0:T(256)} %bitcast.433, f32[256]{0:T(256)} %bitcast.435, f32[256]{0:T(256)S(1)} %bitcast.341, f32[256]{0:T(256)S(1)} %bitcast.343, f32[256]{0:T(256)S(1)} %bitcast.345, f32[256]{0:T(256)S(1)} %bitcast.347, f32[256]{0:T(256)S(1)} %bitcast.349, ...), kind=kLoop, calls=%fused_computation.127 | loop fusion | flops 30195712 | bytes 62309376 | tf_op jit(solution)/shard_map/add | solution.py:296
  111.1 1.8 %collective-permute-start.12 = (f32[12800]{0:T(1024)S(1)}, f32[12800]{0:T(1024)S(1)}, u32[]{:S(2)}, u32[]{:S(2)}) collective-permute-start(f32[12800]{0:T(1024)S(1)} %add.802), channel_id=1, source_target_pairs={{0,4},{1,5},{2,6},{3,7},{4,0},{5,1},{6,2},{7,3},{8,12},{9,13},{10,... | collective-permute-start | bytes 153608 | tf_op jit(solution)/shard_map/ppermute | solution.py:16
  112.9 2.8 %collective-permute-done.12 = f32[12800]{0:T(1024)S(1)} collective-permute-done((f32[12800]{0:T(1024)S(1)}, f32[12800]{0:T(1024)S(1)}, u32[]{:S(2)}, u32[]{:S(2)}) %collective-permute-start.12) | collective-permute-done | bytes 51232 | tf_op jit(solution)/shard_map/ppermute | solution.py:16
  115.7 3.6 %collective-permute-start.13 = (f32[12800]{0:T(1024)S(1)}, f32[12800]{0:T(1024)S(1)}, u32[]{:S(2)}, u32[]{:S(2)}) collective-permute-start(f32[12800]{0:T(1024)S(1)} %add.803), channel_id=1, source_target_pairs={{0,8},{1,9},{2,10},{3,11},{4,12},{5,13},{6,14},{7,15},{8,0},{9,1},... | collective-permute-start | bytes 153608 | tf_op jit(solution)/shard_map/ppermute | solution.py:16
  119.3 3.4 %collective-permute-done.13 = f32[12800]{0:T(1024)S(1)} collective-permute-done((f32[12800]{0:T(1024)S(1)}, f32[12800]{0:T(1024)S(1)}, u32[]{:S(2)}, u32[]{:S(2)}) %collective-permute-start.13) | collective-permute-done | bytes 51232 | tf_op jit(solution)/shard_map/ppermute | solution.py:16
  122.8 1.7 %collective-permute-start.15 = (bf16[33792]{0:T(1024)(128)(2,1)S(1)}, bf16[33792]{0:T(1024)(128)(2,1)S(1)}, u32[]{:S(2)}, u32[]{:S(2)}) collective-permute-start(bf16[33792]{0:T(1024)(128)(2,1)S(1)} %add_convert_fusion.1), channel_id=1, source_target_pairs={{0,8},{1,9},{2,10},{3,11},{4,12},{5,13},{6,14},{7,15},{8,0},{9,1},... | collective-permute-start | bytes 202760 | tf_op jit(solution)/shard_map/ppermute | solution.py:231
  124.5 0.6 mul.1860
  125.1 3.5 %collective-permute-done.15 = bf16[33792]{0:T(1024)(128)(2,1)S(1)} collective-permute-done((bf16[33792]{0:T(1024)(128)(2,1)S(1)}, bf16[33792]{0:T(1024)(128)(2,1)S(1)}, u32[]{:S(2)}, u32[]{:S(2)}) %collective-permute-start.15) | collective-permute-done | bytes 67616 | tf_op jit(solution)/shard_map/ppermute | solution.py:231
  128.8 1.1 collective-permute-start.17
  129.9 2.4 %collective-permute-start.18 = (bf16[67584]{0:T(1024)(128)(2,1)S(1)}, bf16[67584]{0:T(1024)(128)(2,1)S(1)}, u32[]{:S(2)}, u32[]{:S(2)}) collective-permute-start(bf16[67584]{0:T(1024)(128)(2,1)S(1)} %pad_maximum_fusion.12), channel_id=1, source_target_pairs={{0,6},{1,7},{2,4},{3,5},{4,2},{5,3},{6,0},{7,1},{8,14},{9,15},{10,... | collective-permute-start | bytes 405512 | tf_op jit(solution)/shard_map/ppermute | solution.py:231
  132.3 0.6 slice_multiply_fusion.51
  133.0 2.3 %collective-permute-done.16 = bf16[67584]{0:T(1024)(128)(2,1)S(1)} collective-permute-done((bf16[67584]{0:T(1024)(128)(2,1)S(1)}, bf16[67584]{0:T(1024)(128)(2,1)S(1)}, u32[]{:S(2)}, u32[]{:S(2)}) %collective-permute-start.16) | collective-permute-done | bytes 135200 | tf_op jit(solution)/shard_map/ppermute | solution.py:231
  135.2 1.9 %collective-permute-done.17 = bf16[67584]{0:T(1024)(128)(2,1)S(1)} collective-permute-done((bf16[67584]{0:T(1024)(128)(2,1)S(1)}, bf16[67584]{0:T(1024)(128)(2,1)S(1)}, u32[]{:S(2)}, u32[]{:S(2)}) %collective-permute-start.17) | collective-permute-done | bytes 135200 | tf_op jit(solution)/shard_map/ppermute | solution.py:231
  137.3 0.9 pad_maximum_fusion.4
  138.5 0.9 collective-permute-done.9
  139.5 0.9 rev.7
  140.4 0.9 pad_maximum_fusion.8
  141.3 1.2 broadcast_select_fusion.1
  142.9 0.6 convert_multiply_fusion.99
  143.7 0.6 convert_multiply_fusion.100
  144.4 1.1 mul.1868
  145.5 1.1 convert_multiply_fusion.98
  (370 shorter events, 11.5 us)
Async XLA Ops:
  0.6 35.6 %copy-start = (bf16[1024,256]{1,0:T(8,128)(2,1)S(1)}, bf16[1024,256]{1,0:T(8,128)(2,1)}, u32[]{:S(2)}) copy-start(bf16[1024,256]{1,0:T(8,128)(2,1)} %param.23) | copy-start | bytes 1572868
  0.7 22.2 %copy-start.4 = (bf16[4,8,32,256]{3,2,1,0:T(8,128)(2,1)S(1)}, bf16[4,8,32,256]{3,2,1,0:T(8,128)(2,1)}, u32[]{:S(2)}) copy-start(bf16[4,8,32,256]{3,2,1,0:T(8,128)(2,1)} %param.13) | copy-start | bytes 1572868
  0.7 18.3 %copy-start.25 = (s32[8,32]{1,0:T(8,128)S(1)}, s32[8,32]{1,0:T(8,128)}, u32[]{:S(2)}) copy-start(s32[8,32]{1,0:T(8,128)} %param.16) | copy-start | bytes 3076
  1.7 11.2 %collective-permute-start = (bf16[4,8,3,256]{3,2,1,0:T(4,128)(2,1)S(1)}, bf16[4,8,3,256]{3,2,1,0:T(4,128)(2,1)S(1)}, u32[]{:S(2)}, u32[]{:S(2)}) collective-permute-start(bf16[4,8,3,256]{3,2,1,0:T(4,128)(2,1)S(1)} %slice.712), channel_id=1, source_target_pairs={{0,15},{1,14},{2,13},{3,12},{4,11},{5,10},{6,9},{7,8},{8,7},{9,6},... | collective-permute-start | bytes 147464 | tf_op jit(solution)/shard_map/ppermute | solution.py:174
  8.8 15.4 %copy-start.28 = (f32[1,1,256]{2,1,0:T(1,128)}, f32[1,1,256]{2,1,0:T(1,128)S(1)}, u32[]{:S(2)}) copy-start(f32[1,1,256]{2,1,0:T(1,128)S(1)} %get-tuple-element.133) | copy-start | bytes 3076
  8.8 15.4 %copy-start.30 = (f32[1,1,256]{2,1,0:T(1,128)}, f32[1,1,256]{2,1,0:T(1,128)S(1)}, u32[]{:S(2)}) copy-start(f32[1,1,256]{2,1,0:T(1,128)S(1)} %get-tuple-element.134) | copy-start | bytes 3076
  8.8 15.4 %copy-start.32 = (f32[1,1,256]{2,1,0:T(1,128)}, f32[1,1,256]{2,1,0:T(1,128)S(1)}, u32[]{:S(2)}) copy-start(f32[1,1,256]{2,1,0:T(1,128)S(1)} %get-tuple-element.135) | copy-start | bytes 3076
  8.8 15.4 %copy-start.34 = (f32[1,1,256]{2,1,0:T(1,128)}, f32[1,1,256]{2,1,0:T(1,128)S(1)}, u32[]{:S(2)}) copy-start(f32[1,1,256]{2,1,0:T(1,128)S(1)} %get-tuple-element.136) | copy-start | bytes 3076
  8.8 15.4 %copy-start.36 = (f32[1,1,256]{2,1,0:T(1,128)}, f32[1,1,256]{2,1,0:T(1,128)S(1)}, u32[]{:S(2)}) copy-start(f32[1,1,256]{2,1,0:T(1,128)S(1)} %get-tuple-element.137) | copy-start | bytes 3076
  8.8 15.4 %copy-start.38 = (f32[1,1,256]{2,1,0:T(1,128)}, f32[1,1,256]{2,1,0:T(1,128)S(1)}, u32[]{:S(2)}) copy-start(f32[1,1,256]{2,1,0:T(1,128)S(1)} %get-tuple-element.138) | copy-start | bytes 3076
  8.9 15.4 %copy-start.40 = (f32[1,1,256]{2,1,0:T(1,128)}, f32[1,1,256]{2,1,0:T(1,128)S(1)}, u32[]{:S(2)}) copy-start(f32[1,1,256]{2,1,0:T(1,128)S(1)} %get-tuple-element.139) | copy-start | bytes 3076
  8.9 15.4 %copy-start.42 = (f32[1,1,256]{2,1,0:T(1,128)}, f32[1,1,256]{2,1,0:T(1,128)S(1)}, u32[]{:S(2)}) copy-start(f32[1,1,256]{2,1,0:T(1,128)S(1)} %get-tuple-element.140) | copy-start | bytes 3076
  14.4 8.5 %collective-permute-start.1 = (bf16[4,3,38,256]{3,2,1,0:T(8,128)(2,1)S(1)}, bf16[4,3,38,256]{3,2,1,0:T(8,128)(2,1)S(1)}, u32[]{:S(2)}, u32[]{:S(2)}) collective-permute-start(bf16[4,3,38,256]{3,2,1,0:T(8,128)(2,1)S(1)} %get-tuple-element.119), channel_id=1, source_target_pairs={{0,1},{1,2},{2,3},{3,4},{4,5},{5,6},{6,7},{7,8},{8,9},{9,10},{10,1... | collective-permute-start | bytes 700424 | tf_op jit(solution)/shard_map/ppermute | solution.py:26
  15.1 7.8 %collective-permute-start.2 = (bf16[4,3,38,256]{3,2,1,0:T(8,128)(2,1)S(1)}, bf16[4,3,38,256]{3,2,1,0:T(8,128)(2,1)}, u32[]{:S(2)}, u32[]{:S(2)}) collective-permute-start(bf16[4,3,38,256]{3,2,1,0:T(8,128)(2,1)S(1)} %get-tuple-element.120), channel_id=1, source_target_pairs={{1,0},{2,1},{3,2},{4,3},{5,4},{6,5},{7,6},{8,7},{9,8},{10,9},{11,1... | collective-permute-start | bytes 700424 | tf_op jit(solution)/shard_map/ppermute | solution.py:27
  24.7 9.7 %copy-start.27 = (f32[256]{0:T(256)S(1)}, f32[256]{0:T(256)}, u32[]{:S(2)}) copy-start(f32[256]{0:T(256)} %param.19) | copy-start | bytes 3076
  42.6 12.4 %copy-start.11 = (f32[8,32,256]{2,1,0:T(8,128)}, f32[8,32,256]{2,1,0:T(8,128)S(1)}, u32[]{:S(2)}) copy-start(f32[8,32,256]{2,1,0:T(8,128)S(1)} %get-tuple-element.87) | copy-start | bytes 786436
  42.6 12.4 %copy-start.13 = (f32[8,32,256]{2,1,0:T(8,128)}, f32[8,32,256]{2,1,0:T(8,128)S(1)}, u32[]{:S(2)}) copy-start(f32[8,32,256]{2,1,0:T(8,128)S(1)} %get-tuple-element.88) | copy-start | bytes 786436
  42.6 12.4 %copy-start.15 = (f32[8,32,256]{2,1,0:T(8,128)}, f32[8,32,256]{2,1,0:T(8,128)S(1)}, u32[]{:S(2)}) copy-start(f32[8,32,256]{2,1,0:T(8,128)S(1)} %get-tuple-element.89) | copy-start | bytes 786436
  42.6 12.4 %copy-start.17 = (f32[8,32,256]{2,1,0:T(8,128)}, f32[8,32,256]{2,1,0:T(8,128)S(1)}, u32[]{:S(2)}) copy-start(f32[8,32,256]{2,1,0:T(8,128)S(1)} %get-tuple-element.90) | copy-start | bytes 786436
  57.0 3.4 %collective-permute-start.3 = (f32[270336]{0:T(1024)}, f32[270336]{0:T(1024)}, u32[]{:S(2)}, u32[]{:S(2)}) collective-permute-start(f32[270336]{0:T(1024)} %pad_dynamic-slice_fusion), channel_id=1, source_target_pairs={{0,1},{1,0},{2,3},{3,2},{4,5},{5,4},{6,7},{7,6},{8,9},{9,8},{10,11... | collective-permute-start | bytes 3244040 | tf_op jit(solution)/shard_map/ppermute | solution.py:218
  57.7 5.4 %copy-start.7 = (f32[4,8,32,256]{3,2,1,0:T(8,128)S(1)}, f32[4,8,32,256]{3,2,1,0:T(8,128)}, u32[]{:S(2)}) copy-start(f32[4,8,32,256]{3,2,1,0:T(8,128)} %get-tuple-element.17) | copy-start | bytes 3145732
  67.5 6.3 %copy-start.1 = (f32[4,8,32,256]{3,2,1,0:T(8,128)}, f32[4,8,32,256]{3,2,1,0:T(8,128)S(1)}, u32[]{:S(2)}) copy-start(f32[4,8,32,256]{3,2,1,0:T(8,128)S(1)} %get-tuple-element.86) | copy-start | bytes 3145732
  73.9 5.4 %copy-start.126 = (f32[256]{0:T(256)S(1)}, f32[256]{0:T(256)}, u32[]{:S(2)}) copy-start(f32[256]{0:T(256)} %get-tuple-element.34) | copy-start | bytes 3076
  73.9 5.4 %copy-start.127 = (f32[256]{0:T(256)S(1)}, f32[256]{0:T(256)}, u32[]{:S(2)}) copy-start(f32[256]{0:T(256)} %get-tuple-element.35) | copy-start | bytes 3076
  73.9 5.4 %copy-start.128 = (f32[256]{0:T(256)S(1)}, f32[256]{0:T(256)}, u32[]{:S(2)}) copy-start(f32[256]{0:T(256)} %get-tuple-element.36) | copy-start | bytes 3076
  73.9 5.4 %copy-start.129 = (f32[256]{0:T(256)S(1)}, f32[256]{0:T(256)}, u32[]{:S(2)}) copy-start(f32[256]{0:T(256)} %get-tuple-element.37) | copy-start | bytes 3076
  73.9 5.4 %copy-start.130 = (f32[256]{0:T(256)S(1)}, f32[256]{0:T(256)}, u32[]{:S(2)}) copy-start(f32[256]{0:T(256)} %get-tuple-element.38) | copy-start | bytes 3076
  73.9 5.4 %copy-start.131 = (f32[256]{0:T(256)S(1)}, f32[256]{0:T(256)}, u32[]{:S(2)}) copy-start(f32[256]{0:T(256)} %get-tuple-element.39) | copy-start | bytes 3076
  73.9 5.4 %copy-start.132 = (f32[256]{0:T(256)S(1)}, f32[256]{0:T(256)}, u32[]{:S(2)}) copy-start(f32[256]{0:T(256)} %get-tuple-element.40) | copy-start | bytes 3076
  73.9 5.4 %copy-start.119 = (f32[256]{0:T(256)S(1)}, f32[256]{0:T(256)}, u32[]{:S(2)}) copy-start(f32[256]{0:T(256)} %get-tuple-element.27) | copy-start | bytes 3076
  73.9 5.4 %copy-start.120 = (f32[256]{0:T(256)S(1)}, f32[256]{0:T(256)}, u32[]{:S(2)}) copy-start(f32[256]{0:T(256)} %get-tuple-element.28) | copy-start | bytes 3076
  73.9 5.4 %copy-start.121 = (f32[256]{0:T(256)S(1)}, f32[256]{0:T(256)}, u32[]{:S(2)}) copy-start(f32[256]{0:T(256)} %get-tuple-element.29) | copy-start | bytes 3076
  74.0 5.4 %copy-start.122 = (f32[256]{0:T(256)S(1)}, f32[256]{0:T(256)}, u32[]{:S(2)}) copy-start(f32[256]{0:T(256)} %get-tuple-element.30) | copy-start | bytes 3076
  74.0 5.4 %copy-start.123 = (f32[256]{0:T(256)S(1)}, f32[256]{0:T(256)}, u32[]{:S(2)}) copy-start(f32[256]{0:T(256)} %get-tuple-element.31) | copy-start | bytes 3076
  74.0 5.4 %copy-start.124 = (f32[256]{0:T(256)S(1)}, f32[256]{0:T(256)}, u32[]{:S(2)}) copy-start(f32[256]{0:T(256)} %get-tuple-element.32) | copy-start | bytes 3076
  74.0 5.4 %copy-start.125 = (f32[256]{0:T(256)S(1)}, f32[256]{0:T(256)}, u32[]{:S(2)}) copy-start(f32[256]{0:T(256)} %get-tuple-element.33) | copy-start | bytes 3076
  74.0 5.4 %copy-start.113 = (f32[256]{0:T(256)S(1)}, f32[256]{0:T(256)}, u32[]{:S(2)}) copy-start(f32[256]{0:T(256)} %get-tuple-element.21) | copy-start | bytes 3076
  74.0 5.4 %copy-start.114 = (f32[256]{0:T(256)S(1)}, f32[256]{0:T(256)}, u32[]{:S(2)}) copy-start(f32[256]{0:T(256)} %get-tuple-element.22) | copy-start | bytes 3076
  74.0 5.4 %copy-start.115 = (f32[256]{0:T(256)S(1)}, f32[256]{0:T(256)}, u32[]{:S(2)}) copy-start(f32[256]{0:T(256)} %get-tuple-element.23) | copy-start | bytes 3076
  74.0 5.4 %copy-start.116 = (f32[256]{0:T(256)S(1)}, f32[256]{0:T(256)}, u32[]{:S(2)}) copy-start(f32[256]{0:T(256)} %get-tuple-element.24) | copy-start | bytes 3076
  74.0 5.4 %copy-start.117 = (f32[256]{0:T(256)S(1)}, f32[256]{0:T(256)}, u32[]{:S(2)}) copy-start(f32[256]{0:T(256)} %get-tuple-element.25) | copy-start | bytes 3076
  74.0 5.4 %copy-start.118 = (f32[256]{0:T(256)S(1)}, f32[256]{0:T(256)}, u32[]{:S(2)}) copy-start(f32[256]{0:T(256)} %get-tuple-element.26) | copy-start | bytes 3076
  74.1 5.6 %copy-start.10 = (f32[270336]{0:T(1024)S(1)}, f32[270336]{0:T(1024)}, u32[]{:S(2)}) copy-start(f32[270336]{0:T(1024)} %fusion.51) | copy-start | bytes 3244036
  74.5 24.4 %collective-permute-start.7 = (f32[4,3,32,256]{3,2,1,0:T(8,128)}, f32[4,3,32,256]{3,2,1,0:T(8,128)}, u32[]{:S(2)}, u32[]{:S(2)}) collective-permute-start(f32[4,3,32,256]{3,2,1,0:T(8,128)} %get-tuple-element.113), channel_id=1, source_target_pairs={{0,1},{1,2},{2,3},{3,4},{4,5},{5,6},{6,7},{7,8},{8,9},{9,10},{10,1... | collective-permute-start | bytes 1179656 | tf_op jit(solution)/shard_map/ppermute | solution.py:26
  74.9 24.0 %collective-permute-start.8 = (f32[4,3,32,256]{3,2,1,0:T(8,128)}, f32[4,3,32,256]{3,2,1,0:T(8,128)}, u32[]{:S(2)}, u32[]{:S(2)}) collective-permute-start(f32[4,3,32,256]{3,2,1,0:T(8,128)} %get-tuple-element.114), channel_id=1, source_target_pairs={{1,0},{2,1},{3,2},{4,3},{5,4},{6,5},{7,6},{8,7},{9,8},{10,9},{11,1... | collective-permute-start | bytes 1179656 | tf_op jit(solution)/shard_map/ppermute | solution.py:27
  79.6 19.3 %copy-start.2 = (f32[4,8,32,256]{3,2,1,0:T(8,128)S(1)}, f32[4,8,32,256]{3,2,1,0:T(8,128)}, u32[]{:S(2)}) copy-start(f32[4,8,32,256]{3,2,1,0:T(8,128)} %copy-done.1) | copy-start | bytes 3145732
  79.6 1.3 collective-permute-start.10
  79.7 18.6 %collective-permute-start.4 = (f32[67584]{0:T(1024)S(1)}, f32[67584]{0:T(1024)S(1)}, u32[]{:S(2)}, u32[]{:S(2)}) collective-permute-start(f32[67584]{0:T(1024)S(1)} %get-tuple-element.110), channel_id=1, source_target_pairs={{0,2},{1,3},{2,0},{3,1},{4,6},{5,7},{6,4},{7,5},{8,10},{9,11},{10,... | collective-permute-start | bytes 811016 | tf_op jit(solution)/shard_map/ppermute | solution.py:218
  79.8 18.6 %collective-permute-start.5 = (f32[67584]{0:T(1024)S(1)}, f32[67584]{0:T(1024)S(1)}, u32[]{:S(2)}, u32[]{:S(2)}) collective-permute-start(f32[67584]{0:T(1024)S(1)} %get-tuple-element.112), channel_id=1, source_target_pairs={{0,4},{1,5},{2,6},{3,7},{4,0},{5,1},{6,2},{7,3},{8,12},{9,13},{10,... | collective-permute-start | bytes 811016 | tf_op jit(solution)/shard_map/ppermute | solution.py:218
  80.9 17.5 %collective-permute-start.6 = (f32[67584]{0:T(1024)S(1)}, f32[67584]{0:T(1024)S(1)}, u32[]{:S(2)}, u32[]{:S(2)}) collective-permute-start(f32[67584]{0:T(1024)S(1)} %get-tuple-element.111), channel_id=1, source_target_pairs={{0,6},{1,7},{2,4},{3,5},{4,2},{5,3},{6,0},{7,1},{8,14},{9,15},{10,... | collective-permute-start | bytes 811016 | tf_op jit(solution)/shard_map/ppermute | solution.py:218
  98.4 12.8 %collective-permute-start.11 = (f32[12800]{0:T(1024)S(1)}, f32[12800]{0:T(1024)S(1)}, u32[]{:S(2)}, u32[]{:S(2)}) collective-permute-start(f32[12800]{0:T(1024)S(1)} %fusion.262), channel_id=1, source_target_pairs={{0,2},{1,3},{2,0},{3,1},{4,6},{5,7},{6,4},{7,5},{8,10},{9,11},{10,... | collective-permute-start | bytes 153608 | tf_op jit(solution)/shard_map/ppermute | solution.py:16
  110.9 11.8 %collective-permute-start.14 = (f32[33792]{0:T(1024)S(1)}, f32[33792]{0:T(1024)S(1)}, u32[]{:S(2)}, u32[]{:S(2)}) collective-permute-start(f32[33792]{0:T(1024)S(1)} %dynamic_slice.31), channel_id=1, source_target_pairs={{0,8},{1,9},{2,10},{3,11},{4,12},{5,13},{6,14},{7,15},{8,0},{9,1},... | collective-permute-start | bytes 405512 | tf_op jit(solution)/shard_map/ppermute | solution.py:218
  111.1 4.6 %collective-permute-start.12 = (f32[12800]{0:T(1024)S(1)}, f32[12800]{0:T(1024)S(1)}, u32[]{:S(2)}, u32[]{:S(2)}) collective-permute-start(f32[12800]{0:T(1024)S(1)} %add.802), channel_id=1, source_target_pairs={{0,4},{1,5},{2,6},{3,7},{4,0},{5,1},{6,2},{7,3},{8,12},{9,13},{10,... | collective-permute-start | bytes 153608 | tf_op jit(solution)/shard_map/ppermute | solution.py:16
  115.7 7.0 %collective-permute-start.13 = (f32[12800]{0:T(1024)S(1)}, f32[12800]{0:T(1024)S(1)}, u32[]{:S(2)}, u32[]{:S(2)}) collective-permute-start(f32[12800]{0:T(1024)S(1)} %add.803), channel_id=1, source_target_pairs={{0,8},{1,9},{2,10},{3,11},{4,12},{5,13},{6,14},{7,15},{8,0},{9,1},... | collective-permute-start | bytes 153608 | tf_op jit(solution)/shard_map/ppermute | solution.py:16
  122.8 5.9 %collective-permute-start.15 = (bf16[33792]{0:T(1024)(128)(2,1)S(1)}, bf16[33792]{0:T(1024)(128)(2,1)S(1)}, u32[]{:S(2)}, u32[]{:S(2)}) collective-permute-start(bf16[33792]{0:T(1024)(128)(2,1)S(1)} %add_convert_fusion.1), channel_id=1, source_target_pairs={{0,8},{1,9},{2,10},{3,11},{4,12},{5,13},{6,14},{7,15},{8,0},{9,1},... | collective-permute-start | bytes 202760 | tf_op jit(solution)/shard_map/ppermute | solution.py:231
  128.7 9.5 %copy-start.12 = (f32[8,32,256]{2,1,0:T(8,128)S(1)}, f32[8,32,256]{2,1,0:T(8,128)}, u32[]{:S(2)}) copy-start(f32[8,32,256]{2,1,0:T(8,128)} %copy-done.11) | copy-start | bytes 786436
  128.7 9.5 %copy-start.14 = (f32[8,32,256]{2,1,0:T(8,128)S(1)}, f32[8,32,256]{2,1,0:T(8,128)}, u32[]{:S(2)}) copy-start(f32[8,32,256]{2,1,0:T(8,128)} %copy-done.13) | copy-start | bytes 786436
  128.7 9.5 %copy-start.16 = (f32[8,32,256]{2,1,0:T(8,128)S(1)}, f32[8,32,256]{2,1,0:T(8,128)}, u32[]{:S(2)}) copy-start(f32[8,32,256]{2,1,0:T(8,128)} %copy-done.15) | copy-start | bytes 786436
  128.7 9.5 %copy-start.18 = (f32[8,32,256]{2,1,0:T(8,128)S(1)}, f32[8,32,256]{2,1,0:T(8,128)}, u32[]{:S(2)}) copy-start(f32[8,32,256]{2,1,0:T(8,128)} %copy-done.17) | copy-start | bytes 786436
  128.7 6.5 %collective-permute-start.16 = (bf16[67584]{0:T(1024)(128)(2,1)S(1)}, bf16[67584]{0:T(1024)(128)(2,1)S(1)}, u32[]{:S(2)}, u32[]{:S(2)}) collective-permute-start(bf16[67584]{0:T(1024)(128)(2,1)S(1)} %pad_maximum_fusion.12), channel_id=1, source_target_pairs={{0,4},{1,5},{2,6},{3,7},{4,0},{5,1},{6,2},{7,3},{8,12},{9,13},{10,... | collective-permute-start | bytes 405512 | tf_op jit(solution)/shard_map/ppermute | solution.py:231
  128.8 8.3 %collective-permute-start.17 = (bf16[67584]{0:T(1024)(128)(2,1)S(1)}, bf16[67584]{0:T(1024)(128)(2,1)S(1)}, u32[]{:S(2)}, u32[]{:S(2)}) collective-permute-start(bf16[67584]{0:T(1024)(128)(2,1)S(1)} %pad_maximum_fusion.12), channel_id=1, source_target_pairs={{0,2},{1,3},{2,0},{3,1},{4,6},{5,7},{6,4},{7,5},{8,10},{9,11},{10,... | collective-permute-start | bytes 405512 | tf_op jit(solution)/shard_map/ppermute | solution.py:231
  129.9 7.2 %collective-permute-start.18 = (bf16[67584]{0:T(1024)(128)(2,1)S(1)}, bf16[67584]{0:T(1024)(128)(2,1)S(1)}, u32[]{:S(2)}, u32[]{:S(2)}) collective-permute-start(bf16[67584]{0:T(1024)(128)(2,1)S(1)} %pad_maximum_fusion.12), channel_id=1, source_target_pairs={{0,6},{1,7},{2,4},{3,5},{4,2},{5,3},{6,0},{7,1},{8,14},{9,15},{10,... | collective-permute-start | bytes 405512 | tf_op jit(solution)/shard_map/ppermute | solution.py:231
  132.9 6.6 %collective-permute-start.9 = (bf16[4,8,3,256]{3,2,1,0:T(4,128)(2,1)S(1)}, bf16[4,8,3,256]{3,2,1,0:T(4,128)(2,1)}, u32[]{:S(2)}, u32[]{:S(2)}) collective-permute-start(bf16[4,8,3,256]{3,2,1,0:T(4,128)(2,1)S(1)} %slice.1493), channel_id=1, source_target_pairs={{0,15},{1,14},{2,13},{3,12},{4,11},{5,10},{6,9},{7,8},{8,7},{9,6},... | collective-permute-start | bytes 147464 | tf_op jit(solution)/shard_map/ppermute | solution.py:174
  138.2 3.1 %collective-permute-start.19 = (bf16[270336]{0:T(1024)(128)(2,1)}, bf16[270336]{0:T(1024)(128)(2,1)}, u32[]{:S(2)}, u32[]{:S(2)}) collective-permute-start(bf16[270336]{0:T(1024)(128)(2,1)} %pad_maximum_fusion.4), channel_id=1, source_target_pairs={{0,1},{1,0},{2,3},{3,2},{4,5},{5,4},{6,7},{7,6},{8,9},{9,8},{10,11... | collective-permute-start | bytes 1622024 | tf_op jit(solution)/shard_map/ppermute | solution.py:231
  (97 other events, 326.5 us)

commit v12 on v11

--- a/solution.py
+++ b/solution.py
@@ -202,13 +202,16 @@
     return cur.astype(flat.dtype)
 
 
-def radix_allreduce(flat, axis, gather_dtype, operand, work):
+def radix_allreduce(flat, axis, gather_dtype, operand, start, finish):
     size = lax.axis_size(axis)
     nbits = size.bit_length() - 1
     groups = [[0]] + [list(range(b, min(b + 2, nbits))) for b in range(1, nbits, 2)]
     idx = lax.axis_index(axis)
     cur = flat
     for bits in groups:
+        if bits == groups[1]:
+            cur, handoff = lax.optimization_barrier((cur, first[0]))
+            second = finish(handoff)
         radix, low = 1 << len(bits), bits[0]
         sub = (idx >> low) & (radix - 1)
         part = cur.shape[0] // radix
@@ -219,10 +222,9 @@
         cur = total
         if bits == groups[0]:
             cur, operand = lax.optimization_barrier((cur, operand))
-            result = work(operand)
+            first = start(operand)
         elif bits == groups[1]:
-            cur, first = lax.optimization_barrier((cur, result[0]))
-            result = (first,) + tuple(result[1:])
+            cur, second = lax.optimization_barrier((cur, second))
     cur = cur.astype(gather_dtype)
     for bits in reversed(groups):
         radix, low = 1 << len(bits), bits[0]
@@ -238,7 +240,7 @@
                 pick = jnp.where(sub == s, pieces[p ^ s], pick)
             placed.append(pick)
         cur = jnp.concatenate(placed)
-    return cur.astype(flat.dtype), result
+    return cur.astype(flat.dtype), first[1:], second
 
 
 def butterfly_allreduce(flat, axis):
@@ -288,6 +290,9 @@
     def backward(grad_normed):
         grad_depth, kernel_sum, dw_bias_sum = depth_backward(grad_normed)
         grad_halo = with_halo(grad_depth, (("lon", 1),), 3)
+        return grad_halo, kernel_sum, dw_bias_sum
+
+    def backward_conv(grad_halo):
         padded = jnp.pad(grad_halo, ((0, 0), (0, 0), (6, 6), (0, 0)))
         grad_ext = jnp.zeros((members, lon_dev, lat_rows + 6, chans), jnp.float32)
         for lon_off in range(7):
@@ -302,11 +307,11 @@
                         :,
                     ]
                 )
-        return grad_ext, kernel_sum, dw_bias_sum
+        return grad_ext
 
     lon_size = lax.axis_size("lon")
-    reduced, (grad_ext, kernel_sum, dw_bias_sum) = radix_allreduce(
-        pack(sums, lon_size * 1024), "lon", jnp.bfloat16, grad_normed, backward
+    reduced, (kernel_sum, dw_bias_sum), grad_ext = radix_allreduce(
+        pack(sums, lon_size * 1024), "lon", jnp.bfloat16, grad_normed, backward, backward_conv
     )
     gain_sum, bias_sum, w_in_sum, b_in_sum, w_out_sum, b_out_sum, scale_sum = unpack(reduced, sums)
     small = (kernel_sum, dw_bias_sum)

time: 147 us -> 138 us (0.939)
  waiting for transfers between devices: 37 us -> 28.1 us
  starting transfers between devices: 28.7 us -> 31 us
  other arithmetic: 49.5 us -> 47.6 us
    ppermute x5, waiting for transfers between devices: 17.7 us -> 4.43 us  [radix_allreduce(): lax.ppermute(send, axis, [(i, i ^ d << low) for i in range(size)])]
    ppermute x2, waiting for transfers between devices: 3.45 us -> 8.91 us  [with_halo(): before = lax.ppermute(last, axis, up)]
    ppermute x5, starting transfers between devices: 3.41 us -> 6.99 us  [radix_allreduce(): lax.ppermute(send, axis, [(i, i ^ d << low) for i in range(size)])]
    ppermute x4, starting transfers between devices: 5.48 us -> 3.9 us  [swapped(): lax.ppermute(x, axis, [(i, i ^ 1 << bit) for i in range(lax.axis_size(axi...]
    unnamed x294 -> x272, local copies, waits for them, and re-layouts: 4.79 us -> 4.29 us
  transfers between devices with their start and end apart: 20 -> 20, of which waited for: 10 -> 10; matrix products, arithmetic and copies ran while one was open for 15% -> 16% of each run, Pallas kernels for 0% -> 0%
where the time goes in v12:
time: 138 us
  other arithmetic  47.6 us (34%)
  starting transfers between devices  31 us (22%)
  waiting for transfers between devices  28.1 us (20%)
  local copies, waits for them, and re-layouts  16.2 us (12%)
  matrix products  11.8 us (9%)
  between operations  3.08 us (2%)
    add x1, other arithmetic, backward_conv(): grad_ext + dw_kernel[lon_off, lat_off] * padded[:, 6 - lon_off:6 - lon_of...  10.2 us
    reduce_sum x1, other arithmetic, local_step(): mean_val = jnp.mean(depth, axis=-1, keepdims=True)  9.29 us
    ppermute x2, waiting for transfers between devices, with_halo(): before = lax.ppermute(last, axis, up)  8.91 us
    ppermute x5, waiting for transfers between devices, radix_allreduce(): lax.ppermute(cur, axis, [(i, i ^ d << low) for i in range(size)])  8.75 us
    reduce_sum x4, other arithmetic, depth_backward(): jnp.sum(grad_depth * extended[:, lon_off:lon_off + lon_dev, lat_off:lat_o...  8.53 us
    ppermute x2, starting transfers between devices, with_halo(): after = lax.ppermute(leading, axis, down)  8.05 us
    ppermute x5, starting transfers between devices, radix_allreduce(): lax.ppermute(send, axis, [(i, i ^ d << low) for i in range(size)])  6.99 us
    ppermute x4, waiting for transfers between devices, swapped(): lax.ppermute(x, axis, [(i, i ^ 1 << bit) for i in range(lax.axis_size(axi...  6.01 us
  transfers between devices with their start and end apart: 20, of which 10 were waited for; matrix products, arithmetic and copies ran while one was open for 16% of the time, Pallas kernels for 0%

profile of v12, /device:TPU:0, one launch (start us, length us, event | category | flops | bytes accessed | tf_op | source)
XLA Modules:
  0.0 137.6 jit_solution(3338140393798064531)
XLA Ops:
  0.7 1.0 slice.712
  1.7 5.5 %collective-permute-start = (bf16[4,8,3,256]{3,2,1,0:T(4,128)(2,1)S(1)}, bf16[4,8,3,256]{3,2,1,0:T(4,128)(2,1)S(1)}, u32[]{:S(2)}, u32[]{:S(2)}) collective-permute-start(bf16[4,8,3,256]{3,2,1,0:T(4,128)(2,1)S(1)} %slice.712), channel_id=1, source_target_pairs={{0,15},{1,14},{2,13},{3,12},{4,11},{5,10},{6,9},{7,8},{8,7},{9,6},... | collective-permute-start | bytes 147464 | tf_op jit(solution)/shard_map/ppermute | solution.py:174
  7.2 1.6 %fusion.263 = (f32[1,1,256]{2,1,0:T(1,128)S(1)}, f32[1,1,256]{2,1,0:T(1,128)S(1)}, f32[1,1,256]{2,1,0:T(1,128)S(1)}, f32[1,1,256]{2,1,0:T(1,128)S(1)}, f32[1,1,2...) fusion(f32[7,7,256]{2,1,0:T(8,128)} %param.17), kind=kLoop, calls=%fused_computation.543 | loop fusion | bytes 38912 | tf_op jit(solution)/shard_map/slice | solution.py:59
  8.9 1.7 %fusion.264 = (f32[1,1,256]{2,1,0:T(1,128)}, f32[1,1,256]{2,1,0:T(1,128)}, f32[1,1,256]{2,1,0:T(1,128)}, f32[1,1,256]{2,1,0:T(1,128)}, f32[1,1,256]{2,1,0:T(1,12...) fusion(f32[7,7,256]{2,1,0:T(8,128)} %param.17), kind=kLoop, calls=%fused_computation.544 | loop fusion | bytes 38912 | tf_op jit(solution)/shard_map/slice | solution.py:59
  10.6 1.5 %fusion.265 = (f32[1,1,256]{2,1,0:T(1,128)}, f32[1,1,256]{2,1,0:T(1,128)}, f32[1,1,256]{2,1,0:T(1,128)}, f32[1,1,256]{2,1,0:T(1,128)}, f32[1,1,256]{2,1,0:T(1,12...) fusion(f32[7,7,256]{2,1,0:T(8,128)} %param.17), kind=kLoop, calls=%fused_computation.545 | loop fusion | bytes 22528 | tf_op jit(solution)/shard_map/slice | solution.py:59
  12.1 0.8 copy.25
  13.1 1.3 pad_maximum_fusion.12
  14.4 0.7 collective-permute-start.1
  15.1 3.8 %collective-permute-start.2 = (bf16[4,3,38,256]{3,2,1,0:T(8,128)(2,1)S(1)}, bf16[4,3,38,256]{3,2,1,0:T(8,128)(2,1)}, u32[]{:S(2)}, u32[]{:S(2)}) collective-permute-start(bf16[4,3,38,256]{3,2,1,0:T(8,128)(2,1)S(1)} %get-tuple-element.124), channel_id=1, source_target_pairs={{1,0},{2,1},{3,2},{4,3},{5,4},{6,5},{7,6},{8,7},{9,8},{10,9},{11,1... | collective-permute-start | bytes 700424 | tf_op jit(solution)/shard_map/ppermute | solution.py:27
  19.4 3.5 %collective-permute-done.1 = bf16[4,3,38,256]{3,2,1,0:T(8,128)(2,1)S(1)} collective-permute-done((bf16[4,3,38,256]{3,2,1,0:T(8,128)(2,1)S(1)}, bf16[4,3,38,256]{3,2,1,0:T(8,128)(2,1)S(1)}, u32[]{:S(2)}, u32[]{:S(2)}) %collective-permute-start.1) | collective-permute-done | bytes 233504 | tf_op jit(solution)/shard_map/ppermute | solution.py:26
  22.9 1.3 maximum_maximum_fusion
  24.7 9.3 %fusion.258 = (f32[4,8,32]{2,1,0:T(8,128)S(1)}, f32[4,8,32,256]{3,2,1,0:T(8,128)S(1)}) fusion(bf16[4,11,38,256]{3,2,1,0:T(8,128)(2,1)S(1)} %get-tuple-element.122, f32[256]{0:T(256)} %bitcast.432, f32[256]{0:T(256)} %bitcast.434, f32[256]{0:T(256)S(1)} %bitcast.340, f32[256]{0:T(256)S(1)} %bitcast.342, f32[256]{0:T(256)S(1)} %bitcast.344, ...), kind=kLoop, calls=%fused_computation.539 | loop fusion | flops 43514880 | bytes 23746560 | tf_op jit(solution)/shard_map/reduce_sum | solution.py:62
  34.4 1.1 add_convert_fusion
  39.0 1.1 fusion.256
  40.1 2.5 %multiply_reduce_fusion.7 = (f32[256]{0:T(256)S(1)}, f32[256]{0:T(256)S(1)}, f32[256]{0:T(256)S(1)}, f32[256]{0:T(256)S(1)}, f32[8,32,256]{2,1,0:T(8,128)S(1)}, ...) fusion(f32[256]{0:T(256)S(1)} %copy-done.26, ...), kind=kLoop, calls=%fused_computation.479 | loop fusion | flops 7863296 | bytes 2497536 | tf_op jit(solution)/shard_map/reduce_sum | solution.py:117
  42.7 0.6 fusion.247
  43.3 0.9 fusion.250
  44.9 0.9 fusion.248
  45.8 0.6 convolution_add_fusion.2
  46.4 0.9 fusion.252
  47.3 0.6 convolution_add_fusion.1
  47.9 0.9 fusion.254
  48.9 0.6 fusion
  49.5 0.8 copy.28
  52.5 1.3 pad_maximum_fusion.3
  53.8 0.7 copy-done.8
  55.3 1.2 pad_dynamic-slice_fusion
  56.5 0.5 copy-done.9
  57.0 0.7 collective-permute-start.3
  57.6 2.7 %collective-permute-done.3 = f32[270336]{0:T(1024)} collective-permute-done((f32[270336]{0:T(1024)}, f32[270336]{0:T(1024)}, u32[]{:S(2)}, u32[]{:S(2)}) %collective-permute-start.3) | collective-permute-done | bytes 1081376 | tf_op jit(solution)/shard_map/ppermute | solution.py:221
  60.3 2.7 %fusion.99 = f32[270336]{0:T(1024)} fusion(f32[270336]{0:T(1024)} %collective-permute-done.3, s32[]{:T(128)S(6)} %select_n.114, f32[526336]{0:T(1024)} %copy-done.9), kind=kLoop, calls=%fused_computation.272 | loop fusion | flops 270336 | bytes 4268036 | tf_op jit(solution)/shard_map/add | solution.py:221
  63.0 0.6 multiply_reduce_fusion.4
  63.7 3.8 %fusion.196 = (f32[256]{0:T(256)S(1)}, f32[256]{0:T(256)}, f32[256]{0:T(256)}, f32[256]{0:T(256)}, f32[256]{0:T(256)}, /*index=5*/f32[256]{0:T(256)}, f32[256]{0...) fusion(bf16[4,11,38,256]{3,2,1,0:T(8,128)(2,1)S(1)} %get-tuple-, ...), kind=kLoop, calls=%fused_computation.370 | loop fusion | flops 15986176 | bytes 12618752 | tf_op jit(solution)/shard_map/reduce_sum | solution.py:156
  67.5 1.8 %fusion.178 = (f32[256]{0:T(256)S(1)}, f32[256]{0:T(256)S(1)}, f32[256]{0:T(256)S(1)}, f32[256]{0:T(256)S(1)}, f32[256]{0:T(256)S(1)}, /*index=5*/f32[256]{0:T(2...) fusion(f32[4,8,32,256]{3,2,1,0:T(8,128)S(1)} %get-tuple-element.90, ...), kind=kLoop, calls=%fused_computation.352 | loop fusion | flops 12842240 | bytes 3255296 | tf_op jit(solution)/shard_map/reduce_sum | solution.py:156
  69.2 2.6 %fusion.145 = (f32[256]{0:T(256)S(1)}, f32[256]{0:T(256)S(1)}, f32[256]{0:T(256)S(1)}, f32[256]{0:T(256)S(1)}, f32[256]{0:T(256)S(1)}, /*index=5*/f32[256]{0:T(2...) fusion(f32[4,8,32,256]{3,2,1,0:T(8,128)S(1)} %get-tuple-element, ...), kind=kLoop, calls=%fused_computation.319 | loop fusion | flops 14151168 | bytes 10504192 | tf_op jit(solution)/shard_map/reduce_sum | solution.py:156
  73.3 1.2 fusion.261
  74.7 4.3 %collective-permute-start.5 = (f32[4,3,32,256]{3,2,1,0:T(8,128)S(1)}, f32[4,3,32,256]{3,2,1,0:T(8,128)S(1)}, u32[]{:S(2)}, u32[]{:S(2)}) collective-permute-start(f32[4,3,32,256]{3,2,1,0:T(8,128)S(1)} %get-tuple-element.118), channel_id=1, source_target_pairs={{1,0},{2,1},{3,2},{4,3},{5,4},{6,5},{7,6},{8,7},{9,8},{10,9},{11,1... | collective-permute-start | bytes 1179656 | tf_op jit(solution)/shard_map/ppermute | solution.py:27
  79.1 5.5 %collective-permute-done.4 = f32[4,3,32,256]{3,2,1,0:T(8,128)S(1)} collective-permute-done((f32[4,3,32,256]{3,2,1,0:T(8,128)S(1)}, f32[4,3,32,256]{3,2,1,0:T(8,128)S(1)}, u32[]{:S(2)}, u32[]{:S(2)}) %collective-permute-start.4) | collective-permute-done | bytes 393248 | tf_op jit(solution)/shard_map/ppermute | solution.py:26
  85.1 2.1 %collective-permute-start.6 = (f32[67584]{0:T(1024)S(1)}, f32[67584]{0:T(1024)S(1)}, u32[]{:S(2)}, u32[]{:S(2)}) collective-permute-start(f32[67584]{0:T(1024)S(1)} %get-tuple-element.114), channel_id=1, source_target_pairs={{0,2},{1,3},{2,0},{3,1},{4,6},{5,7},{6,4},{7,5},{8,10},{9,11},{10,... | collective-permute-start | bytes 811016 | tf_op jit(solution)/shard_map/ppermute | solution.py:221
  87.2 1.5 %collective-permute-start.8 = (f32[67584]{0:T(1024)S(1)}, f32[67584]{0:T(1024)S(1)}, u32[]{:S(2)}, u32[]{:S(2)}) collective-permute-start(f32[67584]{0:T(1024)S(1)} %get-tuple-element.115), channel_id=1, source_target_pairs={{0,6},{1,7},{2,4},{3,5},{4,2},{5,3},{6,0},{7,1},{8,14},{9,15},{10,... | collective-permute-start | bytes 811016 | tf_op jit(solution)/shard_map/ppermute | solution.py:221
  89.1 10.2 %fusion.95 = f32[4,8,38,256]{3,2,1,0:T(8,128)S(1)} fusion(f32[4,14,32,256]{3,2,1,0:T(8,128)S(1)} %pad_maximum_fusion, f32[256]{0:T(256)} %bitcast.433, f32[256]{0:T(256)} %bitcast.435, f32[256]{0:T(256)S(1)} %bitcast.341, f32[256]{0:T(256)S(1)} %bitcast.343, f32[256]{0:T(256)S(1)} %bitcast.345, f32[256]{0:T(256)S(1)} %bitcast.347, f32[256]{0:T(256)S(1)} %bitcast.349, ...), kind=kLoop, calls=%fused_computation.264 | loop fusion | flops 30195712 | bytes 3130368 | tf_op jit(solution)/shard_map/add | solution.py:301
  99.3 1.7 %collective-permute-done.8 = f32[67584]{0:T(1024)S(1)} collective-permute-done((f32[67584]{0:T(1024)S(1)}, f32[67584]{0:T(1024)S(1)}, u32[]{:S(2)}, u32[]{:S(2)}) %collective-permute-start.8) | collective-permute-done | bytes 270368 | tf_op jit(solution)/shard_map/ppermute | solution.py:221
  101.2 2.7 %collective-permute-start.14 = (f32[33792]{0:T(1024)S(1)}, f32[33792]{0:T(1024)S(1)}, u32[]{:S(2)}, u32[]{:S(2)}) collective-permute-start(f32[33792]{0:T(1024)S(1)} %dynamic_slice.31), channel_id=1, source_target_pairs={{0,8},{1,9},{2,10},{3,11},{4,12},{5,13},{6,14},{7,15},{8,0},{9,1},... | collective-permute-start | bytes 405512 | tf_op jit(solution)/shard_map/ppermute | solution.py:221
  103.9 1.8 %collective-permute-start.12 = (f32[12800]{0:T(1024)S(1)}, f32[12800]{0:T(1024)S(1)}, u32[]{:S(2)}, u32[]{:S(2)}) collective-permute-start(f32[12800]{0:T(1024)S(1)} %add.802), channel_id=1, source_target_pairs={{0,4},{1,5},{2,6},{3,7},{4,0},{5,1},{6,2},{7,3},{8,12},{9,13},{10,... | collective-permute-start | bytes 153608 | tf_op jit(solution)/shard_map/ppermute | solution.py:16
  105.7 2.5 %collective-permute-done.12 = f32[12800]{0:T(1024)S(1)} collective-permute-done((f32[12800]{0:T(1024)S(1)}, f32[12800]{0:T(1024)S(1)}, u32[]{:S(2)}, u32[]{:S(2)}) %collective-permute-start.12) | collective-permute-done | bytes 51232 | tf_op jit(solution)/shard_map/ppermute | solution.py:16
  108.2 1.6 %collective-permute-start.13 = (f32[12800]{0:T(1024)S(1)}, f32[12800]{0:T(1024)S(1)}, u32[]{:S(2)}, u32[]{:S(2)}) collective-permute-start(f32[12800]{0:T(1024)S(1)} %add.803), channel_id=1, source_target_pairs={{0,8},{1,9},{2,10},{3,11},{4,12},{5,13},{6,14},{7,15},{8,0},{9,1},... | collective-permute-start | bytes 153608 | tf_op jit(solution)/shard_map/ppermute | solution.py:16
  109.8 3.5 %collective-permute-done.13 = f32[12800]{0:T(1024)S(1)} collective-permute-done((f32[12800]{0:T(1024)S(1)}, f32[12800]{0:T(1024)S(1)}, u32[]{:S(2)}, u32[]{:S(2)}) %collective-permute-start.13) | collective-permute-done | bytes 51232 | tf_op jit(solution)/shard_map/ppermute | solution.py:16
  113.4 1.6 %collective-permute-start.15 = (bf16[33792]{0:T(1024)(128)(2,1)S(1)}, bf16[33792]{0:T(1024)(128)(2,1)S(1)}, u32[]{:S(2)}, u32[]{:S(2)}) collective-permute-start(bf16[33792]{0:T(1024)(128)(2,1)S(1)} %add_convert_fusion.1), channel_id=1, source_target_pairs={{0,8},{1,9},{2,10},{3,11},{4,12},{5,13},{6,14},{7,15},{8,0},{9,1},... | collective-permute-start | bytes 202760 | tf_op jit(solution)/shard_map/ppermute | solution.py:233
  115.0 0.6 mul.1860
  115.6 3.0 %collective-permute-done.15 = bf16[33792]{0:T(1024)(128)(2,1)S(1)} collective-permute-done((bf16[33792]{0:T(1024)(128)(2,1)S(1)}, bf16[33792]{0:T(1024)(128)(2,1)S(1)}, u32[]{:S(2)}, u32[]{:S(2)}) %collective-permute-start.15) | collective-permute-done | bytes 67616 | tf_op jit(solution)/shard_map/ppermute | solution.py:233
  118.7 2.4 %collective-permute-start.16 = (bf16[67584]{0:T(1024)(128)(2,1)S(1)}, bf16[67584]{0:T(1024)(128)(2,1)S(1)}, u32[]{:S(2)}, u32[]{:S(2)}) collective-permute-start(bf16[67584]{0:T(1024)(128)(2,1)S(1)} %pad_maximum_fusion.13), channel_id=1, source_target_pairs={{0,4},{1,5},{2,6},{3,7},{4,0},{5,1},{6,2},{7,3},{8,12},{9,13},{10,... | collective-permute-start | bytes 405512 | tf_op jit(solution)/shard_map/ppermute | solution.py:233
  121.1 1.3 collective-permute-start.17
  122.6 0.6 slice_multiply_fusion.2
  123.3 0.8 collective-permute-done.16
  124.1 2.0 %collective-permute-done.17 = bf16[67584]{0:T(1024)(128)(2,1)S(1)} collective-permute-done((bf16[67584]{0:T(1024)(128)(2,1)S(1)}, bf16[67584]{0:T(1024)(128)(2,1)S(1)}, u32[]{:S(2)}, u32[]{:S(2)}) %collective-permute-start.17) | collective-permute-done | bytes 135200 | tf_op jit(solution)/shard_map/ppermute | solution.py:233
  126.1 2.9 %collective-permute-done.18 = bf16[67584]{0:T(1024)(128)(2,1)S(1)} collective-permute-done((bf16[67584]{0:T(1024)(128)(2,1)S(1)}, bf16[67584]{0:T(1024)(128)(2,1)S(1)}, u32[]{:S(2)}, u32[]{:S(2)}) %collective-permute-start.18) | collective-permute-done | bytes 135200 | tf_op jit(solution)/shard_map/ppermute | solution.py:233
  129.2 0.9 pad_maximum_fusion.5
  130.4 0.9 rev.7
  131.4 0.9 pad_maximum_fusion.9
  132.4 1.2 broadcast_select_fusion.1
  134.0 0.6 convert_multiply_fusion.99
  134.7 0.6 convert_multiply_fusion.100
  135.4 1.1 mul.1868
  136.5 1.1 convert_multiply_fusion.98
  (348 shorter events, 11.7 us)
Async XLA Ops:
  0.6 35.6 %copy-start = (bf16[1024,256]{1,0:T(8,128)(2,1)S(1)}, bf16[1024,256]{1,0:T(8,128)(2,1)}, u32[]{:S(2)}) copy-start(bf16[1024,256]{1,0:T(8,128)(2,1)} %param.23) | copy-start | bytes 1572868
  0.7 22.2 %copy-start.4 = (bf16[4,8,32,256]{3,2,1,0:T(8,128)(2,1)S(1)}, bf16[4,8,32,256]{3,2,1,0:T(8,128)(2,1)}, u32[]{:S(2)}) copy-start(bf16[4,8,32,256]{3,2,1,0:T(8,128)(2,1)} %param.13) | copy-start | bytes 1572868
  0.7 18.3 %copy-start.25 = (s32[8,32]{1,0:T(8,128)S(1)}, s32[8,32]{1,0:T(8,128)}, u32[]{:S(2)}) copy-start(s32[8,32]{1,0:T(8,128)} %param.16) | copy-start | bytes 3076
  1.7 11.2 %collective-permute-start = (bf16[4,8,3,256]{3,2,1,0:T(4,128)(2,1)S(1)}, bf16[4,8,3,256]{3,2,1,0:T(4,128)(2,1)S(1)}, u32[]{:S(2)}, u32[]{:S(2)}) collective-permute-start(bf16[4,8,3,256]{3,2,1,0:T(4,128)(2,1)S(1)} %slice.712), channel_id=1, source_target_pairs={{0,15},{1,14},{2,13},{3,12},{4,11},{5,10},{6,9},{7,8},{8,7},{9,6},... | collective-permute-start | bytes 147464 | tf_op jit(solution)/shard_map/ppermute | solution.py:174
  8.8 15.4 %copy-start.28 = (f32[1,1,256]{2,1,0:T(1,128)}, f32[1,1,256]{2,1,0:T(1,128)S(1)}, u32[]{:S(2)}) copy-start(f32[1,1,256]{2,1,0:T(1,128)S(1)} %get-tuple-element.137) | copy-start | bytes 3076
  8.8 15.4 %copy-start.30 = (f32[1,1,256]{2,1,0:T(1,128)}, f32[1,1,256]{2,1,0:T(1,128)S(1)}, u32[]{:S(2)}) copy-start(f32[1,1,256]{2,1,0:T(1,128)S(1)} %get-tuple-element.138) | copy-start | bytes 3076
  8.8 15.4 %copy-start.32 = (f32[1,1,256]{2,1,0:T(1,128)}, f32[1,1,256]{2,1,0:T(1,128)S(1)}, u32[]{:S(2)}) copy-start(f32[1,1,256]{2,1,0:T(1,128)S(1)} %get-tuple-element.139) | copy-start | bytes 3076
  8.8 15.4 %copy-start.34 = (f32[1,1,256]{2,1,0:T(1,128)}, f32[1,1,256]{2,1,0:T(1,128)S(1)}, u32[]{:S(2)}) copy-start(f32[1,1,256]{2,1,0:T(1,128)S(1)} %get-tuple-element.140) | copy-start | bytes 3076
  8.8 15.4 %copy-start.36 = (f32[1,1,256]{2,1,0:T(1,128)}, f32[1,1,256]{2,1,0:T(1,128)S(1)}, u32[]{:S(2)}) copy-start(f32[1,1,256]{2,1,0:T(1,128)S(1)} %get-tuple-element.141) | copy-start | bytes 3076
  8.8 15.4 %copy-start.38 = (f32[1,1,256]{2,1,0:T(1,128)}, f32[1,1,256]{2,1,0:T(1,128)S(1)}, u32[]{:S(2)}) copy-start(f32[1,1,256]{2,1,0:T(1,128)S(1)} %get-tuple-element.142) | copy-start | bytes 3076
  8.9 15.4 %copy-start.40 = (f32[1,1,256]{2,1,0:T(1,128)}, f32[1,1,256]{2,1,0:T(1,128)S(1)}, u32[]{:S(2)}) copy-start(f32[1,1,256]{2,1,0:T(1,128)S(1)} %get-tuple-element.143) | copy-start | bytes 3076
  8.9 15.4 %copy-start.42 = (f32[1,1,256]{2,1,0:T(1,128)}, f32[1,1,256]{2,1,0:T(1,128)S(1)}, u32[]{:S(2)}) copy-start(f32[1,1,256]{2,1,0:T(1,128)S(1)} %get-tuple-element.144) | copy-start | bytes 3076
  14.4 8.5 %collective-permute-start.1 = (bf16[4,3,38,256]{3,2,1,0:T(8,128)(2,1)S(1)}, bf16[4,3,38,256]{3,2,1,0:T(8,128)(2,1)S(1)}, u32[]{:S(2)}, u32[]{:S(2)}) collective-permute-start(bf16[4,3,38,256]{3,2,1,0:T(8,128)(2,1)S(1)} %get-tuple-element.123), channel_id=1, source_target_pairs={{0,1},{1,2},{2,3},{3,4},{4,5},{5,6},{6,7},{7,8},{8,9},{9,10},{10,1... | collective-permute-start | bytes 700424 | tf_op jit(solution)/shard_map/ppermute | solution.py:26
  15.1 7.8 %collective-permute-start.2 = (bf16[4,3,38,256]{3,2,1,0:T(8,128)(2,1)S(1)}, bf16[4,3,38,256]{3,2,1,0:T(8,128)(2,1)}, u32[]{:S(2)}, u32[]{:S(2)}) collective-permute-start(bf16[4,3,38,256]{3,2,1,0:T(8,128)(2,1)S(1)} %get-tuple-element.124), channel_id=1, source_target_pairs={{1,0},{2,1},{3,2},{4,3},{5,4},{6,5},{7,6},{8,7},{9,8},{10,9},{11,1... | collective-permute-start | bytes 700424 | tf_op jit(solution)/shard_map/ppermute | solution.py:27
  18.9 5.3 %copy-start.110 = (s32[256]{0:T(256)}, s32[256]{0:T(256)S(1)}, u32[]{:S(2)}) copy-start(s32[256]{0:T(256)S(1)} %and_select_fusion) | copy-start | bytes 3076
  19.1 5.3 %copy-start.5 = (bf16[4,8,32,256]{3,2,1,0:T(8,128)(2,1)S(1)}, bf16[4,8,32,256]{3,2,1,0:T(8,128)(2,1)}, u32[]{:S(2)}) copy-start(bf16[4,8,32,256]{3,2,1,0:T(8,128)(2,1)} %param.13) | copy-start | bytes 1572868
  19.1 5.2 %copy-start.44 = (f32[1,1,256]{2,1,0:T(1,128)S(1)}, f32[1,1,256]{2,1,0:T(1,128)}, u32[]{:S(2)}) copy-start(f32[1,1,256]{2,1,0:T(1,128)} %get-tuple-element.145) | copy-start | bytes 3076
  19.1 5.2 %copy-start.46 = (f32[1,1,256]{2,1,0:T(1,128)S(1)}, f32[1,1,256]{2,1,0:T(1,128)}, u32[]{:S(2)}) copy-start(f32[1,1,256]{2,1,0:T(1,128)} %get-tuple-element.146) | copy-start | bytes 3076
  19.1 5.2 %copy-start.48 = (f32[1,1,256]{2,1,0:T(1,128)S(1)}, f32[1,1,256]{2,1,0:T(1,128)}, u32[]{:S(2)}) copy-start(f32[1,1,256]{2,1,0:T(1,128)} %get-tuple-element.147) | copy-start | bytes 3076
  19.1 5.2 %copy-start.50 = (f32[1,1,256]{2,1,0:T(1,128)S(1)}, f32[1,1,256]{2,1,0:T(1,128)}, u32[]{:S(2)}) copy-start(f32[1,1,256]{2,1,0:T(1,128)} %get-tuple-element.148) | copy-start | bytes 3076
  19.1 5.2 %copy-start.52 = (f32[1,1,256]{2,1,0:T(1,128)S(1)}, f32[1,1,256]{2,1,0:T(1,128)}, u32[]{:S(2)}) copy-start(f32[1,1,256]{2,1,0:T(1,128)} %get-tuple-element.149) | copy-start | bytes 3076
  19.1 5.2 %copy-start.54 = (f32[1,1,256]{2,1,0:T(1,128)S(1)}, f32[1,1,256]{2,1,0:T(1,128)}, u32[]{:S(2)}) copy-start(f32[1,1,256]{2,1,0:T(1,128)} %get-tuple-element.150) | copy-start | bytes 3076
  19.1 5.2 %copy-start.56 = (f32[1,1,256]{2,1,0:T(1,128)S(1)}, f32[1,1,256]{2,1,0:T(1,128)}, u32[]{:S(2)}) copy-start(f32[1,1,256]{2,1,0:T(1,128)} %get-tuple-element.151) | copy-start | bytes 3076
  19.1 5.2 %copy-start.58 = (f32[1,1,256]{2,1,0:T(1,128)S(1)}, f32[1,1,256]{2,1,0:T(1,128)}, u32[]{:S(2)}) copy-start(f32[1,1,256]{2,1,0:T(1,128)} %get-tuple-element.152) | copy-start | bytes 3076
  19.2 5.2 %copy-start.60 = (f32[1,1,256]{2,1,0:T(1,128)S(1)}, f32[1,1,256]{2,1,0:T(1,128)}, u32[]{:S(2)}) copy-start(f32[1,1,256]{2,1,0:T(1,128)} %get-tuple-element.153) | copy-start | bytes 3076
  19.2 5.2 %copy-start.62 = (f32[1,1,256]{2,1,0:T(1,128)S(1)}, f32[1,1,256]{2,1,0:T(1,128)}, u32[]{:S(2)}) copy-start(f32[1,1,256]{2,1,0:T(1,128)} %get-tuple-element.154) | copy-start | bytes 3076
  19.2 5.2 %copy-start.64 = (f32[1,1,256]{2,1,0:T(1,128)S(1)}, f32[1,1,256]{2,1,0:T(1,128)}, u32[]{:S(2)}) copy-start(f32[1,1,256]{2,1,0:T(1,128)} %get-tuple-element.155) | copy-start | bytes 3076
  19.2 5.2 %copy-start.66 = (f32[1,1,256]{2,1,0:T(1,128)S(1)}, f32[1,1,256]{2,1,0:T(1,128)}, u32[]{:S(2)}) copy-start(f32[1,1,256]{2,1,0:T(1,128)} %get-tuple-element.156) | copy-start | bytes 3076
  19.2 5.2 %copy-start.68 = (f32[1,1,256]{2,1,0:T(1,128)S(1)}, f32[1,1,256]{2,1,0:T(1,128)}, u32[]{:S(2)}) copy-start(f32[1,1,256]{2,1,0:T(1,128)} %get-tuple-element.157) | copy-start | bytes 3076
  19.2 5.2 %copy-start.70 = (f32[1,1,256]{2,1,0:T(1,128)S(1)}, f32[1,1,256]{2,1,0:T(1,128)}, u32[]{:S(2)}) copy-start(f32[1,1,256]{2,1,0:T(1,128)} %get-tuple-element.158) | copy-start | bytes 3076
  19.2 5.2 %copy-start.72 = (f32[1,1,256]{2,1,0:T(1,128)S(1)}, f32[1,1,256]{2,1,0:T(1,128)}, u32[]{:S(2)}) copy-start(f32[1,1,256]{2,1,0:T(1,128)} %get-tuple-element.159) | copy-start | bytes 3076
  19.2 5.2 %copy-start.74 = (f32[1,1,256]{2,1,0:T(1,128)S(1)}, f32[1,1,256]{2,1,0:T(1,128)}, u32[]{:S(2)}) copy-start(f32[1,1,256]{2,1,0:T(1,128)} %get-tuple-element.160) | copy-start | bytes 3076
  19.2 5.2 %copy-start.76 = (f32[1,1,256]{2,1,0:T(1,128)S(1)}, f32[1,1,256]{2,1,0:T(1,128)}, u32[]{:S(2)}) copy-start(f32[1,1,256]{2,1,0:T(1,128)} %get-tuple-element.161) | copy-start | bytes 3076
  19.2 5.2 %copy-start.78 = (f32[1,1,256]{2,1,0:T(1,128)S(1)}, f32[1,1,256]{2,1,0:T(1,128)}, u32[]{:S(2)}) copy-start(f32[1,1,256]{2,1,0:T(1,128)} %get-tuple-element.162) | copy-start | bytes 3076
  19.3 5.2 %copy-start.80 = (f32[1,1,256]{2,1,0:T(1,128)S(1)}, f32[1,1,256]{2,1,0:T(1,128)}, u32[]{:S(2)}) copy-start(f32[1,1,256]{2,1,0:T(1,128)} %get-tuple-element.163) | copy-start | bytes 3076
  24.7 9.7 %copy-start.27 = (f32[256]{0:T(256)S(1)}, f32[256]{0:T(256)}, u32[]{:S(2)}) copy-start(f32[256]{0:T(256)} %param.19) | copy-start | bytes 3076
  42.6 12.4 %copy-start.11 = (f32[8,32,256]{2,1,0:T(8,128)}, f32[8,32,256]{2,1,0:T(8,128)S(1)}, u32[]{:S(2)}) copy-start(f32[8,32,256]{2,1,0:T(8,128)S(1)} %get-tuple-element.91) | copy-start | bytes 786436
  42.6 12.4 %copy-start.13 = (f32[8,32,256]{2,1,0:T(8,128)}, f32[8,32,256]{2,1,0:T(8,128)S(1)}, u32[]{:S(2)}) copy-start(f32[8,32,256]{2,1,0:T(8,128)S(1)} %get-tuple-element.92) | copy-start | bytes 786436
  42.6 12.4 %copy-start.15 = (f32[8,32,256]{2,1,0:T(8,128)}, f32[8,32,256]{2,1,0:T(8,128)S(1)}, u32[]{:S(2)}) copy-start(f32[8,32,256]{2,1,0:T(8,128)S(1)} %get-tuple-element.93) | copy-start | bytes 786436
  42.6 12.4 %copy-start.17 = (f32[8,32,256]{2,1,0:T(8,128)}, f32[8,32,256]{2,1,0:T(8,128)S(1)}, u32[]{:S(2)}) copy-start(f32[8,32,256]{2,1,0:T(8,128)S(1)} %get-tuple-element.94) | copy-start | bytes 786436
  57.0 3.3 %collective-permute-start.3 = (f32[270336]{0:T(1024)}, f32[270336]{0:T(1024)}, u32[]{:S(2)}, u32[]{:S(2)}) collective-permute-start(f32[270336]{0:T(1024)} %pad_dynamic-slice_fusion), channel_id=1, source_target_pairs={{0,1},{1,0},{2,3},{3,2},{4,5},{5,4},{6,7},{7,6},{8,9},{9,8},{10,11... | collective-permute-start | bytes 3244040 | tf_op jit(solution)/shard_map/ppermute | solution.py:221
  57.6 5.4 %copy-start.7 = (f32[4,8,32,256]{3,2,1,0:T(8,128)S(1)}, f32[4,8,32,256]{3,2,1,0:T(8,128)}, u32[]{:S(2)}) copy-start(f32[4,8,32,256]{3,2,1,0:T(8,128)} %get-tuple-element.19) | copy-start | bytes 3145732
  72.4 12.1 %copy-start.2 = (f32[4,8,32,256]{3,2,1,0:T(8,128)S(1)}, f32[4,8,32,256]{3,2,1,0:T(8,128)}, u32[]{:S(2)}) copy-start(f32[4,8,32,256]{3,2,1,0:T(8,128)} %copy-done.1) | copy-start | bytes 3145732
  72.9 6.1 %collective-permute-start.10 = (f32[12800]{0:T(1024)S(1)}, f32[12800]{0:T(1024)S(1)}, u32[]{:S(2)}, u32[]{:S(2)}) collective-permute-start(f32[12800]{0:T(1024)S(1)} %pad_maximum_fusion.14), channel_id=1, source_target_pairs={{0,1},{1,0},{2,3},{3,2},{4,5},{5,4},{6,7},{7,6},{8,9},{9,8},{10,11... | collective-permute-start | bytes 153608 | tf_op jit(solution)/shard_map/ppermute | solution.py:16
  74.5 10.1 %collective-permute-start.4 = (f32[4,3,32,256]{3,2,1,0:T(8,128)S(1)}, f32[4,3,32,256]{3,2,1,0:T(8,128)S(1)}, u32[]{:S(2)}, u32[]{:S(2)}) collective-permute-start(f32[4,3,32,256]{3,2,1,0:T(8,128)S(1)} %get-tuple-element.117), channel_id=1, source_target_pairs={{0,1},{1,2},{2,3},{3,4},{4,5},{5,6},{6,7},{7,8},{8,9},{9,10},{10,1... | collective-permute-start | bytes 1179656 | tf_op jit(solution)/shard_map/ppermute | solution.py:26
  74.7 9.9 %collective-permute-start.5 = (f32[4,3,32,256]{3,2,1,0:T(8,128)S(1)}, f32[4,3,32,256]{3,2,1,0:T(8,128)S(1)}, u32[]{:S(2)}, u32[]{:S(2)}) collective-permute-start(f32[4,3,32,256]{3,2,1,0:T(8,128)S(1)} %get-tuple-element.118), channel_id=1, source_target_pairs={{1,0},{2,1},{3,2},{4,3},{5,4},{6,5},{7,6},{8,7},{9,8},{10,9},{11,1... | collective-permute-start | bytes 1179656 | tf_op jit(solution)/shard_map/ppermute | solution.py:27
  79.0 5.7 %copy-start.10 = (f32[270336]{0:T(1024)S(1)}, f32[270336]{0:T(1024)}, u32[]{:S(2)}) copy-start(f32[270336]{0:T(1024)} %fusion.99) | copy-start | bytes 3244036
  79.0 24.9 %collective-permute-start.11 = (f32[12800]{0:T(1024)S(1)}, f32[12800]{0:T(1024)S(1)}, u32[]{:S(2)}, u32[]{:S(2)}) collective-permute-start(f32[12800]{0:T(1024)S(1)} %fusion.310), channel_id=1, source_target_pairs={{0,2},{1,3},{2,0},{3,1},{4,6},{5,7},{6,4},{7,5},{8,10},{9,11},{10,... | collective-permute-start | bytes 153608 | tf_op jit(solution)/shard_map/ppermute | solution.py:16
  85.1 14.2 %collective-permute-start.6 = (f32[67584]{0:T(1024)S(1)}, f32[67584]{0:T(1024)S(1)}, u32[]{:S(2)}, u32[]{:S(2)}) collective-permute-start(f32[67584]{0:T(1024)S(1)} %get-tuple-element.114), channel_id=1, source_target_pairs={{0,2},{1,3},{2,0},{3,1},{4,6},{5,7},{6,4},{7,5},{8,10},{9,11},{10,... | collective-permute-start | bytes 811016 | tf_op jit(solution)/shard_map/ppermute | solution.py:221
  87.2 12.1 %collective-permute-start.7 = (f32[67584]{0:T(1024)S(1)}, f32[67584]{0:T(1024)S(1)}, u32[]{:S(2)}, u32[]{:S(2)}) collective-permute-start(f32[67584]{0:T(1024)S(1)} %get-tuple-element.116), channel_id=1, source_target_pairs={{0,4},{1,5},{2,6},{3,7},{4,0},{5,1},{6,2},{7,3},{8,12},{9,13},{10,... | collective-permute-start | bytes 811016 | tf_op jit(solution)/shard_map/ppermute | solution.py:221
  87.2 13.9 %collective-permute-start.8 = (f32[67584]{0:T(1024)S(1)}, f32[67584]{0:T(1024)S(1)}, u32[]{:S(2)}, u32[]{:S(2)}) collective-permute-start(f32[67584]{0:T(1024)S(1)} %get-tuple-element.115), channel_id=1, source_target_pairs={{0,6},{1,7},{2,4},{3,5},{4,2},{5,3},{6,0},{7,1},{8,14},{9,15},{10,... | collective-permute-start | bytes 811016 | tf_op jit(solution)/shard_map/ppermute | solution.py:221
  101.2 12.2 %collective-permute-start.14 = (f32[33792]{0:T(1024)S(1)}, f32[33792]{0:T(1024)S(1)}, u32[]{:S(2)}, u32[]{:S(2)}) collective-permute-start(f32[33792]{0:T(1024)S(1)} %dynamic_slice.31), channel_id=1, source_target_pairs={{0,8},{1,9},{2,10},{3,11},{4,12},{5,13},{6,14},{7,15},{8,0},{9,1},... | collective-permute-start | bytes 405512 | tf_op jit(solution)/shard_map/ppermute | solution.py:221
  103.9 4.3 %collective-permute-start.12 = (f32[12800]{0:T(1024)S(1)}, f32[12800]{0:T(1024)S(1)}, u32[]{:S(2)}, u32[]{:S(2)}) collective-permute-start(f32[12800]{0:T(1024)S(1)} %add.802), channel_id=1, source_target_pairs={{0,4},{1,5},{2,6},{3,7},{4,0},{5,1},{6,2},{7,3},{8,12},{9,13},{10,... | collective-permute-start | bytes 153608 | tf_op jit(solution)/shard_map/ppermute | solution.py:16
  108.2 5.1 %collective-permute-start.13 = (f32[12800]{0:T(1024)S(1)}, f32[12800]{0:T(1024)S(1)}, u32[]{:S(2)}, u32[]{:S(2)}) collective-permute-start(f32[12800]{0:T(1024)S(1)} %add.803), channel_id=1, source_target_pairs={{0,8},{1,9},{2,10},{3,11},{4,12},{5,13},{6,14},{7,15},{8,0},{9,1},... | collective-permute-start | bytes 153608 | tf_op jit(solution)/shard_map/ppermute | solution.py:16
  113.4 5.3 %collective-permute-start.15 = (bf16[33792]{0:T(1024)(128)(2,1)S(1)}, bf16[33792]{0:T(1024)(128)(2,1)S(1)}, u32[]{:S(2)}, u32[]{:S(2)}) collective-permute-start(bf16[33792]{0:T(1024)(128)(2,1)S(1)} %add_convert_fusion.1), channel_id=1, source_target_pairs={{0,8},{1,9},{2,10},{3,11},{4,12},{5,13},{6,14},{7,15},{8,0},{9,1},... | collective-permute-start | bytes 202760 | tf_op jit(solution)/shard_map/ppermute | solution.py:233
  118.7 11.4 %copy-start.12 = (f32[8,32,256]{2,1,0:T(8,128)S(1)}, f32[8,32,256]{2,1,0:T(8,128)}, u32[]{:S(2)}) copy-start(f32[8,32,256]{2,1,0:T(8,128)} %copy-done.11) | copy-start | bytes 786436
  118.7 11.4 %copy-start.14 = (f32[8,32,256]{2,1,0:T(8,128)S(1)}, f32[8,32,256]{2,1,0:T(8,128)}, u32[]{:S(2)}) copy-start(f32[8,32,256]{2,1,0:T(8,128)} %copy-done.13) | copy-start | bytes 786436
  118.7 11.4 %copy-start.16 = (f32[8,32,256]{2,1,0:T(8,128)S(1)}, f32[8,32,256]{2,1,0:T(8,128)}, u32[]{:S(2)}) copy-start(f32[8,32,256]{2,1,0:T(8,128)} %copy-done.15) | copy-start | bytes 786436
  118.7 11.4 %copy-start.18 = (f32[8,32,256]{2,1,0:T(8,128)S(1)}, f32[8,32,256]{2,1,0:T(8,128)}, u32[]{:S(2)}) copy-start(f32[8,32,256]{2,1,0:T(8,128)} %copy-done.17) | copy-start | bytes 786436
  118.7 5.4 %collective-permute-start.16 = (bf16[67584]{0:T(1024)(128)(2,1)S(1)}, bf16[67584]{0:T(1024)(128)(2,1)S(1)}, u32[]{:S(2)}, u32[]{:S(2)}) collective-permute-start(bf16[67584]{0:T(1024)(128)(2,1)S(1)} %pad_maximum_fusion.13), channel_id=1, source_target_pairs={{0,4},{1,5},{2,6},{3,7},{4,0},{5,1},{6,2},{7,3},{8,12},{9,13},{10,... | collective-permute-start | bytes 405512 | tf_op jit(solution)/shard_map/ppermute | solution.py:233
  121.1 5.0 %collective-permute-start.17 = (bf16[67584]{0:T(1024)(128)(2,1)S(1)}, bf16[67584]{0:T(1024)(128)(2,1)S(1)}, u32[]{:S(2)}, u32[]{:S(2)}) collective-permute-start(bf16[67584]{0:T(1024)(128)(2,1)S(1)} %pad_maximum_fusion.13), channel_id=1, source_target_pairs={{0,2},{1,3},{2,0},{3,1},{4,6},{5,7},{6,4},{7,5},{8,10},{9,11},{10,... | collective-permute-start | bytes 405512 | tf_op jit(solution)/shard_map/ppermute | solution.py:233
  122.4 6.6 %collective-permute-start.18 = (bf16[67584]{0:T(1024)(128)(2,1)S(1)}, bf16[67584]{0:T(1024)(128)(2,1)S(1)}, u32[]{:S(2)}, u32[]{:S(2)}) collective-permute-start(bf16[67584]{0:T(1024)(128)(2,1)S(1)} %pad_maximum_fusion.13), channel_id=1, source_target_pairs={{0,6},{1,7},{2,4},{3,5},{4,2},{5,3},{6,0},{7,1},{8,14},{9,15},{10,... | collective-permute-start | bytes 405512 | tf_op jit(solution)/shard_map/ppermute | solution.py:233
  123.2 7.2 %collective-permute-start.9 = (bf16[4,8,3,256]{3,2,1,0:T(4,128)(2,1)S(1)}, bf16[4,8,3,256]{3,2,1,0:T(4,128)(2,1)}, u32[]{:S(2)}, u32[]{:S(2)}) collective-permute-start(bf16[4,8,3,256]{3,2,1,0:T(4,128)(2,1)S(1)} %slice.1628), channel_id=1, source_target_pairs={{0,15},{1,14},{2,13},{3,12},{4,11},{5,10},{6,9},{7,8},{8,7},{9,6},... | collective-permute-start | bytes 147464 | tf_op jit(solution)/shard_map/ppermute | solution.py:174
  130.1 2.3 %collective-permute-start.19 = (bf16[270336]{0:T(1024)(128)(2,1)}, bf16[270336]{0:T(1024)(128)(2,1)}, u32[]{:S(2)}, u32[]{:S(2)}) collective-permute-start(bf16[270336]{0:T(1024)(128)(2,1)} %pad_maximum_fusion.5), channel_id=1, source_target_pairs={{0,1},{1,0},{2,3},{3,2},{4,5},{5,4},{6,7},{7,6},{8,9},{9,8},{10,11... | collective-permute-start | bytes 1622024 | tf_op jit(solution)/shard_map/ppermute | solution.py:233
  (86 other events, 277.4 us)

commit v13 on v12

--- a/solution.py
+++ b/solution.py
@@ -226,19 +226,32 @@
         elif bits == groups[1]:
             cur, second = lax.optimization_barrier((cur, second))
     cur = cur.astype(gather_dtype)
-    for bits in reversed(groups):
-        radix, low = 1 << len(bits), bits[0]
-        sub = (idx >> low) & (radix - 1)
-        pieces = [cur] + [
-            lax.ppermute(cur, axis, [(i, i ^ (d << low)) for i in range(size)])
-            for d in range(1, radix)
-        ]
-        placed = []
-        for p in range(radix):
-            pick = pieces[p ^ (radix - 1)]
-            for s in range(radix - 1):
-                pick = jnp.where(sub == s, pieces[p ^ s], pick)
-            placed.append(pick)
+    merged = 1
+    while merged < len(groups) and (1 << sum(len(g) for g in groups[-merged - 1 :])) <= 8:
+        merged += 1
+    gathers = [groups[:-merged][k : k + 1] for k in range(len(groups) - merged)]
+    gathers.append(groups[-merged:])
+    for rounds in reversed(gathers):
+        radices = [1 << len(bits) for bits in rounds]
+        mask = sum(1 << b for bits in rounds for b in bits)
+        values = [w for w in range(size) if w & ~mask == 0]
+
+        def position(w):
+            pos = 0
+            for bits, radix in zip(rounds, radices):
+                pos = pos * radix + ((w >> bits[0]) & (radix - 1))
+            return pos
+
+        pieces = {0: cur}
+        for m in values[1:]:
+            pieces[m] = lax.ppermute(cur, axis, [(i, i ^ m) for i in range(size)])
+        own = idx & mask
+        placed = [None] * len(values)
+        for w in values:
+            pick = pieces[values[-1] ^ w]
+            for v in values[:-1]:
+                pick = jnp.where(own == v, pieces[v ^ w], pick)
+            placed[position(w)] = pick
         cur = jnp.concatenate(placed)
     return cur.astype(flat.dtype), first[1:], second
 

time: 138 us -> 142 us (1.029)
  starting transfers between devices: 31 us -> 35.9 us
  waiting for transfers between devices: 28.1 us -> 26.5 us
    ppermute x5 -> x8, starting transfers between devices: 5.51 us -> 10.4 us  [radix_allreduce(): pieces[m] = lax.ppermute(cur, axis, [(i, i ^ m) for i in range(size)])]
    ppermute x5 -> x8, waiting for transfers between devices: 8.75 us -> 6.37 us  [radix_allreduce(): pieces[m] = lax.ppermute(cur, axis, [(i, i ^ m) for i in range(size)])]
    unnamed x272 -> x264, local copies, waits for them, and re-layouts: 4.29 us -> 4.97 us
  transfers between devices with their start and end apart: 20 -> 23, of which waited for: 10 -> 9; matrix products, arithmetic and copies ran while one was open for 16% -> 15% of each run, Pallas kernels for 0% -> 0%
where the time goes in v13:
time: 142 us; the launch traced here: 141 us
  other arithmetic  47.2 us (33%)
  starting transfers between devices  35.9 us (25%)
  waiting for transfers between devices  26.5 us (19%)
  local copies, waits for them, and re-layouts  16.8 us (12%)
  matrix products  11.8 us (8%)
  between operations  3.03 us (2%)
    ppermute x8, starting transfers between devices, radix_allreduce(): pieces[m] = lax.ppermute(cur, axis, [(i, i ^ m) for i in range(size)])  10.4 us
    add x1, other arithmetic, backward_conv(): grad_ext + dw_kernel[lon_off, lat_off] * padded[:, 6 - lon_off:6 - lon_of...  10.2 us
    reduce_sum x1, other arithmetic, local_step(): mean_val = jnp.mean(depth, axis=-1, keepdims=True)  9.29 us
    ppermute x2, waiting for transfers between devices, with_halo(): before = lax.ppermute(last, axis, up)  8.91 us
    reduce_sum x4, other arithmetic, depth_backward(): jnp.sum(grad_depth * extended[:, lon_off:lon_off + lon_dev, lat_off:lat_o...  8.53 us
    ppermute x2, starting transfers between devices, with_halo(): after = lax.ppermute(leading, axis, down)  8.05 us
    ppermute x5, starting transfers between devices, radix_allreduce(): lax.ppermute(send, axis, [(i, i ^ d << low) for i in range(size)])  6.99 us
    ppermute x8, waiting for transfers between devices, radix_allreduce(): pieces[m] = lax.ppermute(cur, axis, [(i, i ^ m) for i in range(size)])  6.37 us
  transfers between devices with their start and end apart: 23, of which 9 were waited for; matrix products, arithmetic and copies ran while one was open for 15% of the time, Pallas kernels for 0%

profile of v13, /device:TPU:0, one launch (start us, length us, event | category | flops | bytes accessed | tf_op | source)
XLA Modules:
  0.0 141.2 jit_solution(3131906714902481380)
XLA Ops:
  0.7 1.0 slice.712
  1.7 5.5 %collective-permute-start = (bf16[4,8,3,256]{3,2,1,0:T(4,128)(2,1)S(1)}, bf16[4,8,3,256]{3,2,1,0:T(4,128)(2,1)S(1)}, u32[]{:S(2)}, u32[]{:S(2)}) collective-permute-start(bf16[4,8,3,256]{3,2,1,0:T(4,128)(2,1)S(1)} %slice.712), channel_id=1, source_target_pairs={{0,15},{1,14},{2,13},{3,12},{4,11},{5,10},{6,9},{7,8},{8,7},{9,6},... | collective-permute-start | bytes 147464 | tf_op jit(solution)/shard_map/ppermute | solution.py:174
  7.2 1.6 %fusion.263 = (f32[1,1,256]{2,1,0:T(1,128)S(1)}, f32[1,1,256]{2,1,0:T(1,128)S(1)}, f32[1,1,256]{2,1,0:T(1,128)S(1)}, f32[1,1,256]{2,1,0:T(1,128)S(1)}, f32[1,1,2...) fusion(f32[7,7,256]{2,1,0:T(8,128)} %param.17), kind=kLoop, calls=%fused_computation.543 | loop fusion | bytes 38912 | tf_op jit(solution)/shard_map/slice | solution.py:59
  8.9 1.7 %fusion.264 = (f32[1,1,256]{2,1,0:T(1,128)}, f32[1,1,256]{2,1,0:T(1,128)}, f32[1,1,256]{2,1,0:T(1,128)}, f32[1,1,256]{2,1,0:T(1,128)}, f32[1,1,256]{2,1,0:T(1,12...) fusion(f32[7,7,256]{2,1,0:T(8,128)} %param.17), kind=kLoop, calls=%fused_computation.544 | loop fusion | bytes 38912 | tf_op jit(solution)/shard_map/slice | solution.py:59
  10.6 1.5 %fusion.265 = (f32[1,1,256]{2,1,0:T(1,128)}, f32[1,1,256]{2,1,0:T(1,128)}, f32[1,1,256]{2,1,0:T(1,128)}, f32[1,1,256]{2,1,0:T(1,128)}, f32[1,1,256]{2,1,0:T(1,12...) fusion(f32[7,7,256]{2,1,0:T(8,128)} %param.17), kind=kLoop, calls=%fused_computation.545 | loop fusion | bytes 22528 | tf_op jit(solution)/shard_map/slice | solution.py:59
  12.1 0.8 copy.25
  13.1 1.3 pad_maximum_fusion.11
  14.4 0.7 collective-permute-start.1
  15.1 3.8 %collective-permute-start.2 = (bf16[4,3,38,256]{3,2,1,0:T(8,128)(2,1)S(1)}, bf16[4,3,38,256]{3,2,1,0:T(8,128)(2,1)}, u32[]{:S(2)}, u32[]{:S(2)}) collective-permute-start(bf16[4,3,38,256]{3,2,1,0:T(8,128)(2,1)S(1)} %get-tuple-element.124), channel_id=1, source_target_pairs={{1,0},{2,1},{3,2},{4,3},{5,4},{6,5},{7,6},{8,7},{9,8},{10,9},{11,1... | collective-permute-start | bytes 700424 | tf_op jit(solution)/shard_map/ppermute | solution.py:27
  19.4 3.5 %collective-permute-done.1 = bf16[4,3,38,256]{3,2,1,0:T(8,128)(2,1)S(1)} collective-permute-done((bf16[4,3,38,256]{3,2,1,0:T(8,128)(2,1)S(1)}, bf16[4,3,38,256]{3,2,1,0:T(8,128)(2,1)S(1)}, u32[]{:S(2)}, u32[]{:S(2)}) %collective-permute-start.1) | collective-permute-done | bytes 233504 | tf_op jit(solution)/shard_map/ppermute | solution.py:26
  22.9 1.3 maximum_maximum_fusion
  24.7 9.3 %fusion.258 = (f32[4,8,32]{2,1,0:T(8,128)S(1)}, f32[4,8,32,256]{3,2,1,0:T(8,128)S(1)}) fusion(bf16[4,11,38,256]{3,2,1,0:T(8,128)(2,1)S(1)} %get-tuple-element.122, f32[256]{0:T(256)} %bitcast.432, f32[256]{0:T(256)} %bitcast.434, f32[256]{0:T(256)S(1)} %bitcast.340, f32[256]{0:T(256)S(1)} %bitcast.342, f32[256]{0:T(256)S(1)} %bitcast.344, ...), kind=kLoop, calls=%fused_computation.539 | loop fusion | flops 43514880 | bytes 23746560 | tf_op jit(solution)/shard_map/reduce_sum | solution.py:62
  34.4 1.1 add_convert_fusion
  39.0 1.1 fusion.256
  40.1 2.5 %multiply_reduce_fusion.7 = (f32[256]{0:T(256)S(1)}, f32[256]{0:T(256)S(1)}, f32[256]{0:T(256)S(1)}, f32[256]{0:T(256)S(1)}, f32[8,32,256]{2,1,0:T(8,128)S(1)}, ...) fusion(f32[256]{0:T(256)S(1)} %copy-done.22, ...), kind=kLoop, calls=%fused_computation.478 | loop fusion | flops 7863296 | bytes 2497536 | tf_op jit(solution)/shard_map/reduce_sum | solution.py:117
  42.7 0.6 fusion.247
  43.3 0.9 fusion.250
  44.9 0.9 fusion.248
  45.8 0.6 convolution_add_fusion.2
  46.4 0.9 fusion.252
  47.3 0.6 convolution_add_fusion.1
  47.9 0.9 fusion.254
  48.9 0.6 fusion
  49.5 0.8 copy.28
  52.5 1.3 pad_maximum_fusion.3
  53.8 0.7 copy-done.8
  55.3 1.2 pad_dynamic-slice_fusion
  57.0 0.7 collective-permute-start.3
  57.6 2.7 %collective-permute-done.3 = f32[270336]{0:T(1024)} collective-permute-done((f32[270336]{0:T(1024)}, f32[270336]{0:T(1024)}, u32[]{:S(2)}, u32[]{:S(2)}) %collective-permute-start.3) | collective-permute-done | bytes 1081376 | tf_op jit(solution)/shard_map/ppermute | solution.py:221
  60.3 2.7 %fusion.99 = f32[270336]{0:T(1024)} fusion(f32[270336]{0:T(1024)} %collective-permute-done.3, s32[]{:T(128)S(6)} %select_n.286, f32[526336]{0:T(1024)} %copy-done.9), kind=kLoop, calls=%fused_computation.272 | loop fusion | flops 270336 | bytes 4268036 | tf_op jit(solution)/shard_map/add | solution.py:221
  63.0 0.6 multiply_reduce_fusion.4
  63.7 3.8 %fusion.196 = (f32[256]{0:T(256)S(1)}, f32[256]{0:T(256)}, f32[256]{0:T(256)}, f32[256]{0:T(256)}, f32[256]{0:T(256)}, /*index=5*/f32[256]{0:T(256)}, f32[256]{0...) fusion(bf16[4,11,38,256]{3,2,1,0:T(8,128)(2,1)S(1)} %get-tuple-, ...), kind=kLoop, calls=%fused_computation.370 | loop fusion | flops 15986176 | bytes 12618752 | tf_op jit(solution)/shard_map/reduce_sum | solution.py:156
  67.5 1.8 %fusion.178 = (f32[256]{0:T(256)S(1)}, f32[256]{0:T(256)S(1)}, f32[256]{0:T(256)S(1)}, f32[256]{0:T(256)S(1)}, f32[256]{0:T(256)S(1)}, /*index=5*/f32[256]{0:T(2...) fusion(f32[4,8,32,256]{3,2,1,0:T(8,128)S(1)} %get-tuple-element.90, ...), kind=kLoop, calls=%fused_computation.352 | loop fusion | flops 12842240 | bytes 3255296 | tf_op jit(solution)/shard_map/reduce_sum | solution.py:156
  69.2 2.6 %fusion.145 = (f32[256]{0:T(256)S(1)}, f32[256]{0:T(256)S(1)}, f32[256]{0:T(256)S(1)}, f32[256]{0:T(256)S(1)}, f32[256]{0:T(256)S(1)}, /*index=5*/f32[256]{0:T(2...) fusion(f32[4,8,32,256]{3,2,1,0:T(8,128)S(1)} %get-tuple-element, ...), kind=kLoop, calls=%fused_computation.319 | loop fusion | flops 14151168 | bytes 10504192 | tf_op jit(solution)/shard_map/reduce_sum | solution.py:156
  73.3 1.2 fusion.261
  74.7 4.3 %collective-permute-start.5 = (f32[4,3,32,256]{3,2,1,0:T(8,128)S(1)}, f32[4,3,32,256]{3,2,1,0:T(8,128)S(1)}, u32[]{:S(2)}, u32[]{:S(2)}) collective-permute-start(f32[4,3,32,256]{3,2,1,0:T(8,128)S(1)} %get-tuple-element.118), channel_id=1, source_target_pairs={{1,0},{2,1},{3,2},{4,3},{5,4},{6,5},{7,6},{8,7},{9,8},{10,9},{11,1... | collective-permute-start | bytes 1179656 | tf_op jit(solution)/shard_map/ppermute | solution.py:27
  79.1 5.5 %collective-permute-done.4 = f32[4,3,32,256]{3,2,1,0:T(8,128)S(1)} collective-permute-done((f32[4,3,32,256]{3,2,1,0:T(8,128)S(1)}, f32[4,3,32,256]{3,2,1,0:T(8,128)S(1)}, u32[]{:S(2)}, u32[]{:S(2)}) %collective-permute-start.4) | collective-permute-done | bytes 393248 | tf_op jit(solution)/shard_map/ppermute | solution.py:26
  85.1 2.1 %collective-permute-start.6 = (f32[67584]{0:T(1024)S(1)}, f32[67584]{0:T(1024)S(1)}, u32[]{:S(2)}, u32[]{:S(2)}) collective-permute-start(f32[67584]{0:T(1024)S(1)} %get-tuple-element.114), channel_id=1, source_target_pairs={{0,2},{1,3},{2,0},{3,1},{4,6},{5,7},{6,4},{7,5},{8,10},{9,11},{10,... | collective-permute-start | bytes 811016 | tf_op jit(solution)/shard_map/ppermute | solution.py:221
  87.2 1.5 %collective-permute-start.8 = (f32[67584]{0:T(1024)S(1)}, f32[67584]{0:T(1024)S(1)}, u32[]{:S(2)}, u32[]{:S(2)}) collective-permute-start(f32[67584]{0:T(1024)S(1)} %get-tuple-element.115), channel_id=1, source_target_pairs={{0,6},{1,7},{2,4},{3,5},{4,2},{5,3},{6,0},{7,1},{8,14},{9,15},{10,... | collective-permute-start | bytes 811016 | tf_op jit(solution)/shard_map/ppermute | solution.py:221
  89.1 10.2 %fusion.95 = f32[4,8,38,256]{3,2,1,0:T(8,128)S(1)} fusion(f32[4,14,32,256]{3,2,1,0:T(8,128)S(1)} %pad_maximum_fusion, f32[256]{0:T(256)} %bitcast.433, f32[256]{0:T(256)} %bitcast.435, f32[256]{0:T(256)S(1)} %bitcast.341, f32[256]{0:T(256)S(1)} %bitcast.343, f32[256]{0:T(256)S(1)} %bitcast.345, f32[256]{0:T(256)S(1)} %bitcast.347, f32[256]{0:T(256)S(1)} %bitcast.349, ...), kind=kLoop, calls=%fused_computation.264 | loop fusion | flops 30195712 | bytes 3130368 | tf_op jit(solution)/shard_map/add | solution.py:314
  99.3 1.7 %collective-permute-done.8 = f32[67584]{0:T(1024)S(1)} collective-permute-done((f32[67584]{0:T(1024)S(1)}, f32[67584]{0:T(1024)S(1)}, u32[]{:S(2)}, u32[]{:S(2)}) %collective-permute-start.8) | collective-permute-done | bytes 270368 | tf_op jit(solution)/shard_map/ppermute | solution.py:221
  101.2 2.7 %collective-permute-start.14 = (f32[33792]{0:T(1024)S(1)}, f32[33792]{0:T(1024)S(1)}, u32[]{:S(2)}, u32[]{:S(2)}) collective-permute-start(f32[33792]{0:T(1024)S(1)} %dynamic_slice.31), channel_id=1, source_target_pairs={{0,8},{1,9},{2,10},{3,11},{4,12},{5,13},{6,14},{7,15},{8,0},{9,1},... | collective-permute-start | bytes 405512 | tf_op jit(solution)/shard_map/ppermute | solution.py:221
  103.9 1.8 %collective-permute-start.12 = (f32[12800]{0:T(1024)S(1)}, f32[12800]{0:T(1024)S(1)}, u32[]{:S(2)}, u32[]{:S(2)}) collective-permute-start(f32[12800]{0:T(1024)S(1)} %add.802), channel_id=1, source_target_pairs={{0,4},{1,5},{2,6},{3,7},{4,0},{5,1},{6,2},{7,3},{8,12},{9,13},{10,... | collective-permute-start | bytes 153608 | tf_op jit(solution)/shard_map/ppermute | solution.py:16
  105.7 2.5 %collective-permute-done.12 = f32[12800]{0:T(1024)S(1)} collective-permute-done((f32[12800]{0:T(1024)S(1)}, f32[12800]{0:T(1024)S(1)}, u32[]{:S(2)}, u32[]{:S(2)}) %collective-permute-start.12) | collective-permute-done | bytes 51232 | tf_op jit(solution)/shard_map/ppermute | solution.py:16
  108.2 1.6 %collective-permute-start.13 = (f32[12800]{0:T(1024)S(1)}, f32[12800]{0:T(1024)S(1)}, u32[]{:S(2)}, u32[]{:S(2)}) collective-permute-start(f32[12800]{0:T(1024)S(1)} %add.803), channel_id=1, source_target_pairs={{0,8},{1,9},{2,10},{3,11},{4,12},{5,13},{6,14},{7,15},{8,0},{9,1},... | collective-permute-start | bytes 153608 | tf_op jit(solution)/shard_map/ppermute | solution.py:16
  109.8 3.5 %collective-permute-done.13 = f32[12800]{0:T(1024)S(1)} collective-permute-done((f32[12800]{0:T(1024)S(1)}, f32[12800]{0:T(1024)S(1)}, u32[]{:S(2)}, u32[]{:S(2)}) %collective-permute-start.13) | collective-permute-done | bytes 51232 | tf_op jit(solution)/shard_map/ppermute | solution.py:16
  113.4 1.8 %collective-permute-start.15 = (bf16[33792]{0:T(1024)(128)(2,1)S(1)}, bf16[33792]{0:T(1024)(128)(2,1)S(1)}, u32[]{:S(2)}, u32[]{:S(2)}) collective-permute-start(bf16[33792]{0:T(1024)(128)(2,1)S(1)} %add_convert_fusion.1), channel_id=1, source_target_pairs={{0,12},{1,13},{2,14},{3,15},{4,8},{5,9},{6,10},{7,11},{8,4},{9,5},... | collective-permute-start | bytes 202760 | tf_op jit(solution)/shard_map/ppermute | solution.py:247
  115.1 2.0 %collective-permute-start.16 = (bf16[33792]{0:T(1024)(128)(2,1)S(1)}, bf16[33792]{0:T(1024)(128)(2,1)S(1)}, u32[]{:S(2)}, u32[]{:S(2)}) collective-permute-start(bf16[33792]{0:T(1024)(128)(2,1)S(1)} %add_convert_fusion.1), channel_id=1, source_target_pairs={{0,10},{1,11},{2,8},{3,9},{4,14},{5,15},{6,12},{7,13},{8,2},{9,3},... | collective-permute-start | bytes 202760 | tf_op jit(solution)/shard_map/ppermute | solution.py:247
  117.2 1.2 collective-permute-start.17
  118.4 1.0 collective-permute-start.18
  119.4 1.6 %collective-permute-start.19 = (bf16[33792]{0:T(1024)(128)(2,1)S(1)}, bf16[33792]{0:T(1024)(128)(2,1)S(1)}, u32[]{:S(2)}, u32[]{:S(2)}) collective-permute-start(bf16[33792]{0:T(1024)(128)(2,1)S(1)} %add_convert_fusion.1), channel_id=1, source_target_pairs={{0,4},{1,5},{2,6},{3,7},{4,0},{5,1},{6,2},{7,3},{8,12},{9,13},{10,... | collective-permute-start | bytes 202760 | tf_op jit(solution)/shard_map/ppermute | solution.py:247
  121.0 0.9 collective-permute-start.20
  121.9 2.6 %collective-permute-done.16 = bf16[33792]{0:T(1024)(128)(2,1)S(1)} collective-permute-done((bf16[33792]{0:T(1024)(128)(2,1)S(1)}, bf16[33792]{0:T(1024)(128)(2,1)S(1)}, u32[]{:S(2)}, u32[]{:S(2)}) %collective-permute-start.16) | collective-permute-done | bytes 67616 | tf_op jit(solution)/shard_map/ppermute | solution.py:247
  124.5 1.9 %collective-permute-start.21 = (bf16[33792]{0:T(1024)(128)(2,1)S(1)}, bf16[33792]{0:T(1024)(128)(2,1)S(1)}, u32[]{:S(2)}, u32[]{:S(2)}) collective-permute-start(bf16[33792]{0:T(1024)(128)(2,1)S(1)} %add_convert_fusion.1), channel_id=1, source_target_pairs={{0,14},{1,15},{2,12},{3,13},{4,10},{5,11},{6,8},{7,9},{8,6},{9,7},... | collective-permute-start | bytes 202760 | tf_op jit(solution)/shard_map/ppermute | solution.py:247
  126.9 0.6 mul.1860
  127.7 3.8 %collective-permute-done.21 = bf16[33792]{0:T(1024)(128)(2,1)S(1)} collective-permute-done((bf16[33792]{0:T(1024)(128)(2,1)S(1)}, bf16[33792]{0:T(1024)(128)(2,1)S(1)}, u32[]{:S(2)}, u32[]{:S(2)}) %collective-permute-start.21) | collective-permute-done | bytes 67616 | tf_op jit(solution)/shard_map/ppermute | solution.py:247
  133.3 0.8 collective-permute-done.9
  134.1 0.9 rev.7
  135.1 0.9 pad_maximum_fusion.8
  136.0 1.1 broadcast_select_fusion.1
  137.5 0.6 convert_multiply_fusion.99
  138.2 0.6 convert_multiply_fusion.100
  138.9 1.1 mul.1868
  140.1 1.1 convert_multiply_fusion.98
  (350 shorter events, 13.8 us)
Async XLA Ops:
  0.6 35.6 %copy-start = (bf16[1024,256]{1,0:T(8,128)(2,1)S(1)}, bf16[1024,256]{1,0:T(8,128)(2,1)}, u32[]{:S(2)}) copy-start(bf16[1024,256]{1,0:T(8,128)(2,1)} %param.23) | copy-start | bytes 1572868
  0.7 22.2 %copy-start.4 = (bf16[4,8,32,256]{3,2,1,0:T(8,128)(2,1)S(1)}, bf16[4,8,32,256]{3,2,1,0:T(8,128)(2,1)}, u32[]{:S(2)}) copy-start(bf16[4,8,32,256]{3,2,1,0:T(8,128)(2,1)} %param.13) | copy-start | bytes 1572868
  0.7 18.3 %copy-start.21 = (s32[8,32]{1,0:T(8,128)S(1)}, s32[8,32]{1,0:T(8,128)}, u32[]{:S(2)}) copy-start(s32[8,32]{1,0:T(8,128)} %param.16) | copy-start | bytes 3076
  1.7 11.2 %collective-permute-start = (bf16[4,8,3,256]{3,2,1,0:T(4,128)(2,1)S(1)}, bf16[4,8,3,256]{3,2,1,0:T(4,128)(2,1)S(1)}, u32[]{:S(2)}, u32[]{:S(2)}) collective-permute-start(bf16[4,8,3,256]{3,2,1,0:T(4,128)(2,1)S(1)} %slice.712), channel_id=1, source_target_pairs={{0,15},{1,14},{2,13},{3,12},{4,11},{5,10},{6,9},{7,8},{8,7},{9,6},... | collective-permute-start | bytes 147464 | tf_op jit(solution)/shard_map/ppermute | solution.py:174
  8.8 15.4 %copy-start.24 = (f32[1,1,256]{2,1,0:T(1,128)}, f32[1,1,256]{2,1,0:T(1,128)S(1)}, u32[]{:S(2)}) copy-start(f32[1,1,256]{2,1,0:T(1,128)S(1)} %get-tuple-element.131) | copy-start | bytes 3076
  8.8 15.4 %copy-start.26 = (f32[1,1,256]{2,1,0:T(1,128)}, f32[1,1,256]{2,1,0:T(1,128)S(1)}, u32[]{:S(2)}) copy-start(f32[1,1,256]{2,1,0:T(1,128)S(1)} %get-tuple-element.132) | copy-start | bytes 3076
  8.8 15.4 %copy-start.28 = (f32[1,1,256]{2,1,0:T(1,128)}, f32[1,1,256]{2,1,0:T(1,128)S(1)}, u32[]{:S(2)}) copy-start(f32[1,1,256]{2,1,0:T(1,128)S(1)} %get-tuple-element.133) | copy-start | bytes 3076
  8.8 15.4 %copy-start.30 = (f32[1,1,256]{2,1,0:T(1,128)}, f32[1,1,256]{2,1,0:T(1,128)S(1)}, u32[]{:S(2)}) copy-start(f32[1,1,256]{2,1,0:T(1,128)S(1)} %get-tuple-element.134) | copy-start | bytes 3076
  8.8 15.4 %copy-start.32 = (f32[1,1,256]{2,1,0:T(1,128)}, f32[1,1,256]{2,1,0:T(1,128)S(1)}, u32[]{:S(2)}) copy-start(f32[1,1,256]{2,1,0:T(1,128)S(1)} %get-tuple-element.135) | copy-start | bytes 3076
  8.8 15.4 %copy-start.34 = (f32[1,1,256]{2,1,0:T(1,128)}, f32[1,1,256]{2,1,0:T(1,128)S(1)}, u32[]{:S(2)}) copy-start(f32[1,1,256]{2,1,0:T(1,128)S(1)} %get-tuple-element.136) | copy-start | bytes 3076
  8.9 15.4 %copy-start.36 = (f32[1,1,256]{2,1,0:T(1,128)}, f32[1,1,256]{2,1,0:T(1,128)S(1)}, u32[]{:S(2)}) copy-start(f32[1,1,256]{2,1,0:T(1,128)S(1)} %get-tuple-element.137) | copy-start | bytes 3076
  8.9 15.4 %copy-start.38 = (f32[1,1,256]{2,1,0:T(1,128)}, f32[1,1,256]{2,1,0:T(1,128)S(1)}, u32[]{:S(2)}) copy-start(f32[1,1,256]{2,1,0:T(1,128)S(1)} %get-tuple-element.138) | copy-start | bytes 3076
  14.4 8.5 %collective-permute-start.1 = (bf16[4,3,38,256]{3,2,1,0:T(8,128)(2,1)S(1)}, bf16[4,3,38,256]{3,2,1,0:T(8,128)(2,1)S(1)}, u32[]{:S(2)}, u32[]{:S(2)}) collective-permute-start(bf16[4,3,38,256]{3,2,1,0:T(8,128)(2,1)S(1)} %get-tuple-element.123), channel_id=1, source_target_pairs={{0,1},{1,2},{2,3},{3,4},{4,5},{5,6},{6,7},{7,8},{8,9},{9,10},{10,1... | collective-permute-start | bytes 700424 | tf_op jit(solution)/shard_map/ppermute | solution.py:26
  15.1 7.8 %collective-permute-start.2 = (bf16[4,3,38,256]{3,2,1,0:T(8,128)(2,1)S(1)}, bf16[4,3,38,256]{3,2,1,0:T(8,128)(2,1)}, u32[]{:S(2)}, u32[]{:S(2)}) collective-permute-start(bf16[4,3,38,256]{3,2,1,0:T(8,128)(2,1)S(1)} %get-tuple-element.124), channel_id=1, source_target_pairs={{1,0},{2,1},{3,2},{4,3},{5,4},{6,5},{7,6},{8,7},{9,8},{10,9},{11,1... | collective-permute-start | bytes 700424 | tf_op jit(solution)/shard_map/ppermute | solution.py:27
  18.9 5.3 %copy-start.106 = (s32[256]{0:T(256)}, s32[256]{0:T(256)S(1)}, u32[]{:S(2)}) copy-start(s32[256]{0:T(256)S(1)} %and_select_fusion) | copy-start | bytes 3076
  19.1 5.3 %copy-start.5 = (bf16[4,8,32,256]{3,2,1,0:T(8,128)(2,1)S(1)}, bf16[4,8,32,256]{3,2,1,0:T(8,128)(2,1)}, u32[]{:S(2)}) copy-start(bf16[4,8,32,256]{3,2,1,0:T(8,128)(2,1)} %param.13) | copy-start | bytes 1572868
  19.1 5.2 %copy-start.40 = (f32[1,1,256]{2,1,0:T(1,128)S(1)}, f32[1,1,256]{2,1,0:T(1,128)}, u32[]{:S(2)}) copy-start(f32[1,1,256]{2,1,0:T(1,128)} %get-tuple-element.139) | copy-start | bytes 3076
  19.1 5.2 %copy-start.42 = (f32[1,1,256]{2,1,0:T(1,128)S(1)}, f32[1,1,256]{2,1,0:T(1,128)}, u32[]{:S(2)}) copy-start(f32[1,1,256]{2,1,0:T(1,128)} %get-tuple-element.140) | copy-start | bytes 3076
  19.1 5.2 %copy-start.44 = (f32[1,1,256]{2,1,0:T(1,128)S(1)}, f32[1,1,256]{2,1,0:T(1,128)}, u32[]{:S(2)}) copy-start(f32[1,1,256]{2,1,0:T(1,128)} %get-tuple-element.141) | copy-start | bytes 3076
  19.1 5.2 %copy-start.46 = (f32[1,1,256]{2,1,0:T(1,128)S(1)}, f32[1,1,256]{2,1,0:T(1,128)}, u32[]{:S(2)}) copy-start(f32[1,1,256]{2,1,0:T(1,128)} %get-tuple-element.142) | copy-start | bytes 3076
  19.1 5.2 %copy-start.48 = (f32[1,1,256]{2,1,0:T(1,128)S(1)}, f32[1,1,256]{2,1,0:T(1,128)}, u32[]{:S(2)}) copy-start(f32[1,1,256]{2,1,0:T(1,128)} %get-tuple-element.143) | copy-start | bytes 3076
  19.1 5.2 %copy-start.50 = (f32[1,1,256]{2,1,0:T(1,128)S(1)}, f32[1,1,256]{2,1,0:T(1,128)}, u32[]{:S(2)}) copy-start(f32[1,1,256]{2,1,0:T(1,128)} %get-tuple-element.144) | copy-start | bytes 3076
  19.1 5.2 %copy-start.52 = (f32[1,1,256]{2,1,0:T(1,128)S(1)}, f32[1,1,256]{2,1,0:T(1,128)}, u32[]{:S(2)}) copy-start(f32[1,1,256]{2,1,0:T(1,128)} %get-tuple-element.145) | copy-start | bytes 3076
  19.1 5.2 %copy-start.54 = (f32[1,1,256]{2,1,0:T(1,128)S(1)}, f32[1,1,256]{2,1,0:T(1,128)}, u32[]{:S(2)}) copy-start(f32[1,1,256]{2,1,0:T(1,128)} %get-tuple-element.146) | copy-start | bytes 3076
  19.2 5.2 %copy-start.56 = (f32[1,1,256]{2,1,0:T(1,128)S(1)}, f32[1,1,256]{2,1,0:T(1,128)}, u32[]{:S(2)}) copy-start(f32[1,1,256]{2,1,0:T(1,128)} %get-tuple-element.147) | copy-start | bytes 3076
  19.2 5.2 %copy-start.58 = (f32[1,1,256]{2,1,0:T(1,128)S(1)}, f32[1,1,256]{2,1,0:T(1,128)}, u32[]{:S(2)}) copy-start(f32[1,1,256]{2,1,0:T(1,128)} %get-tuple-element.148) | copy-start | bytes 3076
  19.2 5.2 %copy-start.60 = (f32[1,1,256]{2,1,0:T(1,128)S(1)}, f32[1,1,256]{2,1,0:T(1,128)}, u32[]{:S(2)}) copy-start(f32[1,1,256]{2,1,0:T(1,128)} %get-tuple-element.149) | copy-start | bytes 3076
  19.2 5.2 %copy-start.62 = (f32[1,1,256]{2,1,0:T(1,128)S(1)}, f32[1,1,256]{2,1,0:T(1,128)}, u32[]{:S(2)}) copy-start(f32[1,1,256]{2,1,0:T(1,128)} %get-tuple-element.150) | copy-start | bytes 3076
  19.2 5.2 %copy-start.64 = (f32[1,1,256]{2,1,0:T(1,128)S(1)}, f32[1,1,256]{2,1,0:T(1,128)}, u32[]{:S(2)}) copy-start(f32[1,1,256]{2,1,0:T(1,128)} %get-tuple-element.151) | copy-start | bytes 3076
  19.2 5.2 %copy-start.66 = (f32[1,1,256]{2,1,0:T(1,128)S(1)}, f32[1,1,256]{2,1,0:T(1,128)}, u32[]{:S(2)}) copy-start(f32[1,1,256]{2,1,0:T(1,128)} %get-tuple-element.152) | copy-start | bytes 3076
  19.2 5.2 %copy-start.68 = (f32[1,1,256]{2,1,0:T(1,128)S(1)}, f32[1,1,256]{2,1,0:T(1,128)}, u32[]{:S(2)}) copy-start(f32[1,1,256]{2,1,0:T(1,128)} %get-tuple-element.153) | copy-start | bytes 3076
  19.2 5.2 %copy-start.70 = (f32[1,1,256]{2,1,0:T(1,128)S(1)}, f32[1,1,256]{2,1,0:T(1,128)}, u32[]{:S(2)}) copy-start(f32[1,1,256]{2,1,0:T(1,128)} %get-tuple-element.154) | copy-start | bytes 3076
  19.2 5.2 %copy-start.72 = (f32[1,1,256]{2,1,0:T(1,128)S(1)}, f32[1,1,256]{2,1,0:T(1,128)}, u32[]{:S(2)}) copy-start(f32[1,1,256]{2,1,0:T(1,128)} %get-tuple-element.155) | copy-start | bytes 3076
  19.2 5.2 %copy-start.74 = (f32[1,1,256]{2,1,0:T(1,128)S(1)}, f32[1,1,256]{2,1,0:T(1,128)}, u32[]{:S(2)}) copy-start(f32[1,1,256]{2,1,0:T(1,128)} %get-tuple-element.156) | copy-start | bytes 3076
  19.3 5.2 %copy-start.76 = (f32[1,1,256]{2,1,0:T(1,128)S(1)}, f32[1,1,256]{2,1,0:T(1,128)}, u32[]{:S(2)}) copy-start(f32[1,1,256]{2,1,0:T(1,128)} %get-tuple-element.157) | copy-start | bytes 3076
  19.3 5.2 %copy-start.78 = (f32[1,1,256]{2,1,0:T(1,128)S(1)}, f32[1,1,256]{2,1,0:T(1,128)}, u32[]{:S(2)}) copy-start(f32[1,1,256]{2,1,0:T(1,128)} %get-tuple-element.158) | copy-start | bytes 3076
  24.7 9.7 %copy-start.23 = (f32[256]{0:T(256)S(1)}, f32[256]{0:T(256)}, u32[]{:S(2)}) copy-start(f32[256]{0:T(256)} %param.19) | copy-start | bytes 3076
  42.6 12.4 %copy-start.11 = (f32[8,32,256]{2,1,0:T(8,128)}, f32[8,32,256]{2,1,0:T(8,128)S(1)}, u32[]{:S(2)}) copy-start(f32[8,32,256]{2,1,0:T(8,128)S(1)} %get-tuple-element.91) | copy-start | bytes 786436
  42.6 12.4 %copy-start.13 = (f32[8,32,256]{2,1,0:T(8,128)}, f32[8,32,256]{2,1,0:T(8,128)S(1)}, u32[]{:S(2)}) copy-start(f32[8,32,256]{2,1,0:T(8,128)S(1)} %get-tuple-element.92) | copy-start | bytes 786436
  42.6 12.4 %copy-start.15 = (f32[8,32,256]{2,1,0:T(8,128)}, f32[8,32,256]{2,1,0:T(8,128)S(1)}, u32[]{:S(2)}) copy-start(f32[8,32,256]{2,1,0:T(8,128)S(1)} %get-tuple-element.93) | copy-start | bytes 786436
  42.6 12.4 %copy-start.17 = (f32[8,32,256]{2,1,0:T(8,128)}, f32[8,32,256]{2,1,0:T(8,128)S(1)}, u32[]{:S(2)}) copy-start(f32[8,32,256]{2,1,0:T(8,128)S(1)} %get-tuple-element.94) | copy-start | bytes 786436
  57.0 3.3 %collective-permute-start.3 = (f32[270336]{0:T(1024)}, f32[270336]{0:T(1024)}, u32[]{:S(2)}, u32[]{:S(2)}) collective-permute-start(f32[270336]{0:T(1024)} %pad_dynamic-slice_fusion), channel_id=1, source_target_pairs={{0,1},{1,0},{2,3},{3,2},{4,5},{5,4},{6,7},{7,6},{8,9},{9,8},{10,11... | collective-permute-start | bytes 3244040 | tf_op jit(solution)/shard_map/ppermute | solution.py:221
  57.6 5.4 %copy-start.7 = (f32[4,8,32,256]{3,2,1,0:T(8,128)S(1)}, f32[4,8,32,256]{3,2,1,0:T(8,128)}, u32[]{:S(2)}) copy-start(f32[4,8,32,256]{3,2,1,0:T(8,128)} %get-tuple-element.19) | copy-start | bytes 3145732
  72.4 12.1 %copy-start.2 = (f32[4,8,32,256]{3,2,1,0:T(8,128)S(1)}, f32[4,8,32,256]{3,2,1,0:T(8,128)}, u32[]{:S(2)}) copy-start(f32[4,8,32,256]{3,2,1,0:T(8,128)} %copy-done.1) | copy-start | bytes 3145732
  72.9 6.1 %collective-permute-start.10 = (f32[12800]{0:T(1024)S(1)}, f32[12800]{0:T(1024)S(1)}, u32[]{:S(2)}, u32[]{:S(2)}) collective-permute-start(f32[12800]{0:T(1024)S(1)} %pad_maximum_fusion.12), channel_id=1, source_target_pairs={{0,1},{1,0},{2,3},{3,2},{4,5},{5,4},{6,7},{7,6},{8,9},{9,8},{10,11... | collective-permute-start | bytes 153608 | tf_op jit(solution)/shard_map/ppermute | solution.py:16
  74.5 10.1 %collective-permute-start.4 = (f32[4,3,32,256]{3,2,1,0:T(8,128)S(1)}, f32[4,3,32,256]{3,2,1,0:T(8,128)S(1)}, u32[]{:S(2)}, u32[]{:S(2)}) collective-permute-start(f32[4,3,32,256]{3,2,1,0:T(8,128)S(1)} %get-tuple-element.117), channel_id=1, source_target_pairs={{0,1},{1,2},{2,3},{3,4},{4,5},{5,6},{6,7},{7,8},{8,9},{9,10},{10,1... | collective-permute-start | bytes 1179656 | tf_op jit(solution)/shard_map/ppermute | solution.py:26
  74.7 9.9 %collective-permute-start.5 = (f32[4,3,32,256]{3,2,1,0:T(8,128)S(1)}, f32[4,3,32,256]{3,2,1,0:T(8,128)S(1)}, u32[]{:S(2)}, u32[]{:S(2)}) collective-permute-start(f32[4,3,32,256]{3,2,1,0:T(8,128)S(1)} %get-tuple-element.118), channel_id=1, source_target_pairs={{1,0},{2,1},{3,2},{4,3},{5,4},{6,5},{7,6},{8,7},{9,8},{10,9},{11,1... | collective-permute-start | bytes 1179656 | tf_op jit(solution)/shard_map/ppermute | solution.py:27
  79.0 5.7 %copy-start.10 = (f32[270336]{0:T(1024)S(1)}, f32[270336]{0:T(1024)}, u32[]{:S(2)}) copy-start(f32[270336]{0:T(1024)} %fusion.99) | copy-start | bytes 3244036
  79.0 24.9 %collective-permute-start.11 = (f32[12800]{0:T(1024)S(1)}, f32[12800]{0:T(1024)S(1)}, u32[]{:S(2)}, u32[]{:S(2)}) collective-permute-start(f32[12800]{0:T(1024)S(1)} %fusion.310), channel_id=1, source_target_pairs={{0,2},{1,3},{2,0},{3,1},{4,6},{5,7},{6,4},{7,5},{8,10},{9,11},{10,... | collective-permute-start | bytes 153608 | tf_op jit(solution)/shard_map/ppermute | solution.py:16
  85.1 14.2 %collective-permute-start.6 = (f32[67584]{0:T(1024)S(1)}, f32[67584]{0:T(1024)S(1)}, u32[]{:S(2)}, u32[]{:S(2)}) collective-permute-start(f32[67584]{0:T(1024)S(1)} %get-tuple-element.114), channel_id=1, source_target_pairs={{0,2},{1,3},{2,0},{3,1},{4,6},{5,7},{6,4},{7,5},{8,10},{9,11},{10,... | collective-permute-start | bytes 811016 | tf_op jit(solution)/shard_map/ppermute | solution.py:221
  87.2 12.1 %collective-permute-start.7 = (f32[67584]{0:T(1024)S(1)}, f32[67584]{0:T(1024)S(1)}, u32[]{:S(2)}, u32[]{:S(2)}) collective-permute-start(f32[67584]{0:T(1024)S(1)} %get-tuple-element.116), channel_id=1, source_target_pairs={{0,4},{1,5},{2,6},{3,7},{4,0},{5,1},{6,2},{7,3},{8,12},{9,13},{10,... | collective-permute-start | bytes 811016 | tf_op jit(solution)/shard_map/ppermute | solution.py:221
  87.2 13.9 %collective-permute-start.8 = (f32[67584]{0:T(1024)S(1)}, f32[67584]{0:T(1024)S(1)}, u32[]{:S(2)}, u32[]{:S(2)}) collective-permute-start(f32[67584]{0:T(1024)S(1)} %get-tuple-element.115), channel_id=1, source_target_pairs={{0,6},{1,7},{2,4},{3,5},{4,2},{5,3},{6,0},{7,1},{8,14},{9,15},{10,... | collective-permute-start | bytes 811016 | tf_op jit(solution)/shard_map/ppermute | solution.py:221
  101.2 12.2 %collective-permute-start.14 = (f32[33792]{0:T(1024)S(1)}, f32[33792]{0:T(1024)S(1)}, u32[]{:S(2)}, u32[]{:S(2)}) collective-permute-start(f32[33792]{0:T(1024)S(1)} %dynamic_slice.31), channel_id=1, source_target_pairs={{0,8},{1,9},{2,10},{3,11},{4,12},{5,13},{6,14},{7,15},{8,0},{9,1},... | collective-permute-start | bytes 405512 | tf_op jit(solution)/shard_map/ppermute | solution.py:221
  103.9 4.3 %collective-permute-start.12 = (f32[12800]{0:T(1024)S(1)}, f32[12800]{0:T(1024)S(1)}, u32[]{:S(2)}, u32[]{:S(2)}) collective-permute-start(f32[12800]{0:T(1024)S(1)} %add.802), channel_id=1, source_target_pairs={{0,4},{1,5},{2,6},{3,7},{4,0},{5,1},{6,2},{7,3},{8,12},{9,13},{10,... | collective-permute-start | bytes 153608 | tf_op jit(solution)/shard_map/ppermute | solution.py:16
  108.2 5.1 %collective-permute-start.13 = (f32[12800]{0:T(1024)S(1)}, f32[12800]{0:T(1024)S(1)}, u32[]{:S(2)}, u32[]{:S(2)}) collective-permute-start(f32[12800]{0:T(1024)S(1)} %add.803), channel_id=1, source_target_pairs={{0,8},{1,9},{2,10},{3,11},{4,12},{5,13},{6,14},{7,15},{8,0},{9,1},... | collective-permute-start | bytes 153608 | tf_op jit(solution)/shard_map/ppermute | solution.py:16
  113.4 7.6 %collective-permute-start.15 = (bf16[33792]{0:T(1024)(128)(2,1)S(1)}, bf16[33792]{0:T(1024)(128)(2,1)S(1)}, u32[]{:S(2)}, u32[]{:S(2)}) collective-permute-start(bf16[33792]{0:T(1024)(128)(2,1)S(1)} %add_convert_fusion.1), channel_id=1, source_target_pairs={{0,12},{1,13},{2,14},{3,15},{4,8},{5,9},{6,10},{7,11},{8,4},{9,5},... | collective-permute-start | bytes 202760 | tf_op jit(solution)/shard_map/ppermute | solution.py:247
  115.1 9.3 %collective-permute-start.16 = (bf16[33792]{0:T(1024)(128)(2,1)S(1)}, bf16[33792]{0:T(1024)(128)(2,1)S(1)}, u32[]{:S(2)}, u32[]{:S(2)}) collective-permute-start(bf16[33792]{0:T(1024)(128)(2,1)S(1)} %add_convert_fusion.1), channel_id=1, source_target_pairs={{0,10},{1,11},{2,8},{3,9},{4,14},{5,15},{6,12},{7,13},{8,2},{9,3},... | collective-permute-start | bytes 202760 | tf_op jit(solution)/shard_map/ppermute | solution.py:247
  117.2 10.4 %collective-permute-start.17 = (bf16[33792]{0:T(1024)(128)(2,1)S(1)}, bf16[33792]{0:T(1024)(128)(2,1)S(1)}, u32[]{:S(2)}, u32[]{:S(2)}) collective-permute-start(bf16[33792]{0:T(1024)(128)(2,1)S(1)} %add_convert_fusion.1), channel_id=1, source_target_pairs={{0,8},{1,9},{2,10},{3,11},{4,12},{5,13},{6,14},{7,15},{8,0},{9,1},... | collective-permute-start | bytes 202760 | tf_op jit(solution)/shard_map/ppermute | solution.py:247
  118.4 9.3 %collective-permute-start.18 = (bf16[33792]{0:T(1024)(128)(2,1)S(1)}, bf16[33792]{0:T(1024)(128)(2,1)S(1)}, u32[]{:S(2)}, u32[]{:S(2)}) collective-permute-start(bf16[33792]{0:T(1024)(128)(2,1)S(1)} %add_convert_fusion.1), channel_id=1, source_target_pairs={{0,6},{1,7},{2,4},{3,5},{4,2},{5,3},{6,0},{7,1},{8,14},{9,15},{10,... | collective-permute-start | bytes 202760 | tf_op jit(solution)/shard_map/ppermute | solution.py:247
  119.4 8.3 %collective-permute-start.19 = (bf16[33792]{0:T(1024)(128)(2,1)S(1)}, bf16[33792]{0:T(1024)(128)(2,1)S(1)}, u32[]{:S(2)}, u32[]{:S(2)}) collective-permute-start(bf16[33792]{0:T(1024)(128)(2,1)S(1)} %add_convert_fusion.1), channel_id=1, source_target_pairs={{0,4},{1,5},{2,6},{3,7},{4,0},{5,1},{6,2},{7,3},{8,12},{9,13},{10,... | collective-permute-start | bytes 202760 | tf_op jit(solution)/shard_map/ppermute | solution.py:247
  121.0 6.7 %collective-permute-start.20 = (bf16[33792]{0:T(1024)(128)(2,1)S(1)}, bf16[33792]{0:T(1024)(128)(2,1)S(1)}, u32[]{:S(2)}, u32[]{:S(2)}) collective-permute-start(bf16[33792]{0:T(1024)(128)(2,1)S(1)} %add_convert_fusion.1), channel_id=1, source_target_pairs={{0,2},{1,3},{2,0},{3,1},{4,6},{5,7},{6,4},{7,5},{8,10},{9,11},{10,... | collective-permute-start | bytes 202760 | tf_op jit(solution)/shard_map/ppermute | solution.py:247
  124.5 7.0 %collective-permute-start.21 = (bf16[33792]{0:T(1024)(128)(2,1)S(1)}, bf16[33792]{0:T(1024)(128)(2,1)S(1)}, u32[]{:S(2)}, u32[]{:S(2)}) collective-permute-start(bf16[33792]{0:T(1024)(128)(2,1)S(1)} %add_convert_fusion.1), channel_id=1, source_target_pairs={{0,14},{1,15},{2,12},{3,13},{4,10},{5,11},{6,8},{7,9},{8,6},{9,7},... | collective-permute-start | bytes 202760 | tf_op jit(solution)/shard_map/ppermute | solution.py:247
  127.6 6.6 %collective-permute-start.9 = (bf16[4,8,3,256]{3,2,1,0:T(4,128)(2,1)S(1)}, bf16[4,8,3,256]{3,2,1,0:T(4,128)(2,1)}, u32[]{:S(2)}, u32[]{:S(2)}) collective-permute-start(bf16[4,8,3,256]{3,2,1,0:T(4,128)(2,1)S(1)} %slice.1628), channel_id=1, source_target_pairs={{0,15},{1,14},{2,13},{3,12},{4,11},{5,10},{6,9},{7,8},{8,7},{9,6},... | collective-permute-start | bytes 147464 | tf_op jit(solution)/shard_map/ppermute | solution.py:174
  132.2 3.8 %collective-permute-start.22 = (bf16[270336]{0:T(1024)(128)(2,1)S(1)}, bf16[270336]{0:T(1024)(128)(2,1)}, u32[]{:S(2)}, u32[]{:S(2)}) collective-permute-start(bf16[270336]{0:T(1024)(128)(2,1)S(1)} %select_dynamic-update-slice_fusion), channel_id=1, source_target_pairs={{0,1},{1,0},{2,3},{3,2},{4,5},{5,4},{6,7},{7,6},{8,9},{9,8},{10,11... | collective-permute-start | bytes 1622024 | tf_op jit(solution)/shard_map/ppermute | solution.py:247
  (85 other events, 270.6 us)

commit v14 on v12

--- a/solution.py
+++ b/solution.py
@@ -202,7 +202,7 @@
     return cur.astype(flat.dtype)
 
 
-def radix_allreduce(flat, axis, gather_dtype, operand, start, finish):
+def radix_allreduce(flat, axis, gather_dtype, scale, operand, start, finish):
     size = lax.axis_size(axis)
     nbits = size.bit_length() - 1
     groups = [[0]] + [list(range(b, min(b + 2, nbits))) for b in range(1, nbits, 2)]
@@ -225,7 +225,7 @@
             first = start(operand)
         elif bits == groups[1]:
             cur, second = lax.optimization_barrier((cur, second))
-    cur = cur.astype(gather_dtype)
+    cur = (cur * scale).astype(gather_dtype)
     for bits in reversed(groups):
         radix, low = 1 << len(bits), bits[0]
         sub = (idx >> low) & (radix - 1)
@@ -310,8 +310,9 @@
         return grad_ext
 
     lon_size = lax.axis_size("lon")
+    factor = 1.0 / math.sqrt(members * lat_rows * lon_dev * lon_size)
     reduced, (kernel_sum, dw_bias_sum), grad_ext = radix_allreduce(
-        pack(sums, lon_size * 1024), "lon", jnp.bfloat16, grad_normed, backward, backward_conv
+        pack(sums, lon_size * 1024), "lon", jnp.bfloat16, factor, grad_normed, backward, backward_conv
     )
     gain_sum, bias_sum, w_in_sum, b_in_sum, w_out_sum, b_out_sum, scale_sum = unpack(reduced, sums)
     small = (kernel_sum, dw_bias_sum)
@@ -332,20 +333,13 @@
     grad_features = jnp.concatenate(
         [inner[:, :, : lat_rows - 3, :], inner[:, :, lat_rows - 3 :, :] + back_rows], axis=2
     ).astype(jnp.bfloat16)
-    factor = 1.0 / math.sqrt(members * lat_rows * lon_dev * lax.axis_size("lon"))
     return (
         predicted,
         crps_field,
         grad_features,
         totals[0] * factor,
         totals[1] * factor,
-        totals[2] * factor,
-        totals[3] * factor,
-        totals[4] * factor,
-        totals[5] * factor,
-        totals[6] * factor,
-        totals[7] * factor,
-        totals[8] * factor,
+        *totals[2:],
     )
 
 

time: 138 us -> 138 us (level)
    mul x4 -> x0, other arithmetic: 2.39 us -> none  [the longest x1 1.11 us: on_device(): totals[6] * factor]
    slice x0 -> x3, other arithmetic: none -> 2.25 us  [unpack(): out.append(flat[at:at + a.size].reshape(a.shape))]
where the time goes in v14:
time: 138 us
  other arithmetic  47.4 us (34%)
  starting transfers between devices  31 us (22%)
  waiting for transfers between devices  28.1 us (20%)
  local copies, waits for them, and re-layouts  16.2 us (12%)
  matrix products  11.8 us (9%)
  between operations  3.08 us (2%)
    add x1, other arithmetic, backward_conv(): grad_ext + dw_kernel[lon_off, lat_off] * padded[:, 6 - lon_off:6 - lon_of...  10.2 us
    reduce_sum x1, other arithmetic, local_step(): mean_val = jnp.mean(depth, axis=-1, keepdims=True)  9.29 us
    ppermute x2, waiting for transfers between devices, with_halo(): before = lax.ppermute(last, axis, up)  8.91 us
    ppermute x5, waiting for transfers between devices, radix_allreduce(): lax.ppermute(cur, axis, [(i, i ^ d << low) for i in range(size)])  8.75 us
    reduce_sum x4, other arithmetic, depth_backward(): jnp.sum(grad_depth * extended[:, lon_off:lon_off + lon_dev, lat_off:lat_o...  8.53 us
    ppermute x2, starting transfers between devices, with_halo(): after = lax.ppermute(leading, axis, down)  8.05 us
    ppermute x5, starting transfers between devices, radix_allreduce(): lax.ppermute(send, axis, [(i, i ^ d << low) for i in range(size)])  6.99 us
    ppermute x4, waiting for transfers between devices, swapped(): lax.ppermute(x, axis, [(i, i ^ 1 << bit) for i in range(lax.axis_size(axi...  6.01 us
  transfers between devices with their start and end apart: 20, of which 10 were waited for; matrix products, arithmetic and copies ran while one was open for 16% of the time, Pallas kernels for 0%

profile of v14, /device:TPU:0, one launch (start us, length us, event | category | flops | bytes accessed | tf_op | source)
XLA Modules:
  0.0 137.6 jit_solution(18328178140116123125)
XLA Ops:
  0.7 1.0 slice.712
  1.7 5.5 %collective-permute-start = (bf16[4,8,3,256]{3,2,1,0:T(4,128)(2,1)S(1)}, bf16[4,8,3,256]{3,2,1,0:T(4,128)(2,1)S(1)}, u32[]{:S(2)}, u32[]{:S(2)}) collective-permute-start(bf16[4,8,3,256]{3,2,1,0:T(4,128)(2,1)S(1)} %slice.712), channel_id=1, source_target_pairs={{0,15},{1,14},{2,13},{3,12},{4,11},{5,10},{6,9},{7,8},{8,7},{9,6},... | collective-permute-start | bytes 147464 | tf_op jit(solution)/shard_map/ppermute | solution.py:174
  7.2 1.6 %fusion.264 = (f32[1,1,256]{2,1,0:T(1,128)S(1)}, f32[1,1,256]{2,1,0:T(1,128)S(1)}, f32[1,1,256]{2,1,0:T(1,128)S(1)}, f32[1,1,256]{2,1,0:T(1,128)S(1)}, f32[1,1,2...) fusion(f32[7,7,256]{2,1,0:T(8,128)} %param.17), kind=kLoop, calls=%fused_computation.542 | loop fusion | bytes 38912 | tf_op jit(solution)/shard_map/slice | solution.py:59
  8.9 1.7 %fusion.265 = (f32[1,1,256]{2,1,0:T(1,128)}, f32[1,1,256]{2,1,0:T(1,128)}, f32[1,1,256]{2,1,0:T(1,128)}, f32[1,1,256]{2,1,0:T(1,128)}, f32[1,1,256]{2,1,0:T(1,12...) fusion(f32[7,7,256]{2,1,0:T(8,128)} %param.17), kind=kLoop, calls=%fused_computation.543 | loop fusion | bytes 38912 | tf_op jit(solution)/shard_map/slice | solution.py:59
  10.6 1.5 %fusion.266 = (f32[1,1,256]{2,1,0:T(1,128)}, f32[1,1,256]{2,1,0:T(1,128)}, f32[1,1,256]{2,1,0:T(1,128)}, f32[1,1,256]{2,1,0:T(1,128)}, f32[1,1,256]{2,1,0:T(1,12...) fusion(f32[7,7,256]{2,1,0:T(8,128)} %param.17), kind=kLoop, calls=%fused_computation.544 | loop fusion | bytes 22528 | tf_op jit(solution)/shard_map/slice | solution.py:59
  12.1 0.8 copy.25
  13.1 1.3 pad_maximum_fusion.12
  14.4 0.7 collective-permute-start.1
  15.1 3.8 %collective-permute-start.2 = (bf16[4,3,38,256]{3,2,1,0:T(8,128)(2,1)S(1)}, bf16[4,3,38,256]{3,2,1,0:T(8,128)(2,1)}, u32[]{:S(2)}, u32[]{:S(2)}) collective-permute-start(bf16[4,3,38,256]{3,2,1,0:T(8,128)(2,1)S(1)} %get-tuple-element.124), channel_id=1, source_target_pairs={{1,0},{2,1},{3,2},{4,3},{5,4},{6,5},{7,6},{8,7},{9,8},{10,9},{11,1... | collective-permute-start | bytes 700424 | tf_op jit(solution)/shard_map/ppermute | solution.py:27
  19.4 3.5 %collective-permute-done.1 = bf16[4,3,38,256]{3,2,1,0:T(8,128)(2,1)S(1)} collective-permute-done((bf16[4,3,38,256]{3,2,1,0:T(8,128)(2,1)S(1)}, bf16[4,3,38,256]{3,2,1,0:T(8,128)(2,1)S(1)}, u32[]{:S(2)}, u32[]{:S(2)}) %collective-permute-start.1) | collective-permute-done | bytes 233504 | tf_op jit(solution)/shard_map/ppermute | solution.py:26
  22.9 1.3 maximum_maximum_fusion
  24.7 9.3 %fusion.259 = (f32[4,8,32]{2,1,0:T(8,128)S(1)}, f32[4,8,32,256]{3,2,1,0:T(8,128)S(1)}) fusion(bf16[4,11,38,256]{3,2,1,0:T(8,128)(2,1)S(1)} %get-tuple-element.122, f32[256]{0:T(256)} %bitcast.432, f32[256]{0:T(256)} %bitcast.434, f32[256]{0:T(256)S(1)} %bitcast.340, f32[256]{0:T(256)S(1)} %bitcast.342, f32[256]{0:T(256)S(1)} %bitcast.344, ...), kind=kLoop, calls=%fused_computation.538 | loop fusion | flops 43514880 | bytes 23746560 | tf_op jit(solution)/shard_map/reduce_sum | solution.py:62
  34.4 1.1 add_convert_fusion
  39.0 1.1 fusion.257
  40.1 2.5 %multiply_reduce_fusion.7 = (f32[256]{0:T(256)S(1)}, f32[256]{0:T(256)S(1)}, f32[256]{0:T(256)S(1)}, f32[256]{0:T(256)S(1)}, f32[8,32,256]{2,1,0:T(8,128)S(1)}, ...) fusion(f32[256]{0:T(256)S(1)} %copy-done.26, ...), kind=kLoop, calls=%fused_computation.478 | loop fusion | flops 7863296 | bytes 2497536 | tf_op jit(solution)/shard_map/reduce_sum | solution.py:117
  42.7 0.6 fusion.248
  43.3 0.9 fusion.251
  44.9 0.9 fusion.249
  45.8 0.6 convolution_add_fusion.2
  46.4 0.9 fusion.253
  47.3 0.6 convolution_add_fusion.1
  47.9 0.9 fusion.255
  48.9 0.6 fusion
  49.5 0.8 copy.28
  52.5 1.3 pad_maximum_fusion.3
  53.8 0.7 copy-done.8
  55.3 1.2 pad_dynamic-slice_fusion
  56.5 0.5 copy-done.9
  57.0 0.7 collective-permute-start.3
  57.6 2.7 %collective-permute-done.3 = f32[270336]{0:T(1024)} collective-permute-done((f32[270336]{0:T(1024)}, f32[270336]{0:T(1024)}, u32[]{:S(2)}, u32[]{:S(2)}) %collective-permute-start.3) | collective-permute-done | bytes 1081376 | tf_op jit(solution)/shard_map/ppermute | solution.py:221
  60.3 2.7 %fusion.99 = f32[270336]{0:T(1024)} fusion(f32[270336]{0:T(1024)} %collective-permute-done.3, s32[]{:T(128)S(6)} %select_n.114, f32[526336]{0:T(1024)} %copy-done.9), kind=kLoop, calls=%fused_computation.272 | loop fusion | flops 270336 | bytes 4268036 | tf_op jit(solution)/shard_map/add | solution.py:221
  63.0 0.6 multiply_reduce_fusion.4
  63.7 3.8 %fusion.196 = (f32[256]{0:T(256)S(1)}, f32[256]{0:T(256)}, f32[256]{0:T(256)}, f32[256]{0:T(256)}, f32[256]{0:T(256)}, /*index=5*/f32[256]{0:T(256)}, f32[256]{0...) fusion(bf16[4,11,38,256]{3,2,1,0:T(8,128)(2,1)S(1)} %get-tuple-, ...), kind=kLoop, calls=%fused_computation.370 | loop fusion | flops 15986176 | bytes 12618752 | tf_op jit(solution)/shard_map/reduce_sum | solution.py:156
  67.5 1.8 %fusion.178 = (f32[256]{0:T(256)S(1)}, f32[256]{0:T(256)S(1)}, f32[256]{0:T(256)S(1)}, f32[256]{0:T(256)S(1)}, f32[256]{0:T(256)S(1)}, /*index=5*/f32[256]{0:T(2...) fusion(f32[4,8,32,256]{3,2,1,0:T(8,128)S(1)} %get-tuple-element.90, ...), kind=kLoop, calls=%fused_computation.352 | loop fusion | flops 12842240 | bytes 3255296 | tf_op jit(solution)/shard_map/reduce_sum | solution.py:156
  69.2 2.6 %fusion.145 = (f32[256]{0:T(256)S(1)}, f32[256]{0:T(256)S(1)}, f32[256]{0:T(256)S(1)}, f32[256]{0:T(256)S(1)}, f32[256]{0:T(256)S(1)}, /*index=5*/f32[256]{0:T(2...) fusion(f32[4,8,32,256]{3,2,1,0:T(8,128)S(1)} %get-tuple-element, ...), kind=kLoop, calls=%fused_computation.319 | loop fusion | flops 14151168 | bytes 10504192 | tf_op jit(solution)/shard_map/reduce_sum | solution.py:156
  73.3 1.2 fusion.262
  74.7 4.3 %collective-permute-start.5 = (f32[4,3,32,256]{3,2,1,0:T(8,128)S(1)}, f32[4,3,32,256]{3,2,1,0:T(8,128)S(1)}, u32[]{:S(2)}, u32[]{:S(2)}) collective-permute-start(f32[4,3,32,256]{3,2,1,0:T(8,128)S(1)} %get-tuple-element.118), channel_id=1, source_target_pairs={{1,0},{2,1},{3,2},{4,3},{5,4},{6,5},{7,6},{8,7},{9,8},{10,9},{11,1... | collective-permute-start | bytes 1179656 | tf_op jit(solution)/shard_map/ppermute | solution.py:27
  79.1 5.5 %collective-permute-done.4 = f32[4,3,32,256]{3,2,1,0:T(8,128)S(1)} collective-permute-done((f32[4,3,32,256]{3,2,1,0:T(8,128)S(1)}, f32[4,3,32,256]{3,2,1,0:T(8,128)S(1)}, u32[]{:S(2)}, u32[]{:S(2)}) %collective-permute-start.4) | collective-permute-done | bytes 393248 | tf_op jit(solution)/shard_map/ppermute | solution.py:26
  85.1 2.1 %collective-permute-start.6 = (f32[67584]{0:T(1024)S(1)}, f32[67584]{0:T(1024)S(1)}, u32[]{:S(2)}, u32[]{:S(2)}) collective-permute-start(f32[67584]{0:T(1024)S(1)} %get-tuple-element.114), channel_id=1, source_target_pairs={{0,2},{1,3},{2,0},{3,1},{4,6},{5,7},{6,4},{7,5},{8,10},{9,11},{10,... | collective-permute-start | bytes 811016 | tf_op jit(solution)/shard_map/ppermute | solution.py:221
  87.2 1.5 %collective-permute-start.8 = (f32[67584]{0:T(1024)S(1)}, f32[67584]{0:T(1024)S(1)}, u32[]{:S(2)}, u32[]{:S(2)}) collective-permute-start(f32[67584]{0:T(1024)S(1)} %get-tuple-element.115), channel_id=1, source_target_pairs={{0,6},{1,7},{2,4},{3,5},{4,2},{5,3},{6,0},{7,1},{8,14},{9,15},{10,... | collective-permute-start | bytes 811016 | tf_op jit(solution)/shard_map/ppermute | solution.py:221
  89.1 10.2 %fusion.95 = f32[4,8,38,256]{3,2,1,0:T(8,128)S(1)} fusion(f32[4,14,32,256]{3,2,1,0:T(8,128)S(1)} %pad_maximum_fusion, f32[256]{0:T(256)} %bitcast.433, f32[256]{0:T(256)} %bitcast.435, f32[256]{0:T(256)S(1)} %bitcast.341, f32[256]{0:T(256)S(1)} %bitcast.343, f32[256]{0:T(256)S(1)} %bitcast.345, f32[256]{0:T(256)S(1)} %bitcast.347, f32[256]{0:T(256)S(1)} %bitcast.349, ...), kind=kLoop, calls=%fused_computation.264 | loop fusion | flops 30195712 | bytes 3130368 | tf_op jit(solution)/shard_map/add | solution.py:301
  99.3 1.7 %collective-permute-done.8 = f32[67584]{0:T(1024)S(1)} collective-permute-done((f32[67584]{0:T(1024)S(1)}, f32[67584]{0:T(1024)S(1)}, u32[]{:S(2)}, u32[]{:S(2)}) %collective-permute-start.8) | collective-permute-done | bytes 270368 | tf_op jit(solution)/shard_map/ppermute | solution.py:221
  101.2 2.7 %collective-permute-start.14 = (f32[33792]{0:T(1024)S(1)}, f32[33792]{0:T(1024)S(1)}, u32[]{:S(2)}, u32[]{:S(2)}) collective-permute-start(f32[33792]{0:T(1024)S(1)} %dynamic_slice.31), channel_id=1, source_target_pairs={{0,8},{1,9},{2,10},{3,11},{4,12},{5,13},{6,14},{7,15},{8,0},{9,1},... | collective-permute-start | bytes 405512 | tf_op jit(solution)/shard_map/ppermute | solution.py:221
  103.9 1.8 %collective-permute-start.12 = (f32[12800]{0:T(1024)S(1)}, f32[12800]{0:T(1024)S(1)}, u32[]{:S(2)}, u32[]{:S(2)}) collective-permute-start(f32[12800]{0:T(1024)S(1)} %add.802), channel_id=1, source_target_pairs={{0,4},{1,5},{2,6},{3,7},{4,0},{5,1},{6,2},{7,3},{8,12},{9,13},{10,... | collective-permute-start | bytes 153608 | tf_op jit(solution)/shard_map/ppermute | solution.py:16
  105.7 2.5 %collective-permute-done.12 = f32[12800]{0:T(1024)S(1)} collective-permute-done((f32[12800]{0:T(1024)S(1)}, f32[12800]{0:T(1024)S(1)}, u32[]{:S(2)}, u32[]{:S(2)}) %collective-permute-start.12) | collective-permute-done | bytes 51232 | tf_op jit(solution)/shard_map/ppermute | solution.py:16
  108.2 1.6 %collective-permute-start.13 = (f32[12800]{0:T(1024)S(1)}, f32[12800]{0:T(1024)S(1)}, u32[]{:S(2)}, u32[]{:S(2)}) collective-permute-start(f32[12800]{0:T(1024)S(1)} %add.803), channel_id=1, source_target_pairs={{0,8},{1,9},{2,10},{3,11},{4,12},{5,13},{6,14},{7,15},{8,0},{9,1},... | collective-permute-start | bytes 153608 | tf_op jit(solution)/shard_map/ppermute | solution.py:16
  109.8 3.5 %collective-permute-done.13 = f32[12800]{0:T(1024)S(1)} collective-permute-done((f32[12800]{0:T(1024)S(1)}, f32[12800]{0:T(1024)S(1)}, u32[]{:S(2)}, u32[]{:S(2)}) %collective-permute-start.13) | collective-permute-done | bytes 51232 | tf_op jit(solution)/shard_map/ppermute | solution.py:16
  113.4 1.6 %collective-permute-start.15 = (bf16[33792]{0:T(1024)(128)(2,1)S(1)}, bf16[33792]{0:T(1024)(128)(2,1)S(1)}, u32[]{:S(2)}, u32[]{:S(2)}) collective-permute-start(bf16[33792]{0:T(1024)(128)(2,1)S(1)} %multiply_convert_fusion.8), channel_id=1, source_target_pairs={{0,8},{1,9},{2,10},{3,11},{4,12},{5,13},{6,14},{7,15},{8,0},{9,1},... | collective-permute-start | bytes 202760 | tf_op jit(solution)/shard_map/ppermute | solution.py:233
  115.0 0.6 mul.1836
  115.6 3.0 %collective-permute-done.15 = bf16[33792]{0:T(1024)(128)(2,1)S(1)} collective-permute-done((bf16[33792]{0:T(1024)(128)(2,1)S(1)}, bf16[33792]{0:T(1024)(128)(2,1)S(1)}, u32[]{:S(2)}, u32[]{:S(2)}) %collective-permute-start.15) | collective-permute-done | bytes 67616 | tf_op jit(solution)/shard_map/ppermute | solution.py:233
  118.7 2.4 %collective-permute-start.16 = (bf16[67584]{0:T(1024)(128)(2,1)S(1)}, bf16[67584]{0:T(1024)(128)(2,1)S(1)}, u32[]{:S(2)}, u32[]{:S(2)}) collective-permute-start(bf16[67584]{0:T(1024)(128)(2,1)S(1)} %pad_maximum_fusion.13), channel_id=1, source_target_pairs={{0,4},{1,5},{2,6},{3,7},{4,0},{5,1},{6,2},{7,3},{8,12},{9,13},{10,... | collective-permute-start | bytes 405512 | tf_op jit(solution)/shard_map/ppermute | solution.py:233
  121.1 1.3 collective-permute-start.17
  122.6 0.6 slice_multiply_fusion.1
  123.3 0.8 collective-permute-done.16
  124.1 2.0 %collective-permute-done.17 = bf16[67584]{0:T(1024)(128)(2,1)S(1)} collective-permute-done((bf16[67584]{0:T(1024)(128)(2,1)S(1)}, bf16[67584]{0:T(1024)(128)(2,1)S(1)}, u32[]{:S(2)}, u32[]{:S(2)}) %collective-permute-start.17) | collective-permute-done | bytes 135200 | tf_op jit(solution)/shard_map/ppermute | solution.py:233
  126.1 2.9 %collective-permute-done.18 = bf16[67584]{0:T(1024)(128)(2,1)S(1)} collective-permute-done((bf16[67584]{0:T(1024)(128)(2,1)S(1)}, bf16[67584]{0:T(1024)(128)(2,1)S(1)}, u32[]{:S(2)}, u32[]{:S(2)}) %collective-permute-start.18) | collective-permute-done | bytes 135200 | tf_op jit(solution)/shard_map/ppermute | solution.py:233
  129.2 0.9 pad_maximum_fusion.5
  130.4 0.9 rev.7
  131.4 0.9 pad_maximum_fusion.9
  132.4 1.2 broadcast_select_fusion.1
  134.0 0.6 maximum_convert_fusion.1
  134.7 0.6 maximum_convert_fusion.2
  135.4 1.1 reshape.152
  136.5 1.1 fusion.227
  (348 shorter events, 11.7 us)
Async XLA Ops:
  0.6 35.6 %copy-start = (bf16[1024,256]{1,0:T(8,128)(2,1)S(1)}, bf16[1024,256]{1,0:T(8,128)(2,1)}, u32[]{:S(2)}) copy-start(bf16[1024,256]{1,0:T(8,128)(2,1)} %param.23) | copy-start | bytes 1572868
  0.7 22.2 %copy-start.4 = (bf16[4,8,32,256]{3,2,1,0:T(8,128)(2,1)S(1)}, bf16[4,8,32,256]{3,2,1,0:T(8,128)(2,1)}, u32[]{:S(2)}) copy-start(bf16[4,8,32,256]{3,2,1,0:T(8,128)(2,1)} %param.13) | copy-start | bytes 1572868
  0.7 18.3 %copy-start.25 = (s32[8,32]{1,0:T(8,128)S(1)}, s32[8,32]{1,0:T(8,128)}, u32[]{:S(2)}) copy-start(s32[8,32]{1,0:T(8,128)} %param.16) | copy-start | bytes 3076
  1.7 11.2 %collective-permute-start = (bf16[4,8,3,256]{3,2,1,0:T(4,128)(2,1)S(1)}, bf16[4,8,3,256]{3,2,1,0:T(4,128)(2,1)S(1)}, u32[]{:S(2)}, u32[]{:S(2)}) collective-permute-start(bf16[4,8,3,256]{3,2,1,0:T(4,128)(2,1)S(1)} %slice.712), channel_id=1, source_target_pairs={{0,15},{1,14},{2,13},{3,12},{4,11},{5,10},{6,9},{7,8},{8,7},{9,6},... | collective-permute-start | bytes 147464 | tf_op jit(solution)/shard_map/ppermute | solution.py:174
  8.8 15.4 %copy-start.28 = (f32[1,1,256]{2,1,0:T(1,128)}, f32[1,1,256]{2,1,0:T(1,128)S(1)}, u32[]{:S(2)}) copy-start(f32[1,1,256]{2,1,0:T(1,128)S(1)} %get-tuple-element.137) | copy-start | bytes 3076
  8.8 15.4 %copy-start.30 = (f32[1,1,256]{2,1,0:T(1,128)}, f32[1,1,256]{2,1,0:T(1,128)S(1)}, u32[]{:S(2)}) copy-start(f32[1,1,256]{2,1,0:T(1,128)S(1)} %get-tuple-element.138) | copy-start | bytes 3076
  8.8 15.4 %copy-start.32 = (f32[1,1,256]{2,1,0:T(1,128)}, f32[1,1,256]{2,1,0:T(1,128)S(1)}, u32[]{:S(2)}) copy-start(f32[1,1,256]{2,1,0:T(1,128)S(1)} %get-tuple-element.139) | copy-start | bytes 3076
  8.8 15.4 %copy-start.34 = (f32[1,1,256]{2,1,0:T(1,128)}, f32[1,1,256]{2,1,0:T(1,128)S(1)}, u32[]{:S(2)}) copy-start(f32[1,1,256]{2,1,0:T(1,128)S(1)} %get-tuple-element.140) | copy-start | bytes 3076
  8.8 15.4 %copy-start.36 = (f32[1,1,256]{2,1,0:T(1,128)}, f32[1,1,256]{2,1,0:T(1,128)S(1)}, u32[]{:S(2)}) copy-start(f32[1,1,256]{2,1,0:T(1,128)S(1)} %get-tuple-element.141) | copy-start | bytes 3076
  8.8 15.4 %copy-start.38 = (f32[1,1,256]{2,1,0:T(1,128)}, f32[1,1,256]{2,1,0:T(1,128)S(1)}, u32[]{:S(2)}) copy-start(f32[1,1,256]{2,1,0:T(1,128)S(1)} %get-tuple-element.142) | copy-start | bytes 3076
  8.9 15.4 %copy-start.40 = (f32[1,1,256]{2,1,0:T(1,128)}, f32[1,1,256]{2,1,0:T(1,128)S(1)}, u32[]{:S(2)}) copy-start(f32[1,1,256]{2,1,0:T(1,128)S(1)} %get-tuple-element.143) | copy-start | bytes 3076
  8.9 15.4 %copy-start.42 = (f32[1,1,256]{2,1,0:T(1,128)}, f32[1,1,256]{2,1,0:T(1,128)S(1)}, u32[]{:S(2)}) copy-start(f32[1,1,256]{2,1,0:T(1,128)S(1)} %get-tuple-element.144) | copy-start | bytes 3076
  14.4 8.5 %collective-permute-start.1 = (bf16[4,3,38,256]{3,2,1,0:T(8,128)(2,1)S(1)}, bf16[4,3,38,256]{3,2,1,0:T(8,128)(2,1)S(1)}, u32[]{:S(2)}, u32[]{:S(2)}) collective-permute-start(bf16[4,3,38,256]{3,2,1,0:T(8,128)(2,1)S(1)} %get-tuple-element.123), channel_id=1, source_target_pairs={{0,1},{1,2},{2,3},{3,4},{4,5},{5,6},{6,7},{7,8},{8,9},{9,10},{10,1... | collective-permute-start | bytes 700424 | tf_op jit(solution)/shard_map/ppermute | solution.py:26
  15.1 7.8 %collective-permute-start.2 = (bf16[4,3,38,256]{3,2,1,0:T(8,128)(2,1)S(1)}, bf16[4,3,38,256]{3,2,1,0:T(8,128)(2,1)}, u32[]{:S(2)}, u32[]{:S(2)}) collective-permute-start(bf16[4,3,38,256]{3,2,1,0:T(8,128)(2,1)S(1)} %get-tuple-element.124), channel_id=1, source_target_pairs={{1,0},{2,1},{3,2},{4,3},{5,4},{6,5},{7,6},{8,7},{9,8},{10,9},{11,1... | collective-permute-start | bytes 700424 | tf_op jit(solution)/shard_map/ppermute | solution.py:27
  18.9 5.3 %copy-start.110 = (s32[256]{0:T(256)}, s32[256]{0:T(256)S(1)}, u32[]{:S(2)}) copy-start(s32[256]{0:T(256)S(1)} %and_select_fusion) | copy-start | bytes 3076
  19.1 5.3 %copy-start.5 = (bf16[4,8,32,256]{3,2,1,0:T(8,128)(2,1)S(1)}, bf16[4,8,32,256]{3,2,1,0:T(8,128)(2,1)}, u32[]{:S(2)}) copy-start(bf16[4,8,32,256]{3,2,1,0:T(8,128)(2,1)} %param.13) | copy-start | bytes 1572868
  19.1 5.2 %copy-start.44 = (f32[1,1,256]{2,1,0:T(1,128)S(1)}, f32[1,1,256]{2,1,0:T(1,128)}, u32[]{:S(2)}) copy-start(f32[1,1,256]{2,1,0:T(1,128)} %get-tuple-element.145) | copy-start | bytes 3076
  19.1 5.2 %copy-start.46 = (f32[1,1,256]{2,1,0:T(1,128)S(1)}, f32[1,1,256]{2,1,0:T(1,128)}, u32[]{:S(2)}) copy-start(f32[1,1,256]{2,1,0:T(1,128)} %get-tuple-element.146) | copy-start | bytes 3076
  19.1 5.2 %copy-start.48 = (f32[1,1,256]{2,1,0:T(1,128)S(1)}, f32[1,1,256]{2,1,0:T(1,128)}, u32[]{:S(2)}) copy-start(f32[1,1,256]{2,1,0:T(1,128)} %get-tuple-element.147) | copy-start | bytes 3076
  19.1 5.2 %copy-start.50 = (f32[1,1,256]{2,1,0:T(1,128)S(1)}, f32[1,1,256]{2,1,0:T(1,128)}, u32[]{:S(2)}) copy-start(f32[1,1,256]{2,1,0:T(1,128)} %get-tuple-element.148) | copy-start | bytes 3076
  19.1 5.2 %copy-start.52 = (f32[1,1,256]{2,1,0:T(1,128)S(1)}, f32[1,1,256]{2,1,0:T(1,128)}, u32[]{:S(2)}) copy-start(f32[1,1,256]{2,1,0:T(1,128)} %get-tuple-element.149) | copy-start | bytes 3076
  19.1 5.2 %copy-start.54 = (f32[1,1,256]{2,1,0:T(1,128)S(1)}, f32[1,1,256]{2,1,0:T(1,128)}, u32[]{:S(2)}) copy-start(f32[1,1,256]{2,1,0:T(1,128)} %get-tuple-element.150) | copy-start | bytes 3076
  19.1 5.2 %copy-start.56 = (f32[1,1,256]{2,1,0:T(1,128)S(1)}, f32[1,1,256]{2,1,0:T(1,128)}, u32[]{:S(2)}) copy-start(f32[1,1,256]{2,1,0:T(1,128)} %get-tuple-element.151) | copy-start | bytes 3076
  19.1 5.2 %copy-start.58 = (f32[1,1,256]{2,1,0:T(1,128)S(1)}, f32[1,1,256]{2,1,0:T(1,128)}, u32[]{:S(2)}) copy-start(f32[1,1,256]{2,1,0:T(1,128)} %get-tuple-element.152) | copy-start | bytes 3076
  19.2 5.2 %copy-start.60 = (f32[1,1,256]{2,1,0:T(1,128)S(1)}, f32[1,1,256]{2,1,0:T(1,128)}, u32[]{:S(2)}) copy-start(f32[1,1,256]{2,1,0:T(1,128)} %get-tuple-element.153) | copy-start | bytes 3076
  19.2 5.2 %copy-start.62 = (f32[1,1,256]{2,1,0:T(1,128)S(1)}, f32[1,1,256]{2,1,0:T(1,128)}, u32[]{:S(2)}) copy-start(f32[1,1,256]{2,1,0:T(1,128)} %get-tuple-element.154) | copy-start | bytes 3076
  19.2 5.2 %copy-start.64 = (f32[1,1,256]{2,1,0:T(1,128)S(1)}, f32[1,1,256]{2,1,0:T(1,128)}, u32[]{:S(2)}) copy-start(f32[1,1,256]{2,1,0:T(1,128)} %get-tuple-element.155) | copy-start | bytes 3076
  19.2 5.2 %copy-start.66 = (f32[1,1,256]{2,1,0:T(1,128)S(1)}, f32[1,1,256]{2,1,0:T(1,128)}, u32[]{:S(2)}) copy-start(f32[1,1,256]{2,1,0:T(1,128)} %get-tuple-element.156) | copy-start | bytes 3076
  19.2 5.2 %copy-start.68 = (f32[1,1,256]{2,1,0:T(1,128)S(1)}, f32[1,1,256]{2,1,0:T(1,128)}, u32[]{:S(2)}) copy-start(f32[1,1,256]{2,1,0:T(1,128)} %get-tuple-element.157) | copy-start | bytes 3076
  19.2 5.2 %copy-start.70 = (f32[1,1,256]{2,1,0:T(1,128)S(1)}, f32[1,1,256]{2,1,0:T(1,128)}, u32[]{:S(2)}) copy-start(f32[1,1,256]{2,1,0:T(1,128)} %get-tuple-element.158) | copy-start | bytes 3076
  19.2 5.2 %copy-start.72 = (f32[1,1,256]{2,1,0:T(1,128)S(1)}, f32[1,1,256]{2,1,0:T(1,128)}, u32[]{:S(2)}) copy-start(f32[1,1,256]{2,1,0:T(1,128)} %get-tuple-element.159) | copy-start | bytes 3076
  19.2 5.2 %copy-start.74 = (f32[1,1,256]{2,1,0:T(1,128)S(1)}, f32[1,1,256]{2,1,0:T(1,128)}, u32[]{:S(2)}) copy-start(f32[1,1,256]{2,1,0:T(1,128)} %get-tuple-element.160) | copy-start | bytes 3076
  19.2 5.2 %copy-start.76 = (f32[1,1,256]{2,1,0:T(1,128)S(1)}, f32[1,1,256]{2,1,0:T(1,128)}, u32[]{:S(2)}) copy-start(f32[1,1,256]{2,1,0:T(1,128)} %get-tuple-element.161) | copy-start | bytes 3076
  19.2 5.2 %copy-start.78 = (f32[1,1,256]{2,1,0:T(1,128)S(1)}, f32[1,1,256]{2,1,0:T(1,128)}, u32[]{:S(2)}) copy-start(f32[1,1,256]{2,1,0:T(1,128)} %get-tuple-element.162) | copy-start | bytes 3076
  19.3 5.2 %copy-start.80 = (f32[1,1,256]{2,1,0:T(1,128)S(1)}, f32[1,1,256]{2,1,0:T(1,128)}, u32[]{:S(2)}) copy-start(f32[1,1,256]{2,1,0:T(1,128)} %get-tuple-element.163) | copy-start | bytes 3076
  24.7 9.7 %copy-start.27 = (f32[256]{0:T(256)S(1)}, f32[256]{0:T(256)}, u32[]{:S(2)}) copy-start(f32[256]{0:T(256)} %param.19) | copy-start | bytes 3076
  42.6 12.4 %copy-start.11 = (f32[8,32,256]{2,1,0:T(8,128)}, f32[8,32,256]{2,1,0:T(8,128)S(1)}, u32[]{:S(2)}) copy-start(f32[8,32,256]{2,1,0:T(8,128)S(1)} %get-tuple-element.91) | copy-start | bytes 786436
  42.6 12.4 %copy-start.13 = (f32[8,32,256]{2,1,0:T(8,128)}, f32[8,32,256]{2,1,0:T(8,128)S(1)}, u32[]{:S(2)}) copy-start(f32[8,32,256]{2,1,0:T(8,128)S(1)} %get-tuple-element.92) | copy-start | bytes 786436
  42.6 12.4 %copy-start.15 = (f32[8,32,256]{2,1,0:T(8,128)}, f32[8,32,256]{2,1,0:T(8,128)S(1)}, u32[]{:S(2)}) copy-start(f32[8,32,256]{2,1,0:T(8,128)S(1)} %get-tuple-element.93) | copy-start | bytes 786436
  42.6 12.4 %copy-start.17 = (f32[8,32,256]{2,1,0:T(8,128)}, f32[8,32,256]{2,1,0:T(8,128)S(1)}, u32[]{:S(2)}) copy-start(f32[8,32,256]{2,1,0:T(8,128)S(1)} %get-tuple-element.94) | copy-start | bytes 786436
  57.0 3.3 %collective-permute-start.3 = (f32[270336]{0:T(1024)}, f32[270336]{0:T(1024)}, u32[]{:S(2)}, u32[]{:S(2)}) collective-permute-start(f32[270336]{0:T(1024)} %pad_dynamic-slice_fusion), channel_id=1, source_target_pairs={{0,1},{1,0},{2,3},{3,2},{4,5},{5,4},{6,7},{7,6},{8,9},{9,8},{10,11... | collective-permute-start | bytes 3244040 | tf_op jit(solution)/shard_map/ppermute | solution.py:221
  57.6 5.4 %copy-start.7 = (f32[4,8,32,256]{3,2,1,0:T(8,128)S(1)}, f32[4,8,32,256]{3,2,1,0:T(8,128)}, u32[]{:S(2)}) copy-start(f32[4,8,32,256]{3,2,1,0:T(8,128)} %get-tuple-element.19) | copy-start | bytes 3145732
  72.4 12.1 %copy-start.2 = (f32[4,8,32,256]{3,2,1,0:T(8,128)S(1)}, f32[4,8,32,256]{3,2,1,0:T(8,128)}, u32[]{:S(2)}) copy-start(f32[4,8,32,256]{3,2,1,0:T(8,128)} %copy-done.1) | copy-start | bytes 3145732
  72.9 6.1 %collective-permute-start.10 = (f32[12800]{0:T(1024)S(1)}, f32[12800]{0:T(1024)S(1)}, u32[]{:S(2)}, u32[]{:S(2)}) collective-permute-start(f32[12800]{0:T(1024)S(1)} %pad_maximum_fusion.14), channel_id=1, source_target_pairs={{0,1},{1,0},{2,3},{3,2},{4,5},{5,4},{6,7},{7,6},{8,9},{9,8},{10,11... | collective-permute-start | bytes 153608 | tf_op jit(solution)/shard_map/ppermute | solution.py:16
  74.5 10.1 %collective-permute-start.4 = (f32[4,3,32,256]{3,2,1,0:T(8,128)S(1)}, f32[4,3,32,256]{3,2,1,0:T(8,128)S(1)}, u32[]{:S(2)}, u32[]{:S(2)}) collective-permute-start(f32[4,3,32,256]{3,2,1,0:T(8,128)S(1)} %get-tuple-element.117), channel_id=1, source_target_pairs={{0,1},{1,2},{2,3},{3,4},{4,5},{5,6},{6,7},{7,8},{8,9},{9,10},{10,1... | collective-permute-start | bytes 1179656 | tf_op jit(solution)/shard_map/ppermute | solution.py:26
  74.7 9.9 %collective-permute-start.5 = (f32[4,3,32,256]{3,2,1,0:T(8,128)S(1)}, f32[4,3,32,256]{3,2,1,0:T(8,128)S(1)}, u32[]{:S(2)}, u32[]{:S(2)}) collective-permute-start(f32[4,3,32,256]{3,2,1,0:T(8,128)S(1)} %get-tuple-element.118), channel_id=1, source_target_pairs={{1,0},{2,1},{3,2},{4,3},{5,4},{6,5},{7,6},{8,7},{9,8},{10,9},{11,1... | collective-permute-start | bytes 1179656 | tf_op jit(solution)/shard_map/ppermute | solution.py:27
  79.0 5.7 %copy-start.10 = (f32[270336]{0:T(1024)S(1)}, f32[270336]{0:T(1024)}, u32[]{:S(2)}) copy-start(f32[270336]{0:T(1024)} %fusion.99) | copy-start | bytes 3244036
  79.0 24.9 %collective-permute-start.11 = (f32[12800]{0:T(1024)S(1)}, f32[12800]{0:T(1024)S(1)}, u32[]{:S(2)}, u32[]{:S(2)}) collective-permute-start(f32[12800]{0:T(1024)S(1)} %fusion.311), channel_id=1, source_target_pairs={{0,2},{1,3},{2,0},{3,1},{4,6},{5,7},{6,4},{7,5},{8,10},{9,11},{10,... | collective-permute-start | bytes 153608 | tf_op jit(solution)/shard_map/ppermute | solution.py:16
  85.1 14.2 %collective-permute-start.6 = (f32[67584]{0:T(1024)S(1)}, f32[67584]{0:T(1024)S(1)}, u32[]{:S(2)}, u32[]{:S(2)}) collective-permute-start(f32[67584]{0:T(1024)S(1)} %get-tuple-element.114), channel_id=1, source_target_pairs={{0,2},{1,3},{2,0},{3,1},{4,6},{5,7},{6,4},{7,5},{8,10},{9,11},{10,... | collective-permute-start | bytes 811016 | tf_op jit(solution)/shard_map/ppermute | solution.py:221
  87.2 12.1 %collective-permute-start.7 = (f32[67584]{0:T(1024)S(1)}, f32[67584]{0:T(1024)S(1)}, u32[]{:S(2)}, u32[]{:S(2)}) collective-permute-start(f32[67584]{0:T(1024)S(1)} %get-tuple-element.116), channel_id=1, source_target_pairs={{0,4},{1,5},{2,6},{3,7},{4,0},{5,1},{6,2},{7,3},{8,12},{9,13},{10,... | collective-permute-start | bytes 811016 | tf_op jit(solution)/shard_map/ppermute | solution.py:221
  87.2 13.9 %collective-permute-start.8 = (f32[67584]{0:T(1024)S(1)}, f32[67584]{0:T(1024)S(1)}, u32[]{:S(2)}, u32[]{:S(2)}) collective-permute-start(f32[67584]{0:T(1024)S(1)} %get-tuple-element.115), channel_id=1, source_target_pairs={{0,6},{1,7},{2,4},{3,5},{4,2},{5,3},{6,0},{7,1},{8,14},{9,15},{10,... | collective-permute-start | bytes 811016 | tf_op jit(solution)/shard_map/ppermute | solution.py:221
  101.2 12.2 %collective-permute-start.14 = (f32[33792]{0:T(1024)S(1)}, f32[33792]{0:T(1024)S(1)}, u32[]{:S(2)}, u32[]{:S(2)}) collective-permute-start(f32[33792]{0:T(1024)S(1)} %dynamic_slice.31), channel_id=1, source_target_pairs={{0,8},{1,9},{2,10},{3,11},{4,12},{5,13},{6,14},{7,15},{8,0},{9,1},... | collective-permute-start | bytes 405512 | tf_op jit(solution)/shard_map/ppermute | solution.py:221
  103.9 4.3 %collective-permute-start.12 = (f32[12800]{0:T(1024)S(1)}, f32[12800]{0:T(1024)S(1)}, u32[]{:S(2)}, u32[]{:S(2)}) collective-permute-start(f32[12800]{0:T(1024)S(1)} %add.802), channel_id=1, source_target_pairs={{0,4},{1,5},{2,6},{3,7},{4,0},{5,1},{6,2},{7,3},{8,12},{9,13},{10,... | collective-permute-start | bytes 153608 | tf_op jit(solution)/shard_map/ppermute | solution.py:16
  108.2 5.1 %collective-permute-start.13 = (f32[12800]{0:T(1024)S(1)}, f32[12800]{0:T(1024)S(1)}, u32[]{:S(2)}, u32[]{:S(2)}) collective-permute-start(f32[12800]{0:T(1024)S(1)} %add.803), channel_id=1, source_target_pairs={{0,8},{1,9},{2,10},{3,11},{4,12},{5,13},{6,14},{7,15},{8,0},{9,1},... | collective-permute-start | bytes 153608 | tf_op jit(solution)/shard_map/ppermute | solution.py:16
  113.4 5.3 %collective-permute-start.15 = (bf16[33792]{0:T(1024)(128)(2,1)S(1)}, bf16[33792]{0:T(1024)(128)(2,1)S(1)}, u32[]{:S(2)}, u32[]{:S(2)}) collective-permute-start(bf16[33792]{0:T(1024)(128)(2,1)S(1)} %multiply_convert_fusion.8), channel_id=1, source_target_pairs={{0,8},{1,9},{2,10},{3,11},{4,12},{5,13},{6,14},{7,15},{8,0},{9,1},... | collective-permute-start | bytes 202760 | tf_op jit(solution)/shard_map/ppermute | solution.py:233
  118.7 11.4 %copy-start.12 = (f32[8,32,256]{2,1,0:T(8,128)S(1)}, f32[8,32,256]{2,1,0:T(8,128)}, u32[]{:S(2)}) copy-start(f32[8,32,256]{2,1,0:T(8,128)} %copy-done.11) | copy-start | bytes 786436
  118.7 11.4 %copy-start.14 = (f32[8,32,256]{2,1,0:T(8,128)S(1)}, f32[8,32,256]{2,1,0:T(8,128)}, u32[]{:S(2)}) copy-start(f32[8,32,256]{2,1,0:T(8,128)} %copy-done.13) | copy-start | bytes 786436
  118.7 11.4 %copy-start.16 = (f32[8,32,256]{2,1,0:T(8,128)S(1)}, f32[8,32,256]{2,1,0:T(8,128)}, u32[]{:S(2)}) copy-start(f32[8,32,256]{2,1,0:T(8,128)} %copy-done.15) | copy-start | bytes 786436
  118.7 11.4 %copy-start.18 = (f32[8,32,256]{2,1,0:T(8,128)S(1)}, f32[8,32,256]{2,1,0:T(8,128)}, u32[]{:S(2)}) copy-start(f32[8,32,256]{2,1,0:T(8,128)} %copy-done.17) | copy-start | bytes 786436
  118.7 5.4 %collective-permute-start.16 = (bf16[67584]{0:T(1024)(128)(2,1)S(1)}, bf16[67584]{0:T(1024)(128)(2,1)S(1)}, u32[]{:S(2)}, u32[]{:S(2)}) collective-permute-start(bf16[67584]{0:T(1024)(128)(2,1)S(1)} %pad_maximum_fusion.13), channel_id=1, source_target_pairs={{0,4},{1,5},{2,6},{3,7},{4,0},{5,1},{6,2},{7,3},{8,12},{9,13},{10,... | collective-permute-start | bytes 405512 | tf_op jit(solution)/shard_map/ppermute | solution.py:233
  121.1 5.0 %collective-permute-start.17 = (bf16[67584]{0:T(1024)(128)(2,1)S(1)}, bf16[67584]{0:T(1024)(128)(2,1)S(1)}, u32[]{:S(2)}, u32[]{:S(2)}) collective-permute-start(bf16[67584]{0:T(1024)(128)(2,1)S(1)} %pad_maximum_fusion.13), channel_id=1, source_target_pairs={{0,2},{1,3},{2,0},{3,1},{4,6},{5,7},{6,4},{7,5},{8,10},{9,11},{10,... | collective-permute-start | bytes 405512 | tf_op jit(solution)/shard_map/ppermute | solution.py:233
  122.4 6.6 %collective-permute-start.18 = (bf16[67584]{0:T(1024)(128)(2,1)S(1)}, bf16[67584]{0:T(1024)(128)(2,1)S(1)}, u32[]{:S(2)}, u32[]{:S(2)}) collective-permute-start(bf16[67584]{0:T(1024)(128)(2,1)S(1)} %pad_maximum_fusion.13), channel_id=1, source_target_pairs={{0,6},{1,7},{2,4},{3,5},{4,2},{5,3},{6,0},{7,1},{8,14},{9,15},{10,... | collective-permute-start | bytes 405512 | tf_op jit(solution)/shard_map/ppermute | solution.py:233
  123.2 7.2 %collective-permute-start.9 = (bf16[4,8,3,256]{3,2,1,0:T(4,128)(2,1)S(1)}, bf16[4,8,3,256]{3,2,1,0:T(4,128)(2,1)}, u32[]{:S(2)}, u32[]{:S(2)}) collective-permute-start(bf16[4,8,3,256]{3,2,1,0:T(4,128)(2,1)S(1)} %slice.1627), channel_id=1, source_target_pairs={{0,15},{1,14},{2,13},{3,12},{4,11},{5,10},{6,9},{7,8},{8,7},{9,6},... | collective-permute-start | bytes 147464 | tf_op jit(solution)/shard_map/ppermute | solution.py:174
  130.1 2.3 %collective-permute-start.19 = (bf16[270336]{0:T(1024)(128)(2,1)}, bf16[270336]{0:T(1024)(128)(2,1)}, u32[]{:S(2)}, u32[]{:S(2)}) collective-permute-start(bf16[270336]{0:T(1024)(128)(2,1)} %pad_maximum_fusion.5), channel_id=1, source_target_pairs={{0,1},{1,0},{2,3},{3,2},{4,5},{5,4},{6,7},{7,6},{8,9},{9,8},{10,11... | collective-permute-start | bytes 1622024 | tf_op jit(solution)/shard_map/ppermute | solution.py:233
  (86 other events, 277.4 us)

commit v15 on v12

--- a/solution.py
+++ b/solution.py
@@ -202,7 +202,7 @@
     return cur.astype(flat.dtype)
 
 
-def radix_allreduce(flat, axis, gather_dtype, operand, start, finish):
+def radix_allreduce(flat, axis, gather_dtype, operand, start, finish, fill):
     size = lax.axis_size(axis)
     nbits = size.bit_length() - 1
     groups = [[0]] + [list(range(b, min(b + 2, nbits))) for b in range(1, nbits, 2)]
@@ -225,6 +225,9 @@
             first = start(operand)
         elif bits == groups[1]:
             cur, second = lax.optimization_barrier((cur, second))
+            third = fill(second)
+        elif bits == groups[2]:
+            cur, third = lax.optimization_barrier((cur, third))
     cur = cur.astype(gather_dtype)
     for bits in reversed(groups):
         radix, low = 1 << len(bits), bits[0]
@@ -240,7 +243,7 @@
                 pick = jnp.where(sub == s, pieces[p ^ s], pick)
             placed.append(pick)
         cur = jnp.concatenate(placed)
-    return cur.astype(flat.dtype), first[1:], second
+    return cur.astype(flat.dtype), first[1:], second, third
 
 
 def butterfly_allreduce(flat, axis):
@@ -310,8 +313,17 @@
         return grad_ext
 
     lon_size = lax.axis_size("lon")
-    reduced, (kernel_sum, dw_bias_sum), grad_ext = radix_allreduce(
-        pack(sums, lon_size * 1024), "lon", jnp.bfloat16, grad_normed, backward, backward_conv
+    def grad_features_main(grad_ext):
+        return (grad_pred[:, :, : lat_rows - 3] + grad_ext[:, :, 3:lat_rows]).astype(jnp.bfloat16)
+
+    reduced, (kernel_sum, dw_bias_sum), grad_ext, main_rows = radix_allreduce(
+        pack(sums, lon_size * 1024),
+        "lon",
+        jnp.bfloat16,
+        grad_normed,
+        backward,
+        backward_conv,
+        grad_features_main,
     )
     gain_sum, bias_sum, w_in_sum, b_in_sum, w_out_sum, b_out_sum, scale_sum = unpack(reduced, sums)
     small = (kernel_sum, dw_bias_sum)
@@ -328,10 +340,10 @@
         scale_sum,
     )
     back_rows = mirror_grads(grad_ext[:, :, lat_rows + 3 :, :])
-    inner = grad_pred + grad_ext[:, :, 3 : lat_rows + 3, :]
-    grad_features = jnp.concatenate(
-        [inner[:, :, : lat_rows - 3, :], inner[:, :, lat_rows - 3 :, :] + back_rows], axis=2
-    ).astype(jnp.bfloat16)
+    fold_rows = (
+        grad_pred[:, :, lat_rows - 3 :] + grad_ext[:, :, lat_rows : lat_rows + 3]
+    ) + back_rows
+    grad_features = jnp.concatenate([main_rows, fold_rows.astype(jnp.bfloat16)], axis=2)
     factor = 1.0 / math.sqrt(members * lat_rows * lon_dev * lax.axis_size("lon"))
     return (
         predicted,

time: 138 us -> 145 us (1.051)
  local copies, waits for them, and re-layouts: 16.2 us -> 19.6 us
  other arithmetic: 47.6 us -> 50.8 us
    ppermute x4, waiting for transfers between devices: 6.01 us -> 13 us  [swapped(): lax.ppermute(x, axis, [(i, i ^ 1 << bit) for i in range(lax.axis_size(axi...]
    ppermute x2, waiting for transfers between devices: 8.91 us -> 3.45 us  [with_halo(): before = lax.ppermute(last, axis, up)]
    ppermute x5, waiting for transfers between devices: 8.75 us -> 3.34 us  [radix_allreduce(): lax.ppermute(cur, axis, [(i, i ^ d << low) for i in range(size)])]
    ppermute x5, waiting for transfers between devices: 4.43 us -> 8.79 us  [radix_allreduce(): lax.ppermute(send, axis, [(i, i ^ d << low) for i in range(size)])]
    ppermute x5, starting transfers between devices: 5.51 us -> 3.63 us  [radix_allreduce(): lax.ppermute(cur, axis, [(i, i ^ d << low) for i in range(size)])]
    unnamed x272 -> x262, local copies, waits for them, and re-layouts: 4.29 us -> 5.79 us
  transfers between devices with their start and end apart: 20 -> 20, of which waited for: 10 -> 7; matrix products, arithmetic and copies ran while one was open for 16% -> 18% of each run, Pallas kernels for 0% -> 0%
where the time goes in v15:
time: 145 us; the launch traced here: 144 us
  other arithmetic  50.8 us (35%)
  starting transfers between devices  29.8 us (21%)
  waiting for transfers between devices  28.6 us (20%)
  local copies, waits for them, and re-layouts  19.6 us (14%)
  matrix products  11.8 us (8%)
  between operations  3.01 us (2%)
    ppermute x4, waiting for transfers between devices, swapped(): lax.ppermute(x, axis, [(i, i ^ 1 << bit) for i in range(lax.axis_size(axi...  13 us
    add x1, other arithmetic, backward_conv(): grad_ext + dw_kernel[lon_off, lat_off] * padded[:, 6 - lon_off:6 - lon_of...  10.2 us
    reduce_sum x1, other arithmetic, local_step(): mean_val = jnp.mean(depth, axis=-1, keepdims=True)  9.29 us
    ppermute x5, waiting for transfers between devices, radix_allreduce(): lax.ppermute(send, axis, [(i, i ^ d << low) for i in range(size)])  8.79 us
    reduce_sum x4, other arithmetic, depth_backward(): jnp.sum(grad_depth * extended[:, lon_off:lon_off + lon_dev, lat_off:lat_o...  8.53 us
    ppermute x2, starting transfers between devices, with_halo(): after = lax.ppermute(leading, axis, down)  8.05 us
    ppermute x5, starting transfers between devices, radix_allreduce(): lax.ppermute(send, axis, [(i, i ^ d << low) for i in range(size)])  7.36 us
    ppermute x2, starting transfers between devices, mirrored(): return lax.ppermute(x, axis, [(i, size - 1 - i) for i in range(size)])  6.33 us
  transfers between devices with their start and end apart: 20, of which 7 were waited for; matrix products, arithmetic and copies ran while one was open for 18% of the time, Pallas kernels for 0%

profile of v15, /device:TPU:0, one launch (start us, length us, event | category | flops | bytes accessed | tf_op | source)
XLA Modules:
  0.0 143.7 jit_solution(508798891683527182)
XLA Ops:
  0.7 1.0 slice.714
  1.7 5.5 %collective-permute-start = (bf16[4,8,3,256]{3,2,1,0:T(4,128)(2,1)S(1)}, bf16[4,8,3,256]{3,2,1,0:T(4,128)(2,1)S(1)}, u32[]{:S(2)}, u32[]{:S(2)}) collective-permute-start(bf16[4,8,3,256]{3,2,1,0:T(4,128)(2,1)S(1)} %slice.714), channel_id=1, source_target_pairs={{0,15},{1,14},{2,13},{3,12},{4,11},{5,10},{6,9},{7,8},{8,7},{9,6},... | collective-permute-start | bytes 147464 | tf_op jit(solution)/shard_map/ppermute | solution.py:174
  7.2 1.6 %fusion.265 = (f32[1,1,256]{2,1,0:T(1,128)S(1)}, f32[1,1,256]{2,1,0:T(1,128)S(1)}, f32[1,1,256]{2,1,0:T(1,128)S(1)}, f32[1,1,256]{2,1,0:T(1,128)S(1)}, f32[1,1,2...) fusion(f32[7,7,256]{2,1,0:T(8,128)} %param.17), kind=kLoop, calls=%fused_computation.544 | loop fusion | bytes 38912 | tf_op jit(solution)/shard_map/slice | solution.py:59
  8.9 1.7 %fusion.266 = (f32[1,1,256]{2,1,0:T(1,128)}, f32[1,1,256]{2,1,0:T(1,128)}, f32[1,1,256]{2,1,0:T(1,128)}, f32[1,1,256]{2,1,0:T(1,128)}, f32[1,1,256]{2,1,0:T(1,12...) fusion(f32[7,7,256]{2,1,0:T(8,128)} %param.17), kind=kLoop, calls=%fused_computation.545 | loop fusion | bytes 38912 | tf_op jit(solution)/shard_map/slice | solution.py:59
  10.5 1.5 %fusion.267 = (f32[1,1,256]{2,1,0:T(1,128)}, f32[1,1,256]{2,1,0:T(1,128)}, f32[1,1,256]{2,1,0:T(1,128)}, f32[1,1,256]{2,1,0:T(1,128)}, f32[1,1,256]{2,1,0:T(1,12...) fusion(f32[7,7,256]{2,1,0:T(8,128)} %param.17), kind=kLoop, calls=%fused_computation.546 | loop fusion | bytes 22528 | tf_op jit(solution)/shard_map/slice | solution.py:59
  12.1 0.8 copy.25
  13.1 1.3 pad_maximum_fusion.12
  14.4 0.7 collective-permute-start.1
  15.2 3.8 %collective-permute-start.2 = (bf16[4,3,38,256]{3,2,1,0:T(8,128)(2,1)S(1)}, bf16[4,3,38,256]{3,2,1,0:T(8,128)(2,1)S(1)}, u32[]{:S(2)}, u32[]{:S(2)}) collective-permute-start(bf16[4,3,38,256]{3,2,1,0:T(8,128)(2,1)S(1)} %get-tuple-element.130), channel_id=1, source_target_pairs={{1,0},{2,1},{3,2},{4,3},{5,4},{6,5},{7,6},{8,7},{9,8},{10,9},{11,1... | collective-permute-start | bytes 700424 | tf_op jit(solution)/shard_map/ppermute | solution.py:27
  19.4 3.5 %collective-permute-done.1 = bf16[4,3,38,256]{3,2,1,0:T(8,128)(2,1)S(1)} collective-permute-done((bf16[4,3,38,256]{3,2,1,0:T(8,128)(2,1)S(1)}, bf16[4,3,38,256]{3,2,1,0:T(8,128)(2,1)S(1)}, u32[]{:S(2)}, u32[]{:S(2)}) %collective-permute-start.1) | collective-permute-done | bytes 233504 | tf_op jit(solution)/shard_map/ppermute | solution.py:26
  23.8 9.3 %fusion.260 = (f32[4,8,32]{2,1,0:T(8,128)S(1)}, f32[4,8,32,256]{3,2,1,0:T(8,128)S(1)}) fusion(bf16[4,11,38,256]{3,2,1,0:T(8,128)(2,1)S(1)} %get-tuple-element.128, f32[256]{0:T(256)} %bitcast.428, f32[256]{0:T(256)} %bitcast.430, f32[256]{0:T(256)S(1)} %bitcast.336, f32[256]{0:T(256)S(1)} %bitcast.338, f32[256]{0:T(256)S(1)} %bitcast.340, ...), kind=kLoop, calls=%fused_computation.540 | loop fusion | flops 43514880 | bytes 23746560 | tf_op jit(solution)/shard_map/reduce_sum | solution.py:62
  33.5 1.1 add_convert_fusion
  38.1 1.1 fusion.258
  39.1 2.5 %multiply_reduce_fusion.7 = (f32[256]{0:T(256)S(1)}, f32[256]{0:T(256)S(1)}, f32[256]{0:T(256)S(1)}, f32[256]{0:T(256)S(1)}, f32[8,32,256]{2,1,0:T(8,128)S(1)}, ...) fusion(f32[256]{0:T(256)S(1)} %copy-done.21, ...), kind=kLoop, calls=%fused_computation.479 | loop fusion | flops 7863296 | bytes 2497536 | tf_op jit(solution)/shard_map/reduce_sum | solution.py:117
  42.4 0.9 fusion.252
  44.0 0.9 fusion.250
  44.9 0.6 convolution_add_fusion.2
  45.5 0.9 fusion.254
  46.4 0.6 convolution_add_fusion.1
  47.0 0.9 fusion.256
  47.9 0.6 fusion
  48.5 0.8 copy.28
  51.5 1.3 pad_maximum_fusion.2
  52.8 0.7 copy-done.8
  54.0 1.1 pad_maximum_fusion.3
  55.2 1.2 pad_dynamic-slice_fusion
  56.8 0.6 collective-permute-start.3
  57.4 2.7 %collective-permute-done.3 = f32[270336]{0:T(1024)} collective-permute-done((f32[270336]{0:T(1024)}, f32[270336]{0:T(1024)}, u32[]{:S(2)}, u32[]{:S(2)}) %collective-permute-start.3) | collective-permute-done | bytes 1081376 | tf_op jit(solution)/shard_map/ppermute | solution.py:221
  60.1 2.7 %fusion.99 = f32[270336]{0:T(1024)} fusion(f32[270336]{0:T(1024)} %collective-permute-done.3, s32[]{:T(128)S(6)} %select_n.114, f32[526336]{0:T(1024)} %copy-done.9), kind=kLoop, calls=%fused_computation.272 | loop fusion | flops 270336 | bytes 4268036 | tf_op jit(solution)/shard_map/add | solution.py:221
  62.8 0.6 multiply_reduce_fusion.4
  63.4 3.8 %fusion.196 = (f32[256]{0:T(256)S(1)}, f32[256]{0:T(256)}, f32[256]{0:T(256)}, f32[256]{0:T(256)}, f32[256]{0:T(256)}, /*index=5*/f32[256]{0:T(256)}, f32[256]{0...) fusion(bf16[4,11,38,256]{3,2,1,0:T(8,128)(2,1)S(1)} %get-tuple-, ...), kind=kLoop, calls=%fused_computation.370 | loop fusion | flops 15986176 | bytes 12618752 | tf_op jit(solution)/shard_map/reduce_sum | solution.py:156
  67.2 1.8 %fusion.178 = (f32[256]{0:T(256)S(1)}, f32[256]{0:T(256)S(1)}, f32[256]{0:T(256)S(1)}, f32[256]{0:T(256)S(1)}, f32[256]{0:T(256)S(1)}, /*index=5*/f32[256]{0:T(2...) fusion(f32[4,8,32,256]{3,2,1,0:T(8,128)S(1)} %get-tuple-element.94, ...), kind=kLoop, calls=%fused_computation.352 | loop fusion | flops 12842240 | bytes 3255296 | tf_op jit(solution)/shard_map/reduce_sum | solution.py:156
  69.0 2.6 %fusion.145 = (f32[256]{0:T(256)S(1)}, f32[256]{0:T(256)S(1)}, f32[256]{0:T(256)S(1)}, f32[256]{0:T(256)S(1)}, f32[256]{0:T(256)S(1)}, /*index=5*/f32[256]{0:T(2...) fusion(f32[4,8,32,256]{3,2,1,0:T(8,128)S(1)} %get-tuple-element, ...), kind=kLoop, calls=%fused_computation.319 | loop fusion | flops 14151168 | bytes 10504192 | tf_op jit(solution)/shard_map/reduce_sum | solution.py:156
  73.1 1.2 fusion.263
  74.5 4.3 %collective-permute-start.5 = (f32[4,3,32,256]{3,2,1,0:T(8,128)S(1)}, f32[4,3,32,256]{3,2,1,0:T(8,128)S(1)}, u32[]{:S(2)}, u32[]{:S(2)}) collective-permute-start(f32[4,3,32,256]{3,2,1,0:T(8,128)S(1)} %get-tuple-element.124), channel_id=1, source_target_pairs={{1,0},{2,1},{3,2},{4,3},{5,4},{6,5},{7,6},{8,7},{9,8},{10,9},{11,1... | collective-permute-start | bytes 1179656 | tf_op jit(solution)/shard_map/ppermute | solution.py:27
  78.9 8.3 %collective-permute-done.12 = f32[12800]{0:T(1024)S(1)} collective-permute-done((f32[12800]{0:T(1024)S(1)}, f32[12800]{0:T(1024)S(1)}, u32[]{:S(2)}, u32[]{:S(2)}) %collective-permute-start.12) | collective-permute-done | bytes 51232 | tf_op jit(solution)/shard_map/ppermute | solution.py:16
  87.6 0.9 copy-done.11
  89.0 1.2 collective-permute-start.7
  90.2 2.3 %collective-permute-start.8 = (f32[67584]{0:T(1024)S(1)}, f32[67584]{0:T(1024)S(1)}, u32[]{:S(2)}, u32[]{:S(2)}) collective-permute-start(f32[67584]{0:T(1024)S(1)} %get-tuple-element.119), channel_id=1, source_target_pairs={{0,6},{1,7},{2,4},{3,5},{4,2},{5,3},{6,0},{7,1},{8,14},{9,15},{10,... | collective-permute-start | bytes 811016 | tf_op jit(solution)/shard_map/ppermute | solution.py:221
  92.8 10.2 %fusion.95 = f32[4,8,38,256]{3,2,1,0:T(8,128)S(1)} fusion(f32[4,14,32,256]{3,2,1,0:T(8,128)S(1)} %pad_maximum_fusion, f32[256]{0:T(256)} %bitcast.429, f32[256]{0:T(256)} %bitcast.431, f32[256]{0:T(256)S(1)} %bitcast.337, f32[256]{0:T(256)S(1)} %bitcast.339, f32[256]{0:T(256)S(1)} %bitcast.341, f32[256]{0:T(256)S(1)} %bitcast.343, f32[256]{0:T(256)S(1)} %bitcast.345, ...), kind=kLoop, calls=%fused_computation.264 | loop fusion | flops 30195712 | bytes 3130368 | tf_op jit(solution)/shard_map/add | solution.py:304
  103.2 3.2 %collective-permute-start.9 = (f32[33792]{0:T(1024)S(1)}, f32[33792]{0:T(1024)S(1)}, u32[]{:S(2)}, u32[]{:S(2)}) collective-permute-start(f32[33792]{0:T(1024)S(1)} %dynamic_slice.31), channel_id=1, source_target_pairs={{0,8},{1,9},{2,10},{3,11},{4,12},{5,13},{6,14},{7,15},{8,0},{9,1},... | collective-permute-start | bytes 405512 | tf_op jit(solution)/shard_map/ppermute | solution.py:221
  106.6 6.1 %collective-permute-done.9 = f32[33792]{0:T(1024)S(1)} collective-permute-done((f32[33792]{0:T(1024)S(1)}, f32[33792]{0:T(1024)S(1)}, u32[]{:S(2)}, u32[]{:S(2)}) %collective-permute-start.9) | collective-permute-done | bytes 135200 | tf_op jit(solution)/shard_map/ppermute | solution.py:221
  112.9 3.0 %collective-permute-start.14 = (f32[12800]{0:T(1024)S(1)}, f32[12800]{0:T(1024)}, u32[]{:S(2)}, u32[]{:S(2)}) collective-permute-start(f32[12800]{0:T(1024)S(1)} %add.810), channel_id=1, source_target_pairs={{0,8},{1,9},{2,10},{3,11},{4,12},{5,13},{6,14},{7,15},{8,0},{9,1},... | collective-permute-start | bytes 153608 | tf_op jit(solution)/shard_map/ppermute | solution.py:16
  115.8 4.7 %collective-permute-done.14 = f32[12800]{0:T(1024)} collective-permute-done((f32[12800]{0:T(1024)S(1)}, f32[12800]{0:T(1024)}, u32[]{:S(2)}, u32[]{:S(2)}) %collective-permute-start.14) | collective-permute-done | bytes 51232 | tf_op jit(solution)/shard_map/ppermute | solution.py:16
  120.5 0.8 add.811
  121.3 0.9 broadcast_select_fusion.3
  122.2 1.6 %collective-permute-start.16 = (bf16[67584]{0:T(1024)(128)(2,1)S(1)}, bf16[67584]{0:T(1024)(128)(2,1)S(1)}, u32[]{:S(2)}, u32[]{:S(2)}) collective-permute-start(bf16[67584]{0:T(1024)(128)(2,1)S(1)} %pad_maximum_fusion.13), channel_id=1, source_target_pairs={{0,4},{1,5},{2,6},{3,7},{4,0},{5,1},{6,2},{7,3},{8,12},{9,13},{10,... | collective-permute-start | bytes 405512 | tf_op jit(solution)/shard_map/ppermute | solution.py:236
  123.9 0.9 collective-permute-start.17
  124.8 1.0 collective-permute-start.18
  125.8 0.6 slice_multiply_fusion.1
  126.4 0.7 slice.1635
  127.1 0.9 collective-permute-start.10
  127.9 0.7 collective-permute-done.16
  128.6 2.6 %collective-permute-done.17 = bf16[67584]{0:T(1024)(128)(2,1)S(1)} collective-permute-done((bf16[67584]{0:T(1024)(128)(2,1)S(1)}, bf16[67584]{0:T(1024)(128)(2,1)S(1)}, u32[]{:S(2)}, u32[]{:S(2)}) %collective-permute-start.17) | collective-permute-done | bytes 135200 | tf_op jit(solution)/shard_map/ppermute | solution.py:236
  131.5 0.6 copy-done.12
  132.1 0.8 pad_maximum_fusion.5
  133.5 1.4 %mul.1862 = f32[7,7,256]{2,1,0:T(8,128)} reshape(f32[12544]{0:T(1024)} %slice_multiply_fusion.1) | data formatting | bytes 100352 | tf_op jit(solution)/shard_map/mul | solution.py:352
  135.0 1.5 %rev.7 = f32[4,8,3,256]{3,2,1,0:T(4,128)} reverse(bf16[4,8,3,256]{3,2,1,0:T(4,128)(2,1)} %collective-permute-done.10), dimensions={1,2} | reverse | bytes 147456 | tf_op jit(solution)/shard_map/rev | solution.py:183
  136.5 1.0 fusion.248
  137.5 0.9 pad_maximum_fusion.9
  138.4 1.2 broadcast_select_fusion.1
  140.0 0.6 convert_multiply_fusion.99
  141.4 1.1 mul.1868
  142.6 1.1 convert_multiply_fusion.98
  (337 shorter events, 13.8 us)
Async XLA Ops:
  0.6 34.6 %copy-start = (bf16[1024,256]{1,0:T(8,128)(2,1)S(1)}, bf16[1024,256]{1,0:T(8,128)(2,1)}, u32[]{:S(2)}) copy-start(bf16[1024,256]{1,0:T(8,128)(2,1)} %param.23) | copy-start | bytes 1572868
  0.7 22.2 %copy-start.4 = (bf16[4,8,32,256]{3,2,1,0:T(8,128)(2,1)S(1)}, bf16[4,8,32,256]{3,2,1,0:T(8,128)(2,1)}, u32[]{:S(2)}) copy-start(bf16[4,8,32,256]{3,2,1,0:T(8,128)(2,1)} %param.13) | copy-start | bytes 1572868
  0.7 18.3 %copy-start.20 = (s32[8,32]{1,0:T(8,128)S(1)}, s32[8,32]{1,0:T(8,128)}, u32[]{:S(2)}) copy-start(s32[8,32]{1,0:T(8,128)} %param.16) | copy-start | bytes 3076
  1.7 11.2 %collective-permute-start = (bf16[4,8,3,256]{3,2,1,0:T(4,128)(2,1)S(1)}, bf16[4,8,3,256]{3,2,1,0:T(4,128)(2,1)S(1)}, u32[]{:S(2)}, u32[]{:S(2)}) collective-permute-start(bf16[4,8,3,256]{3,2,1,0:T(4,128)(2,1)S(1)} %slice.714), channel_id=1, source_target_pairs={{0,15},{1,14},{2,13},{3,12},{4,11},{5,10},{6,9},{7,8},{8,7},{9,6},... | collective-permute-start | bytes 147464 | tf_op jit(solution)/shard_map/ppermute | solution.py:174
  8.8 14.5 %copy-start.23 = (f32[1,1,256]{2,1,0:T(1,128)}, f32[1,1,256]{2,1,0:T(1,128)S(1)}, u32[]{:S(2)}) copy-start(f32[1,1,256]{2,1,0:T(1,128)S(1)} %get-tuple-element.143) | copy-start | bytes 3076
  8.8 14.5 %copy-start.25 = (f32[1,1,256]{2,1,0:T(1,128)}, f32[1,1,256]{2,1,0:T(1,128)S(1)}, u32[]{:S(2)}) copy-start(f32[1,1,256]{2,1,0:T(1,128)S(1)} %get-tuple-element.144) | copy-start | bytes 3076
  8.8 14.5 %copy-start.27 = (f32[1,1,256]{2,1,0:T(1,128)}, f32[1,1,256]{2,1,0:T(1,128)S(1)}, u32[]{:S(2)}) copy-start(f32[1,1,256]{2,1,0:T(1,128)S(1)} %get-tuple-element.145) | copy-start | bytes 3076
  8.8 14.5 %copy-start.29 = (f32[1,1,256]{2,1,0:T(1,128)}, f32[1,1,256]{2,1,0:T(1,128)S(1)}, u32[]{:S(2)}) copy-start(f32[1,1,256]{2,1,0:T(1,128)S(1)} %get-tuple-element.146) | copy-start | bytes 3076
  8.8 14.5 %copy-start.31 = (f32[1,1,256]{2,1,0:T(1,128)}, f32[1,1,256]{2,1,0:T(1,128)S(1)}, u32[]{:S(2)}) copy-start(f32[1,1,256]{2,1,0:T(1,128)S(1)} %get-tuple-element.147) | copy-start | bytes 3076
  8.8 14.5 %copy-start.33 = (f32[1,1,256]{2,1,0:T(1,128)}, f32[1,1,256]{2,1,0:T(1,128)S(1)}, u32[]{:S(2)}) copy-start(f32[1,1,256]{2,1,0:T(1,128)S(1)} %get-tuple-element.148) | copy-start | bytes 3076
  8.8 14.5 %copy-start.35 = (f32[1,1,256]{2,1,0:T(1,128)}, f32[1,1,256]{2,1,0:T(1,128)S(1)}, u32[]{:S(2)}) copy-start(f32[1,1,256]{2,1,0:T(1,128)S(1)} %get-tuple-element.149) | copy-start | bytes 3076
  8.9 14.5 %copy-start.37 = (f32[1,1,256]{2,1,0:T(1,128)}, f32[1,1,256]{2,1,0:T(1,128)S(1)}, u32[]{:S(2)}) copy-start(f32[1,1,256]{2,1,0:T(1,128)S(1)} %get-tuple-element.150) | copy-start | bytes 3076
  14.4 8.5 %collective-permute-start.1 = (bf16[4,3,38,256]{3,2,1,0:T(8,128)(2,1)S(1)}, bf16[4,3,38,256]{3,2,1,0:T(8,128)(2,1)S(1)}, u32[]{:S(2)}, u32[]{:S(2)}) collective-permute-start(bf16[4,3,38,256]{3,2,1,0:T(8,128)(2,1)S(1)} %get-tuple-element.129), channel_id=1, source_target_pairs={{0,1},{1,2},{2,3},{3,4},{4,5},{5,6},{6,7},{7,8},{8,9},{9,10},{10,1... | collective-permute-start | bytes 700424 | tf_op jit(solution)/shard_map/ppermute | solution.py:26
  15.2 7.8 %collective-permute-start.2 = (bf16[4,3,38,256]{3,2,1,0:T(8,128)(2,1)S(1)}, bf16[4,3,38,256]{3,2,1,0:T(8,128)(2,1)S(1)}, u32[]{:S(2)}, u32[]{:S(2)}) collective-permute-start(bf16[4,3,38,256]{3,2,1,0:T(8,128)(2,1)S(1)} %get-tuple-element.130), channel_id=1, source_target_pairs={{1,0},{2,1},{3,2},{4,3},{5,4},{6,5},{7,6},{8,7},{9,8},{10,9},{11,1... | collective-permute-start | bytes 700424 | tf_op jit(solution)/shard_map/ppermute | solution.py:27
  18.9 4.4 %copy-start.105 = (s32[256]{0:T(256)}, s32[256]{0:T(256)S(1)}, u32[]{:S(2)}) copy-start(s32[256]{0:T(256)S(1)} %and_select_fusion) | copy-start | bytes 3076
  19.1 4.3 %copy-start.5 = (bf16[4,8,32,256]{3,2,1,0:T(8,128)(2,1)S(1)}, bf16[4,8,32,256]{3,2,1,0:T(8,128)(2,1)}, u32[]{:S(2)}) copy-start(bf16[4,8,32,256]{3,2,1,0:T(8,128)(2,1)} %param.13) | copy-start | bytes 1572868
  19.1 4.3 %copy-start.39 = (f32[1,1,256]{2,1,0:T(1,128)S(1)}, f32[1,1,256]{2,1,0:T(1,128)}, u32[]{:S(2)}) copy-start(f32[1,1,256]{2,1,0:T(1,128)} %get-tuple-element.151) | copy-start | bytes 3076
  19.1 4.3 %copy-start.41 = (f32[1,1,256]{2,1,0:T(1,128)S(1)}, f32[1,1,256]{2,1,0:T(1,128)}, u32[]{:S(2)}) copy-start(f32[1,1,256]{2,1,0:T(1,128)} %get-tuple-element.152) | copy-start | bytes 3076
  19.1 4.3 %copy-start.43 = (f32[1,1,256]{2,1,0:T(1,128)S(1)}, f32[1,1,256]{2,1,0:T(1,128)}, u32[]{:S(2)}) copy-start(f32[1,1,256]{2,1,0:T(1,128)} %get-tuple-element.153) | copy-start | bytes 3076
  19.1 4.3 %copy-start.45 = (f32[1,1,256]{2,1,0:T(1,128)S(1)}, f32[1,1,256]{2,1,0:T(1,128)}, u32[]{:S(2)}) copy-start(f32[1,1,256]{2,1,0:T(1,128)} %get-tuple-element.154) | copy-start | bytes 3076
  19.1 4.3 %copy-start.47 = (f32[1,1,256]{2,1,0:T(1,128)S(1)}, f32[1,1,256]{2,1,0:T(1,128)}, u32[]{:S(2)}) copy-start(f32[1,1,256]{2,1,0:T(1,128)} %get-tuple-element.155) | copy-start | bytes 3076
  19.1 4.3 %copy-start.49 = (f32[1,1,256]{2,1,0:T(1,128)S(1)}, f32[1,1,256]{2,1,0:T(1,128)}, u32[]{:S(2)}) copy-start(f32[1,1,256]{2,1,0:T(1,128)} %get-tuple-element.156) | copy-start | bytes 3076
  19.1 4.3 %copy-start.51 = (f32[1,1,256]{2,1,0:T(1,128)S(1)}, f32[1,1,256]{2,1,0:T(1,128)}, u32[]{:S(2)}) copy-start(f32[1,1,256]{2,1,0:T(1,128)} %get-tuple-element.157) | copy-start | bytes 3076
  19.2 4.3 %copy-start.53 = (f32[1,1,256]{2,1,0:T(1,128)S(1)}, f32[1,1,256]{2,1,0:T(1,128)}, u32[]{:S(2)}) copy-start(f32[1,1,256]{2,1,0:T(1,128)} %get-tuple-element.158) | copy-start | bytes 3076
  19.2 4.3 %copy-start.55 = (f32[1,1,256]{2,1,0:T(1,128)S(1)}, f32[1,1,256]{2,1,0:T(1,128)}, u32[]{:S(2)}) copy-start(f32[1,1,256]{2,1,0:T(1,128)} %get-tuple-element.159) | copy-start | bytes 3076
  19.2 4.3 %copy-start.57 = (f32[1,1,256]{2,1,0:T(1,128)S(1)}, f32[1,1,256]{2,1,0:T(1,128)}, u32[]{:S(2)}) copy-start(f32[1,1,256]{2,1,0:T(1,128)} %get-tuple-element.160) | copy-start | bytes 3076
  19.2 4.3 %copy-start.59 = (f32[1,1,256]{2,1,0:T(1,128)S(1)}, f32[1,1,256]{2,1,0:T(1,128)}, u32[]{:S(2)}) copy-start(f32[1,1,256]{2,1,0:T(1,128)} %get-tuple-element.161) | copy-start | bytes 3076
  19.2 4.3 %copy-start.61 = (f32[1,1,256]{2,1,0:T(1,128)S(1)}, f32[1,1,256]{2,1,0:T(1,128)}, u32[]{:S(2)}) copy-start(f32[1,1,256]{2,1,0:T(1,128)} %get-tuple-element.162) | copy-start | bytes 3076
  19.2 4.3 %copy-start.63 = (f32[1,1,256]{2,1,0:T(1,128)S(1)}, f32[1,1,256]{2,1,0:T(1,128)}, u32[]{:S(2)}) copy-start(f32[1,1,256]{2,1,0:T(1,128)} %get-tuple-element.163) | copy-start | bytes 3076
  19.2 4.3 %copy-start.65 = (f32[1,1,256]{2,1,0:T(1,128)S(1)}, f32[1,1,256]{2,1,0:T(1,128)}, u32[]{:S(2)}) copy-start(f32[1,1,256]{2,1,0:T(1,128)} %get-tuple-element.164) | copy-start | bytes 3076
  19.2 4.3 %copy-start.67 = (f32[1,1,256]{2,1,0:T(1,128)S(1)}, f32[1,1,256]{2,1,0:T(1,128)}, u32[]{:S(2)}) copy-start(f32[1,1,256]{2,1,0:T(1,128)} %get-tuple-element.165) | copy-start | bytes 3076
  19.2 4.3 %copy-start.69 = (f32[1,1,256]{2,1,0:T(1,128)S(1)}, f32[1,1,256]{2,1,0:T(1,128)}, u32[]{:S(2)}) copy-start(f32[1,1,256]{2,1,0:T(1,128)} %get-tuple-element.166) | copy-start | bytes 3076
  19.2 4.3 %copy-start.71 = (f32[1,1,256]{2,1,0:T(1,128)S(1)}, f32[1,1,256]{2,1,0:T(1,128)}, u32[]{:S(2)}) copy-start(f32[1,1,256]{2,1,0:T(1,128)} %get-tuple-element.167) | copy-start | bytes 3076
  19.3 4.3 %copy-start.73 = (f32[1,1,256]{2,1,0:T(1,128)S(1)}, f32[1,1,256]{2,1,0:T(1,128)}, u32[]{:S(2)}) copy-start(f32[1,1,256]{2,1,0:T(1,128)} %get-tuple-element.168) | copy-start | bytes 3076
  19.3 4.3 %copy-start.75 = (f32[1,1,256]{2,1,0:T(1,128)S(1)}, f32[1,1,256]{2,1,0:T(1,128)}, u32[]{:S(2)}) copy-start(f32[1,1,256]{2,1,0:T(1,128)} %get-tuple-element.169) | copy-start | bytes 3076
  19.3 4.3 %copy-start.77 = (f32[1,1,256]{2,1,0:T(1,128)S(1)}, f32[1,1,256]{2,1,0:T(1,128)}, u32[]{:S(2)}) copy-start(f32[1,1,256]{2,1,0:T(1,128)} %get-tuple-element.170) | copy-start | bytes 3076
  19.3 4.3 %copy-start.79 = (f32[1,1,256]{2,1,0:T(1,128)S(1)}, f32[1,1,256]{2,1,0:T(1,128)}, u32[]{:S(2)}) copy-start(f32[1,1,256]{2,1,0:T(1,128)} %get-tuple-element.171) | copy-start | bytes 3076
  19.3 4.3 %copy-start.81 = (f32[1,1,256]{2,1,0:T(1,128)S(1)}, f32[1,1,256]{2,1,0:T(1,128)}, u32[]{:S(2)}) copy-start(f32[1,1,256]{2,1,0:T(1,128)} %get-tuple-element.172) | copy-start | bytes 3076
  19.3 4.3 %copy-start.83 = (f32[1,1,256]{2,1,0:T(1,128)S(1)}, f32[1,1,256]{2,1,0:T(1,128)}, u32[]{:S(2)}) copy-start(f32[1,1,256]{2,1,0:T(1,128)} %get-tuple-element.173) | copy-start | bytes 3076
  19.3 4.3 %copy-start.85 = (f32[1,1,256]{2,1,0:T(1,128)S(1)}, f32[1,1,256]{2,1,0:T(1,128)}, u32[]{:S(2)}) copy-start(f32[1,1,256]{2,1,0:T(1,128)} %get-tuple-element.174) | copy-start | bytes 3076
  19.3 4.3 %copy-start.87 = (f32[1,1,256]{2,1,0:T(1,128)S(1)}, f32[1,1,256]{2,1,0:T(1,128)}, u32[]{:S(2)}) copy-start(f32[1,1,256]{2,1,0:T(1,128)} %get-tuple-element.175) | copy-start | bytes 3076
  19.3 4.3 %copy-start.89 = (f32[1,1,256]{2,1,0:T(1,128)S(1)}, f32[1,1,256]{2,1,0:T(1,128)}, u32[]{:S(2)}) copy-start(f32[1,1,256]{2,1,0:T(1,128)} %get-tuple-element.176) | copy-start | bytes 3076
  19.3 4.3 %copy-start.91 = (f32[1,1,256]{2,1,0:T(1,128)S(1)}, f32[1,1,256]{2,1,0:T(1,128)}, u32[]{:S(2)}) copy-start(f32[1,1,256]{2,1,0:T(1,128)} %get-tuple-element.177) | copy-start | bytes 3076
  23.8 9.7 %copy-start.22 = (f32[256]{0:T(256)S(1)}, f32[256]{0:T(256)}, u32[]{:S(2)}) copy-start(f32[256]{0:T(256)} %param.19) | copy-start | bytes 3076
  56.8 3.3 %collective-permute-start.3 = (f32[270336]{0:T(1024)}, f32[270336]{0:T(1024)}, u32[]{:S(2)}, u32[]{:S(2)}) collective-permute-start(f32[270336]{0:T(1024)} %pad_dynamic-slice_fusion), channel_id=1, source_target_pairs={{0,1},{1,0},{2,3},{3,2},{4,5},{5,4},{6,7},{7,6},{8,9},{9,8},{10,11... | collective-permute-start | bytes 3244040 | tf_op jit(solution)/shard_map/ppermute | solution.py:221
  57.4 5.4 %copy-start.7 = (f32[4,8,32,256]{3,2,1,0:T(8,128)S(1)}, f32[4,8,32,256]{3,2,1,0:T(8,128)}, u32[]{:S(2)}) copy-start(f32[4,8,32,256]{3,2,1,0:T(8,128)} %get-tuple-element.21) | copy-start | bytes 3145732
  67.2 4.3 %copy-start.1 = (f32[4,8,32,256]{3,2,1,0:T(8,128)}, f32[4,8,32,256]{3,2,1,0:T(8,128)S(1)}, u32[]{:S(2)}) copy-start(f32[4,8,32,256]{3,2,1,0:T(8,128)S(1)} %get-tuple-element.94) | copy-start | bytes 3145732
  72.2 15.2 %copy-start.2 = (f32[4,8,32,256]{3,2,1,0:T(8,128)S(1)}, f32[4,8,32,256]{3,2,1,0:T(8,128)}, u32[]{:S(2)}) copy-start(f32[4,8,32,256]{3,2,1,0:T(8,128)} %copy-done.1) | copy-start | bytes 3145732
  72.7 6.1 %collective-permute-start.11 = (f32[12800]{0:T(1024)S(1)}, f32[12800]{0:T(1024)S(1)}, u32[]{:S(2)}, u32[]{:S(2)}) collective-permute-start(f32[12800]{0:T(1024)S(1)} %pad_maximum_fusion.14), channel_id=1, source_target_pairs={{0,1},{1,0},{2,3},{3,2},{4,5},{5,4},{6,7},{7,6},{8,9},{9,8},{10,11... | collective-permute-start | bytes 153608 | tf_op jit(solution)/shard_map/ppermute | solution.py:16
  74.3 13.1 %collective-permute-start.4 = (f32[4,3,32,256]{3,2,1,0:T(8,128)S(1)}, f32[4,3,32,256]{3,2,1,0:T(8,128)S(1)}, u32[]{:S(2)}, u32[]{:S(2)}) collective-permute-start(f32[4,3,32,256]{3,2,1,0:T(8,128)S(1)} %get-tuple-element.123), channel_id=1, source_target_pairs={{0,1},{1,2},{2,3},{3,4},{4,5},{5,6},{6,7},{7,8},{8,9},{9,10},{10,1... | collective-permute-start | bytes 1179656 | tf_op jit(solution)/shard_map/ppermute | solution.py:26
  74.5 12.9 %collective-permute-start.5 = (f32[4,3,32,256]{3,2,1,0:T(8,128)S(1)}, f32[4,3,32,256]{3,2,1,0:T(8,128)S(1)}, u32[]{:S(2)}, u32[]{:S(2)}) collective-permute-start(f32[4,3,32,256]{3,2,1,0:T(8,128)S(1)} %get-tuple-element.124), channel_id=1, source_target_pairs={{1,0},{2,1},{3,2},{4,3},{5,4},{6,5},{7,6},{8,7},{9,8},{10,9},{11,1... | collective-permute-start | bytes 1179656 | tf_op jit(solution)/shard_map/ppermute | solution.py:27
  78.8 8.4 %collective-permute-start.12 = (f32[12800]{0:T(1024)S(1)}, f32[12800]{0:T(1024)S(1)}, u32[]{:S(2)}, u32[]{:S(2)}) collective-permute-start(f32[12800]{0:T(1024)S(1)} %fusion.312), channel_id=1, source_target_pairs={{0,2},{1,3},{2,0},{3,1},{4,6},{5,7},{6,4},{7,5},{8,10},{9,11},{10,... | collective-permute-start | bytes 153608 | tf_op jit(solution)/shard_map/ppermute | solution.py:16
  87.2 25.6 %collective-permute-start.13 = (f32[12800]{0:T(1024)S(1)}, f32[12800]{0:T(1024)S(1)}, u32[]{:S(2)}, u32[]{:S(2)}) collective-permute-start(f32[12800]{0:T(1024)S(1)} %add.809), channel_id=1, source_target_pairs={{0,4},{1,5},{2,6},{3,7},{4,0},{5,1},{6,2},{7,3},{8,12},{9,13},{10,... | collective-permute-start | bytes 153608 | tf_op jit(solution)/shard_map/ppermute | solution.py:16
  88.9 14.1 %collective-permute-start.6 = (f32[67584]{0:T(1024)S(1)}, f32[67584]{0:T(1024)S(1)}, u32[]{:S(2)}, u32[]{:S(2)}) collective-permute-start(f32[67584]{0:T(1024)S(1)} %get-tuple-element.118), channel_id=1, source_target_pairs={{0,2},{1,3},{2,0},{3,1},{4,6},{5,7},{6,4},{7,5},{8,10},{9,11},{10,... | collective-permute-start | bytes 811016 | tf_op jit(solution)/shard_map/ppermute | solution.py:221
  89.0 14.1 %collective-permute-start.7 = (f32[67584]{0:T(1024)S(1)}, f32[67584]{0:T(1024)S(1)}, u32[]{:S(2)}, u32[]{:S(2)}) collective-permute-start(f32[67584]{0:T(1024)S(1)} %get-tuple-element.120), channel_id=1, source_target_pairs={{0,4},{1,5},{2,6},{3,7},{4,0},{5,1},{6,2},{7,3},{8,12},{9,13},{10,... | collective-permute-start | bytes 811016 | tf_op jit(solution)/shard_map/ppermute | solution.py:221
  90.2 12.9 %collective-permute-start.8 = (f32[67584]{0:T(1024)S(1)}, f32[67584]{0:T(1024)S(1)}, u32[]{:S(2)}, u32[]{:S(2)}) collective-permute-start(f32[67584]{0:T(1024)S(1)} %get-tuple-element.119), channel_id=1, source_target_pairs={{0,6},{1,7},{2,4},{3,5},{4,2},{5,3},{6,0},{7,1},{8,14},{9,15},{10,... | collective-permute-start | bytes 811016 | tf_op jit(solution)/shard_map/ppermute | solution.py:221
  103.2 9.6 %collective-permute-start.9 = (f32[33792]{0:T(1024)S(1)}, f32[33792]{0:T(1024)S(1)}, u32[]{:S(2)}, u32[]{:S(2)}) collective-permute-start(f32[33792]{0:T(1024)S(1)} %dynamic_slice.31), channel_id=1, source_target_pairs={{0,8},{1,9},{2,10},{3,11},{4,12},{5,13},{6,14},{7,15},{8,0},{9,1},... | collective-permute-start | bytes 405512 | tf_op jit(solution)/shard_map/ppermute | solution.py:221
  112.8 8.6 %collective-permute-start.15 = (bf16[33792]{0:T(1024)(128)(2,1)S(1)}, bf16[33792]{0:T(1024)(128)(2,1)}, u32[]{:S(2)}, u32[]{:S(2)}) collective-permute-start(bf16[33792]{0:T(1024)(128)(2,1)S(1)} %dynamic-slice_add_fusion), channel_id=1, source_target_pairs={{0,8},{1,9},{2,10},{3,11},{4,12},{5,13},{6,14},{7,15},{8,0},{9,1},... | collective-permute-start | bytes 202760 | tf_op jit(solution)/shard_map/ppermute | solution.py:236
  112.9 7.6 %collective-permute-start.14 = (f32[12800]{0:T(1024)S(1)}, f32[12800]{0:T(1024)}, u32[]{:S(2)}, u32[]{:S(2)}) collective-permute-start(f32[12800]{0:T(1024)S(1)} %add.810), channel_id=1, source_target_pairs={{0,8},{1,9},{2,10},{3,11},{4,12},{5,13},{6,14},{7,15},{8,0},{9,1},... | collective-permute-start | bytes 153608 | tf_op jit(solution)/shard_map/ppermute | solution.py:16
  122.2 6.4 %collective-permute-start.16 = (bf16[67584]{0:T(1024)(128)(2,1)S(1)}, bf16[67584]{0:T(1024)(128)(2,1)S(1)}, u32[]{:S(2)}, u32[]{:S(2)}) collective-permute-start(bf16[67584]{0:T(1024)(128)(2,1)S(1)} %pad_maximum_fusion.13), channel_id=1, source_target_pairs={{0,4},{1,5},{2,6},{3,7},{4,0},{5,1},{6,2},{7,3},{8,12},{9,13},{10,... | collective-permute-start | bytes 405512 | tf_op jit(solution)/shard_map/ppermute | solution.py:236
  123.9 7.4 %collective-permute-start.17 = (bf16[67584]{0:T(1024)(128)(2,1)S(1)}, bf16[67584]{0:T(1024)(128)(2,1)S(1)}, u32[]{:S(2)}, u32[]{:S(2)}) collective-permute-start(bf16[67584]{0:T(1024)(128)(2,1)S(1)} %pad_maximum_fusion.13), channel_id=1, source_target_pairs={{0,2},{1,3},{2,0},{3,1},{4,6},{5,7},{6,4},{7,5},{8,10},{9,11},{10,... | collective-permute-start | bytes 405512 | tf_op jit(solution)/shard_map/ppermute | solution.py:236
  124.8 6.5 %collective-permute-start.18 = (bf16[67584]{0:T(1024)(128)(2,1)S(1)}, bf16[67584]{0:T(1024)(128)(2,1)S(1)}, u32[]{:S(2)}, u32[]{:S(2)}) collective-permute-start(bf16[67584]{0:T(1024)(128)(2,1)S(1)} %pad_maximum_fusion.13), channel_id=1, source_target_pairs={{0,6},{1,7},{2,4},{3,5},{4,2},{5,3},{6,0},{7,1},{8,14},{9,15},{10,... | collective-permute-start | bytes 405512 | tf_op jit(solution)/shard_map/ppermute | solution.py:236
  127.1 7.9 %collective-permute-start.10 = (bf16[4,8,3,256]{3,2,1,0:T(4,128)(2,1)}, bf16[4,8,3,256]{3,2,1,0:T(4,128)(2,1)}, u32[]{:S(2)}, u32[]{:S(2)}) collective-permute-start(bf16[4,8,3,256]{3,2,1,0:T(4,128)(2,1)} %slice.1635), channel_id=1, source_target_pairs={{0,15},{1,14},{2,13},{3,12},{4,11},{5,10},{6,9},{7,8},{8,7},{9,6},... | collective-permute-start | bytes 147464 | tf_op jit(solution)/shard_map/ppermute | solution.py:174
  132.9 5.4 %collective-permute-start.19 = (bf16[270336]{0:T(1024)(128)(2,1)}, bf16[270336]{0:T(1024)(128)(2,1)}, u32[]{:S(2)}, u32[]{:S(2)}) collective-permute-start(bf16[270336]{0:T(1024)(128)(2,1)} %pad_maximum_fusion.5), channel_id=1, source_target_pairs={{0,1},{1,0},{2,3},{3,2},{4,5},{5,4},{6,7},{7,6},{8,9},{9,8},{10,11... | collective-permute-start | bytes 1622024 | tf_op jit(solution)/shard_map/ppermute | solution.py:236
  (81 other events, 227.7 us)

commit v16 on v15

--- a/solution.py
+++ b/solution.py
@@ -86,13 +86,16 @@
     pred = wet_mask * (features.astype(jnp.float32) + layer_scale * branch)
     target_full = target.astype(jnp.float32)
     pair_weight = 1.0 / (members * (members - 1))
-    skill = jnp.zeros(target.shape, jnp.float32)
-    spread = jnp.zeros(target.shape, jnp.float32)
-    for member in range(members):
-        skill = skill + smooth_abs(pred[member] - target_full)
-        for other in range(member + 1, members):
-            spread = spread + smooth_abs(pred[member] - pred[other])
-    crps_field = wet_mask * (skill / members - pair_weight * spread)
+
+    def crps_of(pred):
+        skill = jnp.zeros(target.shape, jnp.float32)
+        spread = jnp.zeros(target.shape, jnp.float32)
+        for member in range(members):
+            skill = skill + smooth_abs(pred[member] - target_full)
+            for other in range(member + 1, members):
+                spread = spread + smooth_abs(pred[member] - pred[other])
+        return wet_mask * (skill / members - pair_weight * spread)
+
     grad_list = []
     for member in range(members):
         slope_sum = jnp.zeros(target.shape, jnp.float32)
@@ -166,7 +169,8 @@
         return grad_depth, grad_kernel, grad_dw_bias
 
     sums = (grad_ln_gain, grad_ln_bias, grad_w_in, grad_b_in, grad_w_out, grad_b_out, grad_scale)
-    return (pred.astype(jnp.bfloat16), crps_field, grad_pred, grad_normed, sums, depth_backward)
+    deferred = (pred, crps_of)
+    return (pred.astype(jnp.bfloat16), deferred, grad_pred, grad_normed, sums, depth_backward)
 
 
 def mirrored(x, axis):
@@ -286,7 +290,7 @@
     north_rows = mirror_rows(features[:, :, lat_rows - 3 :, :])
     joined = jnp.concatenate([south_rim, features, north_rows], axis=2)
     extended = with_halo(joined, (("lon", 1),), 3)
-    predicted, crps_field, grad_pred, grad_normed, sums, depth_backward = local_step(
+    predicted, deferred, grad_pred, grad_normed, sums, depth_backward = local_step(
         extended, features, target, kmt, *params
     )
 
@@ -312,18 +316,21 @@
                 )
         return grad_ext
 
+    pred_full, crps_fn = deferred
+
+    def crps_of(grad_ext):
+        _, held = lax.optimization_barrier((grad_ext, pred_full))
+        return crps_fn(held)
+
     lon_size = lax.axis_size("lon")
-    def grad_features_main(grad_ext):
-        return (grad_pred[:, :, : lat_rows - 3] + grad_ext[:, :, 3:lat_rows]).astype(jnp.bfloat16)
-
-    reduced, (kernel_sum, dw_bias_sum), grad_ext, main_rows = radix_allreduce(
+    reduced, (kernel_sum, dw_bias_sum), grad_ext, crps_field = radix_allreduce(
         pack(sums, lon_size * 1024),
         "lon",
         jnp.bfloat16,
         grad_normed,
         backward,
         backward_conv,
-        grad_features_main,
+        crps_of,
     )
     gain_sum, bias_sum, w_in_sum, b_in_sum, w_out_sum, b_out_sum, scale_sum = unpack(reduced, sums)
     small = (kernel_sum, dw_bias_sum)
@@ -340,10 +347,10 @@
         scale_sum,
     )
     back_rows = mirror_grads(grad_ext[:, :, lat_rows + 3 :, :])
-    fold_rows = (
-        grad_pred[:, :, lat_rows - 3 :] + grad_ext[:, :, lat_rows : lat_rows + 3]
-    ) + back_rows
-    grad_features = jnp.concatenate([main_rows, fold_rows.astype(jnp.bfloat16)], axis=2)
+    inner = grad_pred + grad_ext[:, :, 3 : lat_rows + 3, :]
+    grad_features = jnp.concatenate(
+        [inner[:, :, : lat_rows - 3, :], inner[:, :, lat_rows - 3 :, :] + back_rows], axis=2
+    ).astype(jnp.bfloat16)
     factor = 1.0 / math.sqrt(members * lat_rows * lon_dev * lax.axis_size("lon"))
     return (
         predicted,

time: 145 us -> 143 us (0.986)
  waiting for transfers between devices: 28.6 us -> 37.3 us
  starting transfers between devices: 29.8 us -> 25.2 us
  local copies, waits for them, and re-layouts: 19.6 us -> 16.7 us
  other arithmetic: 50.8 us -> 47.9 us
    ppermute x5, waiting for transfers between devices: 3.34 us -> 8.12 us  [radix_allreduce(): lax.ppermute(cur, axis, [(i, i ^ d << low) for i in range(size)])]
    ppermute x4, waiting for transfers between devices: 13 us -> 17.2 us  [swapped(): lax.ppermute(x, axis, [(i, i ^ 1 << bit) for i in range(lax.axis_size(axi...]
    ppermute x5, starting transfers between devices: 7.36 us -> 4.82 us  [radix_allreduce(): lax.ppermute(send, axis, [(i, i ^ d << low) for i in range(size)])]
    ppermute x4, starting transfers between devices: 3.52 us -> 1.01 us  [swapped(): lax.ppermute(x, axis, [(i, i ^ 1 << bit) for i in range(lax.axis_size(axi...]
    mul x0 -> x1, other arithmetic: none -> 1.78 us  [crps_of(): return wet_mask * (skill / members - pair_weight * spread)]
    ppermute x5, waiting for transfers between devices: 8.79 us -> 7.13 us  [radix_allreduce(): lax.ppermute(send, axis, [(i, i ^ d << low) for i in range(size)])]
    reduce_sum x1, other arithmetic: 2.5 us -> 0.99 us  [local_step(): grad_b_out = grad_b_out + jnp.sum(grad_out, axis=0)]
    unnamed x262 -> x268, local copies, waits for them, and re-layouts: 5.79 us -> 5.53 us
  transfers between devices with their start and end apart: 20 -> 20, of which waited for: 7 -> 11; matrix products, arithmetic and copies ran while one was open for 18% -> 16% of each run, Pallas kernels for 0% -> 0%
where the time goes in v16:
time: 143 us; the launch traced here: 142 us
  other arithmetic  47.9 us (33%)
  waiting for transfers between devices  37.3 us (26%)
  starting transfers between devices  25.2 us (18%)
  local copies, waits for them, and re-layouts  16.7 us (12%)
  matrix products  12 us (8%)
  between operations  3.09 us (2%)
    ppermute x4, waiting for transfers between devices, swapped(): lax.ppermute(x, axis, [(i, i ^ 1 << bit) for i in range(lax.axis_size(axi...  17.2 us
    add x1, other arithmetic, backward_conv(): grad_ext + dw_kernel[lon_off, lat_off] * padded[:, 6 - lon_off:6 - lon_of...  10.3 us
    reduce_sum x1, other arithmetic, local_step(): mean_val = jnp.mean(depth, axis=-1, keepdims=True)  9.29 us
    reduce_sum x4, other arithmetic, depth_backward(): jnp.sum(grad_depth * extended[:, lon_off:lon_off + lon_dev, lat_off:lat_o...  8.54 us
    ppermute x5, waiting for transfers between devices, radix_allreduce(): lax.ppermute(cur, axis, [(i, i ^ d << low) for i in range(size)])  8.12 us
    ppermute x2, starting transfers between devices, with_halo(): after = lax.ppermute(leading, axis, down)  8.05 us
    ppermute x5, waiting for transfers between devices, radix_allreduce(): lax.ppermute(send, axis, [(i, i ^ d << low) for i in range(size)])  7.13 us
    ppermute x2, starting transfers between devices, mirrored(): return lax.ppermute(x, axis, [(i, size - 1 - i) for i in range(size)])  6.76 us
  transfers between devices with their start and end apart: 20, of which 11 were waited for; matrix products, arithmetic and copies ran while one was open for 16% of the time, Pallas kernels for 0%

profile of v16, /device:TPU:0, one launch (start us, length us, event | category | flops | bytes accessed | tf_op | source)
XLA Modules:
  0.0 142.1 jit_solution(4654055217389727856)
XLA Ops:
  0.7 1.0 slice.720
  1.7 5.5 %collective-permute-start = (bf16[4,8,3,256]{3,2,1,0:T(4,128)(2,1)S(1)}, bf16[4,8,3,256]{3,2,1,0:T(4,128)(2,1)S(1)}, u32[]{:S(2)}, u32[]{:S(2)}) collective-permute-start(bf16[4,8,3,256]{3,2,1,0:T(4,128)(2,1)S(1)} %slice.720), channel_id=1, source_target_pairs={{0,15},{1,14},{2,13},{3,12},{4,11},{5,10},{6,9},{7,8},{8,7},{9,6},... | collective-permute-start | bytes 147464 | tf_op jit(solution)/shard_map/ppermute | solution.py:178
  7.2 1.6 %fusion.308 = (f32[1,1,256]{2,1,0:T(1,128)S(1)}, f32[1,1,256]{2,1,0:T(1,128)S(1)}, f32[1,1,256]{2,1,0:T(1,128)S(1)}, f32[1,1,256]{2,1,0:T(1,128)S(1)}, f32[1,1,2...) fusion(f32[7,7,256]{2,1,0:T(8,128)} %param.17), kind=kLoop, calls=%fused_computation.588 | loop fusion | bytes 38912 | tf_op jit(solution)/shard_map/slice | solution.py:59
  8.9 1.7 %fusion.309 = (f32[1,1,256]{2,1,0:T(1,128)}, f32[1,1,256]{2,1,0:T(1,128)}, f32[1,1,256]{2,1,0:T(1,128)}, f32[1,1,256]{2,1,0:T(1,128)}, f32[1,1,256]{2,1,0:T(1,12...) fusion(f32[7,7,256]{2,1,0:T(8,128)} %param.17), kind=kLoop, calls=%fused_computation.589 | loop fusion | bytes 38912 | tf_op jit(solution)/shard_map/slice | solution.py:59
  10.5 1.5 %fusion.310 = (f32[1,1,256]{2,1,0:T(1,128)}, f32[1,1,256]{2,1,0:T(1,128)}, f32[1,1,256]{2,1,0:T(1,128)}, f32[1,1,256]{2,1,0:T(1,128)}, f32[1,1,256]{2,1,0:T(1,12...) fusion(f32[7,7,256]{2,1,0:T(8,128)} %param.17), kind=kLoop, calls=%fused_computation.590 | loop fusion | bytes 22528 | tf_op jit(solution)/shard_map/slice | solution.py:59
  12.1 0.8 copy.25
  13.1 1.3 pad_maximum_fusion.12
  14.4 0.7 collective-permute-start.1
  15.1 3.8 %collective-permute-start.2 = (bf16[4,3,38,256]{3,2,1,0:T(8,128)(2,1)S(1)}, bf16[4,3,38,256]{3,2,1,0:T(8,128)(2,1)}, u32[]{:S(2)}, u32[]{:S(2)}) collective-permute-start(bf16[4,3,38,256]{3,2,1,0:T(8,128)(2,1)S(1)} %get-tuple-element.129), channel_id=1, source_target_pairs={{1,0},{2,1},{3,2},{4,3},{5,4},{6,5},{7,6},{8,7},{9,8},{10,9},{11,1... | collective-permute-start | bytes 700424 | tf_op jit(solution)/shard_map/ppermute | solution.py:27
  19.4 3.5 %collective-permute-done.1 = bf16[4,3,38,256]{3,2,1,0:T(8,128)(2,1)S(1)} collective-permute-done((bf16[4,3,38,256]{3,2,1,0:T(8,128)(2,1)S(1)}, bf16[4,3,38,256]{3,2,1,0:T(8,128)(2,1)S(1)}, u32[]{:S(2)}, u32[]{:S(2)}) %collective-permute-start.1) | collective-permute-done | bytes 233504 | tf_op jit(solution)/shard_map/ppermute | solution.py:26
  22.9 1.3 maximum_maximum_fusion
  24.7 9.3 %fusion.303 = (f32[4,8,32]{2,1,0:T(8,128)S(1)}, f32[4,8,32,256]{3,2,1,0:T(8,128)S(1)}) fusion(bf16[4,11,38,256]{3,2,1,0:T(8,128)(2,1)S(1)} %get-tuple-element.127, f32[256]{0:T(256)} %bitcast.452, f32[256]{0:T(256)} %bitcast.454, f32[256]{0:T(256)S(1)} %bitcast.360, f32[256]{0:T(256)S(1)} %bitcast.362, f32[256]{0:T(256)S(1)} %bitcast.364, ...), kind=kLoop, calls=%fused_computation.584 | loop fusion | flops 43514880 | bytes 23746560 | tf_op jit(solution)/shard_map/reduce_sum | solution.py:62
  34.4 1.1 add_convert_fusion
  39.0 1.1 fusion.301
  40.1 1.0 multiply_reduce_fusion.7
  41.2 0.6 fusion.292
  41.8 0.9 fusion.295
  43.4 0.9 fusion.293
  44.3 0.6 convolution_add_fusion.2
  44.9 0.9 fusion.297
  45.9 0.6 convolution_add_fusion.1
  46.5 0.9 fusion.299
  47.4 0.6 fusion
  48.0 0.5 copy.28
  49.2 0.6 fusion.312
  51.0 1.3 pad_maximum_fusion.2
  52.3 0.7 copy-done.10
  53.8 1.2 pad_dynamic-slice_fusion
  55.0 0.5 copy-done.11
  55.5 0.6 collective-permute-start.3
  56.1 2.7 %collective-permute-done.3 = f32[270336]{0:T(1024)} collective-permute-done((f32[270336]{0:T(1024)}, f32[270336]{0:T(1024)}, u32[]{:S(2)}, u32[]{:S(2)}) %collective-permute-start.3) | collective-permute-done | bytes 1081376 | tf_op jit(solution)/shard_map/ppermute | solution.py:225
  58.8 2.7 %fusion.99 = f32[270336]{0:T(1024)} fusion(f32[270336]{0:T(1024)} %collective-permute-done.3, s32[]{:T(128)S(6)} %select_n.114, f32[526336]{0:T(1024)} %copy-done.11), kind=kLoop, calls=%fused_computation.272 | loop fusion | flops 270336 | bytes 4268036 | tf_op jit(solution)/shard_map/add | solution.py:225
  61.5 0.6 multiply_reduce_fusion.4
  62.2 3.8 %fusion.196 = (f32[256]{0:T(256)}, f32[256]{0:T(256)}, f32[256]{0:T(256)}, f32[256]{0:T(256)}, f32[256]{0:T(256)}, /*index=5*/f32[256]{0:T(256)}, f32[256]{0:T(2...) fusion(bf16[4,11,38,256]{3,2,1,0:T(8,128)(2,1)S(1)} %get-tuple-, ...), kind=kLoop, calls=%fused_computation.370 | loop fusion | flops 15986176 | bytes 12618752 | tf_op jit(solution)/shard_map/reduce_sum | solution.py:159
  66.0 1.8 %fusion.178 = (f32[256]{0:T(256)S(1)}, f32[256]{0:T(256)S(1)}, f32[256]{0:T(256)S(1)}, f32[256]{0:T(256)S(1)}, f32[256]{0:T(256)S(1)}, /*index=5*/f32[256]{0:T(2...) fusion(f32[4,8,32,256]{3,2,1,0:T(8,128)S(1)} %get-tuple-element.96, ...), kind=kLoop, calls=%fused_computation.352 | loop fusion | flops 12842240 | bytes 3255296 | tf_op jit(solution)/shard_map/reduce_sum | solution.py:159
  67.7 2.6 %fusion.145 = (f32[256]{0:T(256)S(1)}, f32[256]{0:T(256)S(1)}, f32[256]{0:T(256)S(1)}, f32[256]{0:T(256)S(1)}, f32[256]{0:T(256)S(1)}, /*index=5*/f32[256]{0:T(2...) fusion(f32[4,8,32,256]{3,2,1,0:T(8,128)S(1)} %get-tuple-element, ...), kind=kLoop, calls=%fused_computation.319 | loop fusion | flops 14151168 | bytes 10504192 | tf_op jit(solution)/shard_map/reduce_sum | solution.py:159
  71.8 1.2 fusion.306
  73.2 4.3 %collective-permute-start.5 = (f32[4,3,32,256]{3,2,1,0:T(8,128)S(1)}, f32[4,3,32,256]{3,2,1,0:T(8,128)S(1)}, u32[]{:S(2)}, u32[]{:S(2)}) collective-permute-start(f32[4,3,32,256]{3,2,1,0:T(8,128)S(1)} %get-tuple-element.123), channel_id=1, source_target_pairs={{1,0},{2,1},{3,2},{4,3},{5,4},{6,5},{7,6},{8,7},{9,8},{10,9},{11,1... | collective-permute-start | bytes 1179656 | tf_op jit(solution)/shard_map/ppermute | solution.py:27
  77.6 8.4 %collective-permute-done.12 = f32[12800]{0:T(1024)S(1)} collective-permute-done((f32[12800]{0:T(1024)S(1)}, f32[12800]{0:T(1024)S(1)}, u32[]{:S(2)}, u32[]{:S(2)}) %collective-permute-start.12) | collective-permute-done | bytes 51232 | tf_op jit(solution)/shard_map/ppermute | solution.py:16
  86.0 4.1 %collective-permute-done.13 = f32[12800]{0:T(1024)S(1)} collective-permute-done((f32[12800]{0:T(1024)S(1)}, f32[12800]{0:T(1024)S(1)}, u32[]{:S(2)}, u32[]{:S(2)}) %collective-permute-start.13) | collective-permute-done | bytes 51232 | tf_op jit(solution)/shard_map/ppermute | solution.py:16
  90.6 4.7 %collective-permute-done.14 = f32[12800]{0:T(1024)S(1)} collective-permute-done((f32[12800]{0:T(1024)S(1)}, f32[12800]{0:T(1024)S(1)}, u32[]{:S(2)}, u32[]{:S(2)}) %collective-permute-start.14) | collective-permute-done | bytes 51232 | tf_op jit(solution)/shard_map/ppermute | solution.py:16
  95.5 1.0 copy-done.12
  97.1 3.4 %collective-permute-start.8 = (f32[67584]{0:T(1024)S(1)}, f32[67584]{0:T(1024)S(1)}, u32[]{:S(2)}, u32[]{:S(2)}) collective-permute-start(f32[67584]{0:T(1024)S(1)} %get-tuple-element.120), channel_id=1, source_target_pairs={{0,6},{1,7},{2,4},{3,5},{4,2},{5,3},{6,0},{7,1},{8,14},{9,15},{10,... | collective-permute-start | bytes 811016 | tf_op jit(solution)/shard_map/ppermute | solution.py:225
  100.9 10.3 %fusion.95 = f32[4,8,38,256]{3,2,1,0:T(8,128)S(1)} fusion(f32[4,14,32,256]{3,2,1,0:T(8,128)S(1)} %pad_maximum_fusion, f32[256]{0:T(256)} %bitcast.453, f32[256]{0:T(256)} %bitcast.455, f32[256]{0:T(256)S(1)} %bitcast.361, f32[256]{0:T(256)S(1)} %bitcast.363, f32[256]{0:T(256)S(1)} %bitcast.365, f32[256]{0:T(256)S(1)} %bitcast.367, f32[256]{0:T(256)S(1)} %bitcast.369, ...), kind=kLoop, calls=%fused_computation.264 | loop fusion | flops 30195712 | bytes 3130368 | tf_op jit(solution)/shard_map/add | solution.py:308
  111.3 0.6 collective-permute-start.9
  112.4 1.8 %compare_select_fusion = f32[8,32,256]{2,1,0:T(8,128)} fusion(bf16[8,32,256]{2,1,0:T(8,128)(2,1)S(1)} %copy-done.22, f32[4,8,32,256]{3,2,1,0:T(8,128)S(1)} %copy-done.8, s32[8,32]{1,0:T(8,128)S(1)} %copy-done.24, s32[256]{0:T(256)S(1)} %and_select_fusion), kind=kLoop, calls=%fused_computation.434 | loop fusion | flops 3538944 | bytes 1443840 | tf_op jit(solution)/shard_map/mul | solution.py:97
  114.2 4.5 %collective-permute-done.9 = f32[33792]{0:T(1024)S(1)} collective-permute-done((f32[33792]{0:T(1024)S(1)}, f32[33792]{0:T(1024)S(1)}, u32[]{:S(2)}, u32[]{:S(2)}) %collective-permute-start.9) | collective-permute-done | bytes 135200 | tf_op jit(solution)/shard_map/ppermute | solution.py:225
  118.7 0.6 mul.1892
  119.4 4.9 %collective-permute-done.15 = bf16[33792]{0:T(1024)(128)(2,1)S(1)} collective-permute-done((bf16[33792]{0:T(1024)(128)(2,1)S(1)}, bf16[33792]{0:T(1024)(128)(2,1)S(1)}, u32[]{:S(2)}, u32[]{:S(2)}) %collective-permute-start.15) | collective-permute-done | bytes 67616 | tf_op jit(solution)/shard_map/ppermute | solution.py:240
  124.4 2.1 %collective-permute-start.17 = (bf16[67584]{0:T(1024)(128)(2,1)S(1)}, bf16[67584]{0:T(1024)(128)(2,1)S(1)}, u32[]{:S(2)}, u32[]{:S(2)}) collective-permute-start(bf16[67584]{0:T(1024)(128)(2,1)S(1)} %pad_maximum_fusion.13), channel_id=1, source_target_pairs={{0,2},{1,3},{2,0},{3,1},{4,6},{5,7},{6,4},{7,5},{8,10},{9,11},{10,... | collective-permute-start | bytes 405512 | tf_op jit(solution)/shard_map/ppermute | solution.py:240
  126.5 1.4 collective-permute-start.18
  127.9 0.6 slice_multiply_fusion.2
  128.5 1.3 collective-permute-start.10
  129.8 0.6 collective-permute-done.16
  130.4 1.0 collective-permute-done.17
  131.4 1.6 %collective-permute-done.18 = bf16[67584]{0:T(1024)(128)(2,1)S(1)} collective-permute-done((bf16[67584]{0:T(1024)(128)(2,1)S(1)}, bf16[67584]{0:T(1024)(128)(2,1)S(1)}, u32[]{:S(2)}, u32[]{:S(2)}) %collective-permute-start.18) | collective-permute-done | bytes 135200 | tf_op jit(solution)/shard_map/ppermute | solution.py:240
  133.1 0.8 pad_maximum_fusion.5
  134.3 1.4 collective-permute-done.10
  136.0 0.9 pad_maximum_fusion.9
  136.8 1.2 broadcast_select_fusion.1
  138.4 0.6 convert_multiply_fusion.99
  139.2 0.6 convert_multiply_fusion.100
  139.9 1.1 mul.1898
  141.0 1.1 convert_multiply_fusion.98
  (345 shorter events, 12.4 us)
Async XLA Ops:
  0.6 35.6 %copy-start = (bf16[1024,256]{1,0:T(8,128)(2,1)S(1)}, bf16[1024,256]{1,0:T(8,128)(2,1)}, u32[]{:S(2)}) copy-start(bf16[1024,256]{1,0:T(8,128)(2,1)} %param.23) | copy-start | bytes 1572868
  0.7 22.2 %copy-start.4 = (bf16[4,8,32,256]{3,2,1,0:T(8,128)(2,1)S(1)}, bf16[4,8,32,256]{3,2,1,0:T(8,128)(2,1)}, u32[]{:S(2)}) copy-start(bf16[4,8,32,256]{3,2,1,0:T(8,128)(2,1)} %param.13) | copy-start | bytes 1572868
  0.7 18.3 %copy-start.24 = (s32[8,32]{1,0:T(8,128)S(1)}, s32[8,32]{1,0:T(8,128)}, u32[]{:S(2)}) copy-start(s32[8,32]{1,0:T(8,128)} %param.16) | copy-start | bytes 3076
  1.7 11.2 %collective-permute-start = (bf16[4,8,3,256]{3,2,1,0:T(4,128)(2,1)S(1)}, bf16[4,8,3,256]{3,2,1,0:T(4,128)(2,1)S(1)}, u32[]{:S(2)}, u32[]{:S(2)}) collective-permute-start(bf16[4,8,3,256]{3,2,1,0:T(4,128)(2,1)S(1)} %slice.720), channel_id=1, source_target_pairs={{0,15},{1,14},{2,13},{3,12},{4,11},{5,10},{6,9},{7,8},{8,7},{9,6},... | collective-permute-start | bytes 147464 | tf_op jit(solution)/shard_map/ppermute | solution.py:178
  8.8 15.4 %copy-start.27 = (f32[1,1,256]{2,1,0:T(1,128)}, f32[1,1,256]{2,1,0:T(1,128)S(1)}, u32[]{:S(2)}) copy-start(f32[1,1,256]{2,1,0:T(1,128)S(1)} %get-tuple-element.141) | copy-start | bytes 3076
  8.8 15.4 %copy-start.29 = (f32[1,1,256]{2,1,0:T(1,128)}, f32[1,1,256]{2,1,0:T(1,128)S(1)}, u32[]{:S(2)}) copy-start(f32[1,1,256]{2,1,0:T(1,128)S(1)} %get-tuple-element.142) | copy-start | bytes 3076
  8.8 15.4 %copy-start.31 = (f32[1,1,256]{2,1,0:T(1,128)}, f32[1,1,256]{2,1,0:T(1,128)S(1)}, u32[]{:S(2)}) copy-start(f32[1,1,256]{2,1,0:T(1,128)S(1)} %get-tuple-element.143) | copy-start | bytes 3076
  8.8 15.4 %copy-start.33 = (f32[1,1,256]{2,1,0:T(1,128)}, f32[1,1,256]{2,1,0:T(1,128)S(1)}, u32[]{:S(2)}) copy-start(f32[1,1,256]{2,1,0:T(1,128)S(1)} %get-tuple-element.144) | copy-start | bytes 3076
  8.8 15.4 %copy-start.35 = (f32[1,1,256]{2,1,0:T(1,128)}, f32[1,1,256]{2,1,0:T(1,128)S(1)}, u32[]{:S(2)}) copy-start(f32[1,1,256]{2,1,0:T(1,128)S(1)} %get-tuple-element.145) | copy-start | bytes 3076
  8.8 15.4 %copy-start.37 = (f32[1,1,256]{2,1,0:T(1,128)}, f32[1,1,256]{2,1,0:T(1,128)S(1)}, u32[]{:S(2)}) copy-start(f32[1,1,256]{2,1,0:T(1,128)S(1)} %get-tuple-element.146) | copy-start | bytes 3076
  8.8 15.4 %copy-start.39 = (f32[1,1,256]{2,1,0:T(1,128)}, f32[1,1,256]{2,1,0:T(1,128)S(1)}, u32[]{:S(2)}) copy-start(f32[1,1,256]{2,1,0:T(1,128)S(1)} %get-tuple-element.147) | copy-start | bytes 3076
  8.9 15.4 %copy-start.41 = (f32[1,1,256]{2,1,0:T(1,128)}, f32[1,1,256]{2,1,0:T(1,128)S(1)}, u32[]{:S(2)}) copy-start(f32[1,1,256]{2,1,0:T(1,128)S(1)} %get-tuple-element.148) | copy-start | bytes 3076
  14.4 8.5 %collective-permute-start.1 = (bf16[4,3,38,256]{3,2,1,0:T(8,128)(2,1)S(1)}, bf16[4,3,38,256]{3,2,1,0:T(8,128)(2,1)S(1)}, u32[]{:S(2)}, u32[]{:S(2)}) collective-permute-start(bf16[4,3,38,256]{3,2,1,0:T(8,128)(2,1)S(1)} %get-tuple-element.128), channel_id=1, source_target_pairs={{0,1},{1,2},{2,3},{3,4},{4,5},{5,6},{6,7},{7,8},{8,9},{9,10},{10,1... | collective-permute-start | bytes 700424 | tf_op jit(solution)/shard_map/ppermute | solution.py:26
  15.1 7.8 %collective-permute-start.2 = (bf16[4,3,38,256]{3,2,1,0:T(8,128)(2,1)S(1)}, bf16[4,3,38,256]{3,2,1,0:T(8,128)(2,1)}, u32[]{:S(2)}, u32[]{:S(2)}) collective-permute-start(bf16[4,3,38,256]{3,2,1,0:T(8,128)(2,1)S(1)} %get-tuple-element.129), channel_id=1, source_target_pairs={{1,0},{2,1},{3,2},{4,3},{5,4},{6,5},{7,6},{8,7},{9,8},{10,9},{11,1... | collective-permute-start | bytes 700424 | tf_op jit(solution)/shard_map/ppermute | solution.py:27
  19.1 5.3 %copy-start.5 = (bf16[4,8,32,256]{3,2,1,0:T(8,128)(2,1)S(1)}, bf16[4,8,32,256]{3,2,1,0:T(8,128)(2,1)}, u32[]{:S(2)}) copy-start(bf16[4,8,32,256]{3,2,1,0:T(8,128)(2,1)} %param.13) | copy-start | bytes 1572868
  19.1 5.3 %copy-start.43 = (f32[1,1,256]{2,1,0:T(1,128)S(1)}, f32[1,1,256]{2,1,0:T(1,128)}, u32[]{:S(2)}) copy-start(f32[1,1,256]{2,1,0:T(1,128)} %get-tuple-element.149) | copy-start | bytes 3076
  19.1 5.3 %copy-start.45 = (f32[1,1,256]{2,1,0:T(1,128)S(1)}, f32[1,1,256]{2,1,0:T(1,128)}, u32[]{:S(2)}) copy-start(f32[1,1,256]{2,1,0:T(1,128)} %get-tuple-element.150) | copy-start | bytes 3076
  19.1 5.3 %copy-start.47 = (f32[1,1,256]{2,1,0:T(1,128)S(1)}, f32[1,1,256]{2,1,0:T(1,128)}, u32[]{:S(2)}) copy-start(f32[1,1,256]{2,1,0:T(1,128)} %get-tuple-element.151) | copy-start | bytes 3076
  19.1 5.3 %copy-start.49 = (f32[1,1,256]{2,1,0:T(1,128)S(1)}, f32[1,1,256]{2,1,0:T(1,128)}, u32[]{:S(2)}) copy-start(f32[1,1,256]{2,1,0:T(1,128)} %get-tuple-element.152) | copy-start | bytes 3076
  19.1 5.3 %copy-start.51 = (f32[1,1,256]{2,1,0:T(1,128)S(1)}, f32[1,1,256]{2,1,0:T(1,128)}, u32[]{:S(2)}) copy-start(f32[1,1,256]{2,1,0:T(1,128)} %get-tuple-element.153) | copy-start | bytes 3076
  19.1 5.3 %copy-start.53 = (f32[1,1,256]{2,1,0:T(1,128)S(1)}, f32[1,1,256]{2,1,0:T(1,128)}, u32[]{:S(2)}) copy-start(f32[1,1,256]{2,1,0:T(1,128)} %get-tuple-element.154) | copy-start | bytes 3076
  19.1 5.3 %copy-start.55 = (f32[1,1,256]{2,1,0:T(1,128)S(1)}, f32[1,1,256]{2,1,0:T(1,128)}, u32[]{:S(2)}) copy-start(f32[1,1,256]{2,1,0:T(1,128)} %get-tuple-element.155) | copy-start | bytes 3076
  19.1 5.3 %copy-start.57 = (f32[1,1,256]{2,1,0:T(1,128)S(1)}, f32[1,1,256]{2,1,0:T(1,128)}, u32[]{:S(2)}) copy-start(f32[1,1,256]{2,1,0:T(1,128)} %get-tuple-element.156) | copy-start | bytes 3076
  19.1 5.3 %copy-start.59 = (f32[1,1,256]{2,1,0:T(1,128)S(1)}, f32[1,1,256]{2,1,0:T(1,128)}, u32[]{:S(2)}) copy-start(f32[1,1,256]{2,1,0:T(1,128)} %get-tuple-element.157) | copy-start | bytes 3076
  19.2 5.3 %copy-start.61 = (f32[1,1,256]{2,1,0:T(1,128)S(1)}, f32[1,1,256]{2,1,0:T(1,128)}, u32[]{:S(2)}) copy-start(f32[1,1,256]{2,1,0:T(1,128)} %get-tuple-element.158) | copy-start | bytes 3076
  19.2 5.3 %copy-start.63 = (f32[1,1,256]{2,1,0:T(1,128)S(1)}, f32[1,1,256]{2,1,0:T(1,128)}, u32[]{:S(2)}) copy-start(f32[1,1,256]{2,1,0:T(1,128)} %get-tuple-element.159) | copy-start | bytes 3076
  19.2 5.3 %copy-start.65 = (f32[1,1,256]{2,1,0:T(1,128)S(1)}, f32[1,1,256]{2,1,0:T(1,128)}, u32[]{:S(2)}) copy-start(f32[1,1,256]{2,1,0:T(1,128)} %get-tuple-element.160) | copy-start | bytes 3076
  19.2 5.3 %copy-start.67 = (f32[1,1,256]{2,1,0:T(1,128)S(1)}, f32[1,1,256]{2,1,0:T(1,128)}, u32[]{:S(2)}) copy-start(f32[1,1,256]{2,1,0:T(1,128)} %get-tuple-element.161) | copy-start | bytes 3076
  19.2 5.3 %copy-start.69 = (f32[1,1,256]{2,1,0:T(1,128)S(1)}, f32[1,1,256]{2,1,0:T(1,128)}, u32[]{:S(2)}) copy-start(f32[1,1,256]{2,1,0:T(1,128)} %get-tuple-element.162) | copy-start | bytes 3076
  19.2 5.3 %copy-start.71 = (f32[1,1,256]{2,1,0:T(1,128)S(1)}, f32[1,1,256]{2,1,0:T(1,128)}, u32[]{:S(2)}) copy-start(f32[1,1,256]{2,1,0:T(1,128)} %get-tuple-element.163) | copy-start | bytes 3076
  19.2 5.3 %copy-start.73 = (f32[1,1,256]{2,1,0:T(1,128)S(1)}, f32[1,1,256]{2,1,0:T(1,128)}, u32[]{:S(2)}) copy-start(f32[1,1,256]{2,1,0:T(1,128)} %get-tuple-element.164) | copy-start | bytes 3076
  19.2 5.3 %copy-start.75 = (f32[1,1,256]{2,1,0:T(1,128)S(1)}, f32[1,1,256]{2,1,0:T(1,128)}, u32[]{:S(2)}) copy-start(f32[1,1,256]{2,1,0:T(1,128)} %get-tuple-element.165) | copy-start | bytes 3076
  19.2 5.3 %copy-start.77 = (f32[1,1,256]{2,1,0:T(1,128)S(1)}, f32[1,1,256]{2,1,0:T(1,128)}, u32[]{:S(2)}) copy-start(f32[1,1,256]{2,1,0:T(1,128)} %get-tuple-element.166) | copy-start | bytes 3076
  19.2 5.3 %copy-start.79 = (f32[1,1,256]{2,1,0:T(1,128)S(1)}, f32[1,1,256]{2,1,0:T(1,128)}, u32[]{:S(2)}) copy-start(f32[1,1,256]{2,1,0:T(1,128)} %get-tuple-element.167) | copy-start | bytes 3076
  19.3 5.3 %copy-start.81 = (f32[1,1,256]{2,1,0:T(1,128)S(1)}, f32[1,1,256]{2,1,0:T(1,128)}, u32[]{:S(2)}) copy-start(f32[1,1,256]{2,1,0:T(1,128)} %get-tuple-element.168) | copy-start | bytes 3076
  19.3 5.3 %copy-start.83 = (f32[1,1,256]{2,1,0:T(1,128)S(1)}, f32[1,1,256]{2,1,0:T(1,128)}, u32[]{:S(2)}) copy-start(f32[1,1,256]{2,1,0:T(1,128)} %get-tuple-element.169) | copy-start | bytes 3076
  24.7 9.7 %copy-start.26 = (f32[256]{0:T(256)S(1)}, f32[256]{0:T(256)}, u32[]{:S(2)}) copy-start(f32[256]{0:T(256)} %param.19) | copy-start | bytes 3076
  41.1 12.5 %copy-start.13 = (f32[8,32,256]{2,1,0:T(8,128)}, f32[8,32,256]{2,1,0:T(8,128)S(1)}, u32[]{:S(2)}) copy-start(f32[8,32,256]{2,1,0:T(8,128)S(1)} %get-tuple-element.97) | copy-start | bytes 786436
  41.1 12.5 %copy-start.15 = (f32[8,32,256]{2,1,0:T(8,128)}, f32[8,32,256]{2,1,0:T(8,128)S(1)}, u32[]{:S(2)}) copy-start(f32[8,32,256]{2,1,0:T(8,128)S(1)} %get-tuple-element.98) | copy-start | bytes 786436
  41.1 12.5 %copy-start.17 = (f32[8,32,256]{2,1,0:T(8,128)}, f32[8,32,256]{2,1,0:T(8,128)S(1)}, u32[]{:S(2)}) copy-start(f32[8,32,256]{2,1,0:T(8,128)S(1)} %get-tuple-element.99) | copy-start | bytes 786436
  41.1 12.5 %copy-start.19 = (f32[8,32,256]{2,1,0:T(8,128)}, f32[8,32,256]{2,1,0:T(8,128)S(1)}, u32[]{:S(2)}) copy-start(f32[8,32,256]{2,1,0:T(8,128)S(1)} %get-tuple-element.100) | copy-start | bytes 786436
  55.5 3.3 %collective-permute-start.3 = (f32[270336]{0:T(1024)}, f32[270336]{0:T(1024)}, u32[]{:S(2)}, u32[]{:S(2)}) collective-permute-start(f32[270336]{0:T(1024)} %pad_dynamic-slice_fusion), channel_id=1, source_target_pairs={{0,1},{1,0},{2,3},{3,2},{4,5},{5,4},{6,7},{7,6},{8,9},{9,8},{10,11... | collective-permute-start | bytes 3244040 | tf_op jit(solution)/shard_map/ppermute | solution.py:225
  56.1 5.4 %copy-start.9 = (f32[4,8,32,256]{3,2,1,0:T(8,128)S(1)}, f32[4,8,32,256]{3,2,1,0:T(8,128)}, u32[]{:S(2)}) copy-start(f32[4,8,32,256]{3,2,1,0:T(8,128)} %get-tuple-element.22) | copy-start | bytes 3145732
  71.1 24.2 %copy-start.2 = (f32[4,8,32,256]{3,2,1,0:T(8,128)S(1)}, f32[4,8,32,256]{3,2,1,0:T(8,128)}, u32[]{:S(2)}) copy-start(f32[4,8,32,256]{3,2,1,0:T(8,128)} %copy-done.1) | copy-start | bytes 3145732
  71.4 6.1 %collective-permute-start.11 = (f32[12800]{0:T(1024)S(1)}, f32[12800]{0:T(1024)S(1)}, u32[]{:S(2)}, u32[]{:S(2)}) collective-permute-start(f32[12800]{0:T(1024)S(1)} %pad_maximum_fusion.14), channel_id=1, source_target_pairs={{0,1},{1,0},{2,3},{3,2},{4,5},{5,4},{6,7},{7,6},{8,9},{9,8},{10,11... | collective-permute-start | bytes 153608 | tf_op jit(solution)/shard_map/ppermute | solution.py:16
  73.0 22.3 %collective-permute-start.4 = (f32[4,3,32,256]{3,2,1,0:T(8,128)S(1)}, f32[4,3,32,256]{3,2,1,0:T(8,128)S(1)}, u32[]{:S(2)}, u32[]{:S(2)}) collective-permute-start(f32[4,3,32,256]{3,2,1,0:T(8,128)S(1)} %get-tuple-element.122), channel_id=1, source_target_pairs={{0,1},{1,2},{2,3},{3,4},{4,5},{5,6},{6,7},{7,8},{8,9},{9,10},{10,1... | collective-permute-start | bytes 1179656 | tf_op jit(solution)/shard_map/ppermute | solution.py:26
  73.2 22.1 %collective-permute-start.5 = (f32[4,3,32,256]{3,2,1,0:T(8,128)S(1)}, f32[4,3,32,256]{3,2,1,0:T(8,128)S(1)}, u32[]{:S(2)}, u32[]{:S(2)}) collective-permute-start(f32[4,3,32,256]{3,2,1,0:T(8,128)S(1)} %get-tuple-element.123), channel_id=1, source_target_pairs={{1,0},{2,1},{3,2},{4,3},{5,4},{6,5},{7,6},{8,7},{9,8},{10,9},{11,1... | collective-permute-start | bytes 1179656 | tf_op jit(solution)/shard_map/ppermute | solution.py:27
  77.5 8.4 %collective-permute-start.12 = (f32[12800]{0:T(1024)S(1)}, f32[12800]{0:T(1024)S(1)}, u32[]{:S(2)}, u32[]{:S(2)}) collective-permute-start(f32[12800]{0:T(1024)S(1)} %fusion.355), channel_id=1, source_target_pairs={{0,2},{1,3},{2,0},{3,1},{4,6},{5,7},{6,4},{7,5},{8,10},{9,11},{10,... | collective-permute-start | bytes 153608 | tf_op jit(solution)/shard_map/ppermute | solution.py:16
  86.0 4.2 %collective-permute-start.13 = (f32[12800]{0:T(1024)S(1)}, f32[12800]{0:T(1024)S(1)}, u32[]{:S(2)}, u32[]{:S(2)}) collective-permute-start(f32[12800]{0:T(1024)S(1)} %add.835), channel_id=1, source_target_pairs={{0,4},{1,5},{2,6},{3,7},{4,0},{5,1},{6,2},{7,3},{8,12},{9,13},{10,... | collective-permute-start | bytes 153608 | tf_op jit(solution)/shard_map/ppermute | solution.py:16
  90.2 5.1 %collective-permute-start.14 = (f32[12800]{0:T(1024)S(1)}, f32[12800]{0:T(1024)S(1)}, u32[]{:S(2)}, u32[]{:S(2)}) collective-permute-start(f32[12800]{0:T(1024)S(1)} %add.836), channel_id=1, source_target_pairs={{0,8},{1,9},{2,10},{3,11},{4,12},{5,13},{6,14},{7,15},{8,0},{9,1},... | collective-permute-start | bytes 153608 | tf_op jit(solution)/shard_map/ppermute | solution.py:16
  97.0 14.2 %collective-permute-start.6 = (f32[67584]{0:T(1024)S(1)}, f32[67584]{0:T(1024)S(1)}, u32[]{:S(2)}, u32[]{:S(2)}) collective-permute-start(f32[67584]{0:T(1024)S(1)} %get-tuple-element.119), channel_id=1, source_target_pairs={{0,2},{1,3},{2,0},{3,1},{4,6},{5,7},{6,4},{7,5},{8,10},{9,11},{10,... | collective-permute-start | bytes 811016 | tf_op jit(solution)/shard_map/ppermute | solution.py:225
  97.1 14.1 %collective-permute-start.7 = (f32[67584]{0:T(1024)S(1)}, f32[67584]{0:T(1024)S(1)}, u32[]{:S(2)}, u32[]{:S(2)}) collective-permute-start(f32[67584]{0:T(1024)S(1)} %get-tuple-element.121), channel_id=1, source_target_pairs={{0,4},{1,5},{2,6},{3,7},{4,0},{5,1},{6,2},{7,3},{8,12},{9,13},{10,... | collective-permute-start | bytes 811016 | tf_op jit(solution)/shard_map/ppermute | solution.py:225
  97.1 14.1 %collective-permute-start.8 = (f32[67584]{0:T(1024)S(1)}, f32[67584]{0:T(1024)S(1)}, u32[]{:S(2)}, u32[]{:S(2)}) collective-permute-start(f32[67584]{0:T(1024)S(1)} %get-tuple-element.120), channel_id=1, source_target_pairs={{0,6},{1,7},{2,4},{3,5},{4,2},{5,3},{6,0},{7,1},{8,14},{9,15},{10,... | collective-permute-start | bytes 811016 | tf_op jit(solution)/shard_map/ppermute | solution.py:225
  111.3 7.3 %collective-permute-start.9 = (f32[33792]{0:T(1024)S(1)}, f32[33792]{0:T(1024)S(1)}, u32[]{:S(2)}, u32[]{:S(2)}) collective-permute-start(f32[33792]{0:T(1024)S(1)} %dynamic_slice.31), channel_id=1, source_target_pairs={{0,8},{1,9},{2,10},{3,11},{4,12},{5,13},{6,14},{7,15},{8,0},{9,1},... | collective-permute-start | bytes 405512 | tf_op jit(solution)/shard_map/ppermute | solution.py:225
  118.6 5.6 %collective-permute-start.15 = (bf16[33792]{0:T(1024)(128)(2,1)S(1)}, bf16[33792]{0:T(1024)(128)(2,1)S(1)}, u32[]{:S(2)}, u32[]{:S(2)}) collective-permute-start(bf16[33792]{0:T(1024)(128)(2,1)S(1)} %dynamic-slice_add_fusion), channel_id=1, source_target_pairs={{0,8},{1,9},{2,10},{3,11},{4,12},{5,13},{6,14},{7,15},{8,0},{9,1},... | collective-permute-start | bytes 202760 | tf_op jit(solution)/shard_map/ppermute | solution.py:240
  124.3 9.7 %copy-start.14 = (f32[8,32,256]{2,1,0:T(8,128)S(1)}, f32[8,32,256]{2,1,0:T(8,128)}, u32[]{:S(2)}) copy-start(f32[8,32,256]{2,1,0:T(8,128)} %copy-done.13) | copy-start | bytes 786436
  124.3 9.7 %copy-start.16 = (f32[8,32,256]{2,1,0:T(8,128)S(1)}, f32[8,32,256]{2,1,0:T(8,128)}, u32[]{:S(2)}) copy-start(f32[8,32,256]{2,1,0:T(8,128)} %copy-done.15) | copy-start | bytes 786436
  124.3 9.7 %copy-start.18 = (f32[8,32,256]{2,1,0:T(8,128)S(1)}, f32[8,32,256]{2,1,0:T(8,128)}, u32[]{:S(2)}) copy-start(f32[8,32,256]{2,1,0:T(8,128)} %copy-done.17) | copy-start | bytes 786436
  124.3 9.7 %copy-start.20 = (f32[8,32,256]{2,1,0:T(8,128)S(1)}, f32[8,32,256]{2,1,0:T(8,128)}, u32[]{:S(2)}) copy-start(f32[8,32,256]{2,1,0:T(8,128)} %copy-done.19) | copy-start | bytes 786436
  124.3 6.0 %collective-permute-start.16 = (bf16[67584]{0:T(1024)(128)(2,1)S(1)}, bf16[67584]{0:T(1024)(128)(2,1)S(1)}, u32[]{:S(2)}, u32[]{:S(2)}) collective-permute-start(bf16[67584]{0:T(1024)(128)(2,1)S(1)} %pad_maximum_fusion.13), channel_id=1, source_target_pairs={{0,4},{1,5},{2,6},{3,7},{4,0},{5,1},{6,2},{7,3},{8,12},{9,13},{10,... | collective-permute-start | bytes 405512 | tf_op jit(solution)/shard_map/ppermute | solution.py:240
  124.4 6.9 %collective-permute-start.17 = (bf16[67584]{0:T(1024)(128)(2,1)S(1)}, bf16[67584]{0:T(1024)(128)(2,1)S(1)}, u32[]{:S(2)}, u32[]{:S(2)}) collective-permute-start(bf16[67584]{0:T(1024)(128)(2,1)S(1)} %pad_maximum_fusion.13), channel_id=1, source_target_pairs={{0,2},{1,3},{2,0},{3,1},{4,6},{5,7},{6,4},{7,5},{8,10},{9,11},{10,... | collective-permute-start | bytes 405512 | tf_op jit(solution)/shard_map/ppermute | solution.py:240
  126.5 6.5 %collective-permute-start.18 = (bf16[67584]{0:T(1024)(128)(2,1)S(1)}, bf16[67584]{0:T(1024)(128)(2,1)S(1)}, u32[]{:S(2)}, u32[]{:S(2)}) collective-permute-start(bf16[67584]{0:T(1024)(128)(2,1)S(1)} %pad_maximum_fusion.13), channel_id=1, source_target_pairs={{0,6},{1,7},{2,4},{3,5},{4,2},{5,3},{6,0},{7,1},{8,14},{9,15},{10,... | collective-permute-start | bytes 405512 | tf_op jit(solution)/shard_map/ppermute | solution.py:240
  128.5 7.2 %collective-permute-start.10 = (bf16[4,8,3,256]{3,2,1,0:T(4,128)(2,1)S(1)}, bf16[4,8,3,256]{3,2,1,0:T(4,128)(2,1)S(1)}, u32[]{:S(2)}, u32[]{:S(2)}) collective-permute-start(bf16[4,8,3,256]{3,2,1,0:T(4,128)(2,1)S(1)} %slice.1578), channel_id=1, source_target_pairs={{0,15},{1,14},{2,13},{3,12},{4,11},{5,10},{6,9},{7,8},{8,7},{9,6},... | collective-permute-start | bytes 147464 | tf_op jit(solution)/shard_map/ppermute | solution.py:178
  134.0 2.9 %collective-permute-start.19 = (bf16[270336]{0:T(1024)(128)(2,1)}, bf16[270336]{0:T(1024)(128)(2,1)}, u32[]{:S(2)}, u32[]{:S(2)}) collective-permute-start(bf16[270336]{0:T(1024)(128)(2,1)} %pad_maximum_fusion.5), channel_id=1, source_target_pairs={{0,1},{1,0},{2,3},{3,2},{4,5},{5,4},{6,7},{7,6},{8,9},{9,8},{10,11... | collective-permute-start | bytes 1622024 | tf_op jit(solution)/shard_map/ppermute | solution.py:240
  (84 other events, 262.7 us)

commit v17 on v12

--- a/solution.py
+++ b/solution.py
@@ -16,15 +16,17 @@
     return lax.ppermute(x, axis, [(i, i ^ 1 << bit) for i in range(lax.axis_size(axis))])
 
 
-def with_halo(x, sides, width):
+def with_halo(x, sides, width, send_dtype=None):
     for axis, dim in sides:
         size, length = (lax.axis_size(axis), x.shape[dim])
         up = [(i, (i + 1) % size) for i in range(size)]
         down = [(j, i) for i, j in up]
         last = lax.slice_in_dim(x, length - width, length, axis=dim)
         leading = lax.slice_in_dim(x, 0, width, axis=dim)
-        before = lax.ppermute(last, axis, up)
-        after = lax.ppermute(leading, axis, down)
+        if send_dtype is not None:
+            last, leading = last.astype(send_dtype), leading.astype(send_dtype)
+        before = lax.ppermute(last, axis, up).astype(x.dtype)
+        after = lax.ppermute(leading, axis, down).astype(x.dtype)
         x = jnp.concatenate([before, x, after], axis=dim)
     return x
 
@@ -289,7 +291,7 @@
 
     def backward(grad_normed):
         grad_depth, kernel_sum, dw_bias_sum = depth_backward(grad_normed)
-        grad_halo = with_halo(grad_depth, (("lon", 1),), 3)
+        grad_halo = with_halo(grad_depth, (("lon", 1),), 3, jnp.bfloat16)
         return grad_halo, kernel_sum, dw_bias_sum
 
     def backward_conv(grad_halo):

time: 138 us -> 135 us (0.978)
  waiting for transfers between devices: 28.1 us -> 25.6 us
  starting transfers between devices: 31 us -> 29.1 us
    ppermute x5, starting transfers between devices: 6.99 us -> 4.27 us  [radix_allreduce(): lax.ppermute(send, axis, [(i, i ^ d << low) for i in range(size)])]
    ppermute x4, waiting for transfers between devices: 8.91 us -> 6.82 us  [the longest x2 6.81 us: with_halo(): before = lax.ppermute(last, axis, up).astype(x.dtype)]
    unnamed x272 -> x266, local copies, waits for them, and re-layouts: 4.29 us -> 6.32 us
    ppermute x5, starting transfers between devices: 5.51 us -> 6.99 us  [radix_allreduce(): lax.ppermute(cur, axis, [(i, i ^ d << low) for i in range(size)])]
  transfers between devices with their start and end apart: 20 -> 20, of which waited for: 10 -> 9; matrix products, arithmetic and copies ran while one was open for 16% -> 16% of each run, Pallas kernels for 0% -> 0%
where the time goes in v17:
time: 135 us; the launch traced here: 134 us
  other arithmetic  48.6 us (36%)
  starting transfers between devices  29.1 us (22%)
  waiting for transfers between devices  25.6 us (19%)
  local copies, waits for them, and re-layouts  16.3 us (12%)
  matrix products  11.8 us (9%)
  between operations  3.09 us (2%)
    add x1, other arithmetic, backward_conv(): grad_ext + dw_kernel[lon_off, lat_off] * padded[:, 6 - lon_off:6 - lon_of...  10.2 us
    reduce_sum x1, other arithmetic, local_step(): mean_val = jnp.mean(depth, axis=-1, keepdims=True)  9.29 us
    reduce_sum x4, other arithmetic, depth_backward(): jnp.sum(grad_depth * extended[:, lon_off:lon_off + lon_dev, lat_off:lat_o...  8.59 us
    ppermute x2, starting transfers between devices, with_halo(): after = lax.ppermute(leading, axis, down).astype(x.dtype)  8.05 us
    ppermute x5, waiting for transfers between devices, radix_allreduce(): lax.ppermute(cur, axis, [(i, i ^ d << low) for i in range(size)])  7.71 us
    ppermute x4, waiting for transfers between devices, swapped(): lax.ppermute(x, axis, [(i, i ^ 1 << bit) for i in range(lax.axis_size(axi...  7.03 us
    ppermute x5, starting transfers between devices, radix_allreduce(): lax.ppermute(cur, axis, [(i, i ^ d << low) for i in range(size)])  6.99 us
    ppermute x2, waiting for transfers between devices, with_halo(): before = lax.ppermute(last, axis, up).astype(x.dtype)  6.81 us
  transfers between devices with their start and end apart: 20, of which 9 were waited for; matrix products, arithmetic and copies ran while one was open for 16% of the time, Pallas kernels for 0%

profile of v17, /device:TPU:0, one launch (start us, length us, event | category | flops | bytes accessed | tf_op | source)
XLA Modules:
  0.0 134.4 jit_solution(13090395286419206194)
XLA Ops:
  0.7 1.0 slice.714
  1.7 5.5 %collective-permute-start = (bf16[4,8,3,256]{3,2,1,0:T(4,128)(2,1)S(1)}, bf16[4,8,3,256]{3,2,1,0:T(4,128)(2,1)S(1)}, u32[]{:S(2)}, u32[]{:S(2)}) collective-permute-start(bf16[4,8,3,256]{3,2,1,0:T(4,128)(2,1)S(1)} %slice.714), channel_id=1, source_target_pairs={{0,15},{1,14},{2,13},{3,12},{4,11},{5,10},{6,9},{7,8},{8,7},{9,6},... | collective-permute-start | bytes 147464 | tf_op jit(solution)/shard_map/ppermute | solution.py:176
  7.2 1.6 %fusion.263 = (f32[1,1,256]{2,1,0:T(1,128)S(1)}, f32[1,1,256]{2,1,0:T(1,128)S(1)}, f32[1,1,256]{2,1,0:T(1,128)S(1)}, f32[1,1,256]{2,1,0:T(1,128)S(1)}, f32[1,1,2...) fusion(f32[7,7,256]{2,1,0:T(8,128)} %param.17), kind=kLoop, calls=%fused_computation.543 | loop fusion | bytes 38912 | tf_op jit(solution)/shard_map/slice | solution.py:61
  8.9 1.7 %fusion.264 = (f32[1,1,256]{2,1,0:T(1,128)}, f32[1,1,256]{2,1,0:T(1,128)}, f32[1,1,256]{2,1,0:T(1,128)}, f32[1,1,256]{2,1,0:T(1,128)}, f32[1,1,256]{2,1,0:T(1,12...) fusion(f32[7,7,256]{2,1,0:T(8,128)} %param.17), kind=kLoop, calls=%fused_computation.544 | loop fusion | bytes 38912 | tf_op jit(solution)/shard_map/slice | solution.py:61
  10.5 1.5 %fusion.265 = (f32[1,1,256]{2,1,0:T(1,128)}, f32[1,1,256]{2,1,0:T(1,128)}, f32[1,1,256]{2,1,0:T(1,128)}, f32[1,1,256]{2,1,0:T(1,128)}, f32[1,1,256]{2,1,0:T(1,12...) fusion(f32[7,7,256]{2,1,0:T(8,128)} %param.17), kind=kLoop, calls=%fused_computation.545 | loop fusion | bytes 22528 | tf_op jit(solution)/shard_map/slice | solution.py:61
  12.1 0.8 copy.25
  13.1 1.3 pad_maximum_fusion.12
  14.4 0.7 collective-permute-start.1
  15.1 3.8 %collective-permute-start.2 = (bf16[4,3,38,256]{3,2,1,0:T(8,128)(2,1)S(1)}, bf16[4,3,38,256]{3,2,1,0:T(8,128)(2,1)}, u32[]{:S(2)}, u32[]{:S(2)}) collective-permute-start(bf16[4,3,38,256]{3,2,1,0:T(8,128)(2,1)S(1)} %get-tuple-element.123), channel_id=1, source_target_pairs={{1,0},{2,1},{3,2},{4,3},{5,4},{6,5},{7,6},{8,7},{9,8},{10,9},{11,1... | collective-permute-start | bytes 700424 | tf_op jit(solution)/shard_map/ppermute | solution.py:29
  19.4 3.5 %collective-permute-done.1 = bf16[4,3,38,256]{3,2,1,0:T(8,128)(2,1)S(1)} collective-permute-done((bf16[4,3,38,256]{3,2,1,0:T(8,128)(2,1)S(1)}, bf16[4,3,38,256]{3,2,1,0:T(8,128)(2,1)S(1)}, u32[]{:S(2)}, u32[]{:S(2)}) %collective-permute-start.1) | collective-permute-done | bytes 233504 | tf_op jit(solution)/shard_map/ppermute | solution.py:28
  22.9 1.3 maximum_maximum_fusion
  24.7 9.3 %fusion.258 = (f32[4,8,32]{2,1,0:T(8,128)S(1)}, f32[4,8,32,256]{3,2,1,0:T(8,128)S(1)}) fusion(bf16[4,11,38,256]{3,2,1,0:T(8,128)(2,1)S(1)} %get-tuple-element.121, f32[256]{0:T(256)} %bitcast.432, f32[256]{0:T(256)} %bitcast.434, f32[256]{0:T(256)S(1)} %bitcast.340, f32[256]{0:T(256)S(1)} %bitcast.342, f32[256]{0:T(256)S(1)} %bitcast.344, ...), kind=kLoop, calls=%fused_computation.539 | loop fusion | flops 43514880 | bytes 23746560 | tf_op jit(solution)/shard_map/reduce_sum | solution.py:64
  34.4 1.1 add_convert_fusion
  36.7 0.5 convolution_add_fusion.12
  37.5 0.5 convolution_add_fusion.11
  38.3 0.5 convolution_add_fusion.10
  39.0 1.1 fusion.256
  40.1 2.5 %multiply_reduce_fusion.7 = (f32[256]{0:T(256)S(1)}, f32[256]{0:T(256)S(1)}, f32[256]{0:T(256)S(1)}, f32[256]{0:T(256)S(1)}, f32[8,32,256]{2,1,0:T(8,128)S(1)}, ...) fusion(f32[256]{0:T(256)S(1)} %copy-done.23, ...), kind=kLoop, calls=%fused_computation.479 | loop fusion | flops 7863296 | bytes 2497536 | tf_op jit(solution)/shard_map/reduce_sum | solution.py:119
  42.7 0.6 fusion.247
  43.3 0.9 fusion.250
  44.9 0.9 fusion.248
  45.8 0.6 convolution_add_fusion.2
  46.4 0.9 fusion.252
  47.3 0.6 convolution_add_fusion.1
  47.9 0.9 fusion.254
  48.8 0.6 fusion
  49.4 0.8 copy.28
  52.5 1.3 pad_maximum_fusion.3
  53.8 0.7 copy-done.8
  55.3 1.2 pad_dynamic-slice_fusion
  56.5 0.5 copy-done.9
  57.0 0.7 collective-permute-start.3
  57.6 2.7 %collective-permute-done.3 = f32[270336]{0:T(1024)} collective-permute-done((f32[270336]{0:T(1024)}, f32[270336]{0:T(1024)}, u32[]{:S(2)}, u32[]{:S(2)}) %collective-permute-start.3) | collective-permute-done | bytes 1081376 | tf_op jit(solution)/shard_map/ppermute | solution.py:223
  60.3 2.7 %fusion.99 = f32[270336]{0:T(1024)} fusion(f32[270336]{0:T(1024)} %collective-permute-done.3, s32[]{:T(128)S(6)} %select_n.114, f32[526336]{0:T(1024)} %copy-done.9), kind=kLoop, calls=%fused_computation.272 | loop fusion | flops 270336 | bytes 4268036 | tf_op jit(solution)/shard_map/add | solution.py:223
  63.0 0.6 multiply_reduce_fusion.4
  63.6 3.8 %fusion.196 = (f32[256]{0:T(256)S(1)}, f32[256]{0:T(256)}, f32[256]{0:T(256)}, f32[256]{0:T(256)}, f32[256]{0:T(256)}, /*index=5*/f32[256]{0:T(256)}, f32[256]{0...) fusion(bf16[4,11,38,256]{3,2,1,0:T(8,128)(2,1)S(1)} %get-tuple-, ...), kind=kLoop, calls=%fused_computation.370 | loop fusion | flops 15986176 | bytes 12618752 | tf_op jit(solution)/shard_map/reduce_sum | solution.py:158
  67.4 2.6 %fusion.145 = (f32[256]{0:T(256)S(1)}, f32[256]{0:T(256)S(1)}, f32[256]{0:T(256)S(1)}, f32[256]{0:T(256)S(1)}, f32[256]{0:T(256)S(1)}, /*index=5*/f32[256]{0:T(2...) fusion(f32[4,8,32,256]{3,2,1,0:T(8,128)S(1)} %get-tuple-element, ...), kind=kLoop, calls=%fused_computation.319 | loop fusion | flops 14413312 | bytes 11028480 | tf_op jit(solution)/shard_map/reduce_sum | solution.py:158
  70.1 1.8 %fusion.178 = (f32[256]{0:T(256)S(1)}, f32[256]{0:T(256)S(1)}, f32[256]{0:T(256)S(1)}, f32[256]{0:T(256)S(1)}, f32[256]{0:T(256)S(1)}, /*index=5*/f32[256]{0:T(2...) fusion(f32[4,8,32,256]{3,2,1,0:T(8,128)S(1)} %get-tuple-element.90, ...), kind=kLoop, calls=%fused_computation.352 | loop fusion | flops 12842240 | bytes 3255296 | tf_op jit(solution)/shard_map/reduce_sum | solution.py:158
  73.6 4.3 %collective-permute-start.5 = (bf16[4,3,32,256]{3,2,1,0:T(8,128)(2,1)S(1)}, bf16[4,3,32,256]{3,2,1,0:T(8,128)(2,1)S(1)}, u32[]{:S(2)}, u32[]{:S(2)}) collective-permute-start(bf16[4,3,32,256]{3,2,1,0:T(8,128)(2,1)S(1)} %get-tuple-element.129), channel_id=1, source_target_pairs={{1,0},{2,1},{3,2},{4,3},{5,4},{6,5},{7,6},{8,7},{9,8},{10,9},{11,1... | collective-permute-start | bytes 589832 | tf_op jit(solution)/shard_map/ppermute | solution.py:29
  78.0 3.4 %collective-permute-done.4 = bf16[4,3,32,256]{3,2,1,0:T(8,128)(2,1)S(1)} collective-permute-done((bf16[4,3,32,256]{3,2,1,0:T(8,128)(2,1)S(1)}, bf16[4,3,32,256]{3,2,1,0:T(8,128)(2,1)S(1)}, u32[]{:S(2)}, u32[]{:S(2)}) %collective-permute-start.4) | collective-permute-done | bytes 196640 | tf_op jit(solution)/shard_map/ppermute | solution.py:28
  81.6 1.1 copy-done.10
  83.2 3.4 %collective-permute-start.8 = (f32[67584]{0:T(1024)S(1)}, f32[67584]{0:T(1024)S(1)}, u32[]{:S(2)}, u32[]{:S(2)}) collective-permute-start(f32[67584]{0:T(1024)S(1)} %get-tuple-element.115), channel_id=1, source_target_pairs={{0,6},{1,7},{2,4},{3,5},{4,2},{5,3},{6,0},{7,1},{8,14},{9,15},{10,... | collective-permute-start | bytes 811016 | tf_op jit(solution)/shard_map/ppermute | solution.py:223
  87.0 10.2 %fusion.95 = f32[4,8,38,256]{3,2,1,0:T(8,128)S(1)} fusion(f32[4,14,32,256]{3,2,1,0:T(8,128)S(1)} %pad_maximum_fusion, f32[256]{0:T(256)} %bitcast.433, f32[256]{0:T(256)} %bitcast.435, f32[256]{0:T(256)S(1)} %bitcast.341, f32[256]{0:T(256)S(1)} %bitcast.343, f32[256]{0:T(256)S(1)} %bitcast.345, f32[256]{0:T(256)S(1)} %bitcast.347, f32[256]{0:T(256)S(1)} %bitcast.349, ...), kind=kLoop, calls=%fused_computation.264 | loop fusion | flops 30195712 | bytes 3130368 | tf_op jit(solution)/shard_map/add | solution.py:303
  97.2 1.3 %collective-permute-done.8 = f32[67584]{0:T(1024)S(1)} collective-permute-done((f32[67584]{0:T(1024)S(1)}, f32[67584]{0:T(1024)S(1)}, u32[]{:S(2)}, u32[]{:S(2)}) %collective-permute-start.8) | collective-permute-done | bytes 270368 | tf_op jit(solution)/shard_map/ppermute | solution.py:223
  99.1 4.4 %collective-permute-done.12 = f32[12800]{0:T(1024)S(1)} collective-permute-done((f32[12800]{0:T(1024)S(1)}, f32[12800]{0:T(1024)S(1)}, u32[]{:S(2)}, u32[]{:S(2)}) %collective-permute-start.12) | collective-permute-done | bytes 51232 | tf_op jit(solution)/shard_map/ppermute | solution.py:16
  103.5 2.4 %collective-permute-start.13 = (f32[12800]{0:T(1024)S(1)}, f32[12800]{0:T(1024)S(1)}, u32[]{:S(2)}, u32[]{:S(2)}) collective-permute-start(f32[12800]{0:T(1024)S(1)} %add.803), channel_id=1, source_target_pairs={{0,8},{1,9},{2,10},{3,11},{4,12},{5,13},{6,14},{7,15},{8,0},{9,1},... | collective-permute-start | bytes 153608 | tf_op jit(solution)/shard_map/ppermute | solution.py:16
  105.9 2.7 %collective-permute-done.13 = f32[12800]{0:T(1024)S(1)} collective-permute-done((f32[12800]{0:T(1024)S(1)}, f32[12800]{0:T(1024)S(1)}, u32[]{:S(2)}, u32[]{:S(2)}) %collective-permute-start.13) | collective-permute-done | bytes 51232 | tf_op jit(solution)/shard_map/ppermute | solution.py:16
  108.7 2.4 %collective-permute-start.15 = (bf16[33792]{0:T(1024)(128)(2,1)S(1)}, bf16[33792]{0:T(1024)(128)(2,1)S(1)}, u32[]{:S(2)}, u32[]{:S(2)}) collective-permute-start(bf16[33792]{0:T(1024)(128)(2,1)S(1)} %add_convert_fusion.1), channel_id=1, source_target_pairs={{0,8},{1,9},{2,10},{3,11},{4,12},{5,13},{6,14},{7,15},{8,0},{9,1},... | collective-permute-start | bytes 202760 | tf_op jit(solution)/shard_map/ppermute | solution.py:235
  111.1 0.6 mul.1860
  111.7 2.3 %collective-permute-done.15 = bf16[33792]{0:T(1024)(128)(2,1)S(1)} collective-permute-done((bf16[33792]{0:T(1024)(128)(2,1)S(1)}, bf16[33792]{0:T(1024)(128)(2,1)S(1)}, u32[]{:S(2)}, u32[]{:S(2)}) %collective-permute-start.15) | collective-permute-done | bytes 67616 | tf_op jit(solution)/shard_map/ppermute | solution.py:235
  114.1 3.0 %collective-permute-start.16 = (bf16[67584]{0:T(1024)(128)(2,1)S(1)}, bf16[67584]{0:T(1024)(128)(2,1)S(1)}, u32[]{:S(2)}, u32[]{:S(2)}) collective-permute-start(bf16[67584]{0:T(1024)(128)(2,1)S(1)} %pad_maximum_fusion.13), channel_id=1, source_target_pairs={{0,4},{1,5},{2,6},{3,7},{4,0},{5,1},{6,2},{7,3},{8,12},{9,13},{10,... | collective-permute-start | bytes 405512 | tf_op jit(solution)/shard_map/ppermute | solution.py:235
  117.1 1.5 %collective-permute-start.18 = (bf16[67584]{0:T(1024)(128)(2,1)S(1)}, bf16[67584]{0:T(1024)(128)(2,1)S(1)}, u32[]{:S(2)}, u32[]{:S(2)}) collective-permute-start(bf16[67584]{0:T(1024)(128)(2,1)S(1)} %pad_maximum_fusion.13), channel_id=1, source_target_pairs={{0,6},{1,7},{2,4},{3,5},{4,2},{5,3},{6,0},{7,1},{8,14},{9,15},{10,... | collective-permute-start | bytes 405512 | tf_op jit(solution)/shard_map/ppermute | solution.py:235
  118.7 0.6 slice_multiply_fusion.2
  119.3 1.1 collective-permute-done.16
  120.5 4.3 %collective-permute-done.17 = bf16[67584]{0:T(1024)(128)(2,1)S(1)} collective-permute-done((bf16[67584]{0:T(1024)(128)(2,1)S(1)}, bf16[67584]{0:T(1024)(128)(2,1)S(1)}, u32[]{:S(2)}, u32[]{:S(2)}) %collective-permute-start.17) | collective-permute-done | bytes 135200 | tf_op jit(solution)/shard_map/ppermute | solution.py:235
  124.9 0.8 pad_maximum_fusion.5
  126.0 1.0 copy-done.19
  127.3 1.0 fusion.246
  128.3 0.9 pad_maximum_fusion.9
  129.1 1.2 broadcast_select_fusion.1
  130.7 0.6 convert_multiply_fusion.99
  131.5 0.6 convert_multiply_fusion.100
  132.2 1.1 mul.1868
  133.3 1.1 convert_multiply_fusion.98
  (344 shorter events, 10.8 us)
Async XLA Ops:
  0.6 35.6 %copy-start = (bf16[1024,256]{1,0:T(8,128)(2,1)S(1)}, bf16[1024,256]{1,0:T(8,128)(2,1)}, u32[]{:S(2)}) copy-start(bf16[1024,256]{1,0:T(8,128)(2,1)} %param.23) | copy-start | bytes 1572868
  0.7 22.2 %copy-start.4 = (bf16[4,8,32,256]{3,2,1,0:T(8,128)(2,1)S(1)}, bf16[4,8,32,256]{3,2,1,0:T(8,128)(2,1)}, u32[]{:S(2)}) copy-start(bf16[4,8,32,256]{3,2,1,0:T(8,128)(2,1)} %param.13) | copy-start | bytes 1572868
  0.7 18.3 %copy-start.22 = (s32[8,32]{1,0:T(8,128)S(1)}, s32[8,32]{1,0:T(8,128)}, u32[]{:S(2)}) copy-start(s32[8,32]{1,0:T(8,128)} %param.16) | copy-start | bytes 3076
  1.7 11.2 %collective-permute-start = (bf16[4,8,3,256]{3,2,1,0:T(4,128)(2,1)S(1)}, bf16[4,8,3,256]{3,2,1,0:T(4,128)(2,1)S(1)}, u32[]{:S(2)}, u32[]{:S(2)}) collective-permute-start(bf16[4,8,3,256]{3,2,1,0:T(4,128)(2,1)S(1)} %slice.714), channel_id=1, source_target_pairs={{0,15},{1,14},{2,13},{3,12},{4,11},{5,10},{6,9},{7,8},{8,7},{9,6},... | collective-permute-start | bytes 147464 | tf_op jit(solution)/shard_map/ppermute | solution.py:176
  8.8 15.4 %copy-start.25 = (f32[1,1,256]{2,1,0:T(1,128)}, f32[1,1,256]{2,1,0:T(1,128)S(1)}, u32[]{:S(2)}) copy-start(f32[1,1,256]{2,1,0:T(1,128)S(1)} %get-tuple-element.138) | copy-start | bytes 3076
  8.8 15.4 %copy-start.27 = (f32[1,1,256]{2,1,0:T(1,128)}, f32[1,1,256]{2,1,0:T(1,128)S(1)}, u32[]{:S(2)}) copy-start(f32[1,1,256]{2,1,0:T(1,128)S(1)} %get-tuple-element.139) | copy-start | bytes 3076
  8.8 15.4 %copy-start.29 = (f32[1,1,256]{2,1,0:T(1,128)}, f32[1,1,256]{2,1,0:T(1,128)S(1)}, u32[]{:S(2)}) copy-start(f32[1,1,256]{2,1,0:T(1,128)S(1)} %get-tuple-element.140) | copy-start | bytes 3076
  8.8 15.4 %copy-start.31 = (f32[1,1,256]{2,1,0:T(1,128)}, f32[1,1,256]{2,1,0:T(1,128)S(1)}, u32[]{:S(2)}) copy-start(f32[1,1,256]{2,1,0:T(1,128)S(1)} %get-tuple-element.141) | copy-start | bytes 3076
  8.8 15.4 %copy-start.33 = (f32[1,1,256]{2,1,0:T(1,128)}, f32[1,1,256]{2,1,0:T(1,128)S(1)}, u32[]{:S(2)}) copy-start(f32[1,1,256]{2,1,0:T(1,128)S(1)} %get-tuple-element.142) | copy-start | bytes 3076
  8.8 15.4 %copy-start.35 = (f32[1,1,256]{2,1,0:T(1,128)}, f32[1,1,256]{2,1,0:T(1,128)S(1)}, u32[]{:S(2)}) copy-start(f32[1,1,256]{2,1,0:T(1,128)S(1)} %get-tuple-element.143) | copy-start | bytes 3076
  8.8 15.4 %copy-start.37 = (f32[1,1,256]{2,1,0:T(1,128)}, f32[1,1,256]{2,1,0:T(1,128)S(1)}, u32[]{:S(2)}) copy-start(f32[1,1,256]{2,1,0:T(1,128)S(1)} %get-tuple-element.144) | copy-start | bytes 3076
  8.9 15.4 %copy-start.39 = (f32[1,1,256]{2,1,0:T(1,128)}, f32[1,1,256]{2,1,0:T(1,128)S(1)}, u32[]{:S(2)}) copy-start(f32[1,1,256]{2,1,0:T(1,128)S(1)} %get-tuple-element.145) | copy-start | bytes 3076
  14.4 8.5 %collective-permute-start.1 = (bf16[4,3,38,256]{3,2,1,0:T(8,128)(2,1)S(1)}, bf16[4,3,38,256]{3,2,1,0:T(8,128)(2,1)S(1)}, u32[]{:S(2)}, u32[]{:S(2)}) collective-permute-start(bf16[4,3,38,256]{3,2,1,0:T(8,128)(2,1)S(1)} %get-tuple-element.122), channel_id=1, source_target_pairs={{0,1},{1,2},{2,3},{3,4},{4,5},{5,6},{6,7},{7,8},{8,9},{9,10},{10,1... | collective-permute-start | bytes 700424 | tf_op jit(solution)/shard_map/ppermute | solution.py:28
  15.1 7.8 %collective-permute-start.2 = (bf16[4,3,38,256]{3,2,1,0:T(8,128)(2,1)S(1)}, bf16[4,3,38,256]{3,2,1,0:T(8,128)(2,1)}, u32[]{:S(2)}, u32[]{:S(2)}) collective-permute-start(bf16[4,3,38,256]{3,2,1,0:T(8,128)(2,1)S(1)} %get-tuple-element.123), channel_id=1, source_target_pairs={{1,0},{2,1},{3,2},{4,3},{5,4},{6,5},{7,6},{8,7},{9,8},{10,9},{11,1... | collective-permute-start | bytes 700424 | tf_op jit(solution)/shard_map/ppermute | solution.py:29
  18.9 5.3 %copy-start.107 = (s32[256]{0:T(256)}, s32[256]{0:T(256)S(1)}, u32[]{:S(2)}) copy-start(s32[256]{0:T(256)S(1)} %and_select_fusion) | copy-start | bytes 3076
  19.1 5.3 %copy-start.5 = (bf16[4,8,32,256]{3,2,1,0:T(8,128)(2,1)S(1)}, bf16[4,8,32,256]{3,2,1,0:T(8,128)(2,1)}, u32[]{:S(2)}) copy-start(bf16[4,8,32,256]{3,2,1,0:T(8,128)(2,1)} %param.13) | copy-start | bytes 1572868
  19.1 5.2 %copy-start.41 = (f32[1,1,256]{2,1,0:T(1,128)S(1)}, f32[1,1,256]{2,1,0:T(1,128)}, u32[]{:S(2)}) copy-start(f32[1,1,256]{2,1,0:T(1,128)} %get-tuple-element.146) | copy-start | bytes 3076
  19.1 5.2 %copy-start.43 = (f32[1,1,256]{2,1,0:T(1,128)S(1)}, f32[1,1,256]{2,1,0:T(1,128)}, u32[]{:S(2)}) copy-start(f32[1,1,256]{2,1,0:T(1,128)} %get-tuple-element.147) | copy-start | bytes 3076
  19.1 5.2 %copy-start.45 = (f32[1,1,256]{2,1,0:T(1,128)S(1)}, f32[1,1,256]{2,1,0:T(1,128)}, u32[]{:S(2)}) copy-start(f32[1,1,256]{2,1,0:T(1,128)} %get-tuple-element.148) | copy-start | bytes 3076
  19.1 5.2 %copy-start.47 = (f32[1,1,256]{2,1,0:T(1,128)S(1)}, f32[1,1,256]{2,1,0:T(1,128)}, u32[]{:S(2)}) copy-start(f32[1,1,256]{2,1,0:T(1,128)} %get-tuple-element.149) | copy-start | bytes 3076
  19.1 5.2 %copy-start.49 = (f32[1,1,256]{2,1,0:T(1,128)S(1)}, f32[1,1,256]{2,1,0:T(1,128)}, u32[]{:S(2)}) copy-start(f32[1,1,256]{2,1,0:T(1,128)} %get-tuple-element.150) | copy-start | bytes 3076
  19.1 5.2 %copy-start.51 = (f32[1,1,256]{2,1,0:T(1,128)S(1)}, f32[1,1,256]{2,1,0:T(1,128)}, u32[]{:S(2)}) copy-start(f32[1,1,256]{2,1,0:T(1,128)} %get-tuple-element.151) | copy-start | bytes 3076
  19.1 5.2 %copy-start.53 = (f32[1,1,256]{2,1,0:T(1,128)S(1)}, f32[1,1,256]{2,1,0:T(1,128)}, u32[]{:S(2)}) copy-start(f32[1,1,256]{2,1,0:T(1,128)} %get-tuple-element.152) | copy-start | bytes 3076
  19.1 5.2 %copy-start.55 = (f32[1,1,256]{2,1,0:T(1,128)S(1)}, f32[1,1,256]{2,1,0:T(1,128)}, u32[]{:S(2)}) copy-start(f32[1,1,256]{2,1,0:T(1,128)} %get-tuple-element.153) | copy-start | bytes 3076
  19.1 5.2 %copy-start.57 = (f32[1,1,256]{2,1,0:T(1,128)S(1)}, f32[1,1,256]{2,1,0:T(1,128)}, u32[]{:S(2)}) copy-start(f32[1,1,256]{2,1,0:T(1,128)} %get-tuple-element.154) | copy-start | bytes 3076
  19.2 5.2 %copy-start.59 = (f32[1,1,256]{2,1,0:T(1,128)S(1)}, f32[1,1,256]{2,1,0:T(1,128)}, u32[]{:S(2)}) copy-start(f32[1,1,256]{2,1,0:T(1,128)} %get-tuple-element.155) | copy-start | bytes 3076
  19.2 5.2 %copy-start.61 = (f32[1,1,256]{2,1,0:T(1,128)S(1)}, f32[1,1,256]{2,1,0:T(1,128)}, u32[]{:S(2)}) copy-start(f32[1,1,256]{2,1,0:T(1,128)} %get-tuple-element.156) | copy-start | bytes 3076
  19.2 5.2 %copy-start.63 = (f32[1,1,256]{2,1,0:T(1,128)S(1)}, f32[1,1,256]{2,1,0:T(1,128)}, u32[]{:S(2)}) copy-start(f32[1,1,256]{2,1,0:T(1,128)} %get-tuple-element.157) | copy-start | bytes 3076
  19.2 5.2 %copy-start.65 = (f32[1,1,256]{2,1,0:T(1,128)S(1)}, f32[1,1,256]{2,1,0:T(1,128)}, u32[]{:S(2)}) copy-start(f32[1,1,256]{2,1,0:T(1,128)} %get-tuple-element.158) | copy-start | bytes 3076
  19.2 5.2 %copy-start.67 = (f32[1,1,256]{2,1,0:T(1,128)S(1)}, f32[1,1,256]{2,1,0:T(1,128)}, u32[]{:S(2)}) copy-start(f32[1,1,256]{2,1,0:T(1,128)} %get-tuple-element.159) | copy-start | bytes 3076
  19.2 5.2 %copy-start.69 = (f32[1,1,256]{2,1,0:T(1,128)S(1)}, f32[1,1,256]{2,1,0:T(1,128)}, u32[]{:S(2)}) copy-start(f32[1,1,256]{2,1,0:T(1,128)} %get-tuple-element.160) | copy-start | bytes 3076
  19.2 5.2 %copy-start.71 = (f32[1,1,256]{2,1,0:T(1,128)S(1)}, f32[1,1,256]{2,1,0:T(1,128)}, u32[]{:S(2)}) copy-start(f32[1,1,256]{2,1,0:T(1,128)} %get-tuple-element.161) | copy-start | bytes 3076
  19.2 5.2 %copy-start.73 = (f32[1,1,256]{2,1,0:T(1,128)S(1)}, f32[1,1,256]{2,1,0:T(1,128)}, u32[]{:S(2)}) copy-start(f32[1,1,256]{2,1,0:T(1,128)} %get-tuple-element.162) | copy-start | bytes 3076
  19.2 5.2 %copy-start.75 = (f32[1,1,256]{2,1,0:T(1,128)S(1)}, f32[1,1,256]{2,1,0:T(1,128)}, u32[]{:S(2)}) copy-start(f32[1,1,256]{2,1,0:T(1,128)} %get-tuple-element.163) | copy-start | bytes 3076
  19.2 5.2 %copy-start.77 = (f32[1,1,256]{2,1,0:T(1,128)S(1)}, f32[1,1,256]{2,1,0:T(1,128)}, u32[]{:S(2)}) copy-start(f32[1,1,256]{2,1,0:T(1,128)} %get-tuple-element.164) | copy-start | bytes 3076
  19.3 5.2 %copy-start.79 = (f32[1,1,256]{2,1,0:T(1,128)S(1)}, f32[1,1,256]{2,1,0:T(1,128)}, u32[]{:S(2)}) copy-start(f32[1,1,256]{2,1,0:T(1,128)} %get-tuple-element.165) | copy-start | bytes 3076
  24.7 9.7 %copy-start.24 = (f32[256]{0:T(256)S(1)}, f32[256]{0:T(256)}, u32[]{:S(2)}) copy-start(f32[256]{0:T(256)} %param.19) | copy-start | bytes 3076
  42.6 12.4 %copy-start.11 = (f32[8,32,256]{2,1,0:T(8,128)}, f32[8,32,256]{2,1,0:T(8,128)S(1)}, u32[]{:S(2)}) copy-start(f32[8,32,256]{2,1,0:T(8,128)S(1)} %get-tuple-element.91) | copy-start | bytes 786436
  42.6 12.4 %copy-start.13 = (f32[8,32,256]{2,1,0:T(8,128)}, f32[8,32,256]{2,1,0:T(8,128)S(1)}, u32[]{:S(2)}) copy-start(f32[8,32,256]{2,1,0:T(8,128)S(1)} %get-tuple-element.92) | copy-start | bytes 786436
  42.6 12.4 %copy-start.15 = (f32[8,32,256]{2,1,0:T(8,128)}, f32[8,32,256]{2,1,0:T(8,128)S(1)}, u32[]{:S(2)}) copy-start(f32[8,32,256]{2,1,0:T(8,128)S(1)} %get-tuple-element.93) | copy-start | bytes 786436
  42.6 12.4 %copy-start.17 = (f32[8,32,256]{2,1,0:T(8,128)}, f32[8,32,256]{2,1,0:T(8,128)S(1)}, u32[]{:S(2)}) copy-start(f32[8,32,256]{2,1,0:T(8,128)S(1)} %get-tuple-element.94) | copy-start | bytes 786436
  57.0 3.3 %collective-permute-start.3 = (f32[270336]{0:T(1024)}, f32[270336]{0:T(1024)}, u32[]{:S(2)}, u32[]{:S(2)}) collective-permute-start(f32[270336]{0:T(1024)} %pad_dynamic-slice_fusion), channel_id=1, source_target_pairs={{0,1},{1,0},{2,3},{3,2},{4,5},{5,4},{6,7},{7,6},{8,9},{9,8},{10,11... | collective-permute-start | bytes 3244040 | tf_op jit(solution)/shard_map/ppermute | solution.py:223
  57.6 5.4 %copy-start.7 = (f32[4,8,32,256]{3,2,1,0:T(8,128)S(1)}, f32[4,8,32,256]{3,2,1,0:T(8,128)}, u32[]{:S(2)}) copy-start(f32[4,8,32,256]{3,2,1,0:T(8,128)} %get-tuple-element.19) | copy-start | bytes 3145732
  72.5 8.9 %copy-start.3 = (f32[4,8,32,256]{3,2,1,0:T(8,128)S(1)}, f32[4,8,32,256]{3,2,1,0:T(8,128)}, u32[]{:S(2)}) copy-start(f32[4,8,32,256]{3,2,1,0:T(8,128)} %copy-done.2) | copy-start | bytes 3145732
  72.9 4.9 %collective-permute-start.10 = (f32[12800]{0:T(1024)S(1)}, f32[12800]{0:T(1024)S(1)}, u32[]{:S(2)}, u32[]{:S(2)}) collective-permute-start(f32[12800]{0:T(1024)S(1)} %pad_maximum_fusion.14), channel_id=1, source_target_pairs={{0,1},{1,0},{2,3},{3,2},{4,5},{5,4},{6,7},{7,6},{8,9},{9,8},{10,11... | collective-permute-start | bytes 153608 | tf_op jit(solution)/shard_map/ppermute | solution.py:16
  73.4 8.0 %collective-permute-start.4 = (bf16[4,3,32,256]{3,2,1,0:T(8,128)(2,1)S(1)}, bf16[4,3,32,256]{3,2,1,0:T(8,128)(2,1)S(1)}, u32[]{:S(2)}, u32[]{:S(2)}) collective-permute-start(bf16[4,3,32,256]{3,2,1,0:T(8,128)(2,1)S(1)} %get-tuple-element.128), channel_id=1, source_target_pairs={{0,1},{1,2},{2,3},{3,4},{4,5},{5,6},{6,7},{7,8},{8,9},{9,10},{10,1... | collective-permute-start | bytes 589832 | tf_op jit(solution)/shard_map/ppermute | solution.py:28
  73.6 7.8 %collective-permute-start.5 = (bf16[4,3,32,256]{3,2,1,0:T(8,128)(2,1)S(1)}, bf16[4,3,32,256]{3,2,1,0:T(8,128)(2,1)S(1)}, u32[]{:S(2)}, u32[]{:S(2)}) collective-permute-start(bf16[4,3,32,256]{3,2,1,0:T(8,128)(2,1)S(1)} %get-tuple-element.129), channel_id=1, source_target_pairs={{1,0},{2,1},{3,2},{4,3},{5,4},{6,5},{7,6},{8,7},{9,8},{10,9},{11,1... | collective-permute-start | bytes 589832 | tf_op jit(solution)/shard_map/ppermute | solution.py:29
  77.9 20.9 %collective-permute-start.11 = (f32[12800]{0:T(1024)S(1)}, f32[12800]{0:T(1024)S(1)}, u32[]{:S(2)}, u32[]{:S(2)}) collective-permute-start(f32[12800]{0:T(1024)S(1)} %fusion.310), channel_id=1, source_target_pairs={{0,2},{1,3},{2,0},{3,1},{4,6},{5,7},{6,4},{7,5},{8,10},{9,11},{10,... | collective-permute-start | bytes 153608 | tf_op jit(solution)/shard_map/ppermute | solution.py:16
  83.1 14.1 %collective-permute-start.6 = (f32[67584]{0:T(1024)S(1)}, f32[67584]{0:T(1024)S(1)}, u32[]{:S(2)}, u32[]{:S(2)}) collective-permute-start(f32[67584]{0:T(1024)S(1)} %get-tuple-element.114), channel_id=1, source_target_pairs={{0,2},{1,3},{2,0},{3,1},{4,6},{5,7},{6,4},{7,5},{8,10},{9,11},{10,... | collective-permute-start | bytes 811016 | tf_op jit(solution)/shard_map/ppermute | solution.py:223
  83.2 14.0 %collective-permute-start.7 = (f32[67584]{0:T(1024)S(1)}, f32[67584]{0:T(1024)S(1)}, u32[]{:S(2)}, u32[]{:S(2)}) collective-permute-start(f32[67584]{0:T(1024)S(1)} %get-tuple-element.116), channel_id=1, source_target_pairs={{0,4},{1,5},{2,6},{3,7},{4,0},{5,1},{6,2},{7,3},{8,12},{9,13},{10,... | collective-permute-start | bytes 811016 | tf_op jit(solution)/shard_map/ppermute | solution.py:223
  83.2 15.3 %collective-permute-start.8 = (f32[67584]{0:T(1024)S(1)}, f32[67584]{0:T(1024)S(1)}, u32[]{:S(2)}, u32[]{:S(2)}) collective-permute-start(f32[67584]{0:T(1024)S(1)} %get-tuple-element.115), channel_id=1, source_target_pairs={{0,6},{1,7},{2,4},{3,5},{4,2},{5,3},{6,0},{7,1},{8,14},{9,15},{10,... | collective-permute-start | bytes 811016 | tf_op jit(solution)/shard_map/ppermute | solution.py:223
  98.7 10.0 %collective-permute-start.14 = (f32[33792]{0:T(1024)S(1)}, f32[33792]{0:T(1024)S(1)}, u32[]{:S(2)}, u32[]{:S(2)}) collective-permute-start(f32[33792]{0:T(1024)S(1)} %dynamic_slice.31), channel_id=1, source_target_pairs={{0,8},{1,9},{2,10},{3,11},{4,12},{5,13},{6,14},{7,15},{8,0},{9,1},... | collective-permute-start | bytes 405512 | tf_op jit(solution)/shard_map/ppermute | solution.py:223
  98.8 4.7 %collective-permute-start.12 = (f32[12800]{0:T(1024)S(1)}, f32[12800]{0:T(1024)S(1)}, u32[]{:S(2)}, u32[]{:S(2)}) collective-permute-start(f32[12800]{0:T(1024)S(1)} %add.802), channel_id=1, source_target_pairs={{0,4},{1,5},{2,6},{3,7},{4,0},{5,1},{6,2},{7,3},{8,12},{9,13},{10,... | collective-permute-start | bytes 153608 | tf_op jit(solution)/shard_map/ppermute | solution.py:16
  103.5 5.1 %collective-permute-start.13 = (f32[12800]{0:T(1024)S(1)}, f32[12800]{0:T(1024)S(1)}, u32[]{:S(2)}, u32[]{:S(2)}) collective-permute-start(f32[12800]{0:T(1024)S(1)} %add.803), channel_id=1, source_target_pairs={{0,8},{1,9},{2,10},{3,11},{4,12},{5,13},{6,14},{7,15},{8,0},{9,1},... | collective-permute-start | bytes 153608 | tf_op jit(solution)/shard_map/ppermute | solution.py:16
  108.7 5.4 %collective-permute-start.15 = (bf16[33792]{0:T(1024)(128)(2,1)S(1)}, bf16[33792]{0:T(1024)(128)(2,1)S(1)}, u32[]{:S(2)}, u32[]{:S(2)}) collective-permute-start(bf16[33792]{0:T(1024)(128)(2,1)S(1)} %add_convert_fusion.1), channel_id=1, source_target_pairs={{0,8},{1,9},{2,10},{3,11},{4,12},{5,13},{6,14},{7,15},{8,0},{9,1},... | collective-permute-start | bytes 202760 | tf_op jit(solution)/shard_map/ppermute | solution.py:235
  114.1 11.7 %copy-start.12 = (f32[8,32,256]{2,1,0:T(8,128)S(1)}, f32[8,32,256]{2,1,0:T(8,128)}, u32[]{:S(2)}) copy-start(f32[8,32,256]{2,1,0:T(8,128)} %copy-done.11) | copy-start | bytes 786436
  114.1 11.7 %copy-start.14 = (f32[8,32,256]{2,1,0:T(8,128)S(1)}, f32[8,32,256]{2,1,0:T(8,128)}, u32[]{:S(2)}) copy-start(f32[8,32,256]{2,1,0:T(8,128)} %copy-done.13) | copy-start | bytes 786436
  114.1 11.7 %copy-start.16 = (f32[8,32,256]{2,1,0:T(8,128)S(1)}, f32[8,32,256]{2,1,0:T(8,128)}, u32[]{:S(2)}) copy-start(f32[8,32,256]{2,1,0:T(8,128)} %copy-done.15) | copy-start | bytes 786436
  114.1 11.7 %copy-start.18 = (f32[8,32,256]{2,1,0:T(8,128)S(1)}, f32[8,32,256]{2,1,0:T(8,128)}, u32[]{:S(2)}) copy-start(f32[8,32,256]{2,1,0:T(8,128)} %copy-done.17) | copy-start | bytes 786436
  114.1 6.4 %collective-permute-start.16 = (bf16[67584]{0:T(1024)(128)(2,1)S(1)}, bf16[67584]{0:T(1024)(128)(2,1)S(1)}, u32[]{:S(2)}, u32[]{:S(2)}) collective-permute-start(bf16[67584]{0:T(1024)(128)(2,1)S(1)} %pad_maximum_fusion.13), channel_id=1, source_target_pairs={{0,4},{1,5},{2,6},{3,7},{4,0},{5,1},{6,2},{7,3},{8,12},{9,13},{10,... | collective-permute-start | bytes 405512 | tf_op jit(solution)/shard_map/ppermute | solution.py:235
  117.1 7.6 %collective-permute-start.17 = (bf16[67584]{0:T(1024)(128)(2,1)S(1)}, bf16[67584]{0:T(1024)(128)(2,1)S(1)}, u32[]{:S(2)}, u32[]{:S(2)}) collective-permute-start(bf16[67584]{0:T(1024)(128)(2,1)S(1)} %pad_maximum_fusion.13), channel_id=1, source_target_pairs={{0,2},{1,3},{2,0},{3,1},{4,6},{5,7},{6,4},{7,5},{8,10},{9,11},{10,... | collective-permute-start | bytes 405512 | tf_op jit(solution)/shard_map/ppermute | solution.py:235
  117.1 7.6 %collective-permute-start.18 = (bf16[67584]{0:T(1024)(128)(2,1)S(1)}, bf16[67584]{0:T(1024)(128)(2,1)S(1)}, u32[]{:S(2)}, u32[]{:S(2)}) collective-permute-start(bf16[67584]{0:T(1024)(128)(2,1)S(1)} %pad_maximum_fusion.13), channel_id=1, source_target_pairs={{0,6},{1,7},{2,4},{3,5},{4,2},{5,3},{6,0},{7,1},{8,14},{9,15},{10,... | collective-permute-start | bytes 405512 | tf_op jit(solution)/shard_map/ppermute | solution.py:235
  119.3 7.8 %collective-permute-start.9 = (bf16[4,8,3,256]{3,2,1,0:T(4,128)(2,1)S(1)}, bf16[4,8,3,256]{3,2,1,0:T(4,128)(2,1)S(1)}, u32[]{:S(2)}, u32[]{:S(2)}) collective-permute-start(bf16[4,8,3,256]{3,2,1,0:T(4,128)(2,1)S(1)} %slice.1630), channel_id=1, source_target_pairs={{0,15},{1,14},{2,13},{3,12},{4,11},{5,10},{6,9},{7,8},{8,7},{9,6},... | collective-permute-start | bytes 147464 | tf_op jit(solution)/shard_map/ppermute | solution.py:176
  125.8 3.4 %collective-permute-start.19 = (bf16[270336]{0:T(1024)(128)(2,1)}, bf16[270336]{0:T(1024)(128)(2,1)}, u32[]{:S(2)}, u32[]{:S(2)}) collective-permute-start(bf16[270336]{0:T(1024)(128)(2,1)} %pad_maximum_fusion.5), channel_id=1, source_target_pairs={{0,1},{1,0},{2,3},{3,2},{4,5},{5,4},{6,7},{7,6},{8,9},{9,8},{10,11... | collective-permute-start | bytes 1622024 | tf_op jit(solution)/shard_map/ppermute | solution.py:235
  (83 other events, 264.4 us)
